TPU v7x, 32 devices: a whole 2x2x4 slice. The times are simulated.
32 devices in a mesh: row: 4 (over x, core), col: 8 (over z, y).
Axes of the slice: x: 2, y: 2, z: 4, core: 2. Of those that a mesh axis runs over, the one named last changes fastest.
Arguments:
- panel_blocks: bfloat16 [3, 32, 8, 128, 128], P(None, 'col', 'row'), may hold values from -0.5 to 0.5
- user_weights: float32 [3, 32, 128], P(None, 'col'), may hold values from 0.1 to 10
- slot_offset: int32 [3, 32, 8], P(None, 'col', 'row'), may hold values from 0 to 7
Outputs:
- gram: float32 [8192, 8192], P('row', 'col')
All inputs are finite; a program needn't handle non-finite values.
Results may differ from a plain program's by a relative error of at most 0.0022.
Values may be sent and summed in bfloat16 or wider, within the bound.
No kernel may reach another device: no remote copies, remote signals or barrier semaphores. Data moves between devices by JAX's collectives and lax.ppermute only.
A program may use at most 128 MiB of HBM per device.

v0:
```python
import jax
import jax.numpy as jnp
from jax import lax
from jax.sharding import PartitionSpec as P

IBS = 8


def local(panel_blocks, user_weights, slot_offset):
    local_slots = panel_blocks.shape[2]
    blocks = panel_blocks.shape[-1]
    weighted = (user_weights[:, :, None, :, None] * panel_blocks.astype(jnp.float32)).astype(
        jnp.bfloat16
    )
    left_index = jnp.arange(local_slots, dtype=jnp.int32)[None, None, :] * IBS + slot_offset
    all_blocks, all_offset = (
        lax.all_gather(panel_blocks, "row", axis=2, tiled=True),
        lax.all_gather(slot_offset, "row", axis=2, tiled=True),
    )
    segments = local_slots * IBS * IBS
    partial_value = jnp.einsum(
        "pusxa,putxb->tpusab", weighted, all_blocks, preferred_element_type=jnp.float32
    )
    target = left_index[None] * IBS + jnp.transpose(all_offset, (2, 0, 1))[..., None]
    arrived, arrived_target = (
        lax.all_to_all(partial_value, "col", split_axis=0, concat_axis=0, tiled=True),
        lax.all_to_all(target, "col", split_axis=0, concat_axis=0, tiled=True),
    )
    summed = jax.ops.segment_sum(
        arrived.reshape(-1, blocks, blocks), arrived_target.reshape(-1), num_segments=segments
    )
    summed = summed.reshape(local_slots * IBS, IBS, blocks, blocks).transpose(0, 2, 1, 3)
    return summed.reshape(local_slots * IBS * blocks, IBS * blocks)


def solution(mesh):
    return jax.shard_map(
        local,
        mesh=mesh,
        in_specs=(P(None, "col", "row", None, None), P(None, "col", None), P(None, "col", "row")),
        out_specs=P("row", "col"),
        check_vma=False,
    )
```

profile of v0, /device:TPU:0, one launch (start us, length us, event | category | flops | bytes accessed | tf_op | source)
XLA Modules:
  0.0 404.4 jit_solution(7209376521936994303)
XLA Ops:
  6.5 0.0 all-gather.2.cloned.1.call-start
  6.5 0.7 all-gather.2.cloned.1.call-update
  7.3 0.7 copy.16
  7.9 6.2 %all_gather.6 = s32[3,4,8]{1,0,2:T(4,128)S(1)} all-gather(s32[3,4,2]{1,0,2:T(4,128)S(1)} %copy.16), channel_id=1, replica_groups=mesh['row'=4,'col'=8] {'row'}, dimensions={2}, use_global_device_ids=true | all-gather | bytes 480 | tf_op jit(solution)/shard_map/all_gather | solution.py:18
  14.1 0.8 add_multiply_fusion
  14.9 0.6 broadcast_add_fusion
  15.5 6.3 %all-to-all-start = ((s32[8,3,4,2]{2,3,1,0:T(2,128)}), s32[8,3,4,2]{2,3,1,0:T(2,128)S(1)}, u32[]{:S(2)}, u32[]{:S(2)}) async-start(s32[8,3,4,2]{2,3,1,0:T(2,128)} %broadcast_add_fusion), calls=%async_computation | async-start | bytes 49152 | tf_op jit(solution)/shard_map/all_to_all | solution.py:27
  21.8 18.4 %all-gather.2.cloned.1.call-done = bf16[3,4,8,128,128]{4,3,2,1,0:T(8,128)(2,1)} async-done(((bf16[3,4,2,128,128]{4,3,2,1,0:T(8,128)(2,1)}), bf16[3,4,8,128,128]{4,3,2,1,0:T(8,128)(2,1)}) %all-gather.2.cloned.1.call-update) | async-done | bytes 3145744 | tf_op jit(solution)/shard_map/all_gather | solution.py:17
  40.2 8.6 %convolution_bitcast_fusion = f32[8,3,4,2,128,128]{5,4,0,3,2,1:T(8,128)} fusion(bf16[3,4,8,128,128]{4,3,2,1,0:T(8,128)(2,1)} %all-gather.2.cloned.1.call-done, bf16[3,4,2,128,128]{4,3,2,1,0:T(8,128)(2,1)} %param.3, f32[3,4,128]{2,1,0:T(4,128)} %param.4), kind=kOutput, calls=%fused_computation.2 | convolution fusion | flops 806486016 | bytes 16521216 | tf_op jit(solution)/shard_map/pusxa,putxb->tpusab/dot_general | solution.py:21
  48.8 11.2 %copy.19 = f32[8,3,4,2,128,128]{5,4,3,2,1,0:T(8,128)} copy(f32[8,3,4,2,128,128]{5,4,0,3,2,1:T(8,128)} %convolution_bitcast_fusion) | data formatting | bytes 25165824 | tf_op jit(solution)/shard_map/pusxa,putxb->tpusab/transpose | solution.py:21
  60.0 0.0 all-to-all-done
  60.0 5.5 %all-to-all-start.1 = ((f32[8,3,4,2,128,128]{5,4,3,2,1,0:T(8,128)}), f32[8,3,4,2,128,128]{5,4,3,2,1,0:T(8,128)}, u32[]{:S(2)}, u32[]{:S(2)}) async-start(f32[8,3,4,2,128,128]{5,4,3,2,1,0:T(8,128)} %copy.19), calls=%async_computation.1 | async-start | bytes 25165824 | tf_op jit(solution)/shard_map/all_to_all | solution.py:26
  65.5 0.3 copy.17
  65.8 0.1 reshape.23
  65.9 273.0 %all-to-all-done.1 = f32[8,3,4,2,128,128]{5,4,3,2,1,0:T(8,128)} async-done(((f32[8,3,4,2,128,128]{5,4,3,2,1,0:T(8,128)}), f32[8,3,4,2,128,128]{5,4,3,2,1,0:T(8,128)}, u32[]{:S(2)}, u32[]{:S(2)}) %all-to-all-start.1) | async-done | bytes 12582944 | tf_op jit(solution)/shard_map/all_to_all | solution.py:26
  339.0 4.5 %broadcast_in_dim.2 = f32[128,128,128]{2,1,0:T(8,128)} broadcast(f32[]{:T(128)} %constant.2.clone.1), dimensions={} | broadcast | bytes 8388612 | tf_op jit(solution)/shard_map/broadcast_in_dim | solution.py:29
  343.4 38.7 %scatter_fusion = f32[128,128,128]{2,1,0:T(8,128)} fusion(f32[128,128,128]{2,1,0:T(8,128)} %broadcast_in_dim.2, s32[192]{0:T(256)S(1)} %reshape.23, f32[192,128,128]{2,1,0:T(8,128)} %bitcast.5), kind=kCustom, calls=%fused_computation | custom fusion | flops 3145728 | bytes 37749504 | tf_op jit(solution)/shard_map/scatter-add | solution.py:29
  382.2 9.9 %copy.20 = f32[16,128,8,128]{3,2,1,0:T(8,128)S(1)} copy(f32[16,128,8,128]{3,1,2,0:T(8,128)} %bitcast.22) | data formatting | bytes 16777216 | tf_op jit(solution)/shard_map/transpose | solution.py:32
  392.1 5.5 %copy.27 = f32[256,8,8,128]{3,1,2,0:T(8,128)} copy(f32[256,8,8,128]{3,2,1,0:T(8,128)S(1)} %bitcast.23) | data formatting | bytes 16777216
  (1 shorter events, 0.0 us)
Async XLA Ops:
  6.5 33.6 %all-gather.2.cloned.1.call-start = ((), (), s32[]{:S(2)}) async-start(), calls=%async_computation.2 | async-start | bytes 3932160 | tf_op jit(solution)/shard_map/all_gather | solution.py:17
  15.5 44.5 %all-to-all-start = ((s32[8,3,4,2]{2,3,1,0:T(2,128)}), s32[8,3,4,2]{2,3,1,0:T(2,128)S(1)}, u32[]{:S(2)}, u32[]{:S(2)}) async-start(s32[8,3,4,2]{2,3,1,0:T(2,128)} %broadcast_add_fusion), calls=%async_computation | async-start | bytes 49152 | tf_op jit(solution)/shard_map/all_to_all | solution.py:27
  60.0 279.0 %all-to-all-start.1 = ((f32[8,3,4,2,128,128]{5,4,3,2,1,0:T(8,128)}), f32[8,3,4,2,128,128]{5,4,3,2,1,0:T(8,128)}, u32[]{:S(2)}, u32[]{:S(2)}) async-start(f32[8,3,4,2,128,128]{5,4,3,2,1,0:T(8,128)} %copy.19), calls=%async_computation.1 | async-start | bytes 25165824 | tf_op jit(solution)/shard_map/all_to_all | solution.py:26
Sparse Core Ops, SparseCore 0:
  8.9 31.2 all-gather.1
where the time goes:
time: 405 us; the launch traced here: 404 us
  waiting for transfers between devices  292 us (72%)
  other arithmetic  40.1 us (10%)
  local copies, waits for them, and re-layouts  32.2 us (8%)
  between operations  13.4 us (3%)
  starting transfers between devices  11.8 us (3%)
  matrix products  8.59 us (2%)
  blocking collectives  6.17 us (2%)
    all_to_all x1, waiting for transfers between devices, local(): lax.all_to_all(partial_value, 'col', split_axis=0, concat_axis=0, tiled=T...  273 us
    scatter-add x1, other arithmetic, local(): jax.ops.segment_sum(arrived.reshape(-1, blocks, blocks), arrived_target.r...  38.7 us
    all_gather x1, waiting for transfers between devices, local(): lax.all_gather(panel_blocks, 'row', axis=2, tiled=True)  18.4 us
    transpose x1, local copies, waits for them, and re-layouts, local(): jnp.einsum('pusxa,putxb->tpusab', weighted, all_blocks, preferred_element...  11.2 us
    transpose x1, local copies, waits for them, and re-layouts, local(): summed.reshape(local_slots * IBS, IBS, blocks, blocks).transpose(0, 2, 1, 3)  9.92 us
    dot_general x1, matrix products, local(): jnp.einsum('pusxa,putxb->tpusab', weighted, all_blocks, preferred_element...  8.59 us
  transfers between devices with their start and end apart: 3, of which 2 were waited for; matrix products, arithmetic and copies ran while one was open for 6% of the time, Pallas kernels for 0%

commit v1 on v0

v1 whole, which is shorter than its diff:
```python
import functools

import jax
import jax.numpy as jnp
from jax import lax
from jax.experimental import pallas as pl
from jax.experimental.pallas import tpu as pltpu
from jax.sharding import PartitionSpec as P

IBS = 8
CHUNK = 8


def gram_kernel(offs_ref, bs_ref, w_ref, bc_ref, o_ref, *, chunk, local_slots, blk):
    step = pl.program_id(0)

    @pl.when(step == 0)
    def _():
        o_ref[...] = jnp.zeros_like(o_ref)

    stride = local_slots + 1
    for k in range(chunk):
        g = step * chunk + k
        w = w_ref[pl.ds(k, 1), :]
        lhs = jnp.concatenate(
            [
                (bs_ref[k, s].astype(jnp.float32).T * w).astype(jnp.bfloat16)
                for s in range(local_slots)
            ],
            axis=0,
        )
        prod = jnp.dot(lhs, bc_ref[k], preferred_element_type=jnp.float32)
        col = pl.multiple_of(offs_ref[g * stride + local_slots] * blk, blk)
        for s in range(local_slots):
            row = pl.multiple_of((s * IBS + offs_ref[g * stride + s]) * blk, blk)
            o_ref[pl.ds(row, blk), pl.ds(col, blk)] += prod[s * blk : (s + 1) * blk]


def gram_call(offs, bs, w, bc):
    n, local_slots, blk, _ = bs.shape
    chunk = CHUNK
    kernel = functools.partial(gram_kernel, chunk=chunk, local_slots=local_slots, blk=blk)
    out_rows, out_cols = local_slots * IBS * blk, IBS * blk
    return pl.pallas_call(
        kernel,
        grid_spec=pltpu.PrefetchScalarGridSpec(
            num_scalar_prefetch=1,
            grid=(n // chunk,),
            in_specs=[
                pl.BlockSpec((chunk, local_slots, blk, blk), lambda i, o: (i, 0, 0, 0)),
                pl.BlockSpec((chunk, blk), lambda i, o: (i, 0)),
                pl.BlockSpec((chunk, blk, blk), lambda i, o: (i, 0, 0)),
            ],
            out_specs=pl.BlockSpec((out_rows, out_cols), lambda i, o: (0, 0)),
        ),
        out_shape=jax.ShapeDtypeStruct((out_rows, out_cols), jnp.float32),
        compiler_params=pltpu.CompilerParams(
            dimension_semantics=("arbitrary",), vmem_limit_bytes=48 * 1024 * 1024
        ),
        cost_estimate=pl.CostEstimate(
            flops=2 * n * local_slots * blk * blk * blk,
            transcendentals=0,
            bytes_accessed=n * (local_slots + 1) * blk * blk * 2 + out_rows * out_cols * 4,
        ),
    )(offs, bs, w, bc)


def local(panel_blocks, user_weights, slot_offset, *, nrow, ncol):
    panels, _, local_slots, blk, _ = panel_blocks.shape
    r = lax.axis_index("row")
    c = lax.axis_index("col")
    blocks = lax.all_gather(panel_blocks, "col", axis=1, tiled=True)
    weights = lax.all_gather(user_weights, "col", axis=1, tiled=True)
    offsets = lax.all_gather(slot_offset, "col", axis=1, tiled=True)
    all_offsets = lax.all_gather(offsets, "row", axis=2, tiled=True)
    users = blocks.shape[1]

    src = c // local_slots
    own = lax.dynamic_index_in_dim(blocks, c % local_slots, axis=2, keepdims=False)
    received = [own]
    for k in range(1, nrow):
        perm = [
            ((cc // local_slots) * ncol + cc, ((cc // local_slots + k) % nrow) * ncol + cc)
            for cc in range(ncol)
        ]
        received.append(lax.ppermute(own, ("row", "col"), perm))
    which = (r - src + nrow) % nrow
    column_blocks = received[0]
    for k in range(1, nrow):
        column_blocks = jnp.where(which == k, received[k], column_blocks)

    col_offsets = lax.dynamic_index_in_dim(all_offsets, c, axis=2, keepdims=True)
    offs = jnp.concatenate([offsets, col_offsets], axis=2)
    offs = jnp.clip(offs, 0, IBS - 1).reshape(-1).astype(jnp.int32)

    n = panels * users
    return gram_call(
        offs,
        blocks.reshape(n, local_slots, blk, blk),
        weights.reshape(n, blk),
        column_blocks.reshape(n, blk, blk),
    )


def solution(mesh):
    nrow, ncol = mesh.shape["row"], mesh.shape["col"]
    return jax.shard_map(
        functools.partial(local, nrow=nrow, ncol=ncol),
        mesh=mesh,
        in_specs=(P(None, "col", "row", None, None), P(None, "col", None), P(None, "col", "row")),
        out_specs=P("row", "col"),
        check_vma=False,
    )
```

time: 405 us -> 243 us (0.60)
  waiting for transfers between devices: 292 us -> 105 us
  blocking collectives: 6.17 us -> 94.1 us
  other arithmetic: 40.1 us -> 2.49 us
  local copies, waits for them, and re-layouts: 32.2 us -> 2.69 us
  Pallas kernels: 0 us -> 14.4 us
  matrix products: 8.59 us -> 0 us
    all_to_all x2 -> x0, waiting for transfers between devices: 273 us -> none  [the longest x1 273 us: local(): lax.all_to_all(partial_value, 'col', split_axis=0, concat_axis=0, tiled=T...]
    all_gather x1 -> x3, blocking collectives: 6.17 us -> 94.1 us  [the longest x1 33.8 us: local(): weights = lax.all_gather(user_weights, 'col', axis=1, tiled=True)]
    all_gather x1, waiting for transfers between devices: 18.4 us -> 104 us  [local(): blocks = lax.all_gather(panel_blocks, 'col', axis=1, tiled=True)]
    scatter-add x1 -> x0, other arithmetic: 38.7 us -> none  [local(): jax.ops.segment_sum(arrived.reshape(-1, blocks, blocks), arrived_target.r...]
    transpose x2 -> x0, local copies, waits for them, and re-layouts: 21.1 us -> none  [the longest x1 11.2 us: local(): jnp.einsum('pusxa,putxb->tpusab', weighted, all_blocks, preferred_element...]
    pallas_call x0 -> x1, Pallas kernels: none -> 14.4 us  [gram_call(): pl.pallas_call(kernel, grid_spec=pltpu.PrefetchScalarGridSpec(num_scalar_...]
    all_to_all x2 -> x0, starting transfers between devices: 11.8 us -> none  [the longest x1 6.28 us: local(): lax.all_to_all(target, 'col', split_axis=0, concat_axis=0, tiled=True)]
    ppermute x0 -> x3, starting transfers between devices: none -> 10.3 us  [local(): received.append(lax.ppermute(own, ('row', 'col'), perm))]
  transfers between devices with their start and end apart: 3 -> 4, of which waited for: 2 -> 1; matrix products, arithmetic and copies ran while one was open for 6% -> 0% of each run, Pallas kernels for 0% -> 0%
where the time goes in v1:
time: 243 us; the launch traced here: 242 us
  waiting for transfers between devices  105 us (43%)
  blocking collectives  94.1 us (39%)
  Pallas kernels  14.4 us (6%)
  between operations  13.5 us (6%)
  starting transfers between devices  10.3 us (4%)
  local copies, waits for them, and re-layouts  2.69 us (1%)
  other arithmetic  2.49 us (1%)
    all_gather x1, waiting for transfers between devices, local(): blocks = lax.all_gather(panel_blocks, 'col', axis=1, tiled=True)  104 us
    all_gather x1, blocking collectives, local(): weights = lax.all_gather(user_weights, 'col', axis=1, tiled=True)  33.8 us
    all_gather x1, blocking collectives, local(): offsets = lax.all_gather(slot_offset, 'col', axis=1, tiled=True)  30.4 us
    all_gather x1, blocking collectives, local(): all_offsets = lax.all_gather(offsets, 'row', axis=2, tiled=True)  29.9 us
    pallas_call x1, Pallas kernels, gram_call(): pl.pallas_call(kernel, grid_spec=pltpu.PrefetchScalarGridSpec(num_scalar_...  14.4 us
    ppermute x3, starting transfers between devices, local(): received.append(lax.ppermute(own, ('row', 'col'), perm))  10.3 us
  transfers between devices with their start and end apart: 4, of which 1 were waited for; matrix products, arithmetic and copies ran while one was open for 0% of the time, Pallas kernels for 0%

profile of v1, /device:TPU:0, one launch (start us, length us, event | category | flops | bytes accessed | tf_op | source)
XLA Modules:
  0.0 242.2 jit_solution(17347175316752219991)
XLA Ops:
  6.5 0.0 all-gather.2.cloned.1.call-start
  6.5 0.7 all-gather.2.cloned.1.call-update
  7.3 0.0 copy-start.1
  7.3 0.0 copy-start
  7.3 104.0 %all-gather.2.cloned.1.call-done = bf16[3,32,2,128,128]{4,3,2,1,0:T(8,128)(2,1)} async-done(((bf16[3,4,2,128,128]{4,3,2,1,0:T(8,128)(2,1)}), bf16[3,32,2,128,128]{4,3,2,1,0:T(8,128)(2,1)}) %all-gather.2.cloned.1.call-update) | async-done | bytes 6291472 | tf_op jit(solution)/shard_map/all_gather | solution.py:72
  111.3 2.1 dynamic-slice_bitcast_fusion
  113.4 4.0 %collective-permute-start = (bf16[3,32,128,128]{3,2,1,0:T(8,128)(2,1)S(1)}, bf16[3,32,128,128]{3,2,1,0:T(8,128)(2,1)}, u32[]{:S(2)}, u32[]{:S(2)}) collective-permute-start(bf16[3,32,128,128]{3,2,1,0:T(8,128)(2,1)S(1)} %dynamic-slice_bitcast_fusion), channel_id=1, source_target_pairs={{0,24},{1,25},{10,2},{11,3},{20,12},{21,13},{30,22},{31,23}} | collective-permute-start | bytes 9437192 | tf_op jit(solution)/shard_map/ppermute | solution.py:86
  117.4 3.4 %collective-permute-start.1 = (bf16[3,32,128,128]{3,2,1,0:T(8,128)(2,1)S(1)}, bf16[3,32,128,128]{3,2,1,0:T(8,128)(2,1)}, u32[]{:S(2)}, u32[]{:S(2)}) collective-permute-start(bf16[3,32,128,128]{3,2,1,0:T(8,128)(2,1)S(1)} %dynamic-slice_bitcast_fusion), channel_id=1, source_target_pairs={{0,16},{1,17},{10,26},{11,27},{20,4},{21,5},{30,14},{31,15}} | collective-permute-start | bytes 9437192 | tf_op jit(solution)/shard_map/ppermute | solution.py:86
  120.8 2.9 %collective-permute-start.2 = (bf16[3,32,128,128]{3,2,1,0:T(8,128)(2,1)S(1)}, bf16[3,32,128,128]{3,2,1,0:T(8,128)(2,1)}, u32[]{:S(2)}, u32[]{:S(2)}) collective-permute-start(bf16[3,32,128,128]{3,2,1,0:T(8,128)(2,1)S(1)} %dynamic-slice_bitcast_fusion), channel_id=1, source_target_pairs={{0,8},{1,9},{10,18},{11,19},{20,28},{21,29},{30,6},{31,7}} | collective-permute-start | bytes 9437192 | tf_op jit(solution)/shard_map/ppermute | solution.py:86
  123.7 0.0 copy-done.1
  123.7 0.1 copy.11
  123.8 30.4 %all_gather.12 = s32[3,32,2]{0,2,1:T(2,128)S(1)} all-gather(s32[3,4,2]{0,2,1:T(2,128)S(1)} %copy.11), channel_id=1, replica_groups=mesh['row'=4,'col'=8] {'col'}, dimensions={1}, use_global_device_ids=true | all-gather | bytes 864 | tf_op jit(solution)/shard_map/all_gather | solution.py:74
  154.2 0.1 copy.12
  154.3 0.1 copy.13
  154.4 29.9 %all_gather.13 = s32[3,32,8]{1,0,2:T(4,128)S(1)} all-gather(s32[3,32,2]{1,0,2:T(4,128)S(1)} %copy.12), channel_id=1, replica_groups=mesh['row'=4,'col'=8] {'row'}, dimensions={2}, use_global_device_ids=true | all-gather | bytes 3840 | tf_op jit(solution)/shard_map/all_gather | solution.py:75
  184.4 0.1 copy.15
  184.5 0.2 min.12.offs_ref
  184.6 0.0 copy-done
  184.7 33.8 %all_gather.15 = f32[3,32,128]{2,0,1:T(4,128)S(1)} all-gather(f32[3,4,128]{2,0,1:T(4,128)S(1)} %copy.16), channel_id=1, replica_groups=mesh['row'=4,'col'=8] {'col'}, dimensions={1}, use_global_device_ids=true | all-gather | bytes 55296 | tf_op jit(solution)/shard_map/all_gather | solution.py:73
  218.5 0.0 collective-permute-done
  218.5 0.0 collective-permute-done.1
  218.5 0.0 collective-permute-done.2
  218.5 2.5 %select_select_fusion = bf16[3,32,128,128]{3,2,1,0:T(8,128)(2,1)S(1)} fusion(bf16[3,32,128,128]{3,2,1,0:T(8,128)(2,1)} %collective-permute-done, bf16[3,32,128,128]{3,2,1,0:T(8,128)(2,1)} %collective-permute-done.1, bf16[3,32,128,128]{3,2,1,0:T(8,128)(2,1)} %collective-permute-done.2, pred[]{:T(512)S(6)} %eq.14, pred[]{:T(512)S(6)} %eq.13, pred[]{:T(512)S(6)} %eq.12, ...), kind=kLoop, calls=%fused_computation | loop fusion | flops 4718592 | bytes 15728647 | tf_op jit(solution)/shard_map/jit(_where)/select_n | solution.py:90
  221.0 14.4 %shard_map.37 = f32[2048,1024]{1,0:T(8,128)} custom-call(s32[288]{0:T(512)S(1)} %min.12.offs_ref, bf16[96,2,128,128]{3,2,1,0:T(8,128)(2,1)} %bitcast.9, f32[96,128]{1,0:T(8,128)S(1)} %bitcast.8, bf16[96,128,128]{2,1,0:T(8,128)(2,1)S(1)} %bitcast.7), custom_call_target="tpu_custom_call" | custom-call | flops 805306368 | bytes 17825792 | tf_op jit(solution)/shard_map/pallas_call | solution.py:44
  (5 shorter events, 0.0 us)
Async XLA Ops:
  6.5 104.8 %all-gather.2.cloned.1.call-start = ((), (), s32[]{:S(2)}) async-start(), calls=%async_computation | async-start | bytes 7077888 | tf_op jit(solution)/shard_map/all_gather | solution.py:72
  7.3 116.5 %copy-start.1 = (s32[3,4,2]{1,2,0:T(2,128)S(1)}, s32[3,4,2]{1,2,0:T(2,128)}, u32[]{:S(2)}) copy-start(s32[3,4,2]{1,2,0:T(2,128)} %param.5) | copy-start | bytes 292
  7.3 177.4 %copy-start = (f32[3,4,128]{2,1,0:T(4,128)S(1)}, f32[3,4,128]{2,1,0:T(4,128)}, u32[]{:S(2)}) copy-start(f32[3,4,128]{2,1,0:T(4,128)} %param.4) | copy-start | bytes 18436
  113.4 105.0 %collective-permute-start = (bf16[3,32,128,128]{3,2,1,0:T(8,128)(2,1)S(1)}, bf16[3,32,128,128]{3,2,1,0:T(8,128)(2,1)}, u32[]{:S(2)}, u32[]{:S(2)}) collective-permute-start(bf16[3,32,128,128]{3,2,1,0:T(8,128)(2,1)S(1)} %dynamic-slice_bitcast_fusion), channel_id=1, source_target_pairs={{0,24},{1,25},{10,2},{11,3},{20,12},{21,13},{30,22},{31,23}} | collective-permute-start | bytes 9437192 | tf_op jit(solution)/shard_map/ppermute | solution.py:86
  117.4 101.0 %collective-permute-start.1 = (bf16[3,32,128,128]{3,2,1,0:T(8,128)(2,1)S(1)}, bf16[3,32,128,128]{3,2,1,0:T(8,128)(2,1)}, u32[]{:S(2)}, u32[]{:S(2)}) collective-permute-start(bf16[3,32,128,128]{3,2,1,0:T(8,128)(2,1)S(1)} %dynamic-slice_bitcast_fusion), channel_id=1, source_target_pairs={{0,16},{1,17},{10,26},{11,27},{20,4},{21,5},{30,14},{31,15}} | collective-permute-start | bytes 9437192 | tf_op jit(solution)/shard_map/ppermute | solution.py:86
  120.8 97.7 %collective-permute-start.2 = (bf16[3,32,128,128]{3,2,1,0:T(8,128)(2,1)S(1)}, bf16[3,32,128,128]{3,2,1,0:T(8,128)(2,1)}, u32[]{:S(2)}, u32[]{:S(2)}) collective-permute-start(bf16[3,32,128,128]{3,2,1,0:T(8,128)(2,1)S(1)} %dynamic-slice_bitcast_fusion), channel_id=1, source_target_pairs={{0,8},{1,9},{10,18},{11,19},{20,28},{21,29},{30,6},{31,7}} | collective-permute-start | bytes 9437192 | tf_op jit(solution)/shard_map/ppermute | solution.py:86
Sparse Core Ops, SparseCore 0:
  9.5 101.7 all-gather.1

commit v2 on v1

v2 whole, which is shorter than its diff:
```python
import functools

import jax
import jax.numpy as jnp
from jax import lax
from jax.experimental import pallas as pl
from jax.experimental.pallas import tpu as pltpu
from jax.sharding import PartitionSpec as P

IBS = 8
CHUNK = 8
META = 16


def gram_kernel(offs_ref, bs_ref, bc_ref, o_ref, *, chunk, local_slots, blk):
    step = pl.program_id(0)

    @pl.when(step == 0)
    def _():
        o_ref[...] = jnp.zeros_like(o_ref)

    stride = local_slots + 1
    for k in range(chunk):
        g = step * chunk + k
        meta = bs_ref[k, 0, blk : blk + META].astype(jnp.float32)
        w = meta[0:1] + meta[1:2] + meta[2:3]
        lhs = jnp.concatenate(
            [
                (bs_ref[k, s, :blk].astype(jnp.float32).T * w).astype(jnp.bfloat16)
                for s in range(local_slots)
            ],
            axis=0,
        )
        prod = jnp.dot(lhs, bc_ref[k, :blk], preferred_element_type=jnp.float32)
        col = pl.multiple_of(offs_ref[g * stride + local_slots] * blk, blk)
        for s in range(local_slots):
            row = pl.multiple_of((s * IBS + offs_ref[g * stride + s]) * blk, blk)
            o_ref[pl.ds(row, blk), pl.ds(col, blk)] += prod[s * blk : (s + 1) * blk]


def gram_call(offs, bs, bc):
    n, local_slots, rows, blk = bs.shape
    chunk = CHUNK
    kernel = functools.partial(gram_kernel, chunk=chunk, local_slots=local_slots, blk=blk)
    out_rows, out_cols = local_slots * IBS * blk, IBS * blk
    return pl.pallas_call(
        kernel,
        grid_spec=pltpu.PrefetchScalarGridSpec(
            num_scalar_prefetch=1,
            grid=(n // chunk,),
            in_specs=[
                pl.BlockSpec((chunk, local_slots, rows, blk), lambda i, o: (i, 0, 0, 0)),
                pl.BlockSpec((chunk, rows, blk), lambda i, o: (i, 0, 0)),
            ],
            out_specs=pl.BlockSpec((out_rows, out_cols), lambda i, o: (0, 0)),
        ),
        out_shape=jax.ShapeDtypeStruct((out_rows, out_cols), jnp.float32),
        compiler_params=pltpu.CompilerParams(
            dimension_semantics=("arbitrary",), vmem_limit_bytes=48 * 1024 * 1024
        ),
        cost_estimate=pl.CostEstimate(
            flops=2 * n * local_slots * blk * blk * blk,
            transcendentals=0,
            bytes_accessed=n * (local_slots + 1) * blk * blk * 2 + out_rows * out_cols * 4,
        ),
    )(offs, bs, bc)


def with_meta(panel_blocks, user_weights, slot_offset):
    panels, users, local_slots, blk, _ = panel_blocks.shape
    hi = lax.reduce_precision(user_weights, exponent_bits=8, mantissa_bits=7)
    rest = user_weights - hi
    mid = lax.reduce_precision(rest, exponent_bits=8, mantissa_bits=7)
    low = rest - mid
    weight_rows = jnp.stack([hi, mid, low], axis=2).astype(jnp.bfloat16)[:, :, None]
    weight_rows = jnp.broadcast_to(weight_rows, (panels, users, local_slots, 3, blk))
    offset_rows = jnp.broadcast_to(
        slot_offset.astype(jnp.bfloat16)[..., None, None], (panels, users, local_slots, 1, blk)
    )
    pad = jnp.zeros((panels, users, local_slots, META - 4, blk), jnp.bfloat16)
    return jnp.concatenate([panel_blocks, weight_rows, offset_rows, pad], axis=3)


def local(panel_blocks, user_weights, slot_offset, *, nrow, ncol):
    panels, _, local_slots, blk, _ = panel_blocks.shape
    r = lax.axis_index("row")
    c = lax.axis_index("col")
    blocks = lax.all_gather(
        with_meta(panel_blocks, user_weights, slot_offset), "col", axis=1, tiled=True
    )
    users = blocks.shape[1]

    src = c // local_slots
    own = lax.dynamic_index_in_dim(blocks, c % local_slots, axis=2, keepdims=False)
    received = [own]
    for k in range(1, nrow):
        perm = [
            ((cc // local_slots) * ncol + cc, ((cc // local_slots + k) % nrow) * ncol + cc)
            for cc in range(ncol)
        ]
        received.append(lax.ppermute(own, ("row", "col"), perm))
    which = (r - src + nrow) % nrow
    column_blocks = received[0]
    for k in range(1, nrow):
        column_blocks = jnp.where(which == k, received[k], column_blocks)

    offs = jnp.concatenate(
        [blocks[:, :, :, blk + 3, 0], column_blocks[:, :, blk + 3, 0][:, :, None]], axis=2
    )
    offs = jnp.clip(offs.astype(jnp.int32), 0, IBS - 1).reshape(-1)

    n = panels * users
    return gram_call(
        offs,
        blocks.reshape(n, local_slots, blk + META, blk),
        column_blocks.reshape(n, blk + META, blk),
    )


def solution(mesh):
    nrow, ncol = mesh.shape["row"], mesh.shape["col"]
    return jax.shard_map(
        functools.partial(local, nrow=nrow, ncol=ncol),
        mesh=mesh,
        in_specs=(P(None, "col", "row", None, None), P(None, "col", None), P(None, "col", "row")),
        out_specs=P("row", "col"),
        check_vma=False,
    )
```

time: 243 us -> 232 us (0.955)
  blocking collectives: 94.1 us -> 0 us
  waiting for transfers between devices: 105 us -> 170 us
  local copies, waits for them, and re-layouts: 2.69 us -> 14.5 us
  other arithmetic: 2.49 us -> 6.34 us
    all_gather x3 -> x0, blocking collectives: 94.1 us -> none  [the longest x1 33.8 us: local(): weights = lax.all_gather(user_weights, 'col', axis=1, tiled=True)]
    ppermute x3, waiting for transfers between devices: 0.01 us -> 58.7 us  [local(): received.append(lax.ppermute(own, ('row', 'col'), perm))]
    all_gather x1, waiting for transfers between devices: 104 us -> 112 us  [local(): lax.all_gather(with_meta(panel_blocks, user_weights, slot_offset), 'col',...]
    all_gather x3 -> x1, local copies, waits for them, and re-layouts: 0.18 us -> 7.28 us  [local(): lax.all_gather(with_meta(panel_blocks, user_weights, slot_offset), 'col',...]
    slice x0 -> x3, local copies, waits for them, and re-layouts: none -> 3.08 us  [the longest x2 2.75 us: local(): blocks[:, :, :, blk + 3, 0]]
  transfers between devices with their start and end apart: 4 -> 4, of which waited for: 1 -> 3; matrix products, arithmetic and copies ran while one was open for 0% -> 4% of each run, Pallas kernels for 0% -> 0%
where the time goes in v2:
time: 232 us; the launch traced here: 230 us
  waiting for transfers between devices  170 us (73%)
  Pallas kernels  14.6 us (6%)
  local copies, waits for them, and re-layouts  14.5 us (6%)
  between operations  13.4 us (6%)
  starting transfers between devices  10.6 us (5%)
  other arithmetic  6.34 us (3%)
    all_gather x1, waiting for transfers between devices, local(): lax.all_gather(with_meta(panel_blocks, user_weights, slot_offset), 'col',...  112 us
    ppermute x3, waiting for transfers between devices, local(): received.append(lax.ppermute(own, ('row', 'col'), perm))  58.7 us
    pallas_call x1, Pallas kernels, gram_call(): pl.pallas_call(kernel, grid_spec=pltpu.PrefetchScalarGridSpec(num_scalar_...  14.6 us
    ppermute x3, starting transfers between devices, local(): received.append(lax.ppermute(own, ('row', 'col'), perm))  10.6 us
    all_gather x1, local copies, waits for them, and re-layouts, local(): lax.all_gather(with_meta(panel_blocks, user_weights, slot_offset), 'col',...  7.28 us
  transfers between devices with their start and end apart: 4, of which 3 were waited for; matrix products, arithmetic and copies ran while one was open for 4% of the time, Pallas kernels for 0%

profile of v2, /device:TPU:0, one launch (start us, length us, event | category | flops | bytes accessed | tf_op | source)
XLA Modules:
  0.0 229.8 jit_solution(2699374234609279891)
XLA Ops:
  6.5 0.0 all-gather.2.cloned.1.call-start
  6.5 0.7 fusion.2
  7.3 0.7 convert_element_type.13
  8.0 0.1 pad.5.clone
  8.1 0.1 broadcast_in_dim.7
  8.2 2.3 %maximum_maximum_fusion = bf16[3,4,2,144,128]{4,3,1,0,2:T(8,128)(2,1)} fusion(bf16[3,4,2,1,128]{4,3,1,0,2:T(2,128)(2,1)S(1)} %broadcast_in_dim.7, bf16[3,4,2,3,128]{4,3,1,0,2:T(4,128)(2,1)S(1)} %broadcast_in_dim.6, bf16[144]{0:T(256)(128)(2,1)S(1)} %pad.5.clone, bf16[3,4,2,128,128]{4,3,2,1,0:T(8,128)(2,1)} %param.3), kind=kLoop, calls=%fused_computation.2 | loop fusion | flops 3538944 | bytes 1696032 | tf_op jit(solution)/shard_map/concatenate | solution.py:81
  10.5 0.0 all-gather.2.cloned.1.call-update
  10.5 111.6 %all-gather.2.cloned.1.call-done = bf16[3,32,2,144,128]{4,3,1,0,2:T(8,128)(2,1)} async-done(((bf16[3,4,2,144,128]{4,3,1,0,2:T(8,128)(2,1)}), bf16[3,32,2,144,128]{4,3,1,0,2:T(8,128)(2,1)}) %all-gather.2.cloned.1.call-update) | async-done | bytes 7077904 | tf_op jit(solution)/shard_map/all_gather | solution.py:88
  122.1 2.2 dynamic-slice_bitcast_fusion
  124.4 4.1 %collective-permute-start = (bf16[3,32,144,128]{3,2,1,0:T(8,128)(2,1)S(1)}, bf16[3,32,144,128]{3,2,1,0:T(8,128)(2,1)}, u32[]{:S(2)}, u32[]{:S(2)}) collective-permute-start(bf16[3,32,144,128]{3,2,1,0:T(8,128)(2,1)S(1)} %dynamic-slice_bitcast_fusion), channel_id=1, source_target_pairs={{0,24},{1,25},{10,2},{11,3},{20,12},{21,13},{30,22},{31,23}} | collective-permute-start | bytes 10616840 | tf_op jit(solution)/shard_map/ppermute | solution.py:101
  128.5 3.4 %collective-permute-start.1 = (bf16[3,32,144,128]{3,2,1,0:T(8,128)(2,1)S(1)}, bf16[3,32,144,128]{3,2,1,0:T(8,128)(2,1)}, u32[]{:S(2)}, u32[]{:S(2)}) collective-permute-start(bf16[3,32,144,128]{3,2,1,0:T(8,128)(2,1)S(1)} %dynamic-slice_bitcast_fusion), channel_id=1, source_target_pairs={{0,16},{1,17},{10,26},{11,27},{20,4},{21,5},{30,14},{31,15}} | collective-permute-start | bytes 10616840 | tf_op jit(solution)/shard_map/ppermute | solution.py:101
  131.9 3.0 %collective-permute-start.2 = (bf16[3,32,144,128]{3,2,1,0:T(8,128)(2,1)S(1)}, bf16[3,32,144,128]{3,2,1,0:T(8,128)(2,1)}, u32[]{:S(2)}, u32[]{:S(2)}) collective-permute-start(bf16[3,32,144,128]{3,2,1,0:T(8,128)(2,1)S(1)} %dynamic-slice_bitcast_fusion), channel_id=1, source_target_pairs={{0,8},{1,9},{10,18},{11,19},{20,28},{21,29},{30,6},{31,7}} | collective-permute-start | bytes 10616840 | tf_op jit(solution)/shard_map/ppermute | solution.py:101
  134.9 1.7 slice.8
  136.7 1.0 copy.18
  137.7 7.3 %copy.21 = bf16[3,32,2,144,128]{4,3,2,1,0:T(8,128)(2,1)} copy(bf16[3,32,2,144,128]{4,3,1,0,2:T(8,128)(2,1)} %all-gather.2.cloned.1.call-done) | data formatting | bytes 14155776 | tf_op jit(solution)/shard_map/all_gather | solution.py:88
  145.0 20.8 %collective-permute-done = bf16[3,32,144,128]{3,2,1,0:T(8,128)(2,1)} collective-permute-done((bf16[3,32,144,128]{3,2,1,0:T(8,128)(2,1)S(1)}, bf16[3,32,144,128]{3,2,1,0:T(8,128)(2,1)}, u32[]{:S(2)}, u32[]{:S(2)}) %collective-permute-start) | collective-permute-done | bytes 3538976 | tf_op jit(solution)/shard_map/ppermute | solution.py:101
  165.8 37.9 %collective-permute-done.1 = bf16[3,32,144,128]{3,2,1,0:T(8,128)(2,1)} collective-permute-done((bf16[3,32,144,128]{3,2,1,0:T(8,128)(2,1)S(1)}, bf16[3,32,144,128]{3,2,1,0:T(8,128)(2,1)}, u32[]{:S(2)}, u32[]{:S(2)}) %collective-permute-start.1) | collective-permute-done | bytes 3538976 | tf_op jit(solution)/shard_map/ppermute | solution.py:101
  203.7 0.0 collective-permute-done.2
  203.7 2.6 %select_select_fusion = bf16[3,32,144,128]{3,2,1,0:T(8,128)(2,1)S(1)} fusion(bf16[3,32,144,128]{3,2,1,0:T(8,128)(2,1)} %collective-permute-done, bf16[3,32,144,128]{3,2,1,0:T(8,128)(2,1)} %collective-permute-done.1, bf16[3,32,144,128]{3,2,1,0:T(8,128)(2,1)} %collective-permute-done.2, pred[]{:T(512)S(6)} %eq.14, pred[]{:T(512)S(6)} %eq.13, pred[]{:T(512)S(6)} %eq.12, ...), kind=kLoop, calls=%fused_computation | loop fusion | flops 5308416 | bytes 17694728 | tf_op jit(solution)/shard_map/jit(_where)/select_n | solution.py:105
  206.3 0.3 slice_reduce_fusion
  206.7 0.7 copy.20
  207.4 1.0 min.12.offs_ref
  208.4 14.6 %shard_map.37 = f32[2048,1024]{1,0:T(8,128)} custom-call(s32[288]{0:T(512)S(1)} %min.12.offs_ref, bf16[96,2,144,128]{3,2,1,0:T(8,128)(2,1)} %bitcast.14, bf16[96,144,128]{2,1,0:T(8,128)(2,1)S(1)} %bitcast.13), custom_call_target="tpu_custom_call" | custom-call | flops 805306368 | bytes 17825792 | tf_op jit(solution)/shard_map/pallas_call | solution.py:46
  (7 shorter events, 0.1 us)
Async XLA Ops:
  6.5 115.6 %all-gather.2.cloned.1.call-start = ((), (), s32[]{:S(2)}) async-start(), calls=%async_computation | async-start | bytes 7962624 | tf_op jit(solution)/shard_map/all_gather | solution.py:88
  124.4 41.4 %collective-permute-start = (bf16[3,32,144,128]{3,2,1,0:T(8,128)(2,1)S(1)}, bf16[3,32,144,128]{3,2,1,0:T(8,128)(2,1)}, u32[]{:S(2)}, u32[]{:S(2)}) collective-permute-start(bf16[3,32,144,128]{3,2,1,0:T(8,128)(2,1)S(1)} %dynamic-slice_bitcast_fusion), channel_id=1, source_target_pairs={{0,24},{1,25},{10,2},{11,3},{20,12},{21,13},{30,22},{31,23}} | collective-permute-start | bytes 10616840 | tf_op jit(solution)/shard_map/ppermute | solution.py:101
  128.5 75.2 %collective-permute-start.1 = (bf16[3,32,144,128]{3,2,1,0:T(8,128)(2,1)S(1)}, bf16[3,32,144,128]{3,2,1,0:T(8,128)(2,1)}, u32[]{:S(2)}, u32[]{:S(2)}) collective-permute-start(bf16[3,32,144,128]{3,2,1,0:T(8,128)(2,1)S(1)} %dynamic-slice_bitcast_fusion), channel_id=1, source_target_pairs={{0,16},{1,17},{10,26},{11,27},{20,4},{21,5},{30,14},{31,15}} | collective-permute-start | bytes 10616840 | tf_op jit(solution)/shard_map/ppermute | solution.py:101
  131.9 71.8 %collective-permute-start.2 = (bf16[3,32,144,128]{3,2,1,0:T(8,128)(2,1)S(1)}, bf16[3,32,144,128]{3,2,1,0:T(8,128)(2,1)}, u32[]{:S(2)}, u32[]{:S(2)}) collective-permute-start(bf16[3,32,144,128]{3,2,1,0:T(8,128)(2,1)S(1)} %dynamic-slice_bitcast_fusion), channel_id=1, source_target_pairs={{0,8},{1,9},{10,18},{11,19},{20,28},{21,29},{30,6},{31,7}} | collective-permute-start | bytes 10616840 | tf_op jit(solution)/shard_map/ppermute | solution.py:101
Sparse Core Ops, SparseCore 0:
  10.6 111.4 all-gather.1

commit v3 on v2

--- a/solution.py
+++ b/solution.py
@@ -12,12 +12,16 @@
 META = 16
 
 
-def gram_kernel(offs_ref, bs_ref, bc_ref, o_ref, *, chunk, local_slots, blk):
+def gram_kernel(offs_ref, bs_ref, bc_ref, *refs, chunk, local_slots, blk):
+    o_ref = refs[-1]
     step = pl.program_id(0)
 
     @pl.when(step == 0)
     def _():
-        o_ref[...] = jnp.zeros_like(o_ref)
+        if len(refs) == 2:
+            o_ref[...] = refs[0][...]
+        else:
+            o_ref[...] = jnp.zeros_like(o_ref)
 
     stride = local_slots + 1
     for k in range(chunk):
@@ -38,11 +42,13 @@
             o_ref[pl.ds(row, blk), pl.ds(col, blk)] += prod[s * blk : (s + 1) * blk]
 
 
-def gram_call(offs, bs, bc):
+def gram_call(offs, bs, bc, acc=None):
     n, local_slots, rows, blk = bs.shape
     chunk = CHUNK
     kernel = functools.partial(gram_kernel, chunk=chunk, local_slots=local_slots, blk=blk)
     out_rows, out_cols = local_slots * IBS * blk, IBS * blk
+    acc_specs = [] if acc is None else [pl.BlockSpec((out_rows, out_cols), lambda i, o: (0, 0))]
+    acc_args = () if acc is None else (acc,)
     return pl.pallas_call(
         kernel,
         grid_spec=pltpu.PrefetchScalarGridSpec(
@@ -51,19 +57,21 @@
             in_specs=[
                 pl.BlockSpec((chunk, local_slots, rows, blk), lambda i, o: (i, 0, 0, 0)),
                 pl.BlockSpec((chunk, rows, blk), lambda i, o: (i, 0, 0)),
-            ],
+            ]
+            + acc_specs,
             out_specs=pl.BlockSpec((out_rows, out_cols), lambda i, o: (0, 0)),
         ),
         out_shape=jax.ShapeDtypeStruct((out_rows, out_cols), jnp.float32),
+        input_output_aliases={} if acc is None else {3: 0},
         compiler_params=pltpu.CompilerParams(
-            dimension_semantics=("arbitrary",), vmem_limit_bytes=48 * 1024 * 1024
+            dimension_semantics=("arbitrary",), vmem_limit_bytes=56 * 1024 * 1024
         ),
         cost_estimate=pl.CostEstimate(
             flops=2 * n * local_slots * blk * blk * blk,
             transcendentals=0,
             bytes_accessed=n * (local_slots + 1) * blk * blk * 2 + out_rows * out_cols * 4,
         ),
-    )(offs, bs, bc)
+    )(offs, bs, bc, *acc_args)
 
 
 def with_meta(panel_blocks, user_weights, slot_offset):
@@ -85,36 +93,29 @@
     panels, _, local_slots, blk, _ = panel_blocks.shape
     r = lax.axis_index("row")
     c = lax.axis_index("col")
-    blocks = lax.all_gather(
-        with_meta(panel_blocks, user_weights, slot_offset), "col", axis=1, tiled=True
-    )
-    users = blocks.shape[1]
-
+    extended = with_meta(panel_blocks, user_weights, slot_offset)
     src = c // local_slots
-    own = lax.dynamic_index_in_dim(blocks, c % local_slots, axis=2, keepdims=False)
-    received = [own]
-    for k in range(1, nrow):
-        perm = [
-            ((cc // local_slots) * ncol + cc, ((cc // local_slots + k) % nrow) * ncol + cc)
-            for cc in range(ncol)
-        ]
-        received.append(lax.ppermute(own, ("row", "col"), perm))
     which = (r - src + nrow) % nrow
-    column_blocks = received[0]
-    for k in range(1, nrow):
-        column_blocks = jnp.where(which == k, received[k], column_blocks)
-
-    offs = jnp.concatenate(
-        [blocks[:, :, :, blk + 3, 0], column_blocks[:, :, blk + 3, 0][:, :, None]], axis=2
-    )
-    offs = jnp.clip(offs.astype(jnp.int32), 0, IBS - 1).reshape(-1)
-
-    n = panels * users
-    return gram_call(
-        offs,
-        blocks.reshape(n, local_slots, blk + META, blk),
-        column_blocks.reshape(n, blk + META, blk),
-    )
+    acc = None
+    for p in range(panels):
+        blocks = lax.all_gather(extended[p], "col", axis=0, tiled=True)
+        users = blocks.shape[0]
+        own = lax.dynamic_index_in_dim(blocks, c % local_slots, axis=1, keepdims=False)
+        column_blocks = own
+        for k in range(1, nrow):
+            perm = [
+                ((cc // local_slots) * ncol + cc, ((cc // local_slots + k) % nrow) * ncol + cc)
+                for cc in range(ncol)
+            ]
+            column_blocks = jnp.where(
+                which == k, lax.ppermute(own, ("row", "col"), perm), column_blocks
+            )
+        offs = jnp.concatenate(
+            [blocks[:, :, blk + 3, 0], column_blocks[:, blk + 3, 0][:, None]], axis=1
+        )
+        offs = jnp.clip(offs.astype(jnp.int32), 0, IBS - 1).reshape(-1)
+        acc = gram_call(offs, blocks, column_blocks, acc)
+    return acc
 
 
 def solution(mesh):

time: 232 us -> 239 us (1.030)
  waiting for transfers between devices: 170 us -> 141 us
  Pallas kernels: 14.6 us -> 30.6 us
  starting transfers between devices: 10.6 us -> 25.4 us
  local copies, waits for them, and re-layouts: 14.5 us -> 19.9 us
    ppermute x3 -> x9, waiting for transfers between devices: 58.7 us -> 6.28 us  [local(): lax.ppermute(own, ('row', 'col'), perm)]
    all_gather x1 -> x3, waiting for transfers between devices: 112 us -> 134 us  [local(): blocks = lax.all_gather(extended[p], 'col', axis=0, tiled=True)]
    pallas_call x1 -> x3, Pallas kernels: 14.6 us -> 30.6 us  [gram_call(): pl.pallas_call(kernel, grid_spec=pltpu.PrefetchScalarGridSpec(num_scalar_...]
    ppermute x3 -> x9, starting transfers between devices: 10.6 us -> 25.3 us  [local(): lax.ppermute(own, ('row', 'col'), perm)]
    all_gather x1 -> x0, local copies, waits for them, and re-layouts: 7.28 us -> none  [local(): lax.all_gather(with_meta(panel_blocks, user_weights, slot_offset), 'col',...]
    slice x3 -> x10, local copies, waits for them, and re-layouts: 3.08 us -> 9.27 us  [the longest x6 7.37 us: local(): blocks[:, :, blk + 3, 0]]
    squeeze x1 -> x3, local copies, waits for them, and re-layouts: 2.23 us -> 6.37 us  [local(): lax.dynamic_index_in_dim(blocks, c % local_slots, axis=1, keepdims=False)]
  transfers between devices with their start and end apart: 4 -> 12, of which waited for: 3 -> 4; matrix products, arithmetic and copies ran while one was open for 4% -> 8% of each run, Pallas kernels for 0% -> 4%
where the time goes in v3:
time: 239 us; the launch traced here: 235 us
  waiting for transfers between devices  141 us (59%)
  Pallas kernels  30.6 us (13%)
  starting transfers between devices  25.4 us (11%)
  local copies, waits for them, and re-layouts  19.9 us (8%)
  between operations  13.2 us (6%)
  other arithmetic  4.17 us (2%)
    all_gather x3, waiting for transfers between devices, local(): blocks = lax.all_gather(extended[p], 'col', axis=0, tiled=True)  134 us
    pallas_call x3, Pallas kernels, gram_call(): pl.pallas_call(kernel, grid_spec=pltpu.PrefetchScalarGridSpec(num_scalar_...  30.6 us
    ppermute x9, starting transfers between devices, local(): lax.ppermute(own, ('row', 'col'), perm)  25.3 us
    slice x6, local copies, waits for them, and re-layouts, local(): blocks[:, :, blk + 3, 0]  7.37 us
    squeeze x3, local copies, waits for them, and re-layouts, local(): lax.dynamic_index_in_dim(blocks, c % local_slots, axis=1, keepdims=False)  6.37 us
    ppermute x9, waiting for transfers between devices, local(): lax.ppermute(own, ('row', 'col'), perm)  6.28 us
  transfers between devices with their start and end apart: 12, of which 4 were waited for; matrix products, arithmetic and copies ran while one was open for 8% of the time, Pallas kernels for 4%

profile of v3, /device:TPU:0, one launch (start us, length us, event | category | flops | bytes accessed | tf_op | source)
XLA Modules:
  0.0 234.8 jit_solution(3736957437798819029)
XLA Ops:
  6.5 0.7 fusion.2
  7.3 0.7 convert_element_type.23
  8.3 1.4 maximum_maximum_fusion
  9.7 0.9 fusion.4
  10.7 0.7 all-gather.9.cloned.1.call-update
  11.4 0.7 all-gather.7.cloned.1.call-update
  12.1 53.4 %all-gather.11.cloned.1.call-done = bf16[1,32,2,144,128]{4,3,2,0,1:T(8,128)(2,1)} async-done(((bf16[1,4,2,144,128]{4,3,2,0,1:T(8,128)(2,1)}), bf16[1,32,2,144,128]{4,3,2,0,1:T(8,128)(2,1)}) %all-gather.11.cloned.1.call-update) | async-done | bytes 2359312 | tf_op jit(solution)/shard_map/all_gather | solution.py:101
  65.6 2.4 %dynamic-slice_bitcast_fusion = bf16[32,144,128]{2,1,0:T(8,128)(2,1)} fusion(bf16[1,32,2,144,128]{4,3,2,0,1:T(8,128)(2,1)} %all-gather.11.cloned.1.call-done, s32[]{:T(128)S(6)} %select_n.73), kind=kLoop, calls=%fused_computation | loop fusion | bytes 2359300 | tf_op jit(solution)/shard_map/jit(dynamic_index_in_dim)/squeeze | solution.py:103
  67.9 2.6 %collective-permute-start.6 = (bf16[32,144,128]{2,1,0:T(8,128)(2,1)}, bf16[32,144,128]{2,1,0:T(8,128)(2,1)}, u32[]{:S(2)}, u32[]{:S(2)}) collective-permute-start(bf16[32,144,128]{2,1,0:T(8,128)(2,1)} %dynamic-slice_bitcast_fusion), channel_id=1, source_target_pairs={{0,24},{1,25},{10,2},{11,3},{20,12},{21,13},{30,22},{31,23}} | collective-permute-start | bytes 3538952 | tf_op jit(solution)/shard_map/ppermute | solution.py:111
  70.6 3.5 %collective-permute-start.7 = (bf16[32,144,128]{2,1,0:T(8,128)(2,1)}, bf16[32,144,128]{2,1,0:T(8,128)(2,1)}, u32[]{:S(2)}, u32[]{:S(2)}) collective-permute-start(bf16[32,144,128]{2,1,0:T(8,128)(2,1)} %dynamic-slice_bitcast_fusion), channel_id=1, source_target_pairs={{0,16},{1,17},{10,26},{11,27},{20,4},{21,5},{30,14},{31,15}} | collective-permute-start | bytes 3538952 | tf_op jit(solution)/shard_map/ppermute | solution.py:111
  74.0 2.3 collective-permute-start.8
  76.3 42.1 %all-gather.9.cloned.1.call-done = bf16[1,32,2,144,128]{4,3,2,0,1:T(8,128)(2,1)} async-done(((bf16[1,4,2,144,128]{4,3,2,0,1:T(8,128)(2,1)}), bf16[1,32,2,144,128]{4,3,2,0,1:T(8,128)(2,1)}) %all-gather.9.cloned.1.call-update) | async-done | bytes 2359312 | tf_op jit(solution)/shard_map/all_gather | solution.py:101
  118.4 1.5 dynamic-slice_bitcast_fusion.1
  119.9 2.7 %collective-permute-start.3 = (bf16[32,144,128]{2,1,0:T(8,128)(2,1)S(1)}, bf16[32,144,128]{2,1,0:T(8,128)(2,1)}, u32[]{:S(2)}, u32[]{:S(2)}) collective-permute-start(bf16[32,144,128]{2,1,0:T(8,128)(2,1)S(1)} %dynamic-slice_bitcast_fusion.1), channel_id=1, source_target_pairs={{0,24},{1,25},{10,2},{11,3},{20,12},{21,13},{30,22},{31,23}} | collective-permute-start | bytes 3538952 | tf_op jit(solution)/shard_map/ppermute | solution.py:111
  122.6 3.5 %collective-permute-start.4 = (bf16[32,144,128]{2,1,0:T(8,128)(2,1)S(1)}, bf16[32,144,128]{2,1,0:T(8,128)(2,1)}, u32[]{:S(2)}, u32[]{:S(2)}) collective-permute-start(bf16[32,144,128]{2,1,0:T(8,128)(2,1)S(1)} %dynamic-slice_bitcast_fusion.1), channel_id=1, source_target_pairs={{0,16},{1,17},{10,26},{11,27},{20,4},{21,5},{30,14},{31,15}} | collective-permute-start | bytes 3538952 | tf_op jit(solution)/shard_map/ppermute | solution.py:111
  126.1 2.3 collective-permute-start.5
  128.4 1.5 slice.43
  130.0 0.9 copy.29
  131.5 1.4 copy.27
  132.9 38.3 %all-gather.7.cloned.1.call-done = bf16[1,32,2,144,128]{4,3,2,0,1:T(8,128)(2,1)} async-done(((bf16[1,4,2,144,128]{4,3,2,0,1:T(8,128)(2,1)}), bf16[1,32,2,144,128]{4,3,2,0,1:T(8,128)(2,1)}) %all-gather.7.cloned.1.call-update) | async-done | bytes 2359312 | tf_op jit(solution)/shard_map/all_gather | solution.py:101
  171.2 1.5 slice.37
  172.8 1.4 copy.25
  174.1 2.5 %dynamic-slice_bitcast_fusion.2 = bf16[32,144,128]{2,1,0:T(8,128)(2,1)} fusion(bf16[1,32,2,144,128]{4,3,2,0,1:T(8,128)(2,1)} %all-gather.7.cloned.1.call-done, s32[]{:T(128)S(6)} %select_n.73), kind=kLoop, calls=%fused_computation.2 | loop fusion | bytes 2359300 | tf_op jit(solution)/shard_map/jit(dynamic_index_in_dim)/squeeze | solution.py:103
  176.6 2.6 %collective-permute-start = (bf16[32,144,128]{2,1,0:T(8,128)(2,1)}, bf16[32,144,128]{2,1,0:T(8,128)(2,1)}, u32[]{:S(2)}, u32[]{:S(2)}) collective-permute-start(bf16[32,144,128]{2,1,0:T(8,128)(2,1)} %dynamic-slice_bitcast_fusion.2), channel_id=1, source_target_pairs={{0,24},{1,25},{10,2},{11,3},{20,12},{21,13},{30,22},{31,23}} | collective-permute-start | bytes 3538952 | tf_op jit(solution)/shard_map/ppermute | solution.py:111
  179.3 3.4 %collective-permute-start.1 = (bf16[32,144,128]{2,1,0:T(8,128)(2,1)}, bf16[32,144,128]{2,1,0:T(8,128)(2,1)}, u32[]{:S(2)}, u32[]{:S(2)}) collective-permute-start(bf16[32,144,128]{2,1,0:T(8,128)(2,1)} %dynamic-slice_bitcast_fusion.2), channel_id=1, source_target_pairs={{0,16},{1,17},{10,26},{11,27},{20,4},{21,5},{30,14},{31,15}} | collective-permute-start | bytes 3538952 | tf_op jit(solution)/shard_map/ppermute | solution.py:111
  182.7 2.3 collective-permute-start.2
  185.3 1.0 copy-done.4
  187.3 0.8 copy.30
  190.0 8.6 %shard_map.37.refs_0_ = f32[2048,1024]{1,0:T(8,128)} custom-call(s32[96]{0:T(128)} %min.28.offs_ref, bf16[32,2,144,128]{3,2,1,0:T(8,128)(2,1)} %bitcast.32, bf16[32,144,128]{2,1,0:T(8,128)(2,1)} %copy-done.4), custom_call_target="tpu_custom_call" | custom-call | flops 268435456 | bytes 11534336 | tf_op jit(solution)/shard_map/pallas_call | solution.py:52
  198.6 6.3 %collective-permute-done.1 = bf16[32,144,128]{2,1,0:T(8,128)(2,1)} collective-permute-done((bf16[32,144,128]{2,1,0:T(8,128)(2,1)}, bf16[32,144,128]{2,1,0:T(8,128)(2,1)}, u32[]{:S(2)}, u32[]{:S(2)}) %collective-permute-start.1) | collective-permute-done | bytes 1179680 | tf_op jit(solution)/shard_map/ppermute | solution.py:111
  206.2 11.0 %shard_map.38.refs_0_ = f32[2048,1024]{1,0:T(8,128)} custom-call(s32[96]{0:T(128)} %min.26.offs_ref, bf16[32,2,144,128]{3,2,1,0:T(8,128)(2,1)} %bitcast.27, bf16[32,144,128]{2,1,0:T(8,128)(2,1)} %copy-done.3, f32[2048,1024]{1,0:T(8,128)} %shard_map.37.refs_0_), custom_call_target="tpu_custom_call", output_to_operand_aliasing={{}: (3, {})} | custom-call | flops 268435456 | bytes 11534336 | tf_op jit(solution)/shard_map/pallas_call | solution.py:52
  217.2 11.0 %shard_map.39 = f32[2048,1024]{1,0:T(8,128)} custom-call(s32[96]{0:T(128)} %min.24.offs_ref, bf16[32,2,144,128]{3,2,1,0:T(8,128)(2,1)} %bitcast.30, bf16[32,144,128]{2,1,0:T(8,128)(2,1)} %copy-done.5, f32[2048,1024]{1,0:T(8,128)} %shard_map.38.refs_0_), custom_call_target="tpu_custom_call", output_to_operand_aliasing={{}: (3, {})} | custom-call | flops 268435456 | bytes 11534336 | tf_op jit(solution)/shard_map/pallas_call | solution.py:52
  (49 shorter events, 5.6 us)
Async XLA Ops:
  6.5 59.0 %all-gather.11.cloned.1.call-start = ((), (), s32[]{:S(2)}) async-start(), calls=%async_computation.2 | async-start | bytes 2654208 | tf_op jit(solution)/shard_map/all_gather | solution.py:101
  10.6 107.8 %all-gather.9.cloned.1.call-start = ((), (), s32[]{:S(2)}) async-start(), calls=%async_computation.1 | async-start | bytes 2654208 | tf_op jit(solution)/shard_map/all_gather | solution.py:101
  11.4 159.8 %all-gather.7.cloned.1.call-start = ((), (), s32[]{:S(2)}) async-start(), calls=%async_computation | async-start | bytes 2654208 | tf_op jit(solution)/shard_map/all_gather | solution.py:101
  67.9 58.2 %collective-permute-start.6 = (bf16[32,144,128]{2,1,0:T(8,128)(2,1)}, bf16[32,144,128]{2,1,0:T(8,128)(2,1)}, u32[]{:S(2)}, u32[]{:S(2)}) collective-permute-start(bf16[32,144,128]{2,1,0:T(8,128)(2,1)} %dynamic-slice_bitcast_fusion), channel_id=1, source_target_pairs={{0,24},{1,25},{10,2},{11,3},{20,12},{21,13},{30,22},{31,23}} | collective-permute-start | bytes 3538952 | tf_op jit(solution)/shard_map/ppermute | solution.py:111
  70.6 106.1 %collective-permute-start.7 = (bf16[32,144,128]{2,1,0:T(8,128)(2,1)}, bf16[32,144,128]{2,1,0:T(8,128)(2,1)}, u32[]{:S(2)}, u32[]{:S(2)}) collective-permute-start(bf16[32,144,128]{2,1,0:T(8,128)(2,1)} %dynamic-slice_bitcast_fusion), channel_id=1, source_target_pairs={{0,16},{1,17},{10,26},{11,27},{20,4},{21,5},{30,14},{31,15}} | collective-permute-start | bytes 3538952 | tf_op jit(solution)/shard_map/ppermute | solution.py:111
  74.0 105.2 %collective-permute-start.8 = (bf16[32,144,128]{2,1,0:T(8,128)(2,1)}, bf16[32,144,128]{2,1,0:T(8,128)(2,1)}, u32[]{:S(2)}, u32[]{:S(2)}) collective-permute-start(bf16[32,144,128]{2,1,0:T(8,128)(2,1)} %dynamic-slice_bitcast_fusion), channel_id=1, source_target_pairs={{0,8},{1,9},{10,18},{11,19},{20,28},{21,29},{30,6},{31,7}} | collective-permute-start | bytes 3538952 | tf_op jit(solution)/shard_map/ppermute | solution.py:111
  118.4 12.4 %copy-start = (bf16[1,32,2,144,128]{4,3,2,0,1:T(8,128)(2,1)S(1)}, bf16[1,32,2,144,128]{4,3,2,0,1:T(8,128)(2,1)}, u32[]{:S(2)}) copy-start(bf16[1,32,2,144,128]{4,3,2,0,1:T(8,128)(2,1)} %all-gather.9.cloned.1.call-done) | copy-start | bytes 7077892
  119.9 62.8 %collective-permute-start.3 = (bf16[32,144,128]{2,1,0:T(8,128)(2,1)S(1)}, bf16[32,144,128]{2,1,0:T(8,128)(2,1)}, u32[]{:S(2)}, u32[]{:S(2)}) collective-permute-start(bf16[32,144,128]{2,1,0:T(8,128)(2,1)S(1)} %dynamic-slice_bitcast_fusion.1), channel_id=1, source_target_pairs={{0,24},{1,25},{10,2},{11,3},{20,12},{21,13},{30,22},{31,23}} | collective-permute-start | bytes 3538952 | tf_op jit(solution)/shard_map/ppermute | solution.py:111
  122.6 66.1 %collective-permute-start.4 = (bf16[32,144,128]{2,1,0:T(8,128)(2,1)S(1)}, bf16[32,144,128]{2,1,0:T(8,128)(2,1)}, u32[]{:S(2)}, u32[]{:S(2)}) collective-permute-start(bf16[32,144,128]{2,1,0:T(8,128)(2,1)S(1)} %dynamic-slice_bitcast_fusion.1), channel_id=1, source_target_pairs={{0,16},{1,17},{10,26},{11,27},{20,4},{21,5},{30,14},{31,15}} | collective-permute-start | bytes 3538952 | tf_op jit(solution)/shard_map/ppermute | solution.py:111
  126.1 62.6 %collective-permute-start.5 = (bf16[32,144,128]{2,1,0:T(8,128)(2,1)S(1)}, bf16[32,144,128]{2,1,0:T(8,128)(2,1)}, u32[]{:S(2)}, u32[]{:S(2)}) collective-permute-start(bf16[32,144,128]{2,1,0:T(8,128)(2,1)S(1)} %dynamic-slice_bitcast_fusion.1), channel_id=1, source_target_pairs={{0,8},{1,9},{10,18},{11,19},{20,28},{21,29},{30,6},{31,7}} | collective-permute-start | bytes 3538952 | tf_op jit(solution)/shard_map/ppermute | solution.py:111
  174.1 10.9 %copy-start.2 = (bf16[1,32,2,144,128]{4,3,2,0,1:T(8,128)(2,1)S(1)}, bf16[1,32,2,144,128]{4,3,2,0,1:T(8,128)(2,1)}, u32[]{:S(2)}) copy-start(bf16[1,32,2,144,128]{4,3,2,0,1:T(8,128)(2,1)} %all-gather.11.cloned.1.call-done) | copy-start | bytes 7077892
  176.6 22.0 %collective-permute-start = (bf16[32,144,128]{2,1,0:T(8,128)(2,1)}, bf16[32,144,128]{2,1,0:T(8,128)(2,1)}, u32[]{:S(2)}, u32[]{:S(2)}) collective-permute-start(bf16[32,144,128]{2,1,0:T(8,128)(2,1)} %dynamic-slice_bitcast_fusion.2), channel_id=1, source_target_pairs={{0,24},{1,25},{10,2},{11,3},{20,12},{21,13},{30,22},{31,23}} | collective-permute-start | bytes 3538952 | tf_op jit(solution)/shard_map/ppermute | solution.py:111
  179.3 25.6 %collective-permute-start.1 = (bf16[32,144,128]{2,1,0:T(8,128)(2,1)}, bf16[32,144,128]{2,1,0:T(8,128)(2,1)}, u32[]{:S(2)}, u32[]{:S(2)}) collective-permute-start(bf16[32,144,128]{2,1,0:T(8,128)(2,1)} %dynamic-slice_bitcast_fusion.2), channel_id=1, source_target_pairs={{0,16},{1,17},{10,26},{11,27},{20,4},{21,5},{30,14},{31,15}} | collective-permute-start | bytes 3538952 | tf_op jit(solution)/shard_map/ppermute | solution.py:111
  182.7 22.2 %collective-permute-start.2 = (bf16[32,144,128]{2,1,0:T(8,128)(2,1)}, bf16[32,144,128]{2,1,0:T(8,128)(2,1)}, u32[]{:S(2)}, u32[]{:S(2)}) collective-permute-start(bf16[32,144,128]{2,1,0:T(8,128)(2,1)} %dynamic-slice_bitcast_fusion.2), channel_id=1, source_target_pairs={{0,8},{1,9},{10,18},{11,19},{20,28},{21,29},{30,6},{31,7}} | collective-permute-start | bytes 3538952 | tf_op jit(solution)/shard_map/ppermute | solution.py:111
  185.3 1.0 copy-start.4
  188.6 0.7 copy-start.7
  188.9 9.7 %copy-start.3 = (bf16[32,144,128]{2,1,0:T(8,128)(2,1)}, bf16[32,144,128]{2,1,0:T(8,128)(2,1)S(1)}, u32[]{:S(2)}) copy-start(bf16[32,144,128]{2,1,0:T(8,128)(2,1)S(1)} %select_select_fusion.1.bc_ref) | copy-start | bytes 3538948
  190.0 14.9 %copy-start.1 = (bf16[1,32,2,144,128]{4,3,2,0,1:T(8,128)(2,1)S(1)}, bf16[1,32,2,144,128]{4,3,2,0,1:T(8,128)(2,1)}, u32[]{:S(2)}) copy-start(bf16[1,32,2,144,128]{4,3,2,0,1:T(8,128)(2,1)} %all-gather.7.cloned.1.call-done) | copy-start | bytes 7077892
  198.6 6.8 %copy-start.6 = (bf16[32,2,1,1]{0,1,3,2:T(2,128)(2,1)S(1)}, bf16[32,2,1,1]{0,1,3,2:T(2,128)(2,1)}, u32[]{:S(2)}) copy-start(bf16[32,2,1,1]{0,1,3,2:T(2,128)(2,1)} %copy.25) | copy-start | bytes 388
  205.1 12.1 %copy-start.5 = (bf16[32,144,128]{2,1,0:T(8,128)(2,1)}, bf16[32,144,128]{2,1,0:T(8,128)(2,1)S(1)}, u32[]{:S(2)}) copy-start(bf16[32,144,128]{2,1,0:T(8,128)(2,1)S(1)} %select_select_fusion.2.bc_ref) | copy-start | bytes 3538948
Sparse Core Ops, SparseCore 0:
  10.7 54.7 all-gather.10
  67.7 50.5 all-gather.8
  120.6 50.5 all-gather.6

commit v4 on v2

--- a/solution.py
+++ b/solution.py
@@ -81,6 +81,32 @@
     return jnp.concatenate([panel_blocks, weight_rows, offset_rows, pad], axis=3)
 
 
+def broadcast_slot(own, r, src, nrow, ncol, local_slots):
+    nx = nrow // 2
+    half = own.shape[0] // 2
+    source_of = lambda cc: cc // local_slots
+
+    def send(x, pairs):
+        return lax.ppermute(x, ("row", "col"), [(a * ncol + cc, b * ncol + cc) for cc, a, b in pairs])
+
+    partner = send(own, [(cc, source_of(cc), source_of(cc) ^ 1) for cc in range(ncol)])
+    x_r, x_s = r // 2, src // 2
+    j_r = (x_r - x_s + nx) % nx
+    first, second = own[:half], own[half:]
+    result_first, result_second = first, second
+    for j in range(1, nx):
+        to = lambda cc: 2 * ((source_of(cc) // 2 + j) % nx)
+        a_even = send(first, [(cc, source_of(cc), to(cc)) for cc in range(ncol)])
+        b_odd = send(second, [(cc, source_of(cc), to(cc) + 1) for cc in range(ncol)])
+        a_odd = send(a_even, [(cc, to(cc), to(cc) + 1) for cc in range(ncol)])
+        b_even = send(b_odd, [(cc, to(cc) + 1, to(cc)) for cc in range(ncol)])
+        even = r % 2 == 0
+        result_first = jnp.where(j_r == j, jnp.where(even, a_even, a_odd), result_first)
+        result_second = jnp.where(j_r == j, jnp.where(even, b_even, b_odd), result_second)
+    other = jnp.concatenate([result_first, result_second], axis=0)
+    return jnp.where(j_r == 0, jnp.where(r == src, own, partner), other)
+
+
 def local(panel_blocks, user_weights, slot_offset, *, nrow, ncol):
     panels, _, local_slots, blk, _ = panel_blocks.shape
     r = lax.axis_index("row")
@@ -88,33 +114,16 @@
     blocks = lax.all_gather(
         with_meta(panel_blocks, user_weights, slot_offset), "col", axis=1, tiled=True
     )
-    users = blocks.shape[1]
+    n = panels * blocks.shape[1]
+    blocks = blocks.reshape(n, local_slots, blk + META, blk)
 
     src = c // local_slots
-    own = lax.dynamic_index_in_dim(blocks, c % local_slots, axis=2, keepdims=False)
-    received = [own]
-    for k in range(1, nrow):
-        perm = [
-            ((cc // local_slots) * ncol + cc, ((cc // local_slots + k) % nrow) * ncol + cc)
-            for cc in range(ncol)
-        ]
-        received.append(lax.ppermute(own, ("row", "col"), perm))
-    which = (r - src + nrow) % nrow
-    column_blocks = received[0]
-    for k in range(1, nrow):
-        column_blocks = jnp.where(which == k, received[k], column_blocks)
+    own = lax.dynamic_index_in_dim(blocks, c % local_slots, axis=1, keepdims=False)
+    column_blocks = broadcast_slot(own, r, src, nrow, ncol, local_slots)
 
-    offs = jnp.concatenate(
-        [blocks[:, :, :, blk + 3, 0], column_blocks[:, :, blk + 3, 0][:, :, None]], axis=2
-    )
+    offs = jnp.concatenate([blocks[:, :, blk + 3, 0], column_blocks[:, blk + 3, 0][:, None]], axis=1)
     offs = jnp.clip(offs.astype(jnp.int32), 0, IBS - 1).reshape(-1)
-
-    n = panels * users
-    return gram_call(
-        offs,
-        blocks.reshape(n, local_slots, blk + META, blk),
-        column_blocks.reshape(n, blk + META, blk),
-    )
+    return gram_call(offs, blocks, column_blocks)
 
 
 def solution(mesh):

time: 232 us -> 205 us (0.88)
  waiting for transfers between devices: 170 us -> 140 us
  starting transfers between devices: 10.6 us -> 14 us
    ppermute x3 -> x5, waiting for transfers between devices: 58.7 us -> 28.2 us  [send(): lax.ppermute(x, ('row', 'col'), [(a * ncol + cc, b * ncol + cc) for cc, a...]
    ppermute x3 -> x5, starting transfers between devices: 10.6 us -> 14 us  [send(): lax.ppermute(x, ('row', 'col'), [(a * ncol + cc, b * ncol + cc) for cc, a...]
    all_gather x1, local copies, waits for them, and re-layouts: 7.28 us -> 4.22 us  [local(): lax.all_gather(with_meta(panel_blocks, user_weights, slot_offset), 'col',...]
  transfers between devices with their start and end apart: 4 -> 6, of which waited for: 3 -> 3; matrix products, arithmetic and copies ran while one was open for 4% -> 4% of each run, Pallas kernels for 0% -> 0%
where the time goes in v4:
time: 205 us; the launch traced here: 203 us
  waiting for transfers between devices  140 us (68%)
  Pallas kernels  14.6 us (7%)
  starting transfers between devices  14 us (7%)
  between operations  13.5 us (7%)
  local copies, waits for them, and re-layouts  12.8 us (6%)
  other arithmetic  8.16 us (4%)
    all_gather x1, waiting for transfers between devices, local(): lax.all_gather(with_meta(panel_blocks, user_weights, slot_offset), 'col',...  112 us
    ppermute x5, waiting for transfers between devices, send(): lax.ppermute(x, ('row', 'col'), [(a * ncol + cc, b * ncol + cc) for cc, a...  28.2 us
    pallas_call x1, Pallas kernels, gram_call(): pl.pallas_call(kernel, grid_spec=pltpu.PrefetchScalarGridSpec(num_scalar_...  14.6 us
    ppermute x5, starting transfers between devices, send(): lax.ppermute(x, ('row', 'col'), [(a * ncol + cc, b * ncol + cc) for cc, a...  14 us
    all_gather x1, local copies, waits for them, and re-layouts, local(): lax.all_gather(with_meta(panel_blocks, user_weights, slot_offset), 'col',...  4.22 us
  transfers between devices with their start and end apart: 6, of which 3 were waited for; matrix products, arithmetic and copies ran while one was open for 4% of the time, Pallas kernels for 0%

profile of v4, /device:TPU:0, one launch (start us, length us, event | category | flops | bytes accessed | tf_op | source)
XLA Modules:
  0.0 202.9 jit_solution(5110763543594023804)
XLA Ops:
  6.5 0.7 convert_element_type.13
  7.2 0.1 copy.9
  7.3 0.7 fusion.2
  8.1 0.1 pad.7.clone
  8.2 0.1 broadcast_in_dim.7
  8.3 2.3 %maximum_maximum_fusion = bf16[3,4,2,144,128]{4,3,2,1,0:T(8,128)(2,1)} fusion(bf16[3,4,2,1,128]{4,3,2,1,0:T(2,128)(2,1)S(1)} %broadcast_in_dim.7, bf16[3,4,2,3,128]{4,3,2,1,0:T(4,128)(2,1)S(1)} %broadcast_in_dim.6, bf16[3,4,2,128,128]{4,3,2,1,0:T(8,128)(2,1)} %param.3, bf16[144]{0:T(256)(128)(2,1)S(1)} %pad.7.clone), kind=kLoop, calls=%fused_computation.6 | loop fusion | flops 3538944 | bytes 1696032 | tf_op jit(solution)/shard_map/concatenate | solution.py:81
  10.6 0.0 all-gather.2.cloned.1.call-update
  10.6 111.6 %all-gather.2.cloned.1.call-done = bf16[3,32,2,144,128]{4,3,2,1,0:T(8,128)(2,1)} async-done(((bf16[3,4,2,144,128]{4,3,2,1,0:T(8,128)(2,1)}), bf16[3,32,2,144,128]{4,3,2,1,0:T(8,128)(2,1)}) %all-gather.2.cloned.1.call-update) | async-done | bytes 7077904 | tf_op jit(solution)/shard_map/all_gather | solution.py:114
  122.3 4.2 %copy.10 = bf16[3,32,2,144,128]{4,3,1,0,2:T(8,128)(2,1)S(1)} copy(bf16[3,32,2,144,128]{4,3,2,1,0:T(8,128)(2,1)} %all-gather.2.cloned.1.call-done) | data formatting | bytes 14155776 | tf_op jit(solution)/shard_map/all_gather | solution.py:114
  126.5 0.0 copy-start
  126.5 0.2 dynamic-slice_bitcast_fusion.2
  126.8 4.6 %collective-permute-start.1 = (bf16[48,144,128]{2,1,0:T(8,128)(2,1)S(1)}, bf16[48,144,128]{2,1,0:T(8,128)(2,1)}, u32[]{:S(2)}, u32[]{:S(2)}) collective-permute-start(bf16[48,144,128]{2,1,0:T(8,128)(2,1)S(1)} %get-tuple-element.5), channel_id=1, source_target_pairs={{0,16},{1,17},{10,18},{11,19},{20,4},{21,5},{30,6},{31,7}} | collective-permute-start | bytes 5308424 | tf_op jit(solution)/shard_map/ppermute | solution.py:90
  131.3 2.5 %collective-permute-start.3 = (bf16[48,144,128]{2,1,0:T(8,128)(2,1)S(1)}, bf16[48,144,128]{2,1,0:T(8,128)(2,1)}, u32[]{:S(2)}, u32[]{:S(2)}) collective-permute-start(bf16[48,144,128]{2,1,0:T(8,128)(2,1)S(1)} %get-tuple-element.6), channel_id=1, source_target_pairs={{0,24},{1,25},{10,26},{11,27},{20,12},{21,13},{30,14},{31,15}} | collective-permute-start | bytes 5308424 | tf_op jit(solution)/shard_map/ppermute | solution.py:90
  133.9 2.1 %dynamic-slice_bitcast_fusion = bf16[96,144,128]{2,1,0:T(8,128)(2,1)} fusion(bf16[96,2,144,128]{3,2,0,1:T(8,128)(2,1)S(1)} %bitcast.18, s32[]{:T(128)S(6)} %select_n.72), kind=kLoop, calls=%fused_computation.1 | loop fusion | bytes 7077892 | tf_op jit(solution)/shard_map/jit(dynamic_index_in_dim)/squeeze | solution.py:121
  135.9 3.2 %collective-permute-start = (bf16[96,144,128]{2,1,0:T(8,128)(2,1)}, bf16[96,144,128]{2,1,0:T(8,128)(2,1)}, u32[]{:S(2)}, u32[]{:S(2)}) collective-permute-start(bf16[96,144,128]{2,1,0:T(8,128)(2,1)} %dynamic-slice_bitcast_fusion), channel_id=1, source_target_pairs={{0,8},{1,9},{10,2},{11,3},{20,28},{21,29},{30,22},{31,23}} | collective-permute-start | bytes 10616840 | tf_op jit(solution)/shard_map/ppermute | solution.py:90
  139.1 11.1 %collective-permute-done.1 = bf16[48,144,128]{2,1,0:T(8,128)(2,1)} collective-permute-done((bf16[48,144,128]{2,1,0:T(8,128)(2,1)S(1)}, bf16[48,144,128]{2,1,0:T(8,128)(2,1)}, u32[]{:S(2)}, u32[]{:S(2)}) %collective-permute-start.1) | collective-permute-done | bytes 1769504 | tf_op jit(solution)/shard_map/ppermute | solution.py:90
  150.2 1.9 collective-permute-start.2
  152.0 17.1 %collective-permute-done.3 = bf16[48,144,128]{2,1,0:T(8,128)(2,1)} collective-permute-done((bf16[48,144,128]{2,1,0:T(8,128)(2,1)S(1)}, bf16[48,144,128]{2,1,0:T(8,128)(2,1)}, u32[]{:S(2)}, u32[]{:S(2)}) %collective-permute-start.3) | collective-permute-done | bytes 1769504 | tf_op jit(solution)/shard_map/ppermute | solution.py:90
  169.1 1.9 collective-permute-start.4
  171.0 1.8 slice_reduce_fusion
  172.8 0.0 collective-permute-done.2
  172.8 1.7 select_select_fusion.1
  174.6 0.0 collective-permute-done.4
  174.6 0.0 copy-start.1
  174.6 1.9 select_select_fusion
  176.4 0.0 collective-permute-done
  176.5 1.6 copy-done.1
  178.1 0.8 maximum_select_fusion.bc_ref
  179.0 0.8 slice_reduce_fusion.1
  179.8 0.7 copy.11
  180.5 1.0 min.12.offs_ref
  181.5 14.6 %shard_map.37 = f32[2048,1024]{1,0:T(8,128)} custom-call(s32[288]{0:T(512)S(1)} %min.12.offs_ref, bf16[96,2,144,128]{3,2,1,0:T(8,128)(2,1)} %bitcast.21, bf16[96,144,128]{2,1,0:T(8,128)(2,1)S(1)} %maximum_select_fusion.bc_ref), custom_call_target="tpu_custom_call" | custom-call | flops 805306368 | bytes 17825792 | tf_op jit(solution)/shard_map/pallas_call | solution.py:46
  (7 shorter events, 0.0 us)
Async XLA Ops:
  6.5 115.7 %all-gather.2.cloned.1.call-start = ((), (), s32[]{:S(2)}) async-start(), calls=%async_computation | async-start | bytes 7962624 | tf_op jit(solution)/shard_map/all_gather | solution.py:114
  126.5 7.4 %copy-start = (bf16[3,32,2,144,128]{4,3,1,0,2:T(8,128)(2,1)}, bf16[3,32,2,144,128]{4,3,1,0,2:T(8,128)(2,1)S(1)}, u32[]{:S(2)}) copy-start(bf16[3,32,2,144,128]{4,3,1,0,2:T(8,128)(2,1)S(1)} %copy.10) | copy-start | bytes 21233668
  126.8 23.4 %collective-permute-start.1 = (bf16[48,144,128]{2,1,0:T(8,128)(2,1)S(1)}, bf16[48,144,128]{2,1,0:T(8,128)(2,1)}, u32[]{:S(2)}, u32[]{:S(2)}) collective-permute-start(bf16[48,144,128]{2,1,0:T(8,128)(2,1)S(1)} %get-tuple-element.5), channel_id=1, source_target_pairs={{0,16},{1,17},{10,18},{11,19},{20,4},{21,5},{30,6},{31,7}} | collective-permute-start | bytes 5308424 | tf_op jit(solution)/shard_map/ppermute | solution.py:90
  131.3 37.8 %collective-permute-start.3 = (bf16[48,144,128]{2,1,0:T(8,128)(2,1)S(1)}, bf16[48,144,128]{2,1,0:T(8,128)(2,1)}, u32[]{:S(2)}, u32[]{:S(2)}) collective-permute-start(bf16[48,144,128]{2,1,0:T(8,128)(2,1)S(1)} %get-tuple-element.6), channel_id=1, source_target_pairs={{0,24},{1,25},{10,26},{11,27},{20,12},{21,13},{30,14},{31,15}} | collective-permute-start | bytes 5308424 | tf_op jit(solution)/shard_map/ppermute | solution.py:90
  135.9 40.5 %collective-permute-start = (bf16[96,144,128]{2,1,0:T(8,128)(2,1)}, bf16[96,144,128]{2,1,0:T(8,128)(2,1)}, u32[]{:S(2)}, u32[]{:S(2)}) collective-permute-start(bf16[96,144,128]{2,1,0:T(8,128)(2,1)} %dynamic-slice_bitcast_fusion), channel_id=1, source_target_pairs={{0,8},{1,9},{10,2},{11,3},{20,28},{21,29},{30,22},{31,23}} | collective-permute-start | bytes 10616840 | tf_op jit(solution)/shard_map/ppermute | solution.py:90
  150.2 22.7 %collective-permute-start.2 = (bf16[48,144,128]{2,1,0:T(8,128)(2,1)}, bf16[48,144,128]{2,1,0:T(8,128)(2,1)}, u32[]{:S(2)}, u32[]{:S(2)}) collective-permute-start(bf16[48,144,128]{2,1,0:T(8,128)(2,1)} %collective-permute-done.1), channel_id=1, source_target_pairs={{16,24},{17,25},{18,26},{19,27},{4,12},{5,13},{6,14},{7,15}} | collective-permute-start | bytes 5308424 | tf_op jit(solution)/shard_map/ppermute | solution.py:90
  169.1 5.4 %collective-permute-start.4 = (bf16[48,144,128]{2,1,0:T(8,128)(2,1)}, bf16[48,144,128]{2,1,0:T(8,128)(2,1)}, u32[]{:S(2)}, u32[]{:S(2)}) collective-permute-start(bf16[48,144,128]{2,1,0:T(8,128)(2,1)} %collective-permute-done.3), channel_id=1, source_target_pairs={{24,16},{25,17},{26,18},{27,19},{12,4},{13,5},{14,6},{15,7}} | collective-permute-start | bytes 5308424 | tf_op jit(solution)/shard_map/ppermute | solution.py:90
  174.6 3.5 %copy-start.1 = (bf16[3,32,2,144,128]{4,3,1,0,2:T(8,128)(2,1)S(1)}, bf16[3,32,2,144,128]{4,3,1,0,2:T(8,128)(2,1)}, u32[]{:S(2)}) copy-start(bf16[3,32,2,144,128]{4,3,1,0,2:T(8,128)(2,1)} %copy-done) | copy-start | bytes 21233668
Sparse Core Ops, SparseCore 0:
  10.7 111.4 all-gather.1

commit v5 on v4

--- a/solution.py
+++ b/solution.py
@@ -107,13 +107,27 @@
     return jnp.where(j_r == 0, jnp.where(r == src, own, partner), other)
 
 
+def ring_gather(x, ncol):
+    outer = ncol // 2
+    cycle = [a * 2 for a in range(outer)] + [a * 2 + 1 for a in reversed(range(outer))]
+    forward = [(cycle[i], cycle[(i + 1) % ncol]) for i in range(ncol)]
+    backward = [(b, a) for a, b in forward]
+    half = x.shape[1] // 2
+    a, b = x[:, :half], x[:, half:]
+    pieces_a, pieces_b = [a], [b]
+    for _ in range(1, ncol):
+        a = lax.ppermute(a, "col", forward)
+        b = lax.ppermute(b, "col", backward)
+        pieces_a.append(a)
+        pieces_b.append(b)
+    return jnp.concatenate(pieces_a + pieces_b, axis=1)
+
+
 def local(panel_blocks, user_weights, slot_offset, *, nrow, ncol):
     panels, _, local_slots, blk, _ = panel_blocks.shape
     r = lax.axis_index("row")
     c = lax.axis_index("col")
-    blocks = lax.all_gather(
-        with_meta(panel_blocks, user_weights, slot_offset), "col", axis=1, tiled=True
-    )
+    blocks = ring_gather(with_meta(panel_blocks, user_weights, slot_offset), ncol)
     n = panels * blocks.shape[1]
     blocks = blocks.reshape(n, local_slots, blk + META, blk)
 

time: 205 us -> 164 us (0.80)
  waiting for transfers between devices: 140 us -> 79.7 us
  local copies, waits for them, and re-layouts: 12.8 us -> 30.2 us
  starting transfers between devices: 14 us -> 29.3 us
  between operations: 13.5 us -> 0.16 us
    all_gather x1 -> x0, waiting for transfers between devices: 112 us -> none  [local(): lax.all_gather(with_meta(panel_blocks, user_weights, slot_offset), 'col',...]
    ppermute x0 -> x14, waiting for transfers between devices: none -> 51.6 us  [the longest x7 51.6 us: ring_gather(): a = lax.ppermute(a, 'col', forward)]
    unnamed x4 -> x24, local copies, waits for them, and re-layouts: 1.66 us -> 17 us
    ppermute x0 -> x14, starting transfers between devices: none -> 15.2 us  [the longest x7 12.1 us: ring_gather(): a = lax.ppermute(a, 'col', forward)]
    concatenate x0 -> x2, local copies, waits for them, and re-layouts: none -> 5.08 us  [ring_gather(): return jnp.concatenate(pieces_a + pieces_b, axis=1)]
    all_gather x1 -> x0, local copies, waits for them, and re-layouts: 4.22 us -> none  [local(): lax.all_gather(with_meta(panel_blocks, user_weights, slot_offset), 'col',...]
  transfers between devices with their start and end apart: 6 -> 19, of which waited for: 3 -> 8; matrix products, arithmetic and copies ran while one was open for 4% -> 15% of each run, Pallas kernels for 0% -> 0%
where the time goes in v5:
time: 164 us; the launch traced here: 161 us
  waiting for transfers between devices  79.7 us (49%)
  local copies, waits for them, and re-layouts  30.2 us (18%)
  starting transfers between devices  29.3 us (18%)
  Pallas kernels  14.6 us (9%)
  other arithmetic  7.3 us (4%)
    ppermute x7, waiting for transfers between devices, ring_gather(): a = lax.ppermute(a, 'col', forward)  51.6 us
    ppermute x5, waiting for transfers between devices, send(): lax.ppermute(x, ('row', 'col'), [(a * ncol + cc, b * ncol + cc) for cc, a...  28.1 us
    unnamed x24, local copies, waits for them, and re-layouts  17 us
    pallas_call x1, Pallas kernels, gram_call(): pl.pallas_call(kernel, grid_spec=pltpu.PrefetchScalarGridSpec(num_scalar_...  14.6 us
    ppermute x5, starting transfers between devices, send(): lax.ppermute(x, ('row', 'col'), [(a * ncol + cc, b * ncol + cc) for cc, a...  14.1 us
    ppermute x7, starting transfers between devices, ring_gather(): a = lax.ppermute(a, 'col', forward)  12.1 us
    concatenate x2, local copies, waits for them, and re-layouts, ring_gather(): return jnp.concatenate(pieces_a + pieces_b, axis=1)  5.08 us
  transfers between devices with their start and end apart: 19, of which 8 were waited for; matrix products, arithmetic and copies ran while one was open for 15% of the time, Pallas kernels for 0%

profile of v5, /device:TPU:0, one launch (start us, length us, event | category | flops | bytes accessed | tf_op | source)
XLA Modules:
  0.0 161.3 jit_solution(4128628108240239006)
XLA Ops:
  1.7 1.4 maximum_maximum_fusion
  4.2 3.0 %collective-permute-start = (bf16[3,2,2,144,128]{4,3,2,1,0:T(8,128)(2,1)S(1)}, bf16[3,2,2,144,128]{4,3,2,1,0:T(8,128)(2,1)S(1)}, u32[]{:S(2)}, u32[]{:S(2)}) collective-permute-start(bf16[3,2,2,144,128]{4,3,2,1,0:T(8,128)(2,1)S(1)} %get-tuple-element.9), channel_id=1, source_target_pairs={{0,2},{2,4},{4,6},{6,7},{7,5},{5,3},{3,1},{1,0},{8,10},{10,12},{12... | collective-permute-start | bytes 1327112 | tf_op jit(solution)/shard_map/ppermute | solution.py:119
  7.2 10.1 %collective-permute-done = bf16[3,2,2,144,128]{4,3,2,1,0:T(8,128)(2,1)S(1)} collective-permute-done((bf16[3,2,2,144,128]{4,3,2,1,0:T(8,128)(2,1)S(1)}, bf16[3,2,2,144,128]{4,3,2,1,0:T(8,128)(2,1)S(1)}, u32[]{:S(2)}, u32[]{:S(2)}) %collective-permute-start) | collective-permute-done | bytes 442400 | tf_op jit(solution)/shard_map/ppermute | solution.py:119
  17.3 1.8 %collective-permute-start.1 = (bf16[3,2,2,144,128]{4,3,2,1,0:T(8,128)(2,1)S(1)}, bf16[3,2,2,144,128]{4,3,2,1,0:T(8,128)(2,1)S(1)}, u32[]{:S(2)}, u32[]{:S(2)}) collective-permute-start(bf16[3,2,2,144,128]{4,3,2,1,0:T(8,128)(2,1)S(1)} %collective-permute-done), channel_id=1, source_target_pairs={{0,2},{2,4},{4,6},{6,7},{7,5},{5,3},{3,1},{1,0},{8,10},{10,12},{12... | collective-permute-start | bytes 1327112 | tf_op jit(solution)/shard_map/ppermute | solution.py:119
  19.3 9.3 %collective-permute-done.1 = bf16[3,2,2,144,128]{4,3,2,1,0:T(8,128)(2,1)S(1)} collective-permute-done((bf16[3,2,2,144,128]{4,3,2,1,0:T(8,128)(2,1)S(1)}, bf16[3,2,2,144,128]{4,3,2,1,0:T(8,128)(2,1)S(1)}, u32[]{:S(2)}, u32[]{:S(2)}) %collective-permute-start.1) | collective-permute-done | bytes 442400 | tf_op jit(solution)/shard_map/ppermute | solution.py:119
  28.6 1.5 collective-permute-start.2
  30.7 8.4 %collective-permute-done.2 = bf16[3,2,2,144,128]{4,3,2,1,0:T(8,128)(2,1)S(1)} collective-permute-done((bf16[3,2,2,144,128]{4,3,2,1,0:T(8,128)(2,1)S(1)}, bf16[3,2,2,144,128]{4,3,2,1,0:T(8,128)(2,1)S(1)}, u32[]{:S(2)}, u32[]{:S(2)}) %collective-permute-start.2) | collective-permute-done | bytes 442400 | tf_op jit(solution)/shard_map/ppermute | solution.py:119
  39.1 1.4 collective-permute-start.3
  41.1 8.3 %collective-permute-done.3 = bf16[3,2,2,144,128]{4,3,2,1,0:T(8,128)(2,1)S(1)} collective-permute-done((bf16[3,2,2,144,128]{4,3,2,1,0:T(8,128)(2,1)S(1)}, bf16[3,2,2,144,128]{4,3,2,1,0:T(8,128)(2,1)S(1)}, u32[]{:S(2)}, u32[]{:S(2)}) %collective-permute-start.3) | collective-permute-done | bytes 442400 | tf_op jit(solution)/shard_map/ppermute | solution.py:119
  49.4 1.4 collective-permute-start.4
  51.4 8.1 %collective-permute-done.4 = bf16[3,2,2,144,128]{4,3,2,1,0:T(8,128)(2,1)} collective-permute-done((bf16[3,2,2,144,128]{4,3,2,1,0:T(8,128)(2,1)S(1)}, bf16[3,2,2,144,128]{4,3,2,1,0:T(8,128)(2,1)}, u32[]{:S(2)}, u32[]{:S(2)}) %collective-permute-start.4) | collective-permute-done | bytes 442400 | tf_op jit(solution)/shard_map/ppermute | solution.py:119
  59.5 1.4 collective-permute-start.5
  63.2 7.3 %collective-permute-done.5 = bf16[3,2,2,144,128]{4,3,2,1,0:T(8,128)(2,1)} collective-permute-done((bf16[3,2,2,144,128]{4,3,2,1,0:T(8,128)(2,1)}, bf16[3,2,2,144,128]{4,3,2,1,0:T(8,128)(2,1)}, u32[]{:S(2)}, u32[]{:S(2)}) %collective-permute-start.5) | collective-permute-done | bytes 442400 | tf_op jit(solution)/shard_map/ppermute | solution.py:119
  70.6 1.6 %collective-permute-start.6 = (bf16[3,2,2,144,128]{4,3,2,1,0:T(8,128)(2,1)}, bf16[3,2,2,144,128]{4,3,2,1,0:T(8,128)(2,1)S(1)}, u32[]{:S(2)}, u32[]{:S(2)}) collective-permute-start(bf16[3,2,2,144,128]{4,3,2,1,0:T(8,128)(2,1)} %collective-permute-done.5), channel_id=1, source_target_pairs={{0,2},{2,4},{4,6},{6,7},{7,5},{5,3},{3,1},{1,0},{8,10},{10,12},{12... | collective-permute-start | bytes 1327112 | tf_op jit(solution)/shard_map/ppermute | solution.py:119
  72.2 1.9 %constant_dynamic-update-slice_fusion.12 = bf16[3,32,2,144,128]{4,3,2,1,0:T(8,128)(2,1)} fusion(bf16[3,32,2,144,128]{4,3,2,1,0:T(8,128)(2,1)} %constant_dynamic-update-slice_fusion.13, bf16[3,2,2,144,128]{4,3,2,1,0:T(8,128)(2,1)} %copy-done.1), kind=kLoop, calls=%fused_computation.21 | loop fusion | bytes 884736
  74.1 1.9 %constant_dynamic-update-slice_fusion.11 = bf16[3,32,2,144,128]{4,3,2,1,0:T(8,128)(2,1)} fusion(bf16[3,32,2,144,128]{4,3,2,1,0:T(8,128)(2,1)} %constant_dynamic-update-slice_fusion.12, bf16[3,2,2,144,128]{4,3,2,1,0:T(8,128)(2,1)} %copy-done.2), kind=kLoop, calls=%fused_computation.20 | loop fusion | bytes 884736
  76.0 1.9 %constant_dynamic-update-slice_fusion.10 = bf16[3,32,2,144,128]{4,3,2,1,0:T(8,128)(2,1)} fusion(bf16[3,32,2,144,128]{4,3,2,1,0:T(8,128)(2,1)} %constant_dynamic-update-slice_fusion.11, bf16[3,2,2,144,128]{4,3,2,1,0:T(8,128)(2,1)} %collective-permute-done.4), kind=kLoop, calls=%fused_computation.19 | loop fusion | bytes 884736
  78.2 1.9 %constant_dynamic-update-slice_fusion.9 = bf16[3,32,2,144,128]{4,3,2,1,0:T(8,128)(2,1)} fusion(bf16[3,32,2,144,128]{4,3,2,1,0:T(8,128)(2,1)} %constant_dynamic-update-slice_fusion.10, bf16[3,2,2,144,128]{4,3,2,1,0:T(8,128)(2,1)} %collective-permute-done.5), kind=kLoop, calls=%fused_computation.18 | loop fusion | bytes 884736
  85.2 1.9 %constant_dynamic-update-slice_fusion.2 = bf16[3,32,2,144,128]{4,3,2,1,0:T(8,128)(2,1)} fusion(bf16[3,32,2,144,128]{4,3,2,1,0:T(8,128)(2,1)} %constant_dynamic-update-slice_fusion.3, bf16[3,2,2,144,128]{4,3,2,1,0:T(8,128)(2,1)} %collective-permute-done.11), kind=kLoop, calls=%fused_computation.11 | loop fusion | bytes 884736
  88.8 4.2 %copy.10 = bf16[3,32,2,144,128]{4,3,1,0,2:T(8,128)(2,1)S(1)} copy(bf16[3,32,2,144,128]{4,3,2,1,0:T(8,128)(2,1)} %constant_dynamic-update-slice_fusion) | data formatting | bytes 14155776 | tf_op jit(solution)/shard_map/concatenate | solution.py:123
  93.3 4.7 %collective-permute-start.15 = (bf16[48,144,128]{2,1,0:T(8,128)(2,1)S(1)}, bf16[48,144,128]{2,1,0:T(8,128)(2,1)}, u32[]{:S(2)}, u32[]{:S(2)}) collective-permute-start(bf16[48,144,128]{2,1,0:T(8,128)(2,1)S(1)} %get-tuple-element.5), channel_id=1, source_target_pairs={{0,16},{1,17},{10,18},{11,19},{20,4},{21,5},{30,6},{31,7}} | collective-permute-start | bytes 5308424 | tf_op jit(solution)/shard_map/ppermute | solution.py:90
  98.0 2.5 %collective-permute-start.17 = (bf16[48,144,128]{2,1,0:T(8,128)(2,1)S(1)}, bf16[48,144,128]{2,1,0:T(8,128)(2,1)}, u32[]{:S(2)}, u32[]{:S(2)}) collective-permute-start(bf16[48,144,128]{2,1,0:T(8,128)(2,1)S(1)} %get-tuple-element.6), channel_id=1, source_target_pairs={{0,24},{1,25},{10,26},{11,27},{20,12},{21,13},{30,14},{31,15}} | collective-permute-start | bytes 5308424 | tf_op jit(solution)/shard_map/ppermute | solution.py:90
  100.5 2.1 %dynamic-slice_bitcast_fusion = bf16[96,144,128]{2,1,0:T(8,128)(2,1)} fusion(bf16[96,2,144,128]{3,2,0,1:T(8,128)(2,1)S(1)} %bitcast.18, s32[]{:T(128)S(6)} %select_n.72), kind=kLoop, calls=%fused_computation.1 | loop fusion | bytes 7077892 | tf_op jit(solution)/shard_map/jit(dynamic_index_in_dim)/squeeze | solution.py:135
  102.6 3.1 %collective-permute-start.14 = (bf16[96,144,128]{2,1,0:T(8,128)(2,1)}, bf16[96,144,128]{2,1,0:T(8,128)(2,1)}, u32[]{:S(2)}, u32[]{:S(2)}) collective-permute-start(bf16[96,144,128]{2,1,0:T(8,128)(2,1)} %dynamic-slice_bitcast_fusion), channel_id=1, source_target_pairs={{0,8},{1,9},{10,2},{11,3},{20,28},{21,29},{30,22},{31,23}} | collective-permute-start | bytes 10616840 | tf_op jit(solution)/shard_map/ppermute | solution.py:90
  105.7 11.1 %collective-permute-done.15 = bf16[48,144,128]{2,1,0:T(8,128)(2,1)} collective-permute-done((bf16[48,144,128]{2,1,0:T(8,128)(2,1)S(1)}, bf16[48,144,128]{2,1,0:T(8,128)(2,1)}, u32[]{:S(2)}, u32[]{:S(2)}) %collective-permute-start.15) | collective-permute-done | bytes 1769504 | tf_op jit(solution)/shard_map/ppermute | solution.py:90
  116.8 1.9 %collective-permute-start.16 = (bf16[48,144,128]{2,1,0:T(8,128)(2,1)}, bf16[48,144,128]{2,1,0:T(8,128)(2,1)}, u32[]{:S(2)}, u32[]{:S(2)}) collective-permute-start(bf16[48,144,128]{2,1,0:T(8,128)(2,1)} %collective-permute-done.15), channel_id=1, source_target_pairs={{16,24},{17,25},{18,26},{19,27},{4,12},{5,13},{6,14},{7,15}} | collective-permute-start | bytes 5308424 | tf_op jit(solution)/shard_map/ppermute | solution.py:90
  118.7 17.1 %collective-permute-done.17 = bf16[48,144,128]{2,1,0:T(8,128)(2,1)} collective-permute-done((bf16[48,144,128]{2,1,0:T(8,128)(2,1)S(1)}, bf16[48,144,128]{2,1,0:T(8,128)(2,1)}, u32[]{:S(2)}, u32[]{:S(2)}) %collective-permute-start.17) | collective-permute-done | bytes 1769504 | tf_op jit(solution)/shard_map/ppermute | solution.py:90
  135.8 1.9 %collective-permute-start.18 = (bf16[48,144,128]{2,1,0:T(8,128)(2,1)}, bf16[48,144,128]{2,1,0:T(8,128)(2,1)}, u32[]{:S(2)}, u32[]{:S(2)}) collective-permute-start(bf16[48,144,128]{2,1,0:T(8,128)(2,1)} %collective-permute-done.17), channel_id=1, source_target_pairs={{24,16},{25,17},{26,18},{27,19},{12,4},{13,5},{14,6},{15,7}} | collective-permute-start | bytes 5308424 | tf_op jit(solution)/shard_map/ppermute | solution.py:90
  137.7 1.9 %slice_reduce_fusion = bf16[96,2]{0,1:T(2,128)(2,1)S(1)} fusion(bf16[96,2,144,128]{3,2,0,1:T(8,128)(2,1)} %bitcast.19), kind=kLoop, calls=%fused_computation.7 | loop fusion | bytes 768 | tf_op jit(solution)/shard_map/slice | solution.py:138
  139.6 1.9 %select_select_fusion.1 = bf16[48,144,128]{2,1,0:T(8,128)(2,1)S(1)} fusion(bf16[48,144,128]{2,1,0:T(8,128)(2,1)S(1)} %get-tuple-element.5, bf16[48,144,128]{2,1,0:T(8,128)(2,1)} %collective-permute-done.15, bf16[48,144,128]{2,1,0:T(8,128)(2,1)} %collective-permute-done.16, pred[]{:T(512)S(6)} %eq.20, pred[]{:T(512)S(6)} %eq.19), kind=kLoop, calls=%fused_computation.5 | loop fusion | flops 1769472 | bytes 7077890 | tf_op jit(solution)/shard_map/jit(_where)/select_n | solution.py:104
  141.5 1.7 %select_select_fusion = bf16[48,144,128]{2,1,0:T(8,128)(2,1)S(1)} fusion(bf16[48,144,128]{2,1,0:T(8,128)(2,1)S(1)} %get-tuple-element.6, bf16[48,144,128]{2,1,0:T(8,128)(2,1)} %collective-permute-done.18, bf16[48,144,128]{2,1,0:T(8,128)(2,1)} %collective-permute-done.17, pred[]{:T(512)S(6)} %eq.20, pred[]{:T(512)S(6)} %eq.19), kind=kLoop, calls=%fused_computation.4 | loop fusion | flops 1769472 | bytes 7077890 | tf_op jit(solution)/shard_map/jit(_where)/select_n | solution.py:105
  146.7 14.6 %shard_map.37 = f32[2048,1024]{1,0:T(8,128)} custom-call(s32[288]{0:T(512)S(1)} %min.12.offs_ref, bf16[96,2,144,128]{3,2,1,0:T(8,128)(2,1)} %bitcast.23, bf16[96,144,128]{2,1,0:T(8,128)(2,1)S(1)} %maximum_select_fusion.bc_ref), custom_call_target="tpu_custom_call" | custom-call | flops 805306368 | bytes 17825792 | tf_op jit(solution)/shard_map/pallas_call | solution.py:46
  (55 shorter events, 18.0 us)
Async XLA Ops:
  4.2 13.1 %collective-permute-start = (bf16[3,2,2,144,128]{4,3,2,1,0:T(8,128)(2,1)S(1)}, bf16[3,2,2,144,128]{4,3,2,1,0:T(8,128)(2,1)S(1)}, u32[]{:S(2)}, u32[]{:S(2)}) collective-permute-start(bf16[3,2,2,144,128]{4,3,2,1,0:T(8,128)(2,1)S(1)} %get-tuple-element.9), channel_id=1, source_target_pairs={{0,2},{2,4},{4,6},{6,7},{7,5},{5,3},{3,1},{1,0},{8,10},{10,12},{12... | collective-permute-start | bytes 1327112 | tf_op jit(solution)/shard_map/ppermute | solution.py:119
  7.2 11.9 %collective-permute-start.7 = (bf16[3,2,2,144,128]{4,3,2,1,0:T(8,128)(2,1)S(1)}, bf16[3,2,2,144,128]{4,3,2,1,0:T(8,128)(2,1)S(1)}, u32[]{:S(2)}, u32[]{:S(2)}) collective-permute-start(bf16[3,2,2,144,128]{4,3,2,1,0:T(8,128)(2,1)S(1)} %get-tuple-element.7), channel_id=1, source_target_pairs={{2,0},{4,2},{6,4},{7,6},{5,7},{3,5},{1,3},{0,1},{10,8},{12,10},{14... | collective-permute-start | bytes 1327112 | tf_op jit(solution)/shard_map/ppermute | solution.py:120
  17.3 11.4 %collective-permute-start.1 = (bf16[3,2,2,144,128]{4,3,2,1,0:T(8,128)(2,1)S(1)}, bf16[3,2,2,144,128]{4,3,2,1,0:T(8,128)(2,1)S(1)}, u32[]{:S(2)}, u32[]{:S(2)}) collective-permute-start(bf16[3,2,2,144,128]{4,3,2,1,0:T(8,128)(2,1)S(1)} %collective-permute-done), channel_id=1, source_target_pairs={{0,2},{2,4},{4,6},{6,7},{7,5},{5,3},{3,1},{1,0},{8,10},{10,12},{12... | collective-permute-start | bytes 1327112 | tf_op jit(solution)/shard_map/ppermute | solution.py:119
  19.1 11.0 %collective-permute-start.8 = (bf16[3,2,2,144,128]{4,3,2,1,0:T(8,128)(2,1)S(1)}, bf16[3,2,2,144,128]{4,3,2,1,0:T(8,128)(2,1)S(1)}, u32[]{:S(2)}, u32[]{:S(2)}) collective-permute-start(bf16[3,2,2,144,128]{4,3,2,1,0:T(8,128)(2,1)S(1)} %collective-permute-done.7), channel_id=1, source_target_pairs={{2,0},{4,2},{6,4},{7,6},{5,7},{3,5},{1,3},{0,1},{10,8},{12,10},{14... | collective-permute-start | bytes 1327112 | tf_op jit(solution)/shard_map/ppermute | solution.py:120
  28.6 10.4 %collective-permute-start.2 = (bf16[3,2,2,144,128]{4,3,2,1,0:T(8,128)(2,1)S(1)}, bf16[3,2,2,144,128]{4,3,2,1,0:T(8,128)(2,1)S(1)}, u32[]{:S(2)}, u32[]{:S(2)}) collective-permute-start(bf16[3,2,2,144,128]{4,3,2,1,0:T(8,128)(2,1)S(1)} %collective-permute-done.1), channel_id=1, source_target_pairs={{0,2},{2,4},{4,6},{6,7},{7,5},{5,3},{3,1},{1,0},{8,10},{10,12},{12... | collective-permute-start | bytes 1327112 | tf_op jit(solution)/shard_map/ppermute | solution.py:119
  30.1 10.3 %collective-permute-start.9 = (bf16[3,2,2,144,128]{4,3,2,1,0:T(8,128)(2,1)S(1)}, bf16[3,2,2,144,128]{4,3,2,1,0:T(8,128)(2,1)S(1)}, u32[]{:S(2)}, u32[]{:S(2)}) collective-permute-start(bf16[3,2,2,144,128]{4,3,2,1,0:T(8,128)(2,1)S(1)} %collective-permute-done.8), channel_id=1, source_target_pairs={{2,0},{4,2},{6,4},{7,6},{5,7},{3,5},{1,3},{0,1},{10,8},{12,10},{14... | collective-permute-start | bytes 1327112 | tf_op jit(solution)/shard_map/ppermute | solution.py:120
  39.1 11.7 %copy-start.1 = (bf16[3,2,2,144,128]{4,3,2,1,0:T(8,128)(2,1)}, bf16[3,2,2,144,128]{4,3,2,1,0:T(8,128)(2,1)S(1)}, u32[]{:S(2)}) copy-start(bf16[3,2,2,144,128]{4,3,2,1,0:T(8,128)(2,1)S(1)} %collective-permute-done.2) | copy-start | bytes 1327108
  39.1 10.3 %collective-permute-start.3 = (bf16[3,2,2,144,128]{4,3,2,1,0:T(8,128)(2,1)S(1)}, bf16[3,2,2,144,128]{4,3,2,1,0:T(8,128)(2,1)S(1)}, u32[]{:S(2)}, u32[]{:S(2)}) collective-permute-start(bf16[3,2,2,144,128]{4,3,2,1,0:T(8,128)(2,1)S(1)} %collective-permute-done.2), channel_id=1, source_target_pairs={{0,2},{2,4},{4,6},{6,7},{7,5},{5,3},{3,1},{1,0},{8,10},{10,12},{12... | collective-permute-start | bytes 1327112 | tf_op jit(solution)/shard_map/ppermute | solution.py:119
  40.5 10.3 %collective-permute-start.10 = (bf16[3,2,2,144,128]{4,3,2,1,0:T(8,128)(2,1)S(1)}, bf16[3,2,2,144,128]{4,3,2,1,0:T(8,128)(2,1)S(1)}, u32[]{:S(2)}, u32[]{:S(2)}) collective-permute-start(bf16[3,2,2,144,128]{4,3,2,1,0:T(8,128)(2,1)S(1)} %collective-permute-done.9), channel_id=1, source_target_pairs={{2,0},{4,2},{6,4},{7,6},{5,7},{3,5},{1,3},{0,1},{10,8},{12,10},{14... | collective-permute-start | bytes 1327112 | tf_op jit(solution)/shard_map/ppermute | solution.py:120
  49.4 2.0 %copy-start.2 = (bf16[3,2,2,144,128]{4,3,2,1,0:T(8,128)(2,1)}, bf16[3,2,2,144,128]{4,3,2,1,0:T(8,128)(2,1)S(1)}, u32[]{:S(2)}) copy-start(bf16[3,2,2,144,128]{4,3,2,1,0:T(8,128)(2,1)S(1)} %collective-permute-done.3) | copy-start | bytes 1327108
  49.4 10.1 %collective-permute-start.4 = (bf16[3,2,2,144,128]{4,3,2,1,0:T(8,128)(2,1)S(1)}, bf16[3,2,2,144,128]{4,3,2,1,0:T(8,128)(2,1)}, u32[]{:S(2)}, u32[]{:S(2)}) collective-permute-start(bf16[3,2,2,144,128]{4,3,2,1,0:T(8,128)(2,1)S(1)} %collective-permute-done.3), channel_id=1, source_target_pairs={{0,2},{2,4},{4,6},{6,7},{7,5},{5,3},{3,1},{1,0},{8,10},{10,12},{12... | collective-permute-start | bytes 1327112 | tf_op jit(solution)/shard_map/ppermute | solution.py:119
  50.8 11.0 %collective-permute-start.11 = (bf16[3,2,2,144,128]{4,3,2,1,0:T(8,128)(2,1)S(1)}, bf16[3,2,2,144,128]{4,3,2,1,0:T(8,128)(2,1)}, u32[]{:S(2)}, u32[]{:S(2)}) collective-permute-start(bf16[3,2,2,144,128]{4,3,2,1,0:T(8,128)(2,1)S(1)} %collective-permute-done.10), channel_id=1, source_target_pairs={{2,0},{4,2},{6,4},{7,6},{5,7},{3,5},{1,3},{0,1},{10,8},{12,10},{14... | collective-permute-start | bytes 1327112 | tf_op jit(solution)/shard_map/ppermute | solution.py:120
  59.5 11.1 %collective-permute-start.5 = (bf16[3,2,2,144,128]{4,3,2,1,0:T(8,128)(2,1)}, bf16[3,2,2,144,128]{4,3,2,1,0:T(8,128)(2,1)}, u32[]{:S(2)}, u32[]{:S(2)}) collective-permute-start(bf16[3,2,2,144,128]{4,3,2,1,0:T(8,128)(2,1)} %collective-permute-done.4), channel_id=1, source_target_pairs={{0,2},{2,4},{4,6},{6,7},{7,5},{5,3},{3,1},{1,0},{8,10},{10,12},{12... | collective-permute-start | bytes 1327112 | tf_op jit(solution)/shard_map/ppermute | solution.py:119
  61.8 16.1 %collective-permute-start.12 = (bf16[3,2,2,144,128]{4,3,2,1,0:T(8,128)(2,1)}, bf16[3,2,2,144,128]{4,3,2,1,0:T(8,128)(2,1)S(1)}, u32[]{:S(2)}, u32[]{:S(2)}) collective-permute-start(bf16[3,2,2,144,128]{4,3,2,1,0:T(8,128)(2,1)} %collective-permute-done.11), channel_id=1, source_target_pairs={{2,0},{4,2},{6,4},{7,6},{5,7},{3,5},{1,3},{0,1},{10,8},{12,10},{14... | collective-permute-start | bytes 1327112 | tf_op jit(solution)/shard_map/ppermute | solution.py:120
  70.6 9.5 %collective-permute-start.6 = (bf16[3,2,2,144,128]{4,3,2,1,0:T(8,128)(2,1)}, bf16[3,2,2,144,128]{4,3,2,1,0:T(8,128)(2,1)S(1)}, u32[]{:S(2)}, u32[]{:S(2)}) collective-permute-start(bf16[3,2,2,144,128]{4,3,2,1,0:T(8,128)(2,1)} %collective-permute-done.5), channel_id=1, source_target_pairs={{0,2},{2,4},{4,6},{6,7},{7,5},{5,3},{3,1},{1,0},{8,10},{10,12},{12... | collective-permute-start | bytes 1327112 | tf_op jit(solution)/shard_map/ppermute | solution.py:119
  77.9 10.1 %collective-permute-start.13 = (bf16[3,2,2,144,128]{4,3,2,1,0:T(8,128)(2,1)S(1)}, bf16[3,2,2,144,128]{4,3,2,1,0:T(8,128)(2,1)S(1)}, u32[]{:S(2)}, u32[]{:S(2)}) collective-permute-start(bf16[3,2,2,144,128]{4,3,2,1,0:T(8,128)(2,1)S(1)} %collective-permute-done.12), channel_id=1, source_target_pairs={{2,0},{4,2},{6,4},{7,6},{5,7},{3,5},{1,3},{0,1},{10,8},{12,10},{14... | collective-permute-start | bytes 1327112 | tf_op jit(solution)/shard_map/ppermute | solution.py:120
  93.0 9.5 %copy-start = (bf16[3,32,2,144,128]{4,3,1,0,2:T(8,128)(2,1)}, bf16[3,32,2,144,128]{4,3,1,0,2:T(8,128)(2,1)S(1)}, u32[]{:S(2)}) copy-start(bf16[3,32,2,144,128]{4,3,1,0,2:T(8,128)(2,1)S(1)} %copy.10) | copy-start | bytes 21233668
  93.3 23.5 %collective-permute-start.15 = (bf16[48,144,128]{2,1,0:T(8,128)(2,1)S(1)}, bf16[48,144,128]{2,1,0:T(8,128)(2,1)}, u32[]{:S(2)}, u32[]{:S(2)}) collective-permute-start(bf16[48,144,128]{2,1,0:T(8,128)(2,1)S(1)} %get-tuple-element.5), channel_id=1, source_target_pairs={{0,16},{1,17},{10,18},{11,19},{20,4},{21,5},{30,6},{31,7}} | collective-permute-start | bytes 5308424 | tf_op jit(solution)/shard_map/ppermute | solution.py:90
  98.0 37.8 %collective-permute-start.17 = (bf16[48,144,128]{2,1,0:T(8,128)(2,1)S(1)}, bf16[48,144,128]{2,1,0:T(8,128)(2,1)}, u32[]{:S(2)}, u32[]{:S(2)}) collective-permute-start(bf16[48,144,128]{2,1,0:T(8,128)(2,1)S(1)} %get-tuple-element.6), channel_id=1, source_target_pairs={{0,24},{1,25},{10,26},{11,27},{20,12},{21,13},{30,14},{31,15}} | collective-permute-start | bytes 5308424 | tf_op jit(solution)/shard_map/ppermute | solution.py:90
  102.6 40.6 %collective-permute-start.14 = (bf16[96,144,128]{2,1,0:T(8,128)(2,1)}, bf16[96,144,128]{2,1,0:T(8,128)(2,1)}, u32[]{:S(2)}, u32[]{:S(2)}) collective-permute-start(bf16[96,144,128]{2,1,0:T(8,128)(2,1)} %dynamic-slice_bitcast_fusion), channel_id=1, source_target_pairs={{0,8},{1,9},{10,2},{11,3},{20,28},{21,29},{30,22},{31,23}} | collective-permute-start | bytes 10616840 | tf_op jit(solution)/shard_map/ppermute | solution.py:90
  116.8 22.8 %collective-permute-start.16 = (bf16[48,144,128]{2,1,0:T(8,128)(2,1)}, bf16[48,144,128]{2,1,0:T(8,128)(2,1)}, u32[]{:S(2)}, u32[]{:S(2)}) collective-permute-start(bf16[48,144,128]{2,1,0:T(8,128)(2,1)} %collective-permute-done.15), channel_id=1, source_target_pairs={{16,24},{17,25},{18,26},{19,27},{4,12},{5,13},{6,14},{7,15}} | collective-permute-start | bytes 5308424 | tf_op jit(solution)/shard_map/ppermute | solution.py:90
  135.8 5.7 %collective-permute-start.18 = (bf16[48,144,128]{2,1,0:T(8,128)(2,1)}, bf16[48,144,128]{2,1,0:T(8,128)(2,1)}, u32[]{:S(2)}, u32[]{:S(2)}) collective-permute-start(bf16[48,144,128]{2,1,0:T(8,128)(2,1)} %collective-permute-done.17), channel_id=1, source_target_pairs={{24,16},{25,17},{26,18},{27,19},{12,4},{13,5},{14,6},{15,7}} | collective-permute-start | bytes 5308424 | tf_op jit(solution)/shard_map/ppermute | solution.py:90
  137.7 5.6 %slice-start = ((s8[7077888]{0:T(1024)(128)(4,1)}), s8[4194304]{0:T(1024)(128)(4,1)S(1)}, s32[]{:S(2)}) async-start(s8[7077888]{0:T(1024)(128)(4,1)} %bitcast.20), calls=%async_computation | async-start | bytes 8388608
  139.6 3.6 %slice-start.1 = ((s8[7077888]{0:T(1024)(128)(4,1)}), s8[2883584]{0:T(1024)(128)(4,1)S(1)}, s32[]{:S(2)}) async-start(s8[7077888]{0:T(1024)(128)(4,1)} %bitcast.20), calls=%async_computation.1 | async-start | bytes 5767168

commit v6 on v2

--- a/solution.py
+++ b/solution.py
@@ -85,36 +85,50 @@
     panels, _, local_slots, blk, _ = panel_blocks.shape
     r = lax.axis_index("row")
     c = lax.axis_index("col")
-    blocks = lax.all_gather(
-        with_meta(panel_blocks, user_weights, slot_offset), "col", axis=1, tiled=True
-    )
-    users = blocks.shape[1]
+    x = with_meta(panel_blocks, user_weights, slot_offset)
+
+    outer = ncol // 2
+    cycle = [a * 2 for a in range(outer)] + [a * 2 + 1 for a in reversed(range(outer))]
+    forward = [(cycle[i], cycle[(i + 1) % ncol]) for i in range(ncol)]
+    backward = [(b, a) for a, b in forward]
 
     src = c // local_slots
-    own = lax.dynamic_index_in_dim(blocks, c % local_slots, axis=2, keepdims=False)
-    received = [own]
-    for k in range(1, nrow):
-        perm = [
-            ((cc // local_slots) * ncol + cc, ((cc // local_slots + k) % nrow) * ncol + cc)
+    which = (r - src + nrow) % nrow
+    slot = c % local_slots
+    fans = [
+        [
+            ((cc // local_slots) * ncol + cc, ((cc // local_slots + j) % nrow) * ncol + cc)
             for cc in range(ncol)
         ]
-        received.append(lax.ppermute(own, ("row", "col"), perm))
-    which = (r - src + nrow) % nrow
-    column_blocks = received[0]
-    for k in range(1, nrow):
-        column_blocks = jnp.where(which == k, received[k], column_blocks)
+        for j in range(1, nrow)
+    ]
 
-    offs = jnp.concatenate(
-        [blocks[:, :, :, blk + 3, 0], column_blocks[:, :, blk + 3, 0][:, :, None]], axis=2
-    )
+    def pick_slot(piece):
+        return lax.dynamic_index_in_dim(piece, slot, axis=2, keepdims=False)
+
+    half = x.shape[1] // 2
+    a, b = x[:, :half], x[:, half:]
+    pieces, columns = [], []
+    for step in range(ncol):
+        if step:
+            a = lax.ppermute(a, "col", forward)
+            b = lax.ppermute(b, "col", backward)
+        pieces += [a, b]
+        own = jnp.concatenate([pick_slot(a), pick_slot(b)], axis=1)
+        got = own
+        for j, fan in enumerate(fans, start=1):
+            got = jnp.where(which == j, lax.ppermute(own, ("row", "col"), fan), got)
+        columns.append(got)
+
+    blocks = jnp.concatenate(pieces, axis=1)
+    column_blocks = jnp.concatenate(columns, axis=1)
+    n = panels * blocks.shape[1]
+    blocks = blocks.reshape(n, local_slots, blk + META, blk)
+    column_blocks = column_blocks.reshape(n, blk + META, blk)
+
+    offs = jnp.concatenate([blocks[:, :, blk + 3, 0], column_blocks[:, blk + 3, 0][:, None]], axis=1)
     offs = jnp.clip(offs.astype(jnp.int32), 0, IBS - 1).reshape(-1)
-
-    n = panels * users
-    return gram_call(
-        offs,
-        blocks.reshape(n, local_slots, blk + META, blk),
-        column_blocks.reshape(n, blk + META, blk),
-    )
+    return gram_call(offs, blocks, column_blocks)
 
 
 def solution(mesh):

time: 232 us -> 136 us (0.59)
  the two profiles are of different devices: /device:TPU:0 before, /device:TPU:14 now
where the time goes in v6:
time: 136 us; the launch traced here: 135 us
  waiting for transfers between devices  43.8 us (32%)
  starting transfers between devices  42 us (31%)
  local copies, waits for them, and re-layouts  22.6 us (17%)
  Pallas kernels  14.6 us (11%)
  other arithmetic  11.4 us (8%)
    ppermute x24, starting transfers between devices, local(): got = jnp.where(which == j, lax.ppermute(own, ('row', 'col'), fan), got)  23.5 us
    ppermute x7, starting transfers between devices, local(): b = lax.ppermute(b, 'col', backward)  17.2 us
    ppermute x24, waiting for transfers between devices, local(): got = jnp.where(which == j, lax.ppermute(own, ('row', 'col'), fan), got)  15.5 us
    ppermute x7, waiting for transfers between devices, local(): b = lax.ppermute(b, 'col', backward)  15.1 us
    pallas_call x1, Pallas kernels, gram_call(): pl.pallas_call(kernel, grid_spec=pltpu.PrefetchScalarGridSpec(num_scalar_...  14.6 us
    unnamed x33, local copies, waits for them, and re-layouts  14 us
    ppermute x7, waiting for transfers between devices, local(): a = lax.ppermute(a, 'col', forward)  13.2 us
    unnamed x8, other arithmetic  6.67 us
  transfers between devices with their start and end apart: 38, of which 15 were waited for; matrix products, arithmetic and copies ran while one was open for 19% of the time, Pallas kernels for 0%

profile of v6, /device:TPU:14, one launch (start us, length us, event | category | flops | bytes accessed | tf_op | source)
XLA Modules:
  0.0 135.0 jit_solution(16054965062516344398)
XLA Ops:
  1.7 2.5 %constant_dynamic-update-slice_fusion.14 = (bf16[3,32,2,144,128]{4,3,2,1,0:T(8,128)(2,1)}, bf16[3,4,2,144,128]{4,3,2,1,0:T(8,128)(2,1)S(1)}) fusion(bf16[144]{0:T(256)(128)(2,1)S(1)} %pad.21.clone, bf16[3,4,2,1,128]{4,3,2,1,0:T(2,128)(2,1)S(1)} %broadcast_in_dim.7, bf16[3,4,2,3,128]{4,3,2,1,0:T(4,128)(2,1)S(1)} %broadcast_in_dim.6, ...), kind=kLoop, calls=%fused_computation.48 | loop fusion | flops 3538943 | bytes 2580768
  4.2 1.6 %collective-permute-start.1 = (bf16[3,2,2,144,128]{4,3,2,1,0:T(8,128)(2,1)S(1)}, bf16[3,2,2,144,128]{4,3,2,1,0:T(8,128)(2,1)}, u32[]{:S(2)}, u32[]{:S(2)}) collective-permute-start(bf16[3,2,2,144,128]{4,3,2,1,0:T(8,128)(2,1)S(1)} %get-tuple-element.6), channel_id=1, source_target_pairs={{2,0},{4,2},{6,4},{7,6},{5,7},{3,5},{1,3},{0,1},{10,8},{12,10},{14... | collective-permute-start | bytes 1327112 | tf_op jit(solution)/shard_map/ppermute | solution.py:115
  7.8 1.3 collective-permute-start.16
  9.2 7.2 %collective-permute-done.1 = bf16[3,2,2,144,128]{4,3,2,1,0:T(8,128)(2,1)} collective-permute-done((bf16[3,2,2,144,128]{4,3,2,1,0:T(8,128)(2,1)S(1)}, bf16[3,2,2,144,128]{4,3,2,1,0:T(8,128)(2,1)}, u32[]{:S(2)}, u32[]{:S(2)}) %collective-permute-start.1) | collective-permute-done | bytes 442400 | tf_op jit(solution)/shard_map/ppermute | solution.py:115
  16.3 1.6 %collective-permute-start.3 = (bf16[3,2,2,144,128]{4,3,2,1,0:T(8,128)(2,1)}, bf16[3,2,2,144,128]{4,3,2,1,0:T(8,128)(2,1)S(1)}, u32[]{:S(2)}, u32[]{:S(2)}) collective-permute-start(bf16[3,2,2,144,128]{4,3,2,1,0:T(8,128)(2,1)} %collective-permute-done.1), channel_id=1, source_target_pairs={{2,0},{4,2},{6,4},{7,6},{5,7},{3,5},{1,3},{0,1},{10,8},{12,10},{14... | collective-permute-start | bytes 1327112 | tf_op jit(solution)/shard_map/ppermute | solution.py:115
  20.4 1.9 %constant_dynamic-update-slice_fusion.13 = bf16[3,32,2,144,128]{4,3,2,1,0:T(8,128)(2,1)} fusion(bf16[3,32,2,144,128]{4,3,2,1,0:T(8,128)(2,1)} %get-tuple-element.7, bf16[3,2,2,144,128]{4,3,2,1,0:T(8,128)(2,1)} %collective-permute-done), kind=kLoop, calls=%fused_computation.47 | loop fusion | bytes 884736
  22.3 1.8 %constant_dynamic-update-slice_fusion.12 = bf16[3,32,2,144,128]{4,3,2,1,0:T(8,128)(2,1)} fusion(bf16[3,32,2,144,128]{4,3,2,1,0:T(8,128)(2,1)} %constant_dynamic-update-slice_fusion.13, bf16[3,2,2,144,128]{4,3,2,1,0:T(8,128)(2,1)} %collective-permute-done.1), kind=kLoop, calls=%fused_computation.46 | loop fusion | bytes 884736
  27.8 1.4 %select_dynamic-update-slice_fusion.7 = bf16[3,32,144,128]{3,2,1,0:T(8,128)(2,1)S(1)} fusion(bf16[3,4,144,128]{3,2,1,0:T(8,128)(2,1)} %copy-done.6, bf16[3,4,144,128]{3,2,1,0:T(8,128)(2,1)} %copy-done.7, bf16[3,4,144,128]{3,2,1,0:T(8,128)(2,1)} %copy-done.8, pred[]{:T(512)S(6)} %eq.11, pred[]{:T(512)S(6)} %eq.10, pred[]{:T(512)S(6)} %eq.9, ...), kind=kLoop, calls=%fused_computation.16 | loop fusion | flops 1548287 | bytes 2211843
  29.2 3.3 %collective-permute-start.5 = (bf16[3,2,2,144,128]{4,3,2,1,0:T(8,128)(2,1)S(1)}, bf16[3,2,2,144,128]{4,3,2,1,0:T(8,128)(2,1)S(1)}, u32[]{:S(2)}, u32[]{:S(2)}) collective-permute-start(bf16[3,2,2,144,128]{4,3,2,1,0:T(8,128)(2,1)S(1)} %collective-permute-done.3), channel_id=1, source_target_pairs={{2,0},{4,2},{6,4},{7,6},{5,7},{3,5},{1,3},{0,1},{10,8},{12,10},{14... | collective-permute-start | bytes 1327112 | tf_op jit(solution)/shard_map/ppermute | solution.py:115
  35.7 3.0 %collective-permute-done.19 = bf16[3,4,144,128]{3,2,1,0:T(8,128)(2,1)S(1)} collective-permute-done((bf16[3,4,144,128]{3,2,1,0:T(8,128)(2,1)S(1)}, bf16[3,4,144,128]{3,2,1,0:T(8,128)(2,1)S(1)}, u32[]{:S(2)}, u32[]{:S(2)}) %collective-permute-start.19) | collective-permute-done | bytes 442400 | tf_op jit(solution)/shard_map/ppermute | solution.py:120
  38.8 1.3 collective-permute-start.22
  40.3 3.3 %collective-permute-start.7 = (bf16[3,2,2,144,128]{4,3,2,1,0:T(8,128)(2,1)S(1)}, bf16[3,2,2,144,128]{4,3,2,1,0:T(8,128)(2,1)S(1)}, u32[]{:S(2)}, u32[]{:S(2)}) collective-permute-start(bf16[3,2,2,144,128]{4,3,2,1,0:T(8,128)(2,1)S(1)} %collective-permute-done.5), channel_id=1, source_target_pairs={{2,0},{4,2},{6,4},{7,6},{5,7},{3,5},{1,3},{0,1},{10,8},{12,10},{14... | collective-permute-start | bytes 1327112 | tf_op jit(solution)/shard_map/ppermute | solution.py:115
  50.3 2.4 %collective-permute-done.7 = bf16[3,2,2,144,128]{4,3,2,1,0:T(8,128)(2,1)S(1)} collective-permute-done((bf16[3,2,2,144,128]{4,3,2,1,0:T(8,128)(2,1)S(1)}, bf16[3,2,2,144,128]{4,3,2,1,0:T(8,128)(2,1)S(1)}, u32[]{:S(2)}, u32[]{:S(2)}) %collective-permute-start.7) | collective-permute-done | bytes 442400 | tf_op jit(solution)/shard_map/ppermute | solution.py:115
  52.7 2.5 %collective-permute-start.9 = (bf16[3,2,2,144,128]{4,3,2,1,0:T(8,128)(2,1)S(1)}, bf16[3,2,2,144,128]{4,3,2,1,0:T(8,128)(2,1)S(1)}, u32[]{:S(2)}, u32[]{:S(2)}) collective-permute-start(bf16[3,2,2,144,128]{4,3,2,1,0:T(8,128)(2,1)S(1)} %collective-permute-done.7), channel_id=1, source_target_pairs={{2,0},{4,2},{6,4},{7,6},{5,7},{3,5},{1,3},{0,1},{10,8},{12,10},{14... | collective-permute-start | bytes 1327112 | tf_op jit(solution)/shard_map/ppermute | solution.py:115
  59.6 2.1 %collective-permute-done.25 = bf16[3,4,144,128]{3,2,1,0:T(8,128)(2,1)S(1)} collective-permute-done((bf16[3,4,144,128]{3,2,1,0:T(8,128)(2,1)S(1)}, bf16[3,4,144,128]{3,2,1,0:T(8,128)(2,1)S(1)}, u32[]{:S(2)}, u32[]{:S(2)}) %collective-permute-start.25) | collective-permute-done | bytes 442400 | tf_op jit(solution)/shard_map/ppermute | solution.py:120
  61.8 1.3 collective-permute-start.28
  64.6 2.5 %collective-permute-start.11 = (bf16[3,2,2,144,128]{4,3,2,1,0:T(8,128)(2,1)S(1)}, bf16[3,2,2,144,128]{4,3,2,1,0:T(8,128)(2,1)S(1)}, u32[]{:S(2)}, u32[]{:S(2)}) collective-permute-start(bf16[3,2,2,144,128]{4,3,2,1,0:T(8,128)(2,1)S(1)} %collective-permute-done.9), channel_id=1, source_target_pairs={{2,0},{4,2},{6,4},{7,6},{5,7},{3,5},{1,3},{0,1},{10,8},{12,10},{14... | collective-permute-start | bytes 1327112 | tf_op jit(solution)/shard_map/ppermute | solution.py:115
  71.2 2.8 %collective-permute-done.28 = bf16[3,4,144,128]{3,2,1,0:T(8,128)(2,1)S(1)} collective-permute-done((bf16[3,4,144,128]{3,2,1,0:T(8,128)(2,1)S(1)}, bf16[3,4,144,128]{3,2,1,0:T(8,128)(2,1)S(1)}, u32[]{:S(2)}, u32[]{:S(2)}) %collective-permute-start.28) | collective-permute-done | bytes 442400 | tf_op jit(solution)/shard_map/ppermute | solution.py:120
  76.5 3.0 %collective-permute-done.10 = bf16[3,2,2,144,128]{4,3,2,1,0:T(8,128)(2,1)S(1)} collective-permute-done((bf16[3,2,2,144,128]{4,3,2,1,0:T(8,128)(2,1)S(1)}, bf16[3,2,2,144,128]{4,3,2,1,0:T(8,128)(2,1)S(1)}, u32[]{:S(2)}, u32[]{:S(2)}) %collective-permute-start.10) | collective-permute-done | bytes 442400 | tf_op jit(solution)/shard_map/ppermute | solution.py:114
  81.0 2.4 %collective-permute-start.13 = (bf16[3,2,2,144,128]{4,3,2,1,0:T(8,128)(2,1)S(1)}, bf16[3,2,2,144,128]{4,3,2,1,0:T(8,128)(2,1)S(1)}, u32[]{:S(2)}, u32[]{:S(2)}) collective-permute-start(bf16[3,2,2,144,128]{4,3,2,1,0:T(8,128)(2,1)S(1)} %collective-permute-done.11), channel_id=1, source_target_pairs={{2,0},{4,2},{6,4},{7,6},{5,7},{3,5},{1,3},{0,1},{10,8},{12,10},{14... | collective-permute-start | bytes 1327112 | tf_op jit(solution)/shard_map/ppermute | solution.py:115
  84.3 1.4 %collective-permute-start.33 = (bf16[3,4,144,128]{3,2,1,0:T(8,128)(2,1)}, bf16[3,4,144,128]{3,2,1,0:T(8,128)(2,1)}, u32[]{:S(2)}, u32[]{:S(2)}) collective-permute-start(bf16[3,4,144,128]{3,2,1,0:T(8,128)(2,1)} %pad_maximum_fusion.6), channel_id=1, source_target_pairs={{0,16},{1,17},{10,26},{11,27},{20,4},{21,5},{30,14},{31,15}} | collective-permute-start | bytes 1327112 | tf_op jit(solution)/shard_map/ppermute | solution.py:120
  85.7 1.3 collective-permute-start.34
  88.2 3.4 %collective-permute-done.13 = bf16[3,2,2,144,128]{4,3,2,1,0:T(8,128)(2,1)S(1)} collective-permute-done((bf16[3,2,2,144,128]{4,3,2,1,0:T(8,128)(2,1)S(1)}, bf16[3,2,2,144,128]{4,3,2,1,0:T(8,128)(2,1)S(1)}, u32[]{:S(2)}, u32[]{:S(2)}) %collective-permute-start.13) | collective-permute-done | bytes 442400 | tf_op jit(solution)/shard_map/ppermute | solution.py:115
  91.6 7.2 %collective-permute-done.12 = bf16[3,2,2,144,128]{4,3,2,1,0:T(8,128)(2,1)S(1)} collective-permute-done((bf16[3,2,2,144,128]{4,3,2,1,0:T(8,128)(2,1)S(1)}, bf16[3,2,2,144,128]{4,3,2,1,0:T(8,128)(2,1)S(1)}, u32[]{:S(2)}, u32[]{:S(2)}) %collective-permute-start.12) | collective-permute-done | bytes 442400 | tf_op jit(solution)/shard_map/ppermute | solution.py:114
  99.7 1.5 %collective-permute-start.35 = (bf16[3,4,144,128]{3,2,1,0:T(8,128)(2,1)}, bf16[3,4,144,128]{3,2,1,0:T(8,128)(2,1)}, u32[]{:S(2)}, u32[]{:S(2)}) collective-permute-start(bf16[3,4,144,128]{3,2,1,0:T(8,128)(2,1)} %pad_maximum_fusion.7), channel_id=1, source_target_pairs={{0,24},{1,25},{10,2},{11,3},{20,12},{21,13},{30,22},{31,23}} | collective-permute-start | bytes 1327112 | tf_op jit(solution)/shard_map/ppermute | solution.py:120
  101.2 1.5 %collective-permute-start.36 = (bf16[3,4,144,128]{3,2,1,0:T(8,128)(2,1)}, bf16[3,4,144,128]{3,2,1,0:T(8,128)(2,1)}, u32[]{:S(2)}, u32[]{:S(2)}) collective-permute-start(bf16[3,4,144,128]{3,2,1,0:T(8,128)(2,1)} %pad_maximum_fusion.7), channel_id=1, source_target_pairs={{0,16},{1,17},{10,26},{11,27},{20,4},{21,5},{30,14},{31,15}} | collective-permute-start | bytes 1327112 | tf_op jit(solution)/shard_map/ppermute | solution.py:120
  102.6 1.3 collective-permute-start.37
  105.6 1.7 %slice.19 = bf16[96,2,1,1]{3,2,1,0:T(2,128)(2,1)} slice(bf16[96,2,144,128]{3,2,1,0:T(8,128)(2,1)} %bitcast.44), slice={[0:96], [0:2], [131:132], [0:1]} | slice | bytes 768 | tf_op jit(solution)/shard_map/slice | solution.py:129
  108.4 1.5 %select_dynamic-update-slice_fusion.1 = bf16[3,32,144,128]{3,2,1,0:T(8,128)(2,1)S(1)} fusion(bf16[3,32,144,128]{3,2,1,0:T(8,128)(2,1)S(1)} %select_dynamic-update-slice_fusion.2, bf16[3,4,144,128]{3,2,1,0:T(8,128)(2,1)} %copy-done.9, bf16[3,4,144,128]{3,2,1,0:T(8,128)(2,1)} %collective-permute-done.33, bf16[3,4,144,128]{3,2,1,0:T(8,128)(2,1)} %collective-permute-done.34, ...), kind=kLoop, calls=%fused_computation.10 | loop fusion | flops 1548288 | bytes 2211843
  109.8 6.6 %collective-permute-done.37 = bf16[3,4,144,128]{3,2,1,0:T(8,128)(2,1)} collective-permute-done((bf16[3,4,144,128]{3,2,1,0:T(8,128)(2,1)}, bf16[3,4,144,128]{3,2,1,0:T(8,128)(2,1)}, u32[]{:S(2)}, u32[]{:S(2)}) %collective-permute-start.37) | collective-permute-done | bytes 442400 | tf_op jit(solution)/shard_map/ppermute | solution.py:120
  116.5 1.4 %select_dynamic-update-slice_fusion = bf16[3,32,144,128]{3,2,1,0:T(8,128)(2,1)S(1)} fusion(bf16[3,32,144,128]{3,2,1,0:T(8,128)(2,1)S(1)} %select_dynamic-update-slice_fusion.1, bf16[3,4,144,128]{3,2,1,0:T(8,128)(2,1)} %collective-permute-done.35, bf16[3,4,144,128]{3,2,1,0:T(8,128)(2,1)} %collective-permute-done.36, ...), kind=kLoop, calls=%fused_computation.9 | loop fusion | flops 1548288 | bytes 2211843 | tf_op jit(solution)/shard_map/concatenate | solution.py:124
  120.4 14.6 %shard_map.37 = f32[2048,1024]{1,0:T(8,128)} custom-call(s32[288]{0:T(512)S(1)} %min.12.offs_ref, bf16[96,2,144,128]{3,2,1,0:T(8,128)(2,1)} %bitcast.45, bf16[96,144,128]{2,1,0:T(8,128)(2,1)S(1)} %bitcast.43), custom_call_target="tpu_custom_call" | custom-call | flops 805306368 | bytes 17825792 | tf_op jit(solution)/shard_map/pallas_call | solution.py:46
  (127 shorter events, 41.9 us)
Async XLA Ops:
  4.2 12.1 %collective-permute-start.1 = (bf16[3,2,2,144,128]{4,3,2,1,0:T(8,128)(2,1)S(1)}, bf16[3,2,2,144,128]{4,3,2,1,0:T(8,128)(2,1)}, u32[]{:S(2)}, u32[]{:S(2)}) collective-permute-start(bf16[3,2,2,144,128]{4,3,2,1,0:T(8,128)(2,1)S(1)} %get-tuple-element.6), channel_id=1, source_target_pairs={{2,0},{4,2},{6,4},{7,6},{5,7},{3,5},{1,3},{0,1},{10,8},{12,10},{14... | collective-permute-start | bytes 1327112 | tf_op jit(solution)/shard_map/ppermute | solution.py:115
  5.9 13.0 %collective-permute-start = (bf16[3,2,2,144,128]{4,3,2,1,0:T(8,128)(2,1)S(1)}, bf16[3,2,2,144,128]{4,3,2,1,0:T(8,128)(2,1)}, u32[]{:S(2)}, u32[]{:S(2)}) collective-permute-start(bf16[3,2,2,144,128]{4,3,2,1,0:T(8,128)(2,1)S(1)} %get-tuple-element.5), channel_id=1, source_target_pairs={{0,2},{2,4},{4,6},{6,7},{7,5},{5,3},{3,1},{1,0},{8,10},{10,12},{12... | collective-permute-start | bytes 1327112 | tf_op jit(solution)/shard_map/ppermute | solution.py:114
  6.4 17.7 %collective-permute-start.14 = (bf16[3,4,144,128]{3,2,1,0:T(8,128)(2,1)S(1)}, bf16[3,4,144,128]{3,2,1,0:T(8,128)(2,1)S(1)}, u32[]{:S(2)}, u32[]{:S(2)}) collective-permute-start(bf16[3,4,144,128]{3,2,1,0:T(8,128)(2,1)S(1)} %pad_maximum_fusion), channel_id=1, source_target_pairs={{0,24},{1,25},{10,2},{11,3},{20,12},{21,13},{30,22},{31,23}} | collective-permute-start | bytes 1327112 | tf_op jit(solution)/shard_map/ppermute | solution.py:120
  7.1 17.7 %collective-permute-start.15 = (bf16[3,4,144,128]{3,2,1,0:T(8,128)(2,1)S(1)}, bf16[3,4,144,128]{3,2,1,0:T(8,128)(2,1)S(1)}, u32[]{:S(2)}, u32[]{:S(2)}) collective-permute-start(bf16[3,4,144,128]{3,2,1,0:T(8,128)(2,1)S(1)} %pad_maximum_fusion), channel_id=1, source_target_pairs={{0,16},{1,17},{10,26},{11,27},{20,4},{21,5},{30,14},{31,15}} | collective-permute-start | bytes 1327112 | tf_op jit(solution)/shard_map/ppermute | solution.py:120
  7.8 17.8 %collective-permute-start.16 = (bf16[3,4,144,128]{3,2,1,0:T(8,128)(2,1)S(1)}, bf16[3,4,144,128]{3,2,1,0:T(8,128)(2,1)S(1)}, u32[]{:S(2)}, u32[]{:S(2)}) collective-permute-start(bf16[3,4,144,128]{3,2,1,0:T(8,128)(2,1)S(1)} %pad_maximum_fusion), channel_id=1, source_target_pairs={{0,8},{1,9},{10,18},{11,19},{20,28},{21,29},{30,6},{31,7}} | collective-permute-start | bytes 1327112 | tf_op jit(solution)/shard_map/ppermute | solution.py:120
  16.3 12.9 %collective-permute-start.3 = (bf16[3,2,2,144,128]{4,3,2,1,0:T(8,128)(2,1)}, bf16[3,2,2,144,128]{4,3,2,1,0:T(8,128)(2,1)S(1)}, u32[]{:S(2)}, u32[]{:S(2)}) collective-permute-start(bf16[3,2,2,144,128]{4,3,2,1,0:T(8,128)(2,1)} %collective-permute-done.1), channel_id=1, source_target_pairs={{2,0},{4,2},{6,4},{7,6},{5,7},{3,5},{1,3},{0,1},{10,8},{12,10},{14... | collective-permute-start | bytes 1327112 | tf_op jit(solution)/shard_map/ppermute | solution.py:115
  18.9 13.6 %collective-permute-start.2 = (bf16[3,2,2,144,128]{4,3,2,1,0:T(8,128)(2,1)}, bf16[3,2,2,144,128]{4,3,2,1,0:T(8,128)(2,1)S(1)}, u32[]{:S(2)}, u32[]{:S(2)}) collective-permute-start(bf16[3,2,2,144,128]{4,3,2,1,0:T(8,128)(2,1)} %collective-permute-done), channel_id=1, source_target_pairs={{0,2},{2,4},{4,6},{6,7},{7,5},{5,3},{3,1},{1,0},{8,10},{10,12},{12... | collective-permute-start | bytes 1327112 | tf_op jit(solution)/shard_map/ppermute | solution.py:114
  26.5 12.3 %collective-permute-start.19 = (bf16[3,4,144,128]{3,2,1,0:T(8,128)(2,1)S(1)}, bf16[3,4,144,128]{3,2,1,0:T(8,128)(2,1)S(1)}, u32[]{:S(2)}, u32[]{:S(2)}) collective-permute-start(bf16[3,4,144,128]{3,2,1,0:T(8,128)(2,1)S(1)} %pad_maximum_fusion.1), channel_id=1, source_target_pairs={{0,8},{1,9},{10,18},{11,19},{20,28},{21,29},{30,6},{31,7}} | collective-permute-start | bytes 1327112 | tf_op jit(solution)/shard_map/ppermute | solution.py:120
  29.2 11.1 %collective-permute-start.5 = (bf16[3,2,2,144,128]{4,3,2,1,0:T(8,128)(2,1)S(1)}, bf16[3,2,2,144,128]{4,3,2,1,0:T(8,128)(2,1)S(1)}, u32[]{:S(2)}, u32[]{:S(2)}) collective-permute-start(bf16[3,2,2,144,128]{4,3,2,1,0:T(8,128)(2,1)S(1)} %collective-permute-done.3), channel_id=1, source_target_pairs={{2,0},{4,2},{6,4},{7,6},{5,7},{3,5},{1,3},{0,1},{10,8},{12,10},{14... | collective-permute-start | bytes 1327112 | tf_op jit(solution)/shard_map/ppermute | solution.py:115
  32.5 12.3 %collective-permute-start.4 = (bf16[3,2,2,144,128]{4,3,2,1,0:T(8,128)(2,1)S(1)}, bf16[3,2,2,144,128]{4,3,2,1,0:T(8,128)(2,1)S(1)}, u32[]{:S(2)}, u32[]{:S(2)}) collective-permute-start(bf16[3,2,2,144,128]{4,3,2,1,0:T(8,128)(2,1)S(1)} %collective-permute-done.2), channel_id=1, source_target_pairs={{0,2},{2,4},{4,6},{6,7},{7,5},{5,3},{3,1},{1,0},{8,10},{10,12},{12... | collective-permute-start | bytes 1327112 | tf_op jit(solution)/shard_map/ppermute | solution.py:114
  34.4 12.2 %collective-permute-start.20 = (bf16[3,4,144,128]{3,2,1,0:T(8,128)(2,1)S(1)}, bf16[3,4,144,128]{3,2,1,0:T(8,128)(2,1)S(1)}, u32[]{:S(2)}, u32[]{:S(2)}) collective-permute-start(bf16[3,4,144,128]{3,2,1,0:T(8,128)(2,1)S(1)} %pad_maximum_fusion.2), channel_id=1, source_target_pairs={{0,24},{1,25},{10,2},{11,3},{20,12},{21,13},{30,22},{31,23}} | collective-permute-start | bytes 1327112 | tf_op jit(solution)/shard_map/ppermute | solution.py:120
  35.1 12.2 %collective-permute-start.21 = (bf16[3,4,144,128]{3,2,1,0:T(8,128)(2,1)S(1)}, bf16[3,4,144,128]{3,2,1,0:T(8,128)(2,1)S(1)}, u32[]{:S(2)}, u32[]{:S(2)}) collective-permute-start(bf16[3,4,144,128]{3,2,1,0:T(8,128)(2,1)S(1)} %pad_maximum_fusion.2), channel_id=1, source_target_pairs={{0,16},{1,17},{10,26},{11,27},{20,4},{21,5},{30,14},{31,15}} | collective-permute-start | bytes 1327112 | tf_op jit(solution)/shard_map/ppermute | solution.py:120
  40.3 12.4 %collective-permute-start.7 = (bf16[3,2,2,144,128]{4,3,2,1,0:T(8,128)(2,1)S(1)}, bf16[3,2,2,144,128]{4,3,2,1,0:T(8,128)(2,1)S(1)}, u32[]{:S(2)}, u32[]{:S(2)}) collective-permute-start(bf16[3,2,2,144,128]{4,3,2,1,0:T(8,128)(2,1)S(1)} %collective-permute-done.5), channel_id=1, source_target_pairs={{2,0},{4,2},{6,4},{7,6},{5,7},{3,5},{1,3},{0,1},{10,8},{12,10},{14... | collective-permute-start | bytes 1327112 | tf_op jit(solution)/shard_map/ppermute | solution.py:115
  44.8 11.4 %collective-permute-start.6 = (bf16[3,2,2,144,128]{4,3,2,1,0:T(8,128)(2,1)S(1)}, bf16[3,2,2,144,128]{4,3,2,1,0:T(8,128)(2,1)S(1)}, u32[]{:S(2)}, u32[]{:S(2)}) collective-permute-start(bf16[3,2,2,144,128]{4,3,2,1,0:T(8,128)(2,1)S(1)} %collective-permute-done.4), channel_id=1, source_target_pairs={{0,2},{2,4},{4,6},{6,7},{7,5},{5,3},{3,1},{1,0},{8,10},{10,12},{12... | collective-permute-start | bytes 1327112 | tf_op jit(solution)/shard_map/ppermute | solution.py:114
  46.6 11.7 %collective-permute-start.23 = (bf16[3,4,144,128]{3,2,1,0:T(8,128)(2,1)S(1)}, bf16[3,4,144,128]{3,2,1,0:T(8,128)(2,1)S(1)}, u32[]{:S(2)}, u32[]{:S(2)}) collective-permute-start(bf16[3,4,144,128]{3,2,1,0:T(8,128)(2,1)S(1)} %pad_maximum_fusion.3), channel_id=1, source_target_pairs={{0,24},{1,25},{10,2},{11,3},{20,12},{21,13},{30,22},{31,23}} | collective-permute-start | bytes 1327112 | tf_op jit(solution)/shard_map/ppermute | solution.py:120
  47.3 11.7 %collective-permute-start.24 = (bf16[3,4,144,128]{3,2,1,0:T(8,128)(2,1)S(1)}, bf16[3,4,144,128]{3,2,1,0:T(8,128)(2,1)S(1)}, u32[]{:S(2)}, u32[]{:S(2)}) collective-permute-start(bf16[3,4,144,128]{3,2,1,0:T(8,128)(2,1)S(1)} %pad_maximum_fusion.3), channel_id=1, source_target_pairs={{0,16},{1,17},{10,26},{11,27},{20,4},{21,5},{30,14},{31,15}} | collective-permute-start | bytes 1327112 | tf_op jit(solution)/shard_map/ppermute | solution.py:120
  48.8 13.0 %collective-permute-start.25 = (bf16[3,4,144,128]{3,2,1,0:T(8,128)(2,1)S(1)}, bf16[3,4,144,128]{3,2,1,0:T(8,128)(2,1)S(1)}, u32[]{:S(2)}, u32[]{:S(2)}) collective-permute-start(bf16[3,4,144,128]{3,2,1,0:T(8,128)(2,1)S(1)} %pad_maximum_fusion.3), channel_id=1, source_target_pairs={{0,8},{1,9},{10,18},{11,19},{20,28},{21,29},{30,6},{31,7}} | collective-permute-start | bytes 1327112 | tf_op jit(solution)/shard_map/ppermute | solution.py:120
  52.7 11.8 %collective-permute-start.9 = (bf16[3,2,2,144,128]{4,3,2,1,0:T(8,128)(2,1)S(1)}, bf16[3,2,2,144,128]{4,3,2,1,0:T(8,128)(2,1)S(1)}, u32[]{:S(2)}, u32[]{:S(2)}) collective-permute-start(bf16[3,2,2,144,128]{4,3,2,1,0:T(8,128)(2,1)S(1)} %collective-permute-done.7), channel_id=1, source_target_pairs={{2,0},{4,2},{6,4},{7,6},{5,7},{3,5},{1,3},{0,1},{10,8},{12,10},{14... | collective-permute-start | bytes 1327112 | tf_op jit(solution)/shard_map/ppermute | solution.py:115
  56.2 11.8 %collective-permute-start.8 = (bf16[3,2,2,144,128]{4,3,2,1,0:T(8,128)(2,1)S(1)}, bf16[3,2,2,144,128]{4,3,2,1,0:T(8,128)(2,1)S(1)}, u32[]{:S(2)}, u32[]{:S(2)}) collective-permute-start(bf16[3,2,2,144,128]{4,3,2,1,0:T(8,128)(2,1)S(1)} %collective-permute-done.6), channel_id=1, source_target_pairs={{0,2},{2,4},{4,6},{6,7},{7,5},{5,3},{3,1},{1,0},{8,10},{10,12},{12... | collective-permute-start | bytes 1327112 | tf_op jit(solution)/shard_map/ppermute | solution.py:114
  58.2 11.6 %collective-permute-start.26 = (bf16[3,4,144,128]{3,2,1,0:T(8,128)(2,1)S(1)}, bf16[3,4,144,128]{3,2,1,0:T(8,128)(2,1)S(1)}, u32[]{:S(2)}, u32[]{:S(2)}) collective-permute-start(bf16[3,4,144,128]{3,2,1,0:T(8,128)(2,1)S(1)} %pad_maximum_fusion.4), channel_id=1, source_target_pairs={{0,24},{1,25},{10,2},{11,3},{20,12},{21,13},{30,22},{31,23}} | collective-permute-start | bytes 1327112 | tf_op jit(solution)/shard_map/ppermute | solution.py:120
  58.9 11.5 %collective-permute-start.27 = (bf16[3,4,144,128]{3,2,1,0:T(8,128)(2,1)S(1)}, bf16[3,4,144,128]{3,2,1,0:T(8,128)(2,1)S(1)}, u32[]{:S(2)}, u32[]{:S(2)}) collective-permute-start(bf16[3,4,144,128]{3,2,1,0:T(8,128)(2,1)S(1)} %pad_maximum_fusion.4), channel_id=1, source_target_pairs={{0,16},{1,17},{10,26},{11,27},{20,4},{21,5},{30,14},{31,15}} | collective-permute-start | bytes 1327112 | tf_op jit(solution)/shard_map/ppermute | solution.py:120
  61.8 12.2 %collective-permute-start.28 = (bf16[3,4,144,128]{3,2,1,0:T(8,128)(2,1)S(1)}, bf16[3,4,144,128]{3,2,1,0:T(8,128)(2,1)S(1)}, u32[]{:S(2)}, u32[]{:S(2)}) collective-permute-start(bf16[3,4,144,128]{3,2,1,0:T(8,128)(2,1)S(1)} %pad_maximum_fusion.4), channel_id=1, source_target_pairs={{0,8},{1,9},{10,18},{11,19},{20,28},{21,29},{30,6},{31,7}} | collective-permute-start | bytes 1327112 | tf_op jit(solution)/shard_map/ppermute | solution.py:120
  64.6 11.9 %collective-permute-start.11 = (bf16[3,2,2,144,128]{4,3,2,1,0:T(8,128)(2,1)S(1)}, bf16[3,2,2,144,128]{4,3,2,1,0:T(8,128)(2,1)S(1)}, u32[]{:S(2)}, u32[]{:S(2)}) collective-permute-start(bf16[3,2,2,144,128]{4,3,2,1,0:T(8,128)(2,1)S(1)} %collective-permute-done.9), channel_id=1, source_target_pairs={{2,0},{4,2},{6,4},{7,6},{5,7},{3,5},{1,3},{0,1},{10,8},{12,10},{14... | collective-permute-start | bytes 1327112 | tf_op jit(solution)/shard_map/ppermute | solution.py:115
  68.0 11.5 %collective-permute-start.10 = (bf16[3,2,2,144,128]{4,3,2,1,0:T(8,128)(2,1)S(1)}, bf16[3,2,2,144,128]{4,3,2,1,0:T(8,128)(2,1)S(1)}, u32[]{:S(2)}, u32[]{:S(2)}) collective-permute-start(bf16[3,2,2,144,128]{4,3,2,1,0:T(8,128)(2,1)S(1)} %collective-permute-done.8), channel_id=1, source_target_pairs={{0,2},{2,4},{4,6},{6,7},{7,5},{5,3},{3,1},{1,0},{8,10},{10,12},{12... | collective-permute-start | bytes 1327112 | tf_op jit(solution)/shard_map/ppermute | solution.py:114
  69.8 14.5 %collective-permute-start.29 = (bf16[3,4,144,128]{3,2,1,0:T(8,128)(2,1)S(1)}, bf16[3,4,144,128]{3,2,1,0:T(8,128)(2,1)S(1)}, u32[]{:S(2)}, u32[]{:S(2)}) collective-permute-start(bf16[3,4,144,128]{3,2,1,0:T(8,128)(2,1)S(1)} %pad_maximum_fusion.5), channel_id=1, source_target_pairs={{0,24},{1,25},{10,2},{11,3},{20,12},{21,13},{30,22},{31,23}} | collective-permute-start | bytes 1327112 | tf_op jit(solution)/shard_map/ppermute | solution.py:120
  70.5 15.2 %collective-permute-start.30 = (bf16[3,4,144,128]{3,2,1,0:T(8,128)(2,1)S(1)}, bf16[3,4,144,128]{3,2,1,0:T(8,128)(2,1)S(1)}, u32[]{:S(2)}, u32[]{:S(2)}) collective-permute-start(bf16[3,4,144,128]{3,2,1,0:T(8,128)(2,1)S(1)} %pad_maximum_fusion.5), channel_id=1, source_target_pairs={{0,16},{1,17},{10,26},{11,27},{20,4},{21,5},{30,14},{31,15}} | collective-permute-start | bytes 1327112 | tf_op jit(solution)/shard_map/ppermute | solution.py:120
  74.0 13.0 %collective-permute-start.31 = (bf16[3,4,144,128]{3,2,1,0:T(8,128)(2,1)S(1)}, bf16[3,4,144,128]{3,2,1,0:T(8,128)(2,1)S(1)}, u32[]{:S(2)}, u32[]{:S(2)}) collective-permute-start(bf16[3,4,144,128]{3,2,1,0:T(8,128)(2,1)S(1)} %pad_maximum_fusion.5), channel_id=1, source_target_pairs={{0,8},{1,9},{10,18},{11,19},{20,28},{21,29},{30,6},{31,7}} | collective-permute-start | bytes 1327112 | tf_op jit(solution)/shard_map/ppermute | solution.py:120
  80.3 22.3 %collective-permute-start.32 = (bf16[3,4,144,128]{3,2,1,0:T(8,128)(2,1)}, bf16[3,4,144,128]{3,2,1,0:T(8,128)(2,1)S(1)}, u32[]{:S(2)}, u32[]{:S(2)}) collective-permute-start(bf16[3,4,144,128]{3,2,1,0:T(8,128)(2,1)} %pad_maximum_fusion.6), channel_id=1, source_target_pairs={{0,24},{1,25},{10,2},{11,3},{20,12},{21,13},{30,22},{31,23}} | collective-permute-start | bytes 1327112 | tf_op jit(solution)/shard_map/ppermute | solution.py:120
  84.3 24.1 %collective-permute-start.33 = (bf16[3,4,144,128]{3,2,1,0:T(8,128)(2,1)}, bf16[3,4,144,128]{3,2,1,0:T(8,128)(2,1)}, u32[]{:S(2)}, u32[]{:S(2)}) collective-permute-start(bf16[3,4,144,128]{3,2,1,0:T(8,128)(2,1)} %pad_maximum_fusion.6), channel_id=1, source_target_pairs={{0,16},{1,17},{10,26},{11,27},{20,4},{21,5},{30,14},{31,15}} | collective-permute-start | bytes 1327112 | tf_op jit(solution)/shard_map/ppermute | solution.py:120
  85.7 22.6 %collective-permute-start.34 = (bf16[3,4,144,128]{3,2,1,0:T(8,128)(2,1)}, bf16[3,4,144,128]{3,2,1,0:T(8,128)(2,1)}, u32[]{:S(2)}, u32[]{:S(2)}) collective-permute-start(bf16[3,4,144,128]{3,2,1,0:T(8,128)(2,1)} %pad_maximum_fusion.6), channel_id=1, source_target_pairs={{0,8},{1,9},{10,18},{11,19},{20,28},{21,29},{30,6},{31,7}} | collective-permute-start | bytes 1327112 | tf_op jit(solution)/shard_map/ppermute | solution.py:120
  87.0 11.8 %collective-permute-start.12 = (bf16[3,2,2,144,128]{4,3,2,1,0:T(8,128)(2,1)S(1)}, bf16[3,2,2,144,128]{4,3,2,1,0:T(8,128)(2,1)S(1)}, u32[]{:S(2)}, u32[]{:S(2)}) collective-permute-start(bf16[3,2,2,144,128]{4,3,2,1,0:T(8,128)(2,1)S(1)} %collective-permute-done.10), channel_id=1, source_target_pairs={{0,2},{2,4},{4,6},{6,7},{7,5},{5,3},{3,1},{1,0},{8,10},{10,12},{12... | collective-permute-start | bytes 1327112 | tf_op jit(solution)/shard_map/ppermute | solution.py:114
  102.6 13.8 %collective-permute-start.37 = (bf16[3,4,144,128]{3,2,1,0:T(8,128)(2,1)}, bf16[3,4,144,128]{3,2,1,0:T(8,128)(2,1)}, u32[]{:S(2)}, u32[]{:S(2)}) collective-permute-start(bf16[3,4,144,128]{3,2,1,0:T(8,128)(2,1)} %pad_maximum_fusion.7), channel_id=1, source_target_pairs={{0,8},{1,9},{10,18},{11,19},{20,28},{21,29},{30,6},{31,7}} | collective-permute-start | bytes 1327112 | tf_op jit(solution)/shard_map/ppermute | solution.py:120
  (16 other events, 130.4 us)

commit v7 on v6

v7 whole, which is shorter than its diff:
```python
import functools

import jax
import jax.numpy as jnp
from jax import lax
from jax.experimental import pallas as pl
from jax.experimental.pallas import tpu as pltpu
from jax.sharding import PartitionSpec as P

IBS = 8
CHUNK = 8
META = 16


def gram_kernel(offs_ref, *refs, pieces, halves, local_slots, blk):
    o_ref = refs[-1]
    w_refs, c_refs = refs[:pieces], refs[pieces:-1]
    p = pl.program_id(0)

    @pl.when(p == 0)
    def _():
        o_ref[...] = jnp.zeros_like(o_ref)

    stride = local_slots + 1
    for k in range(pieces):
        for h in range(halves):
            g = (p * pieces + k) * halves + h
            w_ref = w_refs[k]
            meta = w_ref[0, h, 0, blk : blk + META].astype(jnp.float32)
            w = meta[0:1] + meta[1:2] + meta[2:3]
            lhs = jnp.concatenate(
                [
                    (w_ref[0, h, s, :blk].astype(jnp.float32).T * w).astype(jnp.bfloat16)
                    for s in range(local_slots)
                ],
                axis=0,
            )
            rhs = c_refs[k // 2][0, (k % 2) * halves + h, :blk]
            prod = jnp.dot(lhs, rhs, preferred_element_type=jnp.float32)
            col = pl.multiple_of(offs_ref[g * stride + local_slots] * blk, blk)
            for s in range(local_slots):
                row = pl.multiple_of((s * IBS + offs_ref[g * stride + s]) * blk, blk)
                o_ref[pl.ds(row, blk), pl.ds(col, blk)] += prod[s * blk : (s + 1) * blk]


def gram_call(offs, w_pieces, c_pieces):
    panels, halves, local_slots, rows, blk = w_pieces[0].shape
    pieces = len(w_pieces)
    kernel = functools.partial(
        gram_kernel, pieces=pieces, halves=halves, local_slots=local_slots, blk=blk
    )
    out_rows, out_cols = local_slots * IBS * blk, IBS * blk
    n = panels * pieces * halves
    w_spec = pl.BlockSpec((1, halves, local_slots, rows, blk), lambda i, o: (i, 0, 0, 0, 0))
    c_spec = pl.BlockSpec((1, 2 * halves, rows, blk), lambda i, o: (i, 0, 0, 0))
    return pl.pallas_call(
        kernel,
        grid_spec=pltpu.PrefetchScalarGridSpec(
            num_scalar_prefetch=1,
            grid=(panels,),
            in_specs=[w_spec] * pieces + [c_spec] * len(c_pieces),
            out_specs=pl.BlockSpec((out_rows, out_cols), lambda i, o: (0, 0)),
        ),
        out_shape=jax.ShapeDtypeStruct((out_rows, out_cols), jnp.float32),
        compiler_params=pltpu.CompilerParams(
            dimension_semantics=("arbitrary",), vmem_limit_bytes=56 * 1024 * 1024
        ),
        cost_estimate=pl.CostEstimate(
            flops=2 * n * local_slots * blk * blk * blk,
            transcendentals=0,
            bytes_accessed=n * (local_slots + 1) * blk * blk * 2 + out_rows * out_cols * 4,
        ),
    )(offs, *w_pieces, *c_pieces)


def with_meta(panel_blocks, user_weights, slot_offset):
    panels, users, local_slots, blk, _ = panel_blocks.shape
    hi = lax.reduce_precision(user_weights, exponent_bits=8, mantissa_bits=7)
    rest = user_weights - hi
    mid = lax.reduce_precision(rest, exponent_bits=8, mantissa_bits=7)
    low = rest - mid
    weight_rows = jnp.stack([hi, mid, low], axis=2).astype(jnp.bfloat16)[:, :, None]
    weight_rows = jnp.broadcast_to(weight_rows, (panels, users, local_slots, 3, blk))
    offset_rows = jnp.broadcast_to(
        slot_offset.astype(jnp.bfloat16)[..., None, None], (panels, users, local_slots, 1, blk)
    )
    pad = jnp.zeros((panels, users, local_slots, META - 4, blk), jnp.bfloat16)
    return jnp.concatenate([panel_blocks, weight_rows, offset_rows, pad], axis=3)


def local(panel_blocks, user_weights, slot_offset, *, nrow, ncol):
    panels, _, local_slots, blk, _ = panel_blocks.shape
    r = lax.axis_index("row")
    c = lax.axis_index("col")
    x = with_meta(panel_blocks, user_weights, slot_offset)

    outer = ncol // 2
    cycle = [a * 2 for a in range(outer)] + [a * 2 + 1 for a in reversed(range(outer))]
    forward = [(cycle[i], cycle[(i + 1) % ncol]) for i in range(ncol)]
    backward = [(b, a) for a, b in forward]

    src = c // local_slots
    slot = c % local_slots
    nx = nrow // 2
    up = (r - src + nrow) % nrow
    is_s, is_p, is_d1 = up == 0, r == src + 1 - 2 * (src % 2), (up % 2 == 0) & (up != 0)
    chip_step = up // 2

    def send(v, pairs):
        return lax.ppermute(v, ("row", "col"), [(a * ncol + cc, b * ncol + cc) for a, b, cc in pairs])

    first_hop = []
    for cc in range(ncol):
        s0 = cc // local_slots
        first_hop.append((s0, s0 ^ 1, cc))
        first_hop += [((s0 + 2 * j) % nrow, ((s0 + 2 * j) % nrow) ^ 1, cc) for j in range(1, nx)]
    cross = [[(cc // local_slots, (cc // local_slots + 2 * j) % nrow, cc) for cc in range(ncol)] for j in range(1, nx)]

    def pick_slot(piece):
        return lax.dynamic_index_in_dim(piece, slot, axis=2, keepdims=False)

    half = x.shape[1] // 2
    a, b = x[:, :half], x[:, half:]
    pieces, owns, hops, crossed = [], [], [], []
    forwarded = None
    for step in range(ncol + 1):
        if step < ncol:
            if step:
                a = lax.ppermute(a, "col", forward)
                b = lax.ppermute(b, "col", backward)
            pieces += [a, b]
            own = jnp.concatenate([pick_slot(a), pick_slot(b)], axis=1)
            owns.append(own)
            operand = own if forwarded is None else jnp.where(is_s, own, forwarded)
        else:
            operand = forwarded
        hops.append(send(operand, first_hop))
        if step < ncol:
            got = None
            for j, pairs in enumerate(cross, start=1):
                v = send(own, pairs)
                got = v if got is None else jnp.where(chip_step == j, v, got)
            crossed.append(got)
            forwarded = got

    columns = [
        jnp.where(is_s, owns[k], jnp.where(is_p, hops[k], jnp.where(is_d1, crossed[k], hops[k + 1])))
        for k in range(ncol)
    ]

    w_offs = jnp.stack([piece[:, :, :, blk + 3, 0] for piece in pieces], axis=1)
    c_offs = jnp.stack(
        [columns[k // 2][:, (k % 2) * half : (k % 2 + 1) * half, blk + 3, 0] for k in range(2 * ncol)],
        axis=1,
    )
    offs = jnp.concatenate([w_offs, c_offs[..., None]], axis=3)
    offs = jnp.clip(offs.astype(jnp.int32), 0, IBS - 1).reshape(-1)
    return gram_call(offs, pieces, columns)


def solution(mesh):
    nrow, ncol = mesh.shape["row"], mesh.shape["col"]
    return jax.shard_map(
        functools.partial(local, nrow=nrow, ncol=ncol),
        mesh=mesh,
        in_specs=(P(None, "col", "row", None, None), P(None, "col", None), P(None, "col", "row")),
        out_specs=P("row", "col"),
        check_vma=False,
    )
```

time: 136 us -> 179 us (1.32)
  the two profiles are of different devices: /device:TPU:14 before, /device:TPU:0 now
where the time goes in v7:
time: 179 us; the launch traced here: 178 us
  starting transfers between devices  58.3 us (33%)
  waiting for transfers between devices  51.3 us (29%)
  local copies, waits for them, and re-layouts  41.5 us (23%)
  other arithmetic  14.3 us (8%)
  Pallas kernels  11.8 us (7%)
    ppermute x17, starting transfers between devices, send(): lax.ppermute(v, ('row', 'col'), [(a * ncol + cc, b * ncol + cc) for a, b,...  43.2 us
    ppermute x7, waiting for transfers between devices, local(): a = lax.ppermute(a, 'col', forward)  41.3 us
    pallas_call x1, Pallas kernels, gram_call(): pl.pallas_call(kernel, grid_spec=pltpu.PrefetchScalarGridSpec(num_scalar_...  11.8 us
    ppermute x7, starting transfers between devices, local(): b = lax.ppermute(b, 'col', backward)  11.3 us
    slice x31, local copies, waits for them, and re-layouts, local(): w_offs = jnp.stack([piece[:, :, :, blk + 3, 0] for piece in pieces], axis=1)  10.8 us
    squeeze x15, local copies, waits for them, and re-layouts, pick_slot(): return lax.dynamic_index_in_dim(piece, slot, axis=2, keepdims=False)  9.1 us
    unnamed x97, local copies, waits for them, and re-layouts  8.71 us
    another operation x17, local copies, waits for them, and re-layouts, local(): jnp.stack([columns[k // 2][:, k % 2 * half:(k % 2 + 1) * half, blk + 3, 0...  8.39 us
  transfers between devices with their start and end apart: 31, of which 13 were waited for; matrix products, arithmetic and copies ran while one was open for 24% of the time, Pallas kernels for 0%

profile of v7, /device:TPU:0, one launch (start us, length us, event | category | flops | bytes accessed | tf_op | source)
XLA Modules:
  0.0 178.0 jit_solution(4687659081435071975)
XLA Ops:
  4.2 4.9 %collective-permute-start.15 = (bf16[3,4,144,128]{3,2,1,0:T(8,128)(2,1)}, bf16[3,4,144,128]{3,2,1,0:T(8,128)(2,1)S(1)}, u32[]{:S(2)}, u32[]{:S(2)}) collective-permute-start(bf16[3,4,144,128]{3,2,1,0:T(8,128)(2,1)} %pad_maximum_fusion), channel_id=1, source_target_pairs={{0,16},{1,17},{10,26},{11,27},{20,4},{21,5},{30,14},{31,15}} | collective-permute-start | bytes 1327112 | tf_op jit(solution)/shard_map/ppermute | solution.py:110
  9.1 2.1 %collective-permute-start.14 = (bf16[3,4,144,128]{3,2,1,0:T(8,128)(2,1)}, bf16[3,4,144,128]{3,2,1,0:T(8,128)(2,1)}, u32[]{:S(2)}, u32[]{:S(2)}) collective-permute-start(bf16[3,4,144,128]{3,2,1,0:T(8,128)(2,1)} %pad_maximum_fusion), channel_id=1, source_target_pairs={{0,8},{16,24},{1,9},{17,25},{10,2},{26,18},{11,3},{27,19},{20,28},... | collective-permute-start | bytes 1327112 | tf_op jit(solution)/shard_map/ppermute | solution.py:110
  11.1 2.0 %collective-permute-start.1 = (bf16[3,2,2,144,128]{4,3,2,1,0:T(8,128)(2,1)S(1)}, bf16[3,2,2,144,128]{4,3,2,1,0:T(8,128)(2,1)S(1)}, u32[]{:S(2)}, u32[]{:S(2)}) collective-permute-start(bf16[3,2,2,144,128]{4,3,2,1,0:T(8,128)(2,1)S(1)} %get-tuple-element.6.refs_1_), channel_id=1, source_target_pairs={{2,0},{4,2},{6,4},{7,6},{5,7},{3,5},{1,3},{0,1},{10,8},{12,10},{14... | collective-permute-start | bytes 1327112 | tf_op jit(solution)/shard_map/ppermute | solution.py:130
  14.6 6.9 %collective-permute-done.refs_2_ = bf16[3,2,2,144,128]{4,3,2,1,0:T(8,128)(2,1)S(1)} collective-permute-done((bf16[3,2,2,144,128]{4,3,2,1,0:T(8,128)(2,1)S(1)}, bf16[3,2,2,144,128]{4,3,2,1,0:T(8,128)(2,1)S(1)}, u32[]{:S(2)}, u32[]{:S(2)}) %collective-permute-start) | collective-permute-done | bytes 442400 | tf_op jit(solution)/shard_map/ppermute | solution.py:129
  21.7 2.4 %collective-permute-done.1.refs_3_ = bf16[3,2,2,144,128]{4,3,2,1,0:T(8,128)(2,1)S(1)} collective-permute-done((bf16[3,2,2,144,128]{4,3,2,1,0:T(8,128)(2,1)S(1)}, bf16[3,2,2,144,128]{4,3,2,1,0:T(8,128)(2,1)S(1)}, u32[]{:S(2)}, u32[]{:S(2)}) %collective-permute-start.1) | collective-permute-done | bytes 442400 | tf_op jit(solution)/shard_map/ppermute | solution.py:130
  25.2 2.2 %collective-permute-start.17 = (bf16[3,4,144,128]{3,2,1,0:T(8,128)(2,1)}, bf16[3,4,144,128]{3,2,1,0:T(8,128)(2,1)S(1)}, u32[]{:S(2)}, u32[]{:S(2)}) collective-permute-start(bf16[3,4,144,128]{3,2,1,0:T(8,128)(2,1)} %get-tuple-element.41), channel_id=1, source_target_pairs={{0,16},{1,17},{10,26},{11,27},{20,4},{21,5},{30,14},{31,15}} | collective-permute-start | bytes 1327112 | tf_op jit(solution)/shard_map/ppermute | solution.py:110
  27.5 2.1 %collective-permute-start.16 = (bf16[3,4,144,128]{3,2,1,0:T(8,128)(2,1)}, bf16[3,4,144,128]{3,2,1,0:T(8,128)(2,1)}, u32[]{:S(2)}, u32[]{:S(2)}) collective-permute-start(bf16[3,4,144,128]{3,2,1,0:T(8,128)(2,1)} %get-tuple-element.42), channel_id=1, source_target_pairs={{0,8},{16,24},{1,9},{17,25},{10,2},{26,18},{11,3},{27,19},{20,28},... | collective-permute-start | bytes 1327112 | tf_op jit(solution)/shard_map/ppermute | solution.py:110
  29.6 2.0 %collective-permute-start.3 = (bf16[3,2,2,144,128]{4,3,2,1,0:T(8,128)(2,1)S(1)}, bf16[3,2,2,144,128]{4,3,2,1,0:T(8,128)(2,1)}, u32[]{:S(2)}, u32[]{:S(2)}) collective-permute-start(bf16[3,2,2,144,128]{4,3,2,1,0:T(8,128)(2,1)S(1)} %collective-permute-done.1.refs_3_), channel_id=1, source_target_pairs={{2,0},{4,2},{6,4},{7,6},{5,7},{3,5},{1,3},{0,1},{10,8},{12,10},{14... | collective-permute-start | bytes 1327112 | tf_op jit(solution)/shard_map/ppermute | solution.py:130
  32.7 6.6 %collective-permute-done.2.refs_4_ = bf16[3,2,2,144,128]{4,3,2,1,0:T(8,128)(2,1)S(1)} collective-permute-done((bf16[3,2,2,144,128]{4,3,2,1,0:T(8,128)(2,1)S(1)}, bf16[3,2,2,144,128]{4,3,2,1,0:T(8,128)(2,1)S(1)}, u32[]{:S(2)}, u32[]{:S(2)}) %collective-permute-start.2) | collective-permute-done | bytes 442400 | tf_op jit(solution)/shard_map/ppermute | solution.py:129
  39.5 1.9 %collective-permute-done.3.refs_5_ = bf16[3,2,2,144,128]{4,3,2,1,0:T(8,128)(2,1)} collective-permute-done((bf16[3,2,2,144,128]{4,3,2,1,0:T(8,128)(2,1)S(1)}, bf16[3,2,2,144,128]{4,3,2,1,0:T(8,128)(2,1)}, u32[]{:S(2)}, u32[]{:S(2)}) %collective-permute-start.3) | collective-permute-done | bytes 442400 | tf_op jit(solution)/shard_map/ppermute | solution.py:130
  46.0 1.7 collective-permute-start.5
  48.8 7.5 %collective-permute-done.4.refs_6_ = bf16[3,2,2,144,128]{4,3,2,1,0:T(8,128)(2,1)S(1)} collective-permute-done((bf16[3,2,2,144,128]{4,3,2,1,0:T(8,128)(2,1)S(1)}, bf16[3,2,2,144,128]{4,3,2,1,0:T(8,128)(2,1)S(1)}, u32[]{:S(2)}, u32[]{:S(2)}) %collective-permute-start.4) | collective-permute-done | bytes 442400 | tf_op jit(solution)/shard_map/ppermute | solution.py:129
  56.3 4.8 %collective-permute-start.19 = (bf16[3,4,144,128]{3,2,1,0:T(8,128)(2,1)}, bf16[3,4,144,128]{3,2,1,0:T(8,128)(2,1)S(1)}, u32[]{:S(2)}, u32[]{:S(2)}) collective-permute-start(bf16[3,4,144,128]{3,2,1,0:T(8,128)(2,1)} %get-tuple-element.35), channel_id=1, source_target_pairs={{0,16},{1,17},{10,26},{11,27},{20,4},{21,5},{30,14},{31,15}} | collective-permute-start | bytes 1327112 | tf_op jit(solution)/shard_map/ppermute | solution.py:110
  69.6 2.9 %collective-permute-start.21 = (bf16[3,4,144,128]{3,2,1,0:T(8,128)(2,1)}, bf16[3,4,144,128]{3,2,1,0:T(8,128)(2,1)S(1)}, u32[]{:S(2)}, u32[]{:S(2)}) collective-permute-start(bf16[3,4,144,128]{3,2,1,0:T(8,128)(2,1)} %get-tuple-element.31), channel_id=1, source_target_pairs={{0,16},{1,17},{10,26},{11,27},{20,4},{21,5},{30,14},{31,15}} | collective-permute-start | bytes 1327112 | tf_op jit(solution)/shard_map/ppermute | solution.py:110
  72.6 2.1 %collective-permute-start.20 = (bf16[3,4,144,128]{3,2,1,0:T(8,128)(2,1)}, bf16[3,4,144,128]{3,2,1,0:T(8,128)(2,1)}, u32[]{:S(2)}, u32[]{:S(2)}) collective-permute-start(bf16[3,4,144,128]{3,2,1,0:T(8,128)(2,1)} %get-tuple-element.32), channel_id=1, source_target_pairs={{0,8},{16,24},{1,9},{17,25},{10,2},{26,18},{11,3},{27,19},{20,28},... | collective-permute-start | bytes 1327112 | tf_op jit(solution)/shard_map/ppermute | solution.py:110
  74.6 2.0 %collective-permute-start.7 = (bf16[3,2,2,144,128]{4,3,2,1,0:T(8,128)(2,1)}, bf16[3,2,2,144,128]{4,3,2,1,0:T(8,128)(2,1)}, u32[]{:S(2)}, u32[]{:S(2)}) collective-permute-start(bf16[3,2,2,144,128]{4,3,2,1,0:T(8,128)(2,1)} %collective-permute-done.5.refs_7_), channel_id=1, source_target_pairs={{2,0},{4,2},{6,4},{7,6},{5,7},{3,5},{1,3},{0,1},{10,8},{12,10},{14... | collective-permute-start | bytes 1327112 | tf_op jit(solution)/shard_map/ppermute | solution.py:130
  77.7 7.1 %collective-permute-done.6.refs_8_ = bf16[3,2,2,144,128]{4,3,2,1,0:T(8,128)(2,1)S(1)} collective-permute-done((bf16[3,2,2,144,128]{4,3,2,1,0:T(8,128)(2,1)S(1)}, bf16[3,2,2,144,128]{4,3,2,1,0:T(8,128)(2,1)S(1)}, u32[]{:S(2)}, u32[]{:S(2)}) %collective-permute-start.6) | collective-permute-done | bytes 442400 | tf_op jit(solution)/shard_map/ppermute | solution.py:129
  85.7 2.1 %collective-permute-done.7.refs_9_ = bf16[3,2,2,144,128]{4,3,2,1,0:T(8,128)(2,1)} collective-permute-done((bf16[3,2,2,144,128]{4,3,2,1,0:T(8,128)(2,1)}, bf16[3,2,2,144,128]{4,3,2,1,0:T(8,128)(2,1)}, u32[]{:S(2)}, u32[]{:S(2)}) %collective-permute-start.7) | collective-permute-done | bytes 442400 | tf_op jit(solution)/shard_map/ppermute | solution.py:130
  91.7 2.0 %collective-permute-start.23 = (bf16[3,4,144,128]{3,2,1,0:T(8,128)(2,1)}, bf16[3,4,144,128]{3,2,1,0:T(8,128)(2,1)S(1)}, u32[]{:S(2)}, u32[]{:S(2)}) collective-permute-start(bf16[3,4,144,128]{3,2,1,0:T(8,128)(2,1)} %get-tuple-element.27), channel_id=1, source_target_pairs={{0,16},{1,17},{10,26},{11,27},{20,4},{21,5},{30,14},{31,15}} | collective-permute-start | bytes 1327112 | tf_op jit(solution)/shard_map/ppermute | solution.py:110
  93.7 2.1 %collective-permute-start.22 = (bf16[3,4,144,128]{3,2,1,0:T(8,128)(2,1)}, bf16[3,4,144,128]{3,2,1,0:T(8,128)(2,1)}, u32[]{:S(2)}, u32[]{:S(2)}) collective-permute-start(bf16[3,4,144,128]{3,2,1,0:T(8,128)(2,1)} %get-tuple-element.28), channel_id=1, source_target_pairs={{0,8},{16,24},{1,9},{17,25},{10,2},{26,18},{11,3},{27,19},{20,28},... | collective-permute-start | bytes 1327112 | tf_op jit(solution)/shard_map/ppermute | solution.py:110
  95.8 2.0 %collective-permute-start.9 = (bf16[3,2,2,144,128]{4,3,2,1,0:T(8,128)(2,1)}, bf16[3,2,2,144,128]{4,3,2,1,0:T(8,128)(2,1)S(1)}, u32[]{:S(2)}, u32[]{:S(2)}) collective-permute-start(bf16[3,2,2,144,128]{4,3,2,1,0:T(8,128)(2,1)} %collective-permute-done.7.refs_9_), channel_id=1, source_target_pairs={{2,0},{4,2},{6,4},{7,6},{5,7},{3,5},{1,3},{0,1},{10,8},{12,10},{14... | collective-permute-start | bytes 1327112 | tf_op jit(solution)/shard_map/ppermute | solution.py:130
  99.0 7.0 %collective-permute-done.8.refs_10_ = bf16[3,2,2,144,128]{4,3,2,1,0:T(8,128)(2,1)S(1)} collective-permute-done((bf16[3,2,2,144,128]{4,3,2,1,0:T(8,128)(2,1)S(1)}, bf16[3,2,2,144,128]{4,3,2,1,0:T(8,128)(2,1)S(1)}, u32[]{:S(2)}, u32[]{:S(2)}) %collective-permute-start.8) | collective-permute-done | bytes 442400 | tf_op jit(solution)/shard_map/ppermute | solution.py:129
  112.5 3.0 %collective-permute-start.25 = (bf16[3,4,144,128]{3,2,1,0:T(8,128)(2,1)S(1)}, bf16[3,4,144,128]{3,2,1,0:T(8,128)(2,1)S(1)}, u32[]{:S(2)}, u32[]{:S(2)}) collective-permute-start(bf16[3,4,144,128]{3,2,1,0:T(8,128)(2,1)S(1)} %get-tuple-element.20), channel_id=1, source_target_pairs={{0,16},{1,17},{10,26},{11,27},{20,4},{21,5},{30,14},{31,15}} | collective-permute-start | bytes 1327112 | tf_op jit(solution)/shard_map/ppermute | solution.py:110
  115.5 6.2 %collective-permute-done.10.refs_12_ = bf16[3,2,2,144,128]{4,3,2,1,0:T(8,128)(2,1)} collective-permute-done((bf16[3,2,2,144,128]{4,3,2,1,0:T(8,128)(2,1)S(1)}, bf16[3,2,2,144,128]{4,3,2,1,0:T(8,128)(2,1)}, u32[]{:S(2)}, u32[]{:S(2)}) %collective-permute-start.10) | collective-permute-done | bytes 442400 | tf_op jit(solution)/shard_map/ppermute | solution.py:129
  121.7 2.5 %collective-permute-start.12 = (bf16[3,2,2,144,128]{4,3,2,1,0:T(8,128)(2,1)}, bf16[3,2,2,144,128]{4,3,2,1,0:T(8,128)(2,1)}, u32[]{:S(2)}, u32[]{:S(2)}) collective-permute-start(bf16[3,2,2,144,128]{4,3,2,1,0:T(8,128)(2,1)} %collective-permute-done.10.refs_12_), channel_id=1, source_target_pairs={{0,2},{2,4},{4,6},{6,7},{7,5},{5,3},{3,1},{1,0},{8,10},{10,12},{12... | collective-permute-start | bytes 1327112 | tf_op jit(solution)/shard_map/ppermute | solution.py:129
  124.7 1.6 select_select_fusion.3
  136.5 2.5 %collective-permute-start.27 = (bf16[3,4,144,128]{3,2,1,0:T(8,128)(2,1)}, bf16[3,4,144,128]{3,2,1,0:T(8,128)(2,1)S(1)}, u32[]{:S(2)}, u32[]{:S(2)}) collective-permute-start(bf16[3,4,144,128]{3,2,1,0:T(8,128)(2,1)} %get-tuple-element.16), channel_id=1, source_target_pairs={{0,16},{1,17},{10,26},{11,27},{20,4},{21,5},{30,14},{31,15}} | collective-permute-start | bytes 1327112 | tf_op jit(solution)/shard_map/ppermute | solution.py:110
  140.6 2.2 %collective-permute-start.26 = (bf16[3,4,144,128]{3,2,1,0:T(8,128)(2,1)}, bf16[3,4,144,128]{3,2,1,0:T(8,128)(2,1)}, u32[]{:S(2)}, u32[]{:S(2)}) collective-permute-start(bf16[3,4,144,128]{3,2,1,0:T(8,128)(2,1)} %get-tuple-element.17), channel_id=1, source_target_pairs={{0,8},{16,24},{1,9},{17,25},{10,2},{26,18},{11,3},{27,19},{20,28},... | collective-permute-start | bytes 1327112 | tf_op jit(solution)/shard_map/ppermute | solution.py:110
  146.1 4.3 %collective-permute-start.29 = (bf16[3,4,144,128]{3,2,1,0:T(8,128)(2,1)}, bf16[3,4,144,128]{3,2,1,0:T(8,128)(2,1)S(1)}, u32[]{:S(2)}, u32[]{:S(2)}) collective-permute-start(bf16[3,4,144,128]{3,2,1,0:T(8,128)(2,1)} %get-tuple-element.12), channel_id=1, source_target_pairs={{0,16},{1,17},{10,26},{11,27},{20,4},{21,5},{30,14},{31,15}} | collective-permute-start | bytes 1327112 | tf_op jit(solution)/shard_map/ppermute | solution.py:110
  154.6 1.9 %collective-permute-done.29 = bf16[3,4,144,128]{3,2,1,0:T(8,128)(2,1)S(1)} collective-permute-done((bf16[3,4,144,128]{3,2,1,0:T(8,128)(2,1)}, bf16[3,4,144,128]{3,2,1,0:T(8,128)(2,1)S(1)}, u32[]{:S(2)}, u32[]{:S(2)}) %collective-permute-start.29) | collective-permute-done | bytes 442400 | tf_op jit(solution)/shard_map/ppermute | solution.py:110
  156.5 2.1 %collective-permute-start.30 = (bf16[3,4,144,128]{3,2,1,0:T(8,128)(2,1)S(1)}, bf16[3,4,144,128]{3,2,1,0:T(8,128)(2,1)}, u32[]{:S(2)}, u32[]{:S(2)}) collective-permute-start(bf16[3,4,144,128]{3,2,1,0:T(8,128)(2,1)S(1)} %collective-permute-done.29), channel_id=1, source_target_pairs={{0,8},{16,24},{1,9},{17,25},{10,2},{26,18},{11,3},{27,19},{20,28},... | collective-permute-start | bytes 1327112 | tf_op jit(solution)/shard_map/ppermute | solution.py:110
  166.2 11.8 %shard_map.37 = f32[2048,1024]{1,0:T(8,128)} custom-call(s32[288]{0:T(512)} %min.12.offs_ref, bf16[3,2,2,144,128]{4,3,2,1,0:T(8,128)(2,1)} %copy-done, bf16[3,2,2,144,128]{4,3,2,1,0:T(8,128)(2,1)} %copy-done.1, bf16[3,2,2,144,128]{4,3,2,1,0:T(8,128)(2,1)} %copy-done.21, bf16[3,2,2,144,128]{4,3,2,1,0:T(8,128)(2,1)} %copy-done.22, ...), custom_call_target="tpu_custom_call" | custom-call | flops 805306368 | bytes 17825792 | tf_op jit(solution)/shard_map/pallas_call | solution.py:56
  (242 shorter events, 62.8 us)
Async XLA Ops:
  4.2 20.1 %collective-permute-start.15 = (bf16[3,4,144,128]{3,2,1,0:T(8,128)(2,1)}, bf16[3,4,144,128]{3,2,1,0:T(8,128)(2,1)S(1)}, u32[]{:S(2)}, u32[]{:S(2)}) collective-permute-start(bf16[3,4,144,128]{3,2,1,0:T(8,128)(2,1)} %pad_maximum_fusion), channel_id=1, source_target_pairs={{0,16},{1,17},{10,26},{11,27},{20,4},{21,5},{30,14},{31,15}} | collective-permute-start | bytes 1327112 | tf_op jit(solution)/shard_map/ppermute | solution.py:110
  9.1 53.1 %collective-permute-start.14 = (bf16[3,4,144,128]{3,2,1,0:T(8,128)(2,1)}, bf16[3,4,144,128]{3,2,1,0:T(8,128)(2,1)}, u32[]{:S(2)}, u32[]{:S(2)}) collective-permute-start(bf16[3,4,144,128]{3,2,1,0:T(8,128)(2,1)} %pad_maximum_fusion), channel_id=1, source_target_pairs={{0,8},{16,24},{1,9},{17,25},{10,2},{26,18},{11,3},{27,19},{20,28},... | collective-permute-start | bytes 1327112 | tf_op jit(solution)/shard_map/ppermute | solution.py:110
  11.1 10.4 %collective-permute-start = (bf16[3,2,2,144,128]{4,3,2,1,0:T(8,128)(2,1)S(1)}, bf16[3,2,2,144,128]{4,3,2,1,0:T(8,128)(2,1)S(1)}, u32[]{:S(2)}, u32[]{:S(2)}) collective-permute-start(bf16[3,2,2,144,128]{4,3,2,1,0:T(8,128)(2,1)S(1)} %get-tuple-element.5.refs_0_), channel_id=1, source_target_pairs={{0,2},{2,4},{4,6},{6,7},{7,5},{5,3},{3,1},{1,0},{8,10},{10,12},{12... | collective-permute-start | bytes 1327112 | tf_op jit(solution)/shard_map/ppermute | solution.py:129
  11.1 12.9 %collective-permute-start.1 = (bf16[3,2,2,144,128]{4,3,2,1,0:T(8,128)(2,1)S(1)}, bf16[3,2,2,144,128]{4,3,2,1,0:T(8,128)(2,1)S(1)}, u32[]{:S(2)}, u32[]{:S(2)}) collective-permute-start(bf16[3,2,2,144,128]{4,3,2,1,0:T(8,128)(2,1)S(1)} %get-tuple-element.6.refs_1_), channel_id=1, source_target_pairs={{2,0},{4,2},{6,4},{7,6},{5,7},{3,5},{1,3},{0,1},{10,8},{12,10},{14... | collective-permute-start | bytes 1327112 | tf_op jit(solution)/shard_map/ppermute | solution.py:130
  25.2 18.0 %collective-permute-start.17 = (bf16[3,4,144,128]{3,2,1,0:T(8,128)(2,1)}, bf16[3,4,144,128]{3,2,1,0:T(8,128)(2,1)S(1)}, u32[]{:S(2)}, u32[]{:S(2)}) collective-permute-start(bf16[3,4,144,128]{3,2,1,0:T(8,128)(2,1)} %get-tuple-element.41), channel_id=1, source_target_pairs={{0,16},{1,17},{10,26},{11,27},{20,4},{21,5},{30,14},{31,15}} | collective-permute-start | bytes 1327112 | tf_op jit(solution)/shard_map/ppermute | solution.py:110
  27.5 34.7 %collective-permute-start.16 = (bf16[3,4,144,128]{3,2,1,0:T(8,128)(2,1)}, bf16[3,4,144,128]{3,2,1,0:T(8,128)(2,1)}, u32[]{:S(2)}, u32[]{:S(2)}) collective-permute-start(bf16[3,4,144,128]{3,2,1,0:T(8,128)(2,1)} %get-tuple-element.42), channel_id=1, source_target_pairs={{0,8},{16,24},{1,9},{17,25},{10,2},{26,18},{11,3},{27,19},{20,28},... | collective-permute-start | bytes 1327112 | tf_op jit(solution)/shard_map/ppermute | solution.py:110
  29.6 9.7 %collective-permute-start.2 = (bf16[3,2,2,144,128]{4,3,2,1,0:T(8,128)(2,1)S(1)}, bf16[3,2,2,144,128]{4,3,2,1,0:T(8,128)(2,1)S(1)}, u32[]{:S(2)}, u32[]{:S(2)}) collective-permute-start(bf16[3,2,2,144,128]{4,3,2,1,0:T(8,128)(2,1)S(1)} %collective-permute-done.refs_2_), channel_id=1, source_target_pairs={{0,2},{2,4},{4,6},{6,7},{7,5},{5,3},{3,1},{1,0},{8,10},{10,12},{12... | collective-permute-start | bytes 1327112 | tf_op jit(solution)/shard_map/ppermute | solution.py:129
  29.6 11.7 %collective-permute-start.3 = (bf16[3,2,2,144,128]{4,3,2,1,0:T(8,128)(2,1)S(1)}, bf16[3,2,2,144,128]{4,3,2,1,0:T(8,128)(2,1)}, u32[]{:S(2)}, u32[]{:S(2)}) collective-permute-start(bf16[3,2,2,144,128]{4,3,2,1,0:T(8,128)(2,1)S(1)} %collective-permute-done.1.refs_3_), channel_id=1, source_target_pairs={{2,0},{4,2},{6,4},{7,6},{5,7},{3,5},{1,3},{0,1},{10,8},{12,10},{14... | collective-permute-start | bytes 1327112 | tf_op jit(solution)/shard_map/ppermute | solution.py:130
  44.3 17.9 %collective-permute-start.18 = (bf16[3,4,144,128]{3,2,1,0:T(8,128)(2,1)}, bf16[3,4,144,128]{3,2,1,0:T(8,128)(2,1)S(1)}, u32[]{:S(2)}, u32[]{:S(2)}) collective-permute-start(bf16[3,4,144,128]{3,2,1,0:T(8,128)(2,1)} %get-tuple-element.36), channel_id=1, source_target_pairs={{0,8},{16,24},{1,9},{17,25},{10,2},{26,18},{11,3},{27,19},{20,28},... | collective-permute-start | bytes 1327112 | tf_op jit(solution)/shard_map/ppermute | solution.py:110
  45.6 10.8 %collective-permute-start.4 = (bf16[3,2,2,144,128]{4,3,2,1,0:T(8,128)(2,1)S(1)}, bf16[3,2,2,144,128]{4,3,2,1,0:T(8,128)(2,1)S(1)}, u32[]{:S(2)}, u32[]{:S(2)}) collective-permute-start(bf16[3,2,2,144,128]{4,3,2,1,0:T(8,128)(2,1)S(1)} %collective-permute-done.2.refs_4_), channel_id=1, source_target_pairs={{0,2},{2,4},{4,6},{6,7},{7,5},{5,3},{3,1},{1,0},{8,10},{10,12},{12... | collective-permute-start | bytes 1327112 | tf_op jit(solution)/shard_map/ppermute | solution.py:129
  46.0 15.3 %collective-permute-start.5 = (bf16[3,2,2,144,128]{4,3,2,1,0:T(8,128)(2,1)}, bf16[3,2,2,144,128]{4,3,2,1,0:T(8,128)(2,1)}, u32[]{:S(2)}, u32[]{:S(2)}) collective-permute-start(bf16[3,2,2,144,128]{4,3,2,1,0:T(8,128)(2,1)} %collective-permute-done.3.refs_5_), channel_id=1, source_target_pairs={{2,0},{4,2},{6,4},{7,6},{5,7},{3,5},{1,3},{0,1},{10,8},{12,10},{14... | collective-permute-start | bytes 1327112 | tf_op jit(solution)/shard_map/ppermute | solution.py:130
  56.3 12.2 %collective-permute-start.19 = (bf16[3,4,144,128]{3,2,1,0:T(8,128)(2,1)}, bf16[3,4,144,128]{3,2,1,0:T(8,128)(2,1)S(1)}, u32[]{:S(2)}, u32[]{:S(2)}) collective-permute-start(bf16[3,4,144,128]{3,2,1,0:T(8,128)(2,1)} %get-tuple-element.35), channel_id=1, source_target_pairs={{0,16},{1,17},{10,26},{11,27},{20,4},{21,5},{30,14},{31,15}} | collective-permute-start | bytes 1327112 | tf_op jit(solution)/shard_map/ppermute | solution.py:110
  69.6 21.1 %collective-permute-start.21 = (bf16[3,4,144,128]{3,2,1,0:T(8,128)(2,1)}, bf16[3,4,144,128]{3,2,1,0:T(8,128)(2,1)S(1)}, u32[]{:S(2)}, u32[]{:S(2)}) collective-permute-start(bf16[3,4,144,128]{3,2,1,0:T(8,128)(2,1)} %get-tuple-element.31), channel_id=1, source_target_pairs={{0,16},{1,17},{10,26},{11,27},{20,4},{21,5},{30,14},{31,15}} | collective-permute-start | bytes 1327112 | tf_op jit(solution)/shard_map/ppermute | solution.py:110
  72.6 40.0 %collective-permute-start.20 = (bf16[3,4,144,128]{3,2,1,0:T(8,128)(2,1)}, bf16[3,4,144,128]{3,2,1,0:T(8,128)(2,1)}, u32[]{:S(2)}, u32[]{:S(2)}) collective-permute-start(bf16[3,4,144,128]{3,2,1,0:T(8,128)(2,1)} %get-tuple-element.32), channel_id=1, source_target_pairs={{0,8},{16,24},{1,9},{17,25},{10,2},{26,18},{11,3},{27,19},{20,28},... | collective-permute-start | bytes 1327112 | tf_op jit(solution)/shard_map/ppermute | solution.py:110
  74.6 10.2 %collective-permute-start.6 = (bf16[3,2,2,144,128]{4,3,2,1,0:T(8,128)(2,1)S(1)}, bf16[3,2,2,144,128]{4,3,2,1,0:T(8,128)(2,1)S(1)}, u32[]{:S(2)}, u32[]{:S(2)}) collective-permute-start(bf16[3,2,2,144,128]{4,3,2,1,0:T(8,128)(2,1)S(1)} %copy-done.25), channel_id=1, source_target_pairs={{0,2},{2,4},{4,6},{6,7},{7,5},{5,3},{3,1},{1,0},{8,10},{10,12},{12... | collective-permute-start | bytes 1327112 | tf_op jit(solution)/shard_map/ppermute | solution.py:129
  74.6 13.2 %collective-permute-start.7 = (bf16[3,2,2,144,128]{4,3,2,1,0:T(8,128)(2,1)}, bf16[3,2,2,144,128]{4,3,2,1,0:T(8,128)(2,1)}, u32[]{:S(2)}, u32[]{:S(2)}) collective-permute-start(bf16[3,2,2,144,128]{4,3,2,1,0:T(8,128)(2,1)} %collective-permute-done.5.refs_7_), channel_id=1, source_target_pairs={{2,0},{4,2},{6,4},{7,6},{5,7},{3,5},{1,3},{0,1},{10,8},{12,10},{14... | collective-permute-start | bytes 1327112 | tf_op jit(solution)/shard_map/ppermute | solution.py:130
  91.7 17.1 %collective-permute-start.23 = (bf16[3,4,144,128]{3,2,1,0:T(8,128)(2,1)}, bf16[3,4,144,128]{3,2,1,0:T(8,128)(2,1)S(1)}, u32[]{:S(2)}, u32[]{:S(2)}) collective-permute-start(bf16[3,4,144,128]{3,2,1,0:T(8,128)(2,1)} %get-tuple-element.27), channel_id=1, source_target_pairs={{0,16},{1,17},{10,26},{11,27},{20,4},{21,5},{30,14},{31,15}} | collective-permute-start | bytes 1327112 | tf_op jit(solution)/shard_map/ppermute | solution.py:110
  93.7 30.9 %collective-permute-start.22 = (bf16[3,4,144,128]{3,2,1,0:T(8,128)(2,1)}, bf16[3,4,144,128]{3,2,1,0:T(8,128)(2,1)}, u32[]{:S(2)}, u32[]{:S(2)}) collective-permute-start(bf16[3,4,144,128]{3,2,1,0:T(8,128)(2,1)} %get-tuple-element.28), channel_id=1, source_target_pairs={{0,8},{16,24},{1,9},{17,25},{10,2},{26,18},{11,3},{27,19},{20,28},... | collective-permute-start | bytes 1327112 | tf_op jit(solution)/shard_map/ppermute | solution.py:110
  95.8 10.2 %collective-permute-start.8 = (bf16[3,2,2,144,128]{4,3,2,1,0:T(8,128)(2,1)S(1)}, bf16[3,2,2,144,128]{4,3,2,1,0:T(8,128)(2,1)S(1)}, u32[]{:S(2)}, u32[]{:S(2)}) collective-permute-start(bf16[3,2,2,144,128]{4,3,2,1,0:T(8,128)(2,1)S(1)} %copy-done.27), channel_id=1, source_target_pairs={{0,2},{2,4},{4,6},{6,7},{7,5},{5,3},{3,1},{1,0},{8,10},{10,12},{12... | collective-permute-start | bytes 1327112 | tf_op jit(solution)/shard_map/ppermute | solution.py:129
  95.8 12.2 %collective-permute-start.9 = (bf16[3,2,2,144,128]{4,3,2,1,0:T(8,128)(2,1)}, bf16[3,2,2,144,128]{4,3,2,1,0:T(8,128)(2,1)S(1)}, u32[]{:S(2)}, u32[]{:S(2)}) collective-permute-start(bf16[3,2,2,144,128]{4,3,2,1,0:T(8,128)(2,1)} %collective-permute-done.7.refs_9_), channel_id=1, source_target_pairs={{2,0},{4,2},{6,4},{7,6},{5,7},{3,5},{1,3},{0,1},{10,8},{12,10},{14... | collective-permute-start | bytes 1327112 | tf_op jit(solution)/shard_map/ppermute | solution.py:130
  109.0 15.7 %collective-permute-start.24 = (bf16[3,4,144,128]{3,2,1,0:T(8,128)(2,1)S(1)}, bf16[3,4,144,128]{3,2,1,0:T(8,128)(2,1)S(1)}, u32[]{:S(2)}, u32[]{:S(2)}) collective-permute-start(bf16[3,4,144,128]{3,2,1,0:T(8,128)(2,1)S(1)} %get-tuple-element.21), channel_id=1, source_target_pairs={{0,8},{16,24},{1,9},{17,25},{10,2},{26,18},{11,3},{27,19},{20,28},... | collective-permute-start | bytes 1327112 | tf_op jit(solution)/shard_map/ppermute | solution.py:110
  110.4 11.3 %collective-permute-start.10 = (bf16[3,2,2,144,128]{4,3,2,1,0:T(8,128)(2,1)S(1)}, bf16[3,2,2,144,128]{4,3,2,1,0:T(8,128)(2,1)}, u32[]{:S(2)}, u32[]{:S(2)}) collective-permute-start(bf16[3,2,2,144,128]{4,3,2,1,0:T(8,128)(2,1)S(1)} %collective-permute-done.8.refs_10_), channel_id=1, source_target_pairs={{0,2},{2,4},{4,6},{6,7},{7,5},{5,3},{3,1},{1,0},{8,10},{10,12},{12... | collective-permute-start | bytes 1327112 | tf_op jit(solution)/shard_map/ppermute | solution.py:129
  111.3 13.0 %collective-permute-start.11 = (bf16[3,2,2,144,128]{4,3,2,1,0:T(8,128)(2,1)S(1)}, bf16[3,2,2,144,128]{4,3,2,1,0:T(8,128)(2,1)}, u32[]{:S(2)}, u32[]{:S(2)}) collective-permute-start(bf16[3,2,2,144,128]{4,3,2,1,0:T(8,128)(2,1)S(1)} %collective-permute-done.9.refs_11_), channel_id=1, source_target_pairs={{2,0},{4,2},{6,4},{7,6},{5,7},{3,5},{1,3},{0,1},{10,8},{12,10},{14... | collective-permute-start | bytes 1327112 | tf_op jit(solution)/shard_map/ppermute | solution.py:130
  112.5 16.0 %collective-permute-start.25 = (bf16[3,4,144,128]{3,2,1,0:T(8,128)(2,1)S(1)}, bf16[3,4,144,128]{3,2,1,0:T(8,128)(2,1)S(1)}, u32[]{:S(2)}, u32[]{:S(2)}) collective-permute-start(bf16[3,4,144,128]{3,2,1,0:T(8,128)(2,1)S(1)} %get-tuple-element.20), channel_id=1, source_target_pairs={{0,16},{1,17},{10,26},{11,27},{20,4},{21,5},{30,14},{31,15}} | collective-permute-start | bytes 1327112 | tf_op jit(solution)/shard_map/ppermute | solution.py:110
  121.7 21.1 %collective-permute-start.12 = (bf16[3,2,2,144,128]{4,3,2,1,0:T(8,128)(2,1)}, bf16[3,2,2,144,128]{4,3,2,1,0:T(8,128)(2,1)}, u32[]{:S(2)}, u32[]{:S(2)}) collective-permute-start(bf16[3,2,2,144,128]{4,3,2,1,0:T(8,128)(2,1)} %collective-permute-done.10.refs_12_), channel_id=1, source_target_pairs={{0,2},{2,4},{4,6},{6,7},{7,5},{5,3},{3,1},{1,0},{8,10},{10,12},{12... | collective-permute-start | bytes 1327112 | tf_op jit(solution)/shard_map/ppermute | solution.py:129
  124.3 19.5 %collective-permute-start.13 = (bf16[3,2,2,144,128]{4,3,2,1,0:T(8,128)(2,1)}, bf16[3,2,2,144,128]{4,3,2,1,0:T(8,128)(2,1)}, u32[]{:S(2)}, u32[]{:S(2)}) collective-permute-start(bf16[3,2,2,144,128]{4,3,2,1,0:T(8,128)(2,1)} %collective-permute-done.11.refs_13_), channel_id=1, source_target_pairs={{2,0},{4,2},{6,4},{7,6},{5,7},{3,5},{1,3},{0,1},{10,8},{12,10},{14... | collective-permute-start | bytes 1327112 | tf_op jit(solution)/shard_map/ppermute | solution.py:130
  130.3 31.1 %copy-start.11 = (bf16[3,4,144,128]{3,2,1,0:T(8,128)(2,1)S(1)}, bf16[3,4,144,128]{3,2,1,0:T(8,128)(2,1)}, u32[]{:S(2)}) copy-start(bf16[3,4,144,128]{3,2,1,0:T(8,128)(2,1)} %copy-done.10) | copy-start | bytes 1327108
  136.5 8.6 %collective-permute-start.27 = (bf16[3,4,144,128]{3,2,1,0:T(8,128)(2,1)}, bf16[3,4,144,128]{3,2,1,0:T(8,128)(2,1)S(1)}, u32[]{:S(2)}, u32[]{:S(2)}) collective-permute-start(bf16[3,4,144,128]{3,2,1,0:T(8,128)(2,1)} %get-tuple-element.16), channel_id=1, source_target_pairs={{0,16},{1,17},{10,26},{11,27},{20,4},{21,5},{30,14},{31,15}} | collective-permute-start | bytes 1327112 | tf_op jit(solution)/shard_map/ppermute | solution.py:110
  140.6 20.0 %collective-permute-start.26 = (bf16[3,4,144,128]{3,2,1,0:T(8,128)(2,1)}, bf16[3,4,144,128]{3,2,1,0:T(8,128)(2,1)}, u32[]{:S(2)}, u32[]{:S(2)}) collective-permute-start(bf16[3,4,144,128]{3,2,1,0:T(8,128)(2,1)} %get-tuple-element.17), channel_id=1, source_target_pairs={{0,8},{16,24},{1,9},{17,25},{10,2},{26,18},{11,3},{27,19},{20,28},... | collective-permute-start | bytes 1327112 | tf_op jit(solution)/shard_map/ppermute | solution.py:110
  146.1 10.4 %collective-permute-start.29 = (bf16[3,4,144,128]{3,2,1,0:T(8,128)(2,1)}, bf16[3,4,144,128]{3,2,1,0:T(8,128)(2,1)S(1)}, u32[]{:S(2)}, u32[]{:S(2)}) collective-permute-start(bf16[3,4,144,128]{3,2,1,0:T(8,128)(2,1)} %get-tuple-element.12), channel_id=1, source_target_pairs={{0,16},{1,17},{10,26},{11,27},{20,4},{21,5},{30,14},{31,15}} | collective-permute-start | bytes 1327112 | tf_op jit(solution)/shard_map/ppermute | solution.py:110
  153.3 7.3 %collective-permute-start.28 = (bf16[3,4,144,128]{3,2,1,0:T(8,128)(2,1)}, bf16[3,4,144,128]{3,2,1,0:T(8,128)(2,1)S(1)}, u32[]{:S(2)}, u32[]{:S(2)}) collective-permute-start(bf16[3,4,144,128]{3,2,1,0:T(8,128)(2,1)} %get-tuple-element.13), channel_id=1, source_target_pairs={{0,8},{16,24},{1,9},{17,25},{10,2},{26,18},{11,3},{27,19},{20,28},... | collective-permute-start | bytes 1327112 | tf_op jit(solution)/shard_map/ppermute | solution.py:110
  156.5 4.9 %collective-permute-start.30 = (bf16[3,4,144,128]{3,2,1,0:T(8,128)(2,1)S(1)}, bf16[3,4,144,128]{3,2,1,0:T(8,128)(2,1)}, u32[]{:S(2)}, u32[]{:S(2)}) collective-permute-start(bf16[3,4,144,128]{3,2,1,0:T(8,128)(2,1)S(1)} %collective-permute-done.29), channel_id=1, source_target_pairs={{0,8},{16,24},{1,9},{17,25},{10,2},{26,18},{11,3},{27,19},{20,28},... | collective-permute-start | bytes 1327112 | tf_op jit(solution)/shard_map/ppermute | solution.py:110
  (40 other events, 462.7 us)

commit v8 on v7

--- a/solution.py
+++ b/solution.py
@@ -100,53 +100,32 @@
     backward = [(b, a) for a, b in forward]
 
     src = c // local_slots
+    which = (r - src + nrow) % nrow
     slot = c % local_slots
-    nx = nrow // 2
-    up = (r - src + nrow) % nrow
-    is_s, is_p, is_d1 = up == 0, r == src + 1 - 2 * (src % 2), (up % 2 == 0) & (up != 0)
-    chip_step = up // 2
-
-    def send(v, pairs):
-        return lax.ppermute(v, ("row", "col"), [(a * ncol + cc, b * ncol + cc) for a, b, cc in pairs])
-
-    first_hop = []
-    for cc in range(ncol):
-        s0 = cc // local_slots
-        first_hop.append((s0, s0 ^ 1, cc))
-        first_hop += [((s0 + 2 * j) % nrow, ((s0 + 2 * j) % nrow) ^ 1, cc) for j in range(1, nx)]
-    cross = [[(cc // local_slots, (cc // local_slots + 2 * j) % nrow, cc) for cc in range(ncol)] for j in range(1, nx)]
+    fans = [
+        [
+            ((cc // local_slots) * ncol + cc, ((cc // local_slots + j) % nrow) * ncol + cc)
+            for cc in range(ncol)
+        ]
+        for j in range(1, nrow)
+    ]
 
     def pick_slot(piece):
         return lax.dynamic_index_in_dim(piece, slot, axis=2, keepdims=False)
 
     half = x.shape[1] // 2
     a, b = x[:, :half], x[:, half:]
-    pieces, owns, hops, crossed = [], [], [], []
-    forwarded = None
-    for step in range(ncol + 1):
-        if step < ncol:
-            if step:
-                a = lax.ppermute(a, "col", forward)
-                b = lax.ppermute(b, "col", backward)
-            pieces += [a, b]
-            own = jnp.concatenate([pick_slot(a), pick_slot(b)], axis=1)
-            owns.append(own)
-            operand = own if forwarded is None else jnp.where(is_s, own, forwarded)
-        else:
-            operand = forwarded
-        hops.append(send(operand, first_hop))
-        if step < ncol:
-            got = None
-            for j, pairs in enumerate(cross, start=1):
-                v = send(own, pairs)
-                got = v if got is None else jnp.where(chip_step == j, v, got)
-            crossed.append(got)
-            forwarded = got
-
-    columns = [
-        jnp.where(is_s, owns[k], jnp.where(is_p, hops[k], jnp.where(is_d1, crossed[k], hops[k + 1])))
-        for k in range(ncol)
-    ]
+    pieces, columns = [], []
+    for step in range(ncol):
+        if step:
+            a = lax.ppermute(a, "col", forward)
+            b = lax.ppermute(b, "col", backward)
+        pieces += [a, b]
+        own = jnp.concatenate([pick_slot(a), pick_slot(b)], axis=1)
+        got = own
+        for j, fan in enumerate(fans, start=1):
+            got = jnp.where(which == j, lax.ppermute(own, ("row", "col"), fan), got)
+        columns.append(got)
 
     w_offs = jnp.stack([piece[:, :, :, blk + 3, 0] for piece in pieces], axis=1)
     c_offs = jnp.stack(

time: 179 us -> 180 us (level)
  local copies, waits for them, and re-layouts: 41.5 us -> 19.7 us
  waiting for transfers between devices: 51.3 us -> 67.6 us
  starting transfers between devices: 58.3 us -> 69.9 us
  other arithmetic: 14.3 us -> 9.29 us
    ppermute x17 -> x24, starting transfers between devices: 43.2 us -> 55.5 us  [local(): got = jnp.where(which == j, lax.ppermute(own, ('row', 'col'), fan), got)]
    ppermute x7, waiting for transfers between devices: 7.73 us -> 16.9 us  [local(): b = lax.ppermute(b, 'col', backward)]
    squeeze x15, local copies, waits for them, and re-layouts: 9.1 us -> 0.25 us  [pick_slot(): return lax.dynamic_index_in_dim(piece, slot, axis=2, keepdims=False)]
    unnamed x97 -> x73, local copies, waits for them, and re-layouts: 8.71 us -> 1.72 us
    slice x31, local copies, waits for them, and re-layouts: 10.8 us -> 5.07 us  [local(): w_offs = jnp.stack([piece[:, :, :, blk + 3, 0] for piece in pieces], axis=1)]
    ppermute x7, waiting for transfers between devices: 41.3 us -> 45.3 us  [local(): a = lax.ppermute(a, 'col', forward)]
    ppermute x7, starting transfers between devices: 3.76 us -> 0.33 us  [local(): a = lax.ppermute(a, 'col', forward)]
    select_n x3 -> x8, other arithmetic: 4.41 us -> 0.98 us  [local(): got = jnp.where(which == j, lax.ppermute(own, ('row', 'col'), fan), got)]
  transfers between devices with their start and end apart: 31 -> 38, of which waited for: 13 -> 16; matrix products, arithmetic and copies ran while one was open for 24% -> 13% of each run, Pallas kernels for 0% -> 0%
where the time goes in v8:
time: 180 us; the launch traced here: 179 us
  starting transfers between devices  69.9 us (39%)
  waiting for transfers between devices  67.6 us (38%)
  local copies, waits for them, and re-layouts  19.7 us (11%)
  Pallas kernels  11.8 us (7%)
  other arithmetic  9.29 us (5%)
    ppermute x24, starting transfers between devices, local(): got = jnp.where(which == j, lax.ppermute(own, ('row', 'col'), fan), got)  55.5 us
    ppermute x7, waiting for transfers between devices, local(): a = lax.ppermute(a, 'col', forward)  45.3 us
    ppermute x7, waiting for transfers between devices, local(): b = lax.ppermute(b, 'col', backward)  16.9 us
    ppermute x7, starting transfers between devices, local(): b = lax.ppermute(b, 'col', backward)  14 us
    pallas_call x1, Pallas kernels, gram_call(): pl.pallas_call(kernel, grid_spec=pltpu.PrefetchScalarGridSpec(num_scalar_...  11.8 us
    another operation x17, local copies, waits for them, and re-layouts, local(): jnp.stack([columns[k // 2][:, k % 2 * half:(k % 2 + 1) * half, blk + 3, 0...  9.42 us
    concatenate x8, other arithmetic, local(): own = jnp.concatenate([pick_slot(a), pick_slot(b)], axis=1)  5.49 us
    ppermute x24, waiting for transfers between devices, local(): got = jnp.where(which == j, lax.ppermute(own, ('row', 'col'), fan), got)  5.41 us
  transfers between devices with their start and end apart: 38, of which 16 were waited for; matrix products, arithmetic and copies ran while one was open for 13% of the time, Pallas kernels for 0%

profile of v8, /device:TPU:0, one launch (start us, length us, event | category | flops | bytes accessed | tf_op | source)
XLA Modules:
  0.0 178.9 jit_solution(14881309754396462525)
XLA Ops:
  3.3 2.4 %collective-permute-start.16 = (bf16[3,4,144,128]{3,2,1,0:T(8,128)(2,1)S(1)}, bf16[3,4,144,128]{3,2,1,0:T(8,128)(2,1)S(1)}, u32[]{:S(2)}, u32[]{:S(2)}) collective-permute-start(bf16[3,4,144,128]{3,2,1,0:T(8,128)(2,1)S(1)} %pad_maximum_fusion), channel_id=1, source_target_pairs={{0,8},{1,9},{10,18},{11,19},{20,28},{21,29},{30,6},{31,7}} | collective-permute-start | bytes 1327112 | tf_op jit(solution)/shard_map/ppermute | solution.py:127
  5.7 3.9 %collective-permute-start.15 = (bf16[3,4,144,128]{3,2,1,0:T(8,128)(2,1)S(1)}, bf16[3,4,144,128]{3,2,1,0:T(8,128)(2,1)}, u32[]{:S(2)}, u32[]{:S(2)}) collective-permute-start(bf16[3,4,144,128]{3,2,1,0:T(8,128)(2,1)S(1)} %pad_maximum_fusion), channel_id=1, source_target_pairs={{0,16},{1,17},{10,26},{11,27},{20,4},{21,5},{30,14},{31,15}} | collective-permute-start | bytes 1327112 | tf_op jit(solution)/shard_map/ppermute | solution.py:127
  14.1 6.8 %collective-permute-done.refs_2_ = bf16[3,2,2,144,128]{4,3,2,1,0:T(8,128)(2,1)S(1)} collective-permute-done((bf16[3,2,2,144,128]{4,3,2,1,0:T(8,128)(2,1)S(1)}, bf16[3,2,2,144,128]{4,3,2,1,0:T(8,128)(2,1)S(1)}, u32[]{:S(2)}, u32[]{:S(2)}) %collective-permute-start) | collective-permute-done | bytes 442400 | tf_op jit(solution)/shard_map/ppermute | solution.py:121
  20.9 2.8 %collective-permute-done.1.refs_3_ = bf16[3,2,2,144,128]{4,3,2,1,0:T(8,128)(2,1)S(1)} collective-permute-done((bf16[3,2,2,144,128]{4,3,2,1,0:T(8,128)(2,1)S(1)}, bf16[3,2,2,144,128]{4,3,2,1,0:T(8,128)(2,1)S(1)}, u32[]{:S(2)}, u32[]{:S(2)}) %collective-permute-start.1) | collective-permute-done | bytes 442400 | tf_op jit(solution)/shard_map/ppermute | solution.py:122
  24.6 3.6 %collective-permute-start.19 = (bf16[3,4,144,128]{3,2,1,0:T(8,128)(2,1)}, bf16[3,4,144,128]{3,2,1,0:T(8,128)(2,1)}, u32[]{:S(2)}, u32[]{:S(2)}) collective-permute-start(bf16[3,4,144,128]{3,2,1,0:T(8,128)(2,1)} %pad_maximum_fusion.1), channel_id=1, source_target_pairs={{0,8},{1,9},{10,18},{11,19},{20,28},{21,29},{30,6},{31,7}} | collective-permute-start | bytes 1327112 | tf_op jit(solution)/shard_map/ppermute | solution.py:127
  28.1 2.1 %collective-permute-start.18 = (bf16[3,4,144,128]{3,2,1,0:T(8,128)(2,1)}, bf16[3,4,144,128]{3,2,1,0:T(8,128)(2,1)}, u32[]{:S(2)}, u32[]{:S(2)}) collective-permute-start(bf16[3,4,144,128]{3,2,1,0:T(8,128)(2,1)} %pad_maximum_fusion.1), channel_id=1, source_target_pairs={{0,16},{1,17},{10,26},{11,27},{20,4},{21,5},{30,14},{31,15}} | collective-permute-start | bytes 1327112 | tf_op jit(solution)/shard_map/ppermute | solution.py:127
  30.2 2.1 %collective-permute-start.17 = (bf16[3,4,144,128]{3,2,1,0:T(8,128)(2,1)}, bf16[3,4,144,128]{3,2,1,0:T(8,128)(2,1)}, u32[]{:S(2)}, u32[]{:S(2)}) collective-permute-start(bf16[3,4,144,128]{3,2,1,0:T(8,128)(2,1)} %pad_maximum_fusion.1), channel_id=1, source_target_pairs={{0,24},{1,25},{10,2},{11,3},{20,12},{21,13},{30,22},{31,23}} | collective-permute-start | bytes 1327112 | tf_op jit(solution)/shard_map/ppermute | solution.py:127
  36.4 5.7 %collective-permute-done.2.refs_4_ = bf16[3,2,2,144,128]{4,3,2,1,0:T(8,128)(2,1)S(1)} collective-permute-done((bf16[3,2,2,144,128]{4,3,2,1,0:T(8,128)(2,1)S(1)}, bf16[3,2,2,144,128]{4,3,2,1,0:T(8,128)(2,1)S(1)}, u32[]{:S(2)}, u32[]{:S(2)}) %collective-permute-start.2) | collective-permute-done | bytes 442400 | tf_op jit(solution)/shard_map/ppermute | solution.py:121
  42.1 2.8 %collective-permute-done.3.refs_5_ = bf16[3,2,2,144,128]{4,3,2,1,0:T(8,128)(2,1)S(1)} collective-permute-done((bf16[3,2,2,144,128]{4,3,2,1,0:T(8,128)(2,1)S(1)}, bf16[3,2,2,144,128]{4,3,2,1,0:T(8,128)(2,1)S(1)}, u32[]{:S(2)}, u32[]{:S(2)}) %collective-permute-start.3) | collective-permute-done | bytes 442400 | tf_op jit(solution)/shard_map/ppermute | solution.py:122
  45.8 3.4 %collective-permute-start.22 = (bf16[3,4,144,128]{3,2,1,0:T(8,128)(2,1)}, bf16[3,4,144,128]{3,2,1,0:T(8,128)(2,1)}, u32[]{:S(2)}, u32[]{:S(2)}) collective-permute-start(bf16[3,4,144,128]{3,2,1,0:T(8,128)(2,1)} %pad_maximum_fusion.2), channel_id=1, source_target_pairs={{0,8},{1,9},{10,18},{11,19},{20,28},{21,29},{30,6},{31,7}} | collective-permute-start | bytes 1327112 | tf_op jit(solution)/shard_map/ppermute | solution.py:127
  51.4 2.1 %collective-permute-start.20 = (bf16[3,4,144,128]{3,2,1,0:T(8,128)(2,1)}, bf16[3,4,144,128]{3,2,1,0:T(8,128)(2,1)}, u32[]{:S(2)}, u32[]{:S(2)}) collective-permute-start(bf16[3,4,144,128]{3,2,1,0:T(8,128)(2,1)} %pad_maximum_fusion.2), channel_id=1, source_target_pairs={{0,24},{1,25},{10,2},{11,3},{20,12},{21,13},{30,22},{31,23}} | collective-permute-start | bytes 1327112 | tf_op jit(solution)/shard_map/ppermute | solution.py:127
  58.2 6.2 %collective-permute-done.4.refs_6_ = bf16[3,2,2,144,128]{4,3,2,1,0:T(8,128)(2,1)S(1)} collective-permute-done((bf16[3,2,2,144,128]{4,3,2,1,0:T(8,128)(2,1)S(1)}, bf16[3,2,2,144,128]{4,3,2,1,0:T(8,128)(2,1)S(1)}, u32[]{:S(2)}, u32[]{:S(2)}) %collective-permute-start.4) | collective-permute-done | bytes 442400 | tf_op jit(solution)/shard_map/ppermute | solution.py:121
  64.4 2.9 %collective-permute-done.5.refs_7_ = bf16[3,2,2,144,128]{4,3,2,1,0:T(8,128)(2,1)S(1)} collective-permute-done((bf16[3,2,2,144,128]{4,3,2,1,0:T(8,128)(2,1)S(1)}, bf16[3,2,2,144,128]{4,3,2,1,0:T(8,128)(2,1)S(1)}, u32[]{:S(2)}, u32[]{:S(2)}) %collective-permute-start.5) | collective-permute-done | bytes 442400 | tf_op jit(solution)/shard_map/ppermute | solution.py:122
  68.3 2.6 %collective-permute-start.25 = (bf16[3,4,144,128]{3,2,1,0:T(8,128)(2,1)}, bf16[3,4,144,128]{3,2,1,0:T(8,128)(2,1)}, u32[]{:S(2)}, u32[]{:S(2)}) collective-permute-start(bf16[3,4,144,128]{3,2,1,0:T(8,128)(2,1)} %pad_maximum_fusion.3), channel_id=1, source_target_pairs={{0,8},{1,9},{10,18},{11,19},{20,28},{21,29},{30,6},{31,7}} | collective-permute-start | bytes 1327112 | tf_op jit(solution)/shard_map/ppermute | solution.py:127
  70.8 2.1 %collective-permute-start.24 = (bf16[3,4,144,128]{3,2,1,0:T(8,128)(2,1)}, bf16[3,4,144,128]{3,2,1,0:T(8,128)(2,1)}, u32[]{:S(2)}, u32[]{:S(2)}) collective-permute-start(bf16[3,4,144,128]{3,2,1,0:T(8,128)(2,1)} %pad_maximum_fusion.3), channel_id=1, source_target_pairs={{0,16},{1,17},{10,26},{11,27},{20,4},{21,5},{30,14},{31,15}} | collective-permute-start | bytes 1327112 | tf_op jit(solution)/shard_map/ppermute | solution.py:127
  73.6 2.1 %collective-permute-start.23 = (bf16[3,4,144,128]{3,2,1,0:T(8,128)(2,1)}, bf16[3,4,144,128]{3,2,1,0:T(8,128)(2,1)}, u32[]{:S(2)}, u32[]{:S(2)}) collective-permute-start(bf16[3,4,144,128]{3,2,1,0:T(8,128)(2,1)} %pad_maximum_fusion.3), channel_id=1, source_target_pairs={{0,24},{1,25},{10,2},{11,3},{20,12},{21,13},{30,22},{31,23}} | collective-permute-start | bytes 1327112 | tf_op jit(solution)/shard_map/ppermute | solution.py:127
  79.7 6.7 %collective-permute-done.6.refs_8_ = bf16[3,2,2,144,128]{4,3,2,1,0:T(8,128)(2,1)S(1)} collective-permute-done((bf16[3,2,2,144,128]{4,3,2,1,0:T(8,128)(2,1)S(1)}, bf16[3,2,2,144,128]{4,3,2,1,0:T(8,128)(2,1)S(1)}, u32[]{:S(2)}, u32[]{:S(2)}) %collective-permute-start.6) | collective-permute-done | bytes 442400 | tf_op jit(solution)/shard_map/ppermute | solution.py:121
  89.4 2.2 %collective-permute-start.28 = (bf16[3,4,144,128]{3,2,1,0:T(8,128)(2,1)}, bf16[3,4,144,128]{3,2,1,0:T(8,128)(2,1)}, u32[]{:S(2)}, u32[]{:S(2)}) collective-permute-start(bf16[3,4,144,128]{3,2,1,0:T(8,128)(2,1)} %pad_maximum_fusion.4), channel_id=1, source_target_pairs={{0,8},{1,9},{10,18},{11,19},{20,28},{21,29},{30,6},{31,7}} | collective-permute-start | bytes 1327112 | tf_op jit(solution)/shard_map/ppermute | solution.py:127
  91.6 2.1 %collective-permute-start.27 = (bf16[3,4,144,128]{3,2,1,0:T(8,128)(2,1)}, bf16[3,4,144,128]{3,2,1,0:T(8,128)(2,1)}, u32[]{:S(2)}, u32[]{:S(2)}) collective-permute-start(bf16[3,4,144,128]{3,2,1,0:T(8,128)(2,1)} %pad_maximum_fusion.4), channel_id=1, source_target_pairs={{0,16},{1,17},{10,26},{11,27},{20,4},{21,5},{30,14},{31,15}} | collective-permute-start | bytes 1327112 | tf_op jit(solution)/shard_map/ppermute | solution.py:127
  94.5 2.1 %collective-permute-start.26 = (bf16[3,4,144,128]{3,2,1,0:T(8,128)(2,1)}, bf16[3,4,144,128]{3,2,1,0:T(8,128)(2,1)}, u32[]{:S(2)}, u32[]{:S(2)}) collective-permute-start(bf16[3,4,144,128]{3,2,1,0:T(8,128)(2,1)} %pad_maximum_fusion.4), channel_id=1, source_target_pairs={{0,24},{1,25},{10,2},{11,3},{20,12},{21,13},{30,22},{31,23}} | collective-permute-start | bytes 1327112 | tf_op jit(solution)/shard_map/ppermute | solution.py:127
  100.6 6.7 %collective-permute-done.8.refs_10_ = bf16[3,2,2,144,128]{4,3,2,1,0:T(8,128)(2,1)S(1)} collective-permute-done((bf16[3,2,2,144,128]{4,3,2,1,0:T(8,128)(2,1)S(1)}, bf16[3,2,2,144,128]{4,3,2,1,0:T(8,128)(2,1)S(1)}, u32[]{:S(2)}, u32[]{:S(2)}) %collective-permute-start.8) | collective-permute-done | bytes 442400 | tf_op jit(solution)/shard_map/ppermute | solution.py:121
  107.2 2.6 %collective-permute-done.9.refs_11_ = bf16[3,2,2,144,128]{4,3,2,1,0:T(8,128)(2,1)S(1)} collective-permute-done((bf16[3,2,2,144,128]{4,3,2,1,0:T(8,128)(2,1)S(1)}, bf16[3,2,2,144,128]{4,3,2,1,0:T(8,128)(2,1)S(1)}, u32[]{:S(2)}, u32[]{:S(2)}) %collective-permute-start.9) | collective-permute-done | bytes 442400 | tf_op jit(solution)/shard_map/ppermute | solution.py:122
  110.7 2.7 %collective-permute-start.31 = (bf16[3,4,144,128]{3,2,1,0:T(8,128)(2,1)}, bf16[3,4,144,128]{3,2,1,0:T(8,128)(2,1)}, u32[]{:S(2)}, u32[]{:S(2)}) collective-permute-start(bf16[3,4,144,128]{3,2,1,0:T(8,128)(2,1)} %pad_maximum_fusion.5), channel_id=1, source_target_pairs={{0,8},{1,9},{10,18},{11,19},{20,28},{21,29},{30,6},{31,7}} | collective-permute-start | bytes 1327112 | tf_op jit(solution)/shard_map/ppermute | solution.py:127
  116.2 2.1 %collective-permute-start.29 = (bf16[3,4,144,128]{3,2,1,0:T(8,128)(2,1)}, bf16[3,4,144,128]{3,2,1,0:T(8,128)(2,1)}, u32[]{:S(2)}, u32[]{:S(2)}) collective-permute-start(bf16[3,4,144,128]{3,2,1,0:T(8,128)(2,1)} %pad_maximum_fusion.5), channel_id=1, source_target_pairs={{0,24},{1,25},{10,2},{11,3},{20,12},{21,13},{30,22},{31,23}} | collective-permute-start | bytes 1327112 | tf_op jit(solution)/shard_map/ppermute | solution.py:127
  122.3 6.7 %collective-permute-done.10.refs_12_ = bf16[3,2,2,144,128]{4,3,2,1,0:T(8,128)(2,1)S(1)} collective-permute-done((bf16[3,2,2,144,128]{4,3,2,1,0:T(8,128)(2,1)S(1)}, bf16[3,2,2,144,128]{4,3,2,1,0:T(8,128)(2,1)S(1)}, u32[]{:S(2)}, u32[]{:S(2)}) %collective-permute-start.10) | collective-permute-done | bytes 442400 | tf_op jit(solution)/shard_map/ppermute | solution.py:121
  131.5 2.1 %collective-permute-start.34 = (bf16[3,4,144,128]{3,2,1,0:T(8,128)(2,1)}, bf16[3,4,144,128]{3,2,1,0:T(8,128)(2,1)}, u32[]{:S(2)}, u32[]{:S(2)}) collective-permute-start(bf16[3,4,144,128]{3,2,1,0:T(8,128)(2,1)} %pad_maximum_fusion.6), channel_id=1, source_target_pairs={{0,8},{1,9},{10,18},{11,19},{20,28},{21,29},{30,6},{31,7}} | collective-permute-start | bytes 1327112 | tf_op jit(solution)/shard_map/ppermute | solution.py:127
  142.4 6.6 %collective-permute-done.12.refs_14_ = bf16[3,2,2,144,128]{4,3,2,1,0:T(8,128)(2,1)S(1)} collective-permute-done((bf16[3,2,2,144,128]{4,3,2,1,0:T(8,128)(2,1)S(1)}, bf16[3,2,2,144,128]{4,3,2,1,0:T(8,128)(2,1)S(1)}, u32[]{:S(2)}, u32[]{:S(2)}) %collective-permute-start.12) | collective-permute-done | bytes 442400 | tf_op jit(solution)/shard_map/ppermute | solution.py:121
  149.0 2.2 %collective-permute-done.13.refs_15_ = bf16[3,2,2,144,128]{4,3,2,1,0:T(8,128)(2,1)S(1)} collective-permute-done((bf16[3,2,2,144,128]{4,3,2,1,0:T(8,128)(2,1)S(1)}, bf16[3,2,2,144,128]{4,3,2,1,0:T(8,128)(2,1)S(1)}, u32[]{:S(2)}, u32[]{:S(2)}) %collective-permute-start.13) | collective-permute-done | bytes 442400 | tf_op jit(solution)/shard_map/ppermute | solution.py:122
  152.9 2.1 %collective-permute-start.36 = (bf16[3,4,144,128]{3,2,1,0:T(8,128)(2,1)S(1)}, bf16[3,4,144,128]{3,2,1,0:T(8,128)(2,1)}, u32[]{:S(2)}, u32[]{:S(2)}) collective-permute-start(bf16[3,4,144,128]{3,2,1,0:T(8,128)(2,1)S(1)} %pad_maximum_fusion.7), channel_id=1, source_target_pairs={{0,16},{1,17},{10,26},{11,27},{20,4},{21,5},{30,14},{31,15}} | collective-permute-start | bytes 1327112 | tf_op jit(solution)/shard_map/ppermute | solution.py:127
  155.7 2.1 %collective-permute-start.35 = (bf16[3,4,144,128]{3,2,1,0:T(8,128)(2,1)S(1)}, bf16[3,4,144,128]{3,2,1,0:T(8,128)(2,1)}, u32[]{:S(2)}, u32[]{:S(2)}) collective-permute-start(bf16[3,4,144,128]{3,2,1,0:T(8,128)(2,1)S(1)} %pad_maximum_fusion.7), channel_id=1, source_target_pairs={{0,24},{1,25},{10,2},{11,3},{20,12},{21,13},{30,22},{31,23}} | collective-permute-start | bytes 1327112 | tf_op jit(solution)/shard_map/ppermute | solution.py:127
  160.0 4.7 %collective-permute-done.35 = bf16[3,4,144,128]{3,2,1,0:T(8,128)(2,1)} collective-permute-done((bf16[3,4,144,128]{3,2,1,0:T(8,128)(2,1)S(1)}, bf16[3,4,144,128]{3,2,1,0:T(8,128)(2,1)}, u32[]{:S(2)}, u32[]{:S(2)}) %collective-permute-start.35) | collective-permute-done | bytes 442400 | tf_op jit(solution)/shard_map/ppermute | solution.py:127
  167.1 11.8 %shard_map.37 = f32[2048,1024]{1,0:T(8,128)} custom-call(s32[288]{0:T(512)} %min.12.offs_ref, bf16[3,2,2,144,128]{4,3,2,1,0:T(8,128)(2,1)} %copy-done, bf16[3,2,2,144,128]{4,3,2,1,0:T(8,128)(2,1)} %copy-done.1, bf16[3,2,2,144,128]{4,3,2,1,0:T(8,128)(2,1)} %copy-done.10, bf16[3,2,2,144,128]{4,3,2,1,0:T(8,128)(2,1)} %copy-done.11, ...), custom_call_target="tpu_custom_call" | custom-call | flops 805306368 | bytes 17825792 | tf_op jit(solution)/shard_map/pallas_call | solution.py:56
  (237 shorter events, 59.5 us)
Async XLA Ops:
  3.3 26.9 %collective-permute-start.16 = (bf16[3,4,144,128]{3,2,1,0:T(8,128)(2,1)S(1)}, bf16[3,4,144,128]{3,2,1,0:T(8,128)(2,1)S(1)}, u32[]{:S(2)}, u32[]{:S(2)}) collective-permute-start(bf16[3,4,144,128]{3,2,1,0:T(8,128)(2,1)S(1)} %pad_maximum_fusion), channel_id=1, source_target_pairs={{0,8},{1,9},{10,18},{11,19},{20,28},{21,29},{30,6},{31,7}} | collective-permute-start | bytes 1327112 | tf_op jit(solution)/shard_map/ppermute | solution.py:127
  5.7 26.6 %collective-permute-start.15 = (bf16[3,4,144,128]{3,2,1,0:T(8,128)(2,1)S(1)}, bf16[3,4,144,128]{3,2,1,0:T(8,128)(2,1)}, u32[]{:S(2)}, u32[]{:S(2)}) collective-permute-start(bf16[3,4,144,128]{3,2,1,0:T(8,128)(2,1)S(1)} %pad_maximum_fusion), channel_id=1, source_target_pairs={{0,16},{1,17},{10,26},{11,27},{20,4},{21,5},{30,14},{31,15}} | collective-permute-start | bytes 1327112 | tf_op jit(solution)/shard_map/ppermute | solution.py:127
  9.6 22.7 %collective-permute-start.14 = (bf16[3,4,144,128]{3,2,1,0:T(8,128)(2,1)S(1)}, bf16[3,4,144,128]{3,2,1,0:T(8,128)(2,1)}, u32[]{:S(2)}, u32[]{:S(2)}) collective-permute-start(bf16[3,4,144,128]{3,2,1,0:T(8,128)(2,1)S(1)} %pad_maximum_fusion), channel_id=1, source_target_pairs={{0,24},{1,25},{10,2},{11,3},{20,12},{21,13},{30,22},{31,23}} | collective-permute-start | bytes 1327112 | tf_op jit(solution)/shard_map/ppermute | solution.py:127
  11.7 12.0 %collective-permute-start.1 = (bf16[3,2,2,144,128]{4,3,2,1,0:T(8,128)(2,1)S(1)}, bf16[3,2,2,144,128]{4,3,2,1,0:T(8,128)(2,1)S(1)}, u32[]{:S(2)}, u32[]{:S(2)}) collective-permute-start(bf16[3,2,2,144,128]{4,3,2,1,0:T(8,128)(2,1)S(1)} %get-tuple-element.6.refs_1_), channel_id=1, source_target_pairs={{2,0},{4,2},{6,4},{7,6},{5,7},{3,5},{1,3},{0,1},{10,8},{12,10},{14... | collective-permute-start | bytes 1327112 | tf_op jit(solution)/shard_map/ppermute | solution.py:122
  24.6 26.8 %collective-permute-start.19 = (bf16[3,4,144,128]{3,2,1,0:T(8,128)(2,1)}, bf16[3,4,144,128]{3,2,1,0:T(8,128)(2,1)}, u32[]{:S(2)}, u32[]{:S(2)}) collective-permute-start(bf16[3,4,144,128]{3,2,1,0:T(8,128)(2,1)} %pad_maximum_fusion.1), channel_id=1, source_target_pairs={{0,8},{1,9},{10,18},{11,19},{20,28},{21,29},{30,6},{31,7}} | collective-permute-start | bytes 1327112 | tf_op jit(solution)/shard_map/ppermute | solution.py:127
  28.1 25.3 %collective-permute-start.18 = (bf16[3,4,144,128]{3,2,1,0:T(8,128)(2,1)}, bf16[3,4,144,128]{3,2,1,0:T(8,128)(2,1)}, u32[]{:S(2)}, u32[]{:S(2)}) collective-permute-start(bf16[3,4,144,128]{3,2,1,0:T(8,128)(2,1)} %pad_maximum_fusion.1), channel_id=1, source_target_pairs={{0,16},{1,17},{10,26},{11,27},{20,4},{21,5},{30,14},{31,15}} | collective-permute-start | bytes 1327112 | tf_op jit(solution)/shard_map/ppermute | solution.py:127
  30.2 23.2 %collective-permute-start.17 = (bf16[3,4,144,128]{3,2,1,0:T(8,128)(2,1)}, bf16[3,4,144,128]{3,2,1,0:T(8,128)(2,1)}, u32[]{:S(2)}, u32[]{:S(2)}) collective-permute-start(bf16[3,4,144,128]{3,2,1,0:T(8,128)(2,1)} %pad_maximum_fusion.1), channel_id=1, source_target_pairs={{0,24},{1,25},{10,2},{11,3},{20,12},{21,13},{30,22},{31,23}} | collective-permute-start | bytes 1327112 | tf_op jit(solution)/shard_map/ppermute | solution.py:127
  32.6 12.3 %collective-permute-start.3 = (bf16[3,2,2,144,128]{4,3,2,1,0:T(8,128)(2,1)S(1)}, bf16[3,2,2,144,128]{4,3,2,1,0:T(8,128)(2,1)S(1)}, u32[]{:S(2)}, u32[]{:S(2)}) collective-permute-start(bf16[3,2,2,144,128]{4,3,2,1,0:T(8,128)(2,1)S(1)} %collective-permute-done.1.refs_3_), channel_id=1, source_target_pairs={{2,0},{4,2},{6,4},{7,6},{5,7},{3,5},{1,3},{0,1},{10,8},{12,10},{14... | collective-permute-start | bytes 1327112 | tf_op jit(solution)/shard_map/ppermute | solution.py:122
  45.8 27.8 %collective-permute-start.22 = (bf16[3,4,144,128]{3,2,1,0:T(8,128)(2,1)}, bf16[3,4,144,128]{3,2,1,0:T(8,128)(2,1)}, u32[]{:S(2)}, u32[]{:S(2)}) collective-permute-start(bf16[3,4,144,128]{3,2,1,0:T(8,128)(2,1)} %pad_maximum_fusion.2), channel_id=1, source_target_pairs={{0,8},{1,9},{10,18},{11,19},{20,28},{21,29},{30,6},{31,7}} | collective-permute-start | bytes 1327112 | tf_op jit(solution)/shard_map/ppermute | solution.py:127
  49.2 26.5 %collective-permute-start.21 = (bf16[3,4,144,128]{3,2,1,0:T(8,128)(2,1)}, bf16[3,4,144,128]{3,2,1,0:T(8,128)(2,1)}, u32[]{:S(2)}, u32[]{:S(2)}) collective-permute-start(bf16[3,4,144,128]{3,2,1,0:T(8,128)(2,1)} %pad_maximum_fusion.2), channel_id=1, source_target_pairs={{0,16},{1,17},{10,26},{11,27},{20,4},{21,5},{30,14},{31,15}} | collective-permute-start | bytes 1327112 | tf_op jit(solution)/shard_map/ppermute | solution.py:127
  51.4 24.3 %collective-permute-start.20 = (bf16[3,4,144,128]{3,2,1,0:T(8,128)(2,1)}, bf16[3,4,144,128]{3,2,1,0:T(8,128)(2,1)}, u32[]{:S(2)}, u32[]{:S(2)}) collective-permute-start(bf16[3,4,144,128]{3,2,1,0:T(8,128)(2,1)} %pad_maximum_fusion.2), channel_id=1, source_target_pairs={{0,24},{1,25},{10,2},{11,3},{20,12},{21,13},{30,22},{31,23}} | collective-permute-start | bytes 1327112 | tf_op jit(solution)/shard_map/ppermute | solution.py:127
  53.7 10.7 %collective-permute-start.4 = (bf16[3,2,2,144,128]{4,3,2,1,0:T(8,128)(2,1)S(1)}, bf16[3,2,2,144,128]{4,3,2,1,0:T(8,128)(2,1)S(1)}, u32[]{:S(2)}, u32[]{:S(2)}) collective-permute-start(bf16[3,2,2,144,128]{4,3,2,1,0:T(8,128)(2,1)S(1)} %collective-permute-done.2.refs_4_), channel_id=1, source_target_pairs={{0,2},{2,4},{4,6},{6,7},{7,5},{5,3},{3,1},{1,0},{8,10},{10,12},{12... | collective-permute-start | bytes 1327112 | tf_op jit(solution)/shard_map/ppermute | solution.py:121
  54.5 12.9 %collective-permute-start.5 = (bf16[3,2,2,144,128]{4,3,2,1,0:T(8,128)(2,1)S(1)}, bf16[3,2,2,144,128]{4,3,2,1,0:T(8,128)(2,1)S(1)}, u32[]{:S(2)}, u32[]{:S(2)}) collective-permute-start(bf16[3,2,2,144,128]{4,3,2,1,0:T(8,128)(2,1)S(1)} %copy-done.14), channel_id=1, source_target_pairs={{2,0},{4,2},{6,4},{7,6},{5,7},{3,5},{1,3},{0,1},{10,8},{12,10},{14... | collective-permute-start | bytes 1327112 | tf_op jit(solution)/shard_map/ppermute | solution.py:122
  68.3 26.2 %collective-permute-start.25 = (bf16[3,4,144,128]{3,2,1,0:T(8,128)(2,1)}, bf16[3,4,144,128]{3,2,1,0:T(8,128)(2,1)}, u32[]{:S(2)}, u32[]{:S(2)}) collective-permute-start(bf16[3,4,144,128]{3,2,1,0:T(8,128)(2,1)} %pad_maximum_fusion.3), channel_id=1, source_target_pairs={{0,8},{1,9},{10,18},{11,19},{20,28},{21,29},{30,6},{31,7}} | collective-permute-start | bytes 1327112 | tf_op jit(solution)/shard_map/ppermute | solution.py:127
  70.8 25.7 %collective-permute-start.24 = (bf16[3,4,144,128]{3,2,1,0:T(8,128)(2,1)}, bf16[3,4,144,128]{3,2,1,0:T(8,128)(2,1)}, u32[]{:S(2)}, u32[]{:S(2)}) collective-permute-start(bf16[3,4,144,128]{3,2,1,0:T(8,128)(2,1)} %pad_maximum_fusion.3), channel_id=1, source_target_pairs={{0,16},{1,17},{10,26},{11,27},{20,4},{21,5},{30,14},{31,15}} | collective-permute-start | bytes 1327112 | tf_op jit(solution)/shard_map/ppermute | solution.py:127
  73.6 22.9 %collective-permute-start.23 = (bf16[3,4,144,128]{3,2,1,0:T(8,128)(2,1)}, bf16[3,4,144,128]{3,2,1,0:T(8,128)(2,1)}, u32[]{:S(2)}, u32[]{:S(2)}) collective-permute-start(bf16[3,4,144,128]{3,2,1,0:T(8,128)(2,1)} %pad_maximum_fusion.3), channel_id=1, source_target_pairs={{0,24},{1,25},{10,2},{11,3},{20,12},{21,13},{30,22},{31,23}} | collective-permute-start | bytes 1327112 | tf_op jit(solution)/shard_map/ppermute | solution.py:127
  75.9 10.5 %collective-permute-start.6 = (bf16[3,2,2,144,128]{4,3,2,1,0:T(8,128)(2,1)S(1)}, bf16[3,2,2,144,128]{4,3,2,1,0:T(8,128)(2,1)S(1)}, u32[]{:S(2)}, u32[]{:S(2)}) collective-permute-start(bf16[3,2,2,144,128]{4,3,2,1,0:T(8,128)(2,1)S(1)} %collective-permute-done.4.refs_6_), channel_id=1, source_target_pairs={{0,2},{2,4},{4,6},{6,7},{7,5},{5,3},{3,1},{1,0},{8,10},{10,12},{12... | collective-permute-start | bytes 1327112 | tf_op jit(solution)/shard_map/ppermute | solution.py:121
  75.9 12.5 %collective-permute-start.7 = (bf16[3,2,2,144,128]{4,3,2,1,0:T(8,128)(2,1)S(1)}, bf16[3,2,2,144,128]{4,3,2,1,0:T(8,128)(2,1)S(1)}, u32[]{:S(2)}, u32[]{:S(2)}) collective-permute-start(bf16[3,2,2,144,128]{4,3,2,1,0:T(8,128)(2,1)S(1)} %collective-permute-done.5.refs_7_), channel_id=1, source_target_pairs={{2,0},{4,2},{6,4},{7,6},{5,7},{3,5},{1,3},{0,1},{10,8},{12,10},{14... | collective-permute-start | bytes 1327112 | tf_op jit(solution)/shard_map/ppermute | solution.py:122
  89.4 26.8 %collective-permute-start.28 = (bf16[3,4,144,128]{3,2,1,0:T(8,128)(2,1)}, bf16[3,4,144,128]{3,2,1,0:T(8,128)(2,1)}, u32[]{:S(2)}, u32[]{:S(2)}) collective-permute-start(bf16[3,4,144,128]{3,2,1,0:T(8,128)(2,1)} %pad_maximum_fusion.4), channel_id=1, source_target_pairs={{0,8},{1,9},{10,18},{11,19},{20,28},{21,29},{30,6},{31,7}} | collective-permute-start | bytes 1327112 | tf_op jit(solution)/shard_map/ppermute | solution.py:127
  91.6 26.6 %collective-permute-start.27 = (bf16[3,4,144,128]{3,2,1,0:T(8,128)(2,1)}, bf16[3,4,144,128]{3,2,1,0:T(8,128)(2,1)}, u32[]{:S(2)}, u32[]{:S(2)}) collective-permute-start(bf16[3,4,144,128]{3,2,1,0:T(8,128)(2,1)} %pad_maximum_fusion.4), channel_id=1, source_target_pairs={{0,16},{1,17},{10,26},{11,27},{20,4},{21,5},{30,14},{31,15}} | collective-permute-start | bytes 1327112 | tf_op jit(solution)/shard_map/ppermute | solution.py:127
  94.5 23.8 %collective-permute-start.26 = (bf16[3,4,144,128]{3,2,1,0:T(8,128)(2,1)}, bf16[3,4,144,128]{3,2,1,0:T(8,128)(2,1)}, u32[]{:S(2)}, u32[]{:S(2)}) collective-permute-start(bf16[3,4,144,128]{3,2,1,0:T(8,128)(2,1)} %pad_maximum_fusion.4), channel_id=1, source_target_pairs={{0,24},{1,25},{10,2},{11,3},{20,12},{21,13},{30,22},{31,23}} | collective-permute-start | bytes 1327112 | tf_op jit(solution)/shard_map/ppermute | solution.py:127
  96.7 10.5 %collective-permute-start.8 = (bf16[3,2,2,144,128]{4,3,2,1,0:T(8,128)(2,1)S(1)}, bf16[3,2,2,144,128]{4,3,2,1,0:T(8,128)(2,1)S(1)}, u32[]{:S(2)}, u32[]{:S(2)}) collective-permute-start(bf16[3,2,2,144,128]{4,3,2,1,0:T(8,128)(2,1)S(1)} %collective-permute-done.6.refs_8_), channel_id=1, source_target_pairs={{0,2},{2,4},{4,6},{6,7},{7,5},{5,3},{3,1},{1,0},{8,10},{10,12},{12... | collective-permute-start | bytes 1327112 | tf_op jit(solution)/shard_map/ppermute | solution.py:121
  96.8 13.0 %collective-permute-start.9 = (bf16[3,2,2,144,128]{4,3,2,1,0:T(8,128)(2,1)S(1)}, bf16[3,2,2,144,128]{4,3,2,1,0:T(8,128)(2,1)S(1)}, u32[]{:S(2)}, u32[]{:S(2)}) collective-permute-start(bf16[3,2,2,144,128]{4,3,2,1,0:T(8,128)(2,1)S(1)} %collective-permute-done.7.refs_9_), channel_id=1, source_target_pairs={{2,0},{4,2},{6,4},{7,6},{5,7},{3,5},{1,3},{0,1},{10,8},{12,10},{14... | collective-permute-start | bytes 1327112 | tf_op jit(solution)/shard_map/ppermute | solution.py:122
  110.7 25.6 %collective-permute-start.31 = (bf16[3,4,144,128]{3,2,1,0:T(8,128)(2,1)}, bf16[3,4,144,128]{3,2,1,0:T(8,128)(2,1)}, u32[]{:S(2)}, u32[]{:S(2)}) collective-permute-start(bf16[3,4,144,128]{3,2,1,0:T(8,128)(2,1)} %pad_maximum_fusion.5), channel_id=1, source_target_pairs={{0,8},{1,9},{10,18},{11,19},{20,28},{21,29},{30,6},{31,7}} | collective-permute-start | bytes 1327112 | tf_op jit(solution)/shard_map/ppermute | solution.py:127
  113.4 25.0 %collective-permute-start.30 = (bf16[3,4,144,128]{3,2,1,0:T(8,128)(2,1)}, bf16[3,4,144,128]{3,2,1,0:T(8,128)(2,1)}, u32[]{:S(2)}, u32[]{:S(2)}) collective-permute-start(bf16[3,4,144,128]{3,2,1,0:T(8,128)(2,1)} %pad_maximum_fusion.5), channel_id=1, source_target_pairs={{0,16},{1,17},{10,26},{11,27},{20,4},{21,5},{30,14},{31,15}} | collective-permute-start | bytes 1327112 | tf_op jit(solution)/shard_map/ppermute | solution.py:127
  116.2 22.2 %collective-permute-start.29 = (bf16[3,4,144,128]{3,2,1,0:T(8,128)(2,1)}, bf16[3,4,144,128]{3,2,1,0:T(8,128)(2,1)}, u32[]{:S(2)}, u32[]{:S(2)}) collective-permute-start(bf16[3,4,144,128]{3,2,1,0:T(8,128)(2,1)} %pad_maximum_fusion.5), channel_id=1, source_target_pairs={{0,24},{1,25},{10,2},{11,3},{20,12},{21,13},{30,22},{31,23}} | collective-permute-start | bytes 1327112 | tf_op jit(solution)/shard_map/ppermute | solution.py:127
  118.4 10.5 %collective-permute-start.10 = (bf16[3,2,2,144,128]{4,3,2,1,0:T(8,128)(2,1)S(1)}, bf16[3,2,2,144,128]{4,3,2,1,0:T(8,128)(2,1)S(1)}, u32[]{:S(2)}, u32[]{:S(2)}) collective-permute-start(bf16[3,2,2,144,128]{4,3,2,1,0:T(8,128)(2,1)S(1)} %collective-permute-done.8.refs_10_), channel_id=1, source_target_pairs={{0,2},{2,4},{4,6},{6,7},{7,5},{5,3},{3,1},{1,0},{8,10},{10,12},{12... | collective-permute-start | bytes 1327112 | tf_op jit(solution)/shard_map/ppermute | solution.py:121
  118.5 12.0 %collective-permute-start.11 = (bf16[3,2,2,144,128]{4,3,2,1,0:T(8,128)(2,1)S(1)}, bf16[3,2,2,144,128]{4,3,2,1,0:T(8,128)(2,1)S(1)}, u32[]{:S(2)}, u32[]{:S(2)}) collective-permute-start(bf16[3,2,2,144,128]{4,3,2,1,0:T(8,128)(2,1)S(1)} %collective-permute-done.9.refs_11_), channel_id=1, source_target_pairs={{2,0},{4,2},{6,4},{7,6},{5,7},{3,5},{1,3},{0,1},{10,8},{12,10},{14... | collective-permute-start | bytes 1327112 | tf_op jit(solution)/shard_map/ppermute | solution.py:122
  131.5 24.2 %collective-permute-start.34 = (bf16[3,4,144,128]{3,2,1,0:T(8,128)(2,1)}, bf16[3,4,144,128]{3,2,1,0:T(8,128)(2,1)}, u32[]{:S(2)}, u32[]{:S(2)}) collective-permute-start(bf16[3,4,144,128]{3,2,1,0:T(8,128)(2,1)} %pad_maximum_fusion.6), channel_id=1, source_target_pairs={{0,8},{1,9},{10,18},{11,19},{20,28},{21,29},{30,6},{31,7}} | collective-permute-start | bytes 1327112 | tf_op jit(solution)/shard_map/ppermute | solution.py:127
  133.6 24.2 %collective-permute-start.33 = (bf16[3,4,144,128]{3,2,1,0:T(8,128)(2,1)}, bf16[3,4,144,128]{3,2,1,0:T(8,128)(2,1)}, u32[]{:S(2)}, u32[]{:S(2)}) collective-permute-start(bf16[3,4,144,128]{3,2,1,0:T(8,128)(2,1)} %pad_maximum_fusion.6), channel_id=1, source_target_pairs={{0,16},{1,17},{10,26},{11,27},{20,4},{21,5},{30,14},{31,15}} | collective-permute-start | bytes 1327112 | tf_op jit(solution)/shard_map/ppermute | solution.py:127
  136.3 21.5 %collective-permute-start.32 = (bf16[3,4,144,128]{3,2,1,0:T(8,128)(2,1)}, bf16[3,4,144,128]{3,2,1,0:T(8,128)(2,1)}, u32[]{:S(2)}, u32[]{:S(2)}) collective-permute-start(bf16[3,4,144,128]{3,2,1,0:T(8,128)(2,1)} %pad_maximum_fusion.6), channel_id=1, source_target_pairs={{0,24},{1,25},{10,2},{11,3},{20,12},{21,13},{30,22},{31,23}} | collective-permute-start | bytes 1327112 | tf_op jit(solution)/shard_map/ppermute | solution.py:127
  138.7 12.6 %collective-permute-start.13 = (bf16[3,2,2,144,128]{4,3,2,1,0:T(8,128)(2,1)S(1)}, bf16[3,2,2,144,128]{4,3,2,1,0:T(8,128)(2,1)S(1)}, u32[]{:S(2)}, u32[]{:S(2)}) collective-permute-start(bf16[3,2,2,144,128]{4,3,2,1,0:T(8,128)(2,1)S(1)} %collective-permute-done.11.refs_13_), channel_id=1, source_target_pairs={{2,0},{4,2},{6,4},{7,6},{5,7},{3,5},{1,3},{0,1},{10,8},{12,10},{14... | collective-permute-start | bytes 1327112 | tf_op jit(solution)/shard_map/ppermute | solution.py:122
  (35 other events, 394.7 us)

commit v9 on v6

--- a/solution.py
+++ b/solution.py
@@ -93,32 +93,53 @@
     backward = [(b, a) for a, b in forward]
 
     src = c // local_slots
-    which = (r - src + nrow) % nrow
     slot = c % local_slots
-    fans = [
-        [
-            ((cc // local_slots) * ncol + cc, ((cc // local_slots + j) % nrow) * ncol + cc)
-            for cc in range(ncol)
-        ]
-        for j in range(1, nrow)
-    ]
+    nx = nrow // 2
+    up = (r - src + nrow) % nrow
+    is_s, is_p, is_d1 = up == 0, r == src + 1 - 2 * (src % 2), (up % 2 == 0) & (up != 0)
+    chip_step = up // 2
+
+    def send(v, pairs):
+        return lax.ppermute(v, ("row", "col"), [(a * ncol + cc, b * ncol + cc) for a, b, cc in pairs])
+
+    first_hop = []
+    for cc in range(ncol):
+        s0 = cc // local_slots
+        first_hop.append((s0, s0 ^ 1, cc))
+        first_hop += [((s0 + 2 * j) % nrow, ((s0 + 2 * j) % nrow) ^ 1, cc) for j in range(1, nx)]
+    cross = [[(cc // local_slots, (cc // local_slots + 2 * j) % nrow, cc) for cc in range(ncol)] for j in range(1, nx)]
 
     def pick_slot(piece):
         return lax.dynamic_index_in_dim(piece, slot, axis=2, keepdims=False)
 
     half = x.shape[1] // 2
     a, b = x[:, :half], x[:, half:]
-    pieces, columns = [], []
-    for step in range(ncol):
-        if step:
-            a = lax.ppermute(a, "col", forward)
-            b = lax.ppermute(b, "col", backward)
-        pieces += [a, b]
-        own = jnp.concatenate([pick_slot(a), pick_slot(b)], axis=1)
-        got = own
-        for j, fan in enumerate(fans, start=1):
-            got = jnp.where(which == j, lax.ppermute(own, ("row", "col"), fan), got)
-        columns.append(got)
+    pieces, owns, hops, crossed = [], [], [], []
+    forwarded = None
+    for step in range(ncol + 1):
+        if step < ncol:
+            if step:
+                a = lax.ppermute(a, "col", forward)
+                b = lax.ppermute(b, "col", backward)
+            pieces += [a, b]
+            own = jnp.concatenate([pick_slot(a), pick_slot(b)], axis=1)
+            owns.append(own)
+            operand = own if forwarded is None else jnp.where(is_s, own, forwarded)
+        else:
+            operand = forwarded
+        hops.append(send(operand, first_hop))
+        if step < ncol:
+            got = None
+            for j, pairs in enumerate(cross, start=1):
+                v = send(own, pairs)
+                got = v if got is None else jnp.where(chip_step == j, v, got)
+            crossed.append(got)
+            forwarded = got
+
+    columns = [
+        jnp.where(is_s, owns[k], jnp.where(is_p, hops[k], jnp.where(is_d1, crossed[k], hops[k + 1])))
+        for k in range(ncol)
+    ]
 
     blocks = jnp.concatenate(pieces, axis=1)
     column_blocks = jnp.concatenate(columns, axis=1)

time: 136 us -> 141 us (1.037)
  the two profiles are of different devices: /device:TPU:14 before, /device:TPU:0 now
where the time goes in v9:
time: 141 us
  starting transfers between devices  55.2 us (39%)
  waiting for transfers between devices  39.5 us (28%)
  local copies, waits for them, and re-layouts  18.6 us (13%)
  Pallas kernels  14.6 us (10%)
  other arithmetic  12 us (9%)
    ppermute x17, starting transfers between devices, send(): lax.ppermute(v, ('row', 'col'), [(a * ncol + cc, b * ncol + cc) for a, b,...  39.3 us
    ppermute x7, waiting for transfers between devices, local(): b = lax.ppermute(b, 'col', backward)  30 us
    pallas_call x1, Pallas kernels, gram_call(): pl.pallas_call(kernel, grid_spec=pltpu.PrefetchScalarGridSpec(num_scalar_...  14.6 us
    unnamed x43, local copies, waits for them, and re-layouts  11.9 us
    ppermute x7, waiting for transfers between devices, local(): a = lax.ppermute(a, 'col', forward)  9.45 us
    ppermute x7, starting transfers between devices, local(): b = lax.ppermute(b, 'col', backward)  8.29 us
    ppermute x7, starting transfers between devices, local(): a = lax.ppermute(a, 'col', forward)  7.59 us
    unnamed x8, other arithmetic  6.65 us
  transfers between devices with their start and end apart: 31, of which 7 were waited for; matrix products, arithmetic and copies ran while one was open for 16% of the time, Pallas kernels for 0%

profile of v9, /device:TPU:0, one launch (start us, length us, event | category | flops | bytes accessed | tf_op | source)
XLA Modules:
  0.0 140.5 jit_solution(5688301333778950333)
XLA Ops:
  1.7 2.4 %constant_dynamic-update-slice_fusion.14 = (bf16[3,32,2,144,128]{4,3,2,1,0:T(8,128)(2,1)}, bf16[3,4,2,144,128]{4,3,2,1,0:T(8,128)(2,1)S(1)}) fusion(bf16[144]{0:T(256)(128)(2,1)S(1)} %pad.21.clone, bf16[3,4,2,1,128]{4,3,2,1,0:T(2,128)(2,1)S(1)} %broadcast_in_dim.7, bf16[3,4,2,3,128]{4,3,2,1,0:T(4,128)(2,1)S(1)} %broadcast_in_dim.6, ...), kind=kLoop, calls=%fused_computation.55 | loop fusion | flops 3538943 | bytes 2580768
  4.2 3.1 %collective-permute-start = (bf16[3,2,2,144,128]{4,3,2,1,0:T(8,128)(2,1)S(1)}, bf16[3,2,2,144,128]{4,3,2,1,0:T(8,128)(2,1)S(1)}, u32[]{:S(2)}, u32[]{:S(2)}) collective-permute-start(bf16[3,2,2,144,128]{4,3,2,1,0:T(8,128)(2,1)S(1)} %get-tuple-element.5), channel_id=1, source_target_pairs={{0,2},{2,4},{4,6},{6,7},{7,5},{5,3},{3,1},{1,0},{8,10},{10,12},{12... | collective-permute-start | bytes 1327112 | tf_op jit(solution)/shard_map/ppermute | solution.py:122
  8.1 3.9 %collective-permute-start.15 = (bf16[3,4,144,128]{3,2,1,0:T(8,128)(2,1)S(1)}, bf16[3,4,144,128]{3,2,1,0:T(8,128)(2,1)S(1)}, u32[]{:S(2)}, u32[]{:S(2)}) collective-permute-start(bf16[3,4,144,128]{3,2,1,0:T(8,128)(2,1)S(1)} %pad_maximum_fusion), channel_id=1, source_target_pairs={{0,16},{1,17},{10,26},{11,27},{20,4},{21,5},{30,14},{31,15}} | collective-permute-start | bytes 1327112 | tf_op jit(solution)/shard_map/ppermute | solution.py:103
  12.0 1.3 collective-permute-start.14
  13.4 4.0 %collective-permute-done = bf16[3,2,2,144,128]{4,3,2,1,0:T(8,128)(2,1)S(1)} collective-permute-done((bf16[3,2,2,144,128]{4,3,2,1,0:T(8,128)(2,1)S(1)}, bf16[3,2,2,144,128]{4,3,2,1,0:T(8,128)(2,1)S(1)}, u32[]{:S(2)}, u32[]{:S(2)}) %collective-permute-start) | collective-permute-done | bytes 442400 | tf_op jit(solution)/shard_map/ppermute | solution.py:122
  17.4 1.8 %collective-permute-start.2 = (bf16[3,2,2,144,128]{4,3,2,1,0:T(8,128)(2,1)S(1)}, bf16[3,2,2,144,128]{4,3,2,1,0:T(8,128)(2,1)S(1)}, u32[]{:S(2)}, u32[]{:S(2)}) collective-permute-start(bf16[3,2,2,144,128]{4,3,2,1,0:T(8,128)(2,1)S(1)} %collective-permute-done), channel_id=1, source_target_pairs={{0,2},{2,4},{4,6},{6,7},{7,5},{5,3},{3,1},{1,0},{8,10},{10,12},{12... | collective-permute-start | bytes 1327112 | tf_op jit(solution)/shard_map/ppermute | solution.py:122
  19.6 3.6 %collective-permute-start.17 = (bf16[3,4,144,128]{3,2,1,0:T(8,128)(2,1)S(1)}, bf16[3,4,144,128]{3,2,1,0:T(8,128)(2,1)S(1)}, u32[]{:S(2)}, u32[]{:S(2)}) collective-permute-start(bf16[3,4,144,128]{3,2,1,0:T(8,128)(2,1)S(1)} %get-tuple-element.21), channel_id=1, source_target_pairs={{0,16},{1,17},{10,26},{11,27},{20,4},{21,5},{30,14},{31,15}} | collective-permute-start | bytes 1327112 | tf_op jit(solution)/shard_map/ppermute | solution.py:103
  23.2 1.3 collective-permute-start.16
  26.3 3.7 %collective-permute-done.3 = bf16[3,2,2,144,128]{4,3,2,1,0:T(8,128)(2,1)S(1)} collective-permute-done((bf16[3,2,2,144,128]{4,3,2,1,0:T(8,128)(2,1)S(1)}, bf16[3,2,2,144,128]{4,3,2,1,0:T(8,128)(2,1)S(1)}, u32[]{:S(2)}, u32[]{:S(2)}) %collective-permute-start.3) | collective-permute-done | bytes 442400 | tf_op jit(solution)/shard_map/ppermute | solution.py:123
  30.1 3.4 %collective-permute-start.19 = (bf16[3,4,144,128]{3,2,1,0:T(8,128)(2,1)S(1)}, bf16[3,4,144,128]{3,2,1,0:T(8,128)(2,1)S(1)}, u32[]{:S(2)}, u32[]{:S(2)}) collective-permute-start(bf16[3,4,144,128]{3,2,1,0:T(8,128)(2,1)S(1)} %get-tuple-element.19), channel_id=1, source_target_pairs={{0,16},{1,17},{10,26},{11,27},{20,4},{21,5},{30,14},{31,15}} | collective-permute-start | bytes 1327112 | tf_op jit(solution)/shard_map/ppermute | solution.py:103
  33.6 2.0 %collective-permute-start.5 = (bf16[3,2,2,144,128]{4,3,2,1,0:T(8,128)(2,1)S(1)}, bf16[3,2,2,144,128]{4,3,2,1,0:T(8,128)(2,1)S(1)}, u32[]{:S(2)}, u32[]{:S(2)}) collective-permute-start(bf16[3,2,2,144,128]{4,3,2,1,0:T(8,128)(2,1)S(1)} %collective-permute-done.3), channel_id=1, source_target_pairs={{2,0},{4,2},{6,4},{7,6},{5,7},{3,5},{1,3},{0,1},{10,8},{12,10},{14... | collective-permute-start | bytes 1327112 | tf_op jit(solution)/shard_map/ppermute | solution.py:123
  39.0 5.5 %collective-permute-done.5 = bf16[3,2,2,144,128]{4,3,2,1,0:T(8,128)(2,1)S(1)} collective-permute-done((bf16[3,2,2,144,128]{4,3,2,1,0:T(8,128)(2,1)S(1)}, bf16[3,2,2,144,128]{4,3,2,1,0:T(8,128)(2,1)S(1)}, u32[]{:S(2)}, u32[]{:S(2)}) %collective-permute-start.5) | collective-permute-done | bytes 442400 | tf_op jit(solution)/shard_map/ppermute | solution.py:123
  44.6 1.6 %collective-permute-start.21 = (bf16[3,4,144,128]{3,2,1,0:T(8,128)(2,1)S(1)}, bf16[3,4,144,128]{3,2,1,0:T(8,128)(2,1)S(1)}, u32[]{:S(2)}, u32[]{:S(2)}) collective-permute-start(bf16[3,4,144,128]{3,2,1,0:T(8,128)(2,1)S(1)} %get-tuple-element.17), channel_id=1, source_target_pairs={{0,16},{1,17},{10,26},{11,27},{20,4},{21,5},{30,14},{31,15}} | collective-permute-start | bytes 1327112 | tf_op jit(solution)/shard_map/ppermute | solution.py:103
  47.6 2.0 %collective-permute-start.7 = (bf16[3,2,2,144,128]{4,3,2,1,0:T(8,128)(2,1)S(1)}, bf16[3,2,2,144,128]{4,3,2,1,0:T(8,128)(2,1)S(1)}, u32[]{:S(2)}, u32[]{:S(2)}) collective-permute-start(bf16[3,2,2,144,128]{4,3,2,1,0:T(8,128)(2,1)S(1)} %collective-permute-done.5), channel_id=1, source_target_pairs={{2,0},{4,2},{6,4},{7,6},{5,7},{3,5},{1,3},{0,1},{10,8},{12,10},{14... | collective-permute-start | bytes 1327112 | tf_op jit(solution)/shard_map/ppermute | solution.py:123
  51.5 8.4 %collective-permute-done.7 = bf16[3,2,2,144,128]{4,3,2,1,0:T(8,128)(2,1)S(1)} collective-permute-done((bf16[3,2,2,144,128]{4,3,2,1,0:T(8,128)(2,1)S(1)}, bf16[3,2,2,144,128]{4,3,2,1,0:T(8,128)(2,1)S(1)}, u32[]{:S(2)}, u32[]{:S(2)}) %collective-permute-start.7) | collective-permute-done | bytes 442400 | tf_op jit(solution)/shard_map/ppermute | solution.py:123
  60.1 3.5 %collective-permute-start.23 = (bf16[3,4,144,128]{3,2,1,0:T(8,128)(2,1)S(1)}, bf16[3,4,144,128]{3,2,1,0:T(8,128)(2,1)S(1)}, u32[]{:S(2)}, u32[]{:S(2)}) collective-permute-start(bf16[3,4,144,128]{3,2,1,0:T(8,128)(2,1)S(1)} %get-tuple-element.15), channel_id=1, source_target_pairs={{0,16},{1,17},{10,26},{11,27},{20,4},{21,5},{30,14},{31,15}} | collective-permute-start | bytes 1327112 | tf_op jit(solution)/shard_map/ppermute | solution.py:103
  64.9 2.0 %collective-permute-start.9 = (bf16[3,2,2,144,128]{4,3,2,1,0:T(8,128)(2,1)S(1)}, bf16[3,2,2,144,128]{4,3,2,1,0:T(8,128)(2,1)S(1)}, u32[]{:S(2)}, u32[]{:S(2)}) collective-permute-start(bf16[3,2,2,144,128]{4,3,2,1,0:T(8,128)(2,1)S(1)} %collective-permute-done.7), channel_id=1, source_target_pairs={{2,0},{4,2},{6,4},{7,6},{5,7},{3,5},{1,3},{0,1},{10,8},{12,10},{14... | collective-permute-start | bytes 1327112 | tf_op jit(solution)/shard_map/ppermute | solution.py:123
  68.9 7.7 %collective-permute-done.9 = bf16[3,2,2,144,128]{4,3,2,1,0:T(8,128)(2,1)S(1)} collective-permute-done((bf16[3,2,2,144,128]{4,3,2,1,0:T(8,128)(2,1)S(1)}, bf16[3,2,2,144,128]{4,3,2,1,0:T(8,128)(2,1)S(1)}, u32[]{:S(2)}, u32[]{:S(2)}) %collective-permute-start.9) | collective-permute-done | bytes 442400 | tf_op jit(solution)/shard_map/ppermute | solution.py:123
  76.8 3.2 %collective-permute-start.25 = (bf16[3,4,144,128]{3,2,1,0:T(8,128)(2,1)S(1)}, bf16[3,4,144,128]{3,2,1,0:T(8,128)(2,1)S(1)}, u32[]{:S(2)}, u32[]{:S(2)}) collective-permute-start(bf16[3,4,144,128]{3,2,1,0:T(8,128)(2,1)S(1)} %get-tuple-element.13), channel_id=1, source_target_pairs={{0,16},{1,17},{10,26},{11,27},{20,4},{21,5},{30,14},{31,15}} | collective-permute-start | bytes 1327112 | tf_op jit(solution)/shard_map/ppermute | solution.py:103
  81.4 2.0 %collective-permute-start.11 = (bf16[3,2,2,144,128]{4,3,2,1,0:T(8,128)(2,1)S(1)}, bf16[3,2,2,144,128]{4,3,2,1,0:T(8,128)(2,1)S(1)}, u32[]{:S(2)}, u32[]{:S(2)}) collective-permute-start(bf16[3,2,2,144,128]{4,3,2,1,0:T(8,128)(2,1)S(1)} %collective-permute-done.9), channel_id=1, source_target_pairs={{2,0},{4,2},{6,4},{7,6},{5,7},{3,5},{1,3},{0,1},{10,8},{12,10},{14... | collective-permute-start | bytes 1327112 | tf_op jit(solution)/shard_map/ppermute | solution.py:123
  85.4 5.5 %collective-permute-done.10 = bf16[3,2,2,144,128]{4,3,2,1,0:T(8,128)(2,1)S(1)} collective-permute-done((bf16[3,2,2,144,128]{4,3,2,1,0:T(8,128)(2,1)S(1)}, bf16[3,2,2,144,128]{4,3,2,1,0:T(8,128)(2,1)S(1)}, u32[]{:S(2)}, u32[]{:S(2)}) %collective-permute-start.10) | collective-permute-done | bytes 442400 | tf_op jit(solution)/shard_map/ppermute | solution.py:122
  90.9 2.5 %collective-permute-start.12 = (bf16[3,2,2,144,128]{4,3,2,1,0:T(8,128)(2,1)S(1)}, bf16[3,2,2,144,128]{4,3,2,1,0:T(8,128)(2,1)S(1)}, u32[]{:S(2)}, u32[]{:S(2)}) collective-permute-start(bf16[3,2,2,144,128]{4,3,2,1,0:T(8,128)(2,1)S(1)} %collective-permute-done.10), channel_id=1, source_target_pairs={{0,2},{2,4},{4,6},{6,7},{7,5},{5,3},{3,1},{1,0},{8,10},{10,12},{12... | collective-permute-start | bytes 1327112 | tf_op jit(solution)/shard_map/ppermute | solution.py:122
  94.5 2.5 %collective-permute-start.27 = (bf16[3,4,144,128]{3,2,1,0:T(8,128)(2,1)S(1)}, bf16[3,4,144,128]{3,2,1,0:T(8,128)(2,1)S(1)}, u32[]{:S(2)}, u32[]{:S(2)}) collective-permute-start(bf16[3,4,144,128]{3,2,1,0:T(8,128)(2,1)S(1)} %get-tuple-element.11), channel_id=1, source_target_pairs={{0,16},{1,17},{10,26},{11,27},{20,4},{21,5},{30,14},{31,15}} | collective-permute-start | bytes 1327112 | tf_op jit(solution)/shard_map/ppermute | solution.py:103
  97.1 2.1 %collective-permute-start.26 = (bf16[3,4,144,128]{3,2,1,0:T(8,128)(2,1)}, bf16[3,4,144,128]{3,2,1,0:T(8,128)(2,1)}, u32[]{:S(2)}, u32[]{:S(2)}) collective-permute-start(bf16[3,4,144,128]{3,2,1,0:T(8,128)(2,1)} %get-tuple-element.12), channel_id=1, source_target_pairs={{0,8},{16,24},{1,9},{17,25},{10,2},{26,18},{11,3},{27,19},{20,28},... | collective-permute-start | bytes 1327112 | tf_op jit(solution)/shard_map/ppermute | solution.py:103
  99.4 4.7 %collective-permute-done.13 = bf16[3,2,2,144,128]{4,3,2,1,0:T(8,128)(2,1)S(1)} collective-permute-done((bf16[3,2,2,144,128]{4,3,2,1,0:T(8,128)(2,1)S(1)}, bf16[3,2,2,144,128]{4,3,2,1,0:T(8,128)(2,1)S(1)}, u32[]{:S(2)}, u32[]{:S(2)}) %collective-permute-start.13) | collective-permute-done | bytes 442400 | tf_op jit(solution)/shard_map/ppermute | solution.py:123
  105.4 4.2 %collective-permute-start.29 = (bf16[3,4,144,128]{3,2,1,0:T(8,128)(2,1)}, bf16[3,4,144,128]{3,2,1,0:T(8,128)(2,1)}, u32[]{:S(2)}, u32[]{:S(2)}) collective-permute-start(bf16[3,4,144,128]{3,2,1,0:T(8,128)(2,1)} %get-tuple-element.9), channel_id=1, source_target_pairs={{0,16},{1,17},{10,26},{11,27},{20,4},{21,5},{30,14},{31,15}} | collective-permute-start | bytes 1327112 | tf_op jit(solution)/shard_map/ppermute | solution.py:103
  111.3 2.1 %collective-permute-start.28 = (bf16[3,4,144,128]{3,2,1,0:T(8,128)(2,1)}, bf16[3,4,144,128]{3,2,1,0:T(8,128)(2,1)}, u32[]{:S(2)}, u32[]{:S(2)}) collective-permute-start(bf16[3,4,144,128]{3,2,1,0:T(8,128)(2,1)} %get-tuple-element.10), channel_id=1, source_target_pairs={{0,8},{16,24},{1,9},{17,25},{10,2},{26,18},{11,3},{27,19},{20,28},... | collective-permute-start | bytes 1327112 | tf_op jit(solution)/shard_map/ppermute | solution.py:103
  115.1 1.7 %slice.19 = bf16[96,2,1,1]{3,2,1,0:T(2,128)(2,1)} slice(bf16[96,2,144,128]{3,2,1,0:T(8,128)(2,1)} %bitcast.44), slice={[0:96], [0:2], [131:132], [0:1]} | slice | bytes 768 | tf_op jit(solution)/shard_map/slice | solution.py:150
  119.2 1.5 %select_dynamic-update-slice_fusion.2 = bf16[3,32,144,128]{3,2,1,0:T(8,128)(2,1)S(1)} fusion(bf16[3,32,144,128]{3,2,1,0:T(8,128)(2,1)S(1)} %select_dynamic-update-slice_fusion.3, bf16[3,4,144,128]{3,2,1,0:T(8,128)(2,1)} %copy-done.13, bf16[3,4,144,128]{3,2,1,0:T(8,128)(2,1)} %copy-done.11, bf16[3,4,144,128]{3,2,1,0:T(8,128)(2,1)} %collective-permute-done.26, ...), kind=kLoop, calls=%fused_computation.11 | loop fusion | flops 1548288 | bytes 2211843
  120.6 1.5 %select_dynamic-update-slice_fusion.1 = bf16[3,32,144,128]{3,2,1,0:T(8,128)(2,1)S(1)} fusion(bf16[3,32,144,128]{3,2,1,0:T(8,128)(2,1)S(1)} %select_dynamic-update-slice_fusion.2, bf16[3,4,144,128]{3,2,1,0:T(8,128)(2,1)} %collective-permute-done.26, bf16[3,4,144,128]{3,2,1,0:T(8,128)(2,1)} %copy-done.12, bf16[3,4,144,128]{3,2,1,0:T(8,128)(2,1)} %collective-permute-done.28, ...), kind=kLoop, calls=%fused_computation.10 | loop fusion | flops 1548288 | bytes 2211843
  122.1 1.3 select_dynamic-update-slice_fusion
  125.9 14.6 %shard_map.37 = f32[2048,1024]{1,0:T(8,128)} custom-call(s32[288]{0:T(512)S(1)} %min.12.offs_ref, bf16[96,2,144,128]{3,2,1,0:T(8,128)(2,1)} %bitcast.45, bf16[96,144,128]{2,1,0:T(8,128)(2,1)S(1)} %bitcast.43), custom_call_target="tpu_custom_call" | custom-call | flops 805306368 | bytes 17825792 | tf_op jit(solution)/shard_map/pallas_call | solution.py:46
  (123 shorter events, 29.3 us)
Async XLA Ops:
  4.2 13.2 %collective-permute-start = (bf16[3,2,2,144,128]{4,3,2,1,0:T(8,128)(2,1)S(1)}, bf16[3,2,2,144,128]{4,3,2,1,0:T(8,128)(2,1)S(1)}, u32[]{:S(2)}, u32[]{:S(2)}) collective-permute-start(bf16[3,2,2,144,128]{4,3,2,1,0:T(8,128)(2,1)S(1)} %get-tuple-element.5), channel_id=1, source_target_pairs={{0,2},{2,4},{4,6},{6,7},{7,5},{5,3},{3,1},{1,0},{8,10},{10,12},{12... | collective-permute-start | bytes 1327112 | tf_op jit(solution)/shard_map/ppermute | solution.py:122
  7.3 11.9 %collective-permute-start.1 = (bf16[3,2,2,144,128]{4,3,2,1,0:T(8,128)(2,1)S(1)}, bf16[3,2,2,144,128]{4,3,2,1,0:T(8,128)(2,1)S(1)}, u32[]{:S(2)}, u32[]{:S(2)}) collective-permute-start(bf16[3,2,2,144,128]{4,3,2,1,0:T(8,128)(2,1)S(1)} %get-tuple-element.6), channel_id=1, source_target_pairs={{2,0},{4,2},{6,4},{7,6},{5,7},{3,5},{1,3},{0,1},{10,8},{12,10},{14... | collective-permute-start | bytes 1327112 | tf_op jit(solution)/shard_map/ppermute | solution.py:123
  8.1 11.3 %collective-permute-start.15 = (bf16[3,4,144,128]{3,2,1,0:T(8,128)(2,1)S(1)}, bf16[3,4,144,128]{3,2,1,0:T(8,128)(2,1)S(1)}, u32[]{:S(2)}, u32[]{:S(2)}) collective-permute-start(bf16[3,4,144,128]{3,2,1,0:T(8,128)(2,1)S(1)} %pad_maximum_fusion), channel_id=1, source_target_pairs={{0,16},{1,17},{10,26},{11,27},{20,4},{21,5},{30,14},{31,15}} | collective-permute-start | bytes 1327112 | tf_op jit(solution)/shard_map/ppermute | solution.py:103
  12.0 25.3 %collective-permute-start.14 = (bf16[3,4,144,128]{3,2,1,0:T(8,128)(2,1)S(1)}, bf16[3,4,144,128]{3,2,1,0:T(8,128)(2,1)S(1)}, u32[]{:S(2)}, u32[]{:S(2)}) collective-permute-start(bf16[3,4,144,128]{3,2,1,0:T(8,128)(2,1)S(1)} %pad_maximum_fusion), channel_id=1, source_target_pairs={{0,8},{16,24},{1,9},{17,25},{10,2},{26,18},{11,3},{27,19},{20,28},... | collective-permute-start | bytes 1327112 | tf_op jit(solution)/shard_map/ppermute | solution.py:103
  17.4 12.6 %collective-permute-start.2 = (bf16[3,2,2,144,128]{4,3,2,1,0:T(8,128)(2,1)S(1)}, bf16[3,2,2,144,128]{4,3,2,1,0:T(8,128)(2,1)S(1)}, u32[]{:S(2)}, u32[]{:S(2)}) collective-permute-start(bf16[3,2,2,144,128]{4,3,2,1,0:T(8,128)(2,1)S(1)} %collective-permute-done), channel_id=1, source_target_pairs={{0,2},{2,4},{4,6},{6,7},{7,5},{5,3},{3,1},{1,0},{8,10},{10,12},{12... | collective-permute-start | bytes 1327112 | tf_op jit(solution)/shard_map/ppermute | solution.py:122
  19.2 10.8 %collective-permute-start.3 = (bf16[3,2,2,144,128]{4,3,2,1,0:T(8,128)(2,1)S(1)}, bf16[3,2,2,144,128]{4,3,2,1,0:T(8,128)(2,1)S(1)}, u32[]{:S(2)}, u32[]{:S(2)}) collective-permute-start(bf16[3,2,2,144,128]{4,3,2,1,0:T(8,128)(2,1)S(1)} %collective-permute-done.1), channel_id=1, source_target_pairs={{2,0},{4,2},{6,4},{7,6},{5,7},{3,5},{1,3},{0,1},{10,8},{12,10},{14... | collective-permute-start | bytes 1327112 | tf_op jit(solution)/shard_map/ppermute | solution.py:123
  19.6 10.4 %collective-permute-start.17 = (bf16[3,4,144,128]{3,2,1,0:T(8,128)(2,1)S(1)}, bf16[3,4,144,128]{3,2,1,0:T(8,128)(2,1)S(1)}, u32[]{:S(2)}, u32[]{:S(2)}) collective-permute-start(bf16[3,4,144,128]{3,2,1,0:T(8,128)(2,1)S(1)} %get-tuple-element.21), channel_id=1, source_target_pairs={{0,16},{1,17},{10,26},{11,27},{20,4},{21,5},{30,14},{31,15}} | collective-permute-start | bytes 1327112 | tf_op jit(solution)/shard_map/ppermute | solution.py:103
  23.2 15.4 %collective-permute-start.16 = (bf16[3,4,144,128]{3,2,1,0:T(8,128)(2,1)S(1)}, bf16[3,4,144,128]{3,2,1,0:T(8,128)(2,1)S(1)}, u32[]{:S(2)}, u32[]{:S(2)}) collective-permute-start(bf16[3,4,144,128]{3,2,1,0:T(8,128)(2,1)S(1)} %get-tuple-element.22), channel_id=1, source_target_pairs={{0,8},{16,24},{1,9},{17,25},{10,2},{26,18},{11,3},{27,19},{20,28},... | collective-permute-start | bytes 1327112 | tf_op jit(solution)/shard_map/ppermute | solution.py:103
  30.1 14.4 %collective-permute-start.19 = (bf16[3,4,144,128]{3,2,1,0:T(8,128)(2,1)S(1)}, bf16[3,4,144,128]{3,2,1,0:T(8,128)(2,1)S(1)}, u32[]{:S(2)}, u32[]{:S(2)}) collective-permute-start(bf16[3,4,144,128]{3,2,1,0:T(8,128)(2,1)S(1)} %get-tuple-element.19), channel_id=1, source_target_pairs={{0,16},{1,17},{10,26},{11,27},{20,4},{21,5},{30,14},{31,15}} | collective-permute-start | bytes 1327112 | tf_op jit(solution)/shard_map/ppermute | solution.py:103
  33.5 10.9 %collective-permute-start.4 = (bf16[3,2,2,144,128]{4,3,2,1,0:T(8,128)(2,1)S(1)}, bf16[3,2,2,144,128]{4,3,2,1,0:T(8,128)(2,1)S(1)}, u32[]{:S(2)}, u32[]{:S(2)}) collective-permute-start(bf16[3,2,2,144,128]{4,3,2,1,0:T(8,128)(2,1)S(1)} %collective-permute-done.2), channel_id=1, source_target_pairs={{0,2},{2,4},{4,6},{6,7},{7,5},{5,3},{3,1},{1,0},{8,10},{10,12},{12... | collective-permute-start | bytes 1327112 | tf_op jit(solution)/shard_map/ppermute | solution.py:122
  33.6 10.8 %collective-permute-start.5 = (bf16[3,2,2,144,128]{4,3,2,1,0:T(8,128)(2,1)S(1)}, bf16[3,2,2,144,128]{4,3,2,1,0:T(8,128)(2,1)S(1)}, u32[]{:S(2)}, u32[]{:S(2)}) collective-permute-start(bf16[3,2,2,144,128]{4,3,2,1,0:T(8,128)(2,1)S(1)} %collective-permute-done.3), channel_id=1, source_target_pairs={{2,0},{4,2},{6,4},{7,6},{5,7},{3,5},{1,3},{0,1},{10,8},{12,10},{14... | collective-permute-start | bytes 1327112 | tf_op jit(solution)/shard_map/ppermute | solution.py:123
  37.3 13.9 %collective-permute-start.18 = (bf16[3,4,144,128]{3,2,1,0:T(8,128)(2,1)S(1)}, bf16[3,4,144,128]{3,2,1,0:T(8,128)(2,1)S(1)}, u32[]{:S(2)}, u32[]{:S(2)}) collective-permute-start(bf16[3,4,144,128]{3,2,1,0:T(8,128)(2,1)S(1)} %get-tuple-element.20), channel_id=1, source_target_pairs={{0,8},{16,24},{1,9},{17,25},{10,2},{26,18},{11,3},{27,19},{20,28},... | collective-permute-start | bytes 1327112 | tf_op jit(solution)/shard_map/ppermute | solution.py:103
  44.6 15.4 %collective-permute-start.21 = (bf16[3,4,144,128]{3,2,1,0:T(8,128)(2,1)S(1)}, bf16[3,4,144,128]{3,2,1,0:T(8,128)(2,1)S(1)}, u32[]{:S(2)}, u32[]{:S(2)}) collective-permute-start(bf16[3,4,144,128]{3,2,1,0:T(8,128)(2,1)S(1)} %get-tuple-element.17), channel_id=1, source_target_pairs={{0,16},{1,17},{10,26},{11,27},{20,4},{21,5},{30,14},{31,15}} | collective-permute-start | bytes 1327112 | tf_op jit(solution)/shard_map/ppermute | solution.py:103
  46.2 22.5 %collective-permute-start.20 = (bf16[3,4,144,128]{3,2,1,0:T(8,128)(2,1)S(1)}, bf16[3,4,144,128]{3,2,1,0:T(8,128)(2,1)S(1)}, u32[]{:S(2)}, u32[]{:S(2)}) collective-permute-start(bf16[3,4,144,128]{3,2,1,0:T(8,128)(2,1)S(1)} %get-tuple-element.18), channel_id=1, source_target_pairs={{0,8},{16,24},{1,9},{17,25},{10,2},{26,18},{11,3},{27,19},{20,28},... | collective-permute-start | bytes 1327112 | tf_op jit(solution)/shard_map/ppermute | solution.py:103
  47.5 12.5 %collective-permute-start.6 = (bf16[3,2,2,144,128]{4,3,2,1,0:T(8,128)(2,1)S(1)}, bf16[3,2,2,144,128]{4,3,2,1,0:T(8,128)(2,1)S(1)}, u32[]{:S(2)}, u32[]{:S(2)}) collective-permute-start(bf16[3,2,2,144,128]{4,3,2,1,0:T(8,128)(2,1)S(1)} %collective-permute-done.4), channel_id=1, source_target_pairs={{0,2},{2,4},{4,6},{6,7},{7,5},{5,3},{3,1},{1,0},{8,10},{10,12},{12... | collective-permute-start | bytes 1327112 | tf_op jit(solution)/shard_map/ppermute | solution.py:122
  47.6 12.4 %collective-permute-start.7 = (bf16[3,2,2,144,128]{4,3,2,1,0:T(8,128)(2,1)S(1)}, bf16[3,2,2,144,128]{4,3,2,1,0:T(8,128)(2,1)S(1)}, u32[]{:S(2)}, u32[]{:S(2)}) collective-permute-start(bf16[3,2,2,144,128]{4,3,2,1,0:T(8,128)(2,1)S(1)} %collective-permute-done.5), channel_id=1, source_target_pairs={{2,0},{4,2},{6,4},{7,6},{5,7},{3,5},{1,3},{0,1},{10,8},{12,10},{14... | collective-permute-start | bytes 1327112 | tf_op jit(solution)/shard_map/ppermute | solution.py:123
  60.1 16.6 %collective-permute-start.23 = (bf16[3,4,144,128]{3,2,1,0:T(8,128)(2,1)S(1)}, bf16[3,4,144,128]{3,2,1,0:T(8,128)(2,1)S(1)}, u32[]{:S(2)}, u32[]{:S(2)}) collective-permute-start(bf16[3,4,144,128]{3,2,1,0:T(8,128)(2,1)S(1)} %get-tuple-element.15), channel_id=1, source_target_pairs={{0,16},{1,17},{10,26},{11,27},{20,4},{21,5},{30,14},{31,15}} | collective-permute-start | bytes 1327112 | tf_op jit(solution)/shard_map/ppermute | solution.py:103
  63.6 21.6 %collective-permute-start.22 = (bf16[3,4,144,128]{3,2,1,0:T(8,128)(2,1)S(1)}, bf16[3,4,144,128]{3,2,1,0:T(8,128)(2,1)S(1)}, u32[]{:S(2)}, u32[]{:S(2)}) collective-permute-start(bf16[3,4,144,128]{3,2,1,0:T(8,128)(2,1)S(1)} %get-tuple-element.16), channel_id=1, source_target_pairs={{0,8},{16,24},{1,9},{17,25},{10,2},{26,18},{11,3},{27,19},{20,28},... | collective-permute-start | bytes 1327112 | tf_op jit(solution)/shard_map/ppermute | solution.py:103
  64.9 11.8 %collective-permute-start.8 = (bf16[3,2,2,144,128]{4,3,2,1,0:T(8,128)(2,1)S(1)}, bf16[3,2,2,144,128]{4,3,2,1,0:T(8,128)(2,1)S(1)}, u32[]{:S(2)}, u32[]{:S(2)}) collective-permute-start(bf16[3,2,2,144,128]{4,3,2,1,0:T(8,128)(2,1)S(1)} %collective-permute-done.6), channel_id=1, source_target_pairs={{0,2},{2,4},{4,6},{6,7},{7,5},{5,3},{3,1},{1,0},{8,10},{10,12},{12... | collective-permute-start | bytes 1327112 | tf_op jit(solution)/shard_map/ppermute | solution.py:122
  64.9 11.7 %collective-permute-start.9 = (bf16[3,2,2,144,128]{4,3,2,1,0:T(8,128)(2,1)S(1)}, bf16[3,2,2,144,128]{4,3,2,1,0:T(8,128)(2,1)S(1)}, u32[]{:S(2)}, u32[]{:S(2)}) collective-permute-start(bf16[3,2,2,144,128]{4,3,2,1,0:T(8,128)(2,1)S(1)} %collective-permute-done.7), channel_id=1, source_target_pairs={{2,0},{4,2},{6,4},{7,6},{5,7},{3,5},{1,3},{0,1},{10,8},{12,10},{14... | collective-permute-start | bytes 1327112 | tf_op jit(solution)/shard_map/ppermute | solution.py:123
  76.6 33.9 %copy-start.4 = (bf16[3,2,144,128]{3,2,1,0:T(8,128)(2,1)}, bf16[3,2,144,128]{3,2,1,0:T(8,128)(2,1)S(1)}, u32[]{:S(2)}) copy-start(bf16[3,2,144,128]{3,2,1,0:T(8,128)(2,1)S(1)} %dynamic-slice_bitcast_fusion.4) | copy-start | bytes 663556
  76.8 16.7 %collective-permute-start.25 = (bf16[3,4,144,128]{3,2,1,0:T(8,128)(2,1)S(1)}, bf16[3,4,144,128]{3,2,1,0:T(8,128)(2,1)S(1)}, u32[]{:S(2)}, u32[]{:S(2)}) collective-permute-start(bf16[3,4,144,128]{3,2,1,0:T(8,128)(2,1)S(1)} %get-tuple-element.13), channel_id=1, source_target_pairs={{0,16},{1,17},{10,26},{11,27},{20,4},{21,5},{30,14},{31,15}} | collective-permute-start | bytes 1327112 | tf_op jit(solution)/shard_map/ppermute | solution.py:103
  80.0 19.1 %collective-permute-start.24 = (bf16[3,4,144,128]{3,2,1,0:T(8,128)(2,1)S(1)}, bf16[3,4,144,128]{3,2,1,0:T(8,128)(2,1)S(1)}, u32[]{:S(2)}, u32[]{:S(2)}) collective-permute-start(bf16[3,4,144,128]{3,2,1,0:T(8,128)(2,1)S(1)} %get-tuple-element.14), channel_id=1, source_target_pairs={{0,8},{16,24},{1,9},{17,25},{10,2},{26,18},{11,3},{27,19},{20,28},... | collective-permute-start | bytes 1327112 | tf_op jit(solution)/shard_map/ppermute | solution.py:103
  81.4 9.5 %collective-permute-start.10 = (bf16[3,2,2,144,128]{4,3,2,1,0:T(8,128)(2,1)S(1)}, bf16[3,2,2,144,128]{4,3,2,1,0:T(8,128)(2,1)S(1)}, u32[]{:S(2)}, u32[]{:S(2)}) collective-permute-start(bf16[3,2,2,144,128]{4,3,2,1,0:T(8,128)(2,1)S(1)} %collective-permute-done.8), channel_id=1, source_target_pairs={{0,2},{2,4},{4,6},{6,7},{7,5},{5,3},{3,1},{1,0},{8,10},{10,12},{12... | collective-permute-start | bytes 1327112 | tf_op jit(solution)/shard_map/ppermute | solution.py:122
  81.4 11.9 %collective-permute-start.11 = (bf16[3,2,2,144,128]{4,3,2,1,0:T(8,128)(2,1)S(1)}, bf16[3,2,2,144,128]{4,3,2,1,0:T(8,128)(2,1)S(1)}, u32[]{:S(2)}, u32[]{:S(2)}) collective-permute-start(bf16[3,2,2,144,128]{4,3,2,1,0:T(8,128)(2,1)S(1)} %collective-permute-done.9), channel_id=1, source_target_pairs={{2,0},{4,2},{6,4},{7,6},{5,7},{3,5},{1,3},{0,1},{10,8},{12,10},{14... | collective-permute-start | bytes 1327112 | tf_op jit(solution)/shard_map/ppermute | solution.py:123
  90.9 13.3 %collective-permute-start.12 = (bf16[3,2,2,144,128]{4,3,2,1,0:T(8,128)(2,1)S(1)}, bf16[3,2,2,144,128]{4,3,2,1,0:T(8,128)(2,1)S(1)}, u32[]{:S(2)}, u32[]{:S(2)}) collective-permute-start(bf16[3,2,2,144,128]{4,3,2,1,0:T(8,128)(2,1)S(1)} %collective-permute-done.10), channel_id=1, source_target_pairs={{0,2},{2,4},{4,6},{6,7},{7,5},{5,3},{3,1},{1,0},{8,10},{10,12},{12... | collective-permute-start | bytes 1327112 | tf_op jit(solution)/shard_map/ppermute | solution.py:122
  93.4 10.8 %collective-permute-start.13 = (bf16[3,2,2,144,128]{4,3,2,1,0:T(8,128)(2,1)S(1)}, bf16[3,2,2,144,128]{4,3,2,1,0:T(8,128)(2,1)S(1)}, u32[]{:S(2)}, u32[]{:S(2)}) collective-permute-start(bf16[3,2,2,144,128]{4,3,2,1,0:T(8,128)(2,1)S(1)} %collective-permute-done.11), channel_id=1, source_target_pairs={{2,0},{4,2},{6,4},{7,6},{5,7},{3,5},{1,3},{0,1},{10,8},{12,10},{14... | collective-permute-start | bytes 1327112 | tf_op jit(solution)/shard_map/ppermute | solution.py:123
  94.5 9.7 %collective-permute-start.27 = (bf16[3,4,144,128]{3,2,1,0:T(8,128)(2,1)S(1)}, bf16[3,4,144,128]{3,2,1,0:T(8,128)(2,1)S(1)}, u32[]{:S(2)}, u32[]{:S(2)}) collective-permute-start(bf16[3,4,144,128]{3,2,1,0:T(8,128)(2,1)S(1)} %get-tuple-element.11), channel_id=1, source_target_pairs={{0,16},{1,17},{10,26},{11,27},{20,4},{21,5},{30,14},{31,15}} | collective-permute-start | bytes 1327112 | tf_op jit(solution)/shard_map/ppermute | solution.py:103
  97.1 22.1 %collective-permute-start.26 = (bf16[3,4,144,128]{3,2,1,0:T(8,128)(2,1)}, bf16[3,4,144,128]{3,2,1,0:T(8,128)(2,1)}, u32[]{:S(2)}, u32[]{:S(2)}) collective-permute-start(bf16[3,4,144,128]{3,2,1,0:T(8,128)(2,1)} %get-tuple-element.12), channel_id=1, source_target_pairs={{0,8},{16,24},{1,9},{17,25},{10,2},{26,18},{11,3},{27,19},{20,28},... | collective-permute-start | bytes 1327112 | tf_op jit(solution)/shard_map/ppermute | solution.py:103
  105.4 12.4 %collective-permute-start.29 = (bf16[3,4,144,128]{3,2,1,0:T(8,128)(2,1)}, bf16[3,4,144,128]{3,2,1,0:T(8,128)(2,1)}, u32[]{:S(2)}, u32[]{:S(2)}) collective-permute-start(bf16[3,4,144,128]{3,2,1,0:T(8,128)(2,1)} %get-tuple-element.9), channel_id=1, source_target_pairs={{0,16},{1,17},{10,26},{11,27},{20,4},{21,5},{30,14},{31,15}} | collective-permute-start | bytes 1327112 | tf_op jit(solution)/shard_map/ppermute | solution.py:103
  111.3 9.3 %collective-permute-start.28 = (bf16[3,4,144,128]{3,2,1,0:T(8,128)(2,1)}, bf16[3,4,144,128]{3,2,1,0:T(8,128)(2,1)}, u32[]{:S(2)}, u32[]{:S(2)}) collective-permute-start(bf16[3,4,144,128]{3,2,1,0:T(8,128)(2,1)} %get-tuple-element.10), channel_id=1, source_target_pairs={{0,8},{16,24},{1,9},{17,25},{10,2},{26,18},{11,3},{27,19},{20,28},... | collective-permute-start | bytes 1327112 | tf_op jit(solution)/shard_map/ppermute | solution.py:103
  117.8 4.3 %collective-permute-start.30 = (bf16[3,4,144,128]{3,2,1,0:T(8,128)(2,1)}, bf16[3,4,144,128]{3,2,1,0:T(8,128)(2,1)S(1)}, u32[]{:S(2)}, u32[]{:S(2)}) collective-permute-start(bf16[3,4,144,128]{3,2,1,0:T(8,128)(2,1)} %collective-permute-done.29), channel_id=1, source_target_pairs={{0,8},{16,24},{1,9},{17,25},{10,2},{26,18},{11,3},{27,19},{20,28},... | collective-permute-start | bytes 1327112 | tf_op jit(solution)/shard_map/ppermute | solution.py:103
  (14 other events, 209.8 us)

commit v10 on v6

--- a/solution.py
+++ b/solution.py
@@ -106,19 +106,23 @@
     def pick_slot(piece):
         return lax.dynamic_index_in_dim(piece, slot, axis=2, keepdims=False)
 
+    batches = [[k, k + 1] for k in range(0, ncol - 2, 2)] + [[ncol - 2], [ncol - 1]]
     half = x.shape[1] // 2
     a, b = x[:, :half], x[:, half:]
-    pieces, columns = [], []
+    pieces, columns, pending = [], [], []
     for step in range(ncol):
         if step:
             a = lax.ppermute(a, "col", forward)
             b = lax.ppermute(b, "col", backward)
         pieces += [a, b]
-        own = jnp.concatenate([pick_slot(a), pick_slot(b)], axis=1)
-        got = own
-        for j, fan in enumerate(fans, start=1):
-            got = jnp.where(which == j, lax.ppermute(own, ("row", "col"), fan), got)
-        columns.append(got)
+        pending += [pick_slot(a), pick_slot(b)]
+        if any(batch[-1] == step for batch in batches):
+            own = jnp.concatenate(pending, axis=1)
+            pending = []
+            got = own
+            for j, fan in enumerate(fans, start=1):
+                got = jnp.where(which == j, lax.ppermute(own, ("row", "col"), fan), got)
+            columns.append(got)
 
     blocks = jnp.concatenate(pieces, axis=1)
     column_blocks = jnp.concatenate(columns, axis=1)

time: 136 us -> 135 us (level)
  the two profiles are of different devices: /device:TPU:14 before, /device:TPU:0 now
where the time goes in v10:
time: 135 us; the launch traced here: 133 us
  waiting for transfers between devices  47 us (35%)
  starting transfers between devices  43.6 us (32%)
  local copies, waits for them, and re-layouts  17.8 us (13%)
  Pallas kernels  14.6 us (11%)
  other arithmetic  10 us (7%)
    ppermute x7, waiting for transfers between devices, local(): a = lax.ppermute(a, 'col', forward)  31.5 us
    ppermute x15, starting transfers between devices, local(): got = jnp.where(which == j, lax.ppermute(own, ('row', 'col'), fan), got)  30.5 us
    pallas_call x1, Pallas kernels, gram_call(): pl.pallas_call(kernel, grid_spec=pltpu.PrefetchScalarGridSpec(num_scalar_...  14.6 us
    ppermute x7, starting transfers between devices, local(): a = lax.ppermute(a, 'col', forward)  11.9 us
    ppermute x7, waiting for transfers between devices, local(): b = lax.ppermute(b, 'col', backward)  11.5 us
    unnamed x23, local copies, waits for them, and re-layouts  11.1 us
    unnamed x5, other arithmetic  5.26 us
    ppermute x15, waiting for transfers between devices, local(): got = jnp.where(which == j, lax.ppermute(own, ('row', 'col'), fan), got)  4.03 us
  transfers between devices with their start and end apart: 29, of which 11 were waited for; matrix products, arithmetic and copies ran while one was open for 15% of the time, Pallas kernels for 0%

profile of v10, /device:TPU:0, one launch (start us, length us, event | category | flops | bytes accessed | tf_op | source)
XLA Modules:
  0.0 133.4 jit_solution(14446981122816938411)
XLA Ops:
  1.7 2.4 %constant_dynamic-update-slice_fusion.14 = (bf16[3,32,2,144,128]{4,3,2,1,0:T(8,128)(2,1)}, bf16[3,4,2,144,128]{4,3,2,1,0:T(8,128)(2,1)S(1)}) fusion(bf16[144]{0:T(256)(128)(2,1)S(1)} %pad.21.clone, bf16[3,4,2,1,128]{4,3,2,1,0:T(2,128)(2,1)S(1)} %broadcast_in_dim.7, bf16[3,4,2,3,128]{4,3,2,1,0:T(4,128)(2,1)S(1)} %broadcast_in_dim.6, ...), kind=kLoop, calls=%fused_computation.42 | loop fusion | flops 3538943 | bytes 2580768
  4.2 3.1 %collective-permute-start = (bf16[3,2,2,144,128]{4,3,2,1,0:T(8,128)(2,1)S(1)}, bf16[3,2,2,144,128]{4,3,2,1,0:T(8,128)(2,1)S(1)}, u32[]{:S(2)}, u32[]{:S(2)}) collective-permute-start(bf16[3,2,2,144,128]{4,3,2,1,0:T(8,128)(2,1)S(1)} %get-tuple-element.5), channel_id=1, source_target_pairs={{0,2},{2,4},{4,6},{6,7},{7,5},{5,3},{3,1},{1,0},{8,10},{10,12},{12... | collective-permute-start | bytes 1327112 | tf_op jit(solution)/shard_map/ppermute | solution.py:115
  7.3 10.1 %collective-permute-done = bf16[3,2,2,144,128]{4,3,2,1,0:T(8,128)(2,1)S(1)} collective-permute-done((bf16[3,2,2,144,128]{4,3,2,1,0:T(8,128)(2,1)S(1)}, bf16[3,2,2,144,128]{4,3,2,1,0:T(8,128)(2,1)S(1)}, u32[]{:S(2)}, u32[]{:S(2)}) %collective-permute-start) | collective-permute-done | bytes 442400 | tf_op jit(solution)/shard_map/ppermute | solution.py:115
  17.4 1.8 %collective-permute-start.2 = (bf16[3,2,2,144,128]{4,3,2,1,0:T(8,128)(2,1)S(1)}, bf16[3,2,2,144,128]{4,3,2,1,0:T(8,128)(2,1)S(1)}, u32[]{:S(2)}, u32[]{:S(2)}) collective-permute-start(bf16[3,2,2,144,128]{4,3,2,1,0:T(8,128)(2,1)S(1)} %collective-permute-done), channel_id=1, source_target_pairs={{0,2},{2,4},{4,6},{6,7},{7,5},{5,3},{3,1},{1,0},{8,10},{10,12},{12... | collective-permute-start | bytes 1327112 | tf_op jit(solution)/shard_map/ppermute | solution.py:115
  19.6 1.3 %collective-permute-start.16 = (bf16[3,8,144,128]{3,2,1,0:T(8,128)(2,1)S(1)}, bf16[3,8,144,128]{3,2,1,0:T(8,128)(2,1)S(1)}, u32[]{:S(2)}, u32[]{:S(2)}) collective-permute-start(bf16[3,8,144,128]{3,2,1,0:T(8,128)(2,1)S(1)} %pad_maximum_fusion), channel_id=1, source_target_pairs={{0,8},{1,9},{10,18},{11,19},{20,28},{21,29},{30,6},{31,7}} | collective-permute-start | bytes 2654216 | tf_op jit(solution)/shard_map/ppermute | solution.py:124
  21.0 3.0 %collective-permute-start.15 = (bf16[3,8,144,128]{3,2,1,0:T(8,128)(2,1)S(1)}, bf16[3,8,144,128]{3,2,1,0:T(8,128)(2,1)S(1)}, u32[]{:S(2)}, u32[]{:S(2)}) collective-permute-start(bf16[3,8,144,128]{3,2,1,0:T(8,128)(2,1)S(1)} %pad_maximum_fusion), channel_id=1, source_target_pairs={{0,16},{1,17},{10,26},{11,27},{20,4},{21,5},{30,14},{31,15}} | collective-permute-start | bytes 2654216 | tf_op jit(solution)/shard_map/ppermute | solution.py:124
  24.0 1.3 %collective-permute-start.14 = (bf16[3,8,144,128]{3,2,1,0:T(8,128)(2,1)S(1)}, bf16[3,8,144,128]{3,2,1,0:T(8,128)(2,1)S(1)}, u32[]{:S(2)}, u32[]{:S(2)}) collective-permute-start(bf16[3,8,144,128]{3,2,1,0:T(8,128)(2,1)S(1)} %pad_maximum_fusion), channel_id=1, source_target_pairs={{0,24},{1,25},{10,2},{11,3},{20,12},{21,13},{30,22},{31,23}} | collective-permute-start | bytes 2654216 | tf_op jit(solution)/shard_map/ppermute | solution.py:124
  27.1 1.6 %collective-permute-done.2 = bf16[3,2,2,144,128]{4,3,2,1,0:T(8,128)(2,1)S(1)} collective-permute-done((bf16[3,2,2,144,128]{4,3,2,1,0:T(8,128)(2,1)S(1)}, bf16[3,2,2,144,128]{4,3,2,1,0:T(8,128)(2,1)S(1)}, u32[]{:S(2)}, u32[]{:S(2)}) %collective-permute-start.2) | collective-permute-done | bytes 442400 | tf_op jit(solution)/shard_map/ppermute | solution.py:115
  28.8 1.5 %collective-permute-start.4 = (bf16[3,2,2,144,128]{4,3,2,1,0:T(8,128)(2,1)S(1)}, bf16[3,2,2,144,128]{4,3,2,1,0:T(8,128)(2,1)S(1)}, u32[]{:S(2)}, u32[]{:S(2)}) collective-permute-start(bf16[3,2,2,144,128]{4,3,2,1,0:T(8,128)(2,1)S(1)} %collective-permute-done.2), channel_id=1, source_target_pairs={{0,2},{2,4},{4,6},{6,7},{7,5},{5,3},{3,1},{1,0},{8,10},{10,12},{12... | collective-permute-start | bytes 1327112 | tf_op jit(solution)/shard_map/ppermute | solution.py:115
  32.5 6.6 %collective-permute-done.4 = bf16[3,2,2,144,128]{4,3,2,1,0:T(8,128)(2,1)S(1)} collective-permute-done((bf16[3,2,2,144,128]{4,3,2,1,0:T(8,128)(2,1)S(1)}, bf16[3,2,2,144,128]{4,3,2,1,0:T(8,128)(2,1)S(1)}, u32[]{:S(2)}, u32[]{:S(2)}) %collective-permute-start.4) | collective-permute-done | bytes 442400 | tf_op jit(solution)/shard_map/ppermute | solution.py:115
  39.2 2.3 %collective-permute-start.6 = (bf16[3,2,2,144,128]{4,3,2,1,0:T(8,128)(2,1)S(1)}, bf16[3,2,2,144,128]{4,3,2,1,0:T(8,128)(2,1)S(1)}, u32[]{:S(2)}, u32[]{:S(2)}) collective-permute-start(bf16[3,2,2,144,128]{4,3,2,1,0:T(8,128)(2,1)S(1)} %collective-permute-done.4), channel_id=1, source_target_pairs={{0,2},{2,4},{4,6},{6,7},{7,5},{5,3},{3,1},{1,0},{8,10},{10,12},{12... | collective-permute-start | bytes 1327112 | tf_op jit(solution)/shard_map/ppermute | solution.py:115
  44.7 2.3 %collective-permute-start.18 = (bf16[3,8,144,128]{3,2,1,0:T(8,128)(2,1)S(1)}, bf16[3,8,144,128]{3,2,1,0:T(8,128)(2,1)S(1)}, u32[]{:S(2)}, u32[]{:S(2)}) collective-permute-start(bf16[3,8,144,128]{3,2,1,0:T(8,128)(2,1)S(1)} %pad_maximum_fusion.1), channel_id=1, source_target_pairs={{0,16},{1,17},{10,26},{11,27},{20,4},{21,5},{30,14},{31,15}} | collective-permute-start | bytes 2654216 | tf_op jit(solution)/shard_map/ppermute | solution.py:124
  47.1 1.3 %collective-permute-start.17 = (bf16[3,8,144,128]{3,2,1,0:T(8,128)(2,1)S(1)}, bf16[3,8,144,128]{3,2,1,0:T(8,128)(2,1)S(1)}, u32[]{:S(2)}, u32[]{:S(2)}) collective-permute-start(bf16[3,8,144,128]{3,2,1,0:T(8,128)(2,1)S(1)} %pad_maximum_fusion.1), channel_id=1, source_target_pairs={{0,24},{1,25},{10,2},{11,3},{20,12},{21,13},{30,22},{31,23}} | collective-permute-start | bytes 2654216 | tf_op jit(solution)/shard_map/ppermute | solution.py:124
  49.7 2.1 %collective-permute-start.8 = (bf16[3,2,2,144,128]{4,3,2,1,0:T(8,128)(2,1)S(1)}, bf16[3,2,2,144,128]{4,3,2,1,0:T(8,128)(2,1)S(1)}, u32[]{:S(2)}, u32[]{:S(2)}) collective-permute-start(bf16[3,2,2,144,128]{4,3,2,1,0:T(8,128)(2,1)S(1)} %collective-permute-done.6), channel_id=1, source_target_pairs={{0,2},{2,4},{4,6},{6,7},{7,5},{5,3},{3,1},{1,0},{8,10},{10,12},{12... | collective-permute-start | bytes 1327112 | tf_op jit(solution)/shard_map/ppermute | solution.py:115
  53.6 7.3 %collective-permute-done.8 = bf16[3,2,2,144,128]{4,3,2,1,0:T(8,128)(2,1)S(1)} collective-permute-done((bf16[3,2,2,144,128]{4,3,2,1,0:T(8,128)(2,1)S(1)}, bf16[3,2,2,144,128]{4,3,2,1,0:T(8,128)(2,1)S(1)}, u32[]{:S(2)}, u32[]{:S(2)}) %collective-permute-start.8) | collective-permute-done | bytes 442400 | tf_op jit(solution)/shard_map/ppermute | solution.py:115
  60.9 2.2 %collective-permute-done.9 = bf16[3,2,2,144,128]{4,3,2,1,0:T(8,128)(2,1)S(1)} collective-permute-done((bf16[3,2,2,144,128]{4,3,2,1,0:T(8,128)(2,1)S(1)}, bf16[3,2,2,144,128]{4,3,2,1,0:T(8,128)(2,1)S(1)}, u32[]{:S(2)}, u32[]{:S(2)}) %collective-permute-start.9) | collective-permute-done | bytes 442400 | tf_op jit(solution)/shard_map/ppermute | solution.py:116
  63.2 1.3 %collective-permute-start.22 = (bf16[3,8,144,128]{3,2,1,0:T(8,128)(2,1)S(1)}, bf16[3,8,144,128]{3,2,1,0:T(8,128)(2,1)S(1)}, u32[]{:S(2)}, u32[]{:S(2)}) collective-permute-start(bf16[3,8,144,128]{3,2,1,0:T(8,128)(2,1)S(1)} %pad_maximum_fusion.2), channel_id=1, source_target_pairs={{0,8},{1,9},{10,18},{11,19},{20,28},{21,29},{30,6},{31,7}} | collective-permute-start | bytes 2654216 | tf_op jit(solution)/shard_map/ppermute | solution.py:124
  66.4 3.8 %collective-permute-start.21 = (bf16[3,8,144,128]{3,2,1,0:T(8,128)(2,1)S(1)}, bf16[3,8,144,128]{3,2,1,0:T(8,128)(2,1)S(1)}, u32[]{:S(2)}, u32[]{:S(2)}) collective-permute-start(bf16[3,8,144,128]{3,2,1,0:T(8,128)(2,1)S(1)} %pad_maximum_fusion.2), channel_id=1, source_target_pairs={{0,16},{1,17},{10,26},{11,27},{20,4},{21,5},{30,14},{31,15}} | collective-permute-start | bytes 2654216 | tf_op jit(solution)/shard_map/ppermute | solution.py:124
  70.2 1.3 %collective-permute-start.20 = (bf16[3,8,144,128]{3,2,1,0:T(8,128)(2,1)S(1)}, bf16[3,8,144,128]{3,2,1,0:T(8,128)(2,1)S(1)}, u32[]{:S(2)}, u32[]{:S(2)}) collective-permute-start(bf16[3,8,144,128]{3,2,1,0:T(8,128)(2,1)S(1)} %pad_maximum_fusion.2), channel_id=1, source_target_pairs={{0,24},{1,25},{10,2},{11,3},{20,12},{21,13},{30,22},{31,23}} | collective-permute-start | bytes 2654216 | tf_op jit(solution)/shard_map/ppermute | solution.py:124
  72.2 2.8 %collective-permute-done.10 = bf16[3,2,2,144,128]{4,3,2,1,0:T(8,128)(2,1)S(1)} collective-permute-done((bf16[3,2,2,144,128]{4,3,2,1,0:T(8,128)(2,1)S(1)}, bf16[3,2,2,144,128]{4,3,2,1,0:T(8,128)(2,1)S(1)}, u32[]{:S(2)}, u32[]{:S(2)}) %collective-permute-start.10) | collective-permute-done | bytes 442400 | tf_op jit(solution)/shard_map/ppermute | solution.py:115
  76.0 6.3 %collective-permute-done.11 = bf16[3,2,2,144,128]{4,3,2,1,0:T(8,128)(2,1)S(1)} collective-permute-done((bf16[3,2,2,144,128]{4,3,2,1,0:T(8,128)(2,1)S(1)}, bf16[3,2,2,144,128]{4,3,2,1,0:T(8,128)(2,1)S(1)}, u32[]{:S(2)}, u32[]{:S(2)}) %collective-permute-start.11) | collective-permute-done | bytes 442400 | tf_op jit(solution)/shard_map/ppermute | solution.py:116
  85.2 2.3 %collective-permute-done.12 = bf16[3,2,2,144,128]{4,3,2,1,0:T(8,128)(2,1)S(1)} collective-permute-done((bf16[3,2,2,144,128]{4,3,2,1,0:T(8,128)(2,1)S(1)}, bf16[3,2,2,144,128]{4,3,2,1,0:T(8,128)(2,1)S(1)}, u32[]{:S(2)}, u32[]{:S(2)}) %collective-permute-start.12) | collective-permute-done | bytes 442400 | tf_op jit(solution)/shard_map/ppermute | solution.py:115
  87.5 1.6 %collective-permute-start.25 = (bf16[3,4,144,128]{3,2,1,0:T(8,128)(2,1)}, bf16[3,4,144,128]{3,2,1,0:T(8,128)(2,1)S(1)}, u32[]{:S(2)}, u32[]{:S(2)}) collective-permute-start(bf16[3,4,144,128]{3,2,1,0:T(8,128)(2,1)} %pad_maximum_fusion.3), channel_id=1, source_target_pairs={{0,8},{1,9},{10,18},{11,19},{20,28},{21,29},{30,6},{31,7}} | collective-permute-start | bytes 1327112 | tf_op jit(solution)/shard_map/ppermute | solution.py:124
  89.1 3.0 %collective-permute-done.13 = bf16[3,2,2,144,128]{4,3,2,1,0:T(8,128)(2,1)S(1)} collective-permute-done((bf16[3,2,2,144,128]{4,3,2,1,0:T(8,128)(2,1)S(1)}, bf16[3,2,2,144,128]{4,3,2,1,0:T(8,128)(2,1)S(1)}, u32[]{:S(2)}, u32[]{:S(2)}) %collective-permute-start.13) | collective-permute-done | bytes 442400 | tf_op jit(solution)/shard_map/ppermute | solution.py:116
  92.1 3.4 %collective-permute-start.24 = (bf16[3,4,144,128]{3,2,1,0:T(8,128)(2,1)}, bf16[3,4,144,128]{3,2,1,0:T(8,128)(2,1)}, u32[]{:S(2)}, u32[]{:S(2)}) collective-permute-start(bf16[3,4,144,128]{3,2,1,0:T(8,128)(2,1)} %pad_maximum_fusion.3), channel_id=1, source_target_pairs={{0,16},{1,17},{10,26},{11,27},{20,4},{21,5},{30,14},{31,15}} | collective-permute-start | bytes 1327112 | tf_op jit(solution)/shard_map/ppermute | solution.py:124
  96.4 2.1 %collective-permute-start.23 = (bf16[3,4,144,128]{3,2,1,0:T(8,128)(2,1)}, bf16[3,4,144,128]{3,2,1,0:T(8,128)(2,1)}, u32[]{:S(2)}, u32[]{:S(2)}) collective-permute-start(bf16[3,4,144,128]{3,2,1,0:T(8,128)(2,1)} %pad_maximum_fusion.3), channel_id=1, source_target_pairs={{0,24},{1,25},{10,2},{11,3},{20,12},{21,13},{30,22},{31,23}} | collective-permute-start | bytes 1327112 | tf_op jit(solution)/shard_map/ppermute | solution.py:124
  98.4 2.1 %collective-permute-start.28 = (bf16[3,4,144,128]{3,2,1,0:T(8,128)(2,1)}, bf16[3,4,144,128]{3,2,1,0:T(8,128)(2,1)}, u32[]{:S(2)}, u32[]{:S(2)}) collective-permute-start(bf16[3,4,144,128]{3,2,1,0:T(8,128)(2,1)} %pad_maximum_fusion.4), channel_id=1, source_target_pairs={{0,8},{1,9},{10,18},{11,19},{20,28},{21,29},{30,6},{31,7}} | collective-permute-start | bytes 1327112 | tf_op jit(solution)/shard_map/ppermute | solution.py:124
  100.5 2.1 %collective-permute-start.27 = (bf16[3,4,144,128]{3,2,1,0:T(8,128)(2,1)}, bf16[3,4,144,128]{3,2,1,0:T(8,128)(2,1)}, u32[]{:S(2)}, u32[]{:S(2)}) collective-permute-start(bf16[3,4,144,128]{3,2,1,0:T(8,128)(2,1)} %pad_maximum_fusion.4), channel_id=1, source_target_pairs={{0,16},{1,17},{10,26},{11,27},{20,4},{21,5},{30,14},{31,15}} | collective-permute-start | bytes 1327112 | tf_op jit(solution)/shard_map/ppermute | solution.py:124
  103.1 2.1 %collective-permute-start.26 = (bf16[3,4,144,128]{3,2,1,0:T(8,128)(2,1)}, bf16[3,4,144,128]{3,2,1,0:T(8,128)(2,1)}, u32[]{:S(2)}, u32[]{:S(2)}) collective-permute-start(bf16[3,4,144,128]{3,2,1,0:T(8,128)(2,1)} %pad_maximum_fusion.4), channel_id=1, source_target_pairs={{0,24},{1,25},{10,2},{11,3},{20,12},{21,13},{30,22},{31,23}} | collective-permute-start | bytes 1327112 | tf_op jit(solution)/shard_map/ppermute | solution.py:124
  107.0 1.7 %slice.19 = bf16[96,2,1,1]{3,2,1,0:T(2,128)(2,1)} slice(bf16[96,2,144,128]{3,2,1,0:T(8,128)(2,1)} %bitcast.44), slice={[0:96], [0:2], [131:132], [0:1]} | slice | bytes 768 | tf_op jit(solution)/shard_map/slice | solution.py:133
  111.0 4.0 %collective-permute-done.26 = bf16[3,4,144,128]{3,2,1,0:T(8,128)(2,1)} collective-permute-done((bf16[3,4,144,128]{3,2,1,0:T(8,128)(2,1)}, bf16[3,4,144,128]{3,2,1,0:T(8,128)(2,1)}, u32[]{:S(2)}, u32[]{:S(2)}) %collective-permute-start.26) | collective-permute-done | bytes 442400 | tf_op jit(solution)/shard_map/ppermute | solution.py:124
  118.8 14.6 %shard_map.37 = f32[2048,1024]{1,0:T(8,128)} custom-call(s32[288]{0:T(512)S(1)} %min.12.offs_ref, bf16[96,2,144,128]{3,2,1,0:T(8,128)(2,1)} %bitcast.45, bf16[96,144,128]{2,1,0:T(8,128)(2,1)S(1)} %bitcast.43), custom_call_target="tpu_custom_call" | custom-call | flops 805306368 | bytes 17825792 | tf_op jit(solution)/shard_map/pallas_call | solution.py:46
  (93 shorter events, 28.1 us)
Async XLA Ops:
  4.2 13.2 %collective-permute-start = (bf16[3,2,2,144,128]{4,3,2,1,0:T(8,128)(2,1)S(1)}, bf16[3,2,2,144,128]{4,3,2,1,0:T(8,128)(2,1)S(1)}, u32[]{:S(2)}, u32[]{:S(2)}) collective-permute-start(bf16[3,2,2,144,128]{4,3,2,1,0:T(8,128)(2,1)S(1)} %get-tuple-element.5), channel_id=1, source_target_pairs={{0,2},{2,4},{4,6},{6,7},{7,5},{5,3},{3,1},{1,0},{8,10},{10,12},{12... | collective-permute-start | bytes 1327112 | tf_op jit(solution)/shard_map/ppermute | solution.py:115
  7.3 11.9 %collective-permute-start.1 = (bf16[3,2,2,144,128]{4,3,2,1,0:T(8,128)(2,1)S(1)}, bf16[3,2,2,144,128]{4,3,2,1,0:T(8,128)(2,1)S(1)}, u32[]{:S(2)}, u32[]{:S(2)}) collective-permute-start(bf16[3,2,2,144,128]{4,3,2,1,0:T(8,128)(2,1)S(1)} %get-tuple-element.6), channel_id=1, source_target_pairs={{2,0},{4,2},{6,4},{7,6},{5,7},{3,5},{1,3},{0,1},{10,8},{12,10},{14... | collective-permute-start | bytes 1327112 | tf_op jit(solution)/shard_map/ppermute | solution.py:116
  17.4 11.4 %collective-permute-start.2 = (bf16[3,2,2,144,128]{4,3,2,1,0:T(8,128)(2,1)S(1)}, bf16[3,2,2,144,128]{4,3,2,1,0:T(8,128)(2,1)S(1)}, u32[]{:S(2)}, u32[]{:S(2)}) collective-permute-start(bf16[3,2,2,144,128]{4,3,2,1,0:T(8,128)(2,1)S(1)} %collective-permute-done), channel_id=1, source_target_pairs={{0,2},{2,4},{4,6},{6,7},{7,5},{5,3},{3,1},{1,0},{8,10},{10,12},{12... | collective-permute-start | bytes 1327112 | tf_op jit(solution)/shard_map/ppermute | solution.py:115
  19.2 11.0 %collective-permute-start.3 = (bf16[3,2,2,144,128]{4,3,2,1,0:T(8,128)(2,1)S(1)}, bf16[3,2,2,144,128]{4,3,2,1,0:T(8,128)(2,1)S(1)}, u32[]{:S(2)}, u32[]{:S(2)}) collective-permute-start(bf16[3,2,2,144,128]{4,3,2,1,0:T(8,128)(2,1)S(1)} %collective-permute-done.1), channel_id=1, source_target_pairs={{2,0},{4,2},{6,4},{7,6},{5,7},{3,5},{1,3},{0,1},{10,8},{12,10},{14... | collective-permute-start | bytes 1327112 | tf_op jit(solution)/shard_map/ppermute | solution.py:116
  19.6 23.7 %collective-permute-start.16 = (bf16[3,8,144,128]{3,2,1,0:T(8,128)(2,1)S(1)}, bf16[3,8,144,128]{3,2,1,0:T(8,128)(2,1)S(1)}, u32[]{:S(2)}, u32[]{:S(2)}) collective-permute-start(bf16[3,8,144,128]{3,2,1,0:T(8,128)(2,1)S(1)} %pad_maximum_fusion), channel_id=1, source_target_pairs={{0,8},{1,9},{10,18},{11,19},{20,28},{21,29},{30,6},{31,7}} | collective-permute-start | bytes 2654216 | tf_op jit(solution)/shard_map/ppermute | solution.py:124
  21.0 23.7 %collective-permute-start.15 = (bf16[3,8,144,128]{3,2,1,0:T(8,128)(2,1)S(1)}, bf16[3,8,144,128]{3,2,1,0:T(8,128)(2,1)S(1)}, u32[]{:S(2)}, u32[]{:S(2)}) collective-permute-start(bf16[3,8,144,128]{3,2,1,0:T(8,128)(2,1)S(1)} %pad_maximum_fusion), channel_id=1, source_target_pairs={{0,16},{1,17},{10,26},{11,27},{20,4},{21,5},{30,14},{31,15}} | collective-permute-start | bytes 2654216 | tf_op jit(solution)/shard_map/ppermute | solution.py:124
  24.0 23.0 %collective-permute-start.14 = (bf16[3,8,144,128]{3,2,1,0:T(8,128)(2,1)S(1)}, bf16[3,8,144,128]{3,2,1,0:T(8,128)(2,1)S(1)}, u32[]{:S(2)}, u32[]{:S(2)}) collective-permute-start(bf16[3,8,144,128]{3,2,1,0:T(8,128)(2,1)S(1)} %pad_maximum_fusion), channel_id=1, source_target_pairs={{0,24},{1,25},{10,2},{11,3},{20,12},{21,13},{30,22},{31,23}} | collective-permute-start | bytes 2654216 | tf_op jit(solution)/shard_map/ppermute | solution.py:124
  28.8 10.4 %collective-permute-start.4 = (bf16[3,2,2,144,128]{4,3,2,1,0:T(8,128)(2,1)S(1)}, bf16[3,2,2,144,128]{4,3,2,1,0:T(8,128)(2,1)S(1)}, u32[]{:S(2)}, u32[]{:S(2)}) collective-permute-start(bf16[3,2,2,144,128]{4,3,2,1,0:T(8,128)(2,1)S(1)} %collective-permute-done.2), channel_id=1, source_target_pairs={{0,2},{2,4},{4,6},{6,7},{7,5},{5,3},{3,1},{1,0},{8,10},{10,12},{12... | collective-permute-start | bytes 1327112 | tf_op jit(solution)/shard_map/ppermute | solution.py:115
  30.2 11.3 %collective-permute-start.5 = (bf16[3,2,2,144,128]{4,3,2,1,0:T(8,128)(2,1)S(1)}, bf16[3,2,2,144,128]{4,3,2,1,0:T(8,128)(2,1)S(1)}, u32[]{:S(2)}, u32[]{:S(2)}) collective-permute-start(bf16[3,2,2,144,128]{4,3,2,1,0:T(8,128)(2,1)S(1)} %collective-permute-done.3), channel_id=1, source_target_pairs={{2,0},{4,2},{6,4},{7,6},{5,7},{3,5},{1,3},{0,1},{10,8},{12,10},{14... | collective-permute-start | bytes 1327112 | tf_op jit(solution)/shard_map/ppermute | solution.py:116
  39.2 10.5 %collective-permute-start.6 = (bf16[3,2,2,144,128]{4,3,2,1,0:T(8,128)(2,1)S(1)}, bf16[3,2,2,144,128]{4,3,2,1,0:T(8,128)(2,1)S(1)}, u32[]{:S(2)}, u32[]{:S(2)}) collective-permute-start(bf16[3,2,2,144,128]{4,3,2,1,0:T(8,128)(2,1)S(1)} %collective-permute-done.4), channel_id=1, source_target_pairs={{0,2},{2,4},{4,6},{6,7},{7,5},{5,3},{3,1},{1,0},{8,10},{10,12},{12... | collective-permute-start | bytes 1327112 | tf_op jit(solution)/shard_map/ppermute | solution.py:115
  41.5 10.3 %collective-permute-start.7 = (bf16[3,2,2,144,128]{4,3,2,1,0:T(8,128)(2,1)S(1)}, bf16[3,2,2,144,128]{4,3,2,1,0:T(8,128)(2,1)S(1)}, u32[]{:S(2)}, u32[]{:S(2)}) collective-permute-start(bf16[3,2,2,144,128]{4,3,2,1,0:T(8,128)(2,1)S(1)} %collective-permute-done.5), channel_id=1, source_target_pairs={{2,0},{4,2},{6,4},{7,6},{5,7},{3,5},{1,3},{0,1},{10,8},{12,10},{14... | collective-permute-start | bytes 1327112 | tf_op jit(solution)/shard_map/ppermute | solution.py:116
  43.4 23.0 %collective-permute-start.19 = (bf16[3,8,144,128]{3,2,1,0:T(8,128)(2,1)S(1)}, bf16[3,8,144,128]{3,2,1,0:T(8,128)(2,1)S(1)}, u32[]{:S(2)}, u32[]{:S(2)}) collective-permute-start(bf16[3,8,144,128]{3,2,1,0:T(8,128)(2,1)S(1)} %pad_maximum_fusion.1), channel_id=1, source_target_pairs={{0,8},{1,9},{10,18},{11,19},{20,28},{21,29},{30,6},{31,7}} | collective-permute-start | bytes 2654216 | tf_op jit(solution)/shard_map/ppermute | solution.py:124
  44.7 25.5 %collective-permute-start.18 = (bf16[3,8,144,128]{3,2,1,0:T(8,128)(2,1)S(1)}, bf16[3,8,144,128]{3,2,1,0:T(8,128)(2,1)S(1)}, u32[]{:S(2)}, u32[]{:S(2)}) collective-permute-start(bf16[3,8,144,128]{3,2,1,0:T(8,128)(2,1)S(1)} %pad_maximum_fusion.1), channel_id=1, source_target_pairs={{0,16},{1,17},{10,26},{11,27},{20,4},{21,5},{30,14},{31,15}} | collective-permute-start | bytes 2654216 | tf_op jit(solution)/shard_map/ppermute | solution.py:124
  47.1 24.5 %collective-permute-start.17 = (bf16[3,8,144,128]{3,2,1,0:T(8,128)(2,1)S(1)}, bf16[3,8,144,128]{3,2,1,0:T(8,128)(2,1)S(1)}, u32[]{:S(2)}, u32[]{:S(2)}) collective-permute-start(bf16[3,8,144,128]{3,2,1,0:T(8,128)(2,1)S(1)} %pad_maximum_fusion.1), channel_id=1, source_target_pairs={{0,24},{1,25},{10,2},{11,3},{20,12},{21,13},{30,22},{31,23}} | collective-permute-start | bytes 2654216 | tf_op jit(solution)/shard_map/ppermute | solution.py:124
  49.7 11.2 %collective-permute-start.8 = (bf16[3,2,2,144,128]{4,3,2,1,0:T(8,128)(2,1)S(1)}, bf16[3,2,2,144,128]{4,3,2,1,0:T(8,128)(2,1)S(1)}, u32[]{:S(2)}, u32[]{:S(2)}) collective-permute-start(bf16[3,2,2,144,128]{4,3,2,1,0:T(8,128)(2,1)S(1)} %collective-permute-done.6), channel_id=1, source_target_pairs={{0,2},{2,4},{4,6},{6,7},{7,5},{5,3},{3,1},{1,0},{8,10},{10,12},{12... | collective-permute-start | bytes 1327112 | tf_op jit(solution)/shard_map/ppermute | solution.py:115
  51.8 11.2 %collective-permute-start.9 = (bf16[3,2,2,144,128]{4,3,2,1,0:T(8,128)(2,1)S(1)}, bf16[3,2,2,144,128]{4,3,2,1,0:T(8,128)(2,1)S(1)}, u32[]{:S(2)}, u32[]{:S(2)}) collective-permute-start(bf16[3,2,2,144,128]{4,3,2,1,0:T(8,128)(2,1)S(1)} %collective-permute-done.7), channel_id=1, source_target_pairs={{2,0},{4,2},{6,4},{7,6},{5,7},{3,5},{1,3},{0,1},{10,8},{12,10},{14... | collective-permute-start | bytes 1327112 | tf_op jit(solution)/shard_map/ppermute | solution.py:116
  63.2 33.1 %collective-permute-start.22 = (bf16[3,8,144,128]{3,2,1,0:T(8,128)(2,1)S(1)}, bf16[3,8,144,128]{3,2,1,0:T(8,128)(2,1)S(1)}, u32[]{:S(2)}, u32[]{:S(2)}) collective-permute-start(bf16[3,8,144,128]{3,2,1,0:T(8,128)(2,1)S(1)} %pad_maximum_fusion.2), channel_id=1, source_target_pairs={{0,8},{1,9},{10,18},{11,19},{20,28},{21,29},{30,6},{31,7}} | collective-permute-start | bytes 2654216 | tf_op jit(solution)/shard_map/ppermute | solution.py:124
  64.6 10.3 %collective-permute-start.10 = (bf16[3,2,2,144,128]{4,3,2,1,0:T(8,128)(2,1)S(1)}, bf16[3,2,2,144,128]{4,3,2,1,0:T(8,128)(2,1)S(1)}, u32[]{:S(2)}, u32[]{:S(2)}) collective-permute-start(bf16[3,2,2,144,128]{4,3,2,1,0:T(8,128)(2,1)S(1)} %collective-permute-done.8), channel_id=1, source_target_pairs={{0,2},{2,4},{4,6},{6,7},{7,5},{5,3},{3,1},{1,0},{8,10},{10,12},{12... | collective-permute-start | bytes 1327112 | tf_op jit(solution)/shard_map/ppermute | solution.py:115
  66.4 32.1 %collective-permute-start.21 = (bf16[3,8,144,128]{3,2,1,0:T(8,128)(2,1)S(1)}, bf16[3,8,144,128]{3,2,1,0:T(8,128)(2,1)S(1)}, u32[]{:S(2)}, u32[]{:S(2)}) collective-permute-start(bf16[3,8,144,128]{3,2,1,0:T(8,128)(2,1)S(1)} %pad_maximum_fusion.2), channel_id=1, source_target_pairs={{0,16},{1,17},{10,26},{11,27},{20,4},{21,5},{30,14},{31,15}} | collective-permute-start | bytes 2654216 | tf_op jit(solution)/shard_map/ppermute | solution.py:124
  70.2 30.3 %collective-permute-start.20 = (bf16[3,8,144,128]{3,2,1,0:T(8,128)(2,1)S(1)}, bf16[3,8,144,128]{3,2,1,0:T(8,128)(2,1)S(1)}, u32[]{:S(2)}, u32[]{:S(2)}) collective-permute-start(bf16[3,8,144,128]{3,2,1,0:T(8,128)(2,1)S(1)} %pad_maximum_fusion.2), channel_id=1, source_target_pairs={{0,24},{1,25},{10,2},{11,3},{20,12},{21,13},{30,22},{31,23}} | collective-permute-start | bytes 2654216 | tf_op jit(solution)/shard_map/ppermute | solution.py:124
  71.6 10.8 %collective-permute-start.11 = (bf16[3,2,2,144,128]{4,3,2,1,0:T(8,128)(2,1)S(1)}, bf16[3,2,2,144,128]{4,3,2,1,0:T(8,128)(2,1)S(1)}, u32[]{:S(2)}, u32[]{:S(2)}) collective-permute-start(bf16[3,2,2,144,128]{4,3,2,1,0:T(8,128)(2,1)S(1)} %collective-permute-done.9), channel_id=1, source_target_pairs={{2,0},{4,2},{6,4},{7,6},{5,7},{3,5},{1,3},{0,1},{10,8},{12,10},{14... | collective-permute-start | bytes 1327112 | tf_op jit(solution)/shard_map/ppermute | solution.py:116
  74.9 25.6 %copy-start = (bf16[3,2,144,128]{3,2,1,0:T(8,128)(2,1)}, bf16[3,2,144,128]{3,2,1,0:T(8,128)(2,1)S(1)}, u32[]{:S(2)}) copy-start(bf16[3,2,144,128]{3,2,1,0:T(8,128)(2,1)S(1)} %dynamic-slice_bitcast_fusion.3) | copy-start | bytes 663556
  74.9 12.6 %collective-permute-start.12 = (bf16[3,2,2,144,128]{4,3,2,1,0:T(8,128)(2,1)S(1)}, bf16[3,2,2,144,128]{4,3,2,1,0:T(8,128)(2,1)S(1)}, u32[]{:S(2)}, u32[]{:S(2)}) collective-permute-start(bf16[3,2,2,144,128]{4,3,2,1,0:T(8,128)(2,1)S(1)} %collective-permute-done.10), channel_id=1, source_target_pairs={{0,2},{2,4},{4,6},{6,7},{7,5},{5,3},{3,1},{1,0},{8,10},{10,12},{12... | collective-permute-start | bytes 1327112 | tf_op jit(solution)/shard_map/ppermute | solution.py:115
  82.3 9.8 %collective-permute-start.13 = (bf16[3,2,2,144,128]{4,3,2,1,0:T(8,128)(2,1)S(1)}, bf16[3,2,2,144,128]{4,3,2,1,0:T(8,128)(2,1)S(1)}, u32[]{:S(2)}, u32[]{:S(2)}) collective-permute-start(bf16[3,2,2,144,128]{4,3,2,1,0:T(8,128)(2,1)S(1)} %collective-permute-done.11), channel_id=1, source_target_pairs={{2,0},{4,2},{6,4},{7,6},{5,7},{3,5},{1,3},{0,1},{10,8},{12,10},{14... | collective-permute-start | bytes 1327112 | tf_op jit(solution)/shard_map/ppermute | solution.py:116
  87.5 15.6 %collective-permute-start.25 = (bf16[3,4,144,128]{3,2,1,0:T(8,128)(2,1)}, bf16[3,4,144,128]{3,2,1,0:T(8,128)(2,1)S(1)}, u32[]{:S(2)}, u32[]{:S(2)}) collective-permute-start(bf16[3,4,144,128]{3,2,1,0:T(8,128)(2,1)} %pad_maximum_fusion.3), channel_id=1, source_target_pairs={{0,8},{1,9},{10,18},{11,19},{20,28},{21,29},{30,6},{31,7}} | collective-permute-start | bytes 1327112 | tf_op jit(solution)/shard_map/ppermute | solution.py:124
  89.1 11.4 %copy-start.1 = (bf16[3,2,144,128]{3,2,1,0:T(8,128)(2,1)}, bf16[3,2,144,128]{3,2,1,0:T(8,128)(2,1)S(1)}, u32[]{:S(2)}) copy-start(bf16[3,2,144,128]{3,2,1,0:T(8,128)(2,1)S(1)} %dynamic-slice_bitcast_fusion.1) | copy-start | bytes 663556
  92.1 17.6 %collective-permute-start.24 = (bf16[3,4,144,128]{3,2,1,0:T(8,128)(2,1)}, bf16[3,4,144,128]{3,2,1,0:T(8,128)(2,1)}, u32[]{:S(2)}, u32[]{:S(2)}) collective-permute-start(bf16[3,4,144,128]{3,2,1,0:T(8,128)(2,1)} %pad_maximum_fusion.3), channel_id=1, source_target_pairs={{0,16},{1,17},{10,26},{11,27},{20,4},{21,5},{30,14},{31,15}} | collective-permute-start | bytes 1327112 | tf_op jit(solution)/shard_map/ppermute | solution.py:124
  95.5 5.0 %copy-start.3 = (bf16[3,2,144,128]{3,2,1,0:T(8,128)(2,1)}, bf16[3,2,144,128]{3,2,1,0:T(8,128)(2,1)S(1)}, u32[]{:S(2)}) copy-start(bf16[3,2,144,128]{3,2,1,0:T(8,128)(2,1)S(1)} %dynamic-slice_bitcast_fusion) | copy-start | bytes 663556
  96.4 13.3 %collective-permute-start.23 = (bf16[3,4,144,128]{3,2,1,0:T(8,128)(2,1)}, bf16[3,4,144,128]{3,2,1,0:T(8,128)(2,1)}, u32[]{:S(2)}, u32[]{:S(2)}) collective-permute-start(bf16[3,4,144,128]{3,2,1,0:T(8,128)(2,1)} %pad_maximum_fusion.3), channel_id=1, source_target_pairs={{0,24},{1,25},{10,2},{11,3},{20,12},{21,13},{30,22},{31,23}} | collective-permute-start | bytes 1327112 | tf_op jit(solution)/shard_map/ppermute | solution.py:124
  98.4 12.6 %collective-permute-start.28 = (bf16[3,4,144,128]{3,2,1,0:T(8,128)(2,1)}, bf16[3,4,144,128]{3,2,1,0:T(8,128)(2,1)}, u32[]{:S(2)}, u32[]{:S(2)}) collective-permute-start(bf16[3,4,144,128]{3,2,1,0:T(8,128)(2,1)} %pad_maximum_fusion.4), channel_id=1, source_target_pairs={{0,8},{1,9},{10,18},{11,19},{20,28},{21,29},{30,6},{31,7}} | collective-permute-start | bytes 1327112 | tf_op jit(solution)/shard_map/ppermute | solution.py:124
  100.5 10.5 %collective-permute-start.27 = (bf16[3,4,144,128]{3,2,1,0:T(8,128)(2,1)}, bf16[3,4,144,128]{3,2,1,0:T(8,128)(2,1)}, u32[]{:S(2)}, u32[]{:S(2)}) collective-permute-start(bf16[3,4,144,128]{3,2,1,0:T(8,128)(2,1)} %pad_maximum_fusion.4), channel_id=1, source_target_pairs={{0,16},{1,17},{10,26},{11,27},{20,4},{21,5},{30,14},{31,15}} | collective-permute-start | bytes 1327112 | tf_op jit(solution)/shard_map/ppermute | solution.py:124
  103.1 11.9 %collective-permute-start.26 = (bf16[3,4,144,128]{3,2,1,0:T(8,128)(2,1)}, bf16[3,4,144,128]{3,2,1,0:T(8,128)(2,1)}, u32[]{:S(2)}, u32[]{:S(2)}) collective-permute-start(bf16[3,4,144,128]{3,2,1,0:T(8,128)(2,1)} %pad_maximum_fusion.4), channel_id=1, source_target_pairs={{0,24},{1,25},{10,2},{11,3},{20,12},{21,13},{30,22},{31,23}} | collective-permute-start | bytes 1327112 | tf_op jit(solution)/shard_map/ppermute | solution.py:124
  (2 other events, 8.7 us)

commit v11 on v10

--- a/solution.py
+++ b/solution.py
@@ -12,12 +12,16 @@
 META = 16
 
 
-def gram_kernel(offs_ref, bs_ref, bc_ref, o_ref, *, chunk, local_slots, blk):
+def gram_kernel(offs_ref, bs_ref, bc_ref, *refs, chunk, local_slots, blk):
+    o_ref = refs[-1]
     step = pl.program_id(0)
 
     @pl.when(step == 0)
     def _():
-        o_ref[...] = jnp.zeros_like(o_ref)
+        if len(refs) == 2:
+            o_ref[...] = refs[0][...]
+        else:
+            o_ref[...] = jnp.zeros_like(o_ref)
 
     stride = local_slots + 1
     for k in range(chunk):
@@ -38,11 +42,13 @@
             o_ref[pl.ds(row, blk), pl.ds(col, blk)] += prod[s * blk : (s + 1) * blk]
 
 
-def gram_call(offs, bs, bc):
+def gram_call(offs, bs, bc, acc=None):
     n, local_slots, rows, blk = bs.shape
     chunk = CHUNK
     kernel = functools.partial(gram_kernel, chunk=chunk, local_slots=local_slots, blk=blk)
     out_rows, out_cols = local_slots * IBS * blk, IBS * blk
+    acc_specs = [] if acc is None else [pl.BlockSpec((out_rows, out_cols), lambda i, o: (0, 0))]
+    acc_args = () if acc is None else (acc,)
     return pl.pallas_call(
         kernel,
         grid_spec=pltpu.PrefetchScalarGridSpec(
@@ -51,19 +57,21 @@
             in_specs=[
                 pl.BlockSpec((chunk, local_slots, rows, blk), lambda i, o: (i, 0, 0, 0)),
                 pl.BlockSpec((chunk, rows, blk), lambda i, o: (i, 0, 0)),
-            ],
+            ]
+            + acc_specs,
             out_specs=pl.BlockSpec((out_rows, out_cols), lambda i, o: (0, 0)),
         ),
         out_shape=jax.ShapeDtypeStruct((out_rows, out_cols), jnp.float32),
+        input_output_aliases={} if acc is None else {3: 0},
         compiler_params=pltpu.CompilerParams(
-            dimension_semantics=("arbitrary",), vmem_limit_bytes=48 * 1024 * 1024
+            dimension_semantics=("arbitrary",), vmem_limit_bytes=56 * 1024 * 1024
         ),
         cost_estimate=pl.CostEstimate(
             flops=2 * n * local_slots * blk * blk * blk,
             transcendentals=0,
             bytes_accessed=n * (local_slots + 1) * blk * blk * 2 + out_rows * out_cols * 4,
         ),
-    )(offs, bs, bc)
+    )(offs, bs, bc, *acc_args)
 
 
 def with_meta(panel_blocks, user_weights, slot_offset):
@@ -124,15 +132,20 @@
                 got = jnp.where(which == j, lax.ppermute(own, ("row", "col"), fan), got)
             columns.append(got)
 
-    blocks = jnp.concatenate(pieces, axis=1)
-    column_blocks = jnp.concatenate(columns, axis=1)
-    n = panels * blocks.shape[1]
-    blocks = blocks.reshape(n, local_slots, blk + META, blk)
-    column_blocks = column_blocks.reshape(n, blk + META, blk)
-
-    offs = jnp.concatenate([blocks[:, :, blk + 3, 0], column_blocks[:, blk + 3, 0][:, None]], axis=1)
-    offs = jnp.clip(offs.astype(jnp.int32), 0, IBS - 1).reshape(-1)
-    return gram_call(offs, blocks, column_blocks)
+    split = len(pieces) - 4
+    acc = None
+    for w_part, c_part in ((pieces[:split], columns[:-2]), (pieces[split:], columns[-2:])):
+        blocks = jnp.concatenate(w_part, axis=1)
+        column_blocks = jnp.concatenate(c_part, axis=1)
+        n = panels * blocks.shape[1]
+        blocks = blocks.reshape(n, local_slots, blk + META, blk)
+        column_blocks = column_blocks.reshape(n, blk + META, blk)
+        offs = jnp.concatenate(
+            [blocks[:, :, blk + 3, 0], column_blocks[:, blk + 3, 0][:, None]], axis=1
+        )
+        offs = jnp.clip(offs.astype(jnp.int32), 0, IBS - 1).reshape(-1)
+        acc = gram_call(offs, blocks, column_blocks, acc)
+    return acc
 
 
 def solution(mesh):

time: 135 us -> 148 us (1.096)
  Pallas kernels: 14.6 us -> 23.5 us
  starting transfers between devices: 43.6 us -> 49.2 us
  waiting for transfers between devices: 47 us -> 49.3 us
  local copies, waits for them, and re-layouts: 17.8 us -> 15.8 us
    ppermute x7, waiting for transfers between devices: 31.5 us -> 42.2 us  [local(): a = lax.ppermute(a, 'col', forward)]
    pallas_call x1 -> x2, Pallas kernels: 14.6 us -> 23.5 us  [gram_call(): pl.pallas_call(kernel, grid_spec=pltpu.PrefetchScalarGridSpec(num_scalar_...]
    ppermute x7, starting transfers between devices: 1.19 us -> 7.58 us  [local(): b = lax.ppermute(b, 'col', backward)]
    ppermute x7, waiting for transfers between devices: 11.5 us -> 7.08 us  [local(): b = lax.ppermute(b, 'col', backward)]
    ppermute x15, waiting for transfers between devices: 4.03 us -> 0.04 us  [local(): got = jnp.where(which == j, lax.ppermute(own, ('row', 'col'), fan), got)]
    unnamed x5 -> x1, other arithmetic: 5.26 us -> 2.39 us
    unnamed x23 -> x45, local copies, waits for them, and re-layouts: 11.1 us -> 8.75 us
    select_n x0 -> x5, other arithmetic: none -> 2.01 us  [local(): got = jnp.where(which == j, lax.ppermute(own, ('row', 'col'), fan), got)]
  transfers between devices with their start and end apart: 29 -> 29, of which waited for: 11 -> 11; matrix products, arithmetic and copies ran while one was open for 15% -> 13% of each run, Pallas kernels for 0% -> 9%
where the time goes in v11:
time: 148 us
  waiting for transfers between devices  49.3 us (33%)
  starting transfers between devices  49.2 us (33%)
  Pallas kernels  23.5 us (16%)
  local copies, waits for them, and re-layouts  15.8 us (11%)
  other arithmetic  9.36 us (6%)
    ppermute x7, waiting for transfers between devices, local(): a = lax.ppermute(a, 'col', forward)  42.2 us
    ppermute x15, starting transfers between devices, local(): got = jnp.where(which == j, lax.ppermute(own, ('row', 'col'), fan), got)  30.4 us
    pallas_call x2, Pallas kernels, gram_call(): pl.pallas_call(kernel, grid_spec=pltpu.PrefetchScalarGridSpec(num_scalar_...  23.5 us
    ppermute x7, starting transfers between devices, local(): a = lax.ppermute(a, 'col', forward)  11.3 us
    unnamed x45, local copies, waits for them, and re-layouts  8.75 us
    ppermute x7, starting transfers between devices, local(): b = lax.ppermute(b, 'col', backward)  7.58 us
    ppermute x7, waiting for transfers between devices, local(): b = lax.ppermute(b, 'col', backward)  7.08 us
  transfers between devices with their start and end apart: 29, of which 11 were waited for; matrix products, arithmetic and copies ran while one was open for 13% of the time, Pallas kernels for 9%

profile of v11, /device:TPU:0, one launch (start us, length us, event | category | flops | bytes accessed | tf_op | source)
XLA Modules:
  0.0 147.6 jit_solution(1830879188419144998)
XLA Ops:
  1.7 2.4 %constant_dynamic-update-slice_fusion.10 = (bf16[3,24,2,144,128]{4,3,2,1,0:T(8,128)(2,1)}, bf16[3,4,2,144,128]{4,3,2,1,0:T(8,128)(2,1)S(1)}) fusion(bf16[144]{0:T(256)(128)(2,1)S(1)} %pad.36.clone, bf16[3,4,2,1,128]{4,3,2,1,0:T(2,128)(2,1)S(1)} %broadcast_in_dim.7, bf16[3,4,2,3,128]{4,3,2,1,0:T(4,128)(2,1)S(1)} %broadcast_in_dim.6, ...), kind=kLoop, calls=%fused_computation.41 | loop fusion | flops 3538943 | bytes 2580768
  4.2 3.1 %collective-permute-start = (bf16[3,2,2,144,128]{4,3,2,1,0:T(8,128)(2,1)S(1)}, bf16[3,2,2,144,128]{4,3,2,1,0:T(8,128)(2,1)S(1)}, u32[]{:S(2)}, u32[]{:S(2)}) collective-permute-start(bf16[3,2,2,144,128]{4,3,2,1,0:T(8,128)(2,1)S(1)} %get-tuple-element.5), channel_id=1, source_target_pairs={{0,2},{2,4},{4,6},{6,7},{7,5},{5,3},{3,1},{1,0},{8,10},{10,12},{12... | collective-permute-start | bytes 1327112 | tf_op jit(solution)/shard_map/ppermute | solution.py:123
  7.3 10.1 %collective-permute-done = bf16[3,2,2,144,128]{4,3,2,1,0:T(8,128)(2,1)S(1)} collective-permute-done((bf16[3,2,2,144,128]{4,3,2,1,0:T(8,128)(2,1)S(1)}, bf16[3,2,2,144,128]{4,3,2,1,0:T(8,128)(2,1)S(1)}, u32[]{:S(2)}, u32[]{:S(2)}) %collective-permute-start) | collective-permute-done | bytes 442400 | tf_op jit(solution)/shard_map/ppermute | solution.py:123
  17.4 1.8 %collective-permute-start.1 = (bf16[3,2,2,144,128]{4,3,2,1,0:T(8,128)(2,1)S(1)}, bf16[3,2,2,144,128]{4,3,2,1,0:T(8,128)(2,1)S(1)}, u32[]{:S(2)}, u32[]{:S(2)}) collective-permute-start(bf16[3,2,2,144,128]{4,3,2,1,0:T(8,128)(2,1)S(1)} %collective-permute-done), channel_id=1, source_target_pairs={{0,2},{2,4},{4,6},{6,7},{7,5},{5,3},{3,1},{1,0},{8,10},{10,12},{12... | collective-permute-start | bytes 1327112 | tf_op jit(solution)/shard_map/ppermute | solution.py:123
  21.0 3.0 %collective-permute-start.21 = (bf16[3,8,144,128]{3,2,1,0:T(8,128)(2,1)S(1)}, bf16[3,8,144,128]{3,2,1,0:T(8,128)(2,1)S(1)}, u32[]{:S(2)}, u32[]{:S(2)}) collective-permute-start(bf16[3,8,144,128]{3,2,1,0:T(8,128)(2,1)S(1)} %pad_maximum_fusion.3), channel_id=1, source_target_pairs={{0,16},{1,17},{10,26},{11,27},{20,4},{21,5},{30,14},{31,15}} | collective-permute-start | bytes 2654216 | tf_op jit(solution)/shard_map/ppermute | solution.py:132
  27.1 1.6 %collective-permute-done.1 = bf16[3,2,2,144,128]{4,3,2,1,0:T(8,128)(2,1)S(1)} collective-permute-done((bf16[3,2,2,144,128]{4,3,2,1,0:T(8,128)(2,1)S(1)}, bf16[3,2,2,144,128]{4,3,2,1,0:T(8,128)(2,1)S(1)}, u32[]{:S(2)}, u32[]{:S(2)}) %collective-permute-start.1) | collective-permute-done | bytes 442400 | tf_op jit(solution)/shard_map/ppermute | solution.py:123
  28.7 1.5 %collective-permute-start.2 = (bf16[3,2,2,144,128]{4,3,2,1,0:T(8,128)(2,1)S(1)}, bf16[3,2,2,144,128]{4,3,2,1,0:T(8,128)(2,1)S(1)}, u32[]{:S(2)}, u32[]{:S(2)}) collective-permute-start(bf16[3,2,2,144,128]{4,3,2,1,0:T(8,128)(2,1)S(1)} %collective-permute-done.1), channel_id=1, source_target_pairs={{0,2},{2,4},{4,6},{6,7},{7,5},{5,3},{3,1},{1,0},{8,10},{10,12},{12... | collective-permute-start | bytes 1327112 | tf_op jit(solution)/shard_map/ppermute | solution.py:123
  32.6 6.6 %collective-permute-done.2 = bf16[3,2,2,144,128]{4,3,2,1,0:T(8,128)(2,1)S(1)} collective-permute-done((bf16[3,2,2,144,128]{4,3,2,1,0:T(8,128)(2,1)S(1)}, bf16[3,2,2,144,128]{4,3,2,1,0:T(8,128)(2,1)S(1)}, u32[]{:S(2)}, u32[]{:S(2)}) %collective-permute-start.2) | collective-permute-done | bytes 442400 | tf_op jit(solution)/shard_map/ppermute | solution.py:123
  39.2 2.1 %collective-permute-done.8 = bf16[3,2,2,144,128]{4,3,2,1,0:T(8,128)(2,1)S(1)} collective-permute-done((bf16[3,2,2,144,128]{4,3,2,1,0:T(8,128)(2,1)S(1)}, bf16[3,2,2,144,128]{4,3,2,1,0:T(8,128)(2,1)S(1)}, u32[]{:S(2)}, u32[]{:S(2)}) %collective-permute-start.8) | collective-permute-done | bytes 442400 | tf_op jit(solution)/shard_map/ppermute | solution.py:124
  42.8 1.6 %collective-permute-start.24 = (bf16[3,8,144,128]{3,2,1,0:T(8,128)(2,1)S(1)}, bf16[3,8,144,128]{3,2,1,0:T(8,128)(2,1)S(1)}, u32[]{:S(2)}, u32[]{:S(2)}) collective-permute-start(bf16[3,8,144,128]{3,2,1,0:T(8,128)(2,1)S(1)} %pad_maximum_fusion.4), channel_id=1, source_target_pairs={{0,16},{1,17},{10,26},{11,27},{20,4},{21,5},{30,14},{31,15}} | collective-permute-start | bytes 2654216 | tf_op jit(solution)/shard_map/ppermute | solution.py:132
  46.7 2.0 %collective-permute-start.9 = (bf16[3,2,2,144,128]{4,3,2,1,0:T(8,128)(2,1)S(1)}, bf16[3,2,2,144,128]{4,3,2,1,0:T(8,128)(2,1)S(1)}, u32[]{:S(2)}, u32[]{:S(2)}) collective-permute-start(bf16[3,2,2,144,128]{4,3,2,1,0:T(8,128)(2,1)S(1)} %collective-permute-done.8), channel_id=1, source_target_pairs={{2,0},{4,2},{6,4},{7,6},{5,7},{3,5},{1,3},{0,1},{10,8},{12,10},{14... | collective-permute-start | bytes 1327112 | tf_op jit(solution)/shard_map/ppermute | solution.py:124
  49.9 6.0 %collective-permute-done.3 = bf16[3,2,2,144,128]{4,3,2,1,0:T(8,128)(2,1)S(1)} collective-permute-done((bf16[3,2,2,144,128]{4,3,2,1,0:T(8,128)(2,1)S(1)}, bf16[3,2,2,144,128]{4,3,2,1,0:T(8,128)(2,1)S(1)}, u32[]{:S(2)}, u32[]{:S(2)}) %collective-permute-start.3) | collective-permute-done | bytes 442400 | tf_op jit(solution)/shard_map/ppermute | solution.py:123
  55.8 2.5 %collective-permute-start.4 = (bf16[3,2,2,144,128]{4,3,2,1,0:T(8,128)(2,1)S(1)}, bf16[3,2,2,144,128]{4,3,2,1,0:T(8,128)(2,1)S(1)}, u32[]{:S(2)}, u32[]{:S(2)}) collective-permute-start(bf16[3,2,2,144,128]{4,3,2,1,0:T(8,128)(2,1)S(1)} %collective-permute-done.3), channel_id=1, source_target_pairs={{0,2},{2,4},{4,6},{6,7},{7,5},{5,3},{3,1},{1,0},{8,10},{10,12},{12... | collective-permute-start | bytes 1327112 | tf_op jit(solution)/shard_map/ppermute | solution.py:123
  58.8 2.4 %collective-permute-start.10 = (bf16[3,2,2,144,128]{4,3,2,1,0:T(8,128)(2,1)S(1)}, bf16[3,2,2,144,128]{4,3,2,1,0:T(8,128)(2,1)}, u32[]{:S(2)}, u32[]{:S(2)}) collective-permute-start(bf16[3,2,2,144,128]{4,3,2,1,0:T(8,128)(2,1)S(1)} %collective-permute-done.9), channel_id=1, source_target_pairs={{2,0},{4,2},{6,4},{7,6},{5,7},{3,5},{1,3},{0,1},{10,8},{12,10},{14... | collective-permute-start | bytes 1327112 | tf_op jit(solution)/shard_map/ppermute | solution.py:124
  62.9 6.9 %collective-permute-done.4 = bf16[3,2,2,144,128]{4,3,2,1,0:T(8,128)(2,1)S(1)} collective-permute-done((bf16[3,2,2,144,128]{4,3,2,1,0:T(8,128)(2,1)S(1)}, bf16[3,2,2,144,128]{4,3,2,1,0:T(8,128)(2,1)S(1)}, u32[]{:S(2)}, u32[]{:S(2)}) %collective-permute-start.4) | collective-permute-done | bytes 442400 | tf_op jit(solution)/shard_map/ppermute | solution.py:123
  69.9 2.0 %collective-permute-done.10 = bf16[3,2,2,144,128]{4,3,2,1,0:T(8,128)(2,1)} collective-permute-done((bf16[3,2,2,144,128]{4,3,2,1,0:T(8,128)(2,1)S(1)}, bf16[3,2,2,144,128]{4,3,2,1,0:T(8,128)(2,1)}, u32[]{:S(2)}, u32[]{:S(2)}) %collective-permute-start.10) | collective-permute-done | bytes 442400 | tf_op jit(solution)/shard_map/ppermute | solution.py:124
  73.8 2.9 %collective-permute-start.28 = (bf16[3,8,144,128]{3,2,1,0:T(8,128)(2,1)}, bf16[3,8,144,128]{3,2,1,0:T(8,128)(2,1)}, u32[]{:S(2)}, u32[]{:S(2)}) collective-permute-start(bf16[3,8,144,128]{3,2,1,0:T(8,128)(2,1)} %pad_maximum_fusion.5), channel_id=1, source_target_pairs={{0,8},{1,9},{10,18},{11,19},{20,28},{21,29},{30,6},{31,7}} | collective-permute-start | bytes 2654216 | tf_op jit(solution)/shard_map/ppermute | solution.py:132
  76.8 2.3 %collective-permute-start.27 = (bf16[3,8,144,128]{3,2,1,0:T(8,128)(2,1)}, bf16[3,8,144,128]{3,2,1,0:T(8,128)(2,1)}, u32[]{:S(2)}, u32[]{:S(2)}) collective-permute-start(bf16[3,8,144,128]{3,2,1,0:T(8,128)(2,1)} %pad_maximum_fusion.5), channel_id=1, source_target_pairs={{0,16},{1,17},{10,26},{11,27},{20,4},{21,5},{30,14},{31,15}} | collective-permute-start | bytes 2654216 | tf_op jit(solution)/shard_map/ppermute | solution.py:132
  79.1 2.2 %collective-permute-start.26 = (bf16[3,8,144,128]{3,2,1,0:T(8,128)(2,1)}, bf16[3,8,144,128]{3,2,1,0:T(8,128)(2,1)}, u32[]{:S(2)}, u32[]{:S(2)}) collective-permute-start(bf16[3,8,144,128]{3,2,1,0:T(8,128)(2,1)} %pad_maximum_fusion.5), channel_id=1, source_target_pairs={{0,24},{1,25},{10,2},{11,3},{20,12},{21,13},{30,22},{31,23}} | collective-permute-start | bytes 2654216 | tf_op jit(solution)/shard_map/ppermute | solution.py:132
  81.3 2.0 %collective-permute-start.11 = (bf16[3,2,2,144,128]{4,3,2,1,0:T(8,128)(2,1)}, bf16[3,2,2,144,128]{4,3,2,1,0:T(8,128)(2,1)S(1)}, u32[]{:S(2)}, u32[]{:S(2)}) collective-permute-start(bf16[3,2,2,144,128]{4,3,2,1,0:T(8,128)(2,1)} %collective-permute-done.10), channel_id=1, source_target_pairs={{2,0},{4,2},{6,4},{7,6},{5,7},{3,5},{1,3},{0,1},{10,8},{12,10},{14... | collective-permute-start | bytes 1327112 | tf_op jit(solution)/shard_map/ppermute | solution.py:124
  85.4 5.0 %collective-permute-done.5 = bf16[3,2,2,144,128]{4,3,2,1,0:T(8,128)(2,1)S(1)} collective-permute-done((bf16[3,2,2,144,128]{4,3,2,1,0:T(8,128)(2,1)S(1)}, bf16[3,2,2,144,128]{4,3,2,1,0:T(8,128)(2,1)S(1)}, u32[]{:S(2)}, u32[]{:S(2)}) %collective-permute-start.5) | collective-permute-done | bytes 442400 | tf_op jit(solution)/shard_map/ppermute | solution.py:123
  90.4 2.4 %collective-permute-start.12 = (bf16[3,2,2,144,128]{4,3,2,1,0:T(8,128)(2,1)S(1)}, bf16[3,2,2,144,128]{4,3,2,1,0:T(8,128)(2,1)S(1)}, u32[]{:S(2)}, u32[]{:S(2)}) collective-permute-start(bf16[3,2,2,144,128]{4,3,2,1,0:T(8,128)(2,1)S(1)} %collective-permute-done.5), channel_id=1, source_target_pairs={{0,2},{2,4},{4,6},{6,7},{7,5},{5,3},{3,1},{1,0},{8,10},{10,12},{12... | collective-permute-start | bytes 1327112 | tf_op jit(solution)/shard_map/ppermute | solution.py:123
  92.8 1.9 %constant_dynamic-update-slice_fusion = bf16[3,24,2,144,128]{4,3,2,1,0:T(8,128)(2,1)} fusion(bf16[3,24,2,144,128]{4,3,2,1,0:T(8,128)(2,1)} %constant_dynamic-update-slice_fusion.1, bf16[3,2,2,144,128]{4,3,2,1,0:T(8,128)(2,1)} %collective-permute-done.10), kind=kLoop, calls=%fused_computation.31 | loop fusion | bytes 884736 | tf_op jit(solution)/shard_map/concatenate | solution.py:138
  97.0 6.1 %collective-permute-done.12 = bf16[3,2,2,144,128]{4,3,2,1,0:T(8,128)(2,1)S(1)} collective-permute-done((bf16[3,2,2,144,128]{4,3,2,1,0:T(8,128)(2,1)S(1)}, bf16[3,2,2,144,128]{4,3,2,1,0:T(8,128)(2,1)S(1)}, u32[]{:S(2)}, u32[]{:S(2)}) %collective-permute-start.12) | collective-permute-done | bytes 442400 | tf_op jit(solution)/shard_map/ppermute | solution.py:123
  103.0 3.2 %collective-permute-start.16 = (bf16[3,4,144,128]{3,2,1,0:T(8,128)(2,1)}, bf16[3,4,144,128]{3,2,1,0:T(8,128)(2,1)}, u32[]{:S(2)}, u32[]{:S(2)}) collective-permute-start(bf16[3,4,144,128]{3,2,1,0:T(8,128)(2,1)} %pad_maximum_fusion.6), channel_id=1, source_target_pairs={{0,8},{1,9},{10,18},{11,19},{20,28},{21,29},{30,6},{31,7}} | collective-permute-start | bytes 1327112 | tf_op jit(solution)/shard_map/ppermute | solution.py:132
  106.3 2.5 %collective-permute-done.13 = bf16[3,2,2,144,128]{4,3,2,1,0:T(8,128)(2,1)S(1)} collective-permute-done((bf16[3,2,2,144,128]{4,3,2,1,0:T(8,128)(2,1)S(1)}, bf16[3,2,2,144,128]{4,3,2,1,0:T(8,128)(2,1)S(1)}, u32[]{:S(2)}, u32[]{:S(2)}) %collective-permute-start.13) | collective-permute-done | bytes 442400 | tf_op jit(solution)/shard_map/ppermute | solution.py:124
  108.8 2.1 %collective-permute-start.15 = (bf16[3,4,144,128]{3,2,1,0:T(8,128)(2,1)}, bf16[3,4,144,128]{3,2,1,0:T(8,128)(2,1)}, u32[]{:S(2)}, u32[]{:S(2)}) collective-permute-start(bf16[3,4,144,128]{3,2,1,0:T(8,128)(2,1)} %pad_maximum_fusion.6), channel_id=1, source_target_pairs={{0,16},{1,17},{10,26},{11,27},{20,4},{21,5},{30,14},{31,15}} | collective-permute-start | bytes 1327112 | tf_op jit(solution)/shard_map/ppermute | solution.py:132
  111.7 2.1 %collective-permute-start.14 = (bf16[3,4,144,128]{3,2,1,0:T(8,128)(2,1)}, bf16[3,4,144,128]{3,2,1,0:T(8,128)(2,1)}, u32[]{:S(2)}, u32[]{:S(2)}) collective-permute-start(bf16[3,4,144,128]{3,2,1,0:T(8,128)(2,1)} %pad_maximum_fusion.6), channel_id=1, source_target_pairs={{0,24},{1,25},{10,2},{11,3},{20,12},{21,13},{30,22},{31,23}} | collective-permute-start | bytes 1327112 | tf_op jit(solution)/shard_map/ppermute | solution.py:132
  113.8 2.1 %collective-permute-start.19 = (bf16[3,4,144,128]{3,2,1,0:T(8,128)(2,1)}, bf16[3,4,144,128]{3,2,1,0:T(8,128)(2,1)}, u32[]{:S(2)}, u32[]{:S(2)}) collective-permute-start(bf16[3,4,144,128]{3,2,1,0:T(8,128)(2,1)} %pad_maximum_fusion.7), channel_id=1, source_target_pairs={{0,8},{1,9},{10,18},{11,19},{20,28},{21,29},{30,6},{31,7}} | collective-permute-start | bytes 1327112 | tf_op jit(solution)/shard_map/ppermute | solution.py:132
  115.9 2.1 %collective-permute-start.18 = (bf16[3,4,144,128]{3,2,1,0:T(8,128)(2,1)}, bf16[3,4,144,128]{3,2,1,0:T(8,128)(2,1)}, u32[]{:S(2)}, u32[]{:S(2)}) collective-permute-start(bf16[3,4,144,128]{3,2,1,0:T(8,128)(2,1)} %pad_maximum_fusion.7), channel_id=1, source_target_pairs={{0,16},{1,17},{10,26},{11,27},{20,4},{21,5},{30,14},{31,15}} | collective-permute-start | bytes 1327112 | tf_op jit(solution)/shard_map/ppermute | solution.py:132
  122.7 13.0 %shard_map.37.refs_0_ = f32[2048,1024]{1,0:T(8,128)} custom-call(s32[216]{0:T(256)} %min.25.offs_ref, bf16[72,2,144,128]{3,2,1,0:T(8,128)(2,1)} %bitcast.49, bf16[72,144,128]{2,1,0:T(8,128)(2,1)} %bitcast.47), custom_call_target="tpu_custom_call" | custom-call | flops 603979776 | bytes 15466496 | tf_op jit(solution)/shard_map/pallas_call | solution.py:52
  137.2 10.4 %shard_map.38 = f32[2048,1024]{1,0:T(8,128)} custom-call(s32[72]{0:T(128)} %min.22.offs_ref, bf16[24,2,144,128]{3,2,1,0:T(8,128)(2,1)} %bitcast.51, bf16[24,144,128]{2,1,0:T(8,128)(2,1)} %bitcast.53, f32[2048,1024]{1,0:T(8,128)} %shard_map.37.refs_0_), custom_call_target="tpu_custom_call", output_to_operand_aliasing={{}: (3, {})} | custom-call | flops 201326592 | bytes 10747904 | tf_op jit(solution)/shard_map/pallas_call | solution.py:52
  (125 shorter events, 29.3 us)
Async XLA Ops:
  4.2 13.2 %collective-permute-start = (bf16[3,2,2,144,128]{4,3,2,1,0:T(8,128)(2,1)S(1)}, bf16[3,2,2,144,128]{4,3,2,1,0:T(8,128)(2,1)S(1)}, u32[]{:S(2)}, u32[]{:S(2)}) collective-permute-start(bf16[3,2,2,144,128]{4,3,2,1,0:T(8,128)(2,1)S(1)} %get-tuple-element.5), channel_id=1, source_target_pairs={{0,2},{2,4},{4,6},{6,7},{7,5},{5,3},{3,1},{1,0},{8,10},{10,12},{12... | collective-permute-start | bytes 1327112 | tf_op jit(solution)/shard_map/ppermute | solution.py:123
  7.3 11.9 %collective-permute-start.6 = (bf16[3,2,2,144,128]{4,3,2,1,0:T(8,128)(2,1)S(1)}, bf16[3,2,2,144,128]{4,3,2,1,0:T(8,128)(2,1)S(1)}, u32[]{:S(2)}, u32[]{:S(2)}) collective-permute-start(bf16[3,2,2,144,128]{4,3,2,1,0:T(8,128)(2,1)S(1)} %get-tuple-element.6), channel_id=1, source_target_pairs={{2,0},{4,2},{6,4},{7,6},{5,7},{3,5},{1,3},{0,1},{10,8},{12,10},{14... | collective-permute-start | bytes 1327112 | tf_op jit(solution)/shard_map/ppermute | solution.py:124
  17.4 11.4 %collective-permute-start.1 = (bf16[3,2,2,144,128]{4,3,2,1,0:T(8,128)(2,1)S(1)}, bf16[3,2,2,144,128]{4,3,2,1,0:T(8,128)(2,1)S(1)}, u32[]{:S(2)}, u32[]{:S(2)}) collective-permute-start(bf16[3,2,2,144,128]{4,3,2,1,0:T(8,128)(2,1)S(1)} %collective-permute-done), channel_id=1, source_target_pairs={{0,2},{2,4},{4,6},{6,7},{7,5},{5,3},{3,1},{1,0},{8,10},{10,12},{12... | collective-permute-start | bytes 1327112 | tf_op jit(solution)/shard_map/ppermute | solution.py:123
  19.2 11.0 %collective-permute-start.7 = (bf16[3,2,2,144,128]{4,3,2,1,0:T(8,128)(2,1)S(1)}, bf16[3,2,2,144,128]{4,3,2,1,0:T(8,128)(2,1)S(1)}, u32[]{:S(2)}, u32[]{:S(2)}) collective-permute-start(bf16[3,2,2,144,128]{4,3,2,1,0:T(8,128)(2,1)S(1)} %collective-permute-done.6), channel_id=1, source_target_pairs={{2,0},{4,2},{6,4},{7,6},{5,7},{3,5},{1,3},{0,1},{10,8},{12,10},{14... | collective-permute-start | bytes 1327112 | tf_op jit(solution)/shard_map/ppermute | solution.py:124
  19.6 25.7 %collective-permute-start.22 = (bf16[3,8,144,128]{3,2,1,0:T(8,128)(2,1)S(1)}, bf16[3,8,144,128]{3,2,1,0:T(8,128)(2,1)S(1)}, u32[]{:S(2)}, u32[]{:S(2)}) collective-permute-start(bf16[3,8,144,128]{3,2,1,0:T(8,128)(2,1)S(1)} %pad_maximum_fusion.3), channel_id=1, source_target_pairs={{0,8},{1,9},{10,18},{11,19},{20,28},{21,29},{30,6},{31,7}} | collective-permute-start | bytes 2654216 | tf_op jit(solution)/shard_map/ppermute | solution.py:132
  21.0 25.7 %collective-permute-start.21 = (bf16[3,8,144,128]{3,2,1,0:T(8,128)(2,1)S(1)}, bf16[3,8,144,128]{3,2,1,0:T(8,128)(2,1)S(1)}, u32[]{:S(2)}, u32[]{:S(2)}) collective-permute-start(bf16[3,8,144,128]{3,2,1,0:T(8,128)(2,1)S(1)} %pad_maximum_fusion.3), channel_id=1, source_target_pairs={{0,16},{1,17},{10,26},{11,27},{20,4},{21,5},{30,14},{31,15}} | collective-permute-start | bytes 2654216 | tf_op jit(solution)/shard_map/ppermute | solution.py:132
  24.0 22.7 %collective-permute-start.20 = (bf16[3,8,144,128]{3,2,1,0:T(8,128)(2,1)S(1)}, bf16[3,8,144,128]{3,2,1,0:T(8,128)(2,1)S(1)}, u32[]{:S(2)}, u32[]{:S(2)}) collective-permute-start(bf16[3,8,144,128]{3,2,1,0:T(8,128)(2,1)S(1)} %pad_maximum_fusion.3), channel_id=1, source_target_pairs={{0,24},{1,25},{10,2},{11,3},{20,12},{21,13},{30,22},{31,23}} | collective-permute-start | bytes 2654216 | tf_op jit(solution)/shard_map/ppermute | solution.py:132
  28.7 10.4 %collective-permute-start.2 = (bf16[3,2,2,144,128]{4,3,2,1,0:T(8,128)(2,1)S(1)}, bf16[3,2,2,144,128]{4,3,2,1,0:T(8,128)(2,1)S(1)}, u32[]{:S(2)}, u32[]{:S(2)}) collective-permute-start(bf16[3,2,2,144,128]{4,3,2,1,0:T(8,128)(2,1)S(1)} %collective-permute-done.1), channel_id=1, source_target_pairs={{0,2},{2,4},{4,6},{6,7},{7,5},{5,3},{3,1},{1,0},{8,10},{10,12},{12... | collective-permute-start | bytes 1327112 | tf_op jit(solution)/shard_map/ppermute | solution.py:123
  30.2 11.1 %collective-permute-start.8 = (bf16[3,2,2,144,128]{4,3,2,1,0:T(8,128)(2,1)S(1)}, bf16[3,2,2,144,128]{4,3,2,1,0:T(8,128)(2,1)S(1)}, u32[]{:S(2)}, u32[]{:S(2)}) collective-permute-start(bf16[3,2,2,144,128]{4,3,2,1,0:T(8,128)(2,1)S(1)} %collective-permute-done.7), channel_id=1, source_target_pairs={{2,0},{4,2},{6,4},{7,6},{5,7},{3,5},{1,3},{0,1},{10,8},{12,10},{14... | collective-permute-start | bytes 1327112 | tf_op jit(solution)/shard_map/ppermute | solution.py:124
  41.5 37.6 %collective-permute-start.25 = (bf16[3,8,144,128]{3,2,1,0:T(8,128)(2,1)S(1)}, bf16[3,8,144,128]{3,2,1,0:T(8,128)(2,1)S(1)}, u32[]{:S(2)}, u32[]{:S(2)}) collective-permute-start(bf16[3,8,144,128]{3,2,1,0:T(8,128)(2,1)S(1)} %pad_maximum_fusion.4), channel_id=1, source_target_pairs={{0,8},{1,9},{10,18},{11,19},{20,28},{21,29},{30,6},{31,7}} | collective-permute-start | bytes 2654216 | tf_op jit(solution)/shard_map/ppermute | solution.py:132
  42.8 38.5 %collective-permute-start.24 = (bf16[3,8,144,128]{3,2,1,0:T(8,128)(2,1)S(1)}, bf16[3,8,144,128]{3,2,1,0:T(8,128)(2,1)S(1)}, u32[]{:S(2)}, u32[]{:S(2)}) collective-permute-start(bf16[3,8,144,128]{3,2,1,0:T(8,128)(2,1)S(1)} %pad_maximum_fusion.4), channel_id=1, source_target_pairs={{0,16},{1,17},{10,26},{11,27},{20,4},{21,5},{30,14},{31,15}} | collective-permute-start | bytes 2654216 | tf_op jit(solution)/shard_map/ppermute | solution.py:132
  45.3 36.0 %collective-permute-start.23 = (bf16[3,8,144,128]{3,2,1,0:T(8,128)(2,1)S(1)}, bf16[3,8,144,128]{3,2,1,0:T(8,128)(2,1)S(1)}, u32[]{:S(2)}, u32[]{:S(2)}) collective-permute-start(bf16[3,8,144,128]{3,2,1,0:T(8,128)(2,1)S(1)} %pad_maximum_fusion.4), channel_id=1, source_target_pairs={{0,24},{1,25},{10,2},{11,3},{20,12},{21,13},{30,22},{31,23}} | collective-permute-start | bytes 2654216 | tf_op jit(solution)/shard_map/ppermute | solution.py:132
  46.7 9.2 %collective-permute-start.3 = (bf16[3,2,2,144,128]{4,3,2,1,0:T(8,128)(2,1)S(1)}, bf16[3,2,2,144,128]{4,3,2,1,0:T(8,128)(2,1)S(1)}, u32[]{:S(2)}, u32[]{:S(2)}) collective-permute-start(bf16[3,2,2,144,128]{4,3,2,1,0:T(8,128)(2,1)S(1)} %collective-permute-done.2), channel_id=1, source_target_pairs={{0,2},{2,4},{4,6},{6,7},{7,5},{5,3},{3,1},{1,0},{8,10},{10,12},{12... | collective-permute-start | bytes 1327112 | tf_op jit(solution)/shard_map/ppermute | solution.py:123
  46.7 12.0 %collective-permute-start.9 = (bf16[3,2,2,144,128]{4,3,2,1,0:T(8,128)(2,1)S(1)}, bf16[3,2,2,144,128]{4,3,2,1,0:T(8,128)(2,1)S(1)}, u32[]{:S(2)}, u32[]{:S(2)}) collective-permute-start(bf16[3,2,2,144,128]{4,3,2,1,0:T(8,128)(2,1)S(1)} %collective-permute-done.8), channel_id=1, source_target_pairs={{2,0},{4,2},{6,4},{7,6},{5,7},{3,5},{1,3},{0,1},{10,8},{12,10},{14... | collective-permute-start | bytes 1327112 | tf_op jit(solution)/shard_map/ppermute | solution.py:124
  55.8 14.0 %collective-permute-start.4 = (bf16[3,2,2,144,128]{4,3,2,1,0:T(8,128)(2,1)S(1)}, bf16[3,2,2,144,128]{4,3,2,1,0:T(8,128)(2,1)S(1)}, u32[]{:S(2)}, u32[]{:S(2)}) collective-permute-start(bf16[3,2,2,144,128]{4,3,2,1,0:T(8,128)(2,1)S(1)} %collective-permute-done.3), channel_id=1, source_target_pairs={{0,2},{2,4},{4,6},{6,7},{7,5},{5,3},{3,1},{1,0},{8,10},{10,12},{12... | collective-permute-start | bytes 1327112 | tf_op jit(solution)/shard_map/ppermute | solution.py:123
  58.8 13.1 %collective-permute-start.10 = (bf16[3,2,2,144,128]{4,3,2,1,0:T(8,128)(2,1)S(1)}, bf16[3,2,2,144,128]{4,3,2,1,0:T(8,128)(2,1)}, u32[]{:S(2)}, u32[]{:S(2)}) collective-permute-start(bf16[3,2,2,144,128]{4,3,2,1,0:T(8,128)(2,1)S(1)} %collective-permute-done.9), channel_id=1, source_target_pairs={{2,0},{4,2},{6,4},{7,6},{5,7},{3,5},{1,3},{0,1},{10,8},{12,10},{14... | collective-permute-start | bytes 1327112 | tf_op jit(solution)/shard_map/ppermute | solution.py:124
  73.8 37.9 %collective-permute-start.28 = (bf16[3,8,144,128]{3,2,1,0:T(8,128)(2,1)}, bf16[3,8,144,128]{3,2,1,0:T(8,128)(2,1)}, u32[]{:S(2)}, u32[]{:S(2)}) collective-permute-start(bf16[3,8,144,128]{3,2,1,0:T(8,128)(2,1)} %pad_maximum_fusion.5), channel_id=1, source_target_pairs={{0,8},{1,9},{10,18},{11,19},{20,28},{21,29},{30,6},{31,7}} | collective-permute-start | bytes 2654216 | tf_op jit(solution)/shard_map/ppermute | solution.py:132
  76.8 37.1 %collective-permute-start.27 = (bf16[3,8,144,128]{3,2,1,0:T(8,128)(2,1)}, bf16[3,8,144,128]{3,2,1,0:T(8,128)(2,1)}, u32[]{:S(2)}, u32[]{:S(2)}) collective-permute-start(bf16[3,8,144,128]{3,2,1,0:T(8,128)(2,1)} %pad_maximum_fusion.5), channel_id=1, source_target_pairs={{0,16},{1,17},{10,26},{11,27},{20,4},{21,5},{30,14},{31,15}} | collective-permute-start | bytes 2654216 | tf_op jit(solution)/shard_map/ppermute | solution.py:132
  79.1 36.9 %collective-permute-start.26 = (bf16[3,8,144,128]{3,2,1,0:T(8,128)(2,1)}, bf16[3,8,144,128]{3,2,1,0:T(8,128)(2,1)}, u32[]{:S(2)}, u32[]{:S(2)}) collective-permute-start(bf16[3,8,144,128]{3,2,1,0:T(8,128)(2,1)} %pad_maximum_fusion.5), channel_id=1, source_target_pairs={{0,24},{1,25},{10,2},{11,3},{20,12},{21,13},{30,22},{31,23}} | collective-permute-start | bytes 2654216 | tf_op jit(solution)/shard_map/ppermute | solution.py:132
  81.3 9.1 %collective-permute-start.5 = (bf16[3,2,2,144,128]{4,3,2,1,0:T(8,128)(2,1)S(1)}, bf16[3,2,2,144,128]{4,3,2,1,0:T(8,128)(2,1)S(1)}, u32[]{:S(2)}, u32[]{:S(2)}) collective-permute-start(bf16[3,2,2,144,128]{4,3,2,1,0:T(8,128)(2,1)S(1)} %collective-permute-done.4), channel_id=1, source_target_pairs={{0,2},{2,4},{4,6},{6,7},{7,5},{5,3},{3,1},{1,0},{8,10},{10,12},{12... | collective-permute-start | bytes 1327112 | tf_op jit(solution)/shard_map/ppermute | solution.py:123
  81.3 14.5 %collective-permute-start.11 = (bf16[3,2,2,144,128]{4,3,2,1,0:T(8,128)(2,1)}, bf16[3,2,2,144,128]{4,3,2,1,0:T(8,128)(2,1)S(1)}, u32[]{:S(2)}, u32[]{:S(2)}) collective-permute-start(bf16[3,2,2,144,128]{4,3,2,1,0:T(8,128)(2,1)} %collective-permute-done.10), channel_id=1, source_target_pairs={{2,0},{4,2},{6,4},{7,6},{5,7},{3,5},{1,3},{0,1},{10,8},{12,10},{14... | collective-permute-start | bytes 1327112 | tf_op jit(solution)/shard_map/ppermute | solution.py:124
  90.4 27.6 %copy-start.12 = (bf16[3,2,2,144,128]{4,3,2,1,0:T(8,128)(2,1)}, bf16[3,2,2,144,128]{4,3,2,1,0:T(8,128)(2,1)S(1)}, u32[]{:S(2)}) copy-start(bf16[3,2,2,144,128]{4,3,2,1,0:T(8,128)(2,1)S(1)} %collective-permute-done.5) | copy-start | bytes 1327108
  90.4 12.6 %collective-permute-start.12 = (bf16[3,2,2,144,128]{4,3,2,1,0:T(8,128)(2,1)S(1)}, bf16[3,2,2,144,128]{4,3,2,1,0:T(8,128)(2,1)S(1)}, u32[]{:S(2)}, u32[]{:S(2)}) collective-permute-start(bf16[3,2,2,144,128]{4,3,2,1,0:T(8,128)(2,1)S(1)} %collective-permute-done.5), channel_id=1, source_target_pairs={{0,2},{2,4},{4,6},{6,7},{7,5},{5,3},{3,1},{1,0},{8,10},{10,12},{12... | collective-permute-start | bytes 1327112 | tf_op jit(solution)/shard_map/ppermute | solution.py:123
  95.8 22.5 %copy-start.3 = (bf16[3,8,144,128]{3,2,1,0:T(8,128)(2,1)S(1)}, bf16[3,8,144,128]{3,2,1,0:T(8,128)(2,1)}, u32[]{:S(2)}) copy-start(bf16[3,8,144,128]{3,2,1,0:T(8,128)(2,1)} %select_select_fusion.1) | copy-start | bytes 2654212
  95.8 22.2 %copy-start.14 = (bf16[3,2,2,144,128]{4,3,2,1,0:T(8,128)(2,1)}, bf16[3,2,2,144,128]{4,3,2,1,0:T(8,128)(2,1)S(1)}, u32[]{:S(2)}) copy-start(bf16[3,2,2,144,128]{4,3,2,1,0:T(8,128)(2,1)S(1)} %collective-permute-done.11) | copy-start | bytes 1327108
  95.8 13.0 %collective-permute-start.13 = (bf16[3,2,2,144,128]{4,3,2,1,0:T(8,128)(2,1)S(1)}, bf16[3,2,2,144,128]{4,3,2,1,0:T(8,128)(2,1)S(1)}, u32[]{:S(2)}, u32[]{:S(2)}) collective-permute-start(bf16[3,2,2,144,128]{4,3,2,1,0:T(8,128)(2,1)S(1)} %collective-permute-done.11), channel_id=1, source_target_pairs={{2,0},{4,2},{6,4},{7,6},{5,7},{3,5},{1,3},{0,1},{10,8},{12,10},{14... | collective-permute-start | bytes 1327112 | tf_op jit(solution)/shard_map/ppermute | solution.py:124
  103.0 16.8 %collective-permute-start.16 = (bf16[3,4,144,128]{3,2,1,0:T(8,128)(2,1)}, bf16[3,4,144,128]{3,2,1,0:T(8,128)(2,1)}, u32[]{:S(2)}, u32[]{:S(2)}) collective-permute-start(bf16[3,4,144,128]{3,2,1,0:T(8,128)(2,1)} %pad_maximum_fusion.6), channel_id=1, source_target_pairs={{0,8},{1,9},{10,18},{11,19},{20,28},{21,29},{30,6},{31,7}} | collective-permute-start | bytes 1327112 | tf_op jit(solution)/shard_map/ppermute | solution.py:132
  108.8 27.0 %collective-permute-start.15 = (bf16[3,4,144,128]{3,2,1,0:T(8,128)(2,1)}, bf16[3,4,144,128]{3,2,1,0:T(8,128)(2,1)}, u32[]{:S(2)}, u32[]{:S(2)}) collective-permute-start(bf16[3,4,144,128]{3,2,1,0:T(8,128)(2,1)} %pad_maximum_fusion.6), channel_id=1, source_target_pairs={{0,16},{1,17},{10,26},{11,27},{20,4},{21,5},{30,14},{31,15}} | collective-permute-start | bytes 1327112 | tf_op jit(solution)/shard_map/ppermute | solution.py:132
  111.7 24.0 %collective-permute-start.14 = (bf16[3,4,144,128]{3,2,1,0:T(8,128)(2,1)}, bf16[3,4,144,128]{3,2,1,0:T(8,128)(2,1)}, u32[]{:S(2)}, u32[]{:S(2)}) collective-permute-start(bf16[3,4,144,128]{3,2,1,0:T(8,128)(2,1)} %pad_maximum_fusion.6), channel_id=1, source_target_pairs={{0,24},{1,25},{10,2},{11,3},{20,12},{21,13},{30,22},{31,23}} | collective-permute-start | bytes 1327112 | tf_op jit(solution)/shard_map/ppermute | solution.py:132
  113.8 22.1 %collective-permute-start.19 = (bf16[3,4,144,128]{3,2,1,0:T(8,128)(2,1)}, bf16[3,4,144,128]{3,2,1,0:T(8,128)(2,1)}, u32[]{:S(2)}, u32[]{:S(2)}) collective-permute-start(bf16[3,4,144,128]{3,2,1,0:T(8,128)(2,1)} %pad_maximum_fusion.7), channel_id=1, source_target_pairs={{0,8},{1,9},{10,18},{11,19},{20,28},{21,29},{30,6},{31,7}} | collective-permute-start | bytes 1327112 | tf_op jit(solution)/shard_map/ppermute | solution.py:132
  115.9 20.0 %collective-permute-start.18 = (bf16[3,4,144,128]{3,2,1,0:T(8,128)(2,1)}, bf16[3,4,144,128]{3,2,1,0:T(8,128)(2,1)}, u32[]{:S(2)}, u32[]{:S(2)}) collective-permute-start(bf16[3,4,144,128]{3,2,1,0:T(8,128)(2,1)} %pad_maximum_fusion.7), channel_id=1, source_target_pairs={{0,16},{1,17},{10,26},{11,27},{20,4},{21,5},{30,14},{31,15}} | collective-permute-start | bytes 1327112 | tf_op jit(solution)/shard_map/ppermute | solution.py:132
  119.8 16.1 %collective-permute-start.17 = (bf16[3,4,144,128]{3,2,1,0:T(8,128)(2,1)}, bf16[3,4,144,128]{3,2,1,0:T(8,128)(2,1)S(1)}, u32[]{:S(2)}, u32[]{:S(2)}) collective-permute-start(bf16[3,4,144,128]{3,2,1,0:T(8,128)(2,1)} %pad_maximum_fusion.7), channel_id=1, source_target_pairs={{0,24},{1,25},{10,2},{11,3},{20,12},{21,13},{30,22},{31,23}} | collective-permute-start | bytes 1327112 | tf_op jit(solution)/shard_map/ppermute | solution.py:132
  (15 other events, 111.5 us)

commit v12 on v10

--- a/solution.py
+++ b/solution.py
@@ -22,11 +22,11 @@
     stride = local_slots + 1
     for k in range(chunk):
         g = step * chunk + k
-        meta = bs_ref[k, 0, blk : blk + META].astype(jnp.float32)
+        meta = bs_ref[k, local_slots * blk : local_slots * blk + META].astype(jnp.float32)
         w = meta[0:1] + meta[1:2] + meta[2:3]
         lhs = jnp.concatenate(
             [
-                (bs_ref[k, s, :blk].astype(jnp.float32).T * w).astype(jnp.bfloat16)
+                (bs_ref[k, s * blk : (s + 1) * blk].astype(jnp.float32).T * w).astype(jnp.bfloat16)
                 for s in range(local_slots)
             ],
             axis=0,
@@ -38,8 +38,8 @@
             o_ref[pl.ds(row, blk), pl.ds(col, blk)] += prod[s * blk : (s + 1) * blk]
 
 
-def gram_call(offs, bs, bc):
-    n, local_slots, rows, blk = bs.shape
+def gram_call(offs, bs, bc, local_slots):
+    n, rows, blk = bs.shape
     chunk = CHUNK
     kernel = functools.partial(gram_kernel, chunk=chunk, local_slots=local_slots, blk=blk)
     out_rows, out_cols = local_slots * IBS * blk, IBS * blk
@@ -49,8 +49,8 @@
             num_scalar_prefetch=1,
             grid=(n // chunk,),
             in_specs=[
-                pl.BlockSpec((chunk, local_slots, rows, blk), lambda i, o: (i, 0, 0, 0)),
                 pl.BlockSpec((chunk, rows, blk), lambda i, o: (i, 0, 0)),
+                pl.BlockSpec((chunk, blk + META, blk), lambda i, o: (i, 0, 0)),
             ],
             out_specs=pl.BlockSpec((out_rows, out_cols), lambda i, o: (0, 0)),
         ),
@@ -72,13 +72,13 @@
     rest = user_weights - hi
     mid = lax.reduce_precision(rest, exponent_bits=8, mantissa_bits=7)
     low = rest - mid
-    weight_rows = jnp.stack([hi, mid, low], axis=2).astype(jnp.bfloat16)[:, :, None]
-    weight_rows = jnp.broadcast_to(weight_rows, (panels, users, local_slots, 3, blk))
+    weight_rows = jnp.stack([hi, mid, low], axis=2).astype(jnp.bfloat16)
     offset_rows = jnp.broadcast_to(
-        slot_offset.astype(jnp.bfloat16)[..., None, None], (panels, users, local_slots, 1, blk)
+        slot_offset.astype(jnp.bfloat16)[..., None], (panels, users, local_slots, blk)
     )
-    pad = jnp.zeros((panels, users, local_slots, META - 4, blk), jnp.bfloat16)
-    return jnp.concatenate([panel_blocks, weight_rows, offset_rows, pad], axis=3)
+    pad = jnp.zeros((panels, users, META - 3 - local_slots, blk), jnp.bfloat16)
+    data = panel_blocks.reshape(panels, users, local_slots * blk, blk)
+    return jnp.concatenate([data, weight_rows, offset_rows, pad], axis=2)
 
 
 def local(panel_blocks, user_weights, slot_offset, *, nrow, ncol):
@@ -104,7 +104,8 @@
     ]
 
     def pick_slot(piece):
-        return lax.dynamic_index_in_dim(piece, slot, axis=2, keepdims=False)
+        rows = lax.dynamic_slice_in_dim(piece, slot * blk, blk, axis=2)
+        return jnp.concatenate([rows, piece[:, :, local_slots * blk :]], axis=2)
 
     batches = [[k, k + 1] for k in range(0, ncol - 2, 2)] + [[ncol - 2], [ncol - 1]]
     half = x.shape[1] // 2
@@ -127,12 +128,14 @@
     blocks = jnp.concatenate(pieces, axis=1)
     column_blocks = jnp.concatenate(columns, axis=1)
     n = panels * blocks.shape[1]
-    blocks = blocks.reshape(n, local_slots, blk + META, blk)
+    blocks = blocks.reshape(n, local_slots * blk + META, blk)
     column_blocks = column_blocks.reshape(n, blk + META, blk)
 
-    offs = jnp.concatenate([blocks[:, :, blk + 3, 0], column_blocks[:, blk + 3, 0][:, None]], axis=1)
+    w_offs = blocks[:, local_slots * blk + 3 : local_slots * blk + 3 + local_slots, 0]
+    c_offs = lax.dynamic_index_in_dim(column_blocks[:, blk + 3 : blk + 3 + local_slots, 0], slot, axis=1)
+    offs = jnp.concatenate([w_offs, c_offs], axis=1)
     offs = jnp.clip(offs.astype(jnp.int32), 0, IBS - 1).reshape(-1)
-    return gram_call(offs, blocks, column_blocks)
+    return gram_call(offs, blocks, column_blocks, local_slots)
 
 
 def solution(mesh):

time: 135 us -> 147 us (1.089)
  the two profiles are of different devices: /device:TPU:0 before, /device:TPU:24 now
where the time goes in v12:
time: 147 us; the launch traced here: 146 us
  waiting for transfers between devices  76.6 us (52%)
  starting transfers between devices  32.4 us (22%)
  local copies, waits for them, and re-layouts  15.2 us (10%)
  Pallas kernels  14.5 us (10%)
  other arithmetic  6.61 us (4%)
    ppermute x7, waiting for transfers between devices, local(): a = lax.ppermute(a, 'col', forward)  51.8 us
    ppermute x15, waiting for transfers between devices, local(): got = jnp.where(which == j, lax.ppermute(own, ('row', 'col'), fan), got)  20.5 us
    ppermute x15, starting transfers between devices, local(): got = jnp.where(which == j, lax.ppermute(own, ('row', 'col'), fan), got)  17 us
    pallas_call x1, Pallas kernels, gram_call(): pl.pallas_call(kernel, grid_spec=pltpu.PrefetchScalarGridSpec(num_scalar_...  14.5 us
    ppermute x7, starting transfers between devices, local(): a = lax.ppermute(a, 'col', forward)  11.2 us
    ppermute x7, waiting for transfers between devices, local(): b = lax.ppermute(b, 'col', backward)  4.25 us
    ppermute x7, starting transfers between devices, local(): b = lax.ppermute(b, 'col', backward)  4.15 us
    unnamed x68, local copies, waits for them, and re-layouts  3.58 us
  transfers between devices with their start and end apart: 29, of which 13 were waited for; matrix products, arithmetic and copies ran while one was open for 8% of the time, Pallas kernels for 0%

profile of v12, /device:TPU:24, one launch (start us, length us, event | category | flops | bytes accessed | tf_op | source)
XLA Modules:
  0.0 146.3 jit_solution(14287978454932554086)
XLA Ops:
  1.6 3.1 %concatenate.82 = bf16[3,4,272,128]{3,2,1,0:T(8,128)(2,1)S(1)} concatenate(bf16[3,4,256,128]{3,2,1,0:T(8,128)(2,1)} %bitcast.15, bf16[3,4,1,128]{3,2,1,0:T(2,128)(2,1)S(1)} %copy.13, bf16[3,4,1,128]{3,2,1,0:T(2,128)(2,1)S(1)} %copy.14, bf16[3,4,1,128]{3,2,1,0:T(2,128)(2,1)S(1)} %copy.15, bf16[3,4,2,128]{3,2,1,0:T(2,128)(2,1)S(1)} %broadcast_in_dim.4, ...), dimensions={2} | concatenate | bytes 1671168 | tf_op jit(solution)/shard_map/concatenate | solution.py:81
  4.9 1.6 %collective-permute-start = (bf16[3,2,272,128]{3,2,1,0:T(8,128)(2,1)S(1)}, bf16[3,2,272,128]{3,2,1,0:T(8,128)(2,1)S(1)}, u32[]{:S(2)}, u32[]{:S(2)}) collective-permute-start(bf16[3,2,272,128]{3,2,1,0:T(8,128)(2,1)S(1)} %get-tuple-element.5), channel_id=1, source_target_pairs={{0,2},{2,4},{4,6},{6,7},{7,5},{5,3},{3,1},{1,0},{8,10},{10,12},{12... | collective-permute-start | bytes 1253384 | tf_op jit(solution)/shard_map/ppermute | solution.py:116
  7.4 8.9 %collective-permute-done = bf16[3,2,272,128]{3,2,1,0:T(8,128)(2,1)S(1)} collective-permute-done((bf16[3,2,272,128]{3,2,1,0:T(8,128)(2,1)S(1)}, bf16[3,2,272,128]{3,2,1,0:T(8,128)(2,1)S(1)}, u32[]{:S(2)}, u32[]{:S(2)}) %collective-permute-start) | collective-permute-done | bytes 417824 | tf_op jit(solution)/shard_map/ppermute | solution.py:116
  16.3 1.5 %collective-permute-start.2 = (bf16[3,2,272,128]{3,2,1,0:T(8,128)(2,1)S(1)}, bf16[3,2,272,128]{3,2,1,0:T(8,128)(2,1)S(1)}, u32[]{:S(2)}, u32[]{:S(2)}) collective-permute-start(bf16[3,2,272,128]{3,2,1,0:T(8,128)(2,1)S(1)} %collective-permute-done), channel_id=1, source_target_pairs={{0,2},{2,4},{4,6},{6,7},{7,5},{5,3},{3,1},{1,0},{8,10},{10,12},{12... | collective-permute-start | bytes 1253384 | tf_op jit(solution)/shard_map/ppermute | solution.py:116
  20.0 1.3 collective-permute-start.16
  21.4 5.4 %collective-permute-done.2 = bf16[3,2,272,128]{3,2,1,0:T(8,128)(2,1)S(1)} collective-permute-done((bf16[3,2,272,128]{3,2,1,0:T(8,128)(2,1)S(1)}, bf16[3,2,272,128]{3,2,1,0:T(8,128)(2,1)S(1)}, u32[]{:S(2)}, u32[]{:S(2)}) %collective-permute-start.2) | collective-permute-done | bytes 417824 | tf_op jit(solution)/shard_map/ppermute | solution.py:116
  26.8 1.5 %collective-permute-start.4 = (bf16[3,2,272,128]{3,2,1,0:T(8,128)(2,1)S(1)}, bf16[3,2,272,128]{3,2,1,0:T(8,128)(2,1)S(1)}, u32[]{:S(2)}, u32[]{:S(2)}) collective-permute-start(bf16[3,2,272,128]{3,2,1,0:T(8,128)(2,1)S(1)} %collective-permute-done.2), channel_id=1, source_target_pairs={{0,2},{2,4},{4,6},{6,7},{7,5},{5,3},{3,1},{1,0},{8,10},{10,12},{12... | collective-permute-start | bytes 1253384 | tf_op jit(solution)/shard_map/ppermute | solution.py:116
  29.0 7.4 %collective-permute-done.4 = bf16[3,2,272,128]{3,2,1,0:T(8,128)(2,1)S(1)} collective-permute-done((bf16[3,2,272,128]{3,2,1,0:T(8,128)(2,1)S(1)}, bf16[3,2,272,128]{3,2,1,0:T(8,128)(2,1)S(1)}, u32[]{:S(2)}, u32[]{:S(2)}) %collective-permute-start.4) | collective-permute-done | bytes 417824 | tf_op jit(solution)/shard_map/ppermute | solution.py:116
  36.4 1.2 collective-permute-done.5
  39.3 1.3 collective-permute-start.19
  41.2 2.4 %collective-permute-done.16 = bf16[3,8,144,128]{3,2,1,0:T(8,128)(2,1)S(1)} collective-permute-done((bf16[3,8,144,128]{3,2,1,0:T(8,128)(2,1)S(1)}, bf16[3,8,144,128]{3,2,1,0:T(8,128)(2,1)S(1)}, u32[]{:S(2)}, u32[]{:S(2)}) %collective-permute-start.16) | collective-permute-done | bytes 884768 | tf_op jit(solution)/shard_map/ppermute | solution.py:125
  44.0 5.0 %collective-permute-done.6 = bf16[3,2,272,128]{3,2,1,0:T(8,128)(2,1)S(1)} collective-permute-done((bf16[3,2,272,128]{3,2,1,0:T(8,128)(2,1)S(1)}, bf16[3,2,272,128]{3,2,1,0:T(8,128)(2,1)S(1)}, u32[]{:S(2)}, u32[]{:S(2)}) %collective-permute-start.6) | collective-permute-done | bytes 417824 | tf_op jit(solution)/shard_map/ppermute | solution.py:116
  49.1 1.9 %collective-permute-start.8 = (bf16[3,2,272,128]{3,2,1,0:T(8,128)(2,1)S(1)}, bf16[3,2,272,128]{3,2,1,0:T(8,128)(2,1)S(1)}, u32[]{:S(2)}, u32[]{:S(2)}) collective-permute-start(bf16[3,2,272,128]{3,2,1,0:T(8,128)(2,1)S(1)} %collective-permute-done.6), channel_id=1, source_target_pairs={{0,2},{2,4},{4,6},{6,7},{7,5},{5,3},{3,1},{1,0},{8,10},{10,12},{12... | collective-permute-start | bytes 1253384 | tf_op jit(solution)/shard_map/ppermute | solution.py:116
  51.6 2.3 %collective-permute-start.9 = (bf16[3,2,272,128]{3,2,1,0:T(8,128)(2,1)S(1)}, bf16[3,2,272,128]{3,2,1,0:T(8,128)(2,1)S(1)}, u32[]{:S(2)}, u32[]{:S(2)}) collective-permute-start(bf16[3,2,272,128]{3,2,1,0:T(8,128)(2,1)S(1)} %collective-permute-done.7), channel_id=1, source_target_pairs={{2,0},{4,2},{6,4},{7,6},{5,7},{3,5},{1,3},{0,1},{10,8},{12,10},{14... | collective-permute-start | bytes 1253384 | tf_op jit(solution)/shard_map/ppermute | solution.py:117
  54.2 8.9 %collective-permute-done.8 = bf16[3,2,272,128]{3,2,1,0:T(8,128)(2,1)S(1)} collective-permute-done((bf16[3,2,272,128]{3,2,1,0:T(8,128)(2,1)S(1)}, bf16[3,2,272,128]{3,2,1,0:T(8,128)(2,1)S(1)}, u32[]{:S(2)}, u32[]{:S(2)}) %collective-permute-start.8) | collective-permute-done | bytes 417824 | tf_op jit(solution)/shard_map/ppermute | solution.py:116
  64.1 1.6 %collective-permute-start.20 = (bf16[3,8,144,128]{3,2,1,0:T(8,128)(2,1)}, bf16[3,8,144,128]{3,2,1,0:T(8,128)(2,1)}, u32[]{:S(2)}, u32[]{:S(2)}) collective-permute-start(bf16[3,8,144,128]{3,2,1,0:T(8,128)(2,1)} %maximum_maximum_fusion.2), channel_id=1, source_target_pairs={{0,24},{1,25},{10,2},{11,3},{20,12},{21,13},{30,22},{31,23}} | collective-permute-start | bytes 2654216 | tf_op jit(solution)/shard_map/ppermute | solution.py:125
  65.7 1.6 %collective-permute-start.21 = (bf16[3,8,144,128]{3,2,1,0:T(8,128)(2,1)}, bf16[3,8,144,128]{3,2,1,0:T(8,128)(2,1)}, u32[]{:S(2)}, u32[]{:S(2)}) collective-permute-start(bf16[3,8,144,128]{3,2,1,0:T(8,128)(2,1)} %maximum_maximum_fusion.2), channel_id=1, source_target_pairs={{0,16},{1,17},{10,26},{11,27},{20,4},{21,5},{30,14},{31,15}} | collective-permute-start | bytes 2654216 | tf_op jit(solution)/shard_map/ppermute | solution.py:125
  67.6 1.3 collective-permute-start.22
  68.9 2.5 %collective-permute-start.10 = (bf16[3,2,272,128]{3,2,1,0:T(8,128)(2,1)S(1)}, bf16[3,2,272,128]{3,2,1,0:T(8,128)(2,1)S(1)}, u32[]{:S(2)}, u32[]{:S(2)}) collective-permute-start(bf16[3,2,272,128]{3,2,1,0:T(8,128)(2,1)S(1)} %collective-permute-done.8), channel_id=1, source_target_pairs={{0,2},{2,4},{4,6},{6,7},{7,5},{5,3},{3,1},{1,0},{8,10},{10,12},{12... | collective-permute-start | bytes 1253384 | tf_op jit(solution)/shard_map/ppermute | solution.py:116
  71.9 8.1 %collective-permute-done.10 = bf16[3,2,272,128]{3,2,1,0:T(8,128)(2,1)S(1)} collective-permute-done((bf16[3,2,272,128]{3,2,1,0:T(8,128)(2,1)S(1)}, bf16[3,2,272,128]{3,2,1,0:T(8,128)(2,1)S(1)}, u32[]{:S(2)}, u32[]{:S(2)}) %collective-permute-start.10) | collective-permute-done | bytes 417824 | tf_op jit(solution)/shard_map/ppermute | solution.py:116
  79.9 1.8 %collective-permute-start.12 = (bf16[3,2,272,128]{3,2,1,0:T(8,128)(2,1)S(1)}, bf16[3,2,272,128]{3,2,1,0:T(8,128)(2,1)S(1)}, u32[]{:S(2)}, u32[]{:S(2)}) collective-permute-start(bf16[3,2,272,128]{3,2,1,0:T(8,128)(2,1)S(1)} %collective-permute-done.10), channel_id=1, source_target_pairs={{0,2},{2,4},{4,6},{6,7},{7,5},{5,3},{3,1},{1,0},{8,10},{10,12},{12... | collective-permute-start | bytes 1253384 | tf_op jit(solution)/shard_map/ppermute | solution.py:116
  83.1 8.2 %collective-permute-done.12 = bf16[3,2,272,128]{3,2,1,0:T(8,128)(2,1)S(1)} collective-permute-done((bf16[3,2,272,128]{3,2,1,0:T(8,128)(2,1)S(1)}, bf16[3,2,272,128]{3,2,1,0:T(8,128)(2,1)S(1)}, u32[]{:S(2)}, u32[]{:S(2)}) %collective-permute-start.12) | collective-permute-done | bytes 417824 | tf_op jit(solution)/shard_map/ppermute | solution.py:116
  91.3 1.4 collective-permute-start.23
  92.8 2.4 %collective-permute-done.13 = bf16[3,2,272,128]{3,2,1,0:T(8,128)(2,1)S(1)} collective-permute-done((bf16[3,2,272,128]{3,2,1,0:T(8,128)(2,1)S(1)}, bf16[3,2,272,128]{3,2,1,0:T(8,128)(2,1)S(1)}, u32[]{:S(2)}, u32[]{:S(2)}) %collective-permute-start.13) | collective-permute-done | bytes 417824 | tf_op jit(solution)/shard_map/ppermute | solution.py:117
  95.1 1.4 collective-permute-start.24
  96.7 2.7 %copy-done = bf16[3,32,272,128]{3,2,1,0:T(8,128)(2,1)} copy-done((bf16[3,32,272,128]{3,2,1,0:T(8,128)(2,1)}, bf16[3,32,272,128]{3,2,1,0:T(8,128)(2,1)S(1)}, u32[]{:S(2)}) %copy-start) | copy-done | bytes 6684696
  104.6 1.4 collective-permute-start.25
  107.4 1.3 collective-permute-start.28
  108.8 1.7 %select_dynamic-update-slice_fusion = bf16[3,32,144,128]{3,2,1,0:T(8,128)(2,1)S(1)} fusion(bf16[3,32,144,128]{3,2,1,0:T(8,128)(2,1)S(1)} %select_dynamic-update-slice_fusion.1, bf16[3,8,144,128]{3,2,1,0:T(8,128)(2,1)} %collective-permute-done.20, bf16[3,8,144,128]{3,2,1,0:T(8,128)(2,1)} %collective-permute-done.21, ...), kind=kLoop, calls=%fused_computation.3 | loop fusion | flops 8404992 | bytes 4423683
  110.5 9.0 %collective-permute-done.25 = bf16[3,4,144,128]{3,2,1,0:T(8,128)(2,1)S(1)} collective-permute-done((bf16[3,4,144,128]{3,2,1,0:T(8,128)(2,1)}, bf16[3,4,144,128]{3,2,1,0:T(8,128)(2,1)S(1)}, u32[]{:S(2)}, u32[]{:S(2)}) %collective-permute-start.25) | collective-permute-done | bytes 442400 | tf_op jit(solution)/shard_map/ppermute | solution.py:125
  119.8 9.2 %collective-permute-done.28 = bf16[3,4,144,128]{3,2,1,0:T(8,128)(2,1)S(1)} collective-permute-done((bf16[3,4,144,128]{3,2,1,0:T(8,128)(2,1)S(1)}, bf16[3,4,144,128]{3,2,1,0:T(8,128)(2,1)S(1)}, u32[]{:S(2)}, u32[]{:S(2)}) %collective-permute-start.28) | collective-permute-done | bytes 442400 | tf_op jit(solution)/shard_map/ppermute | solution.py:125
  131.8 14.5 %shard_map.37 = f32[2048,1024]{1,0:T(8,128)} custom-call(s32[288]{0:T(512)S(1)} %min.12.offs_ref, bf16[96,272,128]{2,1,0:T(8,128)(2,1)} %bitcast.14, bf16[96,144,128]{2,1,0:T(8,128)(2,1)S(1)} %bitcast.12), custom_call_target="tpu_custom_call" | custom-call | flops 805306368 | bytes 17825792 | tf_op jit(solution)/shard_map/pallas_call | solution.py:46
  (154 shorter events, 21.5 us)
Async XLA Ops:
  4.9 11.4 %collective-permute-start = (bf16[3,2,272,128]{3,2,1,0:T(8,128)(2,1)S(1)}, bf16[3,2,272,128]{3,2,1,0:T(8,128)(2,1)S(1)}, u32[]{:S(2)}, u32[]{:S(2)}) collective-permute-start(bf16[3,2,272,128]{3,2,1,0:T(8,128)(2,1)S(1)} %get-tuple-element.5), channel_id=1, source_target_pairs={{0,2},{2,4},{4,6},{6,7},{7,5},{5,3},{3,1},{1,0},{8,10},{10,12},{12... | collective-permute-start | bytes 1253384 | tf_op jit(solution)/shard_map/ppermute | solution.py:116
  6.4 11.4 %collective-permute-start.1 = (bf16[3,2,272,128]{3,2,1,0:T(8,128)(2,1)S(1)}, bf16[3,2,272,128]{3,2,1,0:T(8,128)(2,1)S(1)}, u32[]{:S(2)}, u32[]{:S(2)}) collective-permute-start(bf16[3,2,272,128]{3,2,1,0:T(8,128)(2,1)S(1)} %get-tuple-element.6), channel_id=1, source_target_pairs={{2,0},{4,2},{6,4},{7,6},{5,7},{3,5},{1,3},{0,1},{10,8},{12,10},{14... | collective-permute-start | bytes 1253384 | tf_op jit(solution)/shard_map/ppermute | solution.py:117
  16.3 10.5 %collective-permute-start.2 = (bf16[3,2,272,128]{3,2,1,0:T(8,128)(2,1)S(1)}, bf16[3,2,272,128]{3,2,1,0:T(8,128)(2,1)S(1)}, u32[]{:S(2)}, u32[]{:S(2)}) collective-permute-start(bf16[3,2,272,128]{3,2,1,0:T(8,128)(2,1)S(1)} %collective-permute-done), channel_id=1, source_target_pairs={{0,2},{2,4},{4,6},{6,7},{7,5},{5,3},{3,1},{1,0},{8,10},{10,12},{12... | collective-permute-start | bytes 1253384 | tf_op jit(solution)/shard_map/ppermute | solution.py:116
  17.8 10.5 %collective-permute-start.3 = (bf16[3,2,272,128]{3,2,1,0:T(8,128)(2,1)S(1)}, bf16[3,2,272,128]{3,2,1,0:T(8,128)(2,1)S(1)}, u32[]{:S(2)}, u32[]{:S(2)}) collective-permute-start(bf16[3,2,272,128]{3,2,1,0:T(8,128)(2,1)S(1)} %collective-permute-done.1), channel_id=1, source_target_pairs={{2,0},{4,2},{6,4},{7,6},{5,7},{3,5},{1,3},{0,1},{10,8},{12,10},{14... | collective-permute-start | bytes 1253384 | tf_op jit(solution)/shard_map/ppermute | solution.py:117
  18.5 20.8 %collective-permute-start.14 = (bf16[3,8,144,128]{3,2,1,0:T(8,128)(2,1)S(1)}, bf16[3,8,144,128]{3,2,1,0:T(8,128)(2,1)S(1)}, u32[]{:S(2)}, u32[]{:S(2)}) collective-permute-start(bf16[3,8,144,128]{3,2,1,0:T(8,128)(2,1)S(1)} %maximum_maximum_fusion), channel_id=1, source_target_pairs={{0,24},{1,25},{10,2},{11,3},{20,12},{21,13},{30,22},{31,23}} | collective-permute-start | bytes 2654216 | tf_op jit(solution)/shard_map/ppermute | solution.py:125
  19.2 21.4 %collective-permute-start.15 = (bf16[3,8,144,128]{3,2,1,0:T(8,128)(2,1)S(1)}, bf16[3,8,144,128]{3,2,1,0:T(8,128)(2,1)S(1)}, u32[]{:S(2)}, u32[]{:S(2)}) collective-permute-start(bf16[3,8,144,128]{3,2,1,0:T(8,128)(2,1)S(1)} %maximum_maximum_fusion), channel_id=1, source_target_pairs={{0,16},{1,17},{10,26},{11,27},{20,4},{21,5},{30,14},{31,15}} | collective-permute-start | bytes 2654216 | tf_op jit(solution)/shard_map/ppermute | solution.py:125
  20.0 23.6 %collective-permute-start.16 = (bf16[3,8,144,128]{3,2,1,0:T(8,128)(2,1)S(1)}, bf16[3,8,144,128]{3,2,1,0:T(8,128)(2,1)S(1)}, u32[]{:S(2)}, u32[]{:S(2)}) collective-permute-start(bf16[3,8,144,128]{3,2,1,0:T(8,128)(2,1)S(1)} %maximum_maximum_fusion), channel_id=1, source_target_pairs={{0,8},{1,9},{10,18},{11,19},{20,28},{21,29},{30,6},{31,7}} | collective-permute-start | bytes 2654216 | tf_op jit(solution)/shard_map/ppermute | solution.py:125
  26.8 9.6 %collective-permute-start.4 = (bf16[3,2,272,128]{3,2,1,0:T(8,128)(2,1)S(1)}, bf16[3,2,272,128]{3,2,1,0:T(8,128)(2,1)S(1)}, u32[]{:S(2)}, u32[]{:S(2)}) collective-permute-start(bf16[3,2,272,128]{3,2,1,0:T(8,128)(2,1)S(1)} %collective-permute-done.2), channel_id=1, source_target_pairs={{0,2},{2,4},{4,6},{6,7},{7,5},{5,3},{3,1},{1,0},{8,10},{10,12},{12... | collective-permute-start | bytes 1253384 | tf_op jit(solution)/shard_map/ppermute | solution.py:116
  28.3 9.3 %collective-permute-start.5 = (bf16[3,2,272,128]{3,2,1,0:T(8,128)(2,1)S(1)}, bf16[3,2,272,128]{3,2,1,0:T(8,128)(2,1)S(1)}, u32[]{:S(2)}, u32[]{:S(2)}) collective-permute-start(bf16[3,2,272,128]{3,2,1,0:T(8,128)(2,1)S(1)} %collective-permute-done.3), channel_id=1, source_target_pairs={{2,0},{4,2},{6,4},{7,6},{5,7},{3,5},{1,3},{0,1},{10,8},{12,10},{14... | collective-permute-start | bytes 1253384 | tf_op jit(solution)/shard_map/ppermute | solution.py:117
  37.8 29.8 %collective-permute-start.17 = (bf16[3,8,144,128]{3,2,1,0:T(8,128)(2,1)S(1)}, bf16[3,8,144,128]{3,2,1,0:T(8,128)(2,1)S(1)}, u32[]{:S(2)}, u32[]{:S(2)}) collective-permute-start(bf16[3,8,144,128]{3,2,1,0:T(8,128)(2,1)S(1)} %maximum_maximum_fusion.1), channel_id=1, source_target_pairs={{0,24},{1,25},{10,2},{11,3},{20,12},{21,13},{30,22},{31,23}} | collective-permute-start | bytes 2654216 | tf_op jit(solution)/shard_map/ppermute | solution.py:125
  38.5 30.4 %collective-permute-start.18 = (bf16[3,8,144,128]{3,2,1,0:T(8,128)(2,1)S(1)}, bf16[3,8,144,128]{3,2,1,0:T(8,128)(2,1)S(1)}, u32[]{:S(2)}, u32[]{:S(2)}) collective-permute-start(bf16[3,8,144,128]{3,2,1,0:T(8,128)(2,1)S(1)} %maximum_maximum_fusion.1), channel_id=1, source_target_pairs={{0,16},{1,17},{10,26},{11,27},{20,4},{21,5},{30,14},{31,15}} | collective-permute-start | bytes 2654216 | tf_op jit(solution)/shard_map/ppermute | solution.py:125
  39.3 32.0 %collective-permute-start.19 = (bf16[3,8,144,128]{3,2,1,0:T(8,128)(2,1)S(1)}, bf16[3,8,144,128]{3,2,1,0:T(8,128)(2,1)S(1)}, u32[]{:S(2)}, u32[]{:S(2)}) collective-permute-start(bf16[3,8,144,128]{3,2,1,0:T(8,128)(2,1)S(1)} %maximum_maximum_fusion.1), channel_id=1, source_target_pairs={{0,8},{1,9},{10,18},{11,19},{20,28},{21,29},{30,6},{31,7}} | collective-permute-start | bytes 2654216 | tf_op jit(solution)/shard_map/ppermute | solution.py:125
  40.7 8.4 %collective-permute-start.6 = (bf16[3,2,272,128]{3,2,1,0:T(8,128)(2,1)S(1)}, bf16[3,2,272,128]{3,2,1,0:T(8,128)(2,1)S(1)}, u32[]{:S(2)}, u32[]{:S(2)}) collective-permute-start(bf16[3,2,272,128]{3,2,1,0:T(8,128)(2,1)S(1)} %collective-permute-done.4), channel_id=1, source_target_pairs={{0,2},{2,4},{4,6},{6,7},{7,5},{5,3},{3,1},{1,0},{8,10},{10,12},{12... | collective-permute-start | bytes 1253384 | tf_op jit(solution)/shard_map/ppermute | solution.py:116
  43.6 8.0 %collective-permute-start.7 = (bf16[3,2,272,128]{3,2,1,0:T(8,128)(2,1)S(1)}, bf16[3,2,272,128]{3,2,1,0:T(8,128)(2,1)S(1)}, u32[]{:S(2)}, u32[]{:S(2)}) collective-permute-start(bf16[3,2,272,128]{3,2,1,0:T(8,128)(2,1)S(1)} %collective-permute-done.5), channel_id=1, source_target_pairs={{2,0},{4,2},{6,4},{7,6},{5,7},{3,5},{1,3},{0,1},{10,8},{12,10},{14... | collective-permute-start | bytes 1253384 | tf_op jit(solution)/shard_map/ppermute | solution.py:117
  49.1 13.9 %collective-permute-start.8 = (bf16[3,2,272,128]{3,2,1,0:T(8,128)(2,1)S(1)}, bf16[3,2,272,128]{3,2,1,0:T(8,128)(2,1)S(1)}, u32[]{:S(2)}, u32[]{:S(2)}) collective-permute-start(bf16[3,2,272,128]{3,2,1,0:T(8,128)(2,1)S(1)} %collective-permute-done.6), channel_id=1, source_target_pairs={{0,2},{2,4},{4,6},{6,7},{7,5},{5,3},{3,1},{1,0},{8,10},{10,12},{12... | collective-permute-start | bytes 1253384 | tf_op jit(solution)/shard_map/ppermute | solution.py:116
  51.6 11.4 %collective-permute-start.9 = (bf16[3,2,272,128]{3,2,1,0:T(8,128)(2,1)S(1)}, bf16[3,2,272,128]{3,2,1,0:T(8,128)(2,1)S(1)}, u32[]{:S(2)}, u32[]{:S(2)}) collective-permute-start(bf16[3,2,272,128]{3,2,1,0:T(8,128)(2,1)S(1)} %collective-permute-done.7), channel_id=1, source_target_pairs={{2,0},{4,2},{6,4},{7,6},{5,7},{3,5},{1,3},{0,1},{10,8},{12,10},{14... | collective-permute-start | bytes 1253384 | tf_op jit(solution)/shard_map/ppermute | solution.py:117
  64.1 41.9 %collective-permute-start.20 = (bf16[3,8,144,128]{3,2,1,0:T(8,128)(2,1)}, bf16[3,8,144,128]{3,2,1,0:T(8,128)(2,1)}, u32[]{:S(2)}, u32[]{:S(2)}) collective-permute-start(bf16[3,8,144,128]{3,2,1,0:T(8,128)(2,1)} %maximum_maximum_fusion.2), channel_id=1, source_target_pairs={{0,24},{1,25},{10,2},{11,3},{20,12},{21,13},{30,22},{31,23}} | collective-permute-start | bytes 2654216 | tf_op jit(solution)/shard_map/ppermute | solution.py:125
  65.7 41.0 %collective-permute-start.21 = (bf16[3,8,144,128]{3,2,1,0:T(8,128)(2,1)}, bf16[3,8,144,128]{3,2,1,0:T(8,128)(2,1)}, u32[]{:S(2)}, u32[]{:S(2)}) collective-permute-start(bf16[3,8,144,128]{3,2,1,0:T(8,128)(2,1)} %maximum_maximum_fusion.2), channel_id=1, source_target_pairs={{0,16},{1,17},{10,26},{11,27},{20,4},{21,5},{30,14},{31,15}} | collective-permute-start | bytes 2654216 | tf_op jit(solution)/shard_map/ppermute | solution.py:125
  67.6 39.8 %collective-permute-start.22 = (bf16[3,8,144,128]{3,2,1,0:T(8,128)(2,1)}, bf16[3,8,144,128]{3,2,1,0:T(8,128)(2,1)}, u32[]{:S(2)}, u32[]{:S(2)}) collective-permute-start(bf16[3,8,144,128]{3,2,1,0:T(8,128)(2,1)} %maximum_maximum_fusion.2), channel_id=1, source_target_pairs={{0,8},{1,9},{10,18},{11,19},{20,28},{21,29},{30,6},{31,7}} | collective-permute-start | bytes 2654216 | tf_op jit(solution)/shard_map/ppermute | solution.py:125
  68.9 11.1 %collective-permute-start.10 = (bf16[3,2,272,128]{3,2,1,0:T(8,128)(2,1)S(1)}, bf16[3,2,272,128]{3,2,1,0:T(8,128)(2,1)S(1)}, u32[]{:S(2)}, u32[]{:S(2)}) collective-permute-start(bf16[3,2,272,128]{3,2,1,0:T(8,128)(2,1)S(1)} %collective-permute-done.8), channel_id=1, source_target_pairs={{0,2},{2,4},{4,6},{6,7},{7,5},{5,3},{3,1},{1,0},{8,10},{10,12},{12... | collective-permute-start | bytes 1253384 | tf_op jit(solution)/shard_map/ppermute | solution.py:116
  71.3 10.5 %collective-permute-start.11 = (bf16[3,2,272,128]{3,2,1,0:T(8,128)(2,1)S(1)}, bf16[3,2,272,128]{3,2,1,0:T(8,128)(2,1)S(1)}, u32[]{:S(2)}, u32[]{:S(2)}) collective-permute-start(bf16[3,2,272,128]{3,2,1,0:T(8,128)(2,1)S(1)} %collective-permute-done.9), channel_id=1, source_target_pairs={{2,0},{4,2},{6,4},{7,6},{5,7},{3,5},{1,3},{0,1},{10,8},{12,10},{14... | collective-permute-start | bytes 1253384 | tf_op jit(solution)/shard_map/ppermute | solution.py:117
  79.9 11.3 %collective-permute-start.12 = (bf16[3,2,272,128]{3,2,1,0:T(8,128)(2,1)S(1)}, bf16[3,2,272,128]{3,2,1,0:T(8,128)(2,1)S(1)}, u32[]{:S(2)}, u32[]{:S(2)}) collective-permute-start(bf16[3,2,272,128]{3,2,1,0:T(8,128)(2,1)S(1)} %collective-permute-done.10), channel_id=1, source_target_pairs={{0,2},{2,4},{4,6},{6,7},{7,5},{5,3},{3,1},{1,0},{8,10},{10,12},{12... | collective-permute-start | bytes 1253384 | tf_op jit(solution)/shard_map/ppermute | solution.py:116
  81.8 13.3 %collective-permute-start.13 = (bf16[3,2,272,128]{3,2,1,0:T(8,128)(2,1)S(1)}, bf16[3,2,272,128]{3,2,1,0:T(8,128)(2,1)S(1)}, u32[]{:S(2)}, u32[]{:S(2)}) collective-permute-start(bf16[3,2,272,128]{3,2,1,0:T(8,128)(2,1)S(1)} %collective-permute-done.11), channel_id=1, source_target_pairs={{2,0},{4,2},{6,4},{7,6},{5,7},{3,5},{1,3},{0,1},{10,8},{12,10},{14... | collective-permute-start | bytes 1253384 | tf_op jit(solution)/shard_map/ppermute | solution.py:117
  91.3 13.3 %collective-permute-start.23 = (bf16[3,4,144,128]{3,2,1,0:T(8,128)(2,1)}, bf16[3,4,144,128]{3,2,1,0:T(8,128)(2,1)}, u32[]{:S(2)}, u32[]{:S(2)}) collective-permute-start(bf16[3,4,144,128]{3,2,1,0:T(8,128)(2,1)} %maximum_maximum_fusion.3), channel_id=1, source_target_pairs={{0,24},{1,25},{10,2},{11,3},{20,12},{21,13},{30,22},{31,23}} | collective-permute-start | bytes 1327112 | tf_op jit(solution)/shard_map/ppermute | solution.py:125
  95.1 15.4 %collective-permute-start.24 = (bf16[3,4,144,128]{3,2,1,0:T(8,128)(2,1)}, bf16[3,4,144,128]{3,2,1,0:T(8,128)(2,1)}, u32[]{:S(2)}, u32[]{:S(2)}) collective-permute-start(bf16[3,4,144,128]{3,2,1,0:T(8,128)(2,1)} %maximum_maximum_fusion.3), channel_id=1, source_target_pairs={{0,16},{1,17},{10,26},{11,27},{20,4},{21,5},{30,14},{31,15}} | collective-permute-start | bytes 1327112 | tf_op jit(solution)/shard_map/ppermute | solution.py:125
  104.5 14.9 %copy-start.10 = (bf16[3,2,128,128]{3,2,1,0:T(8,128)(2,1)S(1)}, bf16[3,2,128,128]{3,2,1,0:T(8,128)(2,1)}, u32[]{:S(2)}) copy-start(bf16[3,2,128,128]{3,2,1,0:T(8,128)(2,1)} %copy-done.9) | copy-start | bytes 589828
  104.5 14.9 %copy-start.12 = (bf16[3,2,128,128]{3,2,1,0:T(8,128)(2,1)S(1)}, bf16[3,2,128,128]{3,2,1,0:T(8,128)(2,1)}, u32[]{:S(2)}) copy-start(bf16[3,2,128,128]{3,2,1,0:T(8,128)(2,1)} %copy-done.11) | copy-start | bytes 589828
  104.5 14.9 %copy-start.24 = (bf16[3,2,16,128]{3,2,1,0:T(8,128)(2,1)S(1)}, bf16[3,2,16,128]{3,2,1,0:T(8,128)(2,1)}, u32[]{:S(2)}) copy-start(bf16[3,2,16,128]{3,2,1,0:T(8,128)(2,1)} %copy-done.23) | copy-start | bytes 73732
  104.6 14.9 %collective-permute-start.25 = (bf16[3,4,144,128]{3,2,1,0:T(8,128)(2,1)}, bf16[3,4,144,128]{3,2,1,0:T(8,128)(2,1)S(1)}, u32[]{:S(2)}, u32[]{:S(2)}) collective-permute-start(bf16[3,4,144,128]{3,2,1,0:T(8,128)(2,1)} %maximum_maximum_fusion.3), channel_id=1, source_target_pairs={{0,8},{1,9},{10,18},{11,19},{20,28},{21,29},{30,6},{31,7}} | collective-permute-start | bytes 1327112 | tf_op jit(solution)/shard_map/ppermute | solution.py:125
  106.0 13.8 %collective-permute-start.26 = (bf16[3,4,144,128]{3,2,1,0:T(8,128)(2,1)S(1)}, bf16[3,4,144,128]{3,2,1,0:T(8,128)(2,1)S(1)}, u32[]{:S(2)}, u32[]{:S(2)}) collective-permute-start(bf16[3,4,144,128]{3,2,1,0:T(8,128)(2,1)S(1)} %maximum_maximum_fusion.4), channel_id=1, source_target_pairs={{0,24},{1,25},{10,2},{11,3},{20,12},{21,13},{30,22},{31,23}} | collective-permute-start | bytes 1327112 | tf_op jit(solution)/shard_map/ppermute | solution.py:125
  106.7 13.1 %collective-permute-start.27 = (bf16[3,4,144,128]{3,2,1,0:T(8,128)(2,1)S(1)}, bf16[3,4,144,128]{3,2,1,0:T(8,128)(2,1)S(1)}, u32[]{:S(2)}, u32[]{:S(2)}) collective-permute-start(bf16[3,4,144,128]{3,2,1,0:T(8,128)(2,1)S(1)} %maximum_maximum_fusion.4), channel_id=1, source_target_pairs={{0,16},{1,17},{10,26},{11,27},{20,4},{21,5},{30,14},{31,15}} | collective-permute-start | bytes 1327112 | tf_op jit(solution)/shard_map/ppermute | solution.py:125
  107.4 21.5 %collective-permute-start.28 = (bf16[3,4,144,128]{3,2,1,0:T(8,128)(2,1)S(1)}, bf16[3,4,144,128]{3,2,1,0:T(8,128)(2,1)S(1)}, u32[]{:S(2)}, u32[]{:S(2)}) collective-permute-start(bf16[3,4,144,128]{3,2,1,0:T(8,128)(2,1)S(1)} %maximum_maximum_fusion.4), channel_id=1, source_target_pairs={{0,8},{1,9},{10,18},{11,19},{20,28},{21,29},{30,6},{31,7}} | collective-permute-start | bytes 1327112 | tf_op jit(solution)/shard_map/ppermute | solution.py:125
  (24 other events, 210.2 us)

commit v13 on v10

--- a/solution.py
+++ b/solution.py
@@ -130,7 +130,9 @@
     blocks = blocks.reshape(n, local_slots, blk + META, blk)
     column_blocks = column_blocks.reshape(n, blk + META, blk)
 
-    offs = jnp.concatenate([blocks[:, :, blk + 3, 0], column_blocks[:, blk + 3, 0][:, None]], axis=1)
+    w_offs = jnp.concatenate([piece[:, :, :, blk + 3, 0] for piece in pieces], axis=1)
+    c_offs = jnp.concatenate([got[:, :, blk + 3, 0] for got in columns], axis=1)
+    offs = jnp.concatenate([w_offs, c_offs[..., None]], axis=2)
     offs = jnp.clip(offs.astype(jnp.int32), 0, IBS - 1).reshape(-1)
     return gram_call(offs, blocks, column_blocks)
 

time: 135 us -> 180 us (1.33)
  the two profiles are of different devices: /device:TPU:0 before, /device:TPU:14 now
where the time goes in v13:
time: 180 us; the launch traced here: 178 us
  local copies, waits for them, and re-layouts  60.3 us (34%)
  waiting for transfers between devices  52.3 us (29%)
  starting transfers between devices  37.1 us (21%)
  Pallas kernels  14.6 us (8%)
  other arithmetic  13.2 us (7%)
    ppermute x7, waiting for transfers between devices, local(): b = lax.ppermute(b, 'col', backward)  22.3 us
    unnamed x55, local copies, waits for them, and re-layouts  20.2 us
    ppermute x15, starting transfers between devices, local(): got = jnp.where(which == j, lax.ppermute(own, ('row', 'col'), fan), got)  19.4 us
    ppermute x7, waiting for transfers between devices, local(): a = lax.ppermute(a, 'col', forward)  16.3 us
    ppermute x7, starting transfers between devices, local(): b = lax.ppermute(b, 'col', backward)  15.1 us
    pallas_call x1, Pallas kernels, gram_call(): pl.pallas_call(kernel, grid_spec=pltpu.PrefetchScalarGridSpec(num_scalar_...  14.6 us
    ppermute x15, waiting for transfers between devices, local(): got = jnp.where(which == j, lax.ppermute(own, ('row', 'col'), fan), got)  13.7 us
    squeeze x14, local copies, waits for them, and re-layouts, local(): piece[:, :, :, blk + 3, 0]  9.66 us
  transfers between devices with their start and end apart: 29, of which 12 were waited for; matrix products, arithmetic and copies ran while one was open for 37% of the time, Pallas kernels for 0%

profile of v13, /device:TPU:14, one launch (start us, length us, event | category | flops | bytes accessed | tf_op | source)
XLA Modules:
  0.0 178.0 jit_solution(1787925194640858742)
XLA Ops:
  1.6 2.4 %constant_dynamic-update-slice_fusion.14 = (bf16[3,32,2,144,128]{4,3,1,0,2:T(8,128)(2,1)}, bf16[3,4,2,144,128]{4,3,1,0,2:T(8,128)(2,1)S(1)}) fusion(bf16[144]{0:T(256)(128)(2,1)S(1)} %pad.25.clone, bf16[3,4,2,1,128]{4,3,1,0,2:T(2,128)(2,1)S(1)} %broadcast_in_dim.9, bf16[3,4,2,3,128]{4,3,1,0,2:T(4,128)(2,1)S(1)} %broadcast_in_dim.8, ...), kind=kLoop, calls=%fused_computation.41 | loop fusion | flops 3538943 | bytes 2580768
  6.2 9.8 %collective-permute-done.1 = bf16[3,2,2,144,128]{4,3,1,0,2:T(8,128)(2,1)S(1)} collective-permute-done((bf16[3,2,2,144,128]{4,3,1,0,2:T(8,128)(2,1)S(1)}, bf16[3,2,2,144,128]{4,3,1,0,2:T(8,128)(2,1)S(1)}, u32[]{:S(2)}, u32[]{:S(2)}) %collective-permute-start.1) | collective-permute-done | bytes 442400 | tf_op jit(solution)/shard_map/ppermute | solution.py:116
  25.0 2.1 %collective-permute-done.3 = bf16[3,2,2,144,128]{4,3,1,0,2:T(8,128)(2,1)S(1)} collective-permute-done((bf16[3,2,2,144,128]{4,3,1,0,2:T(8,128)(2,1)S(1)}, bf16[3,2,2,144,128]{4,3,1,0,2:T(8,128)(2,1)S(1)}, u32[]{:S(2)}, u32[]{:S(2)}) %collective-permute-start.3) | collective-permute-done | bytes 442400 | tf_op jit(solution)/shard_map/ppermute | solution.py:116
  27.1 2.2 %collective-permute-start.5 = (bf16[3,2,2,144,128]{4,3,1,0,2:T(8,128)(2,1)S(1)}, bf16[3,2,2,144,128]{4,3,1,0,2:T(8,128)(2,1)}, u32[]{:S(2)}, u32[]{:S(2)}) collective-permute-start(bf16[3,2,2,144,128]{4,3,1,0,2:T(8,128)(2,1)S(1)} %collective-permute-done.3), channel_id=1, source_target_pairs={{2,0},{4,2},{6,4},{7,6},{5,7},{3,5},{1,3},{0,1},{10,8},{12,10},{14... | collective-permute-start | bytes 1327112 | tf_op jit(solution)/shard_map/ppermute | solution.py:116
  32.5 4.8 %collective-permute-done.5 = bf16[3,2,2,144,128]{4,3,1,0,2:T(8,128)(2,1)} collective-permute-done((bf16[3,2,2,144,128]{4,3,1,0,2:T(8,128)(2,1)S(1)}, bf16[3,2,2,144,128]{4,3,1,0,2:T(8,128)(2,1)}, u32[]{:S(2)}, u32[]{:S(2)}) %collective-permute-start.5) | collective-permute-done | bytes 442400 | tf_op jit(solution)/shard_map/ppermute | solution.py:116
  38.2 3.4 %collective-permute-done.4 = bf16[3,2,2,144,128]{4,3,1,0,2:T(8,128)(2,1)} collective-permute-done((bf16[3,2,2,144,128]{4,3,1,0,2:T(8,128)(2,1)S(1)}, bf16[3,2,2,144,128]{4,3,1,0,2:T(8,128)(2,1)}, u32[]{:S(2)}, u32[]{:S(2)}) %collective-permute-start.4) | collective-permute-done | bytes 442400 | tf_op jit(solution)/shard_map/ppermute | solution.py:115
  46.8 1.9 %constant_dynamic-update-slice_fusion.9 = bf16[3,32,2,144,128]{4,3,1,0,2:T(8,128)(2,1)} fusion(bf16[3,32,2,144,128]{4,3,1,0,2:T(8,128)(2,1)} %constant_dynamic-update-slice_fusion.10, bf16[3,2,2,144,128]{4,3,1,0,2:T(8,128)(2,1)} %collective-permute-done.4), kind=kLoop, calls=%fused_computation.36 | loop fusion | bytes 884736
  48.6 1.9 %constant_dynamic-update-slice_fusion.8 = bf16[3,32,2,144,128]{4,3,1,0,2:T(8,128)(2,1)} fusion(bf16[3,32,2,144,128]{4,3,1,0,2:T(8,128)(2,1)} %constant_dynamic-update-slice_fusion.9, bf16[3,2,2,144,128]{4,3,1,0,2:T(8,128)(2,1)} %collective-permute-done.5), kind=kLoop, calls=%fused_computation.35 | loop fusion | bytes 884736
  51.8 3.9 %collective-permute-start.7 = (bf16[3,2,2,144,128]{4,3,1,0,2:T(8,128)(2,1)}, bf16[3,2,2,144,128]{4,3,1,0,2:T(8,128)(2,1)}, u32[]{:S(2)}, u32[]{:S(2)}) collective-permute-start(bf16[3,2,2,144,128]{4,3,1,0,2:T(8,128)(2,1)} %collective-permute-done.5), channel_id=1, source_target_pairs={{2,0},{4,2},{6,4},{7,6},{5,7},{3,5},{1,3},{0,1},{10,8},{12,10},{14... | collective-permute-start | bytes 1327112 | tf_op jit(solution)/shard_map/ppermute | solution.py:116
  55.8 1.9 %constant_dynamic-update-slice_fusion.19 = (bf16[3,32,144,128]{3,2,1,0:T(8,128)(2,1)S(1)}, bf16[3,8,144,128]{3,2,1,0:T(8,128)(2,1)S(1)}) fusion(bf16[3,8,144,128]{3,2,1,0:T(8,128)(2,1)} %copy-done.18, bf16[3,8,144,128]{3,2,1,0:T(8,128)(2,1)} %collective-permute-done.15, bf16[3,8,144,128]{3,2,1,0:T(8,128)(2,1)} %collective-permute-done.16, ...), kind=kLoop, calls=%fused_computation.46 | loop fusion | flops 4866047 | bytes 5308419
  61.4 6.7 %collective-permute-done.6 = bf16[3,2,2,144,128]{4,3,1,0,2:T(8,128)(2,1)} collective-permute-done((bf16[3,2,2,144,128]{4,3,1,0,2:T(8,128)(2,1)}, bf16[3,2,2,144,128]{4,3,1,0,2:T(8,128)(2,1)}, u32[]{:S(2)}, u32[]{:S(2)}) %collective-permute-start.6) | collective-permute-done | bytes 442400 | tf_op jit(solution)/shard_map/ppermute | solution.py:115
  74.9 1.9 %constant_dynamic-update-slice_fusion.7 = bf16[3,32,2,144,128]{4,3,1,0,2:T(8,128)(2,1)} fusion(bf16[3,32,2,144,128]{4,3,1,0,2:T(8,128)(2,1)} %constant_dynamic-update-slice_fusion.8, bf16[3,2,2,144,128]{4,3,1,0,2:T(8,128)(2,1)} %collective-permute-done.6), kind=kLoop, calls=%fused_computation.34 | loop fusion | bytes 884736
  76.9 1.9 %constant_dynamic-update-slice_fusion.6 = bf16[3,32,2,144,128]{4,3,1,0,2:T(8,128)(2,1)} fusion(bf16[3,32,2,144,128]{4,3,1,0,2:T(8,128)(2,1)} %constant_dynamic-update-slice_fusion.7, bf16[3,2,2,144,128]{4,3,1,0,2:T(8,128)(2,1)} %collective-permute-done.7), kind=kLoop, calls=%fused_computation.33 | loop fusion | bytes 884736
  78.7 3.5 %collective-permute-done.9 = bf16[3,2,2,144,128]{4,3,1,0,2:T(8,128)(2,1)S(1)} collective-permute-done((bf16[3,2,2,144,128]{4,3,1,0,2:T(8,128)(2,1)}, bf16[3,2,2,144,128]{4,3,1,0,2:T(8,128)(2,1)S(1)}, u32[]{:S(2)}, u32[]{:S(2)}) %collective-permute-start.9) | collective-permute-done | bytes 442400 | tf_op jit(solution)/shard_map/ppermute | solution.py:116
  84.9 1.6 collective-permute-start.20
  86.6 1.7 collective-permute-start.21
  91.7 3.2 %collective-permute-start.11 = (bf16[3,2,2,144,128]{4,3,1,0,2:T(8,128)(2,1)}, bf16[3,2,2,144,128]{4,3,1,0,2:T(8,128)(2,1)}, u32[]{:S(2)}, u32[]{:S(2)}) collective-permute-start(bf16[3,2,2,144,128]{4,3,1,0,2:T(8,128)(2,1)} %copy-done.17), channel_id=1, source_target_pairs={{2,0},{4,2},{6,4},{7,6},{5,7},{3,5},{1,3},{0,1},{10,8},{12,10},{14... | collective-permute-start | bytes 1327112 | tf_op jit(solution)/shard_map/ppermute | solution.py:116
  94.9 1.9 %constant_dynamic-update-slice_fusion.18 = (bf16[3,32,144,128]{3,2,1,0:T(8,128)(2,1)S(1)}, bf16[3,8,144,128]{3,2,1,0:T(8,128)(2,1)S(1)}) fusion(bf16[3,32,144,128]{3,2,1,0:T(8,128)(2,1)S(1)} %get-tuple-element.13, bf16[3,8,144,128]{3,2,1,0:T(8,128)(2,1)} %collective-permute-done.17, bf16[3,8,144,128]{3,2,1,0:T(8,128)(2,1)} %collective-permute-done.18, ...), kind=kLoop, calls=%fused_computation.45 | loop fusion | flops 4866048 | bytes 5308419
  97.6 1.9 %constant_dynamic-update-slice_fusion.5 = bf16[3,32,2,144,128]{4,3,1,0,2:T(8,128)(2,1)} fusion(bf16[3,32,2,144,128]{4,3,1,0,2:T(8,128)(2,1)} %constant_dynamic-update-slice_fusion.6, bf16[3,2,2,144,128]{4,3,1,0,2:T(8,128)(2,1)} %copy-done.16), kind=kLoop, calls=%fused_computation.32 | loop fusion | bytes 884736
  99.4 1.9 %constant_dynamic-update-slice_fusion.4 = bf16[3,32,2,144,128]{4,3,1,0,2:T(8,128)(2,1)} fusion(bf16[3,32,2,144,128]{4,3,1,0,2:T(8,128)(2,1)} %constant_dynamic-update-slice_fusion.5, bf16[3,2,2,144,128]{4,3,1,0,2:T(8,128)(2,1)} %copy-done.17), kind=kLoop, calls=%fused_computation.31 | loop fusion | bytes 884736
  101.3 2.1 %collective-permute-done.11 = bf16[3,2,2,144,128]{4,3,1,0,2:T(8,128)(2,1)} collective-permute-done((bf16[3,2,2,144,128]{4,3,1,0,2:T(8,128)(2,1)}, bf16[3,2,2,144,128]{4,3,1,0,2:T(8,128)(2,1)}, u32[]{:S(2)}, u32[]{:S(2)}) %collective-permute-start.11) | collective-permute-done | bytes 442400 | tf_op jit(solution)/shard_map/ppermute | solution.py:116
  103.4 2.1 %collective-permute-start.13 = (bf16[3,2,2,144,128]{4,3,1,0,2:T(8,128)(2,1)}, bf16[3,2,2,144,128]{4,3,1,0,2:T(8,128)(2,1)}, u32[]{:S(2)}, u32[]{:S(2)}) collective-permute-start(bf16[3,2,2,144,128]{4,3,1,0,2:T(8,128)(2,1)} %collective-permute-done.11), channel_id=1, source_target_pairs={{2,0},{4,2},{6,4},{7,6},{5,7},{3,5},{1,3},{0,1},{10,8},{12,10},{14... | collective-permute-start | bytes 1327112 | tf_op jit(solution)/shard_map/ppermute | solution.py:116
  111.4 1.9 %constant_dynamic-update-slice_fusion.3 = bf16[3,32,2,144,128]{4,3,1,0,2:T(8,128)(2,1)} fusion(bf16[3,32,2,144,128]{4,3,1,0,2:T(8,128)(2,1)} %constant_dynamic-update-slice_fusion.4, bf16[3,2,2,144,128]{4,3,1,0,2:T(8,128)(2,1)} %collective-permute-done.10), kind=kLoop, calls=%fused_computation.30 | loop fusion | bytes 884736
  113.2 1.9 %constant_dynamic-update-slice_fusion.2 = bf16[3,32,2,144,128]{4,3,1,0,2:T(8,128)(2,1)} fusion(bf16[3,32,2,144,128]{4,3,1,0,2:T(8,128)(2,1)} %constant_dynamic-update-slice_fusion.3, bf16[3,2,2,144,128]{4,3,1,0,2:T(8,128)(2,1)} %collective-permute-done.11), kind=kLoop, calls=%fused_computation.29 | loop fusion | bytes 884736
  115.1 4.5 %collective-permute-done.12 = bf16[3,2,2,144,128]{4,3,1,0,2:T(8,128)(2,1)} collective-permute-done((bf16[3,2,2,144,128]{4,3,1,0,2:T(8,128)(2,1)}, bf16[3,2,2,144,128]{4,3,1,0,2:T(8,128)(2,1)}, u32[]{:S(2)}, u32[]{:S(2)}) %collective-permute-start.12) | collective-permute-done | bytes 442400 | tf_op jit(solution)/shard_map/ppermute | solution.py:115
  125.3 1.9 %constant_dynamic-update-slice_fusion.1 = bf16[3,32,2,144,128]{4,3,1,0,2:T(8,128)(2,1)} fusion(bf16[3,32,2,144,128]{4,3,1,0,2:T(8,128)(2,1)} %constant_dynamic-update-slice_fusion.2, bf16[3,2,2,144,128]{4,3,1,0,2:T(8,128)(2,1)} %collective-permute-done.12), kind=kLoop, calls=%fused_computation.28 | loop fusion | bytes 884736
  127.2 1.9 %constant_dynamic-update-slice_fusion = bf16[3,32,2,144,128]{4,3,1,0,2:T(8,128)(2,1)} fusion(bf16[3,32,2,144,128]{4,3,1,0,2:T(8,128)(2,1)} %constant_dynamic-update-slice_fusion.1, bf16[3,2,2,144,128]{4,3,1,0,2:T(8,128)(2,1)} %collective-permute-done.13), kind=kLoop, calls=%fused_computation.27 | loop fusion | bytes 884736 | tf_op jit(solution)/shard_map/concatenate | solution.py:127
  129.0 7.2 %copy.103 = bf16[3,32,2,144,128]{4,3,2,1,0:T(8,128)(2,1)} copy(bf16[3,32,2,144,128]{4,3,1,0,2:T(8,128)(2,1)} %constant_dynamic-update-slice_fusion) | data formatting | bytes 14155776 | tf_op jit(solution)/shard_map/concatenate | solution.py:127
  141.8 1.9 %constant_dynamic-update-slice_fusion.17 = (bf16[3,32,144,128]{3,2,1,0:T(8,128)(2,1)S(1)}, bf16[3,8,144,128]{3,2,1,0:T(8,128)(2,1)S(1)}) fusion(bf16[3,32,144,128]{3,2,1,0:T(8,128)(2,1)S(1)} %get-tuple-element.11, bf16[3,8,144,128]{3,2,1,0:T(8,128)(2,1)} %collective-permute-done.20, bf16[3,8,144,128]{3,2,1,0:T(8,128)(2,1)} %collective-permute-done.21, ...), kind=kLoop, calls=%fused_computation.44 | loop fusion | flops 4866048 | bytes 5308419
  145.1 4.7 %collective-permute-done.25 = bf16[3,4,144,128]{3,2,1,0:T(8,128)(2,1)S(1)} collective-permute-done((bf16[3,4,144,128]{3,2,1,0:T(8,128)(2,1)}, bf16[3,4,144,128]{3,2,1,0:T(8,128)(2,1)S(1)}, u32[]{:S(2)}, u32[]{:S(2)}) %collective-permute-start.25) | collective-permute-done | bytes 442400 | tf_op jit(solution)/shard_map/ppermute | solution.py:124
  150.4 8.9 %collective-permute-done.28 = bf16[3,4,144,128]{3,2,1,0:T(8,128)(2,1)S(1)} collective-permute-done((bf16[3,4,144,128]{3,2,1,0:T(8,128)(2,1)S(1)}, bf16[3,4,144,128]{3,2,1,0:T(8,128)(2,1)S(1)}, u32[]{:S(2)}, u32[]{:S(2)}) %collective-permute-start.28) | collective-permute-done | bytes 442400 | tf_op jit(solution)/shard_map/ppermute | solution.py:124
  163.4 14.6 %shard_map.37 = f32[2048,1024]{1,0:T(8,128)} custom-call(s32[288]{0:T(512)S(1)} %min.12.offs_ref, bf16[96,2,144,128]{3,2,1,0:T(8,128)(2,1)} %bitcast.70, bf16[96,144,128]{2,1,0:T(8,128)(2,1)S(1)} %bitcast.69), custom_call_target="tpu_custom_call" | custom-call | flops 805306368 | bytes 17825792 | tf_op jit(solution)/shard_map/pallas_call | solution.py:46
  (159 shorter events, 63.8 us)
Async XLA Ops:
  4.1 12.0 %collective-permute-start.1 = (bf16[3,2,2,144,128]{4,3,1,0,2:T(8,128)(2,1)S(1)}, bf16[3,2,2,144,128]{4,3,1,0,2:T(8,128)(2,1)S(1)}, u32[]{:S(2)}, u32[]{:S(2)}) collective-permute-start(bf16[3,2,2,144,128]{4,3,1,0,2:T(8,128)(2,1)S(1)} %get-tuple-element.16), channel_id=1, source_target_pairs={{2,0},{4,2},{6,4},{7,6},{5,7},{3,5},{1,3},{0,1},{10,8},{12,10},{14... | collective-permute-start | bytes 1327112 | tf_op jit(solution)/shard_map/ppermute | solution.py:116
  5.7 11.9 %collective-permute-start = (bf16[3,2,2,144,128]{4,3,1,0,2:T(8,128)(2,1)S(1)}, bf16[3,2,2,144,128]{4,3,1,0,2:T(8,128)(2,1)S(1)}, u32[]{:S(2)}, u32[]{:S(2)}) collective-permute-start(bf16[3,2,2,144,128]{4,3,1,0,2:T(8,128)(2,1)S(1)} %get-tuple-element.15), channel_id=1, source_target_pairs={{0,2},{2,4},{4,6},{6,7},{7,5},{5,3},{3,1},{1,0},{8,10},{10,12},{12... | collective-permute-start | bytes 1327112 | tf_op jit(solution)/shard_map/ppermute | solution.py:115
  16.0 11.0 %collective-permute-start.3 = (bf16[3,2,2,144,128]{4,3,1,0,2:T(8,128)(2,1)S(1)}, bf16[3,2,2,144,128]{4,3,1,0,2:T(8,128)(2,1)S(1)}, u32[]{:S(2)}, u32[]{:S(2)}) collective-permute-start(bf16[3,2,2,144,128]{4,3,1,0,2:T(8,128)(2,1)S(1)} %collective-permute-done.1), channel_id=1, source_target_pairs={{2,0},{4,2},{6,4},{7,6},{5,7},{3,5},{1,3},{0,1},{10,8},{12,10},{14... | collective-permute-start | bytes 1327112 | tf_op jit(solution)/shard_map/ppermute | solution.py:116
  17.6 11.6 %collective-permute-start.2 = (bf16[3,2,2,144,128]{4,3,1,0,2:T(8,128)(2,1)S(1)}, bf16[3,2,2,144,128]{4,3,1,0,2:T(8,128)(2,1)S(1)}, u32[]{:S(2)}, u32[]{:S(2)}) collective-permute-start(bf16[3,2,2,144,128]{4,3,1,0,2:T(8,128)(2,1)S(1)} %collective-permute-done), channel_id=1, source_target_pairs={{0,2},{2,4},{4,6},{6,7},{7,5},{5,3},{3,1},{1,0},{8,10},{10,12},{12... | collective-permute-start | bytes 1327112 | tf_op jit(solution)/shard_map/ppermute | solution.py:115
  18.3 32.2 %collective-permute-start.14 = (bf16[3,8,144,128]{3,2,1,0:T(8,128)(2,1)S(1)}, bf16[3,8,144,128]{3,2,1,0:T(8,128)(2,1)S(1)}, u32[]{:S(2)}, u32[]{:S(2)}) collective-permute-start(bf16[3,8,144,128]{3,2,1,0:T(8,128)(2,1)S(1)} %pad_maximum_fusion), channel_id=1, source_target_pairs={{0,24},{1,25},{10,2},{11,3},{20,12},{21,13},{30,22},{31,23}} | collective-permute-start | bytes 2654216 | tf_op jit(solution)/shard_map/ppermute | solution.py:124
  19.0 32.7 %collective-permute-start.15 = (bf16[3,8,144,128]{3,2,1,0:T(8,128)(2,1)S(1)}, bf16[3,8,144,128]{3,2,1,0:T(8,128)(2,1)}, u32[]{:S(2)}, u32[]{:S(2)}) collective-permute-start(bf16[3,8,144,128]{3,2,1,0:T(8,128)(2,1)S(1)} %pad_maximum_fusion), channel_id=1, source_target_pairs={{0,16},{1,17},{10,26},{11,27},{20,4},{21,5},{30,14},{31,15}} | collective-permute-start | bytes 2654216 | tf_op jit(solution)/shard_map/ppermute | solution.py:124
  20.6 35.1 %collective-permute-start.16 = (bf16[3,8,144,128]{3,2,1,0:T(8,128)(2,1)S(1)}, bf16[3,8,144,128]{3,2,1,0:T(8,128)(2,1)}, u32[]{:S(2)}, u32[]{:S(2)}) collective-permute-start(bf16[3,8,144,128]{3,2,1,0:T(8,128)(2,1)S(1)} %pad_maximum_fusion), channel_id=1, source_target_pairs={{0,8},{1,9},{10,18},{11,19},{20,28},{21,29},{30,6},{31,7}} | collective-permute-start | bytes 2654216 | tf_op jit(solution)/shard_map/ppermute | solution.py:124
  27.1 10.2 %collective-permute-start.5 = (bf16[3,2,2,144,128]{4,3,1,0,2:T(8,128)(2,1)S(1)}, bf16[3,2,2,144,128]{4,3,1,0,2:T(8,128)(2,1)}, u32[]{:S(2)}, u32[]{:S(2)}) collective-permute-start(bf16[3,2,2,144,128]{4,3,1,0,2:T(8,128)(2,1)S(1)} %collective-permute-done.3), channel_id=1, source_target_pairs={{2,0},{4,2},{6,4},{7,6},{5,7},{3,5},{1,3},{0,1},{10,8},{12,10},{14... | collective-permute-start | bytes 1327112 | tf_op jit(solution)/shard_map/ppermute | solution.py:116
  29.3 12.3 %collective-permute-start.4 = (bf16[3,2,2,144,128]{4,3,1,0,2:T(8,128)(2,1)S(1)}, bf16[3,2,2,144,128]{4,3,1,0,2:T(8,128)(2,1)}, u32[]{:S(2)}, u32[]{:S(2)}) collective-permute-start(bf16[3,2,2,144,128]{4,3,1,0,2:T(8,128)(2,1)S(1)} %collective-permute-done.2), channel_id=1, source_target_pairs={{0,2},{2,4},{4,6},{6,7},{7,5},{5,3},{3,1},{1,0},{8,10},{10,12},{12... | collective-permute-start | bytes 1327112 | tf_op jit(solution)/shard_map/ppermute | solution.py:115
  29.3 26.4 %copy-start.4 = (bf16[3,2,144,128]{3,2,1,0:T(8,128)(2,1)}, bf16[3,2,144,128]{3,2,1,0:T(8,128)(2,1)S(1)}, u32[]{:S(2)}) copy-start(bf16[3,2,144,128]{3,2,1,0:T(8,128)(2,1)S(1)} %dynamic-slice_bitcast_fusion.10) | copy-start | bytes 663556
  29.3 26.4 %copy-start.5 = (bf16[3,2,144,128]{3,2,1,0:T(8,128)(2,1)}, bf16[3,2,144,128]{3,2,1,0:T(8,128)(2,1)S(1)}, u32[]{:S(2)}) copy-start(bf16[3,2,144,128]{3,2,1,0:T(8,128)(2,1)S(1)} %dynamic-slice_bitcast_fusion.11) | copy-start | bytes 663556
  38.2 17.5 %copy-start.6 = (bf16[3,2,144,128]{3,2,1,0:T(8,128)(2,1)}, bf16[3,2,144,128]{3,2,1,0:T(8,128)(2,1)S(1)}, u32[]{:S(2)}) copy-start(bf16[3,2,144,128]{3,2,1,0:T(8,128)(2,1)S(1)} %dynamic-slice_bitcast_fusion.8) | copy-start | bytes 663556
  43.6 46.8 %collective-permute-start.17 = (bf16[3,8,144,128]{3,2,1,0:T(8,128)(2,1)}, bf16[3,8,144,128]{3,2,1,0:T(8,128)(2,1)}, u32[]{:S(2)}, u32[]{:S(2)}) collective-permute-start(bf16[3,8,144,128]{3,2,1,0:T(8,128)(2,1)} %pad_maximum_fusion.1), channel_id=1, source_target_pairs={{0,24},{1,25},{10,2},{11,3},{20,12},{21,13},{30,22},{31,23}} | collective-permute-start | bytes 2654216 | tf_op jit(solution)/shard_map/ppermute | solution.py:124
  45.2 46.5 %collective-permute-start.18 = (bf16[3,8,144,128]{3,2,1,0:T(8,128)(2,1)}, bf16[3,8,144,128]{3,2,1,0:T(8,128)(2,1)}, u32[]{:S(2)}, u32[]{:S(2)}) collective-permute-start(bf16[3,8,144,128]{3,2,1,0:T(8,128)(2,1)} %pad_maximum_fusion.1), channel_id=1, source_target_pairs={{0,16},{1,17},{10,26},{11,27},{20,4},{21,5},{30,14},{31,15}} | collective-permute-start | bytes 2654216 | tf_op jit(solution)/shard_map/ppermute | solution.py:124
  50.5 44.5 %collective-permute-start.19 = (bf16[3,8,144,128]{3,2,1,0:T(8,128)(2,1)}, bf16[3,8,144,128]{3,2,1,0:T(8,128)(2,1)}, u32[]{:S(2)}, u32[]{:S(2)}) collective-permute-start(bf16[3,8,144,128]{3,2,1,0:T(8,128)(2,1)} %pad_maximum_fusion.1), channel_id=1, source_target_pairs={{0,8},{1,9},{10,18},{11,19},{20,28},{21,29},{30,6},{31,7}} | collective-permute-start | bytes 2654216 | tf_op jit(solution)/shard_map/ppermute | solution.py:124
  51.8 17.7 %collective-permute-start.7 = (bf16[3,2,2,144,128]{4,3,1,0,2:T(8,128)(2,1)}, bf16[3,2,2,144,128]{4,3,1,0,2:T(8,128)(2,1)}, u32[]{:S(2)}, u32[]{:S(2)}) collective-permute-start(bf16[3,2,2,144,128]{4,3,1,0,2:T(8,128)(2,1)} %collective-permute-done.5), channel_id=1, source_target_pairs={{2,0},{4,2},{6,4},{7,6},{5,7},{3,5},{1,3},{0,1},{10,8},{12,10},{14... | collective-permute-start | bytes 1327112 | tf_op jit(solution)/shard_map/ppermute | solution.py:116
  55.7 12.4 %collective-permute-start.6 = (bf16[3,2,2,144,128]{4,3,1,0,2:T(8,128)(2,1)}, bf16[3,2,2,144,128]{4,3,1,0,2:T(8,128)(2,1)}, u32[]{:S(2)}, u32[]{:S(2)}) collective-permute-start(bf16[3,2,2,144,128]{4,3,1,0,2:T(8,128)(2,1)} %collective-permute-done.4), channel_id=1, source_target_pairs={{0,2},{2,4},{4,6},{6,7},{7,5},{5,3},{3,1},{1,0},{8,10},{10,12},{12... | collective-permute-start | bytes 1327112 | tf_op jit(solution)/shard_map/ppermute | solution.py:115
  70.9 11.3 %collective-permute-start.9 = (bf16[3,2,2,144,128]{4,3,1,0,2:T(8,128)(2,1)}, bf16[3,2,2,144,128]{4,3,1,0,2:T(8,128)(2,1)S(1)}, u32[]{:S(2)}, u32[]{:S(2)}) collective-permute-start(bf16[3,2,2,144,128]{4,3,1,0,2:T(8,128)(2,1)} %collective-permute-done.7), channel_id=1, source_target_pairs={{2,0},{4,2},{6,4},{7,6},{5,7},{3,5},{1,3},{0,1},{10,8},{12,10},{14... | collective-permute-start | bytes 1327112 | tf_op jit(solution)/shard_map/ppermute | solution.py:116
  71.4 12.4 %collective-permute-start.8 = (bf16[3,2,2,144,128]{4,3,1,0,2:T(8,128)(2,1)}, bf16[3,2,2,144,128]{4,3,1,0,2:T(8,128)(2,1)S(1)}, u32[]{:S(2)}, u32[]{:S(2)}) collective-permute-start(bf16[3,2,2,144,128]{4,3,1,0,2:T(8,128)(2,1)} %collective-permute-done.6), channel_id=1, source_target_pairs={{0,2},{2,4},{4,6},{6,7},{7,5},{5,3},{3,1},{1,0},{8,10},{10,12},{12... | collective-permute-start | bytes 1327112 | tf_op jit(solution)/shard_map/ppermute | solution.py:115
  84.9 54.1 %collective-permute-start.20 = (bf16[3,8,144,128]{3,2,1,0:T(8,128)(2,1)}, bf16[3,8,144,128]{3,2,1,0:T(8,128)(2,1)}, u32[]{:S(2)}, u32[]{:S(2)}) collective-permute-start(bf16[3,8,144,128]{3,2,1,0:T(8,128)(2,1)} %pad_maximum_fusion.2), channel_id=1, source_target_pairs={{0,24},{1,25},{10,2},{11,3},{20,12},{21,13},{30,22},{31,23}} | collective-permute-start | bytes 2654216 | tf_op jit(solution)/shard_map/ppermute | solution.py:124
  86.6 53.9 %collective-permute-start.21 = (bf16[3,8,144,128]{3,2,1,0:T(8,128)(2,1)}, bf16[3,8,144,128]{3,2,1,0:T(8,128)(2,1)}, u32[]{:S(2)}, u32[]{:S(2)}) collective-permute-start(bf16[3,8,144,128]{3,2,1,0:T(8,128)(2,1)} %pad_maximum_fusion.2), channel_id=1, source_target_pairs={{0,16},{1,17},{10,26},{11,27},{20,4},{21,5},{30,14},{31,15}} | collective-permute-start | bytes 2654216 | tf_op jit(solution)/shard_map/ppermute | solution.py:124
  90.4 50.7 %collective-permute-start.22 = (bf16[3,8,144,128]{3,2,1,0:T(8,128)(2,1)}, bf16[3,8,144,128]{3,2,1,0:T(8,128)(2,1)}, u32[]{:S(2)}, u32[]{:S(2)}) collective-permute-start(bf16[3,8,144,128]{3,2,1,0:T(8,128)(2,1)} %pad_maximum_fusion.2), channel_id=1, source_target_pairs={{0,8},{1,9},{10,18},{11,19},{20,28},{21,29},{30,6},{31,7}} | collective-permute-start | bytes 2654216 | tf_op jit(solution)/shard_map/ppermute | solution.py:124
  91.7 11.6 %collective-permute-start.11 = (bf16[3,2,2,144,128]{4,3,1,0,2:T(8,128)(2,1)}, bf16[3,2,2,144,128]{4,3,1,0,2:T(8,128)(2,1)}, u32[]{:S(2)}, u32[]{:S(2)}) collective-permute-start(bf16[3,2,2,144,128]{4,3,1,0,2:T(8,128)(2,1)} %copy-done.17), channel_id=1, source_target_pairs={{2,0},{4,2},{6,4},{7,6},{5,7},{3,5},{1,3},{0,1},{10,8},{12,10},{14... | collective-permute-start | bytes 1327112 | tf_op jit(solution)/shard_map/ppermute | solution.py:116
  94.9 11.8 %collective-permute-start.10 = (bf16[3,2,2,144,128]{4,3,1,0,2:T(8,128)(2,1)}, bf16[3,2,2,144,128]{4,3,1,0,2:T(8,128)(2,1)}, u32[]{:S(2)}, u32[]{:S(2)}) collective-permute-start(bf16[3,2,2,144,128]{4,3,1,0,2:T(8,128)(2,1)} %copy-done.16), channel_id=1, source_target_pairs={{0,2},{2,4},{4,6},{6,7},{7,5},{5,3},{3,1},{1,0},{8,10},{10,12},{12... | collective-permute-start | bytes 1327112 | tf_op jit(solution)/shard_map/ppermute | solution.py:115
  103.4 19.1 %collective-permute-start.13 = (bf16[3,2,2,144,128]{4,3,1,0,2:T(8,128)(2,1)}, bf16[3,2,2,144,128]{4,3,1,0,2:T(8,128)(2,1)}, u32[]{:S(2)}, u32[]{:S(2)}) collective-permute-start(bf16[3,2,2,144,128]{4,3,1,0,2:T(8,128)(2,1)} %collective-permute-done.11), channel_id=1, source_target_pairs={{2,0},{4,2},{6,4},{7,6},{5,7},{3,5},{1,3},{0,1},{10,8},{12,10},{14... | collective-permute-start | bytes 1327112 | tf_op jit(solution)/shard_map/ppermute | solution.py:116
  106.7 12.8 %collective-permute-start.12 = (bf16[3,2,2,144,128]{4,3,1,0,2:T(8,128)(2,1)}, bf16[3,2,2,144,128]{4,3,1,0,2:T(8,128)(2,1)}, u32[]{:S(2)}, u32[]{:S(2)}) collective-permute-start(bf16[3,2,2,144,128]{4,3,1,0,2:T(8,128)(2,1)} %collective-permute-done.10), channel_id=1, source_target_pairs={{0,2},{2,4},{4,6},{6,7},{7,5},{5,3},{3,1},{1,0},{8,10},{10,12},{12... | collective-permute-start | bytes 1327112 | tf_op jit(solution)/shard_map/ppermute | solution.py:115
  119.5 24.2 %collective-permute-start.23 = (bf16[3,4,144,128]{3,2,1,0:T(8,128)(2,1)}, bf16[3,4,144,128]{3,2,1,0:T(8,128)(2,1)}, u32[]{:S(2)}, u32[]{:S(2)}) collective-permute-start(bf16[3,4,144,128]{3,2,1,0:T(8,128)(2,1)} %pad_maximum_fusion.3), channel_id=1, source_target_pairs={{0,24},{1,25},{10,2},{11,3},{20,12},{21,13},{30,22},{31,23}} | collective-permute-start | bytes 1327112 | tf_op jit(solution)/shard_map/ppermute | solution.py:124
  122.4 22.6 %collective-permute-start.24 = (bf16[3,4,144,128]{3,2,1,0:T(8,128)(2,1)}, bf16[3,4,144,128]{3,2,1,0:T(8,128)(2,1)}, u32[]{:S(2)}, u32[]{:S(2)}) collective-permute-start(bf16[3,4,144,128]{3,2,1,0:T(8,128)(2,1)} %pad_maximum_fusion.3), channel_id=1, source_target_pairs={{0,16},{1,17},{10,26},{11,27},{20,4},{21,5},{30,14},{31,15}} | collective-permute-start | bytes 1327112 | tf_op jit(solution)/shard_map/ppermute | solution.py:124
  139.1 10.7 %collective-permute-start.25 = (bf16[3,4,144,128]{3,2,1,0:T(8,128)(2,1)}, bf16[3,4,144,128]{3,2,1,0:T(8,128)(2,1)S(1)}, u32[]{:S(2)}, u32[]{:S(2)}) collective-permute-start(bf16[3,4,144,128]{3,2,1,0:T(8,128)(2,1)} %pad_maximum_fusion.3), channel_id=1, source_target_pairs={{0,8},{1,9},{10,18},{11,19},{20,28},{21,29},{30,6},{31,7}} | collective-permute-start | bytes 1327112 | tf_op jit(solution)/shard_map/ppermute | solution.py:124
  140.4 9.9 %collective-permute-start.26 = (bf16[3,4,144,128]{3,2,1,0:T(8,128)(2,1)S(1)}, bf16[3,4,144,128]{3,2,1,0:T(8,128)(2,1)S(1)}, u32[]{:S(2)}, u32[]{:S(2)}) collective-permute-start(bf16[3,4,144,128]{3,2,1,0:T(8,128)(2,1)S(1)} %pad_maximum_fusion.4), channel_id=1, source_target_pairs={{0,24},{1,25},{10,2},{11,3},{20,12},{21,13},{30,22},{31,23}} | collective-permute-start | bytes 1327112 | tf_op jit(solution)/shard_map/ppermute | solution.py:124
  141.1 9.2 %collective-permute-start.27 = (bf16[3,4,144,128]{3,2,1,0:T(8,128)(2,1)S(1)}, bf16[3,4,144,128]{3,2,1,0:T(8,128)(2,1)S(1)}, u32[]{:S(2)}, u32[]{:S(2)}) collective-permute-start(bf16[3,4,144,128]{3,2,1,0:T(8,128)(2,1)S(1)} %pad_maximum_fusion.4), channel_id=1, source_target_pairs={{0,16},{1,17},{10,26},{11,27},{20,4},{21,5},{30,14},{31,15}} | collective-permute-start | bytes 1327112 | tf_op jit(solution)/shard_map/ppermute | solution.py:124
  143.8 15.5 %collective-permute-start.28 = (bf16[3,4,144,128]{3,2,1,0:T(8,128)(2,1)S(1)}, bf16[3,4,144,128]{3,2,1,0:T(8,128)(2,1)S(1)}, u32[]{:S(2)}, u32[]{:S(2)}) collective-permute-start(bf16[3,4,144,128]{3,2,1,0:T(8,128)(2,1)S(1)} %pad_maximum_fusion.4), channel_id=1, source_target_pairs={{0,8},{1,9},{10,18},{11,19},{20,28},{21,29},{30,6},{31,7}} | collective-permute-start | bytes 1327112 | tf_op jit(solution)/shard_map/ppermute | solution.py:124
  (18 other events, 123.1 us)

commit v14 on v10

--- a/solution.py
+++ b/solution.py
@@ -8,12 +8,13 @@
 from jax.sharding import PartitionSpec as P
 
 IBS = 8
-CHUNK = 8
+CHUNK = 32
 META = 16
 
 
 def gram_kernel(offs_ref, bs_ref, bc_ref, o_ref, *, chunk, local_slots, blk):
-    step = pl.program_id(0)
+    s = pl.program_id(0)
+    step = pl.program_id(1)
 
     @pl.when(step == 0)
     def _():
@@ -24,18 +25,11 @@
         g = step * chunk + k
         meta = bs_ref[k, 0, blk : blk + META].astype(jnp.float32)
         w = meta[0:1] + meta[1:2] + meta[2:3]
-        lhs = jnp.concatenate(
-            [
-                (bs_ref[k, s, :blk].astype(jnp.float32).T * w).astype(jnp.bfloat16)
-                for s in range(local_slots)
-            ],
-            axis=0,
-        )
+        lhs = (bs_ref[k, 0, :blk].astype(jnp.float32).T * w).astype(jnp.bfloat16)
         prod = jnp.dot(lhs, bc_ref[k, :blk], preferred_element_type=jnp.float32)
         col = pl.multiple_of(offs_ref[g * stride + local_slots] * blk, blk)
-        for s in range(local_slots):
-            row = pl.multiple_of((s * IBS + offs_ref[g * stride + s]) * blk, blk)
-            o_ref[pl.ds(row, blk), pl.ds(col, blk)] += prod[s * blk : (s + 1) * blk]
+        row = pl.multiple_of(offs_ref[g * stride + s] * blk, blk)
+        o_ref[pl.ds(row, blk), pl.ds(col, blk)] += prod
 
 
 def gram_call(offs, bs, bc):
@@ -47,16 +41,16 @@
         kernel,
         grid_spec=pltpu.PrefetchScalarGridSpec(
             num_scalar_prefetch=1,
-            grid=(n // chunk,),
+            grid=(local_slots, n // chunk),
             in_specs=[
-                pl.BlockSpec((chunk, local_slots, rows, blk), lambda i, o: (i, 0, 0, 0)),
-                pl.BlockSpec((chunk, rows, blk), lambda i, o: (i, 0, 0)),
+                pl.BlockSpec((chunk, 1, rows, blk), lambda s, i, o: (i, s, 0, 0)),
+                pl.BlockSpec((chunk, rows, blk), lambda s, i, o: (i, 0, 0)),
             ],
-            out_specs=pl.BlockSpec((out_rows, out_cols), lambda i, o: (0, 0)),
+            out_specs=pl.BlockSpec((IBS * blk, out_cols), lambda s, i, o: (s, 0)),
         ),
         out_shape=jax.ShapeDtypeStruct((out_rows, out_cols), jnp.float32),
         compiler_params=pltpu.CompilerParams(
-            dimension_semantics=("arbitrary",), vmem_limit_bytes=48 * 1024 * 1024
+            dimension_semantics=("arbitrary", "arbitrary"), vmem_limit_bytes=48 * 1024 * 1024
         ),
         cost_estimate=pl.CostEstimate(
             flops=2 * n * local_slots * blk * blk * blk,

time: 135 us -> 131 us (0.970)
  Pallas kernels: 14.6 us -> 11.1 us
    pallas_call x1, Pallas kernels: 14.6 us -> 11.1 us  [gram_call(): pl.pallas_call(kernel, grid_spec=pltpu.PrefetchScalarGridSpec(num_scalar_...]
where the time goes in v14:
time: 131 us; the launch traced here: 130 us
  waiting for transfers between devices  47 us (36%)
  starting transfers between devices  43.6 us (33%)
  local copies, waits for them, and re-layouts  17.8 us (14%)
  Pallas kernels  11.1 us (8%)
  other arithmetic  10 us (8%)
    ppermute x7, waiting for transfers between devices, local(): a = lax.ppermute(a, 'col', forward)  31.5 us
    ppermute x15, starting transfers between devices, local(): got = jnp.where(which == j, lax.ppermute(own, ('row', 'col'), fan), got)  30.5 us
    ppermute x7, starting transfers between devices, local(): a = lax.ppermute(a, 'col', forward)  11.9 us
    ppermute x7, waiting for transfers between devices, local(): b = lax.ppermute(b, 'col', backward)  11.5 us
    pallas_call x1, Pallas kernels, gram_call(): pl.pallas_call(kernel, grid_spec=pltpu.PrefetchScalarGridSpec(num_scalar_...  11.1 us
    unnamed x23, local copies, waits for them, and re-layouts  11.1 us
    unnamed x5, other arithmetic  5.26 us
    ppermute x15, waiting for transfers between devices, local(): got = jnp.where(which == j, lax.ppermute(own, ('row', 'col'), fan), got)  4.03 us
  transfers between devices with their start and end apart: 29, of which 11 were waited for; matrix products, arithmetic and copies ran while one was open for 15% of the time, Pallas kernels for 0%

profile of v14, /device:TPU:0, one launch (start us, length us, event | category | flops | bytes accessed | tf_op | source)
XLA Modules:
  0.0 130.0 jit_solution(5430052015777789314)
XLA Ops:
  1.7 2.4 %constant_dynamic-update-slice_fusion.14 = (bf16[3,32,2,144,128]{4,3,2,1,0:T(8,128)(2,1)}, bf16[3,4,2,144,128]{4,3,2,1,0:T(8,128)(2,1)S(1)}) fusion(bf16[144]{0:T(256)(128)(2,1)S(1)} %pad.21.clone, bf16[3,4,2,1,128]{4,3,2,1,0:T(2,128)(2,1)S(1)} %broadcast_in_dim.7, bf16[3,4,2,3,128]{4,3,2,1,0:T(4,128)(2,1)S(1)} %broadcast_in_dim.6, ...), kind=kLoop, calls=%fused_computation.42 | loop fusion | flops 3538943 | bytes 2580768
  4.2 3.1 %collective-permute-start = (bf16[3,2,2,144,128]{4,3,2,1,0:T(8,128)(2,1)S(1)}, bf16[3,2,2,144,128]{4,3,2,1,0:T(8,128)(2,1)S(1)}, u32[]{:S(2)}, u32[]{:S(2)}) collective-permute-start(bf16[3,2,2,144,128]{4,3,2,1,0:T(8,128)(2,1)S(1)} %get-tuple-element.5), channel_id=1, source_target_pairs={{0,2},{2,4},{4,6},{6,7},{7,5},{5,3},{3,1},{1,0},{8,10},{10,12},{12... | collective-permute-start | bytes 1327112 | tf_op jit(solution)/shard_map/ppermute | solution.py:109
  7.3 10.1 %collective-permute-done = bf16[3,2,2,144,128]{4,3,2,1,0:T(8,128)(2,1)S(1)} collective-permute-done((bf16[3,2,2,144,128]{4,3,2,1,0:T(8,128)(2,1)S(1)}, bf16[3,2,2,144,128]{4,3,2,1,0:T(8,128)(2,1)S(1)}, u32[]{:S(2)}, u32[]{:S(2)}) %collective-permute-start) | collective-permute-done | bytes 442400 | tf_op jit(solution)/shard_map/ppermute | solution.py:109
  17.4 1.8 %collective-permute-start.2 = (bf16[3,2,2,144,128]{4,3,2,1,0:T(8,128)(2,1)S(1)}, bf16[3,2,2,144,128]{4,3,2,1,0:T(8,128)(2,1)S(1)}, u32[]{:S(2)}, u32[]{:S(2)}) collective-permute-start(bf16[3,2,2,144,128]{4,3,2,1,0:T(8,128)(2,1)S(1)} %collective-permute-done), channel_id=1, source_target_pairs={{0,2},{2,4},{4,6},{6,7},{7,5},{5,3},{3,1},{1,0},{8,10},{10,12},{12... | collective-permute-start | bytes 1327112 | tf_op jit(solution)/shard_map/ppermute | solution.py:109
  19.6 1.3 %collective-permute-start.16 = (bf16[3,8,144,128]{3,2,1,0:T(8,128)(2,1)S(1)}, bf16[3,8,144,128]{3,2,1,0:T(8,128)(2,1)S(1)}, u32[]{:S(2)}, u32[]{:S(2)}) collective-permute-start(bf16[3,8,144,128]{3,2,1,0:T(8,128)(2,1)S(1)} %pad_maximum_fusion), channel_id=1, source_target_pairs={{0,8},{1,9},{10,18},{11,19},{20,28},{21,29},{30,6},{31,7}} | collective-permute-start | bytes 2654216 | tf_op jit(solution)/shard_map/ppermute | solution.py:118
  21.0 3.0 %collective-permute-start.15 = (bf16[3,8,144,128]{3,2,1,0:T(8,128)(2,1)S(1)}, bf16[3,8,144,128]{3,2,1,0:T(8,128)(2,1)S(1)}, u32[]{:S(2)}, u32[]{:S(2)}) collective-permute-start(bf16[3,8,144,128]{3,2,1,0:T(8,128)(2,1)S(1)} %pad_maximum_fusion), channel_id=1, source_target_pairs={{0,16},{1,17},{10,26},{11,27},{20,4},{21,5},{30,14},{31,15}} | collective-permute-start | bytes 2654216 | tf_op jit(solution)/shard_map/ppermute | solution.py:118
  24.0 1.3 %collective-permute-start.14 = (bf16[3,8,144,128]{3,2,1,0:T(8,128)(2,1)S(1)}, bf16[3,8,144,128]{3,2,1,0:T(8,128)(2,1)S(1)}, u32[]{:S(2)}, u32[]{:S(2)}) collective-permute-start(bf16[3,8,144,128]{3,2,1,0:T(8,128)(2,1)S(1)} %pad_maximum_fusion), channel_id=1, source_target_pairs={{0,24},{1,25},{10,2},{11,3},{20,12},{21,13},{30,22},{31,23}} | collective-permute-start | bytes 2654216 | tf_op jit(solution)/shard_map/ppermute | solution.py:118
  27.1 1.6 %collective-permute-done.2 = bf16[3,2,2,144,128]{4,3,2,1,0:T(8,128)(2,1)S(1)} collective-permute-done((bf16[3,2,2,144,128]{4,3,2,1,0:T(8,128)(2,1)S(1)}, bf16[3,2,2,144,128]{4,3,2,1,0:T(8,128)(2,1)S(1)}, u32[]{:S(2)}, u32[]{:S(2)}) %collective-permute-start.2) | collective-permute-done | bytes 442400 | tf_op jit(solution)/shard_map/ppermute | solution.py:109
  28.8 1.5 %collective-permute-start.4 = (bf16[3,2,2,144,128]{4,3,2,1,0:T(8,128)(2,1)S(1)}, bf16[3,2,2,144,128]{4,3,2,1,0:T(8,128)(2,1)S(1)}, u32[]{:S(2)}, u32[]{:S(2)}) collective-permute-start(bf16[3,2,2,144,128]{4,3,2,1,0:T(8,128)(2,1)S(1)} %collective-permute-done.2), channel_id=1, source_target_pairs={{0,2},{2,4},{4,6},{6,7},{7,5},{5,3},{3,1},{1,0},{8,10},{10,12},{12... | collective-permute-start | bytes 1327112 | tf_op jit(solution)/shard_map/ppermute | solution.py:109
  32.5 6.6 %collective-permute-done.4 = bf16[3,2,2,144,128]{4,3,2,1,0:T(8,128)(2,1)S(1)} collective-permute-done((bf16[3,2,2,144,128]{4,3,2,1,0:T(8,128)(2,1)S(1)}, bf16[3,2,2,144,128]{4,3,2,1,0:T(8,128)(2,1)S(1)}, u32[]{:S(2)}, u32[]{:S(2)}) %collective-permute-start.4) | collective-permute-done | bytes 442400 | tf_op jit(solution)/shard_map/ppermute | solution.py:109
  39.2 2.3 %collective-permute-start.6 = (bf16[3,2,2,144,128]{4,3,2,1,0:T(8,128)(2,1)S(1)}, bf16[3,2,2,144,128]{4,3,2,1,0:T(8,128)(2,1)S(1)}, u32[]{:S(2)}, u32[]{:S(2)}) collective-permute-start(bf16[3,2,2,144,128]{4,3,2,1,0:T(8,128)(2,1)S(1)} %collective-permute-done.4), channel_id=1, source_target_pairs={{0,2},{2,4},{4,6},{6,7},{7,5},{5,3},{3,1},{1,0},{8,10},{10,12},{12... | collective-permute-start | bytes 1327112 | tf_op jit(solution)/shard_map/ppermute | solution.py:109
  44.7 2.3 %collective-permute-start.18 = (bf16[3,8,144,128]{3,2,1,0:T(8,128)(2,1)S(1)}, bf16[3,8,144,128]{3,2,1,0:T(8,128)(2,1)S(1)}, u32[]{:S(2)}, u32[]{:S(2)}) collective-permute-start(bf16[3,8,144,128]{3,2,1,0:T(8,128)(2,1)S(1)} %pad_maximum_fusion.1), channel_id=1, source_target_pairs={{0,16},{1,17},{10,26},{11,27},{20,4},{21,5},{30,14},{31,15}} | collective-permute-start | bytes 2654216 | tf_op jit(solution)/shard_map/ppermute | solution.py:118
  47.1 1.3 %collective-permute-start.17 = (bf16[3,8,144,128]{3,2,1,0:T(8,128)(2,1)S(1)}, bf16[3,8,144,128]{3,2,1,0:T(8,128)(2,1)S(1)}, u32[]{:S(2)}, u32[]{:S(2)}) collective-permute-start(bf16[3,8,144,128]{3,2,1,0:T(8,128)(2,1)S(1)} %pad_maximum_fusion.1), channel_id=1, source_target_pairs={{0,24},{1,25},{10,2},{11,3},{20,12},{21,13},{30,22},{31,23}} | collective-permute-start | bytes 2654216 | tf_op jit(solution)/shard_map/ppermute | solution.py:118
  49.7 2.1 %collective-permute-start.8 = (bf16[3,2,2,144,128]{4,3,2,1,0:T(8,128)(2,1)S(1)}, bf16[3,2,2,144,128]{4,3,2,1,0:T(8,128)(2,1)S(1)}, u32[]{:S(2)}, u32[]{:S(2)}) collective-permute-start(bf16[3,2,2,144,128]{4,3,2,1,0:T(8,128)(2,1)S(1)} %collective-permute-done.6), channel_id=1, source_target_pairs={{0,2},{2,4},{4,6},{6,7},{7,5},{5,3},{3,1},{1,0},{8,10},{10,12},{12... | collective-permute-start | bytes 1327112 | tf_op jit(solution)/shard_map/ppermute | solution.py:109
  53.6 7.3 %collective-permute-done.8 = bf16[3,2,2,144,128]{4,3,2,1,0:T(8,128)(2,1)S(1)} collective-permute-done((bf16[3,2,2,144,128]{4,3,2,1,0:T(8,128)(2,1)S(1)}, bf16[3,2,2,144,128]{4,3,2,1,0:T(8,128)(2,1)S(1)}, u32[]{:S(2)}, u32[]{:S(2)}) %collective-permute-start.8) | collective-permute-done | bytes 442400 | tf_op jit(solution)/shard_map/ppermute | solution.py:109
  60.9 2.2 %collective-permute-done.9 = bf16[3,2,2,144,128]{4,3,2,1,0:T(8,128)(2,1)S(1)} collective-permute-done((bf16[3,2,2,144,128]{4,3,2,1,0:T(8,128)(2,1)S(1)}, bf16[3,2,2,144,128]{4,3,2,1,0:T(8,128)(2,1)S(1)}, u32[]{:S(2)}, u32[]{:S(2)}) %collective-permute-start.9) | collective-permute-done | bytes 442400 | tf_op jit(solution)/shard_map/ppermute | solution.py:110
  63.2 1.3 %collective-permute-start.22 = (bf16[3,8,144,128]{3,2,1,0:T(8,128)(2,1)S(1)}, bf16[3,8,144,128]{3,2,1,0:T(8,128)(2,1)S(1)}, u32[]{:S(2)}, u32[]{:S(2)}) collective-permute-start(bf16[3,8,144,128]{3,2,1,0:T(8,128)(2,1)S(1)} %pad_maximum_fusion.2), channel_id=1, source_target_pairs={{0,8},{1,9},{10,18},{11,19},{20,28},{21,29},{30,6},{31,7}} | collective-permute-start | bytes 2654216 | tf_op jit(solution)/shard_map/ppermute | solution.py:118
  66.4 3.8 %collective-permute-start.21 = (bf16[3,8,144,128]{3,2,1,0:T(8,128)(2,1)S(1)}, bf16[3,8,144,128]{3,2,1,0:T(8,128)(2,1)S(1)}, u32[]{:S(2)}, u32[]{:S(2)}) collective-permute-start(bf16[3,8,144,128]{3,2,1,0:T(8,128)(2,1)S(1)} %pad_maximum_fusion.2), channel_id=1, source_target_pairs={{0,16},{1,17},{10,26},{11,27},{20,4},{21,5},{30,14},{31,15}} | collective-permute-start | bytes 2654216 | tf_op jit(solution)/shard_map/ppermute | solution.py:118
  70.2 1.3 %collective-permute-start.20 = (bf16[3,8,144,128]{3,2,1,0:T(8,128)(2,1)S(1)}, bf16[3,8,144,128]{3,2,1,0:T(8,128)(2,1)S(1)}, u32[]{:S(2)}, u32[]{:S(2)}) collective-permute-start(bf16[3,8,144,128]{3,2,1,0:T(8,128)(2,1)S(1)} %pad_maximum_fusion.2), channel_id=1, source_target_pairs={{0,24},{1,25},{10,2},{11,3},{20,12},{21,13},{30,22},{31,23}} | collective-permute-start | bytes 2654216 | tf_op jit(solution)/shard_map/ppermute | solution.py:118
  72.2 2.8 %collective-permute-done.10 = bf16[3,2,2,144,128]{4,3,2,1,0:T(8,128)(2,1)S(1)} collective-permute-done((bf16[3,2,2,144,128]{4,3,2,1,0:T(8,128)(2,1)S(1)}, bf16[3,2,2,144,128]{4,3,2,1,0:T(8,128)(2,1)S(1)}, u32[]{:S(2)}, u32[]{:S(2)}) %collective-permute-start.10) | collective-permute-done | bytes 442400 | tf_op jit(solution)/shard_map/ppermute | solution.py:109
  76.0 6.3 %collective-permute-done.11 = bf16[3,2,2,144,128]{4,3,2,1,0:T(8,128)(2,1)S(1)} collective-permute-done((bf16[3,2,2,144,128]{4,3,2,1,0:T(8,128)(2,1)S(1)}, bf16[3,2,2,144,128]{4,3,2,1,0:T(8,128)(2,1)S(1)}, u32[]{:S(2)}, u32[]{:S(2)}) %collective-permute-start.11) | collective-permute-done | bytes 442400 | tf_op jit(solution)/shard_map/ppermute | solution.py:110
  85.2 2.3 %collective-permute-done.12 = bf16[3,2,2,144,128]{4,3,2,1,0:T(8,128)(2,1)S(1)} collective-permute-done((bf16[3,2,2,144,128]{4,3,2,1,0:T(8,128)(2,1)S(1)}, bf16[3,2,2,144,128]{4,3,2,1,0:T(8,128)(2,1)S(1)}, u32[]{:S(2)}, u32[]{:S(2)}) %collective-permute-start.12) | collective-permute-done | bytes 442400 | tf_op jit(solution)/shard_map/ppermute | solution.py:109
  87.5 1.6 %collective-permute-start.25 = (bf16[3,4,144,128]{3,2,1,0:T(8,128)(2,1)}, bf16[3,4,144,128]{3,2,1,0:T(8,128)(2,1)S(1)}, u32[]{:S(2)}, u32[]{:S(2)}) collective-permute-start(bf16[3,4,144,128]{3,2,1,0:T(8,128)(2,1)} %pad_maximum_fusion.3), channel_id=1, source_target_pairs={{0,8},{1,9},{10,18},{11,19},{20,28},{21,29},{30,6},{31,7}} | collective-permute-start | bytes 1327112 | tf_op jit(solution)/shard_map/ppermute | solution.py:118
  89.1 3.0 %collective-permute-done.13 = bf16[3,2,2,144,128]{4,3,2,1,0:T(8,128)(2,1)S(1)} collective-permute-done((bf16[3,2,2,144,128]{4,3,2,1,0:T(8,128)(2,1)S(1)}, bf16[3,2,2,144,128]{4,3,2,1,0:T(8,128)(2,1)S(1)}, u32[]{:S(2)}, u32[]{:S(2)}) %collective-permute-start.13) | collective-permute-done | bytes 442400 | tf_op jit(solution)/shard_map/ppermute | solution.py:110
  92.1 3.4 %collective-permute-start.24 = (bf16[3,4,144,128]{3,2,1,0:T(8,128)(2,1)}, bf16[3,4,144,128]{3,2,1,0:T(8,128)(2,1)}, u32[]{:S(2)}, u32[]{:S(2)}) collective-permute-start(bf16[3,4,144,128]{3,2,1,0:T(8,128)(2,1)} %pad_maximum_fusion.3), channel_id=1, source_target_pairs={{0,16},{1,17},{10,26},{11,27},{20,4},{21,5},{30,14},{31,15}} | collective-permute-start | bytes 1327112 | tf_op jit(solution)/shard_map/ppermute | solution.py:118
  96.4 2.1 %collective-permute-start.23 = (bf16[3,4,144,128]{3,2,1,0:T(8,128)(2,1)}, bf16[3,4,144,128]{3,2,1,0:T(8,128)(2,1)}, u32[]{:S(2)}, u32[]{:S(2)}) collective-permute-start(bf16[3,4,144,128]{3,2,1,0:T(8,128)(2,1)} %pad_maximum_fusion.3), channel_id=1, source_target_pairs={{0,24},{1,25},{10,2},{11,3},{20,12},{21,13},{30,22},{31,23}} | collective-permute-start | bytes 1327112 | tf_op jit(solution)/shard_map/ppermute | solution.py:118
  98.4 2.1 %collective-permute-start.28 = (bf16[3,4,144,128]{3,2,1,0:T(8,128)(2,1)}, bf16[3,4,144,128]{3,2,1,0:T(8,128)(2,1)}, u32[]{:S(2)}, u32[]{:S(2)}) collective-permute-start(bf16[3,4,144,128]{3,2,1,0:T(8,128)(2,1)} %pad_maximum_fusion.4), channel_id=1, source_target_pairs={{0,8},{1,9},{10,18},{11,19},{20,28},{21,29},{30,6},{31,7}} | collective-permute-start | bytes 1327112 | tf_op jit(solution)/shard_map/ppermute | solution.py:118
  100.5 2.1 %collective-permute-start.27 = (bf16[3,4,144,128]{3,2,1,0:T(8,128)(2,1)}, bf16[3,4,144,128]{3,2,1,0:T(8,128)(2,1)}, u32[]{:S(2)}, u32[]{:S(2)}) collective-permute-start(bf16[3,4,144,128]{3,2,1,0:T(8,128)(2,1)} %pad_maximum_fusion.4), channel_id=1, source_target_pairs={{0,16},{1,17},{10,26},{11,27},{20,4},{21,5},{30,14},{31,15}} | collective-permute-start | bytes 1327112 | tf_op jit(solution)/shard_map/ppermute | solution.py:118
  103.1 2.1 %collective-permute-start.26 = (bf16[3,4,144,128]{3,2,1,0:T(8,128)(2,1)}, bf16[3,4,144,128]{3,2,1,0:T(8,128)(2,1)}, u32[]{:S(2)}, u32[]{:S(2)}) collective-permute-start(bf16[3,4,144,128]{3,2,1,0:T(8,128)(2,1)} %pad_maximum_fusion.4), channel_id=1, source_target_pairs={{0,24},{1,25},{10,2},{11,3},{20,12},{21,13},{30,22},{31,23}} | collective-permute-start | bytes 1327112 | tf_op jit(solution)/shard_map/ppermute | solution.py:118
  107.0 1.7 %slice.19 = bf16[96,2,1,1]{3,2,1,0:T(2,128)(2,1)} slice(bf16[96,2,144,128]{3,2,1,0:T(8,128)(2,1)} %bitcast.44), slice={[0:96], [0:2], [131:132], [0:1]} | slice | bytes 768 | tf_op jit(solution)/shard_map/slice | solution.py:127
  111.0 4.0 %collective-permute-done.26 = bf16[3,4,144,128]{3,2,1,0:T(8,128)(2,1)} collective-permute-done((bf16[3,4,144,128]{3,2,1,0:T(8,128)(2,1)}, bf16[3,4,144,128]{3,2,1,0:T(8,128)(2,1)}, u32[]{:S(2)}, u32[]{:S(2)}) %collective-permute-start.26) | collective-permute-done | bytes 442400 | tf_op jit(solution)/shard_map/ppermute | solution.py:118
  118.8 11.1 %shard_map.37 = f32[2048,1024]{1,0:T(8,128)} custom-call(s32[288]{0:T(512)S(1)} %min.12.offs_ref, bf16[96,2,144,128]{3,2,1,0:T(8,128)(2,1)} %bitcast.45, bf16[96,144,128]{2,1,0:T(8,128)(2,1)S(1)} %bitcast.43), custom_call_target="tpu_custom_call" | custom-call | flops 805306368 | bytes 17825792 | tf_op jit(solution)/shard_map/pallas_call | solution.py:40
  (93 shorter events, 28.1 us)
Async XLA Ops:
  4.2 13.2 %collective-permute-start = (bf16[3,2,2,144,128]{4,3,2,1,0:T(8,128)(2,1)S(1)}, bf16[3,2,2,144,128]{4,3,2,1,0:T(8,128)(2,1)S(1)}, u32[]{:S(2)}, u32[]{:S(2)}) collective-permute-start(bf16[3,2,2,144,128]{4,3,2,1,0:T(8,128)(2,1)S(1)} %get-tuple-element.5), channel_id=1, source_target_pairs={{0,2},{2,4},{4,6},{6,7},{7,5},{5,3},{3,1},{1,0},{8,10},{10,12},{12... | collective-permute-start | bytes 1327112 | tf_op jit(solution)/shard_map/ppermute | solution.py:109
  7.3 11.9 %collective-permute-start.1 = (bf16[3,2,2,144,128]{4,3,2,1,0:T(8,128)(2,1)S(1)}, bf16[3,2,2,144,128]{4,3,2,1,0:T(8,128)(2,1)S(1)}, u32[]{:S(2)}, u32[]{:S(2)}) collective-permute-start(bf16[3,2,2,144,128]{4,3,2,1,0:T(8,128)(2,1)S(1)} %get-tuple-element.6), channel_id=1, source_target_pairs={{2,0},{4,2},{6,4},{7,6},{5,7},{3,5},{1,3},{0,1},{10,8},{12,10},{14... | collective-permute-start | bytes 1327112 | tf_op jit(solution)/shard_map/ppermute | solution.py:110
  17.4 11.4 %collective-permute-start.2 = (bf16[3,2,2,144,128]{4,3,2,1,0:T(8,128)(2,1)S(1)}, bf16[3,2,2,144,128]{4,3,2,1,0:T(8,128)(2,1)S(1)}, u32[]{:S(2)}, u32[]{:S(2)}) collective-permute-start(bf16[3,2,2,144,128]{4,3,2,1,0:T(8,128)(2,1)S(1)} %collective-permute-done), channel_id=1, source_target_pairs={{0,2},{2,4},{4,6},{6,7},{7,5},{5,3},{3,1},{1,0},{8,10},{10,12},{12... | collective-permute-start | bytes 1327112 | tf_op jit(solution)/shard_map/ppermute | solution.py:109
  19.2 11.0 %collective-permute-start.3 = (bf16[3,2,2,144,128]{4,3,2,1,0:T(8,128)(2,1)S(1)}, bf16[3,2,2,144,128]{4,3,2,1,0:T(8,128)(2,1)S(1)}, u32[]{:S(2)}, u32[]{:S(2)}) collective-permute-start(bf16[3,2,2,144,128]{4,3,2,1,0:T(8,128)(2,1)S(1)} %collective-permute-done.1), channel_id=1, source_target_pairs={{2,0},{4,2},{6,4},{7,6},{5,7},{3,5},{1,3},{0,1},{10,8},{12,10},{14... | collective-permute-start | bytes 1327112 | tf_op jit(solution)/shard_map/ppermute | solution.py:110
  19.6 23.7 %collective-permute-start.16 = (bf16[3,8,144,128]{3,2,1,0:T(8,128)(2,1)S(1)}, bf16[3,8,144,128]{3,2,1,0:T(8,128)(2,1)S(1)}, u32[]{:S(2)}, u32[]{:S(2)}) collective-permute-start(bf16[3,8,144,128]{3,2,1,0:T(8,128)(2,1)S(1)} %pad_maximum_fusion), channel_id=1, source_target_pairs={{0,8},{1,9},{10,18},{11,19},{20,28},{21,29},{30,6},{31,7}} | collective-permute-start | bytes 2654216 | tf_op jit(solution)/shard_map/ppermute | solution.py:118
  21.0 23.7 %collective-permute-start.15 = (bf16[3,8,144,128]{3,2,1,0:T(8,128)(2,1)S(1)}, bf16[3,8,144,128]{3,2,1,0:T(8,128)(2,1)S(1)}, u32[]{:S(2)}, u32[]{:S(2)}) collective-permute-start(bf16[3,8,144,128]{3,2,1,0:T(8,128)(2,1)S(1)} %pad_maximum_fusion), channel_id=1, source_target_pairs={{0,16},{1,17},{10,26},{11,27},{20,4},{21,5},{30,14},{31,15}} | collective-permute-start | bytes 2654216 | tf_op jit(solution)/shard_map/ppermute | solution.py:118
  24.0 23.0 %collective-permute-start.14 = (bf16[3,8,144,128]{3,2,1,0:T(8,128)(2,1)S(1)}, bf16[3,8,144,128]{3,2,1,0:T(8,128)(2,1)S(1)}, u32[]{:S(2)}, u32[]{:S(2)}) collective-permute-start(bf16[3,8,144,128]{3,2,1,0:T(8,128)(2,1)S(1)} %pad_maximum_fusion), channel_id=1, source_target_pairs={{0,24},{1,25},{10,2},{11,3},{20,12},{21,13},{30,22},{31,23}} | collective-permute-start | bytes 2654216 | tf_op jit(solution)/shard_map/ppermute | solution.py:118
  28.8 10.4 %collective-permute-start.4 = (bf16[3,2,2,144,128]{4,3,2,1,0:T(8,128)(2,1)S(1)}, bf16[3,2,2,144,128]{4,3,2,1,0:T(8,128)(2,1)S(1)}, u32[]{:S(2)}, u32[]{:S(2)}) collective-permute-start(bf16[3,2,2,144,128]{4,3,2,1,0:T(8,128)(2,1)S(1)} %collective-permute-done.2), channel_id=1, source_target_pairs={{0,2},{2,4},{4,6},{6,7},{7,5},{5,3},{3,1},{1,0},{8,10},{10,12},{12... | collective-permute-start | bytes 1327112 | tf_op jit(solution)/shard_map/ppermute | solution.py:109
  30.2 11.3 %collective-permute-start.5 = (bf16[3,2,2,144,128]{4,3,2,1,0:T(8,128)(2,1)S(1)}, bf16[3,2,2,144,128]{4,3,2,1,0:T(8,128)(2,1)S(1)}, u32[]{:S(2)}, u32[]{:S(2)}) collective-permute-start(bf16[3,2,2,144,128]{4,3,2,1,0:T(8,128)(2,1)S(1)} %collective-permute-done.3), channel_id=1, source_target_pairs={{2,0},{4,2},{6,4},{7,6},{5,7},{3,5},{1,3},{0,1},{10,8},{12,10},{14... | collective-permute-start | bytes 1327112 | tf_op jit(solution)/shard_map/ppermute | solution.py:110
  39.2 10.5 %collective-permute-start.6 = (bf16[3,2,2,144,128]{4,3,2,1,0:T(8,128)(2,1)S(1)}, bf16[3,2,2,144,128]{4,3,2,1,0:T(8,128)(2,1)S(1)}, u32[]{:S(2)}, u32[]{:S(2)}) collective-permute-start(bf16[3,2,2,144,128]{4,3,2,1,0:T(8,128)(2,1)S(1)} %collective-permute-done.4), channel_id=1, source_target_pairs={{0,2},{2,4},{4,6},{6,7},{7,5},{5,3},{3,1},{1,0},{8,10},{10,12},{12... | collective-permute-start | bytes 1327112 | tf_op jit(solution)/shard_map/ppermute | solution.py:109
  41.5 10.3 %collective-permute-start.7 = (bf16[3,2,2,144,128]{4,3,2,1,0:T(8,128)(2,1)S(1)}, bf16[3,2,2,144,128]{4,3,2,1,0:T(8,128)(2,1)S(1)}, u32[]{:S(2)}, u32[]{:S(2)}) collective-permute-start(bf16[3,2,2,144,128]{4,3,2,1,0:T(8,128)(2,1)S(1)} %collective-permute-done.5), channel_id=1, source_target_pairs={{2,0},{4,2},{6,4},{7,6},{5,7},{3,5},{1,3},{0,1},{10,8},{12,10},{14... | collective-permute-start | bytes 1327112 | tf_op jit(solution)/shard_map/ppermute | solution.py:110
  43.4 23.0 %collective-permute-start.19 = (bf16[3,8,144,128]{3,2,1,0:T(8,128)(2,1)S(1)}, bf16[3,8,144,128]{3,2,1,0:T(8,128)(2,1)S(1)}, u32[]{:S(2)}, u32[]{:S(2)}) collective-permute-start(bf16[3,8,144,128]{3,2,1,0:T(8,128)(2,1)S(1)} %pad_maximum_fusion.1), channel_id=1, source_target_pairs={{0,8},{1,9},{10,18},{11,19},{20,28},{21,29},{30,6},{31,7}} | collective-permute-start | bytes 2654216 | tf_op jit(solution)/shard_map/ppermute | solution.py:118
  44.7 25.5 %collective-permute-start.18 = (bf16[3,8,144,128]{3,2,1,0:T(8,128)(2,1)S(1)}, bf16[3,8,144,128]{3,2,1,0:T(8,128)(2,1)S(1)}, u32[]{:S(2)}, u32[]{:S(2)}) collective-permute-start(bf16[3,8,144,128]{3,2,1,0:T(8,128)(2,1)S(1)} %pad_maximum_fusion.1), channel_id=1, source_target_pairs={{0,16},{1,17},{10,26},{11,27},{20,4},{21,5},{30,14},{31,15}} | collective-permute-start | bytes 2654216 | tf_op jit(solution)/shard_map/ppermute | solution.py:118
  47.1 24.5 %collective-permute-start.17 = (bf16[3,8,144,128]{3,2,1,0:T(8,128)(2,1)S(1)}, bf16[3,8,144,128]{3,2,1,0:T(8,128)(2,1)S(1)}, u32[]{:S(2)}, u32[]{:S(2)}) collective-permute-start(bf16[3,8,144,128]{3,2,1,0:T(8,128)(2,1)S(1)} %pad_maximum_fusion.1), channel_id=1, source_target_pairs={{0,24},{1,25},{10,2},{11,3},{20,12},{21,13},{30,22},{31,23}} | collective-permute-start | bytes 2654216 | tf_op jit(solution)/shard_map/ppermute | solution.py:118
  49.7 11.2 %collective-permute-start.8 = (bf16[3,2,2,144,128]{4,3,2,1,0:T(8,128)(2,1)S(1)}, bf16[3,2,2,144,128]{4,3,2,1,0:T(8,128)(2,1)S(1)}, u32[]{:S(2)}, u32[]{:S(2)}) collective-permute-start(bf16[3,2,2,144,128]{4,3,2,1,0:T(8,128)(2,1)S(1)} %collective-permute-done.6), channel_id=1, source_target_pairs={{0,2},{2,4},{4,6},{6,7},{7,5},{5,3},{3,1},{1,0},{8,10},{10,12},{12... | collective-permute-start | bytes 1327112 | tf_op jit(solution)/shard_map/ppermute | solution.py:109
  51.8 11.2 %collective-permute-start.9 = (bf16[3,2,2,144,128]{4,3,2,1,0:T(8,128)(2,1)S(1)}, bf16[3,2,2,144,128]{4,3,2,1,0:T(8,128)(2,1)S(1)}, u32[]{:S(2)}, u32[]{:S(2)}) collective-permute-start(bf16[3,2,2,144,128]{4,3,2,1,0:T(8,128)(2,1)S(1)} %collective-permute-done.7), channel_id=1, source_target_pairs={{2,0},{4,2},{6,4},{7,6},{5,7},{3,5},{1,3},{0,1},{10,8},{12,10},{14... | collective-permute-start | bytes 1327112 | tf_op jit(solution)/shard_map/ppermute | solution.py:110
  63.2 33.1 %collective-permute-start.22 = (bf16[3,8,144,128]{3,2,1,0:T(8,128)(2,1)S(1)}, bf16[3,8,144,128]{3,2,1,0:T(8,128)(2,1)S(1)}, u32[]{:S(2)}, u32[]{:S(2)}) collective-permute-start(bf16[3,8,144,128]{3,2,1,0:T(8,128)(2,1)S(1)} %pad_maximum_fusion.2), channel_id=1, source_target_pairs={{0,8},{1,9},{10,18},{11,19},{20,28},{21,29},{30,6},{31,7}} | collective-permute-start | bytes 2654216 | tf_op jit(solution)/shard_map/ppermute | solution.py:118
  64.6 10.3 %collective-permute-start.10 = (bf16[3,2,2,144,128]{4,3,2,1,0:T(8,128)(2,1)S(1)}, bf16[3,2,2,144,128]{4,3,2,1,0:T(8,128)(2,1)S(1)}, u32[]{:S(2)}, u32[]{:S(2)}) collective-permute-start(bf16[3,2,2,144,128]{4,3,2,1,0:T(8,128)(2,1)S(1)} %collective-permute-done.8), channel_id=1, source_target_pairs={{0,2},{2,4},{4,6},{6,7},{7,5},{5,3},{3,1},{1,0},{8,10},{10,12},{12... | collective-permute-start | bytes 1327112 | tf_op jit(solution)/shard_map/ppermute | solution.py:109
  66.4 32.1 %collective-permute-start.21 = (bf16[3,8,144,128]{3,2,1,0:T(8,128)(2,1)S(1)}, bf16[3,8,144,128]{3,2,1,0:T(8,128)(2,1)S(1)}, u32[]{:S(2)}, u32[]{:S(2)}) collective-permute-start(bf16[3,8,144,128]{3,2,1,0:T(8,128)(2,1)S(1)} %pad_maximum_fusion.2), channel_id=1, source_target_pairs={{0,16},{1,17},{10,26},{11,27},{20,4},{21,5},{30,14},{31,15}} | collective-permute-start | bytes 2654216 | tf_op jit(solution)/shard_map/ppermute | solution.py:118
  70.2 30.3 %collective-permute-start.20 = (bf16[3,8,144,128]{3,2,1,0:T(8,128)(2,1)S(1)}, bf16[3,8,144,128]{3,2,1,0:T(8,128)(2,1)S(1)}, u32[]{:S(2)}, u32[]{:S(2)}) collective-permute-start(bf16[3,8,144,128]{3,2,1,0:T(8,128)(2,1)S(1)} %pad_maximum_fusion.2), channel_id=1, source_target_pairs={{0,24},{1,25},{10,2},{11,3},{20,12},{21,13},{30,22},{31,23}} | collective-permute-start | bytes 2654216 | tf_op jit(solution)/shard_map/ppermute | solution.py:118
  71.6 10.8 %collective-permute-start.11 = (bf16[3,2,2,144,128]{4,3,2,1,0:T(8,128)(2,1)S(1)}, bf16[3,2,2,144,128]{4,3,2,1,0:T(8,128)(2,1)S(1)}, u32[]{:S(2)}, u32[]{:S(2)}) collective-permute-start(bf16[3,2,2,144,128]{4,3,2,1,0:T(8,128)(2,1)S(1)} %collective-permute-done.9), channel_id=1, source_target_pairs={{2,0},{4,2},{6,4},{7,6},{5,7},{3,5},{1,3},{0,1},{10,8},{12,10},{14... | collective-permute-start | bytes 1327112 | tf_op jit(solution)/shard_map/ppermute | solution.py:110
  74.9 25.6 %copy-start = (bf16[3,2,144,128]{3,2,1,0:T(8,128)(2,1)}, bf16[3,2,144,128]{3,2,1,0:T(8,128)(2,1)S(1)}, u32[]{:S(2)}) copy-start(bf16[3,2,144,128]{3,2,1,0:T(8,128)(2,1)S(1)} %dynamic-slice_bitcast_fusion.3) | copy-start | bytes 663556
  74.9 12.6 %collective-permute-start.12 = (bf16[3,2,2,144,128]{4,3,2,1,0:T(8,128)(2,1)S(1)}, bf16[3,2,2,144,128]{4,3,2,1,0:T(8,128)(2,1)S(1)}, u32[]{:S(2)}, u32[]{:S(2)}) collective-permute-start(bf16[3,2,2,144,128]{4,3,2,1,0:T(8,128)(2,1)S(1)} %collective-permute-done.10), channel_id=1, source_target_pairs={{0,2},{2,4},{4,6},{6,7},{7,5},{5,3},{3,1},{1,0},{8,10},{10,12},{12... | collective-permute-start | bytes 1327112 | tf_op jit(solution)/shard_map/ppermute | solution.py:109
  82.3 9.8 %collective-permute-start.13 = (bf16[3,2,2,144,128]{4,3,2,1,0:T(8,128)(2,1)S(1)}, bf16[3,2,2,144,128]{4,3,2,1,0:T(8,128)(2,1)S(1)}, u32[]{:S(2)}, u32[]{:S(2)}) collective-permute-start(bf16[3,2,2,144,128]{4,3,2,1,0:T(8,128)(2,1)S(1)} %collective-permute-done.11), channel_id=1, source_target_pairs={{2,0},{4,2},{6,4},{7,6},{5,7},{3,5},{1,3},{0,1},{10,8},{12,10},{14... | collective-permute-start | bytes 1327112 | tf_op jit(solution)/shard_map/ppermute | solution.py:110
  87.5 15.6 %collective-permute-start.25 = (bf16[3,4,144,128]{3,2,1,0:T(8,128)(2,1)}, bf16[3,4,144,128]{3,2,1,0:T(8,128)(2,1)S(1)}, u32[]{:S(2)}, u32[]{:S(2)}) collective-permute-start(bf16[3,4,144,128]{3,2,1,0:T(8,128)(2,1)} %pad_maximum_fusion.3), channel_id=1, source_target_pairs={{0,8},{1,9},{10,18},{11,19},{20,28},{21,29},{30,6},{31,7}} | collective-permute-start | bytes 1327112 | tf_op jit(solution)/shard_map/ppermute | solution.py:118
  89.1 11.4 %copy-start.1 = (bf16[3,2,144,128]{3,2,1,0:T(8,128)(2,1)}, bf16[3,2,144,128]{3,2,1,0:T(8,128)(2,1)S(1)}, u32[]{:S(2)}) copy-start(bf16[3,2,144,128]{3,2,1,0:T(8,128)(2,1)S(1)} %dynamic-slice_bitcast_fusion.1) | copy-start | bytes 663556
  92.1 17.6 %collective-permute-start.24 = (bf16[3,4,144,128]{3,2,1,0:T(8,128)(2,1)}, bf16[3,4,144,128]{3,2,1,0:T(8,128)(2,1)}, u32[]{:S(2)}, u32[]{:S(2)}) collective-permute-start(bf16[3,4,144,128]{3,2,1,0:T(8,128)(2,1)} %pad_maximum_fusion.3), channel_id=1, source_target_pairs={{0,16},{1,17},{10,26},{11,27},{20,4},{21,5},{30,14},{31,15}} | collective-permute-start | bytes 1327112 | tf_op jit(solution)/shard_map/ppermute | solution.py:118
  95.5 5.0 %copy-start.3 = (bf16[3,2,144,128]{3,2,1,0:T(8,128)(2,1)}, bf16[3,2,144,128]{3,2,1,0:T(8,128)(2,1)S(1)}, u32[]{:S(2)}) copy-start(bf16[3,2,144,128]{3,2,1,0:T(8,128)(2,1)S(1)} %dynamic-slice_bitcast_fusion) | copy-start | bytes 663556
  96.4 13.3 %collective-permute-start.23 = (bf16[3,4,144,128]{3,2,1,0:T(8,128)(2,1)}, bf16[3,4,144,128]{3,2,1,0:T(8,128)(2,1)}, u32[]{:S(2)}, u32[]{:S(2)}) collective-permute-start(bf16[3,4,144,128]{3,2,1,0:T(8,128)(2,1)} %pad_maximum_fusion.3), channel_id=1, source_target_pairs={{0,24},{1,25},{10,2},{11,3},{20,12},{21,13},{30,22},{31,23}} | collective-permute-start | bytes 1327112 | tf_op jit(solution)/shard_map/ppermute | solution.py:118
  98.4 12.6 %collective-permute-start.28 = (bf16[3,4,144,128]{3,2,1,0:T(8,128)(2,1)}, bf16[3,4,144,128]{3,2,1,0:T(8,128)(2,1)}, u32[]{:S(2)}, u32[]{:S(2)}) collective-permute-start(bf16[3,4,144,128]{3,2,1,0:T(8,128)(2,1)} %pad_maximum_fusion.4), channel_id=1, source_target_pairs={{0,8},{1,9},{10,18},{11,19},{20,28},{21,29},{30,6},{31,7}} | collective-permute-start | bytes 1327112 | tf_op jit(solution)/shard_map/ppermute | solution.py:118
  100.5 10.5 %collective-permute-start.27 = (bf16[3,4,144,128]{3,2,1,0:T(8,128)(2,1)}, bf16[3,4,144,128]{3,2,1,0:T(8,128)(2,1)}, u32[]{:S(2)}, u32[]{:S(2)}) collective-permute-start(bf16[3,4,144,128]{3,2,1,0:T(8,128)(2,1)} %pad_maximum_fusion.4), channel_id=1, source_target_pairs={{0,16},{1,17},{10,26},{11,27},{20,4},{21,5},{30,14},{31,15}} | collective-permute-start | bytes 1327112 | tf_op jit(solution)/shard_map/ppermute | solution.py:118
  103.1 11.9 %collective-permute-start.26 = (bf16[3,4,144,128]{3,2,1,0:T(8,128)(2,1)}, bf16[3,4,144,128]{3,2,1,0:T(8,128)(2,1)}, u32[]{:S(2)}, u32[]{:S(2)}) collective-permute-start(bf16[3,4,144,128]{3,2,1,0:T(8,128)(2,1)} %pad_maximum_fusion.4), channel_id=1, source_target_pairs={{0,24},{1,25},{10,2},{11,3},{20,12},{21,13},{30,22},{31,23}} | collective-permute-start | bytes 1327112 | tf_op jit(solution)/shard_map/ppermute | solution.py:118
  (2 other events, 8.7 us)

commit v15 on v14

--- a/solution.py
+++ b/solution.py
@@ -12,13 +12,14 @@
 META = 16
 
 
-def gram_kernel(offs_ref, bs_ref, bc_ref, o_ref, *, chunk, local_slots, blk):
+def gram_kernel(offs_ref, bs_ref, bc_ref, o_ref, seen_ref, *, chunk, local_slots, blk):
     s = pl.program_id(0)
     step = pl.program_id(1)
 
     @pl.when(step == 0)
     def _():
-        o_ref[...] = jnp.zeros_like(o_ref)
+        for q in range(IBS * IBS):
+            seen_ref[q] = 0
 
     stride = local_slots + 1
     for k in range(chunk):
@@ -27,9 +28,33 @@
         w = meta[0:1] + meta[1:2] + meta[2:3]
         lhs = (bs_ref[k, 0, :blk].astype(jnp.float32).T * w).astype(jnp.bfloat16)
         prod = jnp.dot(lhs, bc_ref[k, :blk], preferred_element_type=jnp.float32)
-        col = pl.multiple_of(offs_ref[g * stride + local_slots] * blk, blk)
-        row = pl.multiple_of(offs_ref[g * stride + s] * blk, blk)
-        o_ref[pl.ds(row, blk), pl.ds(col, blk)] += prod
+        ci = offs_ref[g * stride + local_slots]
+        ri = offs_ref[g * stride + s]
+        q = ri * IBS + ci
+        col = pl.multiple_of(ci * blk, blk)
+        row = pl.multiple_of(ri * blk, blk)
+        first = seen_ref[q] == 0
+
+        @pl.when(first)
+        def _():
+            o_ref[pl.ds(row, blk), pl.ds(col, blk)] = prod
+
+        @pl.when(jnp.logical_not(first))
+        def _():
+            o_ref[pl.ds(row, blk), pl.ds(col, blk)] += prod
+
+        seen_ref[q] = 1
+
+    @pl.when(step == pl.num_programs(1) - 1)
+    def _():
+        for q in range(IBS * IBS):
+            i, j = divmod(q, IBS)
+
+            @pl.when(seen_ref[q] == 0)
+            def _():
+                o_ref[i * blk : (i + 1) * blk, j * blk : (j + 1) * blk] = jnp.zeros(
+                    (blk, blk), jnp.float32
+                )
 
 
 def gram_call(offs, bs, bc):
@@ -47,6 +72,7 @@
                 pl.BlockSpec((chunk, rows, blk), lambda s, i, o: (i, 0, 0)),
             ],
             out_specs=pl.BlockSpec((IBS * blk, out_cols), lambda s, i, o: (s, 0)),
+            scratch_shapes=[pltpu.SMEM((IBS * IBS,), jnp.int32)],
         ),
         out_shape=jax.ShapeDtypeStruct((out_rows, out_cols), jnp.float32),
         compiler_params=pltpu.CompilerParams(

time: 131 us -> 168 us (1.28)
  Pallas kernels: 11.1 us -> 48.4 us
    pallas_call x1, Pallas kernels: 11.1 us -> 48.4 us  [gram_call(): pl.pallas_call(kernel, grid_spec=pltpu.PrefetchScalarGridSpec(num_scalar_...]
  transfers between devices with their start and end apart: 29 -> 29, of which waited for: 11 -> 11; matrix products, arithmetic and copies ran while one was open for 15% -> 12% of each run, Pallas kernels for 0% -> 0%
where the time goes in v15:
time: 168 us; the launch traced here: 167 us
  Pallas kernels  48.4 us (29%)
  waiting for transfers between devices  47 us (28%)
  starting transfers between devices  43.6 us (26%)
  local copies, waits for them, and re-layouts  17.8 us (11%)
  other arithmetic  10 us (6%)
    pallas_call x1, Pallas kernels, gram_call(): pl.pallas_call(kernel, grid_spec=pltpu.PrefetchScalarGridSpec(num_scalar_...  48.4 us
    ppermute x7, waiting for transfers between devices, local(): a = lax.ppermute(a, 'col', forward)  31.5 us
    ppermute x15, starting transfers between devices, local(): got = jnp.where(which == j, lax.ppermute(own, ('row', 'col'), fan), got)  30.5 us
    ppermute x7, starting transfers between devices, local(): a = lax.ppermute(a, 'col', forward)  11.9 us
    ppermute x7, waiting for transfers between devices, local(): b = lax.ppermute(b, 'col', backward)  11.5 us
    unnamed x23, local copies, waits for them, and re-layouts  11.1 us
    unnamed x5, other arithmetic  5.26 us
    ppermute x15, waiting for transfers between devices, local(): got = jnp.where(which == j, lax.ppermute(own, ('row', 'col'), fan), got)  4.03 us
  transfers between devices with their start and end apart: 29, of which 11 were waited for; matrix products, arithmetic and copies ran while one was open for 12% of the time, Pallas kernels for 0%

profile of v15, /device:TPU:0, one launch (start us, length us, event | category | flops | bytes accessed | tf_op | source)
XLA Modules:
  0.0 167.2 jit_solution(1462740500755946417)
XLA Ops:
  1.7 2.4 %constant_dynamic-update-slice_fusion.14 = (bf16[3,32,2,144,128]{4,3,2,1,0:T(8,128)(2,1)}, bf16[3,4,2,144,128]{4,3,2,1,0:T(8,128)(2,1)S(1)}) fusion(bf16[144]{0:T(256)(128)(2,1)S(1)} %pad.21.clone, bf16[3,4,2,1,128]{4,3,2,1,0:T(2,128)(2,1)S(1)} %broadcast_in_dim.7, bf16[3,4,2,3,128]{4,3,2,1,0:T(4,128)(2,1)S(1)} %broadcast_in_dim.6, ...), kind=kLoop, calls=%fused_computation.42 | loop fusion | flops 3538943 | bytes 2580768
  4.2 3.1 %collective-permute-start = (bf16[3,2,2,144,128]{4,3,2,1,0:T(8,128)(2,1)S(1)}, bf16[3,2,2,144,128]{4,3,2,1,0:T(8,128)(2,1)S(1)}, u32[]{:S(2)}, u32[]{:S(2)}) collective-permute-start(bf16[3,2,2,144,128]{4,3,2,1,0:T(8,128)(2,1)S(1)} %get-tuple-element.5), channel_id=1, source_target_pairs={{0,2},{2,4},{4,6},{6,7},{7,5},{5,3},{3,1},{1,0},{8,10},{10,12},{12... | collective-permute-start | bytes 1327112 | tf_op jit(solution)/shard_map/ppermute | solution.py:135
  7.3 10.1 %collective-permute-done = bf16[3,2,2,144,128]{4,3,2,1,0:T(8,128)(2,1)S(1)} collective-permute-done((bf16[3,2,2,144,128]{4,3,2,1,0:T(8,128)(2,1)S(1)}, bf16[3,2,2,144,128]{4,3,2,1,0:T(8,128)(2,1)S(1)}, u32[]{:S(2)}, u32[]{:S(2)}) %collective-permute-start) | collective-permute-done | bytes 442400 | tf_op jit(solution)/shard_map/ppermute | solution.py:135
  17.4 1.8 %collective-permute-start.2 = (bf16[3,2,2,144,128]{4,3,2,1,0:T(8,128)(2,1)S(1)}, bf16[3,2,2,144,128]{4,3,2,1,0:T(8,128)(2,1)S(1)}, u32[]{:S(2)}, u32[]{:S(2)}) collective-permute-start(bf16[3,2,2,144,128]{4,3,2,1,0:T(8,128)(2,1)S(1)} %collective-permute-done), channel_id=1, source_target_pairs={{0,2},{2,4},{4,6},{6,7},{7,5},{5,3},{3,1},{1,0},{8,10},{10,12},{12... | collective-permute-start | bytes 1327112 | tf_op jit(solution)/shard_map/ppermute | solution.py:135
  19.6 1.3 collective-permute-start.16
  21.0 3.0 %collective-permute-start.15 = (bf16[3,8,144,128]{3,2,1,0:T(8,128)(2,1)S(1)}, bf16[3,8,144,128]{3,2,1,0:T(8,128)(2,1)S(1)}, u32[]{:S(2)}, u32[]{:S(2)}) collective-permute-start(bf16[3,8,144,128]{3,2,1,0:T(8,128)(2,1)S(1)} %pad_maximum_fusion), channel_id=1, source_target_pairs={{0,16},{1,17},{10,26},{11,27},{20,4},{21,5},{30,14},{31,15}} | collective-permute-start | bytes 2654216 | tf_op jit(solution)/shard_map/ppermute | solution.py:144
  24.0 1.3 collective-permute-start.14
  27.1 1.6 collective-permute-done.2
  28.8 1.5 collective-permute-start.4
  32.5 6.6 %collective-permute-done.4 = bf16[3,2,2,144,128]{4,3,2,1,0:T(8,128)(2,1)S(1)} collective-permute-done((bf16[3,2,2,144,128]{4,3,2,1,0:T(8,128)(2,1)S(1)}, bf16[3,2,2,144,128]{4,3,2,1,0:T(8,128)(2,1)S(1)}, u32[]{:S(2)}, u32[]{:S(2)}) %collective-permute-start.4) | collective-permute-done | bytes 442400 | tf_op jit(solution)/shard_map/ppermute | solution.py:135
  39.2 2.3 %collective-permute-start.6 = (bf16[3,2,2,144,128]{4,3,2,1,0:T(8,128)(2,1)S(1)}, bf16[3,2,2,144,128]{4,3,2,1,0:T(8,128)(2,1)S(1)}, u32[]{:S(2)}, u32[]{:S(2)}) collective-permute-start(bf16[3,2,2,144,128]{4,3,2,1,0:T(8,128)(2,1)S(1)} %collective-permute-done.4), channel_id=1, source_target_pairs={{0,2},{2,4},{4,6},{6,7},{7,5},{5,3},{3,1},{1,0},{8,10},{10,12},{12... | collective-permute-start | bytes 1327112 | tf_op jit(solution)/shard_map/ppermute | solution.py:135
  44.7 2.3 %collective-permute-start.18 = (bf16[3,8,144,128]{3,2,1,0:T(8,128)(2,1)S(1)}, bf16[3,8,144,128]{3,2,1,0:T(8,128)(2,1)S(1)}, u32[]{:S(2)}, u32[]{:S(2)}) collective-permute-start(bf16[3,8,144,128]{3,2,1,0:T(8,128)(2,1)S(1)} %pad_maximum_fusion.1), channel_id=1, source_target_pairs={{0,16},{1,17},{10,26},{11,27},{20,4},{21,5},{30,14},{31,15}} | collective-permute-start | bytes 2654216 | tf_op jit(solution)/shard_map/ppermute | solution.py:144
  47.1 1.3 collective-permute-start.17
  49.7 2.1 %collective-permute-start.8 = (bf16[3,2,2,144,128]{4,3,2,1,0:T(8,128)(2,1)S(1)}, bf16[3,2,2,144,128]{4,3,2,1,0:T(8,128)(2,1)S(1)}, u32[]{:S(2)}, u32[]{:S(2)}) collective-permute-start(bf16[3,2,2,144,128]{4,3,2,1,0:T(8,128)(2,1)S(1)} %collective-permute-done.6), channel_id=1, source_target_pairs={{0,2},{2,4},{4,6},{6,7},{7,5},{5,3},{3,1},{1,0},{8,10},{10,12},{12... | collective-permute-start | bytes 1327112 | tf_op jit(solution)/shard_map/ppermute | solution.py:135
  53.6 7.3 %collective-permute-done.8 = bf16[3,2,2,144,128]{4,3,2,1,0:T(8,128)(2,1)S(1)} collective-permute-done((bf16[3,2,2,144,128]{4,3,2,1,0:T(8,128)(2,1)S(1)}, bf16[3,2,2,144,128]{4,3,2,1,0:T(8,128)(2,1)S(1)}, u32[]{:S(2)}, u32[]{:S(2)}) %collective-permute-start.8) | collective-permute-done | bytes 442400 | tf_op jit(solution)/shard_map/ppermute | solution.py:135
  60.9 2.2 %collective-permute-done.9 = bf16[3,2,2,144,128]{4,3,2,1,0:T(8,128)(2,1)S(1)} collective-permute-done((bf16[3,2,2,144,128]{4,3,2,1,0:T(8,128)(2,1)S(1)}, bf16[3,2,2,144,128]{4,3,2,1,0:T(8,128)(2,1)S(1)}, u32[]{:S(2)}, u32[]{:S(2)}) %collective-permute-start.9) | collective-permute-done | bytes 442400 | tf_op jit(solution)/shard_map/ppermute | solution.py:136
  63.2 1.3 collective-permute-start.22
  66.4 3.8 %collective-permute-start.21 = (bf16[3,8,144,128]{3,2,1,0:T(8,128)(2,1)S(1)}, bf16[3,8,144,128]{3,2,1,0:T(8,128)(2,1)S(1)}, u32[]{:S(2)}, u32[]{:S(2)}) collective-permute-start(bf16[3,8,144,128]{3,2,1,0:T(8,128)(2,1)S(1)} %pad_maximum_fusion.2), channel_id=1, source_target_pairs={{0,16},{1,17},{10,26},{11,27},{20,4},{21,5},{30,14},{31,15}} | collective-permute-start | bytes 2654216 | tf_op jit(solution)/shard_map/ppermute | solution.py:144
  70.2 1.3 collective-permute-start.20
  72.2 2.8 %collective-permute-done.10 = bf16[3,2,2,144,128]{4,3,2,1,0:T(8,128)(2,1)S(1)} collective-permute-done((bf16[3,2,2,144,128]{4,3,2,1,0:T(8,128)(2,1)S(1)}, bf16[3,2,2,144,128]{4,3,2,1,0:T(8,128)(2,1)S(1)}, u32[]{:S(2)}, u32[]{:S(2)}) %collective-permute-start.10) | collective-permute-done | bytes 442400 | tf_op jit(solution)/shard_map/ppermute | solution.py:135
  76.0 6.3 %collective-permute-done.11 = bf16[3,2,2,144,128]{4,3,2,1,0:T(8,128)(2,1)S(1)} collective-permute-done((bf16[3,2,2,144,128]{4,3,2,1,0:T(8,128)(2,1)S(1)}, bf16[3,2,2,144,128]{4,3,2,1,0:T(8,128)(2,1)S(1)}, u32[]{:S(2)}, u32[]{:S(2)}) %collective-permute-start.11) | collective-permute-done | bytes 442400 | tf_op jit(solution)/shard_map/ppermute | solution.py:136
  85.2 2.3 %collective-permute-done.12 = bf16[3,2,2,144,128]{4,3,2,1,0:T(8,128)(2,1)S(1)} collective-permute-done((bf16[3,2,2,144,128]{4,3,2,1,0:T(8,128)(2,1)S(1)}, bf16[3,2,2,144,128]{4,3,2,1,0:T(8,128)(2,1)S(1)}, u32[]{:S(2)}, u32[]{:S(2)}) %collective-permute-start.12) | collective-permute-done | bytes 442400 | tf_op jit(solution)/shard_map/ppermute | solution.py:135
  87.5 1.6 collective-permute-start.25
  89.1 3.0 %collective-permute-done.13 = bf16[3,2,2,144,128]{4,3,2,1,0:T(8,128)(2,1)S(1)} collective-permute-done((bf16[3,2,2,144,128]{4,3,2,1,0:T(8,128)(2,1)S(1)}, bf16[3,2,2,144,128]{4,3,2,1,0:T(8,128)(2,1)S(1)}, u32[]{:S(2)}, u32[]{:S(2)}) %collective-permute-start.13) | collective-permute-done | bytes 442400 | tf_op jit(solution)/shard_map/ppermute | solution.py:136
  92.1 3.4 %collective-permute-start.24 = (bf16[3,4,144,128]{3,2,1,0:T(8,128)(2,1)}, bf16[3,4,144,128]{3,2,1,0:T(8,128)(2,1)}, u32[]{:S(2)}, u32[]{:S(2)}) collective-permute-start(bf16[3,4,144,128]{3,2,1,0:T(8,128)(2,1)} %pad_maximum_fusion.3), channel_id=1, source_target_pairs={{0,16},{1,17},{10,26},{11,27},{20,4},{21,5},{30,14},{31,15}} | collective-permute-start | bytes 1327112 | tf_op jit(solution)/shard_map/ppermute | solution.py:144
  96.4 2.1 %collective-permute-start.23 = (bf16[3,4,144,128]{3,2,1,0:T(8,128)(2,1)}, bf16[3,4,144,128]{3,2,1,0:T(8,128)(2,1)}, u32[]{:S(2)}, u32[]{:S(2)}) collective-permute-start(bf16[3,4,144,128]{3,2,1,0:T(8,128)(2,1)} %pad_maximum_fusion.3), channel_id=1, source_target_pairs={{0,24},{1,25},{10,2},{11,3},{20,12},{21,13},{30,22},{31,23}} | collective-permute-start | bytes 1327112 | tf_op jit(solution)/shard_map/ppermute | solution.py:144
  98.4 2.1 %collective-permute-start.28 = (bf16[3,4,144,128]{3,2,1,0:T(8,128)(2,1)}, bf16[3,4,144,128]{3,2,1,0:T(8,128)(2,1)}, u32[]{:S(2)}, u32[]{:S(2)}) collective-permute-start(bf16[3,4,144,128]{3,2,1,0:T(8,128)(2,1)} %pad_maximum_fusion.4), channel_id=1, source_target_pairs={{0,8},{1,9},{10,18},{11,19},{20,28},{21,29},{30,6},{31,7}} | collective-permute-start | bytes 1327112 | tf_op jit(solution)/shard_map/ppermute | solution.py:144
  100.5 2.1 %collective-permute-start.27 = (bf16[3,4,144,128]{3,2,1,0:T(8,128)(2,1)}, bf16[3,4,144,128]{3,2,1,0:T(8,128)(2,1)}, u32[]{:S(2)}, u32[]{:S(2)}) collective-permute-start(bf16[3,4,144,128]{3,2,1,0:T(8,128)(2,1)} %pad_maximum_fusion.4), channel_id=1, source_target_pairs={{0,16},{1,17},{10,26},{11,27},{20,4},{21,5},{30,14},{31,15}} | collective-permute-start | bytes 1327112 | tf_op jit(solution)/shard_map/ppermute | solution.py:144
  103.1 2.1 %collective-permute-start.26 = (bf16[3,4,144,128]{3,2,1,0:T(8,128)(2,1)}, bf16[3,4,144,128]{3,2,1,0:T(8,128)(2,1)}, u32[]{:S(2)}, u32[]{:S(2)}) collective-permute-start(bf16[3,4,144,128]{3,2,1,0:T(8,128)(2,1)} %pad_maximum_fusion.4), channel_id=1, source_target_pairs={{0,24},{1,25},{10,2},{11,3},{20,12},{21,13},{30,22},{31,23}} | collective-permute-start | bytes 1327112 | tf_op jit(solution)/shard_map/ppermute | solution.py:144
  107.0 1.7 %slice.19 = bf16[96,2,1,1]{3,2,1,0:T(2,128)(2,1)} slice(bf16[96,2,144,128]{3,2,1,0:T(8,128)(2,1)} %bitcast.44), slice={[0:96], [0:2], [131:132], [0:1]} | slice | bytes 768 | tf_op jit(solution)/shard_map/slice | solution.py:153
  111.0 4.0 %collective-permute-done.26 = bf16[3,4,144,128]{3,2,1,0:T(8,128)(2,1)} collective-permute-done((bf16[3,4,144,128]{3,2,1,0:T(8,128)(2,1)}, bf16[3,4,144,128]{3,2,1,0:T(8,128)(2,1)}, u32[]{:S(2)}, u32[]{:S(2)}) %collective-permute-start.26) | collective-permute-done | bytes 442400 | tf_op jit(solution)/shard_map/ppermute | solution.py:144
  118.8 48.4 %shard_map.37 = f32[2048,1024]{1,0:T(8,128)} custom-call(s32[288]{0:T(512)S(1)} %min.12.offs_ref, bf16[96,2,144,128]{3,2,1,0:T(8,128)(2,1)} %bitcast.45, bf16[96,144,128]{2,1,0:T(8,128)(2,1)S(1)} %bitcast.43), custom_call_target="tpu_custom_call" | custom-call | flops 805306368 | bytes 17825792 | tf_op jit(solution)/shard_map/pallas_call | solution.py:65
  (93 shorter events, 28.1 us)
Async XLA Ops:
  4.2 13.2 %collective-permute-start = (bf16[3,2,2,144,128]{4,3,2,1,0:T(8,128)(2,1)S(1)}, bf16[3,2,2,144,128]{4,3,2,1,0:T(8,128)(2,1)S(1)}, u32[]{:S(2)}, u32[]{:S(2)}) collective-permute-start(bf16[3,2,2,144,128]{4,3,2,1,0:T(8,128)(2,1)S(1)} %get-tuple-element.5), channel_id=1, source_target_pairs={{0,2},{2,4},{4,6},{6,7},{7,5},{5,3},{3,1},{1,0},{8,10},{10,12},{12... | collective-permute-start | bytes 1327112 | tf_op jit(solution)/shard_map/ppermute | solution.py:135
  7.3 11.9 %collective-permute-start.1 = (bf16[3,2,2,144,128]{4,3,2,1,0:T(8,128)(2,1)S(1)}, bf16[3,2,2,144,128]{4,3,2,1,0:T(8,128)(2,1)S(1)}, u32[]{:S(2)}, u32[]{:S(2)}) collective-permute-start(bf16[3,2,2,144,128]{4,3,2,1,0:T(8,128)(2,1)S(1)} %get-tuple-element.6), channel_id=1, source_target_pairs={{2,0},{4,2},{6,4},{7,6},{5,7},{3,5},{1,3},{0,1},{10,8},{12,10},{14... | collective-permute-start | bytes 1327112 | tf_op jit(solution)/shard_map/ppermute | solution.py:136
  17.4 11.4 %collective-permute-start.2 = (bf16[3,2,2,144,128]{4,3,2,1,0:T(8,128)(2,1)S(1)}, bf16[3,2,2,144,128]{4,3,2,1,0:T(8,128)(2,1)S(1)}, u32[]{:S(2)}, u32[]{:S(2)}) collective-permute-start(bf16[3,2,2,144,128]{4,3,2,1,0:T(8,128)(2,1)S(1)} %collective-permute-done), channel_id=1, source_target_pairs={{0,2},{2,4},{4,6},{6,7},{7,5},{5,3},{3,1},{1,0},{8,10},{10,12},{12... | collective-permute-start | bytes 1327112 | tf_op jit(solution)/shard_map/ppermute | solution.py:135
  19.2 11.0 %collective-permute-start.3 = (bf16[3,2,2,144,128]{4,3,2,1,0:T(8,128)(2,1)S(1)}, bf16[3,2,2,144,128]{4,3,2,1,0:T(8,128)(2,1)S(1)}, u32[]{:S(2)}, u32[]{:S(2)}) collective-permute-start(bf16[3,2,2,144,128]{4,3,2,1,0:T(8,128)(2,1)S(1)} %collective-permute-done.1), channel_id=1, source_target_pairs={{2,0},{4,2},{6,4},{7,6},{5,7},{3,5},{1,3},{0,1},{10,8},{12,10},{14... | collective-permute-start | bytes 1327112 | tf_op jit(solution)/shard_map/ppermute | solution.py:136
  19.6 23.7 %collective-permute-start.16 = (bf16[3,8,144,128]{3,2,1,0:T(8,128)(2,1)S(1)}, bf16[3,8,144,128]{3,2,1,0:T(8,128)(2,1)S(1)}, u32[]{:S(2)}, u32[]{:S(2)}) collective-permute-start(bf16[3,8,144,128]{3,2,1,0:T(8,128)(2,1)S(1)} %pad_maximum_fusion), channel_id=1, source_target_pairs={{0,8},{1,9},{10,18},{11,19},{20,28},{21,29},{30,6},{31,7}} | collective-permute-start | bytes 2654216 | tf_op jit(solution)/shard_map/ppermute | solution.py:144
  21.0 23.7 %collective-permute-start.15 = (bf16[3,8,144,128]{3,2,1,0:T(8,128)(2,1)S(1)}, bf16[3,8,144,128]{3,2,1,0:T(8,128)(2,1)S(1)}, u32[]{:S(2)}, u32[]{:S(2)}) collective-permute-start(bf16[3,8,144,128]{3,2,1,0:T(8,128)(2,1)S(1)} %pad_maximum_fusion), channel_id=1, source_target_pairs={{0,16},{1,17},{10,26},{11,27},{20,4},{21,5},{30,14},{31,15}} | collective-permute-start | bytes 2654216 | tf_op jit(solution)/shard_map/ppermute | solution.py:144
  24.0 23.0 %collective-permute-start.14 = (bf16[3,8,144,128]{3,2,1,0:T(8,128)(2,1)S(1)}, bf16[3,8,144,128]{3,2,1,0:T(8,128)(2,1)S(1)}, u32[]{:S(2)}, u32[]{:S(2)}) collective-permute-start(bf16[3,8,144,128]{3,2,1,0:T(8,128)(2,1)S(1)} %pad_maximum_fusion), channel_id=1, source_target_pairs={{0,24},{1,25},{10,2},{11,3},{20,12},{21,13},{30,22},{31,23}} | collective-permute-start | bytes 2654216 | tf_op jit(solution)/shard_map/ppermute | solution.py:144
  28.8 10.4 %collective-permute-start.4 = (bf16[3,2,2,144,128]{4,3,2,1,0:T(8,128)(2,1)S(1)}, bf16[3,2,2,144,128]{4,3,2,1,0:T(8,128)(2,1)S(1)}, u32[]{:S(2)}, u32[]{:S(2)}) collective-permute-start(bf16[3,2,2,144,128]{4,3,2,1,0:T(8,128)(2,1)S(1)} %collective-permute-done.2), channel_id=1, source_target_pairs={{0,2},{2,4},{4,6},{6,7},{7,5},{5,3},{3,1},{1,0},{8,10},{10,12},{12... | collective-permute-start | bytes 1327112 | tf_op jit(solution)/shard_map/ppermute | solution.py:135
  30.2 11.3 %collective-permute-start.5 = (bf16[3,2,2,144,128]{4,3,2,1,0:T(8,128)(2,1)S(1)}, bf16[3,2,2,144,128]{4,3,2,1,0:T(8,128)(2,1)S(1)}, u32[]{:S(2)}, u32[]{:S(2)}) collective-permute-start(bf16[3,2,2,144,128]{4,3,2,1,0:T(8,128)(2,1)S(1)} %collective-permute-done.3), channel_id=1, source_target_pairs={{2,0},{4,2},{6,4},{7,6},{5,7},{3,5},{1,3},{0,1},{10,8},{12,10},{14... | collective-permute-start | bytes 1327112 | tf_op jit(solution)/shard_map/ppermute | solution.py:136
  39.2 10.5 %collective-permute-start.6 = (bf16[3,2,2,144,128]{4,3,2,1,0:T(8,128)(2,1)S(1)}, bf16[3,2,2,144,128]{4,3,2,1,0:T(8,128)(2,1)S(1)}, u32[]{:S(2)}, u32[]{:S(2)}) collective-permute-start(bf16[3,2,2,144,128]{4,3,2,1,0:T(8,128)(2,1)S(1)} %collective-permute-done.4), channel_id=1, source_target_pairs={{0,2},{2,4},{4,6},{6,7},{7,5},{5,3},{3,1},{1,0},{8,10},{10,12},{12... | collective-permute-start | bytes 1327112 | tf_op jit(solution)/shard_map/ppermute | solution.py:135
  41.5 10.3 %collective-permute-start.7 = (bf16[3,2,2,144,128]{4,3,2,1,0:T(8,128)(2,1)S(1)}, bf16[3,2,2,144,128]{4,3,2,1,0:T(8,128)(2,1)S(1)}, u32[]{:S(2)}, u32[]{:S(2)}) collective-permute-start(bf16[3,2,2,144,128]{4,3,2,1,0:T(8,128)(2,1)S(1)} %collective-permute-done.5), channel_id=1, source_target_pairs={{2,0},{4,2},{6,4},{7,6},{5,7},{3,5},{1,3},{0,1},{10,8},{12,10},{14... | collective-permute-start | bytes 1327112 | tf_op jit(solution)/shard_map/ppermute | solution.py:136
  43.4 23.0 %collective-permute-start.19 = (bf16[3,8,144,128]{3,2,1,0:T(8,128)(2,1)S(1)}, bf16[3,8,144,128]{3,2,1,0:T(8,128)(2,1)S(1)}, u32[]{:S(2)}, u32[]{:S(2)}) collective-permute-start(bf16[3,8,144,128]{3,2,1,0:T(8,128)(2,1)S(1)} %pad_maximum_fusion.1), channel_id=1, source_target_pairs={{0,8},{1,9},{10,18},{11,19},{20,28},{21,29},{30,6},{31,7}} | collective-permute-start | bytes 2654216 | tf_op jit(solution)/shard_map/ppermute | solution.py:144
  44.7 25.5 %collective-permute-start.18 = (bf16[3,8,144,128]{3,2,1,0:T(8,128)(2,1)S(1)}, bf16[3,8,144,128]{3,2,1,0:T(8,128)(2,1)S(1)}, u32[]{:S(2)}, u32[]{:S(2)}) collective-permute-start(bf16[3,8,144,128]{3,2,1,0:T(8,128)(2,1)S(1)} %pad_maximum_fusion.1), channel_id=1, source_target_pairs={{0,16},{1,17},{10,26},{11,27},{20,4},{21,5},{30,14},{31,15}} | collective-permute-start | bytes 2654216 | tf_op jit(solution)/shard_map/ppermute | solution.py:144
  47.1 24.5 %collective-permute-start.17 = (bf16[3,8,144,128]{3,2,1,0:T(8,128)(2,1)S(1)}, bf16[3,8,144,128]{3,2,1,0:T(8,128)(2,1)S(1)}, u32[]{:S(2)}, u32[]{:S(2)}) collective-permute-start(bf16[3,8,144,128]{3,2,1,0:T(8,128)(2,1)S(1)} %pad_maximum_fusion.1), channel_id=1, source_target_pairs={{0,24},{1,25},{10,2},{11,3},{20,12},{21,13},{30,22},{31,23}} | collective-permute-start | bytes 2654216 | tf_op jit(solution)/shard_map/ppermute | solution.py:144
  49.7 11.2 %collective-permute-start.8 = (bf16[3,2,2,144,128]{4,3,2,1,0:T(8,128)(2,1)S(1)}, bf16[3,2,2,144,128]{4,3,2,1,0:T(8,128)(2,1)S(1)}, u32[]{:S(2)}, u32[]{:S(2)}) collective-permute-start(bf16[3,2,2,144,128]{4,3,2,1,0:T(8,128)(2,1)S(1)} %collective-permute-done.6), channel_id=1, source_target_pairs={{0,2},{2,4},{4,6},{6,7},{7,5},{5,3},{3,1},{1,0},{8,10},{10,12},{12... | collective-permute-start | bytes 1327112 | tf_op jit(solution)/shard_map/ppermute | solution.py:135
  51.8 11.2 %collective-permute-start.9 = (bf16[3,2,2,144,128]{4,3,2,1,0:T(8,128)(2,1)S(1)}, bf16[3,2,2,144,128]{4,3,2,1,0:T(8,128)(2,1)S(1)}, u32[]{:S(2)}, u32[]{:S(2)}) collective-permute-start(bf16[3,2,2,144,128]{4,3,2,1,0:T(8,128)(2,1)S(1)} %collective-permute-done.7), channel_id=1, source_target_pairs={{2,0},{4,2},{6,4},{7,6},{5,7},{3,5},{1,3},{0,1},{10,8},{12,10},{14... | collective-permute-start | bytes 1327112 | tf_op jit(solution)/shard_map/ppermute | solution.py:136
  63.2 33.1 %collective-permute-start.22 = (bf16[3,8,144,128]{3,2,1,0:T(8,128)(2,1)S(1)}, bf16[3,8,144,128]{3,2,1,0:T(8,128)(2,1)S(1)}, u32[]{:S(2)}, u32[]{:S(2)}) collective-permute-start(bf16[3,8,144,128]{3,2,1,0:T(8,128)(2,1)S(1)} %pad_maximum_fusion.2), channel_id=1, source_target_pairs={{0,8},{1,9},{10,18},{11,19},{20,28},{21,29},{30,6},{31,7}} | collective-permute-start | bytes 2654216 | tf_op jit(solution)/shard_map/ppermute | solution.py:144
  64.6 10.3 %collective-permute-start.10 = (bf16[3,2,2,144,128]{4,3,2,1,0:T(8,128)(2,1)S(1)}, bf16[3,2,2,144,128]{4,3,2,1,0:T(8,128)(2,1)S(1)}, u32[]{:S(2)}, u32[]{:S(2)}) collective-permute-start(bf16[3,2,2,144,128]{4,3,2,1,0:T(8,128)(2,1)S(1)} %collective-permute-done.8), channel_id=1, source_target_pairs={{0,2},{2,4},{4,6},{6,7},{7,5},{5,3},{3,1},{1,0},{8,10},{10,12},{12... | collective-permute-start | bytes 1327112 | tf_op jit(solution)/shard_map/ppermute | solution.py:135
  66.4 32.1 %collective-permute-start.21 = (bf16[3,8,144,128]{3,2,1,0:T(8,128)(2,1)S(1)}, bf16[3,8,144,128]{3,2,1,0:T(8,128)(2,1)S(1)}, u32[]{:S(2)}, u32[]{:S(2)}) collective-permute-start(bf16[3,8,144,128]{3,2,1,0:T(8,128)(2,1)S(1)} %pad_maximum_fusion.2), channel_id=1, source_target_pairs={{0,16},{1,17},{10,26},{11,27},{20,4},{21,5},{30,14},{31,15}} | collective-permute-start | bytes 2654216 | tf_op jit(solution)/shard_map/ppermute | solution.py:144
  70.2 30.3 %collective-permute-start.20 = (bf16[3,8,144,128]{3,2,1,0:T(8,128)(2,1)S(1)}, bf16[3,8,144,128]{3,2,1,0:T(8,128)(2,1)S(1)}, u32[]{:S(2)}, u32[]{:S(2)}) collective-permute-start(bf16[3,8,144,128]{3,2,1,0:T(8,128)(2,1)S(1)} %pad_maximum_fusion.2), channel_id=1, source_target_pairs={{0,24},{1,25},{10,2},{11,3},{20,12},{21,13},{30,22},{31,23}} | collective-permute-start | bytes 2654216 | tf_op jit(solution)/shard_map/ppermute | solution.py:144
  71.6 10.8 %collective-permute-start.11 = (bf16[3,2,2,144,128]{4,3,2,1,0:T(8,128)(2,1)S(1)}, bf16[3,2,2,144,128]{4,3,2,1,0:T(8,128)(2,1)S(1)}, u32[]{:S(2)}, u32[]{:S(2)}) collective-permute-start(bf16[3,2,2,144,128]{4,3,2,1,0:T(8,128)(2,1)S(1)} %collective-permute-done.9), channel_id=1, source_target_pairs={{2,0},{4,2},{6,4},{7,6},{5,7},{3,5},{1,3},{0,1},{10,8},{12,10},{14... | collective-permute-start | bytes 1327112 | tf_op jit(solution)/shard_map/ppermute | solution.py:136
  74.9 25.6 %copy-start = (bf16[3,2,144,128]{3,2,1,0:T(8,128)(2,1)}, bf16[3,2,144,128]{3,2,1,0:T(8,128)(2,1)S(1)}, u32[]{:S(2)}) copy-start(bf16[3,2,144,128]{3,2,1,0:T(8,128)(2,1)S(1)} %dynamic-slice_bitcast_fusion.3) | copy-start | bytes 663556
  74.9 12.6 %collective-permute-start.12 = (bf16[3,2,2,144,128]{4,3,2,1,0:T(8,128)(2,1)S(1)}, bf16[3,2,2,144,128]{4,3,2,1,0:T(8,128)(2,1)S(1)}, u32[]{:S(2)}, u32[]{:S(2)}) collective-permute-start(bf16[3,2,2,144,128]{4,3,2,1,0:T(8,128)(2,1)S(1)} %collective-permute-done.10), channel_id=1, source_target_pairs={{0,2},{2,4},{4,6},{6,7},{7,5},{5,3},{3,1},{1,0},{8,10},{10,12},{12... | collective-permute-start | bytes 1327112 | tf_op jit(solution)/shard_map/ppermute | solution.py:135
  82.3 9.8 %collective-permute-start.13 = (bf16[3,2,2,144,128]{4,3,2,1,0:T(8,128)(2,1)S(1)}, bf16[3,2,2,144,128]{4,3,2,1,0:T(8,128)(2,1)S(1)}, u32[]{:S(2)}, u32[]{:S(2)}) collective-permute-start(bf16[3,2,2,144,128]{4,3,2,1,0:T(8,128)(2,1)S(1)} %collective-permute-done.11), channel_id=1, source_target_pairs={{2,0},{4,2},{6,4},{7,6},{5,7},{3,5},{1,3},{0,1},{10,8},{12,10},{14... | collective-permute-start | bytes 1327112 | tf_op jit(solution)/shard_map/ppermute | solution.py:136
  87.5 15.6 %collective-permute-start.25 = (bf16[3,4,144,128]{3,2,1,0:T(8,128)(2,1)}, bf16[3,4,144,128]{3,2,1,0:T(8,128)(2,1)S(1)}, u32[]{:S(2)}, u32[]{:S(2)}) collective-permute-start(bf16[3,4,144,128]{3,2,1,0:T(8,128)(2,1)} %pad_maximum_fusion.3), channel_id=1, source_target_pairs={{0,8},{1,9},{10,18},{11,19},{20,28},{21,29},{30,6},{31,7}} | collective-permute-start | bytes 1327112 | tf_op jit(solution)/shard_map/ppermute | solution.py:144
  89.1 11.4 %copy-start.1 = (bf16[3,2,144,128]{3,2,1,0:T(8,128)(2,1)}, bf16[3,2,144,128]{3,2,1,0:T(8,128)(2,1)S(1)}, u32[]{:S(2)}) copy-start(bf16[3,2,144,128]{3,2,1,0:T(8,128)(2,1)S(1)} %dynamic-slice_bitcast_fusion.1) | copy-start | bytes 663556
  92.1 17.6 %collective-permute-start.24 = (bf16[3,4,144,128]{3,2,1,0:T(8,128)(2,1)}, bf16[3,4,144,128]{3,2,1,0:T(8,128)(2,1)}, u32[]{:S(2)}, u32[]{:S(2)}) collective-permute-start(bf16[3,4,144,128]{3,2,1,0:T(8,128)(2,1)} %pad_maximum_fusion.3), channel_id=1, source_target_pairs={{0,16},{1,17},{10,26},{11,27},{20,4},{21,5},{30,14},{31,15}} | collective-permute-start | bytes 1327112 | tf_op jit(solution)/shard_map/ppermute | solution.py:144
  95.5 5.0 %copy-start.3 = (bf16[3,2,144,128]{3,2,1,0:T(8,128)(2,1)}, bf16[3,2,144,128]{3,2,1,0:T(8,128)(2,1)S(1)}, u32[]{:S(2)}) copy-start(bf16[3,2,144,128]{3,2,1,0:T(8,128)(2,1)S(1)} %dynamic-slice_bitcast_fusion) | copy-start | bytes 663556
  96.4 13.3 %collective-permute-start.23 = (bf16[3,4,144,128]{3,2,1,0:T(8,128)(2,1)}, bf16[3,4,144,128]{3,2,1,0:T(8,128)(2,1)}, u32[]{:S(2)}, u32[]{:S(2)}) collective-permute-start(bf16[3,4,144,128]{3,2,1,0:T(8,128)(2,1)} %pad_maximum_fusion.3), channel_id=1, source_target_pairs={{0,24},{1,25},{10,2},{11,3},{20,12},{21,13},{30,22},{31,23}} | collective-permute-start | bytes 1327112 | tf_op jit(solution)/shard_map/ppermute | solution.py:144
  98.4 12.6 %collective-permute-start.28 = (bf16[3,4,144,128]{3,2,1,0:T(8,128)(2,1)}, bf16[3,4,144,128]{3,2,1,0:T(8,128)(2,1)}, u32[]{:S(2)}, u32[]{:S(2)}) collective-permute-start(bf16[3,4,144,128]{3,2,1,0:T(8,128)(2,1)} %pad_maximum_fusion.4), channel_id=1, source_target_pairs={{0,8},{1,9},{10,18},{11,19},{20,28},{21,29},{30,6},{31,7}} | collective-permute-start | bytes 1327112 | tf_op jit(solution)/shard_map/ppermute | solution.py:144
  100.5 10.5 %collective-permute-start.27 = (bf16[3,4,144,128]{3,2,1,0:T(8,128)(2,1)}, bf16[3,4,144,128]{3,2,1,0:T(8,128)(2,1)}, u32[]{:S(2)}, u32[]{:S(2)}) collective-permute-start(bf16[3,4,144,128]{3,2,1,0:T(8,128)(2,1)} %pad_maximum_fusion.4), channel_id=1, source_target_pairs={{0,16},{1,17},{10,26},{11,27},{20,4},{21,5},{30,14},{31,15}} | collective-permute-start | bytes 1327112 | tf_op jit(solution)/shard_map/ppermute | solution.py:144
  103.1 11.9 %collective-permute-start.26 = (bf16[3,4,144,128]{3,2,1,0:T(8,128)(2,1)}, bf16[3,4,144,128]{3,2,1,0:T(8,128)(2,1)}, u32[]{:S(2)}, u32[]{:S(2)}) collective-permute-start(bf16[3,4,144,128]{3,2,1,0:T(8,128)(2,1)} %pad_maximum_fusion.4), channel_id=1, source_target_pairs={{0,24},{1,25},{10,2},{11,3},{20,12},{21,13},{30,22},{31,23}} | collective-permute-start | bytes 1327112 | tf_op jit(solution)/shard_map/ppermute | solution.py:144
  (2 other events, 8.7 us)

commit v16 on v14

--- a/solution.py
+++ b/solution.py
@@ -25,7 +25,7 @@
         g = step * chunk + k
         meta = bs_ref[k, 0, blk : blk + META].astype(jnp.float32)
         w = meta[0:1] + meta[1:2] + meta[2:3]
-        lhs = (bs_ref[k, 0, :blk].astype(jnp.float32).T * w).astype(jnp.bfloat16)
+        lhs = (bs_ref[k, 0, :blk].T.astype(jnp.float32) * w).astype(jnp.bfloat16)
         prod = jnp.dot(lhs, bc_ref[k, :blk], preferred_element_type=jnp.float32)
         col = pl.multiple_of(offs_ref[g * stride + local_slots] * blk, blk)
         row = pl.multiple_of(offs_ref[g * stride + s] * blk, blk)

time: 131 us -> 131 us (level)
  no operation moved by 1% of the time
where the time goes in v16:
time: 131 us; the launch traced here: 130 us
  waiting for transfers between devices  47 us (36%)
  starting transfers between devices  43.6 us (33%)
  local copies, waits for them, and re-layouts  17.8 us (14%)
  Pallas kernels  10.8 us (8%)
  other arithmetic  10 us (8%)
    ppermute x7, waiting for transfers between devices, local(): a = lax.ppermute(a, 'col', forward)  31.5 us
    ppermute x15, starting transfers between devices, local(): got = jnp.where(which == j, lax.ppermute(own, ('row', 'col'), fan), got)  30.5 us
    ppermute x7, starting transfers between devices, local(): a = lax.ppermute(a, 'col', forward)  11.9 us
    ppermute x7, waiting for transfers between devices, local(): b = lax.ppermute(b, 'col', backward)  11.5 us
    unnamed x23, local copies, waits for them, and re-layouts  11.1 us
    pallas_call x1, Pallas kernels, gram_call(): pl.pallas_call(kernel, grid_spec=pltpu.PrefetchScalarGridSpec(num_scalar_...  10.8 us
    unnamed x5, other arithmetic  5.26 us
    ppermute x15, waiting for transfers between devices, local(): got = jnp.where(which == j, lax.ppermute(own, ('row', 'col'), fan), got)  4.03 us
  transfers between devices with their start and end apart: 29, of which 11 were waited for; matrix products, arithmetic and copies ran while one was open for 15% of the time, Pallas kernels for 0%

profile of v16, /device:TPU:0, one launch (start us, length us, event | category | flops | bytes accessed | tf_op | source)
XLA Modules:
  0.0 129.7 jit_solution(15769589753209616019)
XLA Ops:
  1.7 2.4 %constant_dynamic-update-slice_fusion.14 = (bf16[3,32,2,144,128]{4,3,2,1,0:T(8,128)(2,1)}, bf16[3,4,2,144,128]{4,3,2,1,0:T(8,128)(2,1)S(1)}) fusion(bf16[144]{0:T(256)(128)(2,1)S(1)} %pad.21.clone, bf16[3,4,2,1,128]{4,3,2,1,0:T(2,128)(2,1)S(1)} %broadcast_in_dim.7, bf16[3,4,2,3,128]{4,3,2,1,0:T(4,128)(2,1)S(1)} %broadcast_in_dim.6, ...), kind=kLoop, calls=%fused_computation.42 | loop fusion | flops 3538943 | bytes 2580768
  4.2 3.1 %collective-permute-start = (bf16[3,2,2,144,128]{4,3,2,1,0:T(8,128)(2,1)S(1)}, bf16[3,2,2,144,128]{4,3,2,1,0:T(8,128)(2,1)S(1)}, u32[]{:S(2)}, u32[]{:S(2)}) collective-permute-start(bf16[3,2,2,144,128]{4,3,2,1,0:T(8,128)(2,1)S(1)} %get-tuple-element.5), channel_id=1, source_target_pairs={{0,2},{2,4},{4,6},{6,7},{7,5},{5,3},{3,1},{1,0},{8,10},{10,12},{12... | collective-permute-start | bytes 1327112 | tf_op jit(solution)/shard_map/ppermute | solution.py:109
  7.3 10.1 %collective-permute-done = bf16[3,2,2,144,128]{4,3,2,1,0:T(8,128)(2,1)S(1)} collective-permute-done((bf16[3,2,2,144,128]{4,3,2,1,0:T(8,128)(2,1)S(1)}, bf16[3,2,2,144,128]{4,3,2,1,0:T(8,128)(2,1)S(1)}, u32[]{:S(2)}, u32[]{:S(2)}) %collective-permute-start) | collective-permute-done | bytes 442400 | tf_op jit(solution)/shard_map/ppermute | solution.py:109
  17.4 1.8 %collective-permute-start.2 = (bf16[3,2,2,144,128]{4,3,2,1,0:T(8,128)(2,1)S(1)}, bf16[3,2,2,144,128]{4,3,2,1,0:T(8,128)(2,1)S(1)}, u32[]{:S(2)}, u32[]{:S(2)}) collective-permute-start(bf16[3,2,2,144,128]{4,3,2,1,0:T(8,128)(2,1)S(1)} %collective-permute-done), channel_id=1, source_target_pairs={{0,2},{2,4},{4,6},{6,7},{7,5},{5,3},{3,1},{1,0},{8,10},{10,12},{12... | collective-permute-start | bytes 1327112 | tf_op jit(solution)/shard_map/ppermute | solution.py:109
  19.6 1.3 %collective-permute-start.16 = (bf16[3,8,144,128]{3,2,1,0:T(8,128)(2,1)S(1)}, bf16[3,8,144,128]{3,2,1,0:T(8,128)(2,1)S(1)}, u32[]{:S(2)}, u32[]{:S(2)}) collective-permute-start(bf16[3,8,144,128]{3,2,1,0:T(8,128)(2,1)S(1)} %pad_maximum_fusion), channel_id=1, source_target_pairs={{0,8},{1,9},{10,18},{11,19},{20,28},{21,29},{30,6},{31,7}} | collective-permute-start | bytes 2654216 | tf_op jit(solution)/shard_map/ppermute | solution.py:118
  21.0 3.0 %collective-permute-start.15 = (bf16[3,8,144,128]{3,2,1,0:T(8,128)(2,1)S(1)}, bf16[3,8,144,128]{3,2,1,0:T(8,128)(2,1)S(1)}, u32[]{:S(2)}, u32[]{:S(2)}) collective-permute-start(bf16[3,8,144,128]{3,2,1,0:T(8,128)(2,1)S(1)} %pad_maximum_fusion), channel_id=1, source_target_pairs={{0,16},{1,17},{10,26},{11,27},{20,4},{21,5},{30,14},{31,15}} | collective-permute-start | bytes 2654216 | tf_op jit(solution)/shard_map/ppermute | solution.py:118
  24.0 1.3 %collective-permute-start.14 = (bf16[3,8,144,128]{3,2,1,0:T(8,128)(2,1)S(1)}, bf16[3,8,144,128]{3,2,1,0:T(8,128)(2,1)S(1)}, u32[]{:S(2)}, u32[]{:S(2)}) collective-permute-start(bf16[3,8,144,128]{3,2,1,0:T(8,128)(2,1)S(1)} %pad_maximum_fusion), channel_id=1, source_target_pairs={{0,24},{1,25},{10,2},{11,3},{20,12},{21,13},{30,22},{31,23}} | collective-permute-start | bytes 2654216 | tf_op jit(solution)/shard_map/ppermute | solution.py:118
  27.1 1.6 %collective-permute-done.2 = bf16[3,2,2,144,128]{4,3,2,1,0:T(8,128)(2,1)S(1)} collective-permute-done((bf16[3,2,2,144,128]{4,3,2,1,0:T(8,128)(2,1)S(1)}, bf16[3,2,2,144,128]{4,3,2,1,0:T(8,128)(2,1)S(1)}, u32[]{:S(2)}, u32[]{:S(2)}) %collective-permute-start.2) | collective-permute-done | bytes 442400 | tf_op jit(solution)/shard_map/ppermute | solution.py:109
  28.8 1.5 %collective-permute-start.4 = (bf16[3,2,2,144,128]{4,3,2,1,0:T(8,128)(2,1)S(1)}, bf16[3,2,2,144,128]{4,3,2,1,0:T(8,128)(2,1)S(1)}, u32[]{:S(2)}, u32[]{:S(2)}) collective-permute-start(bf16[3,2,2,144,128]{4,3,2,1,0:T(8,128)(2,1)S(1)} %collective-permute-done.2), channel_id=1, source_target_pairs={{0,2},{2,4},{4,6},{6,7},{7,5},{5,3},{3,1},{1,0},{8,10},{10,12},{12... | collective-permute-start | bytes 1327112 | tf_op jit(solution)/shard_map/ppermute | solution.py:109
  32.5 6.6 %collective-permute-done.4 = bf16[3,2,2,144,128]{4,3,2,1,0:T(8,128)(2,1)S(1)} collective-permute-done((bf16[3,2,2,144,128]{4,3,2,1,0:T(8,128)(2,1)S(1)}, bf16[3,2,2,144,128]{4,3,2,1,0:T(8,128)(2,1)S(1)}, u32[]{:S(2)}, u32[]{:S(2)}) %collective-permute-start.4) | collective-permute-done | bytes 442400 | tf_op jit(solution)/shard_map/ppermute | solution.py:109
  39.2 2.3 %collective-permute-start.6 = (bf16[3,2,2,144,128]{4,3,2,1,0:T(8,128)(2,1)S(1)}, bf16[3,2,2,144,128]{4,3,2,1,0:T(8,128)(2,1)S(1)}, u32[]{:S(2)}, u32[]{:S(2)}) collective-permute-start(bf16[3,2,2,144,128]{4,3,2,1,0:T(8,128)(2,1)S(1)} %collective-permute-done.4), channel_id=1, source_target_pairs={{0,2},{2,4},{4,6},{6,7},{7,5},{5,3},{3,1},{1,0},{8,10},{10,12},{12... | collective-permute-start | bytes 1327112 | tf_op jit(solution)/shard_map/ppermute | solution.py:109
  44.7 2.3 %collective-permute-start.18 = (bf16[3,8,144,128]{3,2,1,0:T(8,128)(2,1)S(1)}, bf16[3,8,144,128]{3,2,1,0:T(8,128)(2,1)S(1)}, u32[]{:S(2)}, u32[]{:S(2)}) collective-permute-start(bf16[3,8,144,128]{3,2,1,0:T(8,128)(2,1)S(1)} %pad_maximum_fusion.1), channel_id=1, source_target_pairs={{0,16},{1,17},{10,26},{11,27},{20,4},{21,5},{30,14},{31,15}} | collective-permute-start | bytes 2654216 | tf_op jit(solution)/shard_map/ppermute | solution.py:118
  47.1 1.3 %collective-permute-start.17 = (bf16[3,8,144,128]{3,2,1,0:T(8,128)(2,1)S(1)}, bf16[3,8,144,128]{3,2,1,0:T(8,128)(2,1)S(1)}, u32[]{:S(2)}, u32[]{:S(2)}) collective-permute-start(bf16[3,8,144,128]{3,2,1,0:T(8,128)(2,1)S(1)} %pad_maximum_fusion.1), channel_id=1, source_target_pairs={{0,24},{1,25},{10,2},{11,3},{20,12},{21,13},{30,22},{31,23}} | collective-permute-start | bytes 2654216 | tf_op jit(solution)/shard_map/ppermute | solution.py:118
  49.7 2.1 %collective-permute-start.8 = (bf16[3,2,2,144,128]{4,3,2,1,0:T(8,128)(2,1)S(1)}, bf16[3,2,2,144,128]{4,3,2,1,0:T(8,128)(2,1)S(1)}, u32[]{:S(2)}, u32[]{:S(2)}) collective-permute-start(bf16[3,2,2,144,128]{4,3,2,1,0:T(8,128)(2,1)S(1)} %collective-permute-done.6), channel_id=1, source_target_pairs={{0,2},{2,4},{4,6},{6,7},{7,5},{5,3},{3,1},{1,0},{8,10},{10,12},{12... | collective-permute-start | bytes 1327112 | tf_op jit(solution)/shard_map/ppermute | solution.py:109
  53.6 7.3 %collective-permute-done.8 = bf16[3,2,2,144,128]{4,3,2,1,0:T(8,128)(2,1)S(1)} collective-permute-done((bf16[3,2,2,144,128]{4,3,2,1,0:T(8,128)(2,1)S(1)}, bf16[3,2,2,144,128]{4,3,2,1,0:T(8,128)(2,1)S(1)}, u32[]{:S(2)}, u32[]{:S(2)}) %collective-permute-start.8) | collective-permute-done | bytes 442400 | tf_op jit(solution)/shard_map/ppermute | solution.py:109
  60.9 2.2 %collective-permute-done.9 = bf16[3,2,2,144,128]{4,3,2,1,0:T(8,128)(2,1)S(1)} collective-permute-done((bf16[3,2,2,144,128]{4,3,2,1,0:T(8,128)(2,1)S(1)}, bf16[3,2,2,144,128]{4,3,2,1,0:T(8,128)(2,1)S(1)}, u32[]{:S(2)}, u32[]{:S(2)}) %collective-permute-start.9) | collective-permute-done | bytes 442400 | tf_op jit(solution)/shard_map/ppermute | solution.py:110
  63.2 1.3 %collective-permute-start.22 = (bf16[3,8,144,128]{3,2,1,0:T(8,128)(2,1)S(1)}, bf16[3,8,144,128]{3,2,1,0:T(8,128)(2,1)S(1)}, u32[]{:S(2)}, u32[]{:S(2)}) collective-permute-start(bf16[3,8,144,128]{3,2,1,0:T(8,128)(2,1)S(1)} %pad_maximum_fusion.2), channel_id=1, source_target_pairs={{0,8},{1,9},{10,18},{11,19},{20,28},{21,29},{30,6},{31,7}} | collective-permute-start | bytes 2654216 | tf_op jit(solution)/shard_map/ppermute | solution.py:118
  66.4 3.8 %collective-permute-start.21 = (bf16[3,8,144,128]{3,2,1,0:T(8,128)(2,1)S(1)}, bf16[3,8,144,128]{3,2,1,0:T(8,128)(2,1)S(1)}, u32[]{:S(2)}, u32[]{:S(2)}) collective-permute-start(bf16[3,8,144,128]{3,2,1,0:T(8,128)(2,1)S(1)} %pad_maximum_fusion.2), channel_id=1, source_target_pairs={{0,16},{1,17},{10,26},{11,27},{20,4},{21,5},{30,14},{31,15}} | collective-permute-start | bytes 2654216 | tf_op jit(solution)/shard_map/ppermute | solution.py:118
  70.2 1.3 %collective-permute-start.20 = (bf16[3,8,144,128]{3,2,1,0:T(8,128)(2,1)S(1)}, bf16[3,8,144,128]{3,2,1,0:T(8,128)(2,1)S(1)}, u32[]{:S(2)}, u32[]{:S(2)}) collective-permute-start(bf16[3,8,144,128]{3,2,1,0:T(8,128)(2,1)S(1)} %pad_maximum_fusion.2), channel_id=1, source_target_pairs={{0,24},{1,25},{10,2},{11,3},{20,12},{21,13},{30,22},{31,23}} | collective-permute-start | bytes 2654216 | tf_op jit(solution)/shard_map/ppermute | solution.py:118
  72.2 2.8 %collective-permute-done.10 = bf16[3,2,2,144,128]{4,3,2,1,0:T(8,128)(2,1)S(1)} collective-permute-done((bf16[3,2,2,144,128]{4,3,2,1,0:T(8,128)(2,1)S(1)}, bf16[3,2,2,144,128]{4,3,2,1,0:T(8,128)(2,1)S(1)}, u32[]{:S(2)}, u32[]{:S(2)}) %collective-permute-start.10) | collective-permute-done | bytes 442400 | tf_op jit(solution)/shard_map/ppermute | solution.py:109
  76.0 6.3 %collective-permute-done.11 = bf16[3,2,2,144,128]{4,3,2,1,0:T(8,128)(2,1)S(1)} collective-permute-done((bf16[3,2,2,144,128]{4,3,2,1,0:T(8,128)(2,1)S(1)}, bf16[3,2,2,144,128]{4,3,2,1,0:T(8,128)(2,1)S(1)}, u32[]{:S(2)}, u32[]{:S(2)}) %collective-permute-start.11) | collective-permute-done | bytes 442400 | tf_op jit(solution)/shard_map/ppermute | solution.py:110
  85.2 2.3 %collective-permute-done.12 = bf16[3,2,2,144,128]{4,3,2,1,0:T(8,128)(2,1)S(1)} collective-permute-done((bf16[3,2,2,144,128]{4,3,2,1,0:T(8,128)(2,1)S(1)}, bf16[3,2,2,144,128]{4,3,2,1,0:T(8,128)(2,1)S(1)}, u32[]{:S(2)}, u32[]{:S(2)}) %collective-permute-start.12) | collective-permute-done | bytes 442400 | tf_op jit(solution)/shard_map/ppermute | solution.py:109
  87.5 1.6 %collective-permute-start.25 = (bf16[3,4,144,128]{3,2,1,0:T(8,128)(2,1)}, bf16[3,4,144,128]{3,2,1,0:T(8,128)(2,1)S(1)}, u32[]{:S(2)}, u32[]{:S(2)}) collective-permute-start(bf16[3,4,144,128]{3,2,1,0:T(8,128)(2,1)} %pad_maximum_fusion.3), channel_id=1, source_target_pairs={{0,8},{1,9},{10,18},{11,19},{20,28},{21,29},{30,6},{31,7}} | collective-permute-start | bytes 1327112 | tf_op jit(solution)/shard_map/ppermute | solution.py:118
  89.1 3.0 %collective-permute-done.13 = bf16[3,2,2,144,128]{4,3,2,1,0:T(8,128)(2,1)S(1)} collective-permute-done((bf16[3,2,2,144,128]{4,3,2,1,0:T(8,128)(2,1)S(1)}, bf16[3,2,2,144,128]{4,3,2,1,0:T(8,128)(2,1)S(1)}, u32[]{:S(2)}, u32[]{:S(2)}) %collective-permute-start.13) | collective-permute-done | bytes 442400 | tf_op jit(solution)/shard_map/ppermute | solution.py:110
  92.1 3.4 %collective-permute-start.24 = (bf16[3,4,144,128]{3,2,1,0:T(8,128)(2,1)}, bf16[3,4,144,128]{3,2,1,0:T(8,128)(2,1)}, u32[]{:S(2)}, u32[]{:S(2)}) collective-permute-start(bf16[3,4,144,128]{3,2,1,0:T(8,128)(2,1)} %pad_maximum_fusion.3), channel_id=1, source_target_pairs={{0,16},{1,17},{10,26},{11,27},{20,4},{21,5},{30,14},{31,15}} | collective-permute-start | bytes 1327112 | tf_op jit(solution)/shard_map/ppermute | solution.py:118
  96.4 2.1 %collective-permute-start.23 = (bf16[3,4,144,128]{3,2,1,0:T(8,128)(2,1)}, bf16[3,4,144,128]{3,2,1,0:T(8,128)(2,1)}, u32[]{:S(2)}, u32[]{:S(2)}) collective-permute-start(bf16[3,4,144,128]{3,2,1,0:T(8,128)(2,1)} %pad_maximum_fusion.3), channel_id=1, source_target_pairs={{0,24},{1,25},{10,2},{11,3},{20,12},{21,13},{30,22},{31,23}} | collective-permute-start | bytes 1327112 | tf_op jit(solution)/shard_map/ppermute | solution.py:118
  98.4 2.1 %collective-permute-start.28 = (bf16[3,4,144,128]{3,2,1,0:T(8,128)(2,1)}, bf16[3,4,144,128]{3,2,1,0:T(8,128)(2,1)}, u32[]{:S(2)}, u32[]{:S(2)}) collective-permute-start(bf16[3,4,144,128]{3,2,1,0:T(8,128)(2,1)} %pad_maximum_fusion.4), channel_id=1, source_target_pairs={{0,8},{1,9},{10,18},{11,19},{20,28},{21,29},{30,6},{31,7}} | collective-permute-start | bytes 1327112 | tf_op jit(solution)/shard_map/ppermute | solution.py:118
  100.5 2.1 %collective-permute-start.27 = (bf16[3,4,144,128]{3,2,1,0:T(8,128)(2,1)}, bf16[3,4,144,128]{3,2,1,0:T(8,128)(2,1)}, u32[]{:S(2)}, u32[]{:S(2)}) collective-permute-start(bf16[3,4,144,128]{3,2,1,0:T(8,128)(2,1)} %pad_maximum_fusion.4), channel_id=1, source_target_pairs={{0,16},{1,17},{10,26},{11,27},{20,4},{21,5},{30,14},{31,15}} | collective-permute-start | bytes 1327112 | tf_op jit(solution)/shard_map/ppermute | solution.py:118
  103.1 2.1 %collective-permute-start.26 = (bf16[3,4,144,128]{3,2,1,0:T(8,128)(2,1)}, bf16[3,4,144,128]{3,2,1,0:T(8,128)(2,1)}, u32[]{:S(2)}, u32[]{:S(2)}) collective-permute-start(bf16[3,4,144,128]{3,2,1,0:T(8,128)(2,1)} %pad_maximum_fusion.4), channel_id=1, source_target_pairs={{0,24},{1,25},{10,2},{11,3},{20,12},{21,13},{30,22},{31,23}} | collective-permute-start | bytes 1327112 | tf_op jit(solution)/shard_map/ppermute | solution.py:118
  107.0 1.7 %slice.19 = bf16[96,2,1,1]{3,2,1,0:T(2,128)(2,1)} slice(bf16[96,2,144,128]{3,2,1,0:T(8,128)(2,1)} %bitcast.44), slice={[0:96], [0:2], [131:132], [0:1]} | slice | bytes 768 | tf_op jit(solution)/shard_map/slice | solution.py:127
  111.0 4.0 %collective-permute-done.26 = bf16[3,4,144,128]{3,2,1,0:T(8,128)(2,1)} collective-permute-done((bf16[3,4,144,128]{3,2,1,0:T(8,128)(2,1)}, bf16[3,4,144,128]{3,2,1,0:T(8,128)(2,1)}, u32[]{:S(2)}, u32[]{:S(2)}) %collective-permute-start.26) | collective-permute-done | bytes 442400 | tf_op jit(solution)/shard_map/ppermute | solution.py:118
  118.8 10.8 %shard_map.37 = f32[2048,1024]{1,0:T(8,128)} custom-call(s32[288]{0:T(512)S(1)} %min.12.offs_ref, bf16[96,2,144,128]{3,2,1,0:T(8,128)(2,1)} %bitcast.45, bf16[96,144,128]{2,1,0:T(8,128)(2,1)S(1)} %bitcast.43), custom_call_target="tpu_custom_call" | custom-call | flops 805306368 | bytes 17825792 | tf_op jit(solution)/shard_map/pallas_call | solution.py:40
  (93 shorter events, 28.1 us)
Async XLA Ops:
  4.2 13.2 %collective-permute-start = (bf16[3,2,2,144,128]{4,3,2,1,0:T(8,128)(2,1)S(1)}, bf16[3,2,2,144,128]{4,3,2,1,0:T(8,128)(2,1)S(1)}, u32[]{:S(2)}, u32[]{:S(2)}) collective-permute-start(bf16[3,2,2,144,128]{4,3,2,1,0:T(8,128)(2,1)S(1)} %get-tuple-element.5), channel_id=1, source_target_pairs={{0,2},{2,4},{4,6},{6,7},{7,5},{5,3},{3,1},{1,0},{8,10},{10,12},{12... | collective-permute-start | bytes 1327112 | tf_op jit(solution)/shard_map/ppermute | solution.py:109
  7.3 11.9 %collective-permute-start.1 = (bf16[3,2,2,144,128]{4,3,2,1,0:T(8,128)(2,1)S(1)}, bf16[3,2,2,144,128]{4,3,2,1,0:T(8,128)(2,1)S(1)}, u32[]{:S(2)}, u32[]{:S(2)}) collective-permute-start(bf16[3,2,2,144,128]{4,3,2,1,0:T(8,128)(2,1)S(1)} %get-tuple-element.6), channel_id=1, source_target_pairs={{2,0},{4,2},{6,4},{7,6},{5,7},{3,5},{1,3},{0,1},{10,8},{12,10},{14... | collective-permute-start | bytes 1327112 | tf_op jit(solution)/shard_map/ppermute | solution.py:110
  17.4 11.4 %collective-permute-start.2 = (bf16[3,2,2,144,128]{4,3,2,1,0:T(8,128)(2,1)S(1)}, bf16[3,2,2,144,128]{4,3,2,1,0:T(8,128)(2,1)S(1)}, u32[]{:S(2)}, u32[]{:S(2)}) collective-permute-start(bf16[3,2,2,144,128]{4,3,2,1,0:T(8,128)(2,1)S(1)} %collective-permute-done), channel_id=1, source_target_pairs={{0,2},{2,4},{4,6},{6,7},{7,5},{5,3},{3,1},{1,0},{8,10},{10,12},{12... | collective-permute-start | bytes 1327112 | tf_op jit(solution)/shard_map/ppermute | solution.py:109
  19.2 11.0 %collective-permute-start.3 = (bf16[3,2,2,144,128]{4,3,2,1,0:T(8,128)(2,1)S(1)}, bf16[3,2,2,144,128]{4,3,2,1,0:T(8,128)(2,1)S(1)}, u32[]{:S(2)}, u32[]{:S(2)}) collective-permute-start(bf16[3,2,2,144,128]{4,3,2,1,0:T(8,128)(2,1)S(1)} %collective-permute-done.1), channel_id=1, source_target_pairs={{2,0},{4,2},{6,4},{7,6},{5,7},{3,5},{1,3},{0,1},{10,8},{12,10},{14... | collective-permute-start | bytes 1327112 | tf_op jit(solution)/shard_map/ppermute | solution.py:110
  19.6 23.7 %collective-permute-start.16 = (bf16[3,8,144,128]{3,2,1,0:T(8,128)(2,1)S(1)}, bf16[3,8,144,128]{3,2,1,0:T(8,128)(2,1)S(1)}, u32[]{:S(2)}, u32[]{:S(2)}) collective-permute-start(bf16[3,8,144,128]{3,2,1,0:T(8,128)(2,1)S(1)} %pad_maximum_fusion), channel_id=1, source_target_pairs={{0,8},{1,9},{10,18},{11,19},{20,28},{21,29},{30,6},{31,7}} | collective-permute-start | bytes 2654216 | tf_op jit(solution)/shard_map/ppermute | solution.py:118
  21.0 23.7 %collective-permute-start.15 = (bf16[3,8,144,128]{3,2,1,0:T(8,128)(2,1)S(1)}, bf16[3,8,144,128]{3,2,1,0:T(8,128)(2,1)S(1)}, u32[]{:S(2)}, u32[]{:S(2)}) collective-permute-start(bf16[3,8,144,128]{3,2,1,0:T(8,128)(2,1)S(1)} %pad_maximum_fusion), channel_id=1, source_target_pairs={{0,16},{1,17},{10,26},{11,27},{20,4},{21,5},{30,14},{31,15}} | collective-permute-start | bytes 2654216 | tf_op jit(solution)/shard_map/ppermute | solution.py:118
  24.0 23.0 %collective-permute-start.14 = (bf16[3,8,144,128]{3,2,1,0:T(8,128)(2,1)S(1)}, bf16[3,8,144,128]{3,2,1,0:T(8,128)(2,1)S(1)}, u32[]{:S(2)}, u32[]{:S(2)}) collective-permute-start(bf16[3,8,144,128]{3,2,1,0:T(8,128)(2,1)S(1)} %pad_maximum_fusion), channel_id=1, source_target_pairs={{0,24},{1,25},{10,2},{11,3},{20,12},{21,13},{30,22},{31,23}} | collective-permute-start | bytes 2654216 | tf_op jit(solution)/shard_map/ppermute | solution.py:118
  28.8 10.4 %collective-permute-start.4 = (bf16[3,2,2,144,128]{4,3,2,1,0:T(8,128)(2,1)S(1)}, bf16[3,2,2,144,128]{4,3,2,1,0:T(8,128)(2,1)S(1)}, u32[]{:S(2)}, u32[]{:S(2)}) collective-permute-start(bf16[3,2,2,144,128]{4,3,2,1,0:T(8,128)(2,1)S(1)} %collective-permute-done.2), channel_id=1, source_target_pairs={{0,2},{2,4},{4,6},{6,7},{7,5},{5,3},{3,1},{1,0},{8,10},{10,12},{12... | collective-permute-start | bytes 1327112 | tf_op jit(solution)/shard_map/ppermute | solution.py:109
  30.2 11.3 %collective-permute-start.5 = (bf16[3,2,2,144,128]{4,3,2,1,0:T(8,128)(2,1)S(1)}, bf16[3,2,2,144,128]{4,3,2,1,0:T(8,128)(2,1)S(1)}, u32[]{:S(2)}, u32[]{:S(2)}) collective-permute-start(bf16[3,2,2,144,128]{4,3,2,1,0:T(8,128)(2,1)S(1)} %collective-permute-done.3), channel_id=1, source_target_pairs={{2,0},{4,2},{6,4},{7,6},{5,7},{3,5},{1,3},{0,1},{10,8},{12,10},{14... | collective-permute-start | bytes 1327112 | tf_op jit(solution)/shard_map/ppermute | solution.py:110
  39.2 10.5 %collective-permute-start.6 = (bf16[3,2,2,144,128]{4,3,2,1,0:T(8,128)(2,1)S(1)}, bf16[3,2,2,144,128]{4,3,2,1,0:T(8,128)(2,1)S(1)}, u32[]{:S(2)}, u32[]{:S(2)}) collective-permute-start(bf16[3,2,2,144,128]{4,3,2,1,0:T(8,128)(2,1)S(1)} %collective-permute-done.4), channel_id=1, source_target_pairs={{0,2},{2,4},{4,6},{6,7},{7,5},{5,3},{3,1},{1,0},{8,10},{10,12},{12... | collective-permute-start | bytes 1327112 | tf_op jit(solution)/shard_map/ppermute | solution.py:109
  41.5 10.3 %collective-permute-start.7 = (bf16[3,2,2,144,128]{4,3,2,1,0:T(8,128)(2,1)S(1)}, bf16[3,2,2,144,128]{4,3,2,1,0:T(8,128)(2,1)S(1)}, u32[]{:S(2)}, u32[]{:S(2)}) collective-permute-start(bf16[3,2,2,144,128]{4,3,2,1,0:T(8,128)(2,1)S(1)} %collective-permute-done.5), channel_id=1, source_target_pairs={{2,0},{4,2},{6,4},{7,6},{5,7},{3,5},{1,3},{0,1},{10,8},{12,10},{14... | collective-permute-start | bytes 1327112 | tf_op jit(solution)/shard_map/ppermute | solution.py:110
  43.4 23.0 %collective-permute-start.19 = (bf16[3,8,144,128]{3,2,1,0:T(8,128)(2,1)S(1)}, bf16[3,8,144,128]{3,2,1,0:T(8,128)(2,1)S(1)}, u32[]{:S(2)}, u32[]{:S(2)}) collective-permute-start(bf16[3,8,144,128]{3,2,1,0:T(8,128)(2,1)S(1)} %pad_maximum_fusion.1), channel_id=1, source_target_pairs={{0,8},{1,9},{10,18},{11,19},{20,28},{21,29},{30,6},{31,7}} | collective-permute-start | bytes 2654216 | tf_op jit(solution)/shard_map/ppermute | solution.py:118
  44.7 25.5 %collective-permute-start.18 = (bf16[3,8,144,128]{3,2,1,0:T(8,128)(2,1)S(1)}, bf16[3,8,144,128]{3,2,1,0:T(8,128)(2,1)S(1)}, u32[]{:S(2)}, u32[]{:S(2)}) collective-permute-start(bf16[3,8,144,128]{3,2,1,0:T(8,128)(2,1)S(1)} %pad_maximum_fusion.1), channel_id=1, source_target_pairs={{0,16},{1,17},{10,26},{11,27},{20,4},{21,5},{30,14},{31,15}} | collective-permute-start | bytes 2654216 | tf_op jit(solution)/shard_map/ppermute | solution.py:118
  47.1 24.5 %collective-permute-start.17 = (bf16[3,8,144,128]{3,2,1,0:T(8,128)(2,1)S(1)}, bf16[3,8,144,128]{3,2,1,0:T(8,128)(2,1)S(1)}, u32[]{:S(2)}, u32[]{:S(2)}) collective-permute-start(bf16[3,8,144,128]{3,2,1,0:T(8,128)(2,1)S(1)} %pad_maximum_fusion.1), channel_id=1, source_target_pairs={{0,24},{1,25},{10,2},{11,3},{20,12},{21,13},{30,22},{31,23}} | collective-permute-start | bytes 2654216 | tf_op jit(solution)/shard_map/ppermute | solution.py:118
  49.7 11.2 %collective-permute-start.8 = (bf16[3,2,2,144,128]{4,3,2,1,0:T(8,128)(2,1)S(1)}, bf16[3,2,2,144,128]{4,3,2,1,0:T(8,128)(2,1)S(1)}, u32[]{:S(2)}, u32[]{:S(2)}) collective-permute-start(bf16[3,2,2,144,128]{4,3,2,1,0:T(8,128)(2,1)S(1)} %collective-permute-done.6), channel_id=1, source_target_pairs={{0,2},{2,4},{4,6},{6,7},{7,5},{5,3},{3,1},{1,0},{8,10},{10,12},{12... | collective-permute-start | bytes 1327112 | tf_op jit(solution)/shard_map/ppermute | solution.py:109
  51.8 11.2 %collective-permute-start.9 = (bf16[3,2,2,144,128]{4,3,2,1,0:T(8,128)(2,1)S(1)}, bf16[3,2,2,144,128]{4,3,2,1,0:T(8,128)(2,1)S(1)}, u32[]{:S(2)}, u32[]{:S(2)}) collective-permute-start(bf16[3,2,2,144,128]{4,3,2,1,0:T(8,128)(2,1)S(1)} %collective-permute-done.7), channel_id=1, source_target_pairs={{2,0},{4,2},{6,4},{7,6},{5,7},{3,5},{1,3},{0,1},{10,8},{12,10},{14... | collective-permute-start | bytes 1327112 | tf_op jit(solution)/shard_map/ppermute | solution.py:110
  63.2 33.1 %collective-permute-start.22 = (bf16[3,8,144,128]{3,2,1,0:T(8,128)(2,1)S(1)}, bf16[3,8,144,128]{3,2,1,0:T(8,128)(2,1)S(1)}, u32[]{:S(2)}, u32[]{:S(2)}) collective-permute-start(bf16[3,8,144,128]{3,2,1,0:T(8,128)(2,1)S(1)} %pad_maximum_fusion.2), channel_id=1, source_target_pairs={{0,8},{1,9},{10,18},{11,19},{20,28},{21,29},{30,6},{31,7}} | collective-permute-start | bytes 2654216 | tf_op jit(solution)/shard_map/ppermute | solution.py:118
  64.6 10.3 %collective-permute-start.10 = (bf16[3,2,2,144,128]{4,3,2,1,0:T(8,128)(2,1)S(1)}, bf16[3,2,2,144,128]{4,3,2,1,0:T(8,128)(2,1)S(1)}, u32[]{:S(2)}, u32[]{:S(2)}) collective-permute-start(bf16[3,2,2,144,128]{4,3,2,1,0:T(8,128)(2,1)S(1)} %collective-permute-done.8), channel_id=1, source_target_pairs={{0,2},{2,4},{4,6},{6,7},{7,5},{5,3},{3,1},{1,0},{8,10},{10,12},{12... | collective-permute-start | bytes 1327112 | tf_op jit(solution)/shard_map/ppermute | solution.py:109
  66.4 32.1 %collective-permute-start.21 = (bf16[3,8,144,128]{3,2,1,0:T(8,128)(2,1)S(1)}, bf16[3,8,144,128]{3,2,1,0:T(8,128)(2,1)S(1)}, u32[]{:S(2)}, u32[]{:S(2)}) collective-permute-start(bf16[3,8,144,128]{3,2,1,0:T(8,128)(2,1)S(1)} %pad_maximum_fusion.2), channel_id=1, source_target_pairs={{0,16},{1,17},{10,26},{11,27},{20,4},{21,5},{30,14},{31,15}} | collective-permute-start | bytes 2654216 | tf_op jit(solution)/shard_map/ppermute | solution.py:118
  70.2 30.3 %collective-permute-start.20 = (bf16[3,8,144,128]{3,2,1,0:T(8,128)(2,1)S(1)}, bf16[3,8,144,128]{3,2,1,0:T(8,128)(2,1)S(1)}, u32[]{:S(2)}, u32[]{:S(2)}) collective-permute-start(bf16[3,8,144,128]{3,2,1,0:T(8,128)(2,1)S(1)} %pad_maximum_fusion.2), channel_id=1, source_target_pairs={{0,24},{1,25},{10,2},{11,3},{20,12},{21,13},{30,22},{31,23}} | collective-permute-start | bytes 2654216 | tf_op jit(solution)/shard_map/ppermute | solution.py:118
  71.6 10.8 %collective-permute-start.11 = (bf16[3,2,2,144,128]{4,3,2,1,0:T(8,128)(2,1)S(1)}, bf16[3,2,2,144,128]{4,3,2,1,0:T(8,128)(2,1)S(1)}, u32[]{:S(2)}, u32[]{:S(2)}) collective-permute-start(bf16[3,2,2,144,128]{4,3,2,1,0:T(8,128)(2,1)S(1)} %collective-permute-done.9), channel_id=1, source_target_pairs={{2,0},{4,2},{6,4},{7,6},{5,7},{3,5},{1,3},{0,1},{10,8},{12,10},{14... | collective-permute-start | bytes 1327112 | tf_op jit(solution)/shard_map/ppermute | solution.py:110
  74.9 25.6 %copy-start = (bf16[3,2,144,128]{3,2,1,0:T(8,128)(2,1)}, bf16[3,2,144,128]{3,2,1,0:T(8,128)(2,1)S(1)}, u32[]{:S(2)}) copy-start(bf16[3,2,144,128]{3,2,1,0:T(8,128)(2,1)S(1)} %dynamic-slice_bitcast_fusion.3) | copy-start | bytes 663556
  74.9 12.6 %collective-permute-start.12 = (bf16[3,2,2,144,128]{4,3,2,1,0:T(8,128)(2,1)S(1)}, bf16[3,2,2,144,128]{4,3,2,1,0:T(8,128)(2,1)S(1)}, u32[]{:S(2)}, u32[]{:S(2)}) collective-permute-start(bf16[3,2,2,144,128]{4,3,2,1,0:T(8,128)(2,1)S(1)} %collective-permute-done.10), channel_id=1, source_target_pairs={{0,2},{2,4},{4,6},{6,7},{7,5},{5,3},{3,1},{1,0},{8,10},{10,12},{12... | collective-permute-start | bytes 1327112 | tf_op jit(solution)/shard_map/ppermute | solution.py:109
  82.3 9.8 %collective-permute-start.13 = (bf16[3,2,2,144,128]{4,3,2,1,0:T(8,128)(2,1)S(1)}, bf16[3,2,2,144,128]{4,3,2,1,0:T(8,128)(2,1)S(1)}, u32[]{:S(2)}, u32[]{:S(2)}) collective-permute-start(bf16[3,2,2,144,128]{4,3,2,1,0:T(8,128)(2,1)S(1)} %collective-permute-done.11), channel_id=1, source_target_pairs={{2,0},{4,2},{6,4},{7,6},{5,7},{3,5},{1,3},{0,1},{10,8},{12,10},{14... | collective-permute-start | bytes 1327112 | tf_op jit(solution)/shard_map/ppermute | solution.py:110
  87.5 15.6 %collective-permute-start.25 = (bf16[3,4,144,128]{3,2,1,0:T(8,128)(2,1)}, bf16[3,4,144,128]{3,2,1,0:T(8,128)(2,1)S(1)}, u32[]{:S(2)}, u32[]{:S(2)}) collective-permute-start(bf16[3,4,144,128]{3,2,1,0:T(8,128)(2,1)} %pad_maximum_fusion.3), channel_id=1, source_target_pairs={{0,8},{1,9},{10,18},{11,19},{20,28},{21,29},{30,6},{31,7}} | collective-permute-start | bytes 1327112 | tf_op jit(solution)/shard_map/ppermute | solution.py:118
  89.1 11.4 %copy-start.1 = (bf16[3,2,144,128]{3,2,1,0:T(8,128)(2,1)}, bf16[3,2,144,128]{3,2,1,0:T(8,128)(2,1)S(1)}, u32[]{:S(2)}) copy-start(bf16[3,2,144,128]{3,2,1,0:T(8,128)(2,1)S(1)} %dynamic-slice_bitcast_fusion.1) | copy-start | bytes 663556
  92.1 17.6 %collective-permute-start.24 = (bf16[3,4,144,128]{3,2,1,0:T(8,128)(2,1)}, bf16[3,4,144,128]{3,2,1,0:T(8,128)(2,1)}, u32[]{:S(2)}, u32[]{:S(2)}) collective-permute-start(bf16[3,4,144,128]{3,2,1,0:T(8,128)(2,1)} %pad_maximum_fusion.3), channel_id=1, source_target_pairs={{0,16},{1,17},{10,26},{11,27},{20,4},{21,5},{30,14},{31,15}} | collective-permute-start | bytes 1327112 | tf_op jit(solution)/shard_map/ppermute | solution.py:118
  95.5 5.0 %copy-start.3 = (bf16[3,2,144,128]{3,2,1,0:T(8,128)(2,1)}, bf16[3,2,144,128]{3,2,1,0:T(8,128)(2,1)S(1)}, u32[]{:S(2)}) copy-start(bf16[3,2,144,128]{3,2,1,0:T(8,128)(2,1)S(1)} %dynamic-slice_bitcast_fusion) | copy-start | bytes 663556
  96.4 13.3 %collective-permute-start.23 = (bf16[3,4,144,128]{3,2,1,0:T(8,128)(2,1)}, bf16[3,4,144,128]{3,2,1,0:T(8,128)(2,1)}, u32[]{:S(2)}, u32[]{:S(2)}) collective-permute-start(bf16[3,4,144,128]{3,2,1,0:T(8,128)(2,1)} %pad_maximum_fusion.3), channel_id=1, source_target_pairs={{0,24},{1,25},{10,2},{11,3},{20,12},{21,13},{30,22},{31,23}} | collective-permute-start | bytes 1327112 | tf_op jit(solution)/shard_map/ppermute | solution.py:118
  98.4 12.6 %collective-permute-start.28 = (bf16[3,4,144,128]{3,2,1,0:T(8,128)(2,1)}, bf16[3,4,144,128]{3,2,1,0:T(8,128)(2,1)}, u32[]{:S(2)}, u32[]{:S(2)}) collective-permute-start(bf16[3,4,144,128]{3,2,1,0:T(8,128)(2,1)} %pad_maximum_fusion.4), channel_id=1, source_target_pairs={{0,8},{1,9},{10,18},{11,19},{20,28},{21,29},{30,6},{31,7}} | collective-permute-start | bytes 1327112 | tf_op jit(solution)/shard_map/ppermute | solution.py:118
  100.5 10.5 %collective-permute-start.27 = (bf16[3,4,144,128]{3,2,1,0:T(8,128)(2,1)}, bf16[3,4,144,128]{3,2,1,0:T(8,128)(2,1)}, u32[]{:S(2)}, u32[]{:S(2)}) collective-permute-start(bf16[3,4,144,128]{3,2,1,0:T(8,128)(2,1)} %pad_maximum_fusion.4), channel_id=1, source_target_pairs={{0,16},{1,17},{10,26},{11,27},{20,4},{21,5},{30,14},{31,15}} | collective-permute-start | bytes 1327112 | tf_op jit(solution)/shard_map/ppermute | solution.py:118
  103.1 11.9 %collective-permute-start.26 = (bf16[3,4,144,128]{3,2,1,0:T(8,128)(2,1)}, bf16[3,4,144,128]{3,2,1,0:T(8,128)(2,1)}, u32[]{:S(2)}, u32[]{:S(2)}) collective-permute-start(bf16[3,4,144,128]{3,2,1,0:T(8,128)(2,1)} %pad_maximum_fusion.4), channel_id=1, source_target_pairs={{0,24},{1,25},{10,2},{11,3},{20,12},{21,13},{30,22},{31,23}} | collective-permute-start | bytes 1327112 | tf_op jit(solution)/shard_map/ppermute | solution.py:118
  (2 other events, 8.7 us)

commit v17 on v16

--- a/solution.py
+++ b/solution.py
@@ -103,12 +103,16 @@
     batches = [[k, k + 1] for k in range(0, ncol - 2, 2)] + [[ncol - 2], [ncol - 1]]
     half = x.shape[1] // 2
     a, b = x[:, :half], x[:, half:]
-    pieces, columns, pending = [], [], []
+    oa, ob = slot_offset[:, :half], slot_offset[:, half:]
+    pieces, columns, pending, w_offs = [], [], [], []
     for step in range(ncol):
         if step:
             a = lax.ppermute(a, "col", forward)
             b = lax.ppermute(b, "col", backward)
+            oa = lax.ppermute(oa, "col", forward)
+            ob = lax.ppermute(ob, "col", backward)
         pieces += [a, b]
+        w_offs += [oa, ob]
         pending += [pick_slot(a), pick_slot(b)]
         if any(batch[-1] == step for batch in batches):
             own = jnp.concatenate(pending, axis=1)
@@ -124,7 +128,8 @@
     blocks = blocks.reshape(n, local_slots, blk + META, blk)
     column_blocks = column_blocks.reshape(n, blk + META, blk)
 
-    offs = jnp.concatenate([blocks[:, :, blk + 3, 0], column_blocks[:, blk + 3, 0][:, None]], axis=1)
+    w_offs = jnp.concatenate(w_offs, axis=1).reshape(n, local_slots).astype(jnp.bfloat16)
+    offs = jnp.concatenate([w_offs, column_blocks[:, blk + 3, 0][:, None]], axis=1)
     offs = jnp.clip(offs.astype(jnp.int32), 0, IBS - 1).reshape(-1)
     return gram_call(offs, blocks, column_blocks)
 

time: 131 us -> 154 us (1.18)
  waiting for transfers between devices: 47 us -> 64.1 us
  starting transfers between devices: 43.6 us -> 53 us
  other arithmetic: 10 us -> 7.41 us
  local copies, waits for them, and re-layouts: 17.8 us -> 16.2 us
    ppermute x0 -> x14, waiting for transfers between devices: none -> 18.6 us  [the longest x7 18.1 us: local(): ob = lax.ppermute(ob, 'col', backward)]
    ppermute x0 -> x14, starting transfers between devices: none -> 14.2 us  [the longest x7 10.5 us: local(): oa = lax.ppermute(oa, 'col', forward)]
    ppermute x15, waiting for transfers between devices: 4.03 us -> 12.1 us  [local(): got = jnp.where(which == j, lax.ppermute(own, ('row', 'col'), fan), got)]
    ppermute x7, waiting for transfers between devices: 31.5 us -> 24.6 us  [local(): a = lax.ppermute(a, 'col', forward)]
    ppermute x15, starting transfers between devices: 30.5 us -> 24.7 us  [local(): got = jnp.where(which == j, lax.ppermute(own, ('row', 'col'), fan), got)]
    ppermute x7, waiting for transfers between devices: 11.5 us -> 8.82 us  [local(): b = lax.ppermute(b, 'col', backward)]
    slice x2 -> x1, local copies, waits for them, and re-layouts: 2.72 us -> 0.83 us  [local(): oa, ob = (slot_offset[:, :half], slot_offset[:, half:])]
    concatenate x5, other arithmetic: 2.03 us -> 0.43 us  [local(): own = jnp.concatenate(pending, axis=1)]
  transfers between devices with their start and end apart: 29 -> 43, of which waited for: 11 -> 21; matrix products, arithmetic and copies ran while one was open for 15% -> 11% of each run, Pallas kernels for 0% -> 0%
where the time goes in v17:
time: 154 us; the launch traced here: 152 us
  waiting for transfers between devices  64.1 us (42%)
  starting transfers between devices  53 us (34%)
  local copies, waits for them, and re-layouts  16.2 us (11%)
  Pallas kernels  10.8 us (7%)
  other arithmetic  7.41 us (5%)
    ppermute x15, starting transfers between devices, local(): got = jnp.where(which == j, lax.ppermute(own, ('row', 'col'), fan), got)  24.7 us
    ppermute x7, waiting for transfers between devices, local(): a = lax.ppermute(a, 'col', forward)  24.6 us
    ppermute x7, waiting for transfers between devices, local(): ob = lax.ppermute(ob, 'col', backward)  18.1 us
    ppermute x15, waiting for transfers between devices, local(): got = jnp.where(which == j, lax.ppermute(own, ('row', 'col'), fan), got)  12.1 us
    ppermute x7, starting transfers between devices, local(): a = lax.ppermute(a, 'col', forward)  11.4 us
    unnamed x17, local copies, waits for them, and re-layouts  11.1 us
    pallas_call x1, Pallas kernels, gram_call(): pl.pallas_call(kernel, grid_spec=pltpu.PrefetchScalarGridSpec(num_scalar_...  10.8 us
    ppermute x7, starting transfers between devices, local(): oa = lax.ppermute(oa, 'col', forward)  10.5 us
  transfers between devices with their start and end apart: 43, of which 21 were waited for; matrix products, arithmetic and copies ran while one was open for 11% of the time, Pallas kernels for 0%

profile of v17, /device:TPU:0, one launch (start us, length us, event | category | flops | bytes accessed | tf_op | source)
XLA Modules:
  0.0 151.9 jit_solution(13145294938058049955)
XLA Ops:
  1.7 2.4 %constant_dynamic-update-slice_fusion.14 = (bf16[3,32,2,144,128]{4,3,2,1,0:T(8,128)(2,1)}, bf16[3,4,2,144,128]{4,3,2,1,0:T(8,128)(2,1)S(1)}) fusion(bf16[144]{0:T(256)(128)(2,1)S(1)} %pad.25.clone, bf16[3,4,2,1,128]{4,3,2,1,0:T(2,128)(2,1)S(1)} %broadcast_in_dim.7, bf16[3,4,2,3,128]{4,3,2,1,0:T(4,128)(2,1)S(1)} %broadcast_in_dim.6, ...), kind=kLoop, calls=%fused_computation.42 | loop fusion | flops 3538943 | bytes 2580768
  4.2 3.1 %collective-permute-start.14 = (bf16[3,2,2,144,128]{4,3,2,1,0:T(8,128)(2,1)S(1)}, bf16[3,2,2,144,128]{4,3,2,1,0:T(8,128)(2,1)S(1)}, u32[]{:S(2)}, u32[]{:S(2)}) collective-permute-start(bf16[3,2,2,144,128]{4,3,2,1,0:T(8,128)(2,1)S(1)} %get-tuple-element.5), channel_id=1, source_target_pairs={{0,2},{2,4},{4,6},{6,7},{7,5},{5,3},{3,1},{1,0},{8,10},{10,12},{12... | collective-permute-start | bytes 1327112 | tf_op jit(solution)/shard_map/ppermute | solution.py:110
  8.1 2.0 %collective-permute-start.1 = (s32[3,2,2]{1,2,0:T(2,128)S(1)}, s32[3,2,2]{1,2,0:T(2,128)S(1)}, u32[]{:S(2)}, u32[]{:S(2)}) collective-permute-start(s32[3,2,2]{1,2,0:T(2,128)S(1)} %get-tuple-element.12), channel_id=1, source_target_pairs={{2,0},{4,2},{6,4},{7,6},{5,7},{3,5},{1,3},{0,1},{10,8},{12,10},{14... | collective-permute-start | bytes 152 | tf_op jit(solution)/shard_map/ppermute | solution.py:113
  10.2 8.8 %collective-permute-done.1 = s32[3,2,2]{1,2,0:T(2,128)S(1)} collective-permute-done((s32[3,2,2]{1,2,0:T(2,128)S(1)}, s32[3,2,2]{1,2,0:T(2,128)S(1)}, u32[]{:S(2)}, u32[]{:S(2)}) %collective-permute-start.1) | collective-permute-done | bytes 80 | tf_op jit(solution)/shard_map/ppermute | solution.py:113
  19.2 1.7 %collective-permute-start.2 = (s32[3,2,2]{1,2,0:T(2,128)S(1)}, s32[3,2,2]{1,2,0:T(2,128)S(1)}, u32[]{:S(2)}, u32[]{:S(2)}) collective-permute-start(s32[3,2,2]{1,2,0:T(2,128)S(1)} %collective-permute-done), channel_id=1, source_target_pairs={{0,2},{2,4},{4,6},{6,7},{7,5},{5,3},{3,1},{1,0},{8,10},{10,12},{12... | collective-permute-start | bytes 152 | tf_op jit(solution)/shard_map/ppermute | solution.py:112
  22.9 1.7 %collective-permute-start.4 = (s32[3,2,2]{1,2,0:T(2,128)S(1)}, s32[3,2,2]{1,2,0:T(2,128)S(1)}, u32[]{:S(2)}, u32[]{:S(2)}) collective-permute-start(s32[3,2,2]{1,2,0:T(2,128)S(1)} %collective-permute-done.2), channel_id=1, source_target_pairs={{0,2},{2,4},{4,6},{6,7},{7,5},{5,3},{3,1},{1,0},{8,10},{10,12},{12... | collective-permute-start | bytes 152 | tf_op jit(solution)/shard_map/ppermute | solution.py:112
  26.5 1.7 %collective-permute-start.6 = (s32[3,2,2]{1,2,0:T(2,128)S(1)}, s32[3,2,2]{1,2,0:T(2,128)S(1)}, u32[]{:S(2)}, u32[]{:S(2)}) collective-permute-start(s32[3,2,2]{1,2,0:T(2,128)S(1)} %collective-permute-done.4), channel_id=1, source_target_pairs={{0,2},{2,4},{4,6},{6,7},{7,5},{5,3},{3,1},{1,0},{8,10},{10,12},{12... | collective-permute-start | bytes 152 | tf_op jit(solution)/shard_map/ppermute | solution.py:112
  30.1 1.7 %collective-permute-start.8 = (s32[3,2,2]{1,2,0:T(2,128)S(1)}, s32[3,2,2]{1,2,0:T(2,128)S(1)}, u32[]{:S(2)}, u32[]{:S(2)}) collective-permute-start(s32[3,2,2]{1,2,0:T(2,128)S(1)} %collective-permute-done.6), channel_id=1, source_target_pairs={{0,2},{2,4},{4,6},{6,7},{7,5},{5,3},{3,1},{1,0},{8,10},{10,12},{12... | collective-permute-start | bytes 152 | tf_op jit(solution)/shard_map/ppermute | solution.py:112
  33.7 1.7 %collective-permute-start.10 = (s32[3,2,2]{1,2,0:T(2,128)S(1)}, s32[3,2,2]{1,2,0:T(2,128)S(1)}, u32[]{:S(2)}, u32[]{:S(2)}) collective-permute-start(s32[3,2,2]{1,2,0:T(2,128)S(1)} %collective-permute-done.8), channel_id=1, source_target_pairs={{0,2},{2,4},{4,6},{6,7},{7,5},{5,3},{3,1},{1,0},{8,10},{10,12},{12... | collective-permute-start | bytes 152 | tf_op jit(solution)/shard_map/ppermute | solution.py:112
  37.4 1.7 %collective-permute-start.12 = (s32[3,2,2]{1,2,0:T(2,128)S(1)}, s32[3,2,2]{1,2,0:T(2,128)S(1)}, u32[]{:S(2)}, u32[]{:S(2)}) collective-permute-start(s32[3,2,2]{1,2,0:T(2,128)S(1)} %collective-permute-done.10), channel_id=1, source_target_pairs={{0,2},{2,4},{4,6},{6,7},{7,5},{5,3},{3,1},{1,0},{8,10},{10,12},{12... | collective-permute-start | bytes 152 | tf_op jit(solution)/shard_map/ppermute | solution.py:112
  41.2 1.7 %collective-permute-start.19 = (bf16[3,2,2,144,128]{4,3,2,1,0:T(8,128)(2,1)S(1)}, bf16[3,2,2,144,128]{4,3,2,1,0:T(8,128)(2,1)S(1)}, u32[]{:S(2)}, u32[]{:S(2)}) collective-permute-start(bf16[3,2,2,144,128]{4,3,2,1,0:T(8,128)(2,1)S(1)} %collective-permute-done.14), channel_id=1, source_target_pairs={{0,2},{2,4},{4,6},{6,7},{7,5},{5,3},{3,1},{1,0},{8,10},{10,12},{12... | collective-permute-start | bytes 1327112 | tf_op jit(solution)/shard_map/ppermute | solution.py:110
  44.8 3.0 %collective-permute-start.17 = (bf16[3,8,144,128]{3,2,1,0:T(8,128)(2,1)S(1)}, bf16[3,8,144,128]{3,2,1,0:T(8,128)(2,1)S(1)}, u32[]{:S(2)}, u32[]{:S(2)}) collective-permute-start(bf16[3,8,144,128]{3,2,1,0:T(8,128)(2,1)S(1)} %pad_maximum_fusion), channel_id=1, source_target_pairs={{0,16},{1,17},{10,26},{11,27},{20,4},{21,5},{30,14},{31,15}} | collective-permute-start | bytes 2654216 | tf_op jit(solution)/shard_map/ppermute | solution.py:122
  52.4 2.0 %collective-permute-start.22 = (bf16[3,2,2,144,128]{4,3,2,1,0:T(8,128)(2,1)S(1)}, bf16[3,2,2,144,128]{4,3,2,1,0:T(8,128)(2,1)S(1)}, u32[]{:S(2)}, u32[]{:S(2)}) collective-permute-start(bf16[3,2,2,144,128]{4,3,2,1,0:T(8,128)(2,1)S(1)} %collective-permute-done.20), channel_id=1, source_target_pairs={{2,0},{4,2},{6,4},{7,6},{5,7},{3,5},{1,3},{0,1},{10,8},{12,10},{14... | collective-permute-start | bytes 1327112 | tf_op jit(solution)/shard_map/ppermute | solution.py:111
  56.2 6.6 %collective-permute-done.21 = bf16[3,2,2,144,128]{4,3,2,1,0:T(8,128)(2,1)S(1)} collective-permute-done((bf16[3,2,2,144,128]{4,3,2,1,0:T(8,128)(2,1)S(1)}, bf16[3,2,2,144,128]{4,3,2,1,0:T(8,128)(2,1)S(1)}, u32[]{:S(2)}, u32[]{:S(2)}) %collective-permute-start.21) | collective-permute-done | bytes 442400 | tf_op jit(solution)/shard_map/ppermute | solution.py:110
  62.8 2.5 %collective-permute-start.26 = (bf16[3,2,2,144,128]{4,3,2,1,0:T(8,128)(2,1)S(1)}, bf16[3,2,2,144,128]{4,3,2,1,0:T(8,128)(2,1)S(1)}, u32[]{:S(2)}, u32[]{:S(2)}) collective-permute-start(bf16[3,2,2,144,128]{4,3,2,1,0:T(8,128)(2,1)S(1)} %collective-permute-done.21), channel_id=1, source_target_pairs={{0,2},{2,4},{4,6},{6,7},{7,5},{5,3},{3,1},{1,0},{8,10},{10,12},{12... | collective-permute-start | bytes 1327112 | tf_op jit(solution)/shard_map/ppermute | solution.py:110
  67.2 1.6 %collective-permute-start.25 = (bf16[3,8,144,128]{3,2,1,0:T(8,128)(2,1)S(1)}, bf16[3,8,144,128]{3,2,1,0:T(8,128)(2,1)S(1)}, u32[]{:S(2)}, u32[]{:S(2)}) collective-permute-start(bf16[3,8,144,128]{3,2,1,0:T(8,128)(2,1)S(1)} %pad_maximum_fusion.1), channel_id=1, source_target_pairs={{0,8},{1,9},{10,18},{11,19},{20,28},{21,29},{30,6},{31,7}} | collective-permute-start | bytes 2654216 | tf_op jit(solution)/shard_map/ppermute | solution.py:122
  68.8 1.8 %collective-permute-start.24 = (bf16[3,8,144,128]{3,2,1,0:T(8,128)(2,1)S(1)}, bf16[3,8,144,128]{3,2,1,0:T(8,128)(2,1)S(1)}, u32[]{:S(2)}, u32[]{:S(2)}) collective-permute-start(bf16[3,8,144,128]{3,2,1,0:T(8,128)(2,1)S(1)} %pad_maximum_fusion.1), channel_id=1, source_target_pairs={{0,16},{1,17},{10,26},{11,27},{20,4},{21,5},{30,14},{31,15}} | collective-permute-start | bytes 2654216 | tf_op jit(solution)/shard_map/ppermute | solution.py:122
  73.6 1.6 %collective-permute-done.26 = bf16[3,2,2,144,128]{4,3,2,1,0:T(8,128)(2,1)S(1)} collective-permute-done((bf16[3,2,2,144,128]{4,3,2,1,0:T(8,128)(2,1)S(1)}, bf16[3,2,2,144,128]{4,3,2,1,0:T(8,128)(2,1)S(1)}, u32[]{:S(2)}, u32[]{:S(2)}) %collective-permute-start.26) | collective-permute-done | bytes 442400 | tf_op jit(solution)/shard_map/ppermute | solution.py:110
  75.2 2.1 %collective-permute-start.28 = (bf16[3,2,2,144,128]{4,3,2,1,0:T(8,128)(2,1)S(1)}, bf16[3,2,2,144,128]{4,3,2,1,0:T(8,128)(2,1)S(1)}, u32[]{:S(2)}, u32[]{:S(2)}) collective-permute-start(bf16[3,2,2,144,128]{4,3,2,1,0:T(8,128)(2,1)S(1)} %collective-permute-done.26), channel_id=1, source_target_pairs={{0,2},{2,4},{4,6},{6,7},{7,5},{5,3},{3,1},{1,0},{8,10},{10,12},{12... | collective-permute-start | bytes 1327112 | tf_op jit(solution)/shard_map/ppermute | solution.py:110
  79.1 7.4 %collective-permute-done.28 = bf16[3,2,2,144,128]{4,3,2,1,0:T(8,128)(2,1)S(1)} collective-permute-done((bf16[3,2,2,144,128]{4,3,2,1,0:T(8,128)(2,1)S(1)}, bf16[3,2,2,144,128]{4,3,2,1,0:T(8,128)(2,1)S(1)}, u32[]{:S(2)}, u32[]{:S(2)}) %collective-permute-start.28) | collective-permute-done | bytes 442400 | tf_op jit(solution)/shard_map/ppermute | solution.py:110
  86.5 1.7 %collective-permute-done.29 = bf16[3,2,2,144,128]{4,3,2,1,0:T(8,128)(2,1)S(1)} collective-permute-done((bf16[3,2,2,144,128]{4,3,2,1,0:T(8,128)(2,1)S(1)}, bf16[3,2,2,144,128]{4,3,2,1,0:T(8,128)(2,1)S(1)}, u32[]{:S(2)}, u32[]{:S(2)}) %collective-permute-start.29) | collective-permute-done | bytes 442400 | tf_op jit(solution)/shard_map/ppermute | solution.py:111
  91.5 3.3 %collective-permute-start.31 = (bf16[3,8,144,128]{3,2,1,0:T(8,128)(2,1)S(1)}, bf16[3,8,144,128]{3,2,1,0:T(8,128)(2,1)S(1)}, u32[]{:S(2)}, u32[]{:S(2)}) collective-permute-start(bf16[3,8,144,128]{3,2,1,0:T(8,128)(2,1)S(1)} %pad_maximum_fusion.2), channel_id=1, source_target_pairs={{0,16},{1,17},{10,26},{11,27},{20,4},{21,5},{30,14},{31,15}} | collective-permute-start | bytes 2654216 | tf_op jit(solution)/shard_map/ppermute | solution.py:122
  96.8 2.8 %collective-permute-done.33 = bf16[3,2,2,144,128]{4,3,2,1,0:T(8,128)(2,1)S(1)} collective-permute-done((bf16[3,2,2,144,128]{4,3,2,1,0:T(8,128)(2,1)S(1)}, bf16[3,2,2,144,128]{4,3,2,1,0:T(8,128)(2,1)S(1)}, u32[]{:S(2)}, u32[]{:S(2)}) %collective-permute-start.33) | collective-permute-done | bytes 442400 | tf_op jit(solution)/shard_map/ppermute | solution.py:110
  99.6 1.9 %collective-permute-start.38 = (bf16[3,2,2,144,128]{4,3,2,1,0:T(8,128)(2,1)S(1)}, bf16[3,2,2,144,128]{4,3,2,1,0:T(8,128)(2,1)S(1)}, u32[]{:S(2)}, u32[]{:S(2)}) collective-permute-start(bf16[3,2,2,144,128]{4,3,2,1,0:T(8,128)(2,1)S(1)} %collective-permute-done.33), channel_id=1, source_target_pairs={{0,2},{2,4},{4,6},{6,7},{7,5},{5,3},{3,1},{1,0},{8,10},{10,12},{12... | collective-permute-start | bytes 1327112 | tf_op jit(solution)/shard_map/ppermute | solution.py:110
  101.6 5.4 %collective-permute-done.34 = bf16[3,2,2,144,128]{4,3,2,1,0:T(8,128)(2,1)S(1)} collective-permute-done((bf16[3,2,2,144,128]{4,3,2,1,0:T(8,128)(2,1)S(1)}, bf16[3,2,2,144,128]{4,3,2,1,0:T(8,128)(2,1)S(1)}, u32[]{:S(2)}, u32[]{:S(2)}) %collective-permute-start.34) | collective-permute-done | bytes 442400 | tf_op jit(solution)/shard_map/ppermute | solution.py:111
  109.0 4.6 %collective-permute-done.38 = bf16[3,2,2,144,128]{4,3,2,1,0:T(8,128)(2,1)S(1)} collective-permute-done((bf16[3,2,2,144,128]{4,3,2,1,0:T(8,128)(2,1)S(1)}, bf16[3,2,2,144,128]{4,3,2,1,0:T(8,128)(2,1)S(1)}, u32[]{:S(2)}, u32[]{:S(2)}) %collective-permute-start.38) | collective-permute-done | bytes 442400 | tf_op jit(solution)/shard_map/ppermute | solution.py:110
  113.6 1.6 %collective-permute-start.37 = (bf16[3,4,144,128]{3,2,1,0:T(8,128)(2,1)S(1)}, bf16[3,4,144,128]{3,2,1,0:T(8,128)(2,1)S(1)}, u32[]{:S(2)}, u32[]{:S(2)}) collective-permute-start(bf16[3,4,144,128]{3,2,1,0:T(8,128)(2,1)S(1)} %pad_maximum_fusion.3), channel_id=1, source_target_pairs={{0,8},{1,9},{10,18},{11,19},{20,28},{21,29},{30,6},{31,7}} | collective-permute-start | bytes 1327112 | tf_op jit(solution)/shard_map/ppermute | solution.py:122
  115.2 1.8 %collective-permute-done.39 = bf16[3,2,2,144,128]{4,3,2,1,0:T(8,128)(2,1)S(1)} collective-permute-done((bf16[3,2,2,144,128]{4,3,2,1,0:T(8,128)(2,1)S(1)}, bf16[3,2,2,144,128]{4,3,2,1,0:T(8,128)(2,1)S(1)}, u32[]{:S(2)}, u32[]{:S(2)}) %collective-permute-start.39) | collective-permute-done | bytes 442400 | tf_op jit(solution)/shard_map/ppermute | solution.py:111
  126.0 2.9 %collective-permute-done.35 = bf16[3,4,144,128]{3,2,1,0:T(8,128)(2,1)S(1)} collective-permute-done((bf16[3,4,144,128]{3,2,1,0:T(8,128)(2,1)S(1)}, bf16[3,4,144,128]{3,2,1,0:T(8,128)(2,1)S(1)}, u32[]{:S(2)}, u32[]{:S(2)}) %collective-permute-start.35) | collective-permute-done | bytes 442400 | tf_op jit(solution)/shard_map/ppermute | solution.py:122
  129.1 4.5 %collective-permute-done.41 = bf16[3,4,144,128]{3,2,1,0:T(8,128)(2,1)S(1)} collective-permute-done((bf16[3,4,144,128]{3,2,1,0:T(8,128)(2,1)S(1)}, bf16[3,4,144,128]{3,2,1,0:T(8,128)(2,1)S(1)}, u32[]{:S(2)}, u32[]{:S(2)}) %collective-permute-start.41) | collective-permute-done | bytes 442400 | tf_op jit(solution)/shard_map/ppermute | solution.py:122
  133.6 4.7 %collective-permute-done.40 = bf16[3,4,144,128]{3,2,1,0:T(8,128)(2,1)S(1)} collective-permute-done((bf16[3,4,144,128]{3,2,1,0:T(8,128)(2,1)S(1)}, bf16[3,4,144,128]{3,2,1,0:T(8,128)(2,1)S(1)}, u32[]{:S(2)}, u32[]{:S(2)}) %collective-permute-start.40) | collective-permute-done | bytes 442400 | tf_op jit(solution)/shard_map/ppermute | solution.py:122
  141.1 10.8 %shard_map.37 = f32[2048,1024]{1,0:T(8,128)} custom-call(s32[288]{0:T(512)S(1)} %min.12.offs_ref, bf16[96,2,144,128]{3,2,1,0:T(8,128)(2,1)} %bitcast.45, bf16[96,144,128]{2,1,0:T(8,128)(2,1)S(1)} %bitcast.44), custom_call_target="tpu_custom_call" | custom-call | flops 805306368 | bytes 17825792 | tf_op jit(solution)/shard_map/pallas_call | solution.py:40
  (131 shorter events, 48.5 us)
Async XLA Ops:
  4.2 37.0 %collective-permute-start.14 = (bf16[3,2,2,144,128]{4,3,2,1,0:T(8,128)(2,1)S(1)}, bf16[3,2,2,144,128]{4,3,2,1,0:T(8,128)(2,1)S(1)}, u32[]{:S(2)}, u32[]{:S(2)}) collective-permute-start(bf16[3,2,2,144,128]{4,3,2,1,0:T(8,128)(2,1)S(1)} %get-tuple-element.5), channel_id=1, source_target_pairs={{0,2},{2,4},{4,6},{6,7},{7,5},{5,3},{3,1},{1,0},{8,10},{10,12},{12... | collective-permute-start | bytes 1327112 | tf_op jit(solution)/shard_map/ppermute | solution.py:110
  7.3 35.7 %collective-permute-start.15 = (bf16[3,2,2,144,128]{4,3,2,1,0:T(8,128)(2,1)S(1)}, bf16[3,2,2,144,128]{4,3,2,1,0:T(8,128)(2,1)S(1)}, u32[]{:S(2)}, u32[]{:S(2)}) collective-permute-start(bf16[3,2,2,144,128]{4,3,2,1,0:T(8,128)(2,1)S(1)} %get-tuple-element.6), channel_id=1, source_target_pairs={{2,0},{4,2},{6,4},{7,6},{5,7},{3,5},{1,3},{0,1},{10,8},{12,10},{14... | collective-permute-start | bytes 1327112 | tf_op jit(solution)/shard_map/ppermute | solution.py:111
  8.1 10.9 %collective-permute-start.1 = (s32[3,2,2]{1,2,0:T(2,128)S(1)}, s32[3,2,2]{1,2,0:T(2,128)S(1)}, u32[]{:S(2)}, u32[]{:S(2)}) collective-permute-start(s32[3,2,2]{1,2,0:T(2,128)S(1)} %get-tuple-element.12), channel_id=1, source_target_pairs={{2,0},{4,2},{6,4},{7,6},{5,7},{3,5},{1,3},{0,1},{10,8},{12,10},{14... | collective-permute-start | bytes 152 | tf_op jit(solution)/shard_map/ppermute | solution.py:113
  10.1 9.2 %collective-permute-start = (s32[3,2,2]{1,2,0:T(2,128)S(1)}, s32[3,2,2]{1,2,0:T(2,128)S(1)}, u32[]{:S(2)}, u32[]{:S(2)}) collective-permute-start(s32[3,2,2]{1,2,0:T(2,128)S(1)} %get-tuple-element.13), channel_id=1, source_target_pairs={{0,2},{2,4},{4,6},{6,7},{7,5},{5,3},{3,1},{1,0},{8,10},{10,12},{12... | collective-permute-start | bytes 152 | tf_op jit(solution)/shard_map/ppermute | solution.py:112
  33.7 3.7 %collective-permute-start.10 = (s32[3,2,2]{1,2,0:T(2,128)S(1)}, s32[3,2,2]{1,2,0:T(2,128)S(1)}, u32[]{:S(2)}, u32[]{:S(2)}) collective-permute-start(s32[3,2,2]{1,2,0:T(2,128)S(1)} %collective-permute-done.8), channel_id=1, source_target_pairs={{0,2},{2,4},{4,6},{6,7},{7,5},{5,3},{3,1},{1,0},{8,10},{10,12},{12... | collective-permute-start | bytes 152 | tf_op jit(solution)/shard_map/ppermute | solution.py:112
  41.2 11.2 %collective-permute-start.19 = (bf16[3,2,2,144,128]{4,3,2,1,0:T(8,128)(2,1)S(1)}, bf16[3,2,2,144,128]{4,3,2,1,0:T(8,128)(2,1)S(1)}, u32[]{:S(2)}, u32[]{:S(2)}) collective-permute-start(bf16[3,2,2,144,128]{4,3,2,1,0:T(8,128)(2,1)S(1)} %collective-permute-done.14), channel_id=1, source_target_pairs={{0,2},{2,4},{4,6},{6,7},{7,5},{5,3},{3,1},{1,0},{8,10},{10,12},{12... | collective-permute-start | bytes 1327112 | tf_op jit(solution)/shard_map/ppermute | solution.py:110
  43.0 9.4 %collective-permute-start.20 = (bf16[3,2,2,144,128]{4,3,2,1,0:T(8,128)(2,1)S(1)}, bf16[3,2,2,144,128]{4,3,2,1,0:T(8,128)(2,1)S(1)}, u32[]{:S(2)}, u32[]{:S(2)}) collective-permute-start(bf16[3,2,2,144,128]{4,3,2,1,0:T(8,128)(2,1)S(1)} %collective-permute-done.15), channel_id=1, source_target_pairs={{2,0},{4,2},{6,4},{7,6},{5,7},{3,5},{1,3},{0,1},{10,8},{12,10},{14... | collective-permute-start | bytes 1327112 | tf_op jit(solution)/shard_map/ppermute | solution.py:111
  43.5 23.7 %collective-permute-start.18 = (bf16[3,8,144,128]{3,2,1,0:T(8,128)(2,1)S(1)}, bf16[3,8,144,128]{3,2,1,0:T(8,128)(2,1)S(1)}, u32[]{:S(2)}, u32[]{:S(2)}) collective-permute-start(bf16[3,8,144,128]{3,2,1,0:T(8,128)(2,1)S(1)} %pad_maximum_fusion), channel_id=1, source_target_pairs={{0,8},{1,9},{10,18},{11,19},{20,28},{21,29},{30,6},{31,7}} | collective-permute-start | bytes 2654216 | tf_op jit(solution)/shard_map/ppermute | solution.py:122
  44.8 24.0 %collective-permute-start.17 = (bf16[3,8,144,128]{3,2,1,0:T(8,128)(2,1)S(1)}, bf16[3,8,144,128]{3,2,1,0:T(8,128)(2,1)S(1)}, u32[]{:S(2)}, u32[]{:S(2)}) collective-permute-start(bf16[3,8,144,128]{3,2,1,0:T(8,128)(2,1)S(1)} %pad_maximum_fusion), channel_id=1, source_target_pairs={{0,16},{1,17},{10,26},{11,27},{20,4},{21,5},{30,14},{31,15}} | collective-permute-start | bytes 2654216 | tf_op jit(solution)/shard_map/ppermute | solution.py:122
  47.8 22.8 %collective-permute-start.16 = (bf16[3,8,144,128]{3,2,1,0:T(8,128)(2,1)S(1)}, bf16[3,8,144,128]{3,2,1,0:T(8,128)(2,1)S(1)}, u32[]{:S(2)}, u32[]{:S(2)}) collective-permute-start(bf16[3,8,144,128]{3,2,1,0:T(8,128)(2,1)S(1)} %pad_maximum_fusion), channel_id=1, source_target_pairs={{0,24},{1,25},{10,2},{11,3},{20,12},{21,13},{30,22},{31,23}} | collective-permute-start | bytes 2654216 | tf_op jit(solution)/shard_map/ppermute | solution.py:122
  52.4 10.4 %collective-permute-start.21 = (bf16[3,2,2,144,128]{4,3,2,1,0:T(8,128)(2,1)S(1)}, bf16[3,2,2,144,128]{4,3,2,1,0:T(8,128)(2,1)S(1)}, u32[]{:S(2)}, u32[]{:S(2)}) collective-permute-start(bf16[3,2,2,144,128]{4,3,2,1,0:T(8,128)(2,1)S(1)} %collective-permute-done.19), channel_id=1, source_target_pairs={{0,2},{2,4},{4,6},{6,7},{7,5},{5,3},{3,1},{1,0},{8,10},{10,12},{12... | collective-permute-start | bytes 1327112 | tf_op jit(solution)/shard_map/ppermute | solution.py:110
  52.4 12.9 %collective-permute-start.22 = (bf16[3,2,2,144,128]{4,3,2,1,0:T(8,128)(2,1)S(1)}, bf16[3,2,2,144,128]{4,3,2,1,0:T(8,128)(2,1)S(1)}, u32[]{:S(2)}, u32[]{:S(2)}) collective-permute-start(bf16[3,2,2,144,128]{4,3,2,1,0:T(8,128)(2,1)S(1)} %collective-permute-done.20), channel_id=1, source_target_pairs={{2,0},{4,2},{6,4},{7,6},{5,7},{3,5},{1,3},{0,1},{10,8},{12,10},{14... | collective-permute-start | bytes 1327112 | tf_op jit(solution)/shard_map/ppermute | solution.py:111
  62.8 12.4 %collective-permute-start.26 = (bf16[3,2,2,144,128]{4,3,2,1,0:T(8,128)(2,1)S(1)}, bf16[3,2,2,144,128]{4,3,2,1,0:T(8,128)(2,1)S(1)}, u32[]{:S(2)}, u32[]{:S(2)}) collective-permute-start(bf16[3,2,2,144,128]{4,3,2,1,0:T(8,128)(2,1)S(1)} %collective-permute-done.21), channel_id=1, source_target_pairs={{0,2},{2,4},{4,6},{6,7},{7,5},{5,3},{3,1},{1,0},{8,10},{10,12},{12... | collective-permute-start | bytes 1327112 | tf_op jit(solution)/shard_map/ppermute | solution.py:110
  65.3 12.0 %collective-permute-start.27 = (bf16[3,2,2,144,128]{4,3,2,1,0:T(8,128)(2,1)S(1)}, bf16[3,2,2,144,128]{4,3,2,1,0:T(8,128)(2,1)S(1)}, u32[]{:S(2)}, u32[]{:S(2)}) collective-permute-start(bf16[3,2,2,144,128]{4,3,2,1,0:T(8,128)(2,1)S(1)} %collective-permute-done.22), channel_id=1, source_target_pairs={{2,0},{4,2},{6,4},{7,6},{5,7},{3,5},{1,3},{0,1},{10,8},{12,10},{14... | collective-permute-start | bytes 1327112 | tf_op jit(solution)/shard_map/ppermute | solution.py:111
  67.2 24.3 %collective-permute-start.25 = (bf16[3,8,144,128]{3,2,1,0:T(8,128)(2,1)S(1)}, bf16[3,8,144,128]{3,2,1,0:T(8,128)(2,1)S(1)}, u32[]{:S(2)}, u32[]{:S(2)}) collective-permute-start(bf16[3,8,144,128]{3,2,1,0:T(8,128)(2,1)S(1)} %pad_maximum_fusion.1), channel_id=1, source_target_pairs={{0,8},{1,9},{10,18},{11,19},{20,28},{21,29},{30,6},{31,7}} | collective-permute-start | bytes 2654216 | tf_op jit(solution)/shard_map/ppermute | solution.py:122
  68.8 26.0 %collective-permute-start.24 = (bf16[3,8,144,128]{3,2,1,0:T(8,128)(2,1)S(1)}, bf16[3,8,144,128]{3,2,1,0:T(8,128)(2,1)S(1)}, u32[]{:S(2)}, u32[]{:S(2)}) collective-permute-start(bf16[3,8,144,128]{3,2,1,0:T(8,128)(2,1)S(1)} %pad_maximum_fusion.1), channel_id=1, source_target_pairs={{0,16},{1,17},{10,26},{11,27},{20,4},{21,5},{30,14},{31,15}} | collective-permute-start | bytes 2654216 | tf_op jit(solution)/shard_map/ppermute | solution.py:122
  70.7 25.5 %collective-permute-start.23 = (bf16[3,8,144,128]{3,2,1,0:T(8,128)(2,1)S(1)}, bf16[3,8,144,128]{3,2,1,0:T(8,128)(2,1)S(1)}, u32[]{:S(2)}, u32[]{:S(2)}) collective-permute-start(bf16[3,8,144,128]{3,2,1,0:T(8,128)(2,1)S(1)} %pad_maximum_fusion.1), channel_id=1, source_target_pairs={{0,24},{1,25},{10,2},{11,3},{20,12},{21,13},{30,22},{31,23}} | collective-permute-start | bytes 2654216 | tf_op jit(solution)/shard_map/ppermute | solution.py:122
  75.2 11.3 %collective-permute-start.28 = (bf16[3,2,2,144,128]{4,3,2,1,0:T(8,128)(2,1)S(1)}, bf16[3,2,2,144,128]{4,3,2,1,0:T(8,128)(2,1)S(1)}, u32[]{:S(2)}, u32[]{:S(2)}) collective-permute-start(bf16[3,2,2,144,128]{4,3,2,1,0:T(8,128)(2,1)S(1)} %collective-permute-done.26), channel_id=1, source_target_pairs={{0,2},{2,4},{4,6},{6,7},{7,5},{5,3},{3,1},{1,0},{8,10},{10,12},{12... | collective-permute-start | bytes 1327112 | tf_op jit(solution)/shard_map/ppermute | solution.py:110
  77.3 10.9 %collective-permute-start.29 = (bf16[3,2,2,144,128]{4,3,2,1,0:T(8,128)(2,1)S(1)}, bf16[3,2,2,144,128]{4,3,2,1,0:T(8,128)(2,1)S(1)}, u32[]{:S(2)}, u32[]{:S(2)}) collective-permute-start(bf16[3,2,2,144,128]{4,3,2,1,0:T(8,128)(2,1)S(1)} %collective-permute-done.27), channel_id=1, source_target_pairs={{2,0},{4,2},{6,4},{7,6},{5,7},{3,5},{1,3},{0,1},{10,8},{12,10},{14... | collective-permute-start | bytes 1327112 | tf_op jit(solution)/shard_map/ppermute | solution.py:111
  88.3 30.1 %collective-permute-start.32 = (bf16[3,8,144,128]{3,2,1,0:T(8,128)(2,1)S(1)}, bf16[3,8,144,128]{3,2,1,0:T(8,128)(2,1)S(1)}, u32[]{:S(2)}, u32[]{:S(2)}) collective-permute-start(bf16[3,8,144,128]{3,2,1,0:T(8,128)(2,1)S(1)} %pad_maximum_fusion.2), channel_id=1, source_target_pairs={{0,8},{1,9},{10,18},{11,19},{20,28},{21,29},{30,6},{31,7}} | collective-permute-start | bytes 2654216 | tf_op jit(solution)/shard_map/ppermute | solution.py:122
  89.7 10.0 %collective-permute-start.33 = (bf16[3,2,2,144,128]{4,3,2,1,0:T(8,128)(2,1)S(1)}, bf16[3,2,2,144,128]{4,3,2,1,0:T(8,128)(2,1)S(1)}, u32[]{:S(2)}, u32[]{:S(2)}) collective-permute-start(bf16[3,2,2,144,128]{4,3,2,1,0:T(8,128)(2,1)S(1)} %collective-permute-done.28), channel_id=1, source_target_pairs={{0,2},{2,4},{4,6},{6,7},{7,5},{5,3},{3,1},{1,0},{8,10},{10,12},{12... | collective-permute-start | bytes 1327112 | tf_op jit(solution)/shard_map/ppermute | solution.py:110
  91.5 28.3 %collective-permute-start.31 = (bf16[3,8,144,128]{3,2,1,0:T(8,128)(2,1)S(1)}, bf16[3,8,144,128]{3,2,1,0:T(8,128)(2,1)S(1)}, u32[]{:S(2)}, u32[]{:S(2)}) collective-permute-start(bf16[3,8,144,128]{3,2,1,0:T(8,128)(2,1)S(1)} %pad_maximum_fusion.2), channel_id=1, source_target_pairs={{0,16},{1,17},{10,26},{11,27},{20,4},{21,5},{30,14},{31,15}} | collective-permute-start | bytes 2654216 | tf_op jit(solution)/shard_map/ppermute | solution.py:122
  94.8 26.2 %collective-permute-start.30 = (bf16[3,8,144,128]{3,2,1,0:T(8,128)(2,1)S(1)}, bf16[3,8,144,128]{3,2,1,0:T(8,128)(2,1)S(1)}, u32[]{:S(2)}, u32[]{:S(2)}) collective-permute-start(bf16[3,8,144,128]{3,2,1,0:T(8,128)(2,1)S(1)} %pad_maximum_fusion.2), channel_id=1, source_target_pairs={{0,24},{1,25},{10,2},{11,3},{20,12},{21,13},{30,22},{31,23}} | collective-permute-start | bytes 2654216 | tf_op jit(solution)/shard_map/ppermute | solution.py:122
  96.2 10.8 %collective-permute-start.34 = (bf16[3,2,2,144,128]{4,3,2,1,0:T(8,128)(2,1)S(1)}, bf16[3,2,2,144,128]{4,3,2,1,0:T(8,128)(2,1)S(1)}, u32[]{:S(2)}, u32[]{:S(2)}) collective-permute-start(bf16[3,2,2,144,128]{4,3,2,1,0:T(8,128)(2,1)S(1)} %collective-permute-done.29), channel_id=1, source_target_pairs={{2,0},{4,2},{6,4},{7,6},{5,7},{3,5},{1,3},{0,1},{10,8},{12,10},{14... | collective-permute-start | bytes 1327112 | tf_op jit(solution)/shard_map/ppermute | solution.py:111
  99.6 13.9 %collective-permute-start.38 = (bf16[3,2,2,144,128]{4,3,2,1,0:T(8,128)(2,1)S(1)}, bf16[3,2,2,144,128]{4,3,2,1,0:T(8,128)(2,1)S(1)}, u32[]{:S(2)}, u32[]{:S(2)}) collective-permute-start(bf16[3,2,2,144,128]{4,3,2,1,0:T(8,128)(2,1)S(1)} %collective-permute-done.33), channel_id=1, source_target_pairs={{0,2},{2,4},{4,6},{6,7},{7,5},{5,3},{3,1},{1,0},{8,10},{10,12},{12... | collective-permute-start | bytes 1327112 | tf_op jit(solution)/shard_map/ppermute | solution.py:110
  107.0 10.1 %collective-permute-start.39 = (bf16[3,2,2,144,128]{4,3,2,1,0:T(8,128)(2,1)S(1)}, bf16[3,2,2,144,128]{4,3,2,1,0:T(8,128)(2,1)S(1)}, u32[]{:S(2)}, u32[]{:S(2)}) collective-permute-start(bf16[3,2,2,144,128]{4,3,2,1,0:T(8,128)(2,1)S(1)} %collective-permute-done.34), channel_id=1, source_target_pairs={{2,0},{4,2},{6,4},{7,6},{5,7},{3,5},{1,3},{0,1},{10,8},{12,10},{14... | collective-permute-start | bytes 1327112 | tf_op jit(solution)/shard_map/ppermute | solution.py:111
  113.6 9.4 %collective-permute-start.37 = (bf16[3,4,144,128]{3,2,1,0:T(8,128)(2,1)S(1)}, bf16[3,4,144,128]{3,2,1,0:T(8,128)(2,1)S(1)}, u32[]{:S(2)}, u32[]{:S(2)}) collective-permute-start(bf16[3,4,144,128]{3,2,1,0:T(8,128)(2,1)S(1)} %pad_maximum_fusion.3), channel_id=1, source_target_pairs={{0,8},{1,9},{10,18},{11,19},{20,28},{21,29},{30,6},{31,7}} | collective-permute-start | bytes 1327112 | tf_op jit(solution)/shard_map/ppermute | solution.py:122
  117.0 9.0 %collective-permute-start.36 = (bf16[3,4,144,128]{3,2,1,0:T(8,128)(2,1)S(1)}, bf16[3,4,144,128]{3,2,1,0:T(8,128)(2,1)S(1)}, u32[]{:S(2)}, u32[]{:S(2)}) collective-permute-start(bf16[3,4,144,128]{3,2,1,0:T(8,128)(2,1)S(1)} %pad_maximum_fusion.3), channel_id=1, source_target_pairs={{0,16},{1,17},{10,26},{11,27},{20,4},{21,5},{30,14},{31,15}} | collective-permute-start | bytes 1327112 | tf_op jit(solution)/shard_map/ppermute | solution.py:122
  118.4 10.4 %collective-permute-start.35 = (bf16[3,4,144,128]{3,2,1,0:T(8,128)(2,1)S(1)}, bf16[3,4,144,128]{3,2,1,0:T(8,128)(2,1)S(1)}, u32[]{:S(2)}, u32[]{:S(2)}) collective-permute-start(bf16[3,4,144,128]{3,2,1,0:T(8,128)(2,1)S(1)} %pad_maximum_fusion.3), channel_id=1, source_target_pairs={{0,24},{1,25},{10,2},{11,3},{20,12},{21,13},{30,22},{31,23}} | collective-permute-start | bytes 1327112 | tf_op jit(solution)/shard_map/ppermute | solution.py:122
  119.8 9.4 %collective-permute-start.42 = (bf16[3,4,144,128]{3,2,1,0:T(8,128)(2,1)S(1)}, bf16[3,4,144,128]{3,2,1,0:T(8,128)(2,1)S(1)}, u32[]{:S(2)}, u32[]{:S(2)}) collective-permute-start(bf16[3,4,144,128]{3,2,1,0:T(8,128)(2,1)S(1)} %pad_maximum_fusion.4), channel_id=1, source_target_pairs={{0,8},{1,9},{10,18},{11,19},{20,28},{21,29},{30,6},{31,7}} | collective-permute-start | bytes 1327112 | tf_op jit(solution)/shard_map/ppermute | solution.py:122
  121.1 12.5 %collective-permute-start.41 = (bf16[3,4,144,128]{3,2,1,0:T(8,128)(2,1)S(1)}, bf16[3,4,144,128]{3,2,1,0:T(8,128)(2,1)S(1)}, u32[]{:S(2)}, u32[]{:S(2)}) collective-permute-start(bf16[3,4,144,128]{3,2,1,0:T(8,128)(2,1)S(1)} %pad_maximum_fusion.4), channel_id=1, source_target_pairs={{0,16},{1,17},{10,26},{11,27},{20,4},{21,5},{30,14},{31,15}} | collective-permute-start | bytes 1327112 | tf_op jit(solution)/shard_map/ppermute | solution.py:122
  123.0 15.4 %collective-permute-start.40 = (bf16[3,4,144,128]{3,2,1,0:T(8,128)(2,1)S(1)}, bf16[3,4,144,128]{3,2,1,0:T(8,128)(2,1)S(1)}, u32[]{:S(2)}, u32[]{:S(2)}) collective-permute-start(bf16[3,4,144,128]{3,2,1,0:T(8,128)(2,1)S(1)} %pad_maximum_fusion.4), channel_id=1, source_target_pairs={{0,24},{1,25},{10,2},{11,3},{20,12},{21,13},{30,22},{31,23}} | collective-permute-start | bytes 1327112 | tf_op jit(solution)/shard_map/ppermute | solution.py:122
  (13 other events, 160.7 us)

commit v18 on v16

--- a/solution.py
+++ b/solution.py
@@ -97,6 +97,26 @@
         for j in range(1, nrow)
     ]
 
+    nx = nrow // 2
+    is_s, is_p = which == 0, r == src + 1 - 2 * (src % 2)
+    is_d1 = (which % 2 == 0) & (which != 0)
+
+    def send(v, pairs):
+        return lax.ppermute(v, ("row", "col"), [(a * ncol + cc, b * ncol + cc) for a, b, cc in pairs])
+
+    def last_fan(own):
+        heads = [cc // local_slots for cc in range(ncol)]
+        to_partner = send(own, [(h, h ^ 1, cc) for cc, h in enumerate(heads)])
+        to_d1 = None
+        for j in range(1, nx):
+            v = send(own, [(h, (h + 2 * j) % nrow, cc) for cc, h in enumerate(heads)])
+            to_d1 = v if to_d1 is None else jnp.where(which // 2 == j, v, to_d1)
+        to_d2 = send(
+            to_d1,
+            [((h + 2 * j) % nrow, ((h + 2 * j) % nrow) ^ 1, cc) for cc, h in enumerate(heads) for j in range(1, nx)],
+        )
+        return jnp.where(is_s, own, jnp.where(is_p, to_partner, jnp.where(is_d1, to_d1, to_d2)))
+
     def pick_slot(piece):
         return lax.dynamic_index_in_dim(piece, slot, axis=2, keepdims=False)
 
@@ -113,9 +133,12 @@
         if any(batch[-1] == step for batch in batches):
             own = jnp.concatenate(pending, axis=1)
             pending = []
-            got = own
-            for j, fan in enumerate(fans, start=1):
-                got = jnp.where(which == j, lax.ppermute(own, ("row", "col"), fan), got)
+            if step < ncol - 1:
+                got = own
+                for j, fan in enumerate(fans, start=1):
+                    got = jnp.where(which == j, lax.ppermute(own, ("row", "col"), fan), got)
+            else:
+                got = last_fan(own)
             columns.append(got)
 
     blocks = jnp.concatenate(pieces, axis=1)

time: 131 us -> 129 us (0.985)
  waiting for transfers between devices: 47 us -> 44.5 us
    ppermute x0 -> x3, starting transfers between devices: none -> 6.88 us  [send(): lax.ppermute(v, ('row', 'col'), [(a * ncol + cc, b * ncol + cc) for a, b,...]
    ppermute x15 -> x12, starting transfers between devices: 30.5 us -> 23.8 us  [local(): got = jnp.where(which == j, lax.ppermute(own, ('row', 'col'), fan), got)]
    ppermute x15 -> x12, waiting for transfers between devices: 4.03 us -> 1.33 us  [local(): got = jnp.where(which == j, lax.ppermute(own, ('row', 'col'), fan), got)]
    unnamed x23 -> x21, local copies, waits for them, and re-layouts: 11.1 us -> 11.1 us
  transfers between devices with their start and end apart: 29 -> 29, of which waited for: 11 -> 11; matrix products, arithmetic and copies ran while one was open for 15% -> 16% of each run, Pallas kernels for 0% -> 0%
where the time goes in v18:
time: 129 us; the launch traced here: 127 us
  waiting for transfers between devices  44.5 us (34%)
  starting transfers between devices  43.7 us (34%)
  local copies, waits for them, and re-layouts  17.8 us (14%)
  Pallas kernels  10.8 us (8%)
  other arithmetic  10.1 us (8%)
    ppermute x7, waiting for transfers between devices, local(): a = lax.ppermute(a, 'col', forward)  32.3 us
    ppermute x12, starting transfers between devices, local(): got = jnp.where(which == j, lax.ppermute(own, ('row', 'col'), fan), got)  23.8 us
    ppermute x7, starting transfers between devices, local(): a = lax.ppermute(a, 'col', forward)  11.8 us
    unnamed x21, local copies, waits for them, and re-layouts  11.1 us
    ppermute x7, waiting for transfers between devices, local(): b = lax.ppermute(b, 'col', backward)  10.9 us
    pallas_call x1, Pallas kernels, gram_call(): pl.pallas_call(kernel, grid_spec=pltpu.PrefetchScalarGridSpec(num_scalar_...  10.8 us
    ppermute x3, starting transfers between devices, send(): lax.ppermute(v, ('row', 'col'), [(a * ncol + cc, b * ncol + cc) for a, b,...  6.88 us
    unnamed x5, other arithmetic  5.22 us
  transfers between devices with their start and end apart: 29, of which 11 were waited for; matrix products, arithmetic and copies ran while one was open for 16% of the time, Pallas kernels for 0%

profile of v18, /device:TPU:0, one launch (start us, length us, event | category | flops | bytes accessed | tf_op | source)
XLA Modules:
  0.0 127.3 jit_solution(15694329428756724671)
XLA Ops:
  1.7 2.4 %constant_dynamic-update-slice_fusion.14 = (bf16[3,32,2,144,128]{4,3,2,1,0:T(8,128)(2,1)}, bf16[3,4,2,144,128]{4,3,2,1,0:T(8,128)(2,1)S(1)}) fusion(bf16[144]{0:T(256)(128)(2,1)S(1)} %pad.21.clone, bf16[3,4,2,1,128]{4,3,2,1,0:T(2,128)(2,1)S(1)} %broadcast_in_dim.7, bf16[3,4,2,3,128]{4,3,2,1,0:T(4,128)(2,1)S(1)} %broadcast_in_dim.6, ...), kind=kLoop, calls=%fused_computation.42 | loop fusion | flops 3538943 | bytes 2580768
  4.2 3.1 %collective-permute-start = (bf16[3,2,2,144,128]{4,3,2,1,0:T(8,128)(2,1)S(1)}, bf16[3,2,2,144,128]{4,3,2,1,0:T(8,128)(2,1)S(1)}, u32[]{:S(2)}, u32[]{:S(2)}) collective-permute-start(bf16[3,2,2,144,128]{4,3,2,1,0:T(8,128)(2,1)S(1)} %get-tuple-element.5), channel_id=1, source_target_pairs={{0,2},{2,4},{4,6},{6,7},{7,5},{5,3},{3,1},{1,0},{8,10},{10,12},{12... | collective-permute-start | bytes 1327112 | tf_op jit(solution)/shard_map/ppermute | solution.py:129
  7.3 10.1 %collective-permute-done = bf16[3,2,2,144,128]{4,3,2,1,0:T(8,128)(2,1)S(1)} collective-permute-done((bf16[3,2,2,144,128]{4,3,2,1,0:T(8,128)(2,1)S(1)}, bf16[3,2,2,144,128]{4,3,2,1,0:T(8,128)(2,1)S(1)}, u32[]{:S(2)}, u32[]{:S(2)}) %collective-permute-start) | collective-permute-done | bytes 442400 | tf_op jit(solution)/shard_map/ppermute | solution.py:129
  17.4 1.8 %collective-permute-start.2 = (bf16[3,2,2,144,128]{4,3,2,1,0:T(8,128)(2,1)S(1)}, bf16[3,2,2,144,128]{4,3,2,1,0:T(8,128)(2,1)S(1)}, u32[]{:S(2)}, u32[]{:S(2)}) collective-permute-start(bf16[3,2,2,144,128]{4,3,2,1,0:T(8,128)(2,1)S(1)} %collective-permute-done), channel_id=1, source_target_pairs={{0,2},{2,4},{4,6},{6,7},{7,5},{5,3},{3,1},{1,0},{8,10},{10,12},{12... | collective-permute-start | bytes 1327112 | tf_op jit(solution)/shard_map/ppermute | solution.py:129
  19.6 1.3 %collective-permute-start.16 = (bf16[3,8,144,128]{3,2,1,0:T(8,128)(2,1)S(1)}, bf16[3,8,144,128]{3,2,1,0:T(8,128)(2,1)S(1)}, u32[]{:S(2)}, u32[]{:S(2)}) collective-permute-start(bf16[3,8,144,128]{3,2,1,0:T(8,128)(2,1)S(1)} %pad_maximum_fusion), channel_id=1, source_target_pairs={{0,8},{1,9},{10,18},{11,19},{20,28},{21,29},{30,6},{31,7}} | collective-permute-start | bytes 2654216 | tf_op jit(solution)/shard_map/ppermute | solution.py:139
  21.0 3.0 %collective-permute-start.15 = (bf16[3,8,144,128]{3,2,1,0:T(8,128)(2,1)S(1)}, bf16[3,8,144,128]{3,2,1,0:T(8,128)(2,1)S(1)}, u32[]{:S(2)}, u32[]{:S(2)}) collective-permute-start(bf16[3,8,144,128]{3,2,1,0:T(8,128)(2,1)S(1)} %pad_maximum_fusion), channel_id=1, source_target_pairs={{0,16},{1,17},{10,26},{11,27},{20,4},{21,5},{30,14},{31,15}} | collective-permute-start | bytes 2654216 | tf_op jit(solution)/shard_map/ppermute | solution.py:139
  24.0 1.3 %collective-permute-start.14 = (bf16[3,8,144,128]{3,2,1,0:T(8,128)(2,1)S(1)}, bf16[3,8,144,128]{3,2,1,0:T(8,128)(2,1)S(1)}, u32[]{:S(2)}, u32[]{:S(2)}) collective-permute-start(bf16[3,8,144,128]{3,2,1,0:T(8,128)(2,1)S(1)} %pad_maximum_fusion), channel_id=1, source_target_pairs={{0,24},{1,25},{10,2},{11,3},{20,12},{21,13},{30,22},{31,23}} | collective-permute-start | bytes 2654216 | tf_op jit(solution)/shard_map/ppermute | solution.py:139
  27.1 1.7 %collective-permute-done.2 = bf16[3,2,2,144,128]{4,3,2,1,0:T(8,128)(2,1)S(1)} collective-permute-done((bf16[3,2,2,144,128]{4,3,2,1,0:T(8,128)(2,1)S(1)}, bf16[3,2,2,144,128]{4,3,2,1,0:T(8,128)(2,1)S(1)}, u32[]{:S(2)}, u32[]{:S(2)}) %collective-permute-start.2) | collective-permute-done | bytes 442400 | tf_op jit(solution)/shard_map/ppermute | solution.py:129
  28.7 1.5 %collective-permute-start.4 = (bf16[3,2,2,144,128]{4,3,2,1,0:T(8,128)(2,1)S(1)}, bf16[3,2,2,144,128]{4,3,2,1,0:T(8,128)(2,1)S(1)}, u32[]{:S(2)}, u32[]{:S(2)}) collective-permute-start(bf16[3,2,2,144,128]{4,3,2,1,0:T(8,128)(2,1)S(1)} %collective-permute-done.2), channel_id=1, source_target_pairs={{0,2},{2,4},{4,6},{6,7},{7,5},{5,3},{3,1},{1,0},{8,10},{10,12},{12... | collective-permute-start | bytes 1327112 | tf_op jit(solution)/shard_map/ppermute | solution.py:129
  32.5 6.6 %collective-permute-done.4 = bf16[3,2,2,144,128]{4,3,2,1,0:T(8,128)(2,1)S(1)} collective-permute-done((bf16[3,2,2,144,128]{4,3,2,1,0:T(8,128)(2,1)S(1)}, bf16[3,2,2,144,128]{4,3,2,1,0:T(8,128)(2,1)S(1)}, u32[]{:S(2)}, u32[]{:S(2)}) %collective-permute-start.4) | collective-permute-done | bytes 442400 | tf_op jit(solution)/shard_map/ppermute | solution.py:129
  39.2 2.3 %collective-permute-start.6 = (bf16[3,2,2,144,128]{4,3,2,1,0:T(8,128)(2,1)S(1)}, bf16[3,2,2,144,128]{4,3,2,1,0:T(8,128)(2,1)S(1)}, u32[]{:S(2)}, u32[]{:S(2)}) collective-permute-start(bf16[3,2,2,144,128]{4,3,2,1,0:T(8,128)(2,1)S(1)} %collective-permute-done.4), channel_id=1, source_target_pairs={{0,2},{2,4},{4,6},{6,7},{7,5},{5,3},{3,1},{1,0},{8,10},{10,12},{12... | collective-permute-start | bytes 1327112 | tf_op jit(solution)/shard_map/ppermute | solution.py:129
  44.7 2.3 %collective-permute-start.18 = (bf16[3,8,144,128]{3,2,1,0:T(8,128)(2,1)S(1)}, bf16[3,8,144,128]{3,2,1,0:T(8,128)(2,1)S(1)}, u32[]{:S(2)}, u32[]{:S(2)}) collective-permute-start(bf16[3,8,144,128]{3,2,1,0:T(8,128)(2,1)S(1)} %pad_maximum_fusion.1), channel_id=1, source_target_pairs={{0,16},{1,17},{10,26},{11,27},{20,4},{21,5},{30,14},{31,15}} | collective-permute-start | bytes 2654216 | tf_op jit(solution)/shard_map/ppermute | solution.py:139
  47.1 1.3 %collective-permute-start.17 = (bf16[3,8,144,128]{3,2,1,0:T(8,128)(2,1)S(1)}, bf16[3,8,144,128]{3,2,1,0:T(8,128)(2,1)S(1)}, u32[]{:S(2)}, u32[]{:S(2)}) collective-permute-start(bf16[3,8,144,128]{3,2,1,0:T(8,128)(2,1)S(1)} %pad_maximum_fusion.1), channel_id=1, source_target_pairs={{0,24},{1,25},{10,2},{11,3},{20,12},{21,13},{30,22},{31,23}} | collective-permute-start | bytes 2654216 | tf_op jit(solution)/shard_map/ppermute | solution.py:139
  49.7 2.1 %collective-permute-start.8 = (bf16[3,2,2,144,128]{4,3,2,1,0:T(8,128)(2,1)S(1)}, bf16[3,2,2,144,128]{4,3,2,1,0:T(8,128)(2,1)S(1)}, u32[]{:S(2)}, u32[]{:S(2)}) collective-permute-start(bf16[3,2,2,144,128]{4,3,2,1,0:T(8,128)(2,1)S(1)} %collective-permute-done.6), channel_id=1, source_target_pairs={{0,2},{2,4},{4,6},{6,7},{7,5},{5,3},{3,1},{1,0},{8,10},{10,12},{12... | collective-permute-start | bytes 1327112 | tf_op jit(solution)/shard_map/ppermute | solution.py:129
  53.6 7.3 %collective-permute-done.8 = bf16[3,2,2,144,128]{4,3,2,1,0:T(8,128)(2,1)S(1)} collective-permute-done((bf16[3,2,2,144,128]{4,3,2,1,0:T(8,128)(2,1)S(1)}, bf16[3,2,2,144,128]{4,3,2,1,0:T(8,128)(2,1)S(1)}, u32[]{:S(2)}, u32[]{:S(2)}) %collective-permute-start.8) | collective-permute-done | bytes 442400 | tf_op jit(solution)/shard_map/ppermute | solution.py:129
  60.9 2.2 %collective-permute-done.9 = bf16[3,2,2,144,128]{4,3,2,1,0:T(8,128)(2,1)S(1)} collective-permute-done((bf16[3,2,2,144,128]{4,3,2,1,0:T(8,128)(2,1)S(1)}, bf16[3,2,2,144,128]{4,3,2,1,0:T(8,128)(2,1)S(1)}, u32[]{:S(2)}, u32[]{:S(2)}) %collective-permute-start.9) | collective-permute-done | bytes 442400 | tf_op jit(solution)/shard_map/ppermute | solution.py:130
  63.2 1.3 %collective-permute-start.22 = (bf16[3,8,144,128]{3,2,1,0:T(8,128)(2,1)S(1)}, bf16[3,8,144,128]{3,2,1,0:T(8,128)(2,1)S(1)}, u32[]{:S(2)}, u32[]{:S(2)}) collective-permute-start(bf16[3,8,144,128]{3,2,1,0:T(8,128)(2,1)S(1)} %pad_maximum_fusion.2), channel_id=1, source_target_pairs={{0,8},{1,9},{10,18},{11,19},{20,28},{21,29},{30,6},{31,7}} | collective-permute-start | bytes 2654216 | tf_op jit(solution)/shard_map/ppermute | solution.py:139
  66.4 3.8 %collective-permute-start.21 = (bf16[3,8,144,128]{3,2,1,0:T(8,128)(2,1)S(1)}, bf16[3,8,144,128]{3,2,1,0:T(8,128)(2,1)S(1)}, u32[]{:S(2)}, u32[]{:S(2)}) collective-permute-start(bf16[3,8,144,128]{3,2,1,0:T(8,128)(2,1)S(1)} %pad_maximum_fusion.2), channel_id=1, source_target_pairs={{0,16},{1,17},{10,26},{11,27},{20,4},{21,5},{30,14},{31,15}} | collective-permute-start | bytes 2654216 | tf_op jit(solution)/shard_map/ppermute | solution.py:139
  70.2 1.3 %collective-permute-start.20 = (bf16[3,8,144,128]{3,2,1,0:T(8,128)(2,1)S(1)}, bf16[3,8,144,128]{3,2,1,0:T(8,128)(2,1)S(1)}, u32[]{:S(2)}, u32[]{:S(2)}) collective-permute-start(bf16[3,8,144,128]{3,2,1,0:T(8,128)(2,1)S(1)} %pad_maximum_fusion.2), channel_id=1, source_target_pairs={{0,24},{1,25},{10,2},{11,3},{20,12},{21,13},{30,22},{31,23}} | collective-permute-start | bytes 2654216 | tf_op jit(solution)/shard_map/ppermute | solution.py:139
  72.2 2.8 %collective-permute-done.10 = bf16[3,2,2,144,128]{4,3,2,1,0:T(8,128)(2,1)S(1)} collective-permute-done((bf16[3,2,2,144,128]{4,3,2,1,0:T(8,128)(2,1)S(1)}, bf16[3,2,2,144,128]{4,3,2,1,0:T(8,128)(2,1)S(1)}, u32[]{:S(2)}, u32[]{:S(2)}) %collective-permute-start.10) | collective-permute-done | bytes 442400 | tf_op jit(solution)/shard_map/ppermute | solution.py:129
  75.9 6.4 %collective-permute-done.11 = bf16[3,2,2,144,128]{4,3,2,1,0:T(8,128)(2,1)S(1)} collective-permute-done((bf16[3,2,2,144,128]{4,3,2,1,0:T(8,128)(2,1)S(1)}, bf16[3,2,2,144,128]{4,3,2,1,0:T(8,128)(2,1)S(1)}, u32[]{:S(2)}, u32[]{:S(2)}) %collective-permute-start.11) | collective-permute-done | bytes 442400 | tf_op jit(solution)/shard_map/ppermute | solution.py:130
  84.3 3.1 %collective-permute-done.12 = bf16[3,2,2,144,128]{4,3,2,1,0:T(8,128)(2,1)S(1)} collective-permute-done((bf16[3,2,2,144,128]{4,3,2,1,0:T(8,128)(2,1)S(1)}, bf16[3,2,2,144,128]{4,3,2,1,0:T(8,128)(2,1)S(1)}, u32[]{:S(2)}, u32[]{:S(2)}) %collective-permute-start.12) | collective-permute-done | bytes 442400 | tf_op jit(solution)/shard_map/ppermute | solution.py:129
  87.4 2.4 %collective-permute-start.25 = (bf16[3,4,144,128]{3,2,1,0:T(8,128)(2,1)}, bf16[3,4,144,128]{3,2,1,0:T(8,128)(2,1)}, u32[]{:S(2)}, u32[]{:S(2)}) collective-permute-start(bf16[3,4,144,128]{3,2,1,0:T(8,128)(2,1)} %pad_maximum_fusion.3), channel_id=1, source_target_pairs={{0,8},{1,9},{10,18},{11,19},{20,28},{21,29},{30,6},{31,7}} | collective-permute-start | bytes 1327112 | tf_op jit(solution)/shard_map/ppermute | solution.py:139
  89.8 2.3 %collective-permute-done.13 = bf16[3,2,2,144,128]{4,3,2,1,0:T(8,128)(2,1)S(1)} collective-permute-done((bf16[3,2,2,144,128]{4,3,2,1,0:T(8,128)(2,1)S(1)}, bf16[3,2,2,144,128]{4,3,2,1,0:T(8,128)(2,1)S(1)}, u32[]{:S(2)}, u32[]{:S(2)}) %collective-permute-start.13) | collective-permute-done | bytes 442400 | tf_op jit(solution)/shard_map/ppermute | solution.py:130
  93.1 3.3 %collective-permute-start.27 = (bf16[3,4,144,128]{3,2,1,0:T(8,128)(2,1)}, bf16[3,4,144,128]{3,2,1,0:T(8,128)(2,1)}, u32[]{:S(2)}, u32[]{:S(2)}) collective-permute-start(bf16[3,4,144,128]{3,2,1,0:T(8,128)(2,1)} %pad_maximum_fusion.4), channel_id=1, source_target_pairs={{0,16},{1,17},{10,26},{11,27},{20,4},{21,5},{30,14},{31,15}} | collective-permute-start | bytes 1327112 | tf_op jit(solution)/shard_map/ppermute | solution.py:105
  97.3 2.1 %collective-permute-start.24 = (bf16[3,4,144,128]{3,2,1,0:T(8,128)(2,1)}, bf16[3,4,144,128]{3,2,1,0:T(8,128)(2,1)}, u32[]{:S(2)}, u32[]{:S(2)}) collective-permute-start(bf16[3,4,144,128]{3,2,1,0:T(8,128)(2,1)} %pad_maximum_fusion.3), channel_id=1, source_target_pairs={{0,16},{1,17},{10,26},{11,27},{20,4},{21,5},{30,14},{31,15}} | collective-permute-start | bytes 1327112 | tf_op jit(solution)/shard_map/ppermute | solution.py:139
  99.3 2.1 %collective-permute-start.23 = (bf16[3,4,144,128]{3,2,1,0:T(8,128)(2,1)}, bf16[3,4,144,128]{3,2,1,0:T(8,128)(2,1)}, u32[]{:S(2)}, u32[]{:S(2)}) collective-permute-start(bf16[3,4,144,128]{3,2,1,0:T(8,128)(2,1)} %pad_maximum_fusion.3), channel_id=1, source_target_pairs={{0,24},{1,25},{10,2},{11,3},{20,12},{21,13},{30,22},{31,23}} | collective-permute-start | bytes 1327112 | tf_op jit(solution)/shard_map/ppermute | solution.py:139
  101.4 2.1 %collective-permute-start.26 = (bf16[3,4,144,128]{3,2,1,0:T(8,128)(2,1)}, bf16[3,4,144,128]{3,2,1,0:T(8,128)(2,1)}, u32[]{:S(2)}, u32[]{:S(2)}) collective-permute-start(bf16[3,4,144,128]{3,2,1,0:T(8,128)(2,1)} %pad_maximum_fusion.4), channel_id=1, source_target_pairs={{0,8},{1,9},{10,2},{11,3},{20,28},{21,29},{30,22},{31,23}} | collective-permute-start | bytes 1327112 | tf_op jit(solution)/shard_map/ppermute | solution.py:105
  104.1 1.4 %collective-permute-start.28 = (bf16[3,4,144,128]{3,2,1,0:T(8,128)(2,1)}, bf16[3,4,144,128]{3,2,1,0:T(8,128)(2,1)}, u32[]{:S(2)}, u32[]{:S(2)}) collective-permute-start(bf16[3,4,144,128]{3,2,1,0:T(8,128)(2,1)} %collective-permute-done.27), channel_id=1, source_target_pairs={{16,24},{17,25},{26,18},{27,19},{4,12},{5,13},{14,6},{15,7}} | collective-permute-start | bytes 1327112 | tf_op jit(solution)/shard_map/ppermute | solution.py:105
  107.2 1.7 %slice.19 = bf16[96,2,1,1]{3,2,1,0:T(2,128)(2,1)} slice(bf16[96,2,144,128]{3,2,1,0:T(8,128)(2,1)} %bitcast.44), slice={[0:96], [0:2], [131:132], [0:1]} | slice | bytes 768 | tf_op jit(solution)/shard_map/slice | solution.py:150
  112.5 1.5 %select_dynamic-update-slice_fusion.3 = bf16[3,32,144,128]{3,2,1,0:T(8,128)(2,1)S(1)} fusion(bf16[3,32,144,128]{3,2,1,0:T(8,128)(2,1)S(1)} %select_dynamic-update-slice_fusion.4, bf16[3,4,144,128]{3,2,1,0:T(8,128)(2,1)} %collective-permute-done.26, bf16[3,4,144,128]{3,2,1,0:T(8,128)(2,1)} %collective-permute-done.27, ...), kind=kLoop, calls=%fused_computation.9 | loop fusion | flops 1548288 | bytes 2211843 | tf_op jit(solution)/shard_map/concatenate | solution.py:145
  116.5 10.8 %shard_map.37 = f32[2048,1024]{1,0:T(8,128)} custom-call(s32[288]{0:T(512)S(1)} %min.12.offs_ref, bf16[96,2,144,128]{3,2,1,0:T(8,128)(2,1)} %bitcast.45, bf16[96,144,128]{2,1,0:T(8,128)(2,1)S(1)} %bitcast.43), custom_call_target="tpu_custom_call" | custom-call | flops 805306368 | bytes 17825792 | tf_op jit(solution)/shard_map/pallas_call | solution.py:40
  (91 shorter events, 28.1 us)
Async XLA Ops:
  4.2 13.2 %collective-permute-start = (bf16[3,2,2,144,128]{4,3,2,1,0:T(8,128)(2,1)S(1)}, bf16[3,2,2,144,128]{4,3,2,1,0:T(8,128)(2,1)S(1)}, u32[]{:S(2)}, u32[]{:S(2)}) collective-permute-start(bf16[3,2,2,144,128]{4,3,2,1,0:T(8,128)(2,1)S(1)} %get-tuple-element.5), channel_id=1, source_target_pairs={{0,2},{2,4},{4,6},{6,7},{7,5},{5,3},{3,1},{1,0},{8,10},{10,12},{12... | collective-permute-start | bytes 1327112 | tf_op jit(solution)/shard_map/ppermute | solution.py:129
  7.3 11.9 %collective-permute-start.1 = (bf16[3,2,2,144,128]{4,3,2,1,0:T(8,128)(2,1)S(1)}, bf16[3,2,2,144,128]{4,3,2,1,0:T(8,128)(2,1)S(1)}, u32[]{:S(2)}, u32[]{:S(2)}) collective-permute-start(bf16[3,2,2,144,128]{4,3,2,1,0:T(8,128)(2,1)S(1)} %get-tuple-element.6), channel_id=1, source_target_pairs={{2,0},{4,2},{6,4},{7,6},{5,7},{3,5},{1,3},{0,1},{10,8},{12,10},{14... | collective-permute-start | bytes 1327112 | tf_op jit(solution)/shard_map/ppermute | solution.py:130
  17.4 11.4 %collective-permute-start.2 = (bf16[3,2,2,144,128]{4,3,2,1,0:T(8,128)(2,1)S(1)}, bf16[3,2,2,144,128]{4,3,2,1,0:T(8,128)(2,1)S(1)}, u32[]{:S(2)}, u32[]{:S(2)}) collective-permute-start(bf16[3,2,2,144,128]{4,3,2,1,0:T(8,128)(2,1)S(1)} %collective-permute-done), channel_id=1, source_target_pairs={{0,2},{2,4},{4,6},{6,7},{7,5},{5,3},{3,1},{1,0},{8,10},{10,12},{12... | collective-permute-start | bytes 1327112 | tf_op jit(solution)/shard_map/ppermute | solution.py:129
  19.2 11.0 %collective-permute-start.3 = (bf16[3,2,2,144,128]{4,3,2,1,0:T(8,128)(2,1)S(1)}, bf16[3,2,2,144,128]{4,3,2,1,0:T(8,128)(2,1)S(1)}, u32[]{:S(2)}, u32[]{:S(2)}) collective-permute-start(bf16[3,2,2,144,128]{4,3,2,1,0:T(8,128)(2,1)S(1)} %collective-permute-done.1), channel_id=1, source_target_pairs={{2,0},{4,2},{6,4},{7,6},{5,7},{3,5},{1,3},{0,1},{10,8},{12,10},{14... | collective-permute-start | bytes 1327112 | tf_op jit(solution)/shard_map/ppermute | solution.py:130
  19.6 23.7 %collective-permute-start.16 = (bf16[3,8,144,128]{3,2,1,0:T(8,128)(2,1)S(1)}, bf16[3,8,144,128]{3,2,1,0:T(8,128)(2,1)S(1)}, u32[]{:S(2)}, u32[]{:S(2)}) collective-permute-start(bf16[3,8,144,128]{3,2,1,0:T(8,128)(2,1)S(1)} %pad_maximum_fusion), channel_id=1, source_target_pairs={{0,8},{1,9},{10,18},{11,19},{20,28},{21,29},{30,6},{31,7}} | collective-permute-start | bytes 2654216 | tf_op jit(solution)/shard_map/ppermute | solution.py:139
  21.0 23.7 %collective-permute-start.15 = (bf16[3,8,144,128]{3,2,1,0:T(8,128)(2,1)S(1)}, bf16[3,8,144,128]{3,2,1,0:T(8,128)(2,1)S(1)}, u32[]{:S(2)}, u32[]{:S(2)}) collective-permute-start(bf16[3,8,144,128]{3,2,1,0:T(8,128)(2,1)S(1)} %pad_maximum_fusion), channel_id=1, source_target_pairs={{0,16},{1,17},{10,26},{11,27},{20,4},{21,5},{30,14},{31,15}} | collective-permute-start | bytes 2654216 | tf_op jit(solution)/shard_map/ppermute | solution.py:139
  24.0 23.0 %collective-permute-start.14 = (bf16[3,8,144,128]{3,2,1,0:T(8,128)(2,1)S(1)}, bf16[3,8,144,128]{3,2,1,0:T(8,128)(2,1)S(1)}, u32[]{:S(2)}, u32[]{:S(2)}) collective-permute-start(bf16[3,8,144,128]{3,2,1,0:T(8,128)(2,1)S(1)} %pad_maximum_fusion), channel_id=1, source_target_pairs={{0,24},{1,25},{10,2},{11,3},{20,12},{21,13},{30,22},{31,23}} | collective-permute-start | bytes 2654216 | tf_op jit(solution)/shard_map/ppermute | solution.py:139
  28.7 10.4 %collective-permute-start.4 = (bf16[3,2,2,144,128]{4,3,2,1,0:T(8,128)(2,1)S(1)}, bf16[3,2,2,144,128]{4,3,2,1,0:T(8,128)(2,1)S(1)}, u32[]{:S(2)}, u32[]{:S(2)}) collective-permute-start(bf16[3,2,2,144,128]{4,3,2,1,0:T(8,128)(2,1)S(1)} %collective-permute-done.2), channel_id=1, source_target_pairs={{0,2},{2,4},{4,6},{6,7},{7,5},{5,3},{3,1},{1,0},{8,10},{10,12},{12... | collective-permute-start | bytes 1327112 | tf_op jit(solution)/shard_map/ppermute | solution.py:129
  30.2 11.3 %collective-permute-start.5 = (bf16[3,2,2,144,128]{4,3,2,1,0:T(8,128)(2,1)S(1)}, bf16[3,2,2,144,128]{4,3,2,1,0:T(8,128)(2,1)S(1)}, u32[]{:S(2)}, u32[]{:S(2)}) collective-permute-start(bf16[3,2,2,144,128]{4,3,2,1,0:T(8,128)(2,1)S(1)} %collective-permute-done.3), channel_id=1, source_target_pairs={{2,0},{4,2},{6,4},{7,6},{5,7},{3,5},{1,3},{0,1},{10,8},{12,10},{14... | collective-permute-start | bytes 1327112 | tf_op jit(solution)/shard_map/ppermute | solution.py:130
  39.2 10.5 %collective-permute-start.6 = (bf16[3,2,2,144,128]{4,3,2,1,0:T(8,128)(2,1)S(1)}, bf16[3,2,2,144,128]{4,3,2,1,0:T(8,128)(2,1)S(1)}, u32[]{:S(2)}, u32[]{:S(2)}) collective-permute-start(bf16[3,2,2,144,128]{4,3,2,1,0:T(8,128)(2,1)S(1)} %collective-permute-done.4), channel_id=1, source_target_pairs={{0,2},{2,4},{4,6},{6,7},{7,5},{5,3},{3,1},{1,0},{8,10},{10,12},{12... | collective-permute-start | bytes 1327112 | tf_op jit(solution)/shard_map/ppermute | solution.py:129
  41.5 10.3 %collective-permute-start.7 = (bf16[3,2,2,144,128]{4,3,2,1,0:T(8,128)(2,1)S(1)}, bf16[3,2,2,144,128]{4,3,2,1,0:T(8,128)(2,1)S(1)}, u32[]{:S(2)}, u32[]{:S(2)}) collective-permute-start(bf16[3,2,2,144,128]{4,3,2,1,0:T(8,128)(2,1)S(1)} %collective-permute-done.5), channel_id=1, source_target_pairs={{2,0},{4,2},{6,4},{7,6},{5,7},{3,5},{1,3},{0,1},{10,8},{12,10},{14... | collective-permute-start | bytes 1327112 | tf_op jit(solution)/shard_map/ppermute | solution.py:130
  43.4 23.0 %collective-permute-start.19 = (bf16[3,8,144,128]{3,2,1,0:T(8,128)(2,1)S(1)}, bf16[3,8,144,128]{3,2,1,0:T(8,128)(2,1)S(1)}, u32[]{:S(2)}, u32[]{:S(2)}) collective-permute-start(bf16[3,8,144,128]{3,2,1,0:T(8,128)(2,1)S(1)} %pad_maximum_fusion.1), channel_id=1, source_target_pairs={{0,8},{1,9},{10,18},{11,19},{20,28},{21,29},{30,6},{31,7}} | collective-permute-start | bytes 2654216 | tf_op jit(solution)/shard_map/ppermute | solution.py:139
  44.7 25.5 %collective-permute-start.18 = (bf16[3,8,144,128]{3,2,1,0:T(8,128)(2,1)S(1)}, bf16[3,8,144,128]{3,2,1,0:T(8,128)(2,1)S(1)}, u32[]{:S(2)}, u32[]{:S(2)}) collective-permute-start(bf16[3,8,144,128]{3,2,1,0:T(8,128)(2,1)S(1)} %pad_maximum_fusion.1), channel_id=1, source_target_pairs={{0,16},{1,17},{10,26},{11,27},{20,4},{21,5},{30,14},{31,15}} | collective-permute-start | bytes 2654216 | tf_op jit(solution)/shard_map/ppermute | solution.py:139
  47.1 24.5 %collective-permute-start.17 = (bf16[3,8,144,128]{3,2,1,0:T(8,128)(2,1)S(1)}, bf16[3,8,144,128]{3,2,1,0:T(8,128)(2,1)S(1)}, u32[]{:S(2)}, u32[]{:S(2)}) collective-permute-start(bf16[3,8,144,128]{3,2,1,0:T(8,128)(2,1)S(1)} %pad_maximum_fusion.1), channel_id=1, source_target_pairs={{0,24},{1,25},{10,2},{11,3},{20,12},{21,13},{30,22},{31,23}} | collective-permute-start | bytes 2654216 | tf_op jit(solution)/shard_map/ppermute | solution.py:139
  49.7 11.2 %collective-permute-start.8 = (bf16[3,2,2,144,128]{4,3,2,1,0:T(8,128)(2,1)S(1)}, bf16[3,2,2,144,128]{4,3,2,1,0:T(8,128)(2,1)S(1)}, u32[]{:S(2)}, u32[]{:S(2)}) collective-permute-start(bf16[3,2,2,144,128]{4,3,2,1,0:T(8,128)(2,1)S(1)} %collective-permute-done.6), channel_id=1, source_target_pairs={{0,2},{2,4},{4,6},{6,7},{7,5},{5,3},{3,1},{1,0},{8,10},{10,12},{12... | collective-permute-start | bytes 1327112 | tf_op jit(solution)/shard_map/ppermute | solution.py:129
  51.8 11.3 %collective-permute-start.9 = (bf16[3,2,2,144,128]{4,3,2,1,0:T(8,128)(2,1)S(1)}, bf16[3,2,2,144,128]{4,3,2,1,0:T(8,128)(2,1)S(1)}, u32[]{:S(2)}, u32[]{:S(2)}) collective-permute-start(bf16[3,2,2,144,128]{4,3,2,1,0:T(8,128)(2,1)S(1)} %collective-permute-done.7), channel_id=1, source_target_pairs={{2,0},{4,2},{6,4},{7,6},{5,7},{3,5},{1,3},{0,1},{10,8},{12,10},{14... | collective-permute-start | bytes 1327112 | tf_op jit(solution)/shard_map/ppermute | solution.py:130
  63.2 34.0 %collective-permute-start.22 = (bf16[3,8,144,128]{3,2,1,0:T(8,128)(2,1)S(1)}, bf16[3,8,144,128]{3,2,1,0:T(8,128)(2,1)S(1)}, u32[]{:S(2)}, u32[]{:S(2)}) collective-permute-start(bf16[3,8,144,128]{3,2,1,0:T(8,128)(2,1)S(1)} %pad_maximum_fusion.2), channel_id=1, source_target_pairs={{0,8},{1,9},{10,18},{11,19},{20,28},{21,29},{30,6},{31,7}} | collective-permute-start | bytes 2654216 | tf_op jit(solution)/shard_map/ppermute | solution.py:139
  64.6 10.3 %collective-permute-start.10 = (bf16[3,2,2,144,128]{4,3,2,1,0:T(8,128)(2,1)S(1)}, bf16[3,2,2,144,128]{4,3,2,1,0:T(8,128)(2,1)S(1)}, u32[]{:S(2)}, u32[]{:S(2)}) collective-permute-start(bf16[3,2,2,144,128]{4,3,2,1,0:T(8,128)(2,1)S(1)} %collective-permute-done.8), channel_id=1, source_target_pairs={{0,2},{2,4},{4,6},{6,7},{7,5},{5,3},{3,1},{1,0},{8,10},{10,12},{12... | collective-permute-start | bytes 1327112 | tf_op jit(solution)/shard_map/ppermute | solution.py:129
  66.4 33.0 %collective-permute-start.21 = (bf16[3,8,144,128]{3,2,1,0:T(8,128)(2,1)S(1)}, bf16[3,8,144,128]{3,2,1,0:T(8,128)(2,1)S(1)}, u32[]{:S(2)}, u32[]{:S(2)}) collective-permute-start(bf16[3,8,144,128]{3,2,1,0:T(8,128)(2,1)S(1)} %pad_maximum_fusion.2), channel_id=1, source_target_pairs={{0,16},{1,17},{10,26},{11,27},{20,4},{21,5},{30,14},{31,15}} | collective-permute-start | bytes 2654216 | tf_op jit(solution)/shard_map/ppermute | solution.py:139
  70.2 31.2 %collective-permute-start.20 = (bf16[3,8,144,128]{3,2,1,0:T(8,128)(2,1)S(1)}, bf16[3,8,144,128]{3,2,1,0:T(8,128)(2,1)S(1)}, u32[]{:S(2)}, u32[]{:S(2)}) collective-permute-start(bf16[3,8,144,128]{3,2,1,0:T(8,128)(2,1)S(1)} %pad_maximum_fusion.2), channel_id=1, source_target_pairs={{0,24},{1,25},{10,2},{11,3},{20,12},{21,13},{30,22},{31,23}} | collective-permute-start | bytes 2654216 | tf_op jit(solution)/shard_map/ppermute | solution.py:139
  71.6 10.8 %collective-permute-start.11 = (bf16[3,2,2,144,128]{4,3,2,1,0:T(8,128)(2,1)S(1)}, bf16[3,2,2,144,128]{4,3,2,1,0:T(8,128)(2,1)S(1)}, u32[]{:S(2)}, u32[]{:S(2)}) collective-permute-start(bf16[3,2,2,144,128]{4,3,2,1,0:T(8,128)(2,1)S(1)} %collective-permute-done.9), channel_id=1, source_target_pairs={{2,0},{4,2},{6,4},{7,6},{5,7},{3,5},{1,3},{0,1},{10,8},{12,10},{14... | collective-permute-start | bytes 1327112 | tf_op jit(solution)/shard_map/ppermute | solution.py:130
  74.9 12.5 %collective-permute-start.12 = (bf16[3,2,2,144,128]{4,3,2,1,0:T(8,128)(2,1)S(1)}, bf16[3,2,2,144,128]{4,3,2,1,0:T(8,128)(2,1)S(1)}, u32[]{:S(2)}, u32[]{:S(2)}) collective-permute-start(bf16[3,2,2,144,128]{4,3,2,1,0:T(8,128)(2,1)S(1)} %collective-permute-done.10), channel_id=1, source_target_pairs={{0,2},{2,4},{4,6},{6,7},{7,5},{5,3},{3,1},{1,0},{8,10},{10,12},{12... | collective-permute-start | bytes 1327112 | tf_op jit(solution)/shard_map/ppermute | solution.py:129
  75.9 25.5 %copy-start = (bf16[3,2,144,128]{3,2,1,0:T(8,128)(2,1)}, bf16[3,2,144,128]{3,2,1,0:T(8,128)(2,1)S(1)}, u32[]{:S(2)}) copy-start(bf16[3,2,144,128]{3,2,1,0:T(8,128)(2,1)S(1)} %dynamic-slice_bitcast_fusion.3) | copy-start | bytes 663556
  82.3 9.8 %collective-permute-start.13 = (bf16[3,2,2,144,128]{4,3,2,1,0:T(8,128)(2,1)S(1)}, bf16[3,2,2,144,128]{4,3,2,1,0:T(8,128)(2,1)S(1)}, u32[]{:S(2)}, u32[]{:S(2)}) collective-permute-start(bf16[3,2,2,144,128]{4,3,2,1,0:T(8,128)(2,1)S(1)} %collective-permute-done.11), channel_id=1, source_target_pairs={{2,0},{4,2},{6,4},{7,6},{5,7},{3,5},{1,3},{0,1},{10,8},{12,10},{14... | collective-permute-start | bytes 1327112 | tf_op jit(solution)/shard_map/ppermute | solution.py:130
  87.4 22.5 %collective-permute-start.25 = (bf16[3,4,144,128]{3,2,1,0:T(8,128)(2,1)}, bf16[3,4,144,128]{3,2,1,0:T(8,128)(2,1)}, u32[]{:S(2)}, u32[]{:S(2)}) collective-permute-start(bf16[3,4,144,128]{3,2,1,0:T(8,128)(2,1)} %pad_maximum_fusion.3), channel_id=1, source_target_pairs={{0,8},{1,9},{10,18},{11,19},{20,28},{21,29},{30,6},{31,7}} | collective-permute-start | bytes 1327112 | tf_op jit(solution)/shard_map/ppermute | solution.py:139
  89.8 11.6 %copy-start.1 = (bf16[3,2,144,128]{3,2,1,0:T(8,128)(2,1)}, bf16[3,2,144,128]{3,2,1,0:T(8,128)(2,1)S(1)}, u32[]{:S(2)}) copy-start(bf16[3,2,144,128]{3,2,1,0:T(8,128)(2,1)S(1)} %dynamic-slice_bitcast_fusion.1) | copy-start | bytes 663556
  92.2 9.3 %copy-start.2 = (bf16[3,2,144,128]{3,2,1,0:T(8,128)(2,1)}, bf16[3,2,144,128]{3,2,1,0:T(8,128)(2,1)S(1)}, u32[]{:S(2)}) copy-start(bf16[3,2,144,128]{3,2,1,0:T(8,128)(2,1)S(1)} %dynamic-slice_bitcast_fusion) | copy-start | bytes 663556
  93.1 11.0 %collective-permute-start.27 = (bf16[3,4,144,128]{3,2,1,0:T(8,128)(2,1)}, bf16[3,4,144,128]{3,2,1,0:T(8,128)(2,1)}, u32[]{:S(2)}, u32[]{:S(2)}) collective-permute-start(bf16[3,4,144,128]{3,2,1,0:T(8,128)(2,1)} %pad_maximum_fusion.4), channel_id=1, source_target_pairs={{0,16},{1,17},{10,26},{11,27},{20,4},{21,5},{30,14},{31,15}} | collective-permute-start | bytes 1327112 | tf_op jit(solution)/shard_map/ppermute | solution.py:105
  97.3 12.7 %collective-permute-start.24 = (bf16[3,4,144,128]{3,2,1,0:T(8,128)(2,1)}, bf16[3,4,144,128]{3,2,1,0:T(8,128)(2,1)}, u32[]{:S(2)}, u32[]{:S(2)}) collective-permute-start(bf16[3,4,144,128]{3,2,1,0:T(8,128)(2,1)} %pad_maximum_fusion.3), channel_id=1, source_target_pairs={{0,16},{1,17},{10,26},{11,27},{20,4},{21,5},{30,14},{31,15}} | collective-permute-start | bytes 1327112 | tf_op jit(solution)/shard_map/ppermute | solution.py:139
  99.3 11.9 %collective-permute-start.23 = (bf16[3,4,144,128]{3,2,1,0:T(8,128)(2,1)}, bf16[3,4,144,128]{3,2,1,0:T(8,128)(2,1)}, u32[]{:S(2)}, u32[]{:S(2)}) collective-permute-start(bf16[3,4,144,128]{3,2,1,0:T(8,128)(2,1)} %pad_maximum_fusion.3), channel_id=1, source_target_pairs={{0,24},{1,25},{10,2},{11,3},{20,12},{21,13},{30,22},{31,23}} | collective-permute-start | bytes 1327112 | tf_op jit(solution)/shard_map/ppermute | solution.py:139
  101.4 11.1 %collective-permute-start.26 = (bf16[3,4,144,128]{3,2,1,0:T(8,128)(2,1)}, bf16[3,4,144,128]{3,2,1,0:T(8,128)(2,1)}, u32[]{:S(2)}, u32[]{:S(2)}) collective-permute-start(bf16[3,4,144,128]{3,2,1,0:T(8,128)(2,1)} %pad_maximum_fusion.4), channel_id=1, source_target_pairs={{0,8},{1,9},{10,2},{11,3},{20,28},{21,29},{30,22},{31,23}} | collective-permute-start | bytes 1327112 | tf_op jit(solution)/shard_map/ppermute | solution.py:105
  104.1 8.5 %collective-permute-start.28 = (bf16[3,4,144,128]{3,2,1,0:T(8,128)(2,1)}, bf16[3,4,144,128]{3,2,1,0:T(8,128)(2,1)}, u32[]{:S(2)}, u32[]{:S(2)}) collective-permute-start(bf16[3,4,144,128]{3,2,1,0:T(8,128)(2,1)} %collective-permute-done.27), channel_id=1, source_target_pairs={{16,24},{17,25},{26,18},{27,19},{4,12},{5,13},{14,6},{15,7}} | collective-permute-start | bytes 1327112 | tf_op jit(solution)/shard_map/ppermute | solution.py:105
  (1 other events, 4.8 us)

commit v19 on v18

--- a/solution.py
+++ b/solution.py
@@ -133,7 +133,7 @@
         if any(batch[-1] == step for batch in batches):
             own = jnp.concatenate(pending, axis=1)
             pending = []
-            if step < ncol - 1:
+            if step < ncol - 2:
                 got = own
                 for j, fan in enumerate(fans, start=1):
                     got = jnp.where(which == j, lax.ppermute(own, ("row", "col"), fan), got)

time: 129 us -> 126 us (0.977)
    ppermute x12 -> x9, starting transfers between devices: 23.8 us -> 17.3 us  [local(): got = jnp.where(which == j, lax.ppermute(own, ('row', 'col'), fan), got)]
    ppermute x3 -> x6, starting transfers between devices: 6.88 us -> 12.5 us  [send(): lax.ppermute(v, ('row', 'col'), [(a * ncol + cc, b * ncol + cc) for a, b,...]
    ppermute x12 -> x9, waiting for transfers between devices: 1.33 us -> 0.02 us  [local(): got = jnp.where(which == j, lax.ppermute(own, ('row', 'col'), fan), got)]
  transfers between devices with their start and end apart: 29 -> 29, of which waited for: 11 -> 10; matrix products, arithmetic and copies ran while one was open for 16% -> 16% of each run, Pallas kernels for 0% -> 0%
where the time goes in v19:
time: 126 us
  waiting for transfers between devices  43.5 us (35%)
  starting transfers between devices  42.8 us (34%)
  local copies, waits for them, and re-layouts  17.8 us (14%)
  Pallas kernels  10.8 us (9%)
  other arithmetic  10.3 us (8%)
    ppermute x7, waiting for transfers between devices, local(): a = lax.ppermute(a, 'col', forward)  32.3 us
    ppermute x9, starting transfers between devices, local(): got = jnp.where(which == j, lax.ppermute(own, ('row', 'col'), fan), got)  17.3 us
    ppermute x6, starting transfers between devices, send(): lax.ppermute(v, ('row', 'col'), [(a * ncol + cc, b * ncol + cc) for a, b,...  12.5 us
    ppermute x7, starting transfers between devices, local(): a = lax.ppermute(a, 'col', forward)  11.8 us
    ppermute x7, waiting for transfers between devices, local(): b = lax.ppermute(b, 'col', backward)  11.2 us
    unnamed x21, local copies, waits for them, and re-layouts  11.1 us
    pallas_call x1, Pallas kernels, gram_call(): pl.pallas_call(kernel, grid_spec=pltpu.PrefetchScalarGridSpec(num_scalar_...  10.8 us
    unnamed x5, other arithmetic  5.37 us
  transfers between devices with their start and end apart: 29, of which 10 were waited for; matrix products, arithmetic and copies ran while one was open for 16% of the time, Pallas kernels for 0%

profile of v19, /device:TPU:0, one launch (start us, length us, event | category | flops | bytes accessed | tf_op | source)
XLA Modules:
  0.0 125.5 jit_solution(5338481772749693653)
XLA Ops:
  1.7 2.4 %constant_dynamic-update-slice_fusion.14 = (bf16[3,32,2,144,128]{4,3,2,1,0:T(8,128)(2,1)}, bf16[3,4,2,144,128]{4,3,2,1,0:T(8,128)(2,1)S(1)}) fusion(bf16[144]{0:T(256)(128)(2,1)S(1)} %pad.21.clone, bf16[3,4,2,1,128]{4,3,2,1,0:T(2,128)(2,1)S(1)} %broadcast_in_dim.7, bf16[3,4,2,3,128]{4,3,2,1,0:T(4,128)(2,1)S(1)} %broadcast_in_dim.6, ...), kind=kLoop, calls=%fused_computation.42 | loop fusion | flops 3538943 | bytes 2580768
  4.2 3.1 %collective-permute-start = (bf16[3,2,2,144,128]{4,3,2,1,0:T(8,128)(2,1)S(1)}, bf16[3,2,2,144,128]{4,3,2,1,0:T(8,128)(2,1)S(1)}, u32[]{:S(2)}, u32[]{:S(2)}) collective-permute-start(bf16[3,2,2,144,128]{4,3,2,1,0:T(8,128)(2,1)S(1)} %get-tuple-element.5), channel_id=1, source_target_pairs={{0,2},{2,4},{4,6},{6,7},{7,5},{5,3},{3,1},{1,0},{8,10},{10,12},{12... | collective-permute-start | bytes 1327112 | tf_op jit(solution)/shard_map/ppermute | solution.py:129
  7.3 10.1 %collective-permute-done = bf16[3,2,2,144,128]{4,3,2,1,0:T(8,128)(2,1)S(1)} collective-permute-done((bf16[3,2,2,144,128]{4,3,2,1,0:T(8,128)(2,1)S(1)}, bf16[3,2,2,144,128]{4,3,2,1,0:T(8,128)(2,1)S(1)}, u32[]{:S(2)}, u32[]{:S(2)}) %collective-permute-start) | collective-permute-done | bytes 442400 | tf_op jit(solution)/shard_map/ppermute | solution.py:129
  17.4 1.8 %collective-permute-start.2 = (bf16[3,2,2,144,128]{4,3,2,1,0:T(8,128)(2,1)S(1)}, bf16[3,2,2,144,128]{4,3,2,1,0:T(8,128)(2,1)S(1)}, u32[]{:S(2)}, u32[]{:S(2)}) collective-permute-start(bf16[3,2,2,144,128]{4,3,2,1,0:T(8,128)(2,1)S(1)} %collective-permute-done), channel_id=1, source_target_pairs={{0,2},{2,4},{4,6},{6,7},{7,5},{5,3},{3,1},{1,0},{8,10},{10,12},{12... | collective-permute-start | bytes 1327112 | tf_op jit(solution)/shard_map/ppermute | solution.py:129
  19.6 1.3 %collective-permute-start.16 = (bf16[3,8,144,128]{3,2,1,0:T(8,128)(2,1)S(1)}, bf16[3,8,144,128]{3,2,1,0:T(8,128)(2,1)S(1)}, u32[]{:S(2)}, u32[]{:S(2)}) collective-permute-start(bf16[3,8,144,128]{3,2,1,0:T(8,128)(2,1)S(1)} %pad_maximum_fusion), channel_id=1, source_target_pairs={{0,8},{1,9},{10,18},{11,19},{20,28},{21,29},{30,6},{31,7}} | collective-permute-start | bytes 2654216 | tf_op jit(solution)/shard_map/ppermute | solution.py:139
  21.0 3.0 %collective-permute-start.15 = (bf16[3,8,144,128]{3,2,1,0:T(8,128)(2,1)S(1)}, bf16[3,8,144,128]{3,2,1,0:T(8,128)(2,1)S(1)}, u32[]{:S(2)}, u32[]{:S(2)}) collective-permute-start(bf16[3,8,144,128]{3,2,1,0:T(8,128)(2,1)S(1)} %pad_maximum_fusion), channel_id=1, source_target_pairs={{0,16},{1,17},{10,26},{11,27},{20,4},{21,5},{30,14},{31,15}} | collective-permute-start | bytes 2654216 | tf_op jit(solution)/shard_map/ppermute | solution.py:139
  24.0 1.3 %collective-permute-start.14 = (bf16[3,8,144,128]{3,2,1,0:T(8,128)(2,1)S(1)}, bf16[3,8,144,128]{3,2,1,0:T(8,128)(2,1)S(1)}, u32[]{:S(2)}, u32[]{:S(2)}) collective-permute-start(bf16[3,8,144,128]{3,2,1,0:T(8,128)(2,1)S(1)} %pad_maximum_fusion), channel_id=1, source_target_pairs={{0,24},{1,25},{10,2},{11,3},{20,12},{21,13},{30,22},{31,23}} | collective-permute-start | bytes 2654216 | tf_op jit(solution)/shard_map/ppermute | solution.py:139
  27.1 1.7 %collective-permute-done.2 = bf16[3,2,2,144,128]{4,3,2,1,0:T(8,128)(2,1)S(1)} collective-permute-done((bf16[3,2,2,144,128]{4,3,2,1,0:T(8,128)(2,1)S(1)}, bf16[3,2,2,144,128]{4,3,2,1,0:T(8,128)(2,1)S(1)}, u32[]{:S(2)}, u32[]{:S(2)}) %collective-permute-start.2) | collective-permute-done | bytes 442400 | tf_op jit(solution)/shard_map/ppermute | solution.py:129
  28.7 1.5 %collective-permute-start.4 = (bf16[3,2,2,144,128]{4,3,2,1,0:T(8,128)(2,1)S(1)}, bf16[3,2,2,144,128]{4,3,2,1,0:T(8,128)(2,1)S(1)}, u32[]{:S(2)}, u32[]{:S(2)}) collective-permute-start(bf16[3,2,2,144,128]{4,3,2,1,0:T(8,128)(2,1)S(1)} %collective-permute-done.2), channel_id=1, source_target_pairs={{0,2},{2,4},{4,6},{6,7},{7,5},{5,3},{3,1},{1,0},{8,10},{10,12},{12... | collective-permute-start | bytes 1327112 | tf_op jit(solution)/shard_map/ppermute | solution.py:129
  32.5 6.6 %collective-permute-done.4 = bf16[3,2,2,144,128]{4,3,2,1,0:T(8,128)(2,1)S(1)} collective-permute-done((bf16[3,2,2,144,128]{4,3,2,1,0:T(8,128)(2,1)S(1)}, bf16[3,2,2,144,128]{4,3,2,1,0:T(8,128)(2,1)S(1)}, u32[]{:S(2)}, u32[]{:S(2)}) %collective-permute-start.4) | collective-permute-done | bytes 442400 | tf_op jit(solution)/shard_map/ppermute | solution.py:129
  39.2 2.3 %collective-permute-start.6 = (bf16[3,2,2,144,128]{4,3,2,1,0:T(8,128)(2,1)S(1)}, bf16[3,2,2,144,128]{4,3,2,1,0:T(8,128)(2,1)S(1)}, u32[]{:S(2)}, u32[]{:S(2)}) collective-permute-start(bf16[3,2,2,144,128]{4,3,2,1,0:T(8,128)(2,1)S(1)} %collective-permute-done.4), channel_id=1, source_target_pairs={{0,2},{2,4},{4,6},{6,7},{7,5},{5,3},{3,1},{1,0},{8,10},{10,12},{12... | collective-permute-start | bytes 1327112 | tf_op jit(solution)/shard_map/ppermute | solution.py:129
  44.7 2.3 %collective-permute-start.18 = (bf16[3,8,144,128]{3,2,1,0:T(8,128)(2,1)S(1)}, bf16[3,8,144,128]{3,2,1,0:T(8,128)(2,1)S(1)}, u32[]{:S(2)}, u32[]{:S(2)}) collective-permute-start(bf16[3,8,144,128]{3,2,1,0:T(8,128)(2,1)S(1)} %pad_maximum_fusion.1), channel_id=1, source_target_pairs={{0,16},{1,17},{10,26},{11,27},{20,4},{21,5},{30,14},{31,15}} | collective-permute-start | bytes 2654216 | tf_op jit(solution)/shard_map/ppermute | solution.py:139
  47.1 1.3 %collective-permute-start.17 = (bf16[3,8,144,128]{3,2,1,0:T(8,128)(2,1)S(1)}, bf16[3,8,144,128]{3,2,1,0:T(8,128)(2,1)S(1)}, u32[]{:S(2)}, u32[]{:S(2)}) collective-permute-start(bf16[3,8,144,128]{3,2,1,0:T(8,128)(2,1)S(1)} %pad_maximum_fusion.1), channel_id=1, source_target_pairs={{0,24},{1,25},{10,2},{11,3},{20,12},{21,13},{30,22},{31,23}} | collective-permute-start | bytes 2654216 | tf_op jit(solution)/shard_map/ppermute | solution.py:139
  49.7 2.1 %collective-permute-start.8 = (bf16[3,2,2,144,128]{4,3,2,1,0:T(8,128)(2,1)S(1)}, bf16[3,2,2,144,128]{4,3,2,1,0:T(8,128)(2,1)S(1)}, u32[]{:S(2)}, u32[]{:S(2)}) collective-permute-start(bf16[3,2,2,144,128]{4,3,2,1,0:T(8,128)(2,1)S(1)} %collective-permute-done.6), channel_id=1, source_target_pairs={{0,2},{2,4},{4,6},{6,7},{7,5},{5,3},{3,1},{1,0},{8,10},{10,12},{12... | collective-permute-start | bytes 1327112 | tf_op jit(solution)/shard_map/ppermute | solution.py:129
  53.6 7.3 %collective-permute-done.8 = bf16[3,2,2,144,128]{4,3,2,1,0:T(8,128)(2,1)S(1)} collective-permute-done((bf16[3,2,2,144,128]{4,3,2,1,0:T(8,128)(2,1)S(1)}, bf16[3,2,2,144,128]{4,3,2,1,0:T(8,128)(2,1)S(1)}, u32[]{:S(2)}, u32[]{:S(2)}) %collective-permute-start.8) | collective-permute-done | bytes 442400 | tf_op jit(solution)/shard_map/ppermute | solution.py:129
  60.9 2.2 %collective-permute-done.9 = bf16[3,2,2,144,128]{4,3,2,1,0:T(8,128)(2,1)S(1)} collective-permute-done((bf16[3,2,2,144,128]{4,3,2,1,0:T(8,128)(2,1)S(1)}, bf16[3,2,2,144,128]{4,3,2,1,0:T(8,128)(2,1)S(1)}, u32[]{:S(2)}, u32[]{:S(2)}) %collective-permute-start.9) | collective-permute-done | bytes 442400 | tf_op jit(solution)/shard_map/ppermute | solution.py:130
  66.4 3.8 %collective-permute-start.21 = (bf16[3,8,144,128]{3,2,1,0:T(8,128)(2,1)S(1)}, bf16[3,8,144,128]{3,2,1,0:T(8,128)(2,1)S(1)}, u32[]{:S(2)}, u32[]{:S(2)}) collective-permute-start(bf16[3,8,144,128]{3,2,1,0:T(8,128)(2,1)S(1)} %pad_maximum_fusion.2), channel_id=1, source_target_pairs={{0,16},{1,17},{10,26},{11,27},{20,4},{21,5},{30,14},{31,15}} | collective-permute-start | bytes 2654216 | tf_op jit(solution)/shard_map/ppermute | solution.py:139
  70.2 1.3 %collective-permute-start.20 = (bf16[3,8,144,128]{3,2,1,0:T(8,128)(2,1)S(1)}, bf16[3,8,144,128]{3,2,1,0:T(8,128)(2,1)S(1)}, u32[]{:S(2)}, u32[]{:S(2)}) collective-permute-start(bf16[3,8,144,128]{3,2,1,0:T(8,128)(2,1)S(1)} %pad_maximum_fusion.2), channel_id=1, source_target_pairs={{0,24},{1,25},{10,2},{11,3},{20,12},{21,13},{30,22},{31,23}} | collective-permute-start | bytes 2654216 | tf_op jit(solution)/shard_map/ppermute | solution.py:139
  72.2 2.8 %collective-permute-done.10 = bf16[3,2,2,144,128]{4,3,2,1,0:T(8,128)(2,1)S(1)} collective-permute-done((bf16[3,2,2,144,128]{4,3,2,1,0:T(8,128)(2,1)S(1)}, bf16[3,2,2,144,128]{4,3,2,1,0:T(8,128)(2,1)S(1)}, u32[]{:S(2)}, u32[]{:S(2)}) %collective-permute-start.10) | collective-permute-done | bytes 442400 | tf_op jit(solution)/shard_map/ppermute | solution.py:129
  75.9 6.4 %collective-permute-done.11 = bf16[3,2,2,144,128]{4,3,2,1,0:T(8,128)(2,1)S(1)} collective-permute-done((bf16[3,2,2,144,128]{4,3,2,1,0:T(8,128)(2,1)S(1)}, bf16[3,2,2,144,128]{4,3,2,1,0:T(8,128)(2,1)S(1)}, u32[]{:S(2)}, u32[]{:S(2)}) %collective-permute-start.11) | collective-permute-done | bytes 442400 | tf_op jit(solution)/shard_map/ppermute | solution.py:130
  84.3 3.1 %collective-permute-done.12 = bf16[3,2,2,144,128]{4,3,2,1,0:T(8,128)(2,1)S(1)} collective-permute-done((bf16[3,2,2,144,128]{4,3,2,1,0:T(8,128)(2,1)S(1)}, bf16[3,2,2,144,128]{4,3,2,1,0:T(8,128)(2,1)S(1)}, u32[]{:S(2)}, u32[]{:S(2)}) %collective-permute-start.12) | collective-permute-done | bytes 442400 | tf_op jit(solution)/shard_map/ppermute | solution.py:129
  87.4 2.1 %collective-permute-start.24 = (bf16[3,4,144,128]{3,2,1,0:T(8,128)(2,1)}, bf16[3,4,144,128]{3,2,1,0:T(8,128)(2,1)}, u32[]{:S(2)}, u32[]{:S(2)}) collective-permute-start(bf16[3,4,144,128]{3,2,1,0:T(8,128)(2,1)} %pad_maximum_fusion.3), channel_id=1, source_target_pairs={{0,16},{1,17},{10,26},{11,27},{20,4},{21,5},{30,14},{31,15}} | collective-permute-start | bytes 1327112 | tf_op jit(solution)/shard_map/ppermute | solution.py:105
  89.6 2.6 %collective-permute-done.13 = bf16[3,2,2,144,128]{4,3,2,1,0:T(8,128)(2,1)S(1)} collective-permute-done((bf16[3,2,2,144,128]{4,3,2,1,0:T(8,128)(2,1)S(1)}, bf16[3,2,2,144,128]{4,3,2,1,0:T(8,128)(2,1)S(1)}, u32[]{:S(2)}, u32[]{:S(2)}) %collective-permute-start.13) | collective-permute-done | bytes 442400 | tf_op jit(solution)/shard_map/ppermute | solution.py:130
  93.1 3.3 %collective-permute-start.27 = (bf16[3,4,144,128]{3,2,1,0:T(8,128)(2,1)}, bf16[3,4,144,128]{3,2,1,0:T(8,128)(2,1)}, u32[]{:S(2)}, u32[]{:S(2)}) collective-permute-start(bf16[3,4,144,128]{3,2,1,0:T(8,128)(2,1)} %pad_maximum_fusion.4), channel_id=1, source_target_pairs={{0,16},{1,17},{10,26},{11,27},{20,4},{21,5},{30,14},{31,15}} | collective-permute-start | bytes 1327112 | tf_op jit(solution)/shard_map/ppermute | solution.py:105
  97.3 2.1 %collective-permute-start.23 = (bf16[3,4,144,128]{3,2,1,0:T(8,128)(2,1)}, bf16[3,4,144,128]{3,2,1,0:T(8,128)(2,1)}, u32[]{:S(2)}, u32[]{:S(2)}) collective-permute-start(bf16[3,4,144,128]{3,2,1,0:T(8,128)(2,1)} %pad_maximum_fusion.3), channel_id=1, source_target_pairs={{0,8},{1,9},{10,2},{11,3},{20,28},{21,29},{30,22},{31,23}} | collective-permute-start | bytes 1327112 | tf_op jit(solution)/shard_map/ppermute | solution.py:105
  99.3 2.1 %collective-permute-start.26 = (bf16[3,4,144,128]{3,2,1,0:T(8,128)(2,1)}, bf16[3,4,144,128]{3,2,1,0:T(8,128)(2,1)}, u32[]{:S(2)}, u32[]{:S(2)}) collective-permute-start(bf16[3,4,144,128]{3,2,1,0:T(8,128)(2,1)} %pad_maximum_fusion.4), channel_id=1, source_target_pairs={{0,8},{1,9},{10,2},{11,3},{20,28},{21,29},{30,22},{31,23}} | collective-permute-start | bytes 1327112 | tf_op jit(solution)/shard_map/ppermute | solution.py:105
  101.4 1.4 %collective-permute-start.25 = (bf16[3,4,144,128]{3,2,1,0:T(8,128)(2,1)}, bf16[3,4,144,128]{3,2,1,0:T(8,128)(2,1)}, u32[]{:S(2)}, u32[]{:S(2)}) collective-permute-start(bf16[3,4,144,128]{3,2,1,0:T(8,128)(2,1)} %collective-permute-done.24), channel_id=1, source_target_pairs={{16,24},{17,25},{26,18},{27,19},{4,12},{5,13},{14,6},{15,7}} | collective-permute-start | bytes 1327112 | tf_op jit(solution)/shard_map/ppermute | solution.py:105
  103.4 1.4 %collective-permute-start.28 = (bf16[3,4,144,128]{3,2,1,0:T(8,128)(2,1)}, bf16[3,4,144,128]{3,2,1,0:T(8,128)(2,1)}, u32[]{:S(2)}, u32[]{:S(2)}) collective-permute-start(bf16[3,4,144,128]{3,2,1,0:T(8,128)(2,1)} %collective-permute-done.27), channel_id=1, source_target_pairs={{16,24},{17,25},{26,18},{27,19},{4,12},{5,13},{14,6},{15,7}} | collective-permute-start | bytes 1327112 | tf_op jit(solution)/shard_map/ppermute | solution.py:105
  106.6 1.7 %slice.19 = bf16[96,2,1,1]{3,2,1,0:T(2,128)(2,1)} slice(bf16[96,2,144,128]{3,2,1,0:T(8,128)(2,1)} %bitcast.44), slice={[0:96], [0:2], [131:132], [0:1]} | slice | bytes 768 | tf_op jit(solution)/shard_map/slice | solution.py:150
  109.3 1.5 %select_dynamic-update-slice_fusion.4 = bf16[3,32,144,128]{3,2,1,0:T(8,128)(2,1)S(1)} fusion(bf16[3,32,144,128]{3,2,1,0:T(8,128)(2,1)S(1)} %select_dynamic-update-slice_fusion, bf16[3,4,144,128]{3,2,1,0:T(8,128)(2,1)} %collective-permute-done.23, bf16[3,4,144,128]{3,2,1,0:T(8,128)(2,1)} %collective-permute-done.24, ...), kind=kLoop, calls=%fused_computation.10 | loop fusion | flops 1548288 | bytes 2211843
  110.8 1.5 %select_dynamic-update-slice_fusion.3 = bf16[3,32,144,128]{3,2,1,0:T(8,128)(2,1)S(1)} fusion(bf16[3,32,144,128]{3,2,1,0:T(8,128)(2,1)S(1)} %select_dynamic-update-slice_fusion.4, bf16[3,4,144,128]{3,2,1,0:T(8,128)(2,1)} %collective-permute-done.26, bf16[3,4,144,128]{3,2,1,0:T(8,128)(2,1)} %collective-permute-done.27, ...), kind=kLoop, calls=%fused_computation.9 | loop fusion | flops 1548288 | bytes 2211843 | tf_op jit(solution)/shard_map/concatenate | solution.py:145
  114.7 10.8 %shard_map.37 = f32[2048,1024]{1,0:T(8,128)} custom-call(s32[288]{0:T(512)S(1)} %min.12.offs_ref, bf16[96,2,144,128]{3,2,1,0:T(8,128)(2,1)} %bitcast.45, bf16[96,144,128]{2,1,0:T(8,128)(2,1)S(1)} %bitcast.43), custom_call_target="tpu_custom_call" | custom-call | flops 805306368 | bytes 17825792 | tf_op jit(solution)/shard_map/pallas_call | solution.py:40
  (91 shorter events, 26.8 us)
Async XLA Ops:
  4.2 13.2 %collective-permute-start = (bf16[3,2,2,144,128]{4,3,2,1,0:T(8,128)(2,1)S(1)}, bf16[3,2,2,144,128]{4,3,2,1,0:T(8,128)(2,1)S(1)}, u32[]{:S(2)}, u32[]{:S(2)}) collective-permute-start(bf16[3,2,2,144,128]{4,3,2,1,0:T(8,128)(2,1)S(1)} %get-tuple-element.5), channel_id=1, source_target_pairs={{0,2},{2,4},{4,6},{6,7},{7,5},{5,3},{3,1},{1,0},{8,10},{10,12},{12... | collective-permute-start | bytes 1327112 | tf_op jit(solution)/shard_map/ppermute | solution.py:129
  7.3 11.9 %collective-permute-start.1 = (bf16[3,2,2,144,128]{4,3,2,1,0:T(8,128)(2,1)S(1)}, bf16[3,2,2,144,128]{4,3,2,1,0:T(8,128)(2,1)S(1)}, u32[]{:S(2)}, u32[]{:S(2)}) collective-permute-start(bf16[3,2,2,144,128]{4,3,2,1,0:T(8,128)(2,1)S(1)} %get-tuple-element.6), channel_id=1, source_target_pairs={{2,0},{4,2},{6,4},{7,6},{5,7},{3,5},{1,3},{0,1},{10,8},{12,10},{14... | collective-permute-start | bytes 1327112 | tf_op jit(solution)/shard_map/ppermute | solution.py:130
  17.4 11.4 %collective-permute-start.2 = (bf16[3,2,2,144,128]{4,3,2,1,0:T(8,128)(2,1)S(1)}, bf16[3,2,2,144,128]{4,3,2,1,0:T(8,128)(2,1)S(1)}, u32[]{:S(2)}, u32[]{:S(2)}) collective-permute-start(bf16[3,2,2,144,128]{4,3,2,1,0:T(8,128)(2,1)S(1)} %collective-permute-done), channel_id=1, source_target_pairs={{0,2},{2,4},{4,6},{6,7},{7,5},{5,3},{3,1},{1,0},{8,10},{10,12},{12... | collective-permute-start | bytes 1327112 | tf_op jit(solution)/shard_map/ppermute | solution.py:129
  19.2 11.0 %collective-permute-start.3 = (bf16[3,2,2,144,128]{4,3,2,1,0:T(8,128)(2,1)S(1)}, bf16[3,2,2,144,128]{4,3,2,1,0:T(8,128)(2,1)S(1)}, u32[]{:S(2)}, u32[]{:S(2)}) collective-permute-start(bf16[3,2,2,144,128]{4,3,2,1,0:T(8,128)(2,1)S(1)} %collective-permute-done.1), channel_id=1, source_target_pairs={{2,0},{4,2},{6,4},{7,6},{5,7},{3,5},{1,3},{0,1},{10,8},{12,10},{14... | collective-permute-start | bytes 1327112 | tf_op jit(solution)/shard_map/ppermute | solution.py:130
  19.6 23.7 %collective-permute-start.16 = (bf16[3,8,144,128]{3,2,1,0:T(8,128)(2,1)S(1)}, bf16[3,8,144,128]{3,2,1,0:T(8,128)(2,1)S(1)}, u32[]{:S(2)}, u32[]{:S(2)}) collective-permute-start(bf16[3,8,144,128]{3,2,1,0:T(8,128)(2,1)S(1)} %pad_maximum_fusion), channel_id=1, source_target_pairs={{0,8},{1,9},{10,18},{11,19},{20,28},{21,29},{30,6},{31,7}} | collective-permute-start | bytes 2654216 | tf_op jit(solution)/shard_map/ppermute | solution.py:139
  21.0 23.7 %collective-permute-start.15 = (bf16[3,8,144,128]{3,2,1,0:T(8,128)(2,1)S(1)}, bf16[3,8,144,128]{3,2,1,0:T(8,128)(2,1)S(1)}, u32[]{:S(2)}, u32[]{:S(2)}) collective-permute-start(bf16[3,8,144,128]{3,2,1,0:T(8,128)(2,1)S(1)} %pad_maximum_fusion), channel_id=1, source_target_pairs={{0,16},{1,17},{10,26},{11,27},{20,4},{21,5},{30,14},{31,15}} | collective-permute-start | bytes 2654216 | tf_op jit(solution)/shard_map/ppermute | solution.py:139
  24.0 23.0 %collective-permute-start.14 = (bf16[3,8,144,128]{3,2,1,0:T(8,128)(2,1)S(1)}, bf16[3,8,144,128]{3,2,1,0:T(8,128)(2,1)S(1)}, u32[]{:S(2)}, u32[]{:S(2)}) collective-permute-start(bf16[3,8,144,128]{3,2,1,0:T(8,128)(2,1)S(1)} %pad_maximum_fusion), channel_id=1, source_target_pairs={{0,24},{1,25},{10,2},{11,3},{20,12},{21,13},{30,22},{31,23}} | collective-permute-start | bytes 2654216 | tf_op jit(solution)/shard_map/ppermute | solution.py:139
  28.7 10.4 %collective-permute-start.4 = (bf16[3,2,2,144,128]{4,3,2,1,0:T(8,128)(2,1)S(1)}, bf16[3,2,2,144,128]{4,3,2,1,0:T(8,128)(2,1)S(1)}, u32[]{:S(2)}, u32[]{:S(2)}) collective-permute-start(bf16[3,2,2,144,128]{4,3,2,1,0:T(8,128)(2,1)S(1)} %collective-permute-done.2), channel_id=1, source_target_pairs={{0,2},{2,4},{4,6},{6,7},{7,5},{5,3},{3,1},{1,0},{8,10},{10,12},{12... | collective-permute-start | bytes 1327112 | tf_op jit(solution)/shard_map/ppermute | solution.py:129
  30.2 11.3 %collective-permute-start.5 = (bf16[3,2,2,144,128]{4,3,2,1,0:T(8,128)(2,1)S(1)}, bf16[3,2,2,144,128]{4,3,2,1,0:T(8,128)(2,1)S(1)}, u32[]{:S(2)}, u32[]{:S(2)}) collective-permute-start(bf16[3,2,2,144,128]{4,3,2,1,0:T(8,128)(2,1)S(1)} %collective-permute-done.3), channel_id=1, source_target_pairs={{2,0},{4,2},{6,4},{7,6},{5,7},{3,5},{1,3},{0,1},{10,8},{12,10},{14... | collective-permute-start | bytes 1327112 | tf_op jit(solution)/shard_map/ppermute | solution.py:130
  39.2 10.5 %collective-permute-start.6 = (bf16[3,2,2,144,128]{4,3,2,1,0:T(8,128)(2,1)S(1)}, bf16[3,2,2,144,128]{4,3,2,1,0:T(8,128)(2,1)S(1)}, u32[]{:S(2)}, u32[]{:S(2)}) collective-permute-start(bf16[3,2,2,144,128]{4,3,2,1,0:T(8,128)(2,1)S(1)} %collective-permute-done.4), channel_id=1, source_target_pairs={{0,2},{2,4},{4,6},{6,7},{7,5},{5,3},{3,1},{1,0},{8,10},{10,12},{12... | collective-permute-start | bytes 1327112 | tf_op jit(solution)/shard_map/ppermute | solution.py:129
  41.5 10.3 %collective-permute-start.7 = (bf16[3,2,2,144,128]{4,3,2,1,0:T(8,128)(2,1)S(1)}, bf16[3,2,2,144,128]{4,3,2,1,0:T(8,128)(2,1)S(1)}, u32[]{:S(2)}, u32[]{:S(2)}) collective-permute-start(bf16[3,2,2,144,128]{4,3,2,1,0:T(8,128)(2,1)S(1)} %collective-permute-done.5), channel_id=1, source_target_pairs={{2,0},{4,2},{6,4},{7,6},{5,7},{3,5},{1,3},{0,1},{10,8},{12,10},{14... | collective-permute-start | bytes 1327112 | tf_op jit(solution)/shard_map/ppermute | solution.py:130
  43.4 23.0 %collective-permute-start.19 = (bf16[3,8,144,128]{3,2,1,0:T(8,128)(2,1)S(1)}, bf16[3,8,144,128]{3,2,1,0:T(8,128)(2,1)S(1)}, u32[]{:S(2)}, u32[]{:S(2)}) collective-permute-start(bf16[3,8,144,128]{3,2,1,0:T(8,128)(2,1)S(1)} %pad_maximum_fusion.1), channel_id=1, source_target_pairs={{0,8},{1,9},{10,18},{11,19},{20,28},{21,29},{30,6},{31,7}} | collective-permute-start | bytes 2654216 | tf_op jit(solution)/shard_map/ppermute | solution.py:139
  44.7 25.5 %collective-permute-start.18 = (bf16[3,8,144,128]{3,2,1,0:T(8,128)(2,1)S(1)}, bf16[3,8,144,128]{3,2,1,0:T(8,128)(2,1)S(1)}, u32[]{:S(2)}, u32[]{:S(2)}) collective-permute-start(bf16[3,8,144,128]{3,2,1,0:T(8,128)(2,1)S(1)} %pad_maximum_fusion.1), channel_id=1, source_target_pairs={{0,16},{1,17},{10,26},{11,27},{20,4},{21,5},{30,14},{31,15}} | collective-permute-start | bytes 2654216 | tf_op jit(solution)/shard_map/ppermute | solution.py:139
  47.1 24.5 %collective-permute-start.17 = (bf16[3,8,144,128]{3,2,1,0:T(8,128)(2,1)S(1)}, bf16[3,8,144,128]{3,2,1,0:T(8,128)(2,1)S(1)}, u32[]{:S(2)}, u32[]{:S(2)}) collective-permute-start(bf16[3,8,144,128]{3,2,1,0:T(8,128)(2,1)S(1)} %pad_maximum_fusion.1), channel_id=1, source_target_pairs={{0,24},{1,25},{10,2},{11,3},{20,12},{21,13},{30,22},{31,23}} | collective-permute-start | bytes 2654216 | tf_op jit(solution)/shard_map/ppermute | solution.py:139
  49.7 11.2 %collective-permute-start.8 = (bf16[3,2,2,144,128]{4,3,2,1,0:T(8,128)(2,1)S(1)}, bf16[3,2,2,144,128]{4,3,2,1,0:T(8,128)(2,1)S(1)}, u32[]{:S(2)}, u32[]{:S(2)}) collective-permute-start(bf16[3,2,2,144,128]{4,3,2,1,0:T(8,128)(2,1)S(1)} %collective-permute-done.6), channel_id=1, source_target_pairs={{0,2},{2,4},{4,6},{6,7},{7,5},{5,3},{3,1},{1,0},{8,10},{10,12},{12... | collective-permute-start | bytes 1327112 | tf_op jit(solution)/shard_map/ppermute | solution.py:129
  51.8 11.3 %collective-permute-start.9 = (bf16[3,2,2,144,128]{4,3,2,1,0:T(8,128)(2,1)S(1)}, bf16[3,2,2,144,128]{4,3,2,1,0:T(8,128)(2,1)S(1)}, u32[]{:S(2)}, u32[]{:S(2)}) collective-permute-start(bf16[3,2,2,144,128]{4,3,2,1,0:T(8,128)(2,1)S(1)} %collective-permute-done.7), channel_id=1, source_target_pairs={{2,0},{4,2},{6,4},{7,6},{5,7},{3,5},{1,3},{0,1},{10,8},{12,10},{14... | collective-permute-start | bytes 1327112 | tf_op jit(solution)/shard_map/ppermute | solution.py:130
  63.2 36.1 %collective-permute-start.22 = (bf16[3,8,144,128]{3,2,1,0:T(8,128)(2,1)S(1)}, bf16[3,8,144,128]{3,2,1,0:T(8,128)(2,1)S(1)}, u32[]{:S(2)}, u32[]{:S(2)}) collective-permute-start(bf16[3,8,144,128]{3,2,1,0:T(8,128)(2,1)S(1)} %pad_maximum_fusion.2), channel_id=1, source_target_pairs={{0,8},{1,9},{10,18},{11,19},{20,28},{21,29},{30,6},{31,7}} | collective-permute-start | bytes 2654216 | tf_op jit(solution)/shard_map/ppermute | solution.py:139
  64.6 10.3 %collective-permute-start.10 = (bf16[3,2,2,144,128]{4,3,2,1,0:T(8,128)(2,1)S(1)}, bf16[3,2,2,144,128]{4,3,2,1,0:T(8,128)(2,1)S(1)}, u32[]{:S(2)}, u32[]{:S(2)}) collective-permute-start(bf16[3,2,2,144,128]{4,3,2,1,0:T(8,128)(2,1)S(1)} %collective-permute-done.8), channel_id=1, source_target_pairs={{0,2},{2,4},{4,6},{6,7},{7,5},{5,3},{3,1},{1,0},{8,10},{10,12},{12... | collective-permute-start | bytes 1327112 | tf_op jit(solution)/shard_map/ppermute | solution.py:129
  66.4 35.1 %collective-permute-start.21 = (bf16[3,8,144,128]{3,2,1,0:T(8,128)(2,1)S(1)}, bf16[3,8,144,128]{3,2,1,0:T(8,128)(2,1)S(1)}, u32[]{:S(2)}, u32[]{:S(2)}) collective-permute-start(bf16[3,8,144,128]{3,2,1,0:T(8,128)(2,1)S(1)} %pad_maximum_fusion.2), channel_id=1, source_target_pairs={{0,16},{1,17},{10,26},{11,27},{20,4},{21,5},{30,14},{31,15}} | collective-permute-start | bytes 2654216 | tf_op jit(solution)/shard_map/ppermute | solution.py:139
  70.2 32.7 %collective-permute-start.20 = (bf16[3,8,144,128]{3,2,1,0:T(8,128)(2,1)S(1)}, bf16[3,8,144,128]{3,2,1,0:T(8,128)(2,1)S(1)}, u32[]{:S(2)}, u32[]{:S(2)}) collective-permute-start(bf16[3,8,144,128]{3,2,1,0:T(8,128)(2,1)S(1)} %pad_maximum_fusion.2), channel_id=1, source_target_pairs={{0,24},{1,25},{10,2},{11,3},{20,12},{21,13},{30,22},{31,23}} | collective-permute-start | bytes 2654216 | tf_op jit(solution)/shard_map/ppermute | solution.py:139
  71.6 10.8 %collective-permute-start.11 = (bf16[3,2,2,144,128]{4,3,2,1,0:T(8,128)(2,1)S(1)}, bf16[3,2,2,144,128]{4,3,2,1,0:T(8,128)(2,1)S(1)}, u32[]{:S(2)}, u32[]{:S(2)}) collective-permute-start(bf16[3,2,2,144,128]{4,3,2,1,0:T(8,128)(2,1)S(1)} %collective-permute-done.9), channel_id=1, source_target_pairs={{2,0},{4,2},{6,4},{7,6},{5,7},{3,5},{1,3},{0,1},{10,8},{12,10},{14... | collective-permute-start | bytes 1327112 | tf_op jit(solution)/shard_map/ppermute | solution.py:130
  74.9 12.5 %collective-permute-start.12 = (bf16[3,2,2,144,128]{4,3,2,1,0:T(8,128)(2,1)S(1)}, bf16[3,2,2,144,128]{4,3,2,1,0:T(8,128)(2,1)S(1)}, u32[]{:S(2)}, u32[]{:S(2)}) collective-permute-start(bf16[3,2,2,144,128]{4,3,2,1,0:T(8,128)(2,1)S(1)} %collective-permute-done.10), channel_id=1, source_target_pairs={{0,2},{2,4},{4,6},{6,7},{7,5},{5,3},{3,1},{1,0},{8,10},{10,12},{12... | collective-permute-start | bytes 1327112 | tf_op jit(solution)/shard_map/ppermute | solution.py:129
  75.9 26.9 %copy-start = (bf16[3,2,144,128]{3,2,1,0:T(8,128)(2,1)}, bf16[3,2,144,128]{3,2,1,0:T(8,128)(2,1)S(1)}, u32[]{:S(2)}) copy-start(bf16[3,2,144,128]{3,2,1,0:T(8,128)(2,1)S(1)} %dynamic-slice_bitcast_fusion.3) | copy-start | bytes 663556
  82.3 9.8 %collective-permute-start.13 = (bf16[3,2,2,144,128]{4,3,2,1,0:T(8,128)(2,1)S(1)}, bf16[3,2,2,144,128]{4,3,2,1,0:T(8,128)(2,1)S(1)}, u32[]{:S(2)}, u32[]{:S(2)}) collective-permute-start(bf16[3,2,2,144,128]{4,3,2,1,0:T(8,128)(2,1)S(1)} %collective-permute-done.11), channel_id=1, source_target_pairs={{2,0},{4,2},{6,4},{7,6},{5,7},{3,5},{1,3},{0,1},{10,8},{12,10},{14... | collective-permute-start | bytes 1327112 | tf_op jit(solution)/shard_map/ppermute | solution.py:130
  87.4 9.8 %collective-permute-start.24 = (bf16[3,4,144,128]{3,2,1,0:T(8,128)(2,1)}, bf16[3,4,144,128]{3,2,1,0:T(8,128)(2,1)}, u32[]{:S(2)}, u32[]{:S(2)}) collective-permute-start(bf16[3,4,144,128]{3,2,1,0:T(8,128)(2,1)} %pad_maximum_fusion.3), channel_id=1, source_target_pairs={{0,16},{1,17},{10,26},{11,27},{20,4},{21,5},{30,14},{31,15}} | collective-permute-start | bytes 1327112 | tf_op jit(solution)/shard_map/ppermute | solution.py:105
  89.5 13.3 %copy-start.1 = (bf16[3,2,144,128]{3,2,1,0:T(8,128)(2,1)}, bf16[3,2,144,128]{3,2,1,0:T(8,128)(2,1)S(1)}, u32[]{:S(2)}) copy-start(bf16[3,2,144,128]{3,2,1,0:T(8,128)(2,1)S(1)} %dynamic-slice_bitcast_fusion.1) | copy-start | bytes 663556
  92.2 10.7 %copy-start.2 = (bf16[3,2,144,128]{3,2,1,0:T(8,128)(2,1)}, bf16[3,2,144,128]{3,2,1,0:T(8,128)(2,1)S(1)}, u32[]{:S(2)}) copy-start(bf16[3,2,144,128]{3,2,1,0:T(8,128)(2,1)S(1)} %dynamic-slice_bitcast_fusion) | copy-start | bytes 663556
  93.1 10.4 %collective-permute-start.27 = (bf16[3,4,144,128]{3,2,1,0:T(8,128)(2,1)}, bf16[3,4,144,128]{3,2,1,0:T(8,128)(2,1)}, u32[]{:S(2)}, u32[]{:S(2)}) collective-permute-start(bf16[3,4,144,128]{3,2,1,0:T(8,128)(2,1)} %pad_maximum_fusion.4), channel_id=1, source_target_pairs={{0,16},{1,17},{10,26},{11,27},{20,4},{21,5},{30,14},{31,15}} | collective-permute-start | bytes 1327112 | tf_op jit(solution)/shard_map/ppermute | solution.py:105
  97.3 12.0 %collective-permute-start.23 = (bf16[3,4,144,128]{3,2,1,0:T(8,128)(2,1)}, bf16[3,4,144,128]{3,2,1,0:T(8,128)(2,1)}, u32[]{:S(2)}, u32[]{:S(2)}) collective-permute-start(bf16[3,4,144,128]{3,2,1,0:T(8,128)(2,1)} %pad_maximum_fusion.3), channel_id=1, source_target_pairs={{0,8},{1,9},{10,2},{11,3},{20,28},{21,29},{30,22},{31,23}} | collective-permute-start | bytes 1327112 | tf_op jit(solution)/shard_map/ppermute | solution.py:105
  99.3 11.4 %collective-permute-start.26 = (bf16[3,4,144,128]{3,2,1,0:T(8,128)(2,1)}, bf16[3,4,144,128]{3,2,1,0:T(8,128)(2,1)}, u32[]{:S(2)}, u32[]{:S(2)}) collective-permute-start(bf16[3,4,144,128]{3,2,1,0:T(8,128)(2,1)} %pad_maximum_fusion.4), channel_id=1, source_target_pairs={{0,8},{1,9},{10,2},{11,3},{20,28},{21,29},{30,22},{31,23}} | collective-permute-start | bytes 1327112 | tf_op jit(solution)/shard_map/ppermute | solution.py:105
  101.4 7.8 %collective-permute-start.25 = (bf16[3,4,144,128]{3,2,1,0:T(8,128)(2,1)}, bf16[3,4,144,128]{3,2,1,0:T(8,128)(2,1)}, u32[]{:S(2)}, u32[]{:S(2)}) collective-permute-start(bf16[3,4,144,128]{3,2,1,0:T(8,128)(2,1)} %collective-permute-done.24), channel_id=1, source_target_pairs={{16,24},{17,25},{26,18},{27,19},{4,12},{5,13},{14,6},{15,7}} | collective-permute-start | bytes 1327112 | tf_op jit(solution)/shard_map/ppermute | solution.py:105
  103.4 7.3 %collective-permute-start.28 = (bf16[3,4,144,128]{3,2,1,0:T(8,128)(2,1)}, bf16[3,4,144,128]{3,2,1,0:T(8,128)(2,1)}, u32[]{:S(2)}, u32[]{:S(2)}) collective-permute-start(bf16[3,4,144,128]{3,2,1,0:T(8,128)(2,1)} %collective-permute-done.27), channel_id=1, source_target_pairs={{16,24},{17,25},{26,18},{27,19},{4,12},{5,13},{14,6},{15,7}} | collective-permute-start | bytes 1327112 | tf_op jit(solution)/shard_map/ppermute | solution.py:105
  (1 other events, 4.8 us)

commit v20 on v19

--- a/solution.py
+++ b/solution.py
@@ -133,7 +133,7 @@
         if any(batch[-1] == step for batch in batches):
             own = jnp.concatenate(pending, axis=1)
             pending = []
-            if step < ncol - 2:
+            if step < 0:
                 got = own
                 for j, fan in enumerate(fans, start=1):
                     got = jnp.where(which == j, lax.ppermute(own, ("row", "col"), fan), got)

time: 126 us -> 124 us (0.984)
  waiting for transfers between devices: 43.5 us -> 35 us
  starting transfers between devices: 42.8 us -> 46 us
  other arithmetic: 10.3 us -> 12.5 us
    ppermute x6 -> x15, starting transfers between devices: 12.5 us -> 30.8 us  [send(): lax.ppermute(v, ('row', 'col'), [(a * ncol + cc, b * ncol + cc) for a, b,...]
    ppermute x9 -> x0, starting transfers between devices: 17.3 us -> none  [local(): got = jnp.where(which == j, lax.ppermute(own, ('row', 'col'), fan), got)]
    ppermute x7, waiting for transfers between devices: 11.2 us -> 0.02 us  [local(): b = lax.ppermute(b, 'col', backward)]
    ppermute x7, starting transfers between devices: 1.17 us -> 4.8 us  [local(): b = lax.ppermute(b, 'col', backward)]
    ppermute x7, waiting for transfers between devices: 32.3 us -> 35 us  [local(): a = lax.ppermute(a, 'col', forward)]
    unnamed x5, other arithmetic: 5.37 us -> 6.78 us
    ppermute x7, starting transfers between devices: 11.8 us -> 10.5 us  [local(): a = lax.ppermute(a, 'col', forward)]
    unnamed x21 -> x29, local copies, waits for them, and re-layouts: 11.1 us -> 11.2 us
  transfers between devices with their start and end apart: 29 -> 29, of which waited for: 10 -> 7; matrix products, arithmetic and copies ran while one was open for 16% -> 18% of each run, Pallas kernels for 0% -> 0%
where the time goes in v20:
time: 124 us; the launch traced here: 123 us
  starting transfers between devices  46 us (37%)
  waiting for transfers between devices  35 us (28%)
  local copies, waits for them, and re-layouts  18 us (15%)
  other arithmetic  12.5 us (10%)
  Pallas kernels  10.8 us (9%)
    ppermute x7, waiting for transfers between devices, local(): a = lax.ppermute(a, 'col', forward)  35 us
    ppermute x15, starting transfers between devices, send(): lax.ppermute(v, ('row', 'col'), [(a * ncol + cc, b * ncol + cc) for a, b,...  30.8 us
    unnamed x29, local copies, waits for them, and re-layouts  11.2 us
    pallas_call x1, Pallas kernels, gram_call(): pl.pallas_call(kernel, grid_spec=pltpu.PrefetchScalarGridSpec(num_scalar_...  10.8 us
    ppermute x7, starting transfers between devices, local(): a = lax.ppermute(a, 'col', forward)  10.5 us
    unnamed x5, other arithmetic  6.78 us
    ppermute x7, starting transfers between devices, local(): b = lax.ppermute(b, 'col', backward)  4.8 us
    concatenate x5, other arithmetic, local(): own = jnp.concatenate(pending, axis=1)  2.99 us
  transfers between devices with their start and end apart: 29, of which 7 were waited for; matrix products, arithmetic and copies ran while one was open for 18% of the time, Pallas kernels for 0%

profile of v20, /device:TPU:0, one launch (start us, length us, event | category | flops | bytes accessed | tf_op | source)
XLA Modules:
  0.0 122.7 jit_solution(7490260753856835719)
XLA Ops:
  1.7 2.4 %constant_dynamic-update-slice_fusion.14 = (bf16[3,32,2,144,128]{4,3,2,1,0:T(8,128)(2,1)}, bf16[3,4,2,144,128]{4,3,2,1,0:T(8,128)(2,1)S(1)}) fusion(bf16[144]{0:T(256)(128)(2,1)S(1)} %pad.21.clone, bf16[3,4,2,1,128]{4,3,2,1,0:T(2,128)(2,1)S(1)} %broadcast_in_dim.7, bf16[3,4,2,3,128]{4,3,2,1,0:T(4,128)(2,1)S(1)} %broadcast_in_dim.6, ...), kind=kLoop, calls=%fused_computation.42 | loop fusion | flops 3538943 | bytes 2580768
  4.2 3.1 %collective-permute-start = (bf16[3,2,2,144,128]{4,3,2,1,0:T(8,128)(2,1)S(1)}, bf16[3,2,2,144,128]{4,3,2,1,0:T(8,128)(2,1)S(1)}, u32[]{:S(2)}, u32[]{:S(2)}) collective-permute-start(bf16[3,2,2,144,128]{4,3,2,1,0:T(8,128)(2,1)S(1)} %get-tuple-element.5), channel_id=1, source_target_pairs={{0,2},{2,4},{4,6},{6,7},{7,5},{5,3},{3,1},{1,0},{8,10},{10,12},{12... | collective-permute-start | bytes 1327112 | tf_op jit(solution)/shard_map/ppermute | solution.py:129
  7.3 10.1 %collective-permute-done = bf16[3,2,2,144,128]{4,3,2,1,0:T(8,128)(2,1)S(1)} collective-permute-done((bf16[3,2,2,144,128]{4,3,2,1,0:T(8,128)(2,1)S(1)}, bf16[3,2,2,144,128]{4,3,2,1,0:T(8,128)(2,1)S(1)}, u32[]{:S(2)}, u32[]{:S(2)}) %collective-permute-start) | collective-permute-done | bytes 442400 | tf_op jit(solution)/shard_map/ppermute | solution.py:129
  17.4 1.8 %collective-permute-start.2 = (bf16[3,2,2,144,128]{4,3,2,1,0:T(8,128)(2,1)S(1)}, bf16[3,2,2,144,128]{4,3,2,1,0:T(8,128)(2,1)S(1)}, u32[]{:S(2)}, u32[]{:S(2)}) collective-permute-start(bf16[3,2,2,144,128]{4,3,2,1,0:T(8,128)(2,1)S(1)} %collective-permute-done), channel_id=1, source_target_pairs={{0,2},{2,4},{4,6},{6,7},{7,5},{5,3},{3,1},{1,0},{8,10},{10,12},{12... | collective-permute-start | bytes 1327112 | tf_op jit(solution)/shard_map/ppermute | solution.py:129
  19.6 3.7 %collective-permute-start.15 = (bf16[3,8,144,128]{3,2,1,0:T(8,128)(2,1)S(1)}, bf16[3,8,144,128]{3,2,1,0:T(8,128)(2,1)S(1)}, u32[]{:S(2)}, u32[]{:S(2)}) collective-permute-start(bf16[3,8,144,128]{3,2,1,0:T(8,128)(2,1)S(1)} %pad_maximum_fusion), channel_id=1, source_target_pairs={{0,16},{1,17},{10,26},{11,27},{20,4},{21,5},{30,14},{31,15}} | collective-permute-start | bytes 2654216 | tf_op jit(solution)/shard_map/ppermute | solution.py:105
  23.3 1.3 %collective-permute-start.14 = (bf16[3,8,144,128]{3,2,1,0:T(8,128)(2,1)S(1)}, bf16[3,8,144,128]{3,2,1,0:T(8,128)(2,1)S(1)}, u32[]{:S(2)}, u32[]{:S(2)}) collective-permute-start(bf16[3,8,144,128]{3,2,1,0:T(8,128)(2,1)S(1)} %pad_maximum_fusion), channel_id=1, source_target_pairs={{0,8},{1,9},{10,2},{11,3},{20,28},{21,29},{30,22},{31,23}} | collective-permute-start | bytes 2654216 | tf_op jit(solution)/shard_map/ppermute | solution.py:105
  26.4 2.4 %collective-permute-done.2 = bf16[3,2,2,144,128]{4,3,2,1,0:T(8,128)(2,1)S(1)} collective-permute-done((bf16[3,2,2,144,128]{4,3,2,1,0:T(8,128)(2,1)S(1)}, bf16[3,2,2,144,128]{4,3,2,1,0:T(8,128)(2,1)S(1)}, u32[]{:S(2)}, u32[]{:S(2)}) %collective-permute-start.2) | collective-permute-done | bytes 442400 | tf_op jit(solution)/shard_map/ppermute | solution.py:129
  28.8 1.5 %collective-permute-start.4 = (bf16[3,2,2,144,128]{4,3,2,1,0:T(8,128)(2,1)S(1)}, bf16[3,2,2,144,128]{4,3,2,1,0:T(8,128)(2,1)S(1)}, u32[]{:S(2)}, u32[]{:S(2)}) collective-permute-start(bf16[3,2,2,144,128]{4,3,2,1,0:T(8,128)(2,1)S(1)} %collective-permute-done.2), channel_id=1, source_target_pairs={{0,2},{2,4},{4,6},{6,7},{7,5},{5,3},{3,1},{1,0},{8,10},{10,12},{12... | collective-permute-start | bytes 1327112 | tf_op jit(solution)/shard_map/ppermute | solution.py:129
  32.5 6.6 %collective-permute-done.4 = bf16[3,2,2,144,128]{4,3,2,1,0:T(8,128)(2,1)S(1)} collective-permute-done((bf16[3,2,2,144,128]{4,3,2,1,0:T(8,128)(2,1)S(1)}, bf16[3,2,2,144,128]{4,3,2,1,0:T(8,128)(2,1)S(1)}, u32[]{:S(2)}, u32[]{:S(2)}) %collective-permute-start.4) | collective-permute-done | bytes 442400 | tf_op jit(solution)/shard_map/ppermute | solution.py:129
  39.2 1.4 %collective-permute-start.6 = (bf16[3,2,2,144,128]{4,3,2,1,0:T(8,128)(2,1)S(1)}, bf16[3,2,2,144,128]{4,3,2,1,0:T(8,128)(2,1)S(1)}, u32[]{:S(2)}, u32[]{:S(2)}) collective-permute-start(bf16[3,2,2,144,128]{4,3,2,1,0:T(8,128)(2,1)S(1)} %collective-permute-done.4), channel_id=1, source_target_pairs={{0,2},{2,4},{4,6},{6,7},{7,5},{5,3},{3,1},{1,0},{8,10},{10,12},{12... | collective-permute-start | bytes 1327112 | tf_op jit(solution)/shard_map/ppermute | solution.py:129
  41.4 3.3 %collective-permute-start.18 = (bf16[3,8,144,128]{3,2,1,0:T(8,128)(2,1)S(1)}, bf16[3,8,144,128]{3,2,1,0:T(8,128)(2,1)S(1)}, u32[]{:S(2)}, u32[]{:S(2)}) collective-permute-start(bf16[3,8,144,128]{3,2,1,0:T(8,128)(2,1)S(1)} %pad_maximum_fusion.1), channel_id=1, source_target_pairs={{0,16},{1,17},{10,26},{11,27},{20,4},{21,5},{30,14},{31,15}} | collective-permute-start | bytes 2654216 | tf_op jit(solution)/shard_map/ppermute | solution.py:105
  47.1 2.4 %collective-permute-done.6 = bf16[3,2,2,144,128]{4,3,2,1,0:T(8,128)(2,1)S(1)} collective-permute-done((bf16[3,2,2,144,128]{4,3,2,1,0:T(8,128)(2,1)S(1)}, bf16[3,2,2,144,128]{4,3,2,1,0:T(8,128)(2,1)S(1)}, u32[]{:S(2)}, u32[]{:S(2)}) %collective-permute-start.6) | collective-permute-done | bytes 442400 | tf_op jit(solution)/shard_map/ppermute | solution.py:129
  49.5 1.4 %collective-permute-start.8 = (bf16[3,2,2,144,128]{4,3,2,1,0:T(8,128)(2,1)S(1)}, bf16[3,2,2,144,128]{4,3,2,1,0:T(8,128)(2,1)S(1)}, u32[]{:S(2)}, u32[]{:S(2)}) collective-permute-start(bf16[3,2,2,144,128]{4,3,2,1,0:T(8,128)(2,1)S(1)} %collective-permute-done.6), channel_id=1, source_target_pairs={{0,2},{2,4},{4,6},{6,7},{7,5},{5,3},{3,1},{1,0},{8,10},{10,12},{12... | collective-permute-start | bytes 1327112 | tf_op jit(solution)/shard_map/ppermute | solution.py:129
  53.4 6.5 %collective-permute-done.8 = bf16[3,2,2,144,128]{4,3,2,1,0:T(8,128)(2,1)S(1)} collective-permute-done((bf16[3,2,2,144,128]{4,3,2,1,0:T(8,128)(2,1)S(1)}, bf16[3,2,2,144,128]{4,3,2,1,0:T(8,128)(2,1)S(1)}, u32[]{:S(2)}, u32[]{:S(2)}) %collective-permute-start.8) | collective-permute-done | bytes 442400 | tf_op jit(solution)/shard_map/ppermute | solution.py:129
  59.9 1.4 %collective-permute-start.10 = (bf16[3,2,2,144,128]{4,3,2,1,0:T(8,128)(2,1)S(1)}, bf16[3,2,2,144,128]{4,3,2,1,0:T(8,128)(2,1)S(1)}, u32[]{:S(2)}, u32[]{:S(2)}) collective-permute-start(bf16[3,2,2,144,128]{4,3,2,1,0:T(8,128)(2,1)S(1)} %collective-permute-done.8), channel_id=1, source_target_pairs={{0,2},{2,4},{4,6},{6,7},{7,5},{5,3},{3,1},{1,0},{8,10},{10,12},{12... | collective-permute-start | bytes 1327112 | tf_op jit(solution)/shard_map/ppermute | solution.py:129
  64.7 1.3 %collective-permute-start.17 = (bf16[3,8,144,128]{3,2,1,0:T(8,128)(2,1)S(1)}, bf16[3,8,144,128]{3,2,1,0:T(8,128)(2,1)S(1)}, u32[]{:S(2)}, u32[]{:S(2)}) collective-permute-start(bf16[3,8,144,128]{3,2,1,0:T(8,128)(2,1)S(1)} %pad_maximum_fusion.1), channel_id=1, source_target_pairs={{0,8},{1,9},{10,2},{11,3},{20,28},{21,29},{30,22},{31,23}} | collective-permute-start | bytes 2654216 | tf_op jit(solution)/shard_map/ppermute | solution.py:105
  66.1 2.3 %collective-permute-start.21 = (bf16[3,8,144,128]{3,2,1,0:T(8,128)(2,1)}, bf16[3,8,144,128]{3,2,1,0:T(8,128)(2,1)}, u32[]{:S(2)}, u32[]{:S(2)}) collective-permute-start(bf16[3,8,144,128]{3,2,1,0:T(8,128)(2,1)} %pad_maximum_fusion.2), channel_id=1, source_target_pairs={{0,16},{1,17},{10,26},{11,27},{20,4},{21,5},{30,14},{31,15}} | collective-permute-start | bytes 2654216 | tf_op jit(solution)/shard_map/ppermute | solution.py:105
  69.5 1.4 %collective-permute-done.10 = bf16[3,2,2,144,128]{4,3,2,1,0:T(8,128)(2,1)S(1)} collective-permute-done((bf16[3,2,2,144,128]{4,3,2,1,0:T(8,128)(2,1)S(1)}, bf16[3,2,2,144,128]{4,3,2,1,0:T(8,128)(2,1)S(1)}, u32[]{:S(2)}, u32[]{:S(2)}) %collective-permute-start.10) | collective-permute-done | bytes 442400 | tf_op jit(solution)/shard_map/ppermute | solution.py:129
  70.9 2.0 %collective-permute-start.13 = (bf16[3,2,2,144,128]{4,3,2,1,0:T(8,128)(2,1)S(1)}, bf16[3,2,2,144,128]{4,3,2,1,0:T(8,128)(2,1)S(1)}, u32[]{:S(2)}, u32[]{:S(2)}) collective-permute-start(bf16[3,2,2,144,128]{4,3,2,1,0:T(8,128)(2,1)S(1)} %collective-permute-done.11), channel_id=1, source_target_pairs={{2,0},{4,2},{6,4},{7,6},{5,7},{3,5},{1,3},{0,1},{10,8},{12,10},{14... | collective-permute-start | bytes 1327112 | tf_op jit(solution)/shard_map/ppermute | solution.py:130
  75.6 5.6 %collective-permute-done.12 = bf16[3,2,2,144,128]{4,3,2,1,0:T(8,128)(2,1)S(1)} collective-permute-done((bf16[3,2,2,144,128]{4,3,2,1,0:T(8,128)(2,1)S(1)}, bf16[3,2,2,144,128]{4,3,2,1,0:T(8,128)(2,1)S(1)}, u32[]{:S(2)}, u32[]{:S(2)}) %collective-permute-start.12) | collective-permute-done | bytes 442400 | tf_op jit(solution)/shard_map/ppermute | solution.py:129
  81.3 3.2 %collective-permute-start.20 = (bf16[3,8,144,128]{3,2,1,0:T(8,128)(2,1)}, bf16[3,8,144,128]{3,2,1,0:T(8,128)(2,1)}, u32[]{:S(2)}, u32[]{:S(2)}) collective-permute-start(bf16[3,8,144,128]{3,2,1,0:T(8,128)(2,1)} %pad_maximum_fusion.2), channel_id=1, source_target_pairs={{0,8},{1,9},{10,2},{11,3},{20,28},{21,29},{30,22},{31,23}} | collective-permute-start | bytes 2654216 | tf_op jit(solution)/shard_map/ppermute | solution.py:105
  84.5 2.1 %collective-permute-start.24 = (bf16[3,4,144,128]{3,2,1,0:T(8,128)(2,1)}, bf16[3,4,144,128]{3,2,1,0:T(8,128)(2,1)}, u32[]{:S(2)}, u32[]{:S(2)}) collective-permute-start(bf16[3,4,144,128]{3,2,1,0:T(8,128)(2,1)} %pad_maximum_fusion.3), channel_id=1, source_target_pairs={{0,16},{1,17},{10,26},{11,27},{20,4},{21,5},{30,14},{31,15}} | collective-permute-start | bytes 1327112 | tf_op jit(solution)/shard_map/ppermute | solution.py:105
  86.6 1.6 %collective-permute-start.22 = (bf16[3,8,144,128]{3,2,1,0:T(8,128)(2,1)}, bf16[3,8,144,128]{3,2,1,0:T(8,128)(2,1)}, u32[]{:S(2)}, u32[]{:S(2)}) collective-permute-start(bf16[3,8,144,128]{3,2,1,0:T(8,128)(2,1)} %collective-permute-done.21), channel_id=1, source_target_pairs={{16,24},{17,25},{26,18},{27,19},{4,12},{5,13},{14,6},{15,7}} | collective-permute-start | bytes 2654216 | tf_op jit(solution)/shard_map/ppermute | solution.py:105
  89.9 2.1 %collective-permute-start.23 = (bf16[3,4,144,128]{3,2,1,0:T(8,128)(2,1)}, bf16[3,4,144,128]{3,2,1,0:T(8,128)(2,1)}, u32[]{:S(2)}, u32[]{:S(2)}) collective-permute-start(bf16[3,4,144,128]{3,2,1,0:T(8,128)(2,1)} %pad_maximum_fusion.3), channel_id=1, source_target_pairs={{0,8},{1,9},{10,2},{11,3},{20,28},{21,29},{30,22},{31,23}} | collective-permute-start | bytes 1327112 | tf_op jit(solution)/shard_map/ppermute | solution.py:105
  92.0 5.1 %collective-permute-start.27 = (bf16[3,4,144,128]{3,2,1,0:T(8,128)(2,1)}, bf16[3,4,144,128]{3,2,1,0:T(8,128)(2,1)}, u32[]{:S(2)}, u32[]{:S(2)}) collective-permute-start(bf16[3,4,144,128]{3,2,1,0:T(8,128)(2,1)} %pad_maximum_fusion.4), channel_id=1, source_target_pairs={{0,16},{1,17},{10,26},{11,27},{20,4},{21,5},{30,14},{31,15}} | collective-permute-start | bytes 1327112 | tf_op jit(solution)/shard_map/ppermute | solution.py:105
  97.1 1.4 %collective-permute-start.25 = (bf16[3,4,144,128]{3,2,1,0:T(8,128)(2,1)}, bf16[3,4,144,128]{3,2,1,0:T(8,128)(2,1)}, u32[]{:S(2)}, u32[]{:S(2)}) collective-permute-start(bf16[3,4,144,128]{3,2,1,0:T(8,128)(2,1)} %collective-permute-done.24), channel_id=1, source_target_pairs={{16,24},{17,25},{26,18},{27,19},{4,12},{5,13},{14,6},{15,7}} | collective-permute-start | bytes 1327112 | tf_op jit(solution)/shard_map/ppermute | solution.py:105
  99.9 1.7 %slice.19 = bf16[96,2,1,1]{3,2,1,0:T(2,128)(2,1)} slice(bf16[96,2,144,128]{3,2,1,0:T(8,128)(2,1)} %bitcast.44), slice={[0:96], [0:2], [131:132], [0:1]} | slice | bytes 768 | tf_op jit(solution)/shard_map/slice | solution.py:150
  102.6 1.3 %collective-permute-start.26 = (bf16[3,4,144,128]{3,2,1,0:T(8,128)(2,1)}, bf16[3,4,144,128]{3,2,1,0:T(8,128)(2,1)S(1)}, u32[]{:S(2)}, u32[]{:S(2)}) collective-permute-start(bf16[3,4,144,128]{3,2,1,0:T(8,128)(2,1)} %pad_maximum_fusion.4), channel_id=1, source_target_pairs={{0,8},{1,9},{10,2},{11,3},{20,28},{21,29},{30,22},{31,23}} | collective-permute-start | bytes 1327112 | tf_op jit(solution)/shard_map/ppermute | solution.py:105
  104.7 1.9 %select_dynamic-update-slice_fusion = bf16[3,32,144,128]{3,2,1,0:T(8,128)(2,1)S(1)} fusion(bf16[3,32,144,128]{3,2,1,0:T(8,128)(2,1)S(1)} %select_dynamic-update-slice_fusion.1, bf16[3,8,144,128]{3,2,1,0:T(8,128)(2,1)} %collective-permute-done.20, bf16[3,8,144,128]{3,2,1,0:T(8,128)(2,1)} %collective-permute-done.21, ...), kind=kLoop, calls=%fused_computation.4 | loop fusion | flops 4866048 | bytes 4423683
  106.6 1.5 %select_dynamic-update-slice_fusion.4 = bf16[3,32,144,128]{3,2,1,0:T(8,128)(2,1)S(1)} fusion(bf16[3,32,144,128]{3,2,1,0:T(8,128)(2,1)S(1)} %select_dynamic-update-slice_fusion, bf16[3,4,144,128]{3,2,1,0:T(8,128)(2,1)} %collective-permute-done.23, bf16[3,4,144,128]{3,2,1,0:T(8,128)(2,1)} %collective-permute-done.24, ...), kind=kLoop, calls=%fused_computation.10 | loop fusion | flops 1548288 | bytes 2211843
  108.1 1.3 %select_dynamic-update-slice_fusion.3 = bf16[3,32,144,128]{3,2,1,0:T(8,128)(2,1)S(1)} fusion(bf16[3,32,144,128]{3,2,1,0:T(8,128)(2,1)S(1)} %select_dynamic-update-slice_fusion.4, bf16[3,4,144,128]{3,2,1,0:T(8,128)(2,1)S(1)} %collective-permute-done.26, bf16[3,4,144,128]{3,2,1,0:T(8,128)(2,1)} %collective-permute-done.27, ...), kind=kLoop, calls=%fused_computation.9 | loop fusion | flops 1548288 | bytes 2211843 | tf_op jit(solution)/shard_map/concatenate | solution.py:145
  111.9 10.8 %shard_map.37 = f32[2048,1024]{1,0:T(8,128)} custom-call(s32[288]{0:T(512)S(1)} %min.12.offs_ref, bf16[96,2,144,128]{3,2,1,0:T(8,128)(2,1)} %bitcast.45, bf16[96,144,128]{2,1,0:T(8,128)(2,1)S(1)} %bitcast.43), custom_call_target="tpu_custom_call" | custom-call | flops 805306368 | bytes 17825792 | tf_op jit(solution)/shard_map/pallas_call | solution.py:40
  (99 shorter events, 26.6 us)
Async XLA Ops:
  4.2 13.2 %collective-permute-start = (bf16[3,2,2,144,128]{4,3,2,1,0:T(8,128)(2,1)S(1)}, bf16[3,2,2,144,128]{4,3,2,1,0:T(8,128)(2,1)S(1)}, u32[]{:S(2)}, u32[]{:S(2)}) collective-permute-start(bf16[3,2,2,144,128]{4,3,2,1,0:T(8,128)(2,1)S(1)} %get-tuple-element.5), channel_id=1, source_target_pairs={{0,2},{2,4},{4,6},{6,7},{7,5},{5,3},{3,1},{1,0},{8,10},{10,12},{12... | collective-permute-start | bytes 1327112 | tf_op jit(solution)/shard_map/ppermute | solution.py:129
  7.3 11.9 %collective-permute-start.1 = (bf16[3,2,2,144,128]{4,3,2,1,0:T(8,128)(2,1)S(1)}, bf16[3,2,2,144,128]{4,3,2,1,0:T(8,128)(2,1)S(1)}, u32[]{:S(2)}, u32[]{:S(2)}) collective-permute-start(bf16[3,2,2,144,128]{4,3,2,1,0:T(8,128)(2,1)S(1)} %get-tuple-element.6), channel_id=1, source_target_pairs={{2,0},{4,2},{6,4},{7,6},{5,7},{3,5},{1,3},{0,1},{10,8},{12,10},{14... | collective-permute-start | bytes 1327112 | tf_op jit(solution)/shard_map/ppermute | solution.py:130
  17.4 11.4 %collective-permute-start.2 = (bf16[3,2,2,144,128]{4,3,2,1,0:T(8,128)(2,1)S(1)}, bf16[3,2,2,144,128]{4,3,2,1,0:T(8,128)(2,1)S(1)}, u32[]{:S(2)}, u32[]{:S(2)}) collective-permute-start(bf16[3,2,2,144,128]{4,3,2,1,0:T(8,128)(2,1)S(1)} %collective-permute-done), channel_id=1, source_target_pairs={{0,2},{2,4},{4,6},{6,7},{7,5},{5,3},{3,1},{1,0},{8,10},{10,12},{12... | collective-permute-start | bytes 1327112 | tf_op jit(solution)/shard_map/ppermute | solution.py:129
  19.2 11.0 %collective-permute-start.3 = (bf16[3,2,2,144,128]{4,3,2,1,0:T(8,128)(2,1)S(1)}, bf16[3,2,2,144,128]{4,3,2,1,0:T(8,128)(2,1)S(1)}, u32[]{:S(2)}, u32[]{:S(2)}) collective-permute-start(bf16[3,2,2,144,128]{4,3,2,1,0:T(8,128)(2,1)S(1)} %collective-permute-done.1), channel_id=1, source_target_pairs={{2,0},{4,2},{6,4},{7,6},{5,7},{3,5},{1,3},{0,1},{10,8},{12,10},{14... | collective-permute-start | bytes 1327112 | tf_op jit(solution)/shard_map/ppermute | solution.py:130
  19.6 25.0 %collective-permute-start.15 = (bf16[3,8,144,128]{3,2,1,0:T(8,128)(2,1)S(1)}, bf16[3,8,144,128]{3,2,1,0:T(8,128)(2,1)S(1)}, u32[]{:S(2)}, u32[]{:S(2)}) collective-permute-start(bf16[3,8,144,128]{3,2,1,0:T(8,128)(2,1)S(1)} %pad_maximum_fusion), channel_id=1, source_target_pairs={{0,16},{1,17},{10,26},{11,27},{20,4},{21,5},{30,14},{31,15}} | collective-permute-start | bytes 2654216 | tf_op jit(solution)/shard_map/ppermute | solution.py:105
  23.3 41.4 %collective-permute-start.14 = (bf16[3,8,144,128]{3,2,1,0:T(8,128)(2,1)S(1)}, bf16[3,8,144,128]{3,2,1,0:T(8,128)(2,1)S(1)}, u32[]{:S(2)}, u32[]{:S(2)}) collective-permute-start(bf16[3,8,144,128]{3,2,1,0:T(8,128)(2,1)S(1)} %pad_maximum_fusion), channel_id=1, source_target_pairs={{0,8},{1,9},{10,2},{11,3},{20,28},{21,29},{30,22},{31,23}} | collective-permute-start | bytes 2654216 | tf_op jit(solution)/shard_map/ppermute | solution.py:105
  28.8 10.4 %collective-permute-start.4 = (bf16[3,2,2,144,128]{4,3,2,1,0:T(8,128)(2,1)S(1)}, bf16[3,2,2,144,128]{4,3,2,1,0:T(8,128)(2,1)S(1)}, u32[]{:S(2)}, u32[]{:S(2)}) collective-permute-start(bf16[3,2,2,144,128]{4,3,2,1,0:T(8,128)(2,1)S(1)} %collective-permute-done.2), channel_id=1, source_target_pairs={{0,2},{2,4},{4,6},{6,7},{7,5},{5,3},{3,1},{1,0},{8,10},{10,12},{12... | collective-permute-start | bytes 1327112 | tf_op jit(solution)/shard_map/ppermute | solution.py:129
  30.2 10.3 %collective-permute-start.5 = (bf16[3,2,2,144,128]{4,3,2,1,0:T(8,128)(2,1)S(1)}, bf16[3,2,2,144,128]{4,3,2,1,0:T(8,128)(2,1)S(1)}, u32[]{:S(2)}, u32[]{:S(2)}) collective-permute-start(bf16[3,2,2,144,128]{4,3,2,1,0:T(8,128)(2,1)S(1)} %collective-permute-done.3), channel_id=1, source_target_pairs={{2,0},{4,2},{6,4},{7,6},{5,7},{3,5},{1,3},{0,1},{10,8},{12,10},{14... | collective-permute-start | bytes 1327112 | tf_op jit(solution)/shard_map/ppermute | solution.py:130
  39.2 10.3 %collective-permute-start.6 = (bf16[3,2,2,144,128]{4,3,2,1,0:T(8,128)(2,1)S(1)}, bf16[3,2,2,144,128]{4,3,2,1,0:T(8,128)(2,1)S(1)}, u32[]{:S(2)}, u32[]{:S(2)}) collective-permute-start(bf16[3,2,2,144,128]{4,3,2,1,0:T(8,128)(2,1)S(1)} %collective-permute-done.4), channel_id=1, source_target_pairs={{0,2},{2,4},{4,6},{6,7},{7,5},{5,3},{3,1},{1,0},{8,10},{10,12},{12... | collective-permute-start | bytes 1327112 | tf_op jit(solution)/shard_map/ppermute | solution.py:129
  40.6 10.3 %collective-permute-start.7 = (bf16[3,2,2,144,128]{4,3,2,1,0:T(8,128)(2,1)S(1)}, bf16[3,2,2,144,128]{4,3,2,1,0:T(8,128)(2,1)S(1)}, u32[]{:S(2)}, u32[]{:S(2)}) collective-permute-start(bf16[3,2,2,144,128]{4,3,2,1,0:T(8,128)(2,1)S(1)} %collective-permute-done.5), channel_id=1, source_target_pairs={{2,0},{4,2},{6,4},{7,6},{5,7},{3,5},{1,3},{0,1},{10,8},{12,10},{14... | collective-permute-start | bytes 1327112 | tf_op jit(solution)/shard_map/ppermute | solution.py:130
  41.4 26.9 %collective-permute-start.18 = (bf16[3,8,144,128]{3,2,1,0:T(8,128)(2,1)S(1)}, bf16[3,8,144,128]{3,2,1,0:T(8,128)(2,1)S(1)}, u32[]{:S(2)}, u32[]{:S(2)}) collective-permute-start(bf16[3,8,144,128]{3,2,1,0:T(8,128)(2,1)S(1)} %pad_maximum_fusion.1), channel_id=1, source_target_pairs={{0,16},{1,17},{10,26},{11,27},{20,4},{21,5},{30,14},{31,15}} | collective-permute-start | bytes 2654216 | tf_op jit(solution)/shard_map/ppermute | solution.py:105
  44.7 21.4 %collective-permute-start.16 = (bf16[3,8,144,128]{3,2,1,0:T(8,128)(2,1)S(1)}, bf16[3,8,144,128]{3,2,1,0:T(8,128)(2,1)S(1)}, u32[]{:S(2)}, u32[]{:S(2)}) collective-permute-start(bf16[3,8,144,128]{3,2,1,0:T(8,128)(2,1)S(1)} %collective-permute-done.15), channel_id=1, source_target_pairs={{16,24},{17,25},{26,18},{27,19},{4,12},{5,13},{14,6},{15,7}} | collective-permute-start | bytes 2654216 | tf_op jit(solution)/shard_map/ppermute | solution.py:105
  49.5 10.3 %collective-permute-start.8 = (bf16[3,2,2,144,128]{4,3,2,1,0:T(8,128)(2,1)S(1)}, bf16[3,2,2,144,128]{4,3,2,1,0:T(8,128)(2,1)S(1)}, u32[]{:S(2)}, u32[]{:S(2)}) collective-permute-start(bf16[3,2,2,144,128]{4,3,2,1,0:T(8,128)(2,1)S(1)} %collective-permute-done.6), channel_id=1, source_target_pairs={{0,2},{2,4},{4,6},{6,7},{7,5},{5,3},{3,1},{1,0},{8,10},{10,12},{12... | collective-permute-start | bytes 1327112 | tf_op jit(solution)/shard_map/ppermute | solution.py:129
  50.9 10.3 %collective-permute-start.9 = (bf16[3,2,2,144,128]{4,3,2,1,0:T(8,128)(2,1)S(1)}, bf16[3,2,2,144,128]{4,3,2,1,0:T(8,128)(2,1)S(1)}, u32[]{:S(2)}, u32[]{:S(2)}) collective-permute-start(bf16[3,2,2,144,128]{4,3,2,1,0:T(8,128)(2,1)S(1)} %collective-permute-done.7), channel_id=1, source_target_pairs={{2,0},{4,2},{6,4},{7,6},{5,7},{3,5},{1,3},{0,1},{10,8},{12,10},{14... | collective-permute-start | bytes 1327112 | tf_op jit(solution)/shard_map/ppermute | solution.py:130
  51.6 16.8 %copy-start.4 = (bf16[3,2,144,128]{3,2,1,0:T(8,128)(2,1)}, bf16[3,2,144,128]{3,2,1,0:T(8,128)(2,1)S(1)}, u32[]{:S(2)}) copy-start(bf16[3,2,144,128]{3,2,1,0:T(8,128)(2,1)S(1)} %dynamic-slice_bitcast_fusion.7) | copy-start | bytes 663556
  59.9 11.1 %collective-permute-start.10 = (bf16[3,2,2,144,128]{4,3,2,1,0:T(8,128)(2,1)S(1)}, bf16[3,2,2,144,128]{4,3,2,1,0:T(8,128)(2,1)S(1)}, u32[]{:S(2)}, u32[]{:S(2)}) collective-permute-start(bf16[3,2,2,144,128]{4,3,2,1,0:T(8,128)(2,1)S(1)} %collective-permute-done.8), channel_id=1, source_target_pairs={{0,2},{2,4},{4,6},{6,7},{7,5},{5,3},{3,1},{1,0},{8,10},{10,12},{12... | collective-permute-start | bytes 1327112 | tf_op jit(solution)/shard_map/ppermute | solution.py:129
  61.2 9.7 %collective-permute-start.11 = (bf16[3,2,2,144,128]{4,3,2,1,0:T(8,128)(2,1)S(1)}, bf16[3,2,2,144,128]{4,3,2,1,0:T(8,128)(2,1)S(1)}, u32[]{:S(2)}, u32[]{:S(2)}) collective-permute-start(bf16[3,2,2,144,128]{4,3,2,1,0:T(8,128)(2,1)S(1)} %collective-permute-done.9), channel_id=1, source_target_pairs={{2,0},{4,2},{6,4},{7,6},{5,7},{3,5},{1,3},{0,1},{10,8},{12,10},{14... | collective-permute-start | bytes 1327112 | tf_op jit(solution)/shard_map/ppermute | solution.py:130
  64.7 25.2 %collective-permute-start.17 = (bf16[3,8,144,128]{3,2,1,0:T(8,128)(2,1)S(1)}, bf16[3,8,144,128]{3,2,1,0:T(8,128)(2,1)S(1)}, u32[]{:S(2)}, u32[]{:S(2)}) collective-permute-start(bf16[3,8,144,128]{3,2,1,0:T(8,128)(2,1)S(1)} %pad_maximum_fusion.1), channel_id=1, source_target_pairs={{0,8},{1,9},{10,2},{11,3},{20,28},{21,29},{30,22},{31,23}} | collective-permute-start | bytes 2654216 | tf_op jit(solution)/shard_map/ppermute | solution.py:105
  66.1 20.5 %collective-permute-start.21 = (bf16[3,8,144,128]{3,2,1,0:T(8,128)(2,1)}, bf16[3,8,144,128]{3,2,1,0:T(8,128)(2,1)}, u32[]{:S(2)}, u32[]{:S(2)}) collective-permute-start(bf16[3,8,144,128]{3,2,1,0:T(8,128)(2,1)} %pad_maximum_fusion.2), channel_id=1, source_target_pairs={{0,16},{1,17},{10,26},{11,27},{20,4},{21,5},{30,14},{31,15}} | collective-permute-start | bytes 2654216 | tf_op jit(solution)/shard_map/ppermute | solution.py:105
  68.3 28.7 %collective-permute-start.19 = (bf16[3,8,144,128]{3,2,1,0:T(8,128)(2,1)S(1)}, bf16[3,8,144,128]{3,2,1,0:T(8,128)(2,1)S(1)}, u32[]{:S(2)}, u32[]{:S(2)}) collective-permute-start(bf16[3,8,144,128]{3,2,1,0:T(8,128)(2,1)S(1)} %collective-permute-done.18), channel_id=1, source_target_pairs={{16,24},{17,25},{26,18},{27,19},{4,12},{5,13},{14,6},{15,7}} | collective-permute-start | bytes 2654216 | tf_op jit(solution)/shard_map/ppermute | solution.py:105
  70.9 10.3 %collective-permute-start.12 = (bf16[3,2,2,144,128]{4,3,2,1,0:T(8,128)(2,1)S(1)}, bf16[3,2,2,144,128]{4,3,2,1,0:T(8,128)(2,1)S(1)}, u32[]{:S(2)}, u32[]{:S(2)}) collective-permute-start(bf16[3,2,2,144,128]{4,3,2,1,0:T(8,128)(2,1)S(1)} %collective-permute-done.10), channel_id=1, source_target_pairs={{0,2},{2,4},{4,6},{6,7},{7,5},{5,3},{3,1},{1,0},{8,10},{10,12},{12... | collective-permute-start | bytes 1327112 | tf_op jit(solution)/shard_map/ppermute | solution.py:129
  70.9 13.6 %collective-permute-start.13 = (bf16[3,2,2,144,128]{4,3,2,1,0:T(8,128)(2,1)S(1)}, bf16[3,2,2,144,128]{4,3,2,1,0:T(8,128)(2,1)S(1)}, u32[]{:S(2)}, u32[]{:S(2)}) collective-permute-start(bf16[3,2,2,144,128]{4,3,2,1,0:T(8,128)(2,1)S(1)} %collective-permute-done.11), channel_id=1, source_target_pairs={{2,0},{4,2},{6,4},{7,6},{5,7},{3,5},{1,3},{0,1},{10,8},{12,10},{14... | collective-permute-start | bytes 1327112 | tf_op jit(solution)/shard_map/ppermute | solution.py:130
  73.0 24.1 %copy-start = (bf16[3,2,144,128]{3,2,1,0:T(8,128)(2,1)}, bf16[3,2,144,128]{3,2,1,0:T(8,128)(2,1)S(1)}, u32[]{:S(2)}) copy-start(bf16[3,2,144,128]{3,2,1,0:T(8,128)(2,1)S(1)} %dynamic-slice_bitcast_fusion.3) | copy-start | bytes 663556
  73.0 24.1 %copy-start.1 = (bf16[3,2,144,128]{3,2,1,0:T(8,128)(2,1)}, bf16[3,2,144,128]{3,2,1,0:T(8,128)(2,1)S(1)}, u32[]{:S(2)}) copy-start(bf16[3,2,144,128]{3,2,1,0:T(8,128)(2,1)S(1)} %dynamic-slice_bitcast_fusion.2) | copy-start | bytes 663556
  81.3 21.4 %collective-permute-start.20 = (bf16[3,8,144,128]{3,2,1,0:T(8,128)(2,1)}, bf16[3,8,144,128]{3,2,1,0:T(8,128)(2,1)}, u32[]{:S(2)}, u32[]{:S(2)}) collective-permute-start(bf16[3,8,144,128]{3,2,1,0:T(8,128)(2,1)} %pad_maximum_fusion.2), channel_id=1, source_target_pairs={{0,8},{1,9},{10,2},{11,3},{20,28},{21,29},{30,22},{31,23}} | collective-permute-start | bytes 2654216 | tf_op jit(solution)/shard_map/ppermute | solution.py:105
  84.5 7.5 %collective-permute-start.24 = (bf16[3,4,144,128]{3,2,1,0:T(8,128)(2,1)}, bf16[3,4,144,128]{3,2,1,0:T(8,128)(2,1)}, u32[]{:S(2)}, u32[]{:S(2)}) collective-permute-start(bf16[3,4,144,128]{3,2,1,0:T(8,128)(2,1)} %pad_maximum_fusion.3), channel_id=1, source_target_pairs={{0,16},{1,17},{10,26},{11,27},{20,4},{21,5},{30,14},{31,15}} | collective-permute-start | bytes 1327112 | tf_op jit(solution)/shard_map/ppermute | solution.py:105
  86.6 18.1 %collective-permute-start.22 = (bf16[3,8,144,128]{3,2,1,0:T(8,128)(2,1)}, bf16[3,8,144,128]{3,2,1,0:T(8,128)(2,1)}, u32[]{:S(2)}, u32[]{:S(2)}) collective-permute-start(bf16[3,8,144,128]{3,2,1,0:T(8,128)(2,1)} %collective-permute-done.21), channel_id=1, source_target_pairs={{16,24},{17,25},{26,18},{27,19},{4,12},{5,13},{14,6},{15,7}} | collective-permute-start | bytes 2654216 | tf_op jit(solution)/shard_map/ppermute | solution.py:105
  89.9 16.7 %collective-permute-start.23 = (bf16[3,4,144,128]{3,2,1,0:T(8,128)(2,1)}, bf16[3,4,144,128]{3,2,1,0:T(8,128)(2,1)}, u32[]{:S(2)}, u32[]{:S(2)}) collective-permute-start(bf16[3,4,144,128]{3,2,1,0:T(8,128)(2,1)} %pad_maximum_fusion.3), channel_id=1, source_target_pairs={{0,8},{1,9},{10,2},{11,3},{20,28},{21,29},{30,22},{31,23}} | collective-permute-start | bytes 1327112 | tf_op jit(solution)/shard_map/ppermute | solution.py:105
  92.0 12.0 %collective-permute-start.27 = (bf16[3,4,144,128]{3,2,1,0:T(8,128)(2,1)}, bf16[3,4,144,128]{3,2,1,0:T(8,128)(2,1)}, u32[]{:S(2)}, u32[]{:S(2)}) collective-permute-start(bf16[3,4,144,128]{3,2,1,0:T(8,128)(2,1)} %pad_maximum_fusion.4), channel_id=1, source_target_pairs={{0,16},{1,17},{10,26},{11,27},{20,4},{21,5},{30,14},{31,15}} | collective-permute-start | bytes 1327112 | tf_op jit(solution)/shard_map/ppermute | solution.py:105
  97.1 9.5 %collective-permute-start.25 = (bf16[3,4,144,128]{3,2,1,0:T(8,128)(2,1)}, bf16[3,4,144,128]{3,2,1,0:T(8,128)(2,1)}, u32[]{:S(2)}, u32[]{:S(2)}) collective-permute-start(bf16[3,4,144,128]{3,2,1,0:T(8,128)(2,1)} %collective-permute-done.24), channel_id=1, source_target_pairs={{16,24},{17,25},{26,18},{27,19},{4,12},{5,13},{14,6},{15,7}} | collective-permute-start | bytes 1327112 | tf_op jit(solution)/shard_map/ppermute | solution.py:105
  102.6 5.5 %collective-permute-start.26 = (bf16[3,4,144,128]{3,2,1,0:T(8,128)(2,1)}, bf16[3,4,144,128]{3,2,1,0:T(8,128)(2,1)S(1)}, u32[]{:S(2)}, u32[]{:S(2)}) collective-permute-start(bf16[3,4,144,128]{3,2,1,0:T(8,128)(2,1)} %pad_maximum_fusion.4), channel_id=1, source_target_pairs={{0,8},{1,9},{10,2},{11,3},{20,28},{21,29},{30,22},{31,23}} | collective-permute-start | bytes 1327112 | tf_op jit(solution)/shard_map/ppermute | solution.py:105
  104.0 4.1 %collective-permute-start.28 = (bf16[3,4,144,128]{3,2,1,0:T(8,128)(2,1)}, bf16[3,4,144,128]{3,2,1,0:T(8,128)(2,1)S(1)}, u32[]{:S(2)}, u32[]{:S(2)}) collective-permute-start(bf16[3,4,144,128]{3,2,1,0:T(8,128)(2,1)} %collective-permute-done.27), channel_id=1, source_target_pairs={{16,24},{17,25},{26,18},{27,19},{4,12},{5,13},{14,6},{15,7}} | collective-permute-start | bytes 1327112 | tf_op jit(solution)/shard_map/ppermute | solution.py:105
  (5 other events, 47.3 us)

commit v21 on v20

--- a/solution.py
+++ b/solution.py
@@ -106,16 +106,18 @@
 
     def last_fan(own):
         heads = [cc // local_slots for cc in range(ncol)]
-        to_partner = send(own, [(h, h ^ 1, cc) for cc, h in enumerate(heads)])
         to_d1 = None
         for j in range(1, nx):
             v = send(own, [(h, (h + 2 * j) % nrow, cc) for cc, h in enumerate(heads)])
             to_d1 = v if to_d1 is None else jnp.where(which // 2 == j, v, to_d1)
-        to_d2 = send(
-            to_d1,
-            [((h + 2 * j) % nrow, ((h + 2 * j) % nrow) ^ 1, cc) for cc, h in enumerate(heads) for j in range(1, nx)],
-        )
-        return jnp.where(is_s, own, jnp.where(is_p, to_partner, jnp.where(is_d1, to_d1, to_d2)))
+        second_pairs = [(h, h ^ 1, cc) for cc, h in enumerate(heads)]
+        second_pairs += [
+            ((h + 2 * j) % nrow, ((h + 2 * j) % nrow) ^ 1, cc)
+            for cc, h in enumerate(heads)
+            for j in range(1, nx)
+        ]
+        second = send(jnp.where(is_s, own, to_d1), second_pairs)
+        return jnp.where(is_s, own, jnp.where(is_d1, to_d1, second))
 
     def pick_slot(piece):
         return lax.dynamic_index_in_dim(piece, slot, axis=2, keepdims=False)

time: 124 us -> 132 us (1.065)
  waiting for transfers between devices: 35 us -> 41.6 us
  other arithmetic: 12.5 us -> 15.4 us
    ppermute x7, waiting for transfers between devices: 0.02 us -> 17.2 us  [local(): b = lax.ppermute(b, 'col', backward)]
    ppermute x7, waiting for transfers between devices: 35 us -> 24.1 us  [local(): a = lax.ppermute(a, 'col', forward)]
    select_n x0 -> x5, other arithmetic: none -> 4.75 us  [last_fan(): second = send(jnp.where(is_s, own, to_d1), second_pairs)]
    ppermute x7, starting transfers between devices: 10.5 us -> 7.97 us  [local(): a = lax.ppermute(a, 'col', forward)]
    concatenate x5, other arithmetic: 2.99 us -> 1.26 us  [local(): own = jnp.concatenate(pending, axis=1)]
    ppermute x15 -> x10, starting transfers between devices: 30.8 us -> 30.7 us  [send(): lax.ppermute(v, ('row', 'col'), [(a * ncol + cc, b * ncol + cc) for a, b,...]
    unnamed x29 -> x53, local copies, waits for them, and re-layouts: 11.2 us -> 11.2 us
  transfers between devices with their start and end apart: 29 -> 24, of which waited for: 7 -> 10; matrix products, arithmetic and copies ran while one was open for 18% -> 20% of each run, Pallas kernels for 0% -> 0%
where the time goes in v21:
time: 132 us; the launch traced here: 131 us
  starting transfers between devices  44.7 us (34%)
  waiting for transfers between devices  41.6 us (32%)
  local copies, waits for them, and re-layouts  17.9 us (14%)
  other arithmetic  15.4 us (12%)
  Pallas kernels  10.8 us (8%)
    ppermute x10, starting transfers between devices, send(): lax.ppermute(v, ('row', 'col'), [(a * ncol + cc, b * ncol + cc) for a, b,...  30.7 us
    ppermute x7, waiting for transfers between devices, local(): a = lax.ppermute(a, 'col', forward)  24.1 us
    ppermute x7, waiting for transfers between devices, local(): b = lax.ppermute(b, 'col', backward)  17.2 us
    unnamed x53, local copies, waits for them, and re-layouts  11.2 us
    pallas_call x1, Pallas kernels, gram_call(): pl.pallas_call(kernel, grid_spec=pltpu.PrefetchScalarGridSpec(num_scalar_...  10.8 us
    ppermute x7, starting transfers between devices, local(): a = lax.ppermute(a, 'col', forward)  7.97 us
    unnamed x5, other arithmetic  7.72 us
    ppermute x7, starting transfers between devices, local(): b = lax.ppermute(b, 'col', backward)  5.98 us
  transfers between devices with their start and end apart: 24, of which 10 were waited for; matrix products, arithmetic and copies ran while one was open for 20% of the time, Pallas kernels for 0%

profile of v21, /device:TPU:0, one launch (start us, length us, event | category | flops | bytes accessed | tf_op | source)
XLA Modules:
  0.0 130.8 jit_solution(999073645098660688)
XLA Ops:
  1.7 2.4 %constant_dynamic-update-slice_fusion.14 = (bf16[3,32,2,144,128]{4,3,2,1,0:T(8,128)(2,1)}, bf16[3,4,2,144,128]{4,3,2,1,0:T(8,128)(2,1)S(1)}) fusion(bf16[144]{0:T(256)(128)(2,1)S(1)} %pad.21.clone, bf16[3,4,2,1,128]{4,3,2,1,0:T(2,128)(2,1)S(1)} %broadcast_in_dim.7, bf16[3,4,2,3,128]{4,3,2,1,0:T(4,128)(2,1)S(1)} %broadcast_in_dim.6, ...), kind=kLoop, calls=%fused_computation.47 | loop fusion | flops 3538943 | bytes 2580768
  4.2 3.1 %collective-permute-start = (bf16[3,2,2,144,128]{4,3,2,1,0:T(8,128)(2,1)S(1)}, bf16[3,2,2,144,128]{4,3,2,1,0:T(8,128)(2,1)S(1)}, u32[]{:S(2)}, u32[]{:S(2)}) collective-permute-start(bf16[3,2,2,144,128]{4,3,2,1,0:T(8,128)(2,1)S(1)} %get-tuple-element.5), channel_id=1, source_target_pairs={{0,2},{2,4},{4,6},{6,7},{7,5},{5,3},{3,1},{1,0},{8,10},{10,12},{12... | collective-permute-start | bytes 1327112 | tf_op jit(solution)/shard_map/ppermute | solution.py:131
  7.3 10.1 %collective-permute-done = bf16[3,2,2,144,128]{4,3,2,1,0:T(8,128)(2,1)S(1)} collective-permute-done((bf16[3,2,2,144,128]{4,3,2,1,0:T(8,128)(2,1)S(1)}, bf16[3,2,2,144,128]{4,3,2,1,0:T(8,128)(2,1)S(1)}, u32[]{:S(2)}, u32[]{:S(2)}) %collective-permute-start) | collective-permute-done | bytes 442400 | tf_op jit(solution)/shard_map/ppermute | solution.py:131
  17.4 1.8 %collective-permute-start.2 = (bf16[3,2,2,144,128]{4,3,2,1,0:T(8,128)(2,1)S(1)}, bf16[3,2,2,144,128]{4,3,2,1,0:T(8,128)(2,1)S(1)}, u32[]{:S(2)}, u32[]{:S(2)}) collective-permute-start(bf16[3,2,2,144,128]{4,3,2,1,0:T(8,128)(2,1)S(1)} %collective-permute-done), channel_id=1, source_target_pairs={{0,2},{2,4},{4,6},{6,7},{7,5},{5,3},{3,1},{1,0},{8,10},{10,12},{12... | collective-permute-start | bytes 1327112 | tf_op jit(solution)/shard_map/ppermute | solution.py:131
  19.6 3.7 %collective-permute-start.14 = (bf16[3,8,144,128]{3,2,1,0:T(8,128)(2,1)S(1)}, bf16[3,8,144,128]{3,2,1,0:T(8,128)(2,1)S(1)}, u32[]{:S(2)}, u32[]{:S(2)}) collective-permute-start(bf16[3,8,144,128]{3,2,1,0:T(8,128)(2,1)S(1)} %pad_maximum_fusion), channel_id=1, source_target_pairs={{0,16},{1,17},{10,26},{11,27},{20,4},{21,5},{30,14},{31,15}} | collective-permute-start | bytes 2654216 | tf_op jit(solution)/shard_map/ppermute | solution.py:105
  25.0 3.7 %collective-permute-done.2 = bf16[3,2,2,144,128]{4,3,2,1,0:T(8,128)(2,1)S(1)} collective-permute-done((bf16[3,2,2,144,128]{4,3,2,1,0:T(8,128)(2,1)S(1)}, bf16[3,2,2,144,128]{4,3,2,1,0:T(8,128)(2,1)S(1)}, u32[]{:S(2)}, u32[]{:S(2)}) %collective-permute-start.2) | collective-permute-done | bytes 442400 | tf_op jit(solution)/shard_map/ppermute | solution.py:131
  28.7 1.5 %collective-permute-start.4 = (bf16[3,2,2,144,128]{4,3,2,1,0:T(8,128)(2,1)S(1)}, bf16[3,2,2,144,128]{4,3,2,1,0:T(8,128)(2,1)S(1)}, u32[]{:S(2)}, u32[]{:S(2)}) collective-permute-start(bf16[3,2,2,144,128]{4,3,2,1,0:T(8,128)(2,1)S(1)} %collective-permute-done.2), channel_id=1, source_target_pairs={{0,2},{2,4},{4,6},{6,7},{7,5},{5,3},{3,1},{1,0},{8,10},{10,12},{12... | collective-permute-start | bytes 1327112 | tf_op jit(solution)/shard_map/ppermute | solution.py:131
  32.6 6.6 %collective-permute-done.4 = bf16[3,2,2,144,128]{4,3,2,1,0:T(8,128)(2,1)S(1)} collective-permute-done((bf16[3,2,2,144,128]{4,3,2,1,0:T(8,128)(2,1)S(1)}, bf16[3,2,2,144,128]{4,3,2,1,0:T(8,128)(2,1)S(1)}, u32[]{:S(2)}, u32[]{:S(2)}) %collective-permute-start.4) | collective-permute-done | bytes 442400 | tf_op jit(solution)/shard_map/ppermute | solution.py:131
  40.2 3.5 %collective-permute-start.16 = (bf16[3,8,144,128]{3,2,1,0:T(8,128)(2,1)S(1)}, bf16[3,8,144,128]{3,2,1,0:T(8,128)(2,1)S(1)}, u32[]{:S(2)}, u32[]{:S(2)}) collective-permute-start(bf16[3,8,144,128]{3,2,1,0:T(8,128)(2,1)S(1)} %pad_maximum_fusion.1), channel_id=1, source_target_pairs={{0,16},{1,17},{10,26},{11,27},{20,4},{21,5},{30,14},{31,15}} | collective-permute-start | bytes 2654216 | tf_op jit(solution)/shard_map/ppermute | solution.py:105
  43.9 1.3 %collective-permute-start.15 = (bf16[3,8,144,128]{3,2,1,0:T(8,128)(2,1)S(1)}, bf16[3,8,144,128]{3,2,1,0:T(8,128)(2,1)S(1)}, u32[]{:S(2)}, u32[]{:S(2)}) collective-permute-start(bf16[3,8,144,128]{3,2,1,0:T(8,128)(2,1)S(1)} %broadcast_select_fusion.2), channel_id=1, source_target_pairs={{0,8},{1,9},{10,2},{11,3},{20,28},{21,29},{30,22},{31,23},{16,24},... | collective-permute-start | bytes 2654216 | tf_op jit(solution)/shard_map/ppermute | solution.py:105
  45.3 2.1 %collective-permute-start.7 = (bf16[3,2,2,144,128]{4,3,2,1,0:T(8,128)(2,1)S(1)}, bf16[3,2,2,144,128]{4,3,2,1,0:T(8,128)(2,1)S(1)}, u32[]{:S(2)}, u32[]{:S(2)}) collective-permute-start(bf16[3,2,2,144,128]{4,3,2,1,0:T(8,128)(2,1)S(1)} %collective-permute-done.5), channel_id=1, source_target_pairs={{2,0},{4,2},{6,4},{7,6},{5,7},{3,5},{1,3},{0,1},{10,8},{12,10},{14... | collective-permute-start | bytes 1327112 | tf_op jit(solution)/shard_map/ppermute | solution.py:132
  49.0 3.7 %collective-permute-done.6 = bf16[3,2,2,144,128]{4,3,2,1,0:T(8,128)(2,1)S(1)} collective-permute-done((bf16[3,2,2,144,128]{4,3,2,1,0:T(8,128)(2,1)S(1)}, bf16[3,2,2,144,128]{4,3,2,1,0:T(8,128)(2,1)S(1)}, u32[]{:S(2)}, u32[]{:S(2)}) %collective-permute-start.6) | collective-permute-done | bytes 442400 | tf_op jit(solution)/shard_map/ppermute | solution.py:131
  52.7 1.3 %collective-permute-start.8 = (bf16[3,2,2,144,128]{4,3,2,1,0:T(8,128)(2,1)S(1)}, bf16[3,2,2,144,128]{4,3,2,1,0:T(8,128)(2,1)S(1)}, u32[]{:S(2)}, u32[]{:S(2)}) collective-permute-start(bf16[3,2,2,144,128]{4,3,2,1,0:T(8,128)(2,1)S(1)} %collective-permute-done.6), channel_id=1, source_target_pairs={{0,2},{2,4},{4,6},{6,7},{7,5},{5,3},{3,1},{1,0},{8,10},{10,12},{12... | collective-permute-start | bytes 1327112 | tf_op jit(solution)/shard_map/ppermute | solution.py:131
  55.0 2.8 %collective-permute-done.7 = bf16[3,2,2,144,128]{4,3,2,1,0:T(8,128)(2,1)S(1)} collective-permute-done((bf16[3,2,2,144,128]{4,3,2,1,0:T(8,128)(2,1)S(1)}, bf16[3,2,2,144,128]{4,3,2,1,0:T(8,128)(2,1)S(1)}, u32[]{:S(2)}, u32[]{:S(2)}) %collective-permute-start.7) | collective-permute-done | bytes 442400 | tf_op jit(solution)/shard_map/ppermute | solution.py:132
  58.9 1.3 broadcast_select_fusion.1
  60.2 2.9 %collective-permute-start.17 = (bf16[3,8,144,128]{3,2,1,0:T(8,128)(2,1)}, bf16[3,8,144,128]{3,2,1,0:T(8,128)(2,1)}, u32[]{:S(2)}, u32[]{:S(2)}) collective-permute-start(bf16[3,8,144,128]{3,2,1,0:T(8,128)(2,1)} %broadcast_select_fusion.1), channel_id=1, source_target_pairs={{0,8},{1,9},{10,2},{11,3},{20,28},{21,29},{30,22},{31,23},{16,24},... | collective-permute-start | bytes 2654216 | tf_op jit(solution)/shard_map/ppermute | solution.py:105
  63.4 6.3 %collective-permute-done.9 = bf16[3,2,2,144,128]{4,3,2,1,0:T(8,128)(2,1)S(1)} collective-permute-done((bf16[3,2,2,144,128]{4,3,2,1,0:T(8,128)(2,1)S(1)}, bf16[3,2,2,144,128]{4,3,2,1,0:T(8,128)(2,1)S(1)}, u32[]{:S(2)}, u32[]{:S(2)}) %collective-permute-start.9) | collective-permute-done | bytes 442400 | tf_op jit(solution)/shard_map/ppermute | solution.py:132
  70.7 3.9 %collective-permute-start.18 = (bf16[3,8,144,128]{3,2,1,0:T(8,128)(2,1)S(1)}, bf16[3,8,144,128]{3,2,1,0:T(8,128)(2,1)S(1)}, u32[]{:S(2)}, u32[]{:S(2)}) collective-permute-start(bf16[3,8,144,128]{3,2,1,0:T(8,128)(2,1)S(1)} %pad_maximum_fusion.2), channel_id=1, source_target_pairs={{0,16},{1,17},{10,26},{11,27},{20,4},{21,5},{30,14},{31,15}} | collective-permute-start | bytes 2654216 | tf_op jit(solution)/shard_map/ppermute | solution.py:105
  75.0 6.3 %collective-permute-done.11 = bf16[3,2,2,144,128]{4,3,2,1,0:T(8,128)(2,1)S(1)} collective-permute-done((bf16[3,2,2,144,128]{4,3,2,1,0:T(8,128)(2,1)S(1)}, bf16[3,2,2,144,128]{4,3,2,1,0:T(8,128)(2,1)S(1)}, u32[]{:S(2)}, u32[]{:S(2)}) %collective-permute-start.11) | collective-permute-done | bytes 442400 | tf_op jit(solution)/shard_map/ppermute | solution.py:132
  81.4 4.9 %collective-permute-start.20 = (bf16[3,4,144,128]{3,2,1,0:T(8,128)(2,1)S(1)}, bf16[3,4,144,128]{3,2,1,0:T(8,128)(2,1)S(1)}, u32[]{:S(2)}, u32[]{:S(2)}) collective-permute-start(bf16[3,4,144,128]{3,2,1,0:T(8,128)(2,1)S(1)} %pad_maximum_fusion.3), channel_id=1, source_target_pairs={{0,16},{1,17},{10,26},{11,27},{20,4},{21,5},{30,14},{31,15}} | collective-permute-start | bytes 1327112 | tf_op jit(solution)/shard_map/ppermute | solution.py:105
  88.1 2.0 %collective-permute-start.13 = (bf16[3,2,2,144,128]{4,3,2,1,0:T(8,128)(2,1)S(1)}, bf16[3,2,2,144,128]{4,3,2,1,0:T(8,128)(2,1)S(1)}, u32[]{:S(2)}, u32[]{:S(2)}) collective-permute-start(bf16[3,2,2,144,128]{4,3,2,1,0:T(8,128)(2,1)S(1)} %collective-permute-done.11), channel_id=1, source_target_pairs={{2,0},{4,2},{6,4},{7,6},{5,7},{3,5},{1,3},{0,1},{10,8},{12,10},{14... | collective-permute-start | bytes 1327112 | tf_op jit(solution)/shard_map/ppermute | solution.py:132
  93.1 2.1 %collective-permute-start.21 = (bf16[3,4,144,128]{3,2,1,0:T(8,128)(2,1)}, bf16[3,4,144,128]{3,2,1,0:T(8,128)(2,1)}, u32[]{:S(2)}, u32[]{:S(2)}) collective-permute-start(bf16[3,4,144,128]{3,2,1,0:T(8,128)(2,1)} %broadcast_select_fusion.4), channel_id=1, source_target_pairs={{0,8},{1,9},{10,2},{11,3},{20,28},{21,29},{30,22},{31,23},{16,24},... | collective-permute-start | bytes 1327112 | tf_op jit(solution)/shard_map/ppermute | solution.py:105
  95.2 1.2 broadcast_select_fusion
  96.4 2.2 %collective-permute-start.19 = (bf16[3,8,144,128]{3,2,1,0:T(8,128)(2,1)}, bf16[3,8,144,128]{3,2,1,0:T(8,128)(2,1)}, u32[]{:S(2)}, u32[]{:S(2)}) collective-permute-start(bf16[3,8,144,128]{3,2,1,0:T(8,128)(2,1)} %broadcast_select_fusion), channel_id=1, source_target_pairs={{0,8},{1,9},{10,2},{11,3},{20,28},{21,29},{30,22},{31,23},{16,24},... | collective-permute-start | bytes 2654216 | tf_op jit(solution)/shard_map/ppermute | solution.py:105
  100.5 4.8 %collective-permute-start.22 = (bf16[3,4,144,128]{3,2,1,0:T(8,128)(2,1)}, bf16[3,4,144,128]{3,2,1,0:T(8,128)(2,1)}, u32[]{:S(2)}, u32[]{:S(2)}) collective-permute-start(bf16[3,4,144,128]{3,2,1,0:T(8,128)(2,1)} %pad_maximum_fusion.4), channel_id=1, source_target_pairs={{0,16},{1,17},{10,26},{11,27},{20,4},{21,5},{30,14},{31,15}} | collective-permute-start | bytes 1327112 | tf_op jit(solution)/shard_map/ppermute | solution.py:105
  107.0 1.7 %slice.19 = bf16[96,2,1,1]{3,2,1,0:T(2,128)(2,1)} slice(bf16[96,2,144,128]{3,2,1,0:T(8,128)(2,1)} %bitcast.44), slice={[0:96], [0:2], [131:132], [0:1]} | slice | bytes 768 | tf_op jit(solution)/shard_map/slice | solution.py:152
  109.8 1.9 %select_dynamic-update-slice_fusion.1 = bf16[3,32,144,128]{3,2,1,0:T(8,128)(2,1)S(1)} fusion(bf16[3,32,144,128]{3,2,1,0:T(8,128)(2,1)S(1)} %select_dynamic-update-slice_fusion.2, bf16[3,8,144,128]{3,2,1,0:T(8,128)(2,1)} %copy-done.16, bf16[3,8,144,128]{3,2,1,0:T(8,128)(2,1)} %collective-permute-done.17, pred[]{:T(512)S(6)} %and.27, pred[]{:T(512)S(6)} %eq.10, ...), kind=kLoop, calls=%fused_computation.5 | loop fusion | flops 4423680 | bytes 3538946
  111.7 1.1 broadcast_select_fusion.3
  112.8 1.3 %collective-permute-start.23 = (bf16[3,4,144,128]{3,2,1,0:T(8,128)(2,1)S(1)}, bf16[3,4,144,128]{3,2,1,0:T(8,128)(2,1)S(1)}, u32[]{:S(2)}, u32[]{:S(2)}) collective-permute-start(bf16[3,4,144,128]{3,2,1,0:T(8,128)(2,1)S(1)} %broadcast_select_fusion.3), channel_id=1, source_target_pairs={{0,8},{1,9},{10,2},{11,3},{20,28},{21,29},{30,22},{31,23},{16,24},... | collective-permute-start | bytes 1327112 | tf_op jit(solution)/shard_map/ppermute | solution.py:105
  114.2 1.8 %select_dynamic-update-slice_fusion = bf16[3,32,144,128]{3,2,1,0:T(8,128)(2,1)S(1)} fusion(bf16[3,32,144,128]{3,2,1,0:T(8,128)(2,1)S(1)} %select_dynamic-update-slice_fusion.1, bf16[3,8,144,128]{3,2,1,0:T(8,128)(2,1)} %copy-done.17, bf16[3,8,144,128]{3,2,1,0:T(8,128)(2,1)} %collective-permute-done.19, pred[]{:T(512)S(6)} %and.27, pred[]{:T(512)S(6)} %eq.10, ...), kind=kLoop, calls=%fused_computation.4 | loop fusion | flops 4423680 | bytes 3538946
  116.0 1.2 select_dynamic-update-slice_fusion.4
  120.0 10.8 %shard_map.37 = f32[2048,1024]{1,0:T(8,128)} custom-call(s32[288]{0:T(512)S(1)} %min.12.offs_ref, bf16[96,2,144,128]{3,2,1,0:T(8,128)(2,1)} %bitcast.45, bf16[96,144,128]{2,1,0:T(8,128)(2,1)S(1)} %bitcast.43), custom_call_target="tpu_custom_call" | custom-call | flops 805306368 | bytes 17825792 | tf_op jit(solution)/shard_map/pallas_call | solution.py:40
  (118 shorter events, 24.9 us)
Async XLA Ops:
  4.2 13.2 %collective-permute-start = (bf16[3,2,2,144,128]{4,3,2,1,0:T(8,128)(2,1)S(1)}, bf16[3,2,2,144,128]{4,3,2,1,0:T(8,128)(2,1)S(1)}, u32[]{:S(2)}, u32[]{:S(2)}) collective-permute-start(bf16[3,2,2,144,128]{4,3,2,1,0:T(8,128)(2,1)S(1)} %get-tuple-element.5), channel_id=1, source_target_pairs={{0,2},{2,4},{4,6},{6,7},{7,5},{5,3},{3,1},{1,0},{8,10},{10,12},{12... | collective-permute-start | bytes 1327112 | tf_op jit(solution)/shard_map/ppermute | solution.py:131
  7.3 11.9 %collective-permute-start.1 = (bf16[3,2,2,144,128]{4,3,2,1,0:T(8,128)(2,1)S(1)}, bf16[3,2,2,144,128]{4,3,2,1,0:T(8,128)(2,1)S(1)}, u32[]{:S(2)}, u32[]{:S(2)}) collective-permute-start(bf16[3,2,2,144,128]{4,3,2,1,0:T(8,128)(2,1)S(1)} %get-tuple-element.6), channel_id=1, source_target_pairs={{2,0},{4,2},{6,4},{7,6},{5,7},{3,5},{1,3},{0,1},{10,8},{12,10},{14... | collective-permute-start | bytes 1327112 | tf_op jit(solution)/shard_map/ppermute | solution.py:132
  17.4 11.4 %collective-permute-start.2 = (bf16[3,2,2,144,128]{4,3,2,1,0:T(8,128)(2,1)S(1)}, bf16[3,2,2,144,128]{4,3,2,1,0:T(8,128)(2,1)S(1)}, u32[]{:S(2)}, u32[]{:S(2)}) collective-permute-start(bf16[3,2,2,144,128]{4,3,2,1,0:T(8,128)(2,1)S(1)} %collective-permute-done), channel_id=1, source_target_pairs={{0,2},{2,4},{4,6},{6,7},{7,5},{5,3},{3,1},{1,0},{8,10},{10,12},{12... | collective-permute-start | bytes 1327112 | tf_op jit(solution)/shard_map/ppermute | solution.py:131
  19.2 11.0 %collective-permute-start.3 = (bf16[3,2,2,144,128]{4,3,2,1,0:T(8,128)(2,1)S(1)}, bf16[3,2,2,144,128]{4,3,2,1,0:T(8,128)(2,1)S(1)}, u32[]{:S(2)}, u32[]{:S(2)}) collective-permute-start(bf16[3,2,2,144,128]{4,3,2,1,0:T(8,128)(2,1)S(1)} %collective-permute-done.1), channel_id=1, source_target_pairs={{2,0},{4,2},{6,4},{7,6},{5,7},{3,5},{1,3},{0,1},{10,8},{12,10},{14... | collective-permute-start | bytes 1327112 | tf_op jit(solution)/shard_map/ppermute | solution.py:132
  19.6 24.1 %collective-permute-start.14 = (bf16[3,8,144,128]{3,2,1,0:T(8,128)(2,1)S(1)}, bf16[3,8,144,128]{3,2,1,0:T(8,128)(2,1)S(1)}, u32[]{:S(2)}, u32[]{:S(2)}) collective-permute-start(bf16[3,8,144,128]{3,2,1,0:T(8,128)(2,1)S(1)} %pad_maximum_fusion), channel_id=1, source_target_pairs={{0,16},{1,17},{10,26},{11,27},{20,4},{21,5},{30,14},{31,15}} | collective-permute-start | bytes 2654216 | tf_op jit(solution)/shard_map/ppermute | solution.py:105
  28.7 10.4 %collective-permute-start.4 = (bf16[3,2,2,144,128]{4,3,2,1,0:T(8,128)(2,1)S(1)}, bf16[3,2,2,144,128]{4,3,2,1,0:T(8,128)(2,1)S(1)}, u32[]{:S(2)}, u32[]{:S(2)}) collective-permute-start(bf16[3,2,2,144,128]{4,3,2,1,0:T(8,128)(2,1)S(1)} %collective-permute-done.2), channel_id=1, source_target_pairs={{0,2},{2,4},{4,6},{6,7},{7,5},{5,3},{3,1},{1,0},{8,10},{10,12},{12... | collective-permute-start | bytes 1327112 | tf_op jit(solution)/shard_map/ppermute | solution.py:131
  30.2 9.8 %collective-permute-start.5 = (bf16[3,2,2,144,128]{4,3,2,1,0:T(8,128)(2,1)S(1)}, bf16[3,2,2,144,128]{4,3,2,1,0:T(8,128)(2,1)S(1)}, u32[]{:S(2)}, u32[]{:S(2)}) collective-permute-start(bf16[3,2,2,144,128]{4,3,2,1,0:T(8,128)(2,1)S(1)} %collective-permute-done.3), channel_id=1, source_target_pairs={{2,0},{4,2},{6,4},{7,6},{5,7},{3,5},{1,3},{0,1},{10,8},{12,10},{14... | collective-permute-start | bytes 1327112 | tf_op jit(solution)/shard_map/ppermute | solution.py:132
  30.8 29.5 %copy-start = (bf16[3,2,144,128]{3,2,1,0:T(8,128)(2,1)}, bf16[3,2,144,128]{3,2,1,0:T(8,128)(2,1)S(1)}, u32[]{:S(2)}) copy-start(bf16[3,2,144,128]{3,2,1,0:T(8,128)(2,1)S(1)} %dynamic-slice_bitcast_fusion.11) | copy-start | bytes 663556
  30.8 29.4 %copy-start.1 = (bf16[3,2,144,128]{3,2,1,0:T(8,128)(2,1)}, bf16[3,2,144,128]{3,2,1,0:T(8,128)(2,1)S(1)}, u32[]{:S(2)}) copy-start(bf16[3,2,144,128]{3,2,1,0:T(8,128)(2,1)S(1)} %dynamic-slice_bitcast_fusion.10) | copy-start | bytes 663556
  39.2 31.5 %copy-start.2 = (bf16[3,2,144,128]{3,2,1,0:T(8,128)(2,1)}, bf16[3,2,144,128]{3,2,1,0:T(8,128)(2,1)S(1)}, u32[]{:S(2)}) copy-start(bf16[3,2,144,128]{3,2,1,0:T(8,128)(2,1)S(1)} %dynamic-slice_bitcast_fusion.9) | copy-start | bytes 663556
  40.1 30.6 %copy-start.3 = (bf16[3,2,144,128]{3,2,1,0:T(8,128)(2,1)}, bf16[3,2,144,128]{3,2,1,0:T(8,128)(2,1)S(1)}, u32[]{:S(2)}) copy-start(bf16[3,2,144,128]{3,2,1,0:T(8,128)(2,1)S(1)} %dynamic-slice_bitcast_fusion.8) | copy-start | bytes 663556
  40.2 18.7 %collective-permute-start.16 = (bf16[3,8,144,128]{3,2,1,0:T(8,128)(2,1)S(1)}, bf16[3,8,144,128]{3,2,1,0:T(8,128)(2,1)S(1)}, u32[]{:S(2)}, u32[]{:S(2)}) collective-permute-start(bf16[3,8,144,128]{3,2,1,0:T(8,128)(2,1)S(1)} %pad_maximum_fusion.1), channel_id=1, source_target_pairs={{0,16},{1,17},{10,26},{11,27},{20,4},{21,5},{30,14},{31,15}} | collective-permute-start | bytes 2654216 | tf_op jit(solution)/shard_map/ppermute | solution.py:105
  43.7 9.1 %collective-permute-start.6 = (bf16[3,2,2,144,128]{4,3,2,1,0:T(8,128)(2,1)S(1)}, bf16[3,2,2,144,128]{4,3,2,1,0:T(8,128)(2,1)S(1)}, u32[]{:S(2)}, u32[]{:S(2)}) collective-permute-start(bf16[3,2,2,144,128]{4,3,2,1,0:T(8,128)(2,1)S(1)} %collective-permute-done.4), channel_id=1, source_target_pairs={{0,2},{2,4},{4,6},{6,7},{7,5},{5,3},{3,1},{1,0},{8,10},{10,12},{12... | collective-permute-start | bytes 1327112 | tf_op jit(solution)/shard_map/ppermute | solution.py:131
  43.9 30.7 %collective-permute-start.15 = (bf16[3,8,144,128]{3,2,1,0:T(8,128)(2,1)S(1)}, bf16[3,8,144,128]{3,2,1,0:T(8,128)(2,1)S(1)}, u32[]{:S(2)}, u32[]{:S(2)}) collective-permute-start(bf16[3,8,144,128]{3,2,1,0:T(8,128)(2,1)S(1)} %broadcast_select_fusion.2), channel_id=1, source_target_pairs={{0,8},{1,9},{10,2},{11,3},{20,28},{21,29},{30,22},{31,23},{16,24},... | collective-permute-start | bytes 2654216 | tf_op jit(solution)/shard_map/ppermute | solution.py:105
  45.3 12.5 %collective-permute-start.7 = (bf16[3,2,2,144,128]{4,3,2,1,0:T(8,128)(2,1)S(1)}, bf16[3,2,2,144,128]{4,3,2,1,0:T(8,128)(2,1)S(1)}, u32[]{:S(2)}, u32[]{:S(2)}) collective-permute-start(bf16[3,2,2,144,128]{4,3,2,1,0:T(8,128)(2,1)S(1)} %collective-permute-done.5), channel_id=1, source_target_pairs={{2,0},{4,2},{6,4},{7,6},{5,7},{3,5},{1,3},{0,1},{10,8},{12,10},{14... | collective-permute-start | bytes 1327112 | tf_op jit(solution)/shard_map/ppermute | solution.py:132
  52.7 10.5 %collective-permute-start.8 = (bf16[3,2,2,144,128]{4,3,2,1,0:T(8,128)(2,1)S(1)}, bf16[3,2,2,144,128]{4,3,2,1,0:T(8,128)(2,1)S(1)}, u32[]{:S(2)}, u32[]{:S(2)}) collective-permute-start(bf16[3,2,2,144,128]{4,3,2,1,0:T(8,128)(2,1)S(1)} %collective-permute-done.6), channel_id=1, source_target_pairs={{0,2},{2,4},{4,6},{6,7},{7,5},{5,3},{3,1},{1,0},{8,10},{10,12},{12... | collective-permute-start | bytes 1327112 | tf_op jit(solution)/shard_map/ppermute | solution.py:131
  54.1 41.1 %copy-start.4 = (bf16[3,2,144,128]{3,2,1,0:T(8,128)(2,1)}, bf16[3,2,144,128]{3,2,1,0:T(8,128)(2,1)S(1)}, u32[]{:S(2)}) copy-start(bf16[3,2,144,128]{3,2,1,0:T(8,128)(2,1)S(1)} %dynamic-slice_bitcast_fusion.7) | copy-start | bytes 663556
  57.7 12.0 %collective-permute-start.9 = (bf16[3,2,2,144,128]{4,3,2,1,0:T(8,128)(2,1)S(1)}, bf16[3,2,2,144,128]{4,3,2,1,0:T(8,128)(2,1)S(1)}, u32[]{:S(2)}, u32[]{:S(2)}) collective-permute-start(bf16[3,2,2,144,128]{4,3,2,1,0:T(8,128)(2,1)S(1)} %collective-permute-done.7), channel_id=1, source_target_pairs={{2,0},{4,2},{6,4},{7,6},{5,7},{3,5},{1,3},{0,1},{10,8},{12,10},{14... | collective-permute-start | bytes 1327112 | tf_op jit(solution)/shard_map/ppermute | solution.py:132
  58.1 37.1 %copy-start.5 = (bf16[3,2,144,128]{3,2,1,0:T(8,128)(2,1)}, bf16[3,2,144,128]{3,2,1,0:T(8,128)(2,1)S(1)}, u32[]{:S(2)}) copy-start(bf16[3,2,144,128]{3,2,1,0:T(8,128)(2,1)S(1)} %dynamic-slice_bitcast_fusion.6) | copy-start | bytes 663556
  60.2 49.5 %collective-permute-start.17 = (bf16[3,8,144,128]{3,2,1,0:T(8,128)(2,1)}, bf16[3,8,144,128]{3,2,1,0:T(8,128)(2,1)}, u32[]{:S(2)}, u32[]{:S(2)}) collective-permute-start(bf16[3,8,144,128]{3,2,1,0:T(8,128)(2,1)} %broadcast_select_fusion.1), channel_id=1, source_target_pairs={{0,8},{1,9},{10,2},{11,3},{20,28},{21,29},{30,22},{31,23},{16,24},... | collective-permute-start | bytes 2654216 | tf_op jit(solution)/shard_map/ppermute | solution.py:105
  63.2 11.8 %collective-permute-start.10 = (bf16[3,2,2,144,128]{4,3,2,1,0:T(8,128)(2,1)S(1)}, bf16[3,2,2,144,128]{4,3,2,1,0:T(8,128)(2,1)S(1)}, u32[]{:S(2)}, u32[]{:S(2)}) collective-permute-start(bf16[3,2,2,144,128]{4,3,2,1,0:T(8,128)(2,1)S(1)} %collective-permute-done.8), channel_id=1, source_target_pairs={{0,2},{2,4},{4,6},{6,7},{7,5},{5,3},{3,1},{1,0},{8,10},{10,12},{12... | collective-permute-start | bytes 1327112 | tf_op jit(solution)/shard_map/ppermute | solution.py:131
  69.7 11.6 %collective-permute-start.11 = (bf16[3,2,2,144,128]{4,3,2,1,0:T(8,128)(2,1)S(1)}, bf16[3,2,2,144,128]{4,3,2,1,0:T(8,128)(2,1)S(1)}, u32[]{:S(2)}, u32[]{:S(2)}) collective-permute-start(bf16[3,2,2,144,128]{4,3,2,1,0:T(8,128)(2,1)S(1)} %collective-permute-done.9), channel_id=1, source_target_pairs={{2,0},{4,2},{6,4},{7,6},{5,7},{3,5},{1,3},{0,1},{10,8},{12,10},{14... | collective-permute-start | bytes 1327112 | tf_op jit(solution)/shard_map/ppermute | solution.py:132
  70.5 25.9 %copy-start.6 = (bf16[3,2,144,128]{3,2,1,0:T(8,128)(2,1)}, bf16[3,2,144,128]{3,2,1,0:T(8,128)(2,1)S(1)}, u32[]{:S(2)}) copy-start(bf16[3,2,144,128]{3,2,1,0:T(8,128)(2,1)S(1)} %dynamic-slice_bitcast_fusion.5) | copy-start | bytes 663556
  70.5 25.9 %copy-start.7 = (bf16[3,2,144,128]{3,2,1,0:T(8,128)(2,1)}, bf16[3,2,144,128]{3,2,1,0:T(8,128)(2,1)S(1)}, u32[]{:S(2)}) copy-start(bf16[3,2,144,128]{3,2,1,0:T(8,128)(2,1)S(1)} %dynamic-slice_bitcast_fusion.4) | copy-start | bytes 663556
  70.7 24.5 %collective-permute-start.18 = (bf16[3,8,144,128]{3,2,1,0:T(8,128)(2,1)S(1)}, bf16[3,8,144,128]{3,2,1,0:T(8,128)(2,1)S(1)}, u32[]{:S(2)}, u32[]{:S(2)}) collective-permute-start(bf16[3,8,144,128]{3,2,1,0:T(8,128)(2,1)S(1)} %pad_maximum_fusion.2), channel_id=1, source_target_pairs={{0,16},{1,17},{10,26},{11,27},{20,4},{21,5},{30,14},{31,15}} | collective-permute-start | bytes 2654216 | tf_op jit(solution)/shard_map/ppermute | solution.py:105
  81.4 10.7 %collective-permute-start.20 = (bf16[3,4,144,128]{3,2,1,0:T(8,128)(2,1)S(1)}, bf16[3,4,144,128]{3,2,1,0:T(8,128)(2,1)S(1)}, u32[]{:S(2)}, u32[]{:S(2)}) collective-permute-start(bf16[3,4,144,128]{3,2,1,0:T(8,128)(2,1)S(1)} %pad_maximum_fusion.3), channel_id=1, source_target_pairs={{0,16},{1,17},{10,26},{11,27},{20,4},{21,5},{30,14},{31,15}} | collective-permute-start | bytes 1327112 | tf_op jit(solution)/shard_map/ppermute | solution.py:105
  88.0 10.5 %collective-permute-start.12 = (bf16[3,2,2,144,128]{4,3,2,1,0:T(8,128)(2,1)S(1)}, bf16[3,2,2,144,128]{4,3,2,1,0:T(8,128)(2,1)S(1)}, u32[]{:S(2)}, u32[]{:S(2)}) collective-permute-start(bf16[3,2,2,144,128]{4,3,2,1,0:T(8,128)(2,1)S(1)} %collective-permute-done.10), channel_id=1, source_target_pairs={{0,2},{2,4},{4,6},{6,7},{7,5},{5,3},{3,1},{1,0},{8,10},{10,12},{12... | collective-permute-start | bytes 1327112 | tf_op jit(solution)/shard_map/ppermute | solution.py:131
  88.1 11.5 %collective-permute-start.13 = (bf16[3,2,2,144,128]{4,3,2,1,0:T(8,128)(2,1)S(1)}, bf16[3,2,2,144,128]{4,3,2,1,0:T(8,128)(2,1)S(1)}, u32[]{:S(2)}, u32[]{:S(2)}) collective-permute-start(bf16[3,2,2,144,128]{4,3,2,1,0:T(8,128)(2,1)S(1)} %collective-permute-done.11), channel_id=1, source_target_pairs={{2,0},{4,2},{6,4},{7,6},{5,7},{3,5},{1,3},{0,1},{10,8},{12,10},{14... | collective-permute-start | bytes 1327112 | tf_op jit(solution)/shard_map/ppermute | solution.py:132
  93.1 22.9 %collective-permute-start.21 = (bf16[3,4,144,128]{3,2,1,0:T(8,128)(2,1)}, bf16[3,4,144,128]{3,2,1,0:T(8,128)(2,1)}, u32[]{:S(2)}, u32[]{:S(2)}) collective-permute-start(bf16[3,4,144,128]{3,2,1,0:T(8,128)(2,1)} %broadcast_select_fusion.4), channel_id=1, source_target_pairs={{0,8},{1,9},{10,2},{11,3},{20,28},{21,29},{30,22},{31,23},{16,24},... | collective-permute-start | bytes 1327112 | tf_op jit(solution)/shard_map/ppermute | solution.py:105
  96.4 17.8 %collective-permute-start.19 = (bf16[3,8,144,128]{3,2,1,0:T(8,128)(2,1)}, bf16[3,8,144,128]{3,2,1,0:T(8,128)(2,1)}, u32[]{:S(2)}, u32[]{:S(2)}) collective-permute-start(bf16[3,8,144,128]{3,2,1,0:T(8,128)(2,1)} %broadcast_select_fusion), channel_id=1, source_target_pairs={{0,8},{1,9},{10,2},{11,3},{20,28},{21,29},{30,22},{31,23},{16,24},... | collective-permute-start | bytes 2654216 | tf_op jit(solution)/shard_map/ppermute | solution.py:105
  100.5 11.2 %collective-permute-start.22 = (bf16[3,4,144,128]{3,2,1,0:T(8,128)(2,1)}, bf16[3,4,144,128]{3,2,1,0:T(8,128)(2,1)}, u32[]{:S(2)}, u32[]{:S(2)}) collective-permute-start(bf16[3,4,144,128]{3,2,1,0:T(8,128)(2,1)} %pad_maximum_fusion.4), channel_id=1, source_target_pairs={{0,16},{1,17},{10,26},{11,27},{20,4},{21,5},{30,14},{31,15}} | collective-permute-start | bytes 1327112 | tf_op jit(solution)/shard_map/ppermute | solution.py:105
  112.8 4.4 %collective-permute-start.23 = (bf16[3,4,144,128]{3,2,1,0:T(8,128)(2,1)S(1)}, bf16[3,4,144,128]{3,2,1,0:T(8,128)(2,1)S(1)}, u32[]{:S(2)}, u32[]{:S(2)}) collective-permute-start(bf16[3,4,144,128]{3,2,1,0:T(8,128)(2,1)S(1)} %broadcast_select_fusion.3), channel_id=1, source_target_pairs={{0,8},{1,9},{10,2},{11,3},{20,28},{21,29},{30,22},{31,23},{16,24},... | collective-permute-start | bytes 1327112 | tf_op jit(solution)/shard_map/ppermute | solution.py:105
  (12 other events, 111.5 us)

commit v22 on v20

--- a/solution.py
+++ b/solution.py
@@ -120,7 +120,7 @@
     def pick_slot(piece):
         return lax.dynamic_index_in_dim(piece, slot, axis=2, keepdims=False)
 
-    batches = [[k, k + 1] for k in range(0, ncol - 2, 2)] + [[ncol - 2], [ncol - 1]]
+    batches = [list(range(k, min(k + 3, ncol - 2))) for k in range(0, ncol - 2, 3)] + [[ncol - 2], [ncol - 1]]
     half = x.shape[1] // 2
     a, b = x[:, :half], x[:, half:]
     pieces, columns, pending = [], [], []

time: 124 us -> 126 us (1.016)
  other arithmetic: 12.5 us -> 9.77 us
  starting transfers between devices: 46 us -> 48.4 us
  local copies, waits for them, and re-layouts: 18 us -> 19.9 us
    select_n x0 -> x4, other arithmetic: none -> 4.41 us  [last_fan(): jnp.where(is_s, own, jnp.where(is_p, to_partner, jnp.where(is_d1, to_d1,...]
    unnamed x5 -> x1, other arithmetic: 6.78 us -> 2.39 us
    unnamed x29, local copies, waits for them, and re-layouts: 11.2 us -> 13.4 us
    concatenate x5 -> x2, other arithmetic: 2.99 us -> 0.85 us  [local(): own = jnp.concatenate(pending, axis=1)]
    ppermute x15 -> x12, starting transfers between devices: 30.8 us -> 32.7 us  [send(): lax.ppermute(v, ('row', 'col'), [(a * ncol + cc, b * ncol + cc) for a, b,...]
  transfers between devices with their start and end apart: 29 -> 26, of which waited for: 7 -> 6; matrix products, arithmetic and copies ran while one was open for 18% -> 17% of each run, Pallas kernels for 0% -> 0%
where the time goes in v22:
time: 126 us; the launch traced here: 125 us
  starting transfers between devices  48.4 us (38%)
  waiting for transfers between devices  36.2 us (29%)
  local copies, waits for them, and re-layouts  19.9 us (16%)
  Pallas kernels  10.8 us (9%)
  other arithmetic  9.77 us (8%)
    ppermute x7, waiting for transfers between devices, local(): a = lax.ppermute(a, 'col', forward)  36.2 us
    ppermute x12, starting transfers between devices, send(): lax.ppermute(v, ('row', 'col'), [(a * ncol + cc, b * ncol + cc) for a, b,...  32.7 us
    unnamed x29, local copies, waits for them, and re-layouts  13.4 us
    ppermute x7, starting transfers between devices, local(): a = lax.ppermute(a, 'col', forward)  11.1 us
    pallas_call x1, Pallas kernels, gram_call(): pl.pallas_call(kernel, grid_spec=pltpu.PrefetchScalarGridSpec(num_scalar_...  10.8 us
    ppermute x7, starting transfers between devices, local(): b = lax.ppermute(b, 'col', backward)  4.58 us
    select_n x4, other arithmetic, last_fan(): jnp.where(is_s, own, jnp.where(is_p, to_partner, jnp.where(is_d1, to_d1,...  4.41 us
    slice x2, local copies, waits for them, and re-layouts, local(): blocks[:, :, blk + 3, 0]  2.72 us
  transfers between devices with their start and end apart: 26, of which 6 were waited for; matrix products, arithmetic and copies ran while one was open for 17% of the time, Pallas kernels for 0%

profile of v22, /device:TPU:0, one launch (start us, length us, event | category | flops | bytes accessed | tf_op | source)
XLA Modules:
  0.0 125.4 jit_solution(8942023939650349157)
XLA Ops:
  1.7 2.4 %constant_dynamic-update-slice_fusion.14 = (bf16[3,32,2,144,128]{4,3,2,1,0:T(8,128)(2,1)}, bf16[3,4,2,144,128]{4,3,2,1,0:T(8,128)(2,1)S(1)}) fusion(bf16[144]{0:T(256)(128)(2,1)S(1)} %pad.13.clone, bf16[3,4,2,1,128]{4,3,2,1,0:T(2,128)(2,1)S(1)} %broadcast_in_dim.7, bf16[3,4,2,3,128]{4,3,2,1,0:T(4,128)(2,1)S(1)} %broadcast_in_dim.6, ...), kind=kLoop, calls=%fused_computation.38 | loop fusion | flops 3538943 | bytes 2580768
  4.2 3.1 %collective-permute-start = (bf16[3,2,2,144,128]{4,3,2,1,0:T(8,128)(2,1)S(1)}, bf16[3,2,2,144,128]{4,3,2,1,0:T(8,128)(2,1)S(1)}, u32[]{:S(2)}, u32[]{:S(2)}) collective-permute-start(bf16[3,2,2,144,128]{4,3,2,1,0:T(8,128)(2,1)S(1)} %get-tuple-element.5), channel_id=1, source_target_pairs={{0,2},{2,4},{4,6},{6,7},{7,5},{5,3},{3,1},{1,0},{8,10},{10,12},{12... | collective-permute-start | bytes 1327112 | tf_op jit(solution)/shard_map/ppermute | solution.py:129
  7.3 10.1 %collective-permute-done = bf16[3,2,2,144,128]{4,3,2,1,0:T(8,128)(2,1)S(1)} collective-permute-done((bf16[3,2,2,144,128]{4,3,2,1,0:T(8,128)(2,1)S(1)}, bf16[3,2,2,144,128]{4,3,2,1,0:T(8,128)(2,1)S(1)}, u32[]{:S(2)}, u32[]{:S(2)}) %collective-permute-start) | collective-permute-done | bytes 442400 | tf_op jit(solution)/shard_map/ppermute | solution.py:129
  17.4 1.8 %collective-permute-start.2 = (bf16[3,2,2,144,128]{4,3,2,1,0:T(8,128)(2,1)S(1)}, bf16[3,2,2,144,128]{4,3,2,1,0:T(8,128)(2,1)S(1)}, u32[]{:S(2)}, u32[]{:S(2)}) collective-permute-start(bf16[3,2,2,144,128]{4,3,2,1,0:T(8,128)(2,1)S(1)} %collective-permute-done), channel_id=1, source_target_pairs={{0,2},{2,4},{4,6},{6,7},{7,5},{5,3},{3,1},{1,0},{8,10},{10,12},{12... | collective-permute-start | bytes 1327112 | tf_op jit(solution)/shard_map/ppermute | solution.py:129
  19.5 9.3 %collective-permute-done.2 = bf16[3,2,2,144,128]{4,3,2,1,0:T(8,128)(2,1)S(1)} collective-permute-done((bf16[3,2,2,144,128]{4,3,2,1,0:T(8,128)(2,1)S(1)}, bf16[3,2,2,144,128]{4,3,2,1,0:T(8,128)(2,1)S(1)}, u32[]{:S(2)}, u32[]{:S(2)}) %collective-permute-start.2) | collective-permute-done | bytes 442400 | tf_op jit(solution)/shard_map/ppermute | solution.py:129
  28.8 1.5 %collective-permute-start.4 = (bf16[3,2,2,144,128]{4,3,2,1,0:T(8,128)(2,1)S(1)}, bf16[3,2,2,144,128]{4,3,2,1,0:T(8,128)(2,1)S(1)}, u32[]{:S(2)}, u32[]{:S(2)}) collective-permute-start(bf16[3,2,2,144,128]{4,3,2,1,0:T(8,128)(2,1)S(1)} %collective-permute-done.2), channel_id=1, source_target_pairs={{0,2},{2,4},{4,6},{6,7},{7,5},{5,3},{3,1},{1,0},{8,10},{10,12},{12... | collective-permute-start | bytes 1327112 | tf_op jit(solution)/shard_map/ppermute | solution.py:129
  30.9 1.0 bitcast_dynamic-update-slice_fusion.8
  32.7 1.9 %constant_dynamic-update-slice_fusion.12 = bf16[3,32,2,144,128]{4,3,2,1,0:T(8,128)(2,1)} fusion(bf16[3,32,2,144,128]{4,3,2,1,0:T(8,128)(2,1)} %constant_dynamic-update-slice_fusion.13, bf16[3,2,2,144,128]{4,3,2,1,0:T(8,128)(2,1)} %collective-permute-done.1), kind=kLoop, calls=%fused_computation.36 | loop fusion | bytes 884736
  34.6 4.8 %collective-permute-done.4 = bf16[3,2,2,144,128]{4,3,2,1,0:T(8,128)(2,1)S(1)} collective-permute-done((bf16[3,2,2,144,128]{4,3,2,1,0:T(8,128)(2,1)S(1)}, bf16[3,2,2,144,128]{4,3,2,1,0:T(8,128)(2,1)S(1)}, u32[]{:S(2)}, u32[]{:S(2)}) %collective-permute-start.4) | collective-permute-done | bytes 442400 | tf_op jit(solution)/shard_map/ppermute | solution.py:129
  39.4 1.3 %collective-permute-start.6 = (bf16[3,2,2,144,128]{4,3,2,1,0:T(8,128)(2,1)S(1)}, bf16[3,2,2,144,128]{4,3,2,1,0:T(8,128)(2,1)S(1)}, u32[]{:S(2)}, u32[]{:S(2)}) collective-permute-start(bf16[3,2,2,144,128]{4,3,2,1,0:T(8,128)(2,1)S(1)} %collective-permute-done.4), channel_id=1, source_target_pairs={{0,2},{2,4},{4,6},{6,7},{7,5},{5,3},{3,1},{1,0},{8,10},{10,12},{12... | collective-permute-start | bytes 1327112 | tf_op jit(solution)/shard_map/ppermute | solution.py:129
  41.4 4.3 %collective-permute-start.15 = (bf16[3,12,144,128]{3,2,1,0:T(8,128)(2,1)S(1)}, bf16[3,12,144,128]{3,2,1,0:T(8,128)(2,1)}, u32[]{:S(2)}, u32[]{:S(2)}) collective-permute-start(bf16[3,12,144,128]{3,2,1,0:T(8,128)(2,1)S(1)} %bitcast_dynamic-update-slice_fusion.6), channel_id=1, source_target_pairs={{0,16},{1,17},{10,26},{11,27},{20,4},{21,5},{30,14},{31,15}} | collective-permute-start | bytes 3981320 | tf_op jit(solution)/shard_map/ppermute | solution.py:105
  45.7 1.4 %collective-permute-start.14 = (bf16[3,12,144,128]{3,2,1,0:T(8,128)(2,1)S(1)}, bf16[3,12,144,128]{3,2,1,0:T(8,128)(2,1)S(1)}, u32[]{:S(2)}, u32[]{:S(2)}) collective-permute-start(bf16[3,12,144,128]{3,2,1,0:T(8,128)(2,1)S(1)} %bitcast_dynamic-update-slice_fusion.6), channel_id=1, source_target_pairs={{0,8},{1,9},{10,2},{11,3},{20,28},{21,29},{30,22},{31,23}} | collective-permute-start | bytes 3981320 | tf_op jit(solution)/shard_map/ppermute | solution.py:105
  50.0 1.7 %collective-permute-start.9 = (bf16[3,2,2,144,128]{4,3,2,1,0:T(8,128)(2,1)S(1)}, bf16[3,2,2,144,128]{4,3,2,1,0:T(8,128)(2,1)S(1)}, u32[]{:S(2)}, u32[]{:S(2)}) collective-permute-start(bf16[3,2,2,144,128]{4,3,2,1,0:T(8,128)(2,1)S(1)} %collective-permute-done.7), channel_id=1, source_target_pairs={{2,0},{4,2},{6,4},{7,6},{5,7},{3,5},{1,3},{0,1},{10,8},{12,10},{14... | collective-permute-start | bytes 1327112 | tf_op jit(solution)/shard_map/ppermute | solution.py:130
  52.7 5.8 %collective-permute-done.8 = bf16[3,2,2,144,128]{4,3,2,1,0:T(8,128)(2,1)S(1)} collective-permute-done((bf16[3,2,2,144,128]{4,3,2,1,0:T(8,128)(2,1)S(1)}, bf16[3,2,2,144,128]{4,3,2,1,0:T(8,128)(2,1)S(1)}, u32[]{:S(2)}, u32[]{:S(2)}) %collective-permute-start.8) | collective-permute-done | bytes 442400 | tf_op jit(solution)/shard_map/ppermute | solution.py:129
  58.5 2.4 %collective-permute-start.10 = (bf16[3,2,2,144,128]{4,3,2,1,0:T(8,128)(2,1)S(1)}, bf16[3,2,2,144,128]{4,3,2,1,0:T(8,128)(2,1)S(1)}, u32[]{:S(2)}, u32[]{:S(2)}) collective-permute-start(bf16[3,2,2,144,128]{4,3,2,1,0:T(8,128)(2,1)S(1)} %collective-permute-done.8), channel_id=1, source_target_pairs={{0,2},{2,4},{4,6},{6,7},{7,5},{5,3},{3,1},{1,0},{8,10},{10,12},{12... | collective-permute-start | bytes 1327112 | tf_op jit(solution)/shard_map/ppermute | solution.py:129
  61.0 5.3 %collective-permute-start.18 = (bf16[3,12,144,128]{3,2,1,0:T(8,128)(2,1)S(1)}, bf16[3,12,144,128]{3,2,1,0:T(8,128)(2,1)}, u32[]{:S(2)}, u32[]{:S(2)}) collective-permute-start(bf16[3,12,144,128]{3,2,1,0:T(8,128)(2,1)S(1)} %bitcast_dynamic-update-slice_fusion), channel_id=1, source_target_pairs={{0,16},{1,17},{10,26},{11,27},{20,4},{21,5},{30,14},{31,15}} | collective-permute-start | bytes 3981320 | tf_op jit(solution)/shard_map/ppermute | solution.py:105
  68.8 1.7 %collective-permute-start.16 = (bf16[3,12,144,128]{3,2,1,0:T(8,128)(2,1)}, bf16[3,12,144,128]{3,2,1,0:T(8,128)(2,1)}, u32[]{:S(2)}, u32[]{:S(2)}) collective-permute-start(bf16[3,12,144,128]{3,2,1,0:T(8,128)(2,1)} %collective-permute-done.15), channel_id=1, source_target_pairs={{16,24},{17,25},{26,18},{27,19},{4,12},{5,13},{14,6},{15,7}} | collective-permute-start | bytes 3981320 | tf_op jit(solution)/shard_map/ppermute | solution.py:105
  71.3 1.3 %collective-permute-start.13 = (bf16[3,2,2,144,128]{4,3,2,1,0:T(8,128)(2,1)S(1)}, bf16[3,2,2,144,128]{4,3,2,1,0:T(8,128)(2,1)S(1)}, u32[]{:S(2)}, u32[]{:S(2)}) collective-permute-start(bf16[3,2,2,144,128]{4,3,2,1,0:T(8,128)(2,1)S(1)} %collective-permute-done.11), channel_id=1, source_target_pairs={{2,0},{4,2},{6,4},{7,6},{5,7},{3,5},{1,3},{0,1},{10,8},{12,10},{14... | collective-permute-start | bytes 1327112 | tf_op jit(solution)/shard_map/ppermute | solution.py:130
  73.5 5.3 %collective-permute-done.12 = bf16[3,2,2,144,128]{4,3,2,1,0:T(8,128)(2,1)S(1)} collective-permute-done((bf16[3,2,2,144,128]{4,3,2,1,0:T(8,128)(2,1)S(1)}, bf16[3,2,2,144,128]{4,3,2,1,0:T(8,128)(2,1)S(1)}, u32[]{:S(2)}, u32[]{:S(2)}) %collective-permute-start.12) | collective-permute-done | bytes 442400 | tf_op jit(solution)/shard_map/ppermute | solution.py:129
  78.8 6.1 %collective-permute-start.21 = (bf16[3,4,144,128]{3,2,1,0:T(8,128)(2,1)S(1)}, bf16[3,4,144,128]{3,2,1,0:T(8,128)(2,1)}, u32[]{:S(2)}, u32[]{:S(2)}) collective-permute-start(bf16[3,4,144,128]{3,2,1,0:T(8,128)(2,1)S(1)} %pad_maximum_fusion.1), channel_id=1, source_target_pairs={{0,16},{1,17},{10,26},{11,27},{20,4},{21,5},{30,14},{31,15}} | collective-permute-start | bytes 1327112 | tf_op jit(solution)/shard_map/ppermute | solution.py:105
  85.0 1.3 %collective-permute-start.20 = (bf16[3,4,144,128]{3,2,1,0:T(8,128)(2,1)S(1)}, bf16[3,4,144,128]{3,2,1,0:T(8,128)(2,1)S(1)}, u32[]{:S(2)}, u32[]{:S(2)}) collective-permute-start(bf16[3,4,144,128]{3,2,1,0:T(8,128)(2,1)S(1)} %pad_maximum_fusion.1), channel_id=1, source_target_pairs={{0,8},{1,9},{10,2},{11,3},{20,28},{21,29},{30,22},{31,23}} | collective-permute-start | bytes 1327112 | tf_op jit(solution)/shard_map/ppermute | solution.py:105
  88.0 2.4 %collective-permute-start.17 = (bf16[3,12,144,128]{3,2,1,0:T(8,128)(2,1)S(1)}, bf16[3,12,144,128]{3,2,1,0:T(8,128)(2,1)}, u32[]{:S(2)}, u32[]{:S(2)}) collective-permute-start(bf16[3,12,144,128]{3,2,1,0:T(8,128)(2,1)S(1)} %bitcast_dynamic-update-slice_fusion), channel_id=1, source_target_pairs={{0,8},{1,9},{10,2},{11,3},{20,28},{21,29},{30,22},{31,23}} | collective-permute-start | bytes 3981320 | tf_op jit(solution)/shard_map/ppermute | solution.py:105
  90.4 4.9 %collective-permute-start.24 = (bf16[3,4,144,128]{3,2,1,0:T(8,128)(2,1)}, bf16[3,4,144,128]{3,2,1,0:T(8,128)(2,1)}, u32[]{:S(2)}, u32[]{:S(2)}) collective-permute-start(bf16[3,4,144,128]{3,2,1,0:T(8,128)(2,1)} %pad_maximum_fusion.2), channel_id=1, source_target_pairs={{0,16},{1,17},{10,26},{11,27},{20,4},{21,5},{30,14},{31,15}} | collective-permute-start | bytes 1327112 | tf_op jit(solution)/shard_map/ppermute | solution.py:105
  95.3 1.4 %collective-permute-start.22 = (bf16[3,4,144,128]{3,2,1,0:T(8,128)(2,1)}, bf16[3,4,144,128]{3,2,1,0:T(8,128)(2,1)}, u32[]{:S(2)}, u32[]{:S(2)}) collective-permute-start(bf16[3,4,144,128]{3,2,1,0:T(8,128)(2,1)} %collective-permute-done.21), channel_id=1, source_target_pairs={{16,24},{17,25},{26,18},{27,19},{4,12},{5,13},{14,6},{15,7}} | collective-permute-start | bytes 1327112 | tf_op jit(solution)/shard_map/ppermute | solution.py:105
  96.8 1.8 %collective-permute-start.19 = (bf16[3,12,144,128]{3,2,1,0:T(8,128)(2,1)}, bf16[3,12,144,128]{3,2,1,0:T(8,128)(2,1)}, u32[]{:S(2)}, u32[]{:S(2)}) collective-permute-start(bf16[3,12,144,128]{3,2,1,0:T(8,128)(2,1)} %collective-permute-done.18), channel_id=1, source_target_pairs={{16,24},{17,25},{26,18},{27,19},{4,12},{5,13},{14,6},{15,7}} | collective-permute-start | bytes 3981320 | tf_op jit(solution)/shard_map/ppermute | solution.py:105
  102.0 1.7 %slice.19 = bf16[96,2,1,1]{3,2,1,0:T(2,128)(2,1)} slice(bf16[96,2,144,128]{3,2,1,0:T(8,128)(2,1)} %bitcast.44), slice={[0:96], [0:2], [131:132], [0:1]} | slice | bytes 768 | tf_op jit(solution)/shard_map/slice | solution.py:150
  103.7 1.0 copy.9
  104.7 1.4 %collective-permute-start.23 = (bf16[3,4,144,128]{3,2,1,0:T(8,128)(2,1)}, bf16[3,4,144,128]{3,2,1,0:T(8,128)(2,1)S(1)}, u32[]{:S(2)}, u32[]{:S(2)}) collective-permute-start(bf16[3,4,144,128]{3,2,1,0:T(8,128)(2,1)} %pad_maximum_fusion.2), channel_id=1, source_target_pairs={{0,8},{1,9},{10,2},{11,3},{20,28},{21,29},{30,22},{31,23}} | collective-permute-start | bytes 1327112 | tf_op jit(solution)/shard_map/ppermute | solution.py:105
  106.9 1.1 select_select_fusion.3
  108.0 1.6 %select_select_fusion.1 = bf16[3,12,144,128]{3,2,1,0:T(8,128)(2,1)S(1)} fusion(bf16[3,12,144,128]{3,2,1,0:T(8,128)(2,1)S(1)} %bitcast_dynamic-update-slice_fusion.6, bf16[3,12,144,128]{3,2,1,0:T(8,128)(2,1)S(1)} %copy-done.1, bf16[3,12,144,128]{3,2,1,0:T(8,128)(2,1)} %collective-permute-done.15, bf16[3,12,144,128]{3,2,1,0:T(8,128)(2,1)} %collective-permute-done.16, ...), kind=kLoop, calls=%fused_computation.2 | loop fusion | flops 1990656 | bytes 6635523 | tf_op jit(solution)/shard_map/jit(_where)/select_n | solution.py:118
  109.8 1.6 %select_select_fusion = bf16[3,12,144,128]{3,2,1,0:T(8,128)(2,1)S(1)} fusion(bf16[3,12,144,128]{3,2,1,0:T(8,128)(2,1)S(1)} %bitcast_dynamic-update-slice_fusion, bf16[3,12,144,128]{3,2,1,0:T(8,128)(2,1)} %collective-permute-done.17, bf16[3,12,144,128]{3,2,1,0:T(8,128)(2,1)} %collective-permute-done.18, bf16[3,12,144,128]{3,2,1,0:T(8,128)(2,1)} %collective-permute-done.19, ...), kind=kLoop, calls=%fused_computation.1 | loop fusion | flops 1990656 | bytes 6635523 | tf_op jit(solution)/shard_map/jit(_where)/select_n | solution.py:118
  114.6 10.8 %shard_map.37 = f32[2048,1024]{1,0:T(8,128)} custom-call(s32[288]{0:T(512)S(1)} %min.12.offs_ref, bf16[96,2,144,128]{3,2,1,0:T(8,128)(2,1)} %bitcast.45, bf16[96,144,128]{2,1,0:T(8,128)(2,1)S(1)} %bitcast.43), custom_call_target="tpu_custom_call" | custom-call | flops 805306368 | bytes 17825792 | tf_op jit(solution)/shard_map/pallas_call | solution.py:40
  (81 shorter events, 21.7 us)
Async XLA Ops:
  4.2 13.2 %collective-permute-start = (bf16[3,2,2,144,128]{4,3,2,1,0:T(8,128)(2,1)S(1)}, bf16[3,2,2,144,128]{4,3,2,1,0:T(8,128)(2,1)S(1)}, u32[]{:S(2)}, u32[]{:S(2)}) collective-permute-start(bf16[3,2,2,144,128]{4,3,2,1,0:T(8,128)(2,1)S(1)} %get-tuple-element.5), channel_id=1, source_target_pairs={{0,2},{2,4},{4,6},{6,7},{7,5},{5,3},{3,1},{1,0},{8,10},{10,12},{12... | collective-permute-start | bytes 1327112 | tf_op jit(solution)/shard_map/ppermute | solution.py:129
  7.3 11.9 %collective-permute-start.1 = (bf16[3,2,2,144,128]{4,3,2,1,0:T(8,128)(2,1)S(1)}, bf16[3,2,2,144,128]{4,3,2,1,0:T(8,128)(2,1)}, u32[]{:S(2)}, u32[]{:S(2)}) collective-permute-start(bf16[3,2,2,144,128]{4,3,2,1,0:T(8,128)(2,1)S(1)} %get-tuple-element.6), channel_id=1, source_target_pairs={{2,0},{4,2},{6,4},{7,6},{5,7},{3,5},{1,3},{0,1},{10,8},{12,10},{14... | collective-permute-start | bytes 1327112 | tf_op jit(solution)/shard_map/ppermute | solution.py:130
  17.4 11.5 %collective-permute-start.2 = (bf16[3,2,2,144,128]{4,3,2,1,0:T(8,128)(2,1)S(1)}, bf16[3,2,2,144,128]{4,3,2,1,0:T(8,128)(2,1)S(1)}, u32[]{:S(2)}, u32[]{:S(2)}) collective-permute-start(bf16[3,2,2,144,128]{4,3,2,1,0:T(8,128)(2,1)S(1)} %collective-permute-done), channel_id=1, source_target_pairs={{0,2},{2,4},{4,6},{6,7},{7,5},{5,3},{3,1},{1,0},{8,10},{10,12},{12... | collective-permute-start | bytes 1327112 | tf_op jit(solution)/shard_map/ppermute | solution.py:129
  19.2 11.1 %collective-permute-start.3 = (bf16[3,2,2,144,128]{4,3,2,1,0:T(8,128)(2,1)}, bf16[3,2,2,144,128]{4,3,2,1,0:T(8,128)(2,1)S(1)}, u32[]{:S(2)}, u32[]{:S(2)}) collective-permute-start(bf16[3,2,2,144,128]{4,3,2,1,0:T(8,128)(2,1)} %collective-permute-done.1), channel_id=1, source_target_pairs={{2,0},{4,2},{6,4},{7,6},{5,7},{3,5},{1,3},{0,1},{10,8},{12,10},{14... | collective-permute-start | bytes 1327112 | tf_op jit(solution)/shard_map/ppermute | solution.py:130
  28.8 10.5 %collective-permute-start.4 = (bf16[3,2,2,144,128]{4,3,2,1,0:T(8,128)(2,1)S(1)}, bf16[3,2,2,144,128]{4,3,2,1,0:T(8,128)(2,1)S(1)}, u32[]{:S(2)}, u32[]{:S(2)}) collective-permute-start(bf16[3,2,2,144,128]{4,3,2,1,0:T(8,128)(2,1)S(1)} %collective-permute-done.2), channel_id=1, source_target_pairs={{0,2},{2,4},{4,6},{6,7},{7,5},{5,3},{3,1},{1,0},{8,10},{10,12},{12... | collective-permute-start | bytes 1327112 | tf_op jit(solution)/shard_map/ppermute | solution.py:129
  30.3 10.3 %collective-permute-start.5 = (bf16[3,2,2,144,128]{4,3,2,1,0:T(8,128)(2,1)S(1)}, bf16[3,2,2,144,128]{4,3,2,1,0:T(8,128)(2,1)S(1)}, u32[]{:S(2)}, u32[]{:S(2)}) collective-permute-start(bf16[3,2,2,144,128]{4,3,2,1,0:T(8,128)(2,1)S(1)} %collective-permute-done.3), channel_id=1, source_target_pairs={{2,0},{4,2},{6,4},{7,6},{5,7},{3,5},{1,3},{0,1},{10,8},{12,10},{14... | collective-permute-start | bytes 1327112 | tf_op jit(solution)/shard_map/ppermute | solution.py:130
  39.4 10.3 %collective-permute-start.6 = (bf16[3,2,2,144,128]{4,3,2,1,0:T(8,128)(2,1)S(1)}, bf16[3,2,2,144,128]{4,3,2,1,0:T(8,128)(2,1)S(1)}, u32[]{:S(2)}, u32[]{:S(2)}) collective-permute-start(bf16[3,2,2,144,128]{4,3,2,1,0:T(8,128)(2,1)S(1)} %collective-permute-done.4), channel_id=1, source_target_pairs={{0,2},{2,4},{4,6},{6,7},{7,5},{5,3},{3,1},{1,0},{8,10},{10,12},{12... | collective-permute-start | bytes 1327112 | tf_op jit(solution)/shard_map/ppermute | solution.py:129
  40.7 9.4 %collective-permute-start.7 = (bf16[3,2,2,144,128]{4,3,2,1,0:T(8,128)(2,1)S(1)}, bf16[3,2,2,144,128]{4,3,2,1,0:T(8,128)(2,1)S(1)}, u32[]{:S(2)}, u32[]{:S(2)}) collective-permute-start(bf16[3,2,2,144,128]{4,3,2,1,0:T(8,128)(2,1)S(1)} %collective-permute-done.5), channel_id=1, source_target_pairs={{2,0},{4,2},{6,4},{7,6},{5,7},{3,5},{1,3},{0,1},{10,8},{12,10},{14... | collective-permute-start | bytes 1327112 | tf_op jit(solution)/shard_map/ppermute | solution.py:130
  41.4 27.4 %collective-permute-start.15 = (bf16[3,12,144,128]{3,2,1,0:T(8,128)(2,1)S(1)}, bf16[3,12,144,128]{3,2,1,0:T(8,128)(2,1)}, u32[]{:S(2)}, u32[]{:S(2)}) collective-permute-start(bf16[3,12,144,128]{3,2,1,0:T(8,128)(2,1)S(1)} %bitcast_dynamic-update-slice_fusion.6), channel_id=1, source_target_pairs={{0,16},{1,17},{10,26},{11,27},{20,4},{21,5},{30,14},{31,15}} | collective-permute-start | bytes 3981320 | tf_op jit(solution)/shard_map/ppermute | solution.py:105
  45.7 42.3 %collective-permute-start.14 = (bf16[3,12,144,128]{3,2,1,0:T(8,128)(2,1)S(1)}, bf16[3,12,144,128]{3,2,1,0:T(8,128)(2,1)S(1)}, u32[]{:S(2)}, u32[]{:S(2)}) collective-permute-start(bf16[3,12,144,128]{3,2,1,0:T(8,128)(2,1)S(1)} %bitcast_dynamic-update-slice_fusion.6), channel_id=1, source_target_pairs={{0,8},{1,9},{10,2},{11,3},{20,28},{21,29},{30,22},{31,23}} | collective-permute-start | bytes 3981320 | tf_op jit(solution)/shard_map/ppermute | solution.py:105
  49.7 8.8 %collective-permute-start.8 = (bf16[3,2,2,144,128]{4,3,2,1,0:T(8,128)(2,1)S(1)}, bf16[3,2,2,144,128]{4,3,2,1,0:T(8,128)(2,1)S(1)}, u32[]{:S(2)}, u32[]{:S(2)}) collective-permute-start(bf16[3,2,2,144,128]{4,3,2,1,0:T(8,128)(2,1)S(1)} %collective-permute-done.6), channel_id=1, source_target_pairs={{0,2},{2,4},{4,6},{6,7},{7,5},{5,3},{3,1},{1,0},{8,10},{10,12},{12... | collective-permute-start | bytes 1327112 | tf_op jit(solution)/shard_map/ppermute | solution.py:129
  50.0 10.9 %collective-permute-start.9 = (bf16[3,2,2,144,128]{4,3,2,1,0:T(8,128)(2,1)S(1)}, bf16[3,2,2,144,128]{4,3,2,1,0:T(8,128)(2,1)S(1)}, u32[]{:S(2)}, u32[]{:S(2)}) collective-permute-start(bf16[3,2,2,144,128]{4,3,2,1,0:T(8,128)(2,1)S(1)} %collective-permute-done.7), channel_id=1, source_target_pairs={{2,0},{4,2},{6,4},{7,6},{5,7},{3,5},{1,3},{0,1},{10,8},{12,10},{14... | collective-permute-start | bytes 1327112 | tf_op jit(solution)/shard_map/ppermute | solution.py:130
  58.5 12.1 %collective-permute-start.10 = (bf16[3,2,2,144,128]{4,3,2,1,0:T(8,128)(2,1)S(1)}, bf16[3,2,2,144,128]{4,3,2,1,0:T(8,128)(2,1)S(1)}, u32[]{:S(2)}, u32[]{:S(2)}) collective-permute-start(bf16[3,2,2,144,128]{4,3,2,1,0:T(8,128)(2,1)S(1)} %collective-permute-done.8), channel_id=1, source_target_pairs={{0,2},{2,4},{4,6},{6,7},{7,5},{5,3},{3,1},{1,0},{8,10},{10,12},{12... | collective-permute-start | bytes 1327112 | tf_op jit(solution)/shard_map/ppermute | solution.py:129
  60.9 10.3 %collective-permute-start.11 = (bf16[3,2,2,144,128]{4,3,2,1,0:T(8,128)(2,1)S(1)}, bf16[3,2,2,144,128]{4,3,2,1,0:T(8,128)(2,1)S(1)}, u32[]{:S(2)}, u32[]{:S(2)}) collective-permute-start(bf16[3,2,2,144,128]{4,3,2,1,0:T(8,128)(2,1)S(1)} %collective-permute-done.9), channel_id=1, source_target_pairs={{2,0},{4,2},{6,4},{7,6},{5,7},{3,5},{1,3},{0,1},{10,8},{12,10},{14... | collective-permute-start | bytes 1327112 | tf_op jit(solution)/shard_map/ppermute | solution.py:130
  61.0 35.8 %collective-permute-start.18 = (bf16[3,12,144,128]{3,2,1,0:T(8,128)(2,1)S(1)}, bf16[3,12,144,128]{3,2,1,0:T(8,128)(2,1)}, u32[]{:S(2)}, u32[]{:S(2)}) collective-permute-start(bf16[3,12,144,128]{3,2,1,0:T(8,128)(2,1)S(1)} %bitcast_dynamic-update-slice_fusion), channel_id=1, source_target_pairs={{0,16},{1,17},{10,26},{11,27},{20,4},{21,5},{30,14},{31,15}} | collective-permute-start | bytes 3981320 | tf_op jit(solution)/shard_map/ppermute | solution.py:105
  68.8 39.2 %collective-permute-start.16 = (bf16[3,12,144,128]{3,2,1,0:T(8,128)(2,1)}, bf16[3,12,144,128]{3,2,1,0:T(8,128)(2,1)}, u32[]{:S(2)}, u32[]{:S(2)}) collective-permute-start(bf16[3,12,144,128]{3,2,1,0:T(8,128)(2,1)} %collective-permute-done.15), channel_id=1, source_target_pairs={{16,24},{17,25},{26,18},{27,19},{4,12},{5,13},{14,6},{15,7}} | collective-permute-start | bytes 3981320 | tf_op jit(solution)/shard_map/ppermute | solution.py:105
  70.5 8.3 %collective-permute-start.12 = (bf16[3,2,2,144,128]{4,3,2,1,0:T(8,128)(2,1)S(1)}, bf16[3,2,2,144,128]{4,3,2,1,0:T(8,128)(2,1)S(1)}, u32[]{:S(2)}, u32[]{:S(2)}) collective-permute-start(bf16[3,2,2,144,128]{4,3,2,1,0:T(8,128)(2,1)S(1)} %collective-permute-done.10), channel_id=1, source_target_pairs={{0,2},{2,4},{4,6},{6,7},{7,5},{5,3},{3,1},{1,0},{8,10},{10,12},{12... | collective-permute-start | bytes 1327112 | tf_op jit(solution)/shard_map/ppermute | solution.py:129
  71.3 13.7 %collective-permute-start.13 = (bf16[3,2,2,144,128]{4,3,2,1,0:T(8,128)(2,1)S(1)}, bf16[3,2,2,144,128]{4,3,2,1,0:T(8,128)(2,1)S(1)}, u32[]{:S(2)}, u32[]{:S(2)}) collective-permute-start(bf16[3,2,2,144,128]{4,3,2,1,0:T(8,128)(2,1)S(1)} %collective-permute-done.11), channel_id=1, source_target_pairs={{2,0},{4,2},{6,4},{7,6},{5,7},{3,5},{1,3},{0,1},{10,8},{12,10},{14... | collective-permute-start | bytes 1327112 | tf_op jit(solution)/shard_map/ppermute | solution.py:130
  78.8 11.6 %collective-permute-start.21 = (bf16[3,4,144,128]{3,2,1,0:T(8,128)(2,1)S(1)}, bf16[3,4,144,128]{3,2,1,0:T(8,128)(2,1)}, u32[]{:S(2)}, u32[]{:S(2)}) collective-permute-start(bf16[3,4,144,128]{3,2,1,0:T(8,128)(2,1)S(1)} %pad_maximum_fusion.1), channel_id=1, source_target_pairs={{0,16},{1,17},{10,26},{11,27},{20,4},{21,5},{30,14},{31,15}} | collective-permute-start | bytes 1327112 | tf_op jit(solution)/shard_map/ppermute | solution.py:105
  85.0 10.3 %collective-permute-start.20 = (bf16[3,4,144,128]{3,2,1,0:T(8,128)(2,1)S(1)}, bf16[3,4,144,128]{3,2,1,0:T(8,128)(2,1)S(1)}, u32[]{:S(2)}, u32[]{:S(2)}) collective-permute-start(bf16[3,4,144,128]{3,2,1,0:T(8,128)(2,1)S(1)} %pad_maximum_fusion.1), channel_id=1, source_target_pairs={{0,8},{1,9},{10,2},{11,3},{20,28},{21,29},{30,22},{31,23}} | collective-permute-start | bytes 1327112 | tf_op jit(solution)/shard_map/ppermute | solution.py:105
  88.0 14.0 %copy-start = (bf16[3,12,144,128]{3,2,1,0:T(8,128)(2,1)}, bf16[3,12,144,128]{3,2,1,0:T(8,128)(2,1)S(1)}, u32[]{:S(2)}) copy-start(bf16[3,12,144,128]{3,2,1,0:T(8,128)(2,1)S(1)} %collective-permute-done.14) | copy-start | bytes 3981316
  88.0 21.7 %collective-permute-start.17 = (bf16[3,12,144,128]{3,2,1,0:T(8,128)(2,1)S(1)}, bf16[3,12,144,128]{3,2,1,0:T(8,128)(2,1)}, u32[]{:S(2)}, u32[]{:S(2)}) collective-permute-start(bf16[3,12,144,128]{3,2,1,0:T(8,128)(2,1)S(1)} %bitcast_dynamic-update-slice_fusion), channel_id=1, source_target_pairs={{0,8},{1,9},{10,2},{11,3},{20,28},{21,29},{30,22},{31,23}} | collective-permute-start | bytes 3981320 | tf_op jit(solution)/shard_map/ppermute | solution.py:105
  90.4 15.8 %collective-permute-start.24 = (bf16[3,4,144,128]{3,2,1,0:T(8,128)(2,1)}, bf16[3,4,144,128]{3,2,1,0:T(8,128)(2,1)}, u32[]{:S(2)}, u32[]{:S(2)}) collective-permute-start(bf16[3,4,144,128]{3,2,1,0:T(8,128)(2,1)} %pad_maximum_fusion.2), channel_id=1, source_target_pairs={{0,16},{1,17},{10,26},{11,27},{20,4},{21,5},{30,14},{31,15}} | collective-permute-start | bytes 1327112 | tf_op jit(solution)/shard_map/ppermute | solution.py:105
  95.3 6.7 %copy-start.2 = (bf16[3,4,144,128]{3,2,1,0:T(8,128)(2,1)}, bf16[3,4,144,128]{3,2,1,0:T(8,128)(2,1)S(1)}, u32[]{:S(2)}) copy-start(bf16[3,4,144,128]{3,2,1,0:T(8,128)(2,1)S(1)} %collective-permute-done.20) | copy-start | bytes 1327108
  95.3 9.4 %collective-permute-start.22 = (bf16[3,4,144,128]{3,2,1,0:T(8,128)(2,1)}, bf16[3,4,144,128]{3,2,1,0:T(8,128)(2,1)}, u32[]{:S(2)}, u32[]{:S(2)}) collective-permute-start(bf16[3,4,144,128]{3,2,1,0:T(8,128)(2,1)} %collective-permute-done.21), channel_id=1, source_target_pairs={{16,24},{17,25},{26,18},{27,19},{4,12},{5,13},{14,6},{15,7}} | collective-permute-start | bytes 1327112 | tf_op jit(solution)/shard_map/ppermute | solution.py:105
  96.8 13.0 %collective-permute-start.19 = (bf16[3,12,144,128]{3,2,1,0:T(8,128)(2,1)}, bf16[3,12,144,128]{3,2,1,0:T(8,128)(2,1)}, u32[]{:S(2)}, u32[]{:S(2)}) collective-permute-start(bf16[3,12,144,128]{3,2,1,0:T(8,128)(2,1)} %collective-permute-done.18), channel_id=1, source_target_pairs={{16,24},{17,25},{26,18},{27,19},{4,12},{5,13},{14,6},{15,7}} | collective-permute-start | bytes 3981320 | tf_op jit(solution)/shard_map/ppermute | solution.py:105
  104.7 3.3 %copy-start.1 = (bf16[3,12,144,128]{3,2,1,0:T(8,128)(2,1)S(1)}, bf16[3,12,144,128]{3,2,1,0:T(8,128)(2,1)}, u32[]{:S(2)}) copy-start(bf16[3,12,144,128]{3,2,1,0:T(8,128)(2,1)} %copy-done) | copy-start | bytes 3981316
  104.7 4.9 %collective-permute-start.23 = (bf16[3,4,144,128]{3,2,1,0:T(8,128)(2,1)}, bf16[3,4,144,128]{3,2,1,0:T(8,128)(2,1)S(1)}, u32[]{:S(2)}, u32[]{:S(2)}) collective-permute-start(bf16[3,4,144,128]{3,2,1,0:T(8,128)(2,1)} %pad_maximum_fusion.2), channel_id=1, source_target_pairs={{0,8},{1,9},{10,2},{11,3},{20,28},{21,29},{30,22},{31,23}} | collective-permute-start | bytes 1327112 | tf_op jit(solution)/shard_map/ppermute | solution.py:105
  106.2 3.4 %collective-permute-start.25 = (bf16[3,4,144,128]{3,2,1,0:T(8,128)(2,1)}, bf16[3,4,144,128]{3,2,1,0:T(8,128)(2,1)S(1)}, u32[]{:S(2)}, u32[]{:S(2)}) collective-permute-start(bf16[3,4,144,128]{3,2,1,0:T(8,128)(2,1)} %collective-permute-done.24), channel_id=1, source_target_pairs={{16,24},{17,25},{26,18},{27,19},{4,12},{5,13},{14,6},{15,7}} | collective-permute-start | bytes 1327112 | tf_op jit(solution)/shard_map/ppermute | solution.py:105

commit v23 on v20

--- a/solution.py
+++ b/solution.py
@@ -79,7 +79,6 @@
     panels, _, local_slots, blk, _ = panel_blocks.shape
     r = lax.axis_index("row")
     c = lax.axis_index("col")
-    x = with_meta(panel_blocks, user_weights, slot_offset)
 
     outer = ncol // 2
     cycle = [a * 2 for a in range(outer)] + [a * 2 + 1 for a in reversed(range(outer))]
@@ -121,8 +120,9 @@
         return lax.dynamic_index_in_dim(piece, slot, axis=2, keepdims=False)
 
     batches = [[k, k + 1] for k in range(0, ncol - 2, 2)] + [[ncol - 2], [ncol - 1]]
-    half = x.shape[1] // 2
-    a, b = x[:, :half], x[:, half:]
+    half = panel_blocks.shape[1] // 2
+    a = with_meta(panel_blocks[:, :half], user_weights[:, :half], slot_offset[:, :half])
+    b = with_meta(panel_blocks[:, half:], user_weights[:, half:], slot_offset[:, half:])
     pieces, columns, pending = [], [], []
     for step in range(ncol):
         if step:

time: 124 us -> 125 us (level)
  local copies, waits for them, and re-layouts: 18 us -> 19.3 us
    ppermute x7, waiting for transfers between devices: 35 us -> 0.37 us  [local(): a = lax.ppermute(a, 'col', forward)]
    ppermute x7, waiting for transfers between devices: 0.02 us -> 34.2 us  [local(): b = lax.ppermute(b, 'col', backward)]
    ppermute x7, starting transfers between devices: 4.8 us -> 12.3 us  [local(): b = lax.ppermute(b, 'col', backward)]
    ppermute x7, starting transfers between devices: 10.5 us -> 3.31 us  [local(): a = lax.ppermute(a, 'col', forward)]
    slice x1 -> x4, local copies, waits for them, and re-layouts: 0.06 us -> 1.5 us  [the longest x1 1.19 us: local(): panel_blocks[:, :half]]
    unnamed x5 -> x6, other arithmetic: 6.78 us -> 6.31 us
  transfers between devices with their start and end apart: 29 -> 29, of which waited for: 7 -> 9; matrix products, arithmetic and copies ran while one was open for 18% -> 18% of each run, Pallas kernels for 0% -> 0%
where the time goes in v23:
time: 125 us; the launch traced here: 123 us
  starting transfers between devices  46.2 us (37%)
  waiting for transfers between devices  34.6 us (28%)
  local copies, waits for them, and re-layouts  19.3 us (15%)
  other arithmetic  12.1 us (10%)
  Pallas kernels  10.8 us (9%)
    ppermute x7, waiting for transfers between devices, local(): b = lax.ppermute(b, 'col', backward)  34.2 us
    ppermute x15, starting transfers between devices, send(): lax.ppermute(v, ('row', 'col'), [(a * ncol + cc, b * ncol + cc) for a, b,...  30.5 us
    ppermute x7, starting transfers between devices, local(): b = lax.ppermute(b, 'col', backward)  12.3 us
    unnamed x29, local copies, waits for them, and re-layouts  11.2 us
    pallas_call x1, Pallas kernels, gram_call(): pl.pallas_call(kernel, grid_spec=pltpu.PrefetchScalarGridSpec(num_scalar_...  10.8 us
    unnamed x6, other arithmetic  6.31 us
    ppermute x7, starting transfers between devices, local(): a = lax.ppermute(a, 'col', forward)  3.31 us
    concatenate x5, other arithmetic, local(): own = jnp.concatenate(pending, axis=1)  3 us
  transfers between devices with their start and end apart: 29, of which 9 were waited for; matrix products, arithmetic and copies ran while one was open for 18% of the time, Pallas kernels for 0%

profile of v23, /device:TPU:0, one launch (start us, length us, event | category | flops | bytes accessed | tf_op | source)
XLA Modules:
  0.0 123.4 jit_solution(17123436425281680223)
XLA Ops:
  1.8 1.2 fusion.8
  5.3 3.0 %collective-permute-start.1 = (bf16[3,2,2,144,128]{4,3,2,1,0:T(8,128)(2,1)S(1)}, bf16[3,2,2,144,128]{4,3,2,1,0:T(8,128)(2,1)S(1)}, u32[]{:S(2)}, u32[]{:S(2)}) collective-permute-start(bf16[3,2,2,144,128]{4,3,2,1,0:T(8,128)(2,1)S(1)} %get-tuple-element.8), channel_id=1, source_target_pairs={{2,0},{4,2},{6,4},{7,6},{5,7},{3,5},{1,3},{0,1},{10,8},{12,10},{14... | collective-permute-start | bytes 1327112 | tf_op jit(solution)/shard_map/ppermute | solution.py:130
  8.3 10.1 %collective-permute-done.1 = bf16[3,2,2,144,128]{4,3,2,1,0:T(8,128)(2,1)S(1)} collective-permute-done((bf16[3,2,2,144,128]{4,3,2,1,0:T(8,128)(2,1)S(1)}, bf16[3,2,2,144,128]{4,3,2,1,0:T(8,128)(2,1)S(1)}, u32[]{:S(2)}, u32[]{:S(2)}) %collective-permute-start.1) | collective-permute-done | bytes 442400 | tf_op jit(solution)/shard_map/ppermute | solution.py:130
  18.4 1.7 %collective-permute-start.3 = (bf16[3,2,2,144,128]{4,3,2,1,0:T(8,128)(2,1)S(1)}, bf16[3,2,2,144,128]{4,3,2,1,0:T(8,128)(2,1)S(1)}, u32[]{:S(2)}, u32[]{:S(2)}) collective-permute-start(bf16[3,2,2,144,128]{4,3,2,1,0:T(8,128)(2,1)S(1)} %collective-permute-done.1), channel_id=1, source_target_pairs={{2,0},{4,2},{6,4},{7,6},{5,7},{3,5},{1,3},{0,1},{10,8},{12,10},{14... | collective-permute-start | bytes 1327112 | tf_op jit(solution)/shard_map/ppermute | solution.py:130
  20.7 3.6 %collective-permute-start.15 = (bf16[3,8,144,128]{3,2,1,0:T(8,128)(2,1)S(1)}, bf16[3,8,144,128]{3,2,1,0:T(8,128)(2,1)S(1)}, u32[]{:S(2)}, u32[]{:S(2)}) collective-permute-start(bf16[3,8,144,128]{3,2,1,0:T(8,128)(2,1)S(1)} %pad_maximum_fusion), channel_id=1, source_target_pairs={{0,16},{1,17},{10,26},{11,27},{20,4},{21,5},{30,14},{31,15}} | collective-permute-start | bytes 2654216 | tf_op jit(solution)/shard_map/ppermute | solution.py:104
  24.3 1.3 %collective-permute-start.14 = (bf16[3,8,144,128]{3,2,1,0:T(8,128)(2,1)S(1)}, bf16[3,8,144,128]{3,2,1,0:T(8,128)(2,1)S(1)}, u32[]{:S(2)}, u32[]{:S(2)}) collective-permute-start(bf16[3,8,144,128]{3,2,1,0:T(8,128)(2,1)S(1)} %pad_maximum_fusion), channel_id=1, source_target_pairs={{0,8},{1,9},{10,2},{11,3},{20,28},{21,29},{30,22},{31,23}} | collective-permute-start | bytes 2654216 | tf_op jit(solution)/shard_map/ppermute | solution.py:104
  27.4 2.4 %collective-permute-done.3 = bf16[3,2,2,144,128]{4,3,2,1,0:T(8,128)(2,1)S(1)} collective-permute-done((bf16[3,2,2,144,128]{4,3,2,1,0:T(8,128)(2,1)S(1)}, bf16[3,2,2,144,128]{4,3,2,1,0:T(8,128)(2,1)S(1)}, u32[]{:S(2)}, u32[]{:S(2)}) %collective-permute-start.3) | collective-permute-done | bytes 442400 | tf_op jit(solution)/shard_map/ppermute | solution.py:130
  29.8 1.4 %collective-permute-start.5 = (bf16[3,2,2,144,128]{4,3,2,1,0:T(8,128)(2,1)S(1)}, bf16[3,2,2,144,128]{4,3,2,1,0:T(8,128)(2,1)S(1)}, u32[]{:S(2)}, u32[]{:S(2)}) collective-permute-start(bf16[3,2,2,144,128]{4,3,2,1,0:T(8,128)(2,1)S(1)} %collective-permute-done.3), channel_id=1, source_target_pairs={{2,0},{4,2},{6,4},{7,6},{5,7},{3,5},{1,3},{0,1},{10,8},{12,10},{14... | collective-permute-start | bytes 1327112 | tf_op jit(solution)/shard_map/ppermute | solution.py:130
  33.6 6.7 %collective-permute-done.5 = bf16[3,2,2,144,128]{4,3,2,1,0:T(8,128)(2,1)S(1)} collective-permute-done((bf16[3,2,2,144,128]{4,3,2,1,0:T(8,128)(2,1)S(1)}, bf16[3,2,2,144,128]{4,3,2,1,0:T(8,128)(2,1)S(1)}, u32[]{:S(2)}, u32[]{:S(2)}) %collective-permute-start.5) | collective-permute-done | bytes 442400 | tf_op jit(solution)/shard_map/ppermute | solution.py:130
  40.2 1.3 %collective-permute-start.7 = (bf16[3,2,2,144,128]{4,3,2,1,0:T(8,128)(2,1)S(1)}, bf16[3,2,2,144,128]{4,3,2,1,0:T(8,128)(2,1)S(1)}, u32[]{:S(2)}, u32[]{:S(2)}) collective-permute-start(bf16[3,2,2,144,128]{4,3,2,1,0:T(8,128)(2,1)S(1)} %collective-permute-done.5), channel_id=1, source_target_pairs={{2,0},{4,2},{6,4},{7,6},{5,7},{3,5},{1,3},{0,1},{10,8},{12,10},{14... | collective-permute-start | bytes 1327112 | tf_op jit(solution)/shard_map/ppermute | solution.py:130
  42.4 3.2 %collective-permute-start.18 = (bf16[3,8,144,128]{3,2,1,0:T(8,128)(2,1)S(1)}, bf16[3,8,144,128]{3,2,1,0:T(8,128)(2,1)S(1)}, u32[]{:S(2)}, u32[]{:S(2)}) collective-permute-start(bf16[3,8,144,128]{3,2,1,0:T(8,128)(2,1)S(1)} %pad_maximum_fusion.1), channel_id=1, source_target_pairs={{0,16},{1,17},{10,26},{11,27},{20,4},{21,5},{30,14},{31,15}} | collective-permute-start | bytes 2654216 | tf_op jit(solution)/shard_map/ppermute | solution.py:104
  48.1 2.5 %collective-permute-done.7 = bf16[3,2,2,144,128]{4,3,2,1,0:T(8,128)(2,1)S(1)} collective-permute-done((bf16[3,2,2,144,128]{4,3,2,1,0:T(8,128)(2,1)S(1)}, bf16[3,2,2,144,128]{4,3,2,1,0:T(8,128)(2,1)S(1)}, u32[]{:S(2)}, u32[]{:S(2)}) %collective-permute-start.7) | collective-permute-done | bytes 442400 | tf_op jit(solution)/shard_map/ppermute | solution.py:130
  50.6 1.3 %collective-permute-start.9 = (bf16[3,2,2,144,128]{4,3,2,1,0:T(8,128)(2,1)S(1)}, bf16[3,2,2,144,128]{4,3,2,1,0:T(8,128)(2,1)S(1)}, u32[]{:S(2)}, u32[]{:S(2)}) collective-permute-start(bf16[3,2,2,144,128]{4,3,2,1,0:T(8,128)(2,1)S(1)} %collective-permute-done.7), channel_id=1, source_target_pairs={{2,0},{4,2},{6,4},{7,6},{5,7},{3,5},{1,3},{0,1},{10,8},{12,10},{14... | collective-permute-start | bytes 1327112 | tf_op jit(solution)/shard_map/ppermute | solution.py:130
  54.4 6.5 %collective-permute-done.9 = bf16[3,2,2,144,128]{4,3,2,1,0:T(8,128)(2,1)S(1)} collective-permute-done((bf16[3,2,2,144,128]{4,3,2,1,0:T(8,128)(2,1)S(1)}, bf16[3,2,2,144,128]{4,3,2,1,0:T(8,128)(2,1)S(1)}, u32[]{:S(2)}, u32[]{:S(2)}) %collective-permute-start.9) | collective-permute-done | bytes 442400 | tf_op jit(solution)/shard_map/ppermute | solution.py:130
  60.9 1.3 %collective-permute-start.11 = (bf16[3,2,2,144,128]{4,3,2,1,0:T(8,128)(2,1)S(1)}, bf16[3,2,2,144,128]{4,3,2,1,0:T(8,128)(2,1)S(1)}, u32[]{:S(2)}, u32[]{:S(2)}) collective-permute-start(bf16[3,2,2,144,128]{4,3,2,1,0:T(8,128)(2,1)S(1)} %collective-permute-done.9), channel_id=1, source_target_pairs={{2,0},{4,2},{6,4},{7,6},{5,7},{3,5},{1,3},{0,1},{10,8},{12,10},{14... | collective-permute-start | bytes 1327112 | tf_op jit(solution)/shard_map/ppermute | solution.py:130
  63.9 1.0 pad_maximum_fusion.2
  65.8 1.3 %collective-permute-start.17 = (bf16[3,8,144,128]{3,2,1,0:T(8,128)(2,1)S(1)}, bf16[3,8,144,128]{3,2,1,0:T(8,128)(2,1)S(1)}, u32[]{:S(2)}, u32[]{:S(2)}) collective-permute-start(bf16[3,8,144,128]{3,2,1,0:T(8,128)(2,1)S(1)} %pad_maximum_fusion.1), channel_id=1, source_target_pairs={{0,8},{1,9},{10,2},{11,3},{20,28},{21,29},{30,22},{31,23}} | collective-permute-start | bytes 2654216 | tf_op jit(solution)/shard_map/ppermute | solution.py:104
  67.1 2.6 %collective-permute-start.21 = (bf16[3,8,144,128]{3,2,1,0:T(8,128)(2,1)}, bf16[3,8,144,128]{3,2,1,0:T(8,128)(2,1)}, u32[]{:S(2)}, u32[]{:S(2)}) collective-permute-start(bf16[3,8,144,128]{3,2,1,0:T(8,128)(2,1)} %pad_maximum_fusion.2), channel_id=1, source_target_pairs={{0,16},{1,17},{10,26},{11,27},{20,4},{21,5},{30,14},{31,15}} | collective-permute-start | bytes 2654216 | tf_op jit(solution)/shard_map/ppermute | solution.py:104
  71.0 2.5 %collective-permute-start.13 = (bf16[3,2,2,144,128]{4,3,2,1,0:T(8,128)(2,1)S(1)}, bf16[3,2,2,144,128]{4,3,2,1,0:T(8,128)(2,1)S(1)}, u32[]{:S(2)}, u32[]{:S(2)}) collective-permute-start(bf16[3,2,2,144,128]{4,3,2,1,0:T(8,128)(2,1)S(1)} %collective-permute-done.11), channel_id=1, source_target_pairs={{2,0},{4,2},{6,4},{7,6},{5,7},{3,5},{1,3},{0,1},{10,8},{12,10},{14... | collective-permute-start | bytes 1327112 | tf_op jit(solution)/shard_map/ppermute | solution.py:130
  76.1 6.0 %collective-permute-done.13 = bf16[3,2,2,144,128]{4,3,2,1,0:T(8,128)(2,1)S(1)} collective-permute-done((bf16[3,2,2,144,128]{4,3,2,1,0:T(8,128)(2,1)S(1)}, bf16[3,2,2,144,128]{4,3,2,1,0:T(8,128)(2,1)S(1)}, u32[]{:S(2)}, u32[]{:S(2)}) %collective-permute-start.13) | collective-permute-done | bytes 442400 | tf_op jit(solution)/shard_map/ppermute | solution.py:130
  82.1 2.3 %collective-permute-start.20 = (bf16[3,8,144,128]{3,2,1,0:T(8,128)(2,1)}, bf16[3,8,144,128]{3,2,1,0:T(8,128)(2,1)}, u32[]{:S(2)}, u32[]{:S(2)}) collective-permute-start(bf16[3,8,144,128]{3,2,1,0:T(8,128)(2,1)} %pad_maximum_fusion.2), channel_id=1, source_target_pairs={{0,8},{1,9},{10,2},{11,3},{20,28},{21,29},{30,22},{31,23}} | collective-permute-start | bytes 2654216 | tf_op jit(solution)/shard_map/ppermute | solution.py:104
  84.7 2.6 %collective-permute-start.24 = (bf16[3,4,144,128]{3,2,1,0:T(8,128)(2,1)}, bf16[3,4,144,128]{3,2,1,0:T(8,128)(2,1)}, u32[]{:S(2)}, u32[]{:S(2)}) collective-permute-start(bf16[3,4,144,128]{3,2,1,0:T(8,128)(2,1)} %pad_maximum_fusion.3), channel_id=1, source_target_pairs={{0,16},{1,17},{10,26},{11,27},{20,4},{21,5},{30,14},{31,15}} | collective-permute-start | bytes 1327112 | tf_op jit(solution)/shard_map/ppermute | solution.py:104
  87.3 1.6 %collective-permute-start.22 = (bf16[3,8,144,128]{3,2,1,0:T(8,128)(2,1)}, bf16[3,8,144,128]{3,2,1,0:T(8,128)(2,1)}, u32[]{:S(2)}, u32[]{:S(2)}) collective-permute-start(bf16[3,8,144,128]{3,2,1,0:T(8,128)(2,1)} %collective-permute-done.21), channel_id=1, source_target_pairs={{16,24},{17,25},{26,18},{27,19},{4,12},{5,13},{14,6},{15,7}} | collective-permute-start | bytes 2654216 | tf_op jit(solution)/shard_map/ppermute | solution.py:104
  90.6 2.1 %collective-permute-start.23 = (bf16[3,4,144,128]{3,2,1,0:T(8,128)(2,1)}, bf16[3,4,144,128]{3,2,1,0:T(8,128)(2,1)}, u32[]{:S(2)}, u32[]{:S(2)}) collective-permute-start(bf16[3,4,144,128]{3,2,1,0:T(8,128)(2,1)} %pad_maximum_fusion.3), channel_id=1, source_target_pairs={{0,8},{1,9},{10,2},{11,3},{20,28},{21,29},{30,22},{31,23}} | collective-permute-start | bytes 1327112 | tf_op jit(solution)/shard_map/ppermute | solution.py:104
  92.7 5.0 %collective-permute-start.27 = (bf16[3,4,144,128]{3,2,1,0:T(8,128)(2,1)}, bf16[3,4,144,128]{3,2,1,0:T(8,128)(2,1)}, u32[]{:S(2)}, u32[]{:S(2)}) collective-permute-start(bf16[3,4,144,128]{3,2,1,0:T(8,128)(2,1)} %pad_maximum_fusion.4), channel_id=1, source_target_pairs={{0,16},{1,17},{10,26},{11,27},{20,4},{21,5},{30,14},{31,15}} | collective-permute-start | bytes 1327112 | tf_op jit(solution)/shard_map/ppermute | solution.py:104
  97.8 1.5 %collective-permute-start.25 = (bf16[3,4,144,128]{3,2,1,0:T(8,128)(2,1)}, bf16[3,4,144,128]{3,2,1,0:T(8,128)(2,1)}, u32[]{:S(2)}, u32[]{:S(2)}) collective-permute-start(bf16[3,4,144,128]{3,2,1,0:T(8,128)(2,1)} %collective-permute-done.24), channel_id=1, source_target_pairs={{16,24},{17,25},{26,18},{27,19},{4,12},{5,13},{14,6},{15,7}} | collective-permute-start | bytes 1327112 | tf_op jit(solution)/shard_map/ppermute | solution.py:104
  100.6 1.8 %slice.36 = bf16[96,2,1,1]{3,2,1,0:T(2,128)(2,1)} slice(bf16[96,2,144,128]{3,2,1,0:T(8,128)(2,1)} %bitcast.6.bs_ref), slice={[0:96], [0:2], [131:132], [0:1]} | slice | bytes 768 | tf_op jit(solution)/shard_map/slice | solution.py:150
  103.3 1.3 %collective-permute-start.26 = (bf16[3,4,144,128]{3,2,1,0:T(8,128)(2,1)}, bf16[3,4,144,128]{3,2,1,0:T(8,128)(2,1)S(1)}, u32[]{:S(2)}, u32[]{:S(2)}) collective-permute-start(bf16[3,4,144,128]{3,2,1,0:T(8,128)(2,1)} %pad_maximum_fusion.4), channel_id=1, source_target_pairs={{0,8},{1,9},{10,2},{11,3},{20,28},{21,29},{30,22},{31,23}} | collective-permute-start | bytes 1327112 | tf_op jit(solution)/shard_map/ppermute | solution.py:104
  105.4 1.9 %select_dynamic-update-slice_fusion = bf16[3,32,144,128]{3,2,1,0:T(8,128)(2,1)S(1)} fusion(bf16[3,32,144,128]{3,2,1,0:T(8,128)(2,1)S(1)} %select_dynamic-update-slice_fusion.1, bf16[3,8,144,128]{3,2,1,0:T(8,128)(2,1)} %collective-permute-done.20, bf16[3,8,144,128]{3,2,1,0:T(8,128)(2,1)} %collective-permute-done.21, ...), kind=kLoop, calls=%fused_computation.3 | loop fusion | flops 4866048 | bytes 4423683
  107.3 1.5 %select_dynamic-update-slice_fusion.4 = bf16[3,32,144,128]{3,2,1,0:T(8,128)(2,1)S(1)} fusion(bf16[3,32,144,128]{3,2,1,0:T(8,128)(2,1)S(1)} %select_dynamic-update-slice_fusion, bf16[3,4,144,128]{3,2,1,0:T(8,128)(2,1)} %collective-permute-done.23, bf16[3,4,144,128]{3,2,1,0:T(8,128)(2,1)} %collective-permute-done.24, ...), kind=kLoop, calls=%fused_computation.11 | loop fusion | flops 1548288 | bytes 2211843
  108.8 1.3 %select_dynamic-update-slice_fusion.3 = bf16[3,32,144,128]{3,2,1,0:T(8,128)(2,1)S(1)} fusion(bf16[3,32,144,128]{3,2,1,0:T(8,128)(2,1)S(1)} %select_dynamic-update-slice_fusion.4, bf16[3,4,144,128]{3,2,1,0:T(8,128)(2,1)S(1)} %collective-permute-done.26, bf16[3,4,144,128]{3,2,1,0:T(8,128)(2,1)} %collective-permute-done.27, ...), kind=kLoop, calls=%fused_computation.10 | loop fusion | flops 1548288 | bytes 2211843 | tf_op jit(solution)/shard_map/concatenate | solution.py:145
  112.6 10.8 %shard_map.37 = f32[2048,1024]{1,0:T(8,128)} custom-call(s32[288]{0:T(512)S(1)} %min.12.offs_ref, bf16[96,2,144,128]{3,2,1,0:T(8,128)(2,1)} %bitcast.6.bs_ref, bf16[96,144,128]{2,1,0:T(8,128)(2,1)S(1)} %bitcast.49), custom_call_target="tpu_custom_call" | custom-call | flops 805306368 | bytes 17825792 | tf_op jit(solution)/shard_map/pallas_call | solution.py:40
  (106 shorter events, 28.7 us)
Async XLA Ops:
  5.3 13.2 %collective-permute-start.1 = (bf16[3,2,2,144,128]{4,3,2,1,0:T(8,128)(2,1)S(1)}, bf16[3,2,2,144,128]{4,3,2,1,0:T(8,128)(2,1)S(1)}, u32[]{:S(2)}, u32[]{:S(2)}) collective-permute-start(bf16[3,2,2,144,128]{4,3,2,1,0:T(8,128)(2,1)S(1)} %get-tuple-element.8), channel_id=1, source_target_pairs={{2,0},{4,2},{6,4},{7,6},{5,7},{3,5},{1,3},{0,1},{10,8},{12,10},{14... | collective-permute-start | bytes 1327112 | tf_op jit(solution)/shard_map/ppermute | solution.py:130
  8.2 11.9 %collective-permute-start = (bf16[3,2,2,144,128]{4,3,2,1,0:T(8,128)(2,1)S(1)}, bf16[3,2,2,144,128]{4,3,2,1,0:T(8,128)(2,1)S(1)}, u32[]{:S(2)}, u32[]{:S(2)}) collective-permute-start(bf16[3,2,2,144,128]{4,3,2,1,0:T(8,128)(2,1)S(1)} %get-tuple-element.10), channel_id=1, source_target_pairs={{0,2},{2,4},{4,6},{6,7},{7,5},{5,3},{3,1},{1,0},{8,10},{10,12},{12... | collective-permute-start | bytes 1327112 | tf_op jit(solution)/shard_map/ppermute | solution.py:129
  18.4 11.4 %collective-permute-start.3 = (bf16[3,2,2,144,128]{4,3,2,1,0:T(8,128)(2,1)S(1)}, bf16[3,2,2,144,128]{4,3,2,1,0:T(8,128)(2,1)S(1)}, u32[]{:S(2)}, u32[]{:S(2)}) collective-permute-start(bf16[3,2,2,144,128]{4,3,2,1,0:T(8,128)(2,1)S(1)} %collective-permute-done.1), channel_id=1, source_target_pairs={{2,0},{4,2},{6,4},{7,6},{5,7},{3,5},{1,3},{0,1},{10,8},{12,10},{14... | collective-permute-start | bytes 1327112 | tf_op jit(solution)/shard_map/ppermute | solution.py:130
  20.2 11.0 %collective-permute-start.2 = (bf16[3,2,2,144,128]{4,3,2,1,0:T(8,128)(2,1)S(1)}, bf16[3,2,2,144,128]{4,3,2,1,0:T(8,128)(2,1)S(1)}, u32[]{:S(2)}, u32[]{:S(2)}) collective-permute-start(bf16[3,2,2,144,128]{4,3,2,1,0:T(8,128)(2,1)S(1)} %collective-permute-done), channel_id=1, source_target_pairs={{0,2},{2,4},{4,6},{6,7},{7,5},{5,3},{3,1},{1,0},{8,10},{10,12},{12... | collective-permute-start | bytes 1327112 | tf_op jit(solution)/shard_map/ppermute | solution.py:129
  20.7 25.0 %collective-permute-start.15 = (bf16[3,8,144,128]{3,2,1,0:T(8,128)(2,1)S(1)}, bf16[3,8,144,128]{3,2,1,0:T(8,128)(2,1)S(1)}, u32[]{:S(2)}, u32[]{:S(2)}) collective-permute-start(bf16[3,8,144,128]{3,2,1,0:T(8,128)(2,1)S(1)} %pad_maximum_fusion), channel_id=1, source_target_pairs={{0,16},{1,17},{10,26},{11,27},{20,4},{21,5},{30,14},{31,15}} | collective-permute-start | bytes 2654216 | tf_op jit(solution)/shard_map/ppermute | solution.py:104
  24.3 41.4 %collective-permute-start.14 = (bf16[3,8,144,128]{3,2,1,0:T(8,128)(2,1)S(1)}, bf16[3,8,144,128]{3,2,1,0:T(8,128)(2,1)S(1)}, u32[]{:S(2)}, u32[]{:S(2)}) collective-permute-start(bf16[3,8,144,128]{3,2,1,0:T(8,128)(2,1)S(1)} %pad_maximum_fusion), channel_id=1, source_target_pairs={{0,8},{1,9},{10,2},{11,3},{20,28},{21,29},{30,22},{31,23}} | collective-permute-start | bytes 2654216 | tf_op jit(solution)/shard_map/ppermute | solution.py:104
  29.8 10.4 %collective-permute-start.5 = (bf16[3,2,2,144,128]{4,3,2,1,0:T(8,128)(2,1)S(1)}, bf16[3,2,2,144,128]{4,3,2,1,0:T(8,128)(2,1)S(1)}, u32[]{:S(2)}, u32[]{:S(2)}) collective-permute-start(bf16[3,2,2,144,128]{4,3,2,1,0:T(8,128)(2,1)S(1)} %collective-permute-done.3), channel_id=1, source_target_pairs={{2,0},{4,2},{6,4},{7,6},{5,7},{3,5},{1,3},{0,1},{10,8},{12,10},{14... | collective-permute-start | bytes 1327112 | tf_op jit(solution)/shard_map/ppermute | solution.py:130
  31.2 10.3 %collective-permute-start.4 = (bf16[3,2,2,144,128]{4,3,2,1,0:T(8,128)(2,1)S(1)}, bf16[3,2,2,144,128]{4,3,2,1,0:T(8,128)(2,1)S(1)}, u32[]{:S(2)}, u32[]{:S(2)}) collective-permute-start(bf16[3,2,2,144,128]{4,3,2,1,0:T(8,128)(2,1)S(1)} %collective-permute-done.2), channel_id=1, source_target_pairs={{0,2},{2,4},{4,6},{6,7},{7,5},{5,3},{3,1},{1,0},{8,10},{10,12},{12... | collective-permute-start | bytes 1327112 | tf_op jit(solution)/shard_map/ppermute | solution.py:129
  40.2 10.3 %collective-permute-start.7 = (bf16[3,2,2,144,128]{4,3,2,1,0:T(8,128)(2,1)S(1)}, bf16[3,2,2,144,128]{4,3,2,1,0:T(8,128)(2,1)S(1)}, u32[]{:S(2)}, u32[]{:S(2)}) collective-permute-start(bf16[3,2,2,144,128]{4,3,2,1,0:T(8,128)(2,1)S(1)} %collective-permute-done.5), channel_id=1, source_target_pairs={{2,0},{4,2},{6,4},{7,6},{5,7},{3,5},{1,3},{0,1},{10,8},{12,10},{14... | collective-permute-start | bytes 1327112 | tf_op jit(solution)/shard_map/ppermute | solution.py:130
  41.5 10.3 %collective-permute-start.6 = (bf16[3,2,2,144,128]{4,3,2,1,0:T(8,128)(2,1)S(1)}, bf16[3,2,2,144,128]{4,3,2,1,0:T(8,128)(2,1)S(1)}, u32[]{:S(2)}, u32[]{:S(2)}) collective-permute-start(bf16[3,2,2,144,128]{4,3,2,1,0:T(8,128)(2,1)S(1)} %collective-permute-done.4), channel_id=1, source_target_pairs={{0,2},{2,4},{4,6},{6,7},{7,5},{5,3},{3,1},{1,0},{8,10},{10,12},{12... | collective-permute-start | bytes 1327112 | tf_op jit(solution)/shard_map/ppermute | solution.py:129
  42.4 27.3 %collective-permute-start.18 = (bf16[3,8,144,128]{3,2,1,0:T(8,128)(2,1)S(1)}, bf16[3,8,144,128]{3,2,1,0:T(8,128)(2,1)S(1)}, u32[]{:S(2)}, u32[]{:S(2)}) collective-permute-start(bf16[3,8,144,128]{3,2,1,0:T(8,128)(2,1)S(1)} %pad_maximum_fusion.1), channel_id=1, source_target_pairs={{0,16},{1,17},{10,26},{11,27},{20,4},{21,5},{30,14},{31,15}} | collective-permute-start | bytes 2654216 | tf_op jit(solution)/shard_map/ppermute | solution.py:104
  45.7 21.4 %collective-permute-start.16 = (bf16[3,8,144,128]{3,2,1,0:T(8,128)(2,1)S(1)}, bf16[3,8,144,128]{3,2,1,0:T(8,128)(2,1)S(1)}, u32[]{:S(2)}, u32[]{:S(2)}) collective-permute-start(bf16[3,8,144,128]{3,2,1,0:T(8,128)(2,1)S(1)} %collective-permute-done.15), channel_id=1, source_target_pairs={{16,24},{17,25},{26,18},{27,19},{4,12},{5,13},{14,6},{15,7}} | collective-permute-start | bytes 2654216 | tf_op jit(solution)/shard_map/ppermute | solution.py:104
  50.6 10.3 %collective-permute-start.9 = (bf16[3,2,2,144,128]{4,3,2,1,0:T(8,128)(2,1)S(1)}, bf16[3,2,2,144,128]{4,3,2,1,0:T(8,128)(2,1)S(1)}, u32[]{:S(2)}, u32[]{:S(2)}) collective-permute-start(bf16[3,2,2,144,128]{4,3,2,1,0:T(8,128)(2,1)S(1)} %collective-permute-done.7), channel_id=1, source_target_pairs={{2,0},{4,2},{6,4},{7,6},{5,7},{3,5},{1,3},{0,1},{10,8},{12,10},{14... | collective-permute-start | bytes 1327112 | tf_op jit(solution)/shard_map/ppermute | solution.py:130
  51.8 10.4 %collective-permute-start.8 = (bf16[3,2,2,144,128]{4,3,2,1,0:T(8,128)(2,1)S(1)}, bf16[3,2,2,144,128]{4,3,2,1,0:T(8,128)(2,1)S(1)}, u32[]{:S(2)}, u32[]{:S(2)}) collective-permute-start(bf16[3,2,2,144,128]{4,3,2,1,0:T(8,128)(2,1)S(1)} %collective-permute-done.6), channel_id=1, source_target_pairs={{0,2},{2,4},{4,6},{6,7},{7,5},{5,3},{3,1},{1,0},{8,10},{10,12},{12... | collective-permute-start | bytes 1327112 | tf_op jit(solution)/shard_map/ppermute | solution.py:129
  52.6 17.1 %copy-start.4 = (bf16[3,2,144,128]{3,2,1,0:T(8,128)(2,1)}, bf16[3,2,144,128]{3,2,1,0:T(8,128)(2,1)S(1)}, u32[]{:S(2)}) copy-start(bf16[3,2,144,128]{3,2,1,0:T(8,128)(2,1)S(1)} %dynamic-slice_bitcast_fusion.6) | copy-start | bytes 663556
  60.9 10.1 %collective-permute-start.11 = (bf16[3,2,2,144,128]{4,3,2,1,0:T(8,128)(2,1)S(1)}, bf16[3,2,2,144,128]{4,3,2,1,0:T(8,128)(2,1)S(1)}, u32[]{:S(2)}, u32[]{:S(2)}) collective-permute-start(bf16[3,2,2,144,128]{4,3,2,1,0:T(8,128)(2,1)S(1)} %collective-permute-done.9), channel_id=1, source_target_pairs={{2,0},{4,2},{6,4},{7,6},{5,7},{3,5},{1,3},{0,1},{10,8},{12,10},{14... | collective-permute-start | bytes 1327112 | tf_op jit(solution)/shard_map/ppermute | solution.py:130
  62.3 11.2 %collective-permute-start.10 = (bf16[3,2,2,144,128]{4,3,2,1,0:T(8,128)(2,1)S(1)}, bf16[3,2,2,144,128]{4,3,2,1,0:T(8,128)(2,1)S(1)}, u32[]{:S(2)}, u32[]{:S(2)}) collective-permute-start(bf16[3,2,2,144,128]{4,3,2,1,0:T(8,128)(2,1)S(1)} %collective-permute-done.8), channel_id=1, source_target_pairs={{0,2},{2,4},{4,6},{6,7},{7,5},{5,3},{3,1},{1,0},{8,10},{10,12},{12... | collective-permute-start | bytes 1327112 | tf_op jit(solution)/shard_map/ppermute | solution.py:129
  65.8 24.9 %collective-permute-start.17 = (bf16[3,8,144,128]{3,2,1,0:T(8,128)(2,1)S(1)}, bf16[3,8,144,128]{3,2,1,0:T(8,128)(2,1)S(1)}, u32[]{:S(2)}, u32[]{:S(2)}) collective-permute-start(bf16[3,8,144,128]{3,2,1,0:T(8,128)(2,1)S(1)} %pad_maximum_fusion.1), channel_id=1, source_target_pairs={{0,8},{1,9},{10,2},{11,3},{20,28},{21,29},{30,22},{31,23}} | collective-permute-start | bytes 2654216 | tf_op jit(solution)/shard_map/ppermute | solution.py:104
  67.1 20.2 %collective-permute-start.21 = (bf16[3,8,144,128]{3,2,1,0:T(8,128)(2,1)}, bf16[3,8,144,128]{3,2,1,0:T(8,128)(2,1)}, u32[]{:S(2)}, u32[]{:S(2)}) collective-permute-start(bf16[3,8,144,128]{3,2,1,0:T(8,128)(2,1)} %pad_maximum_fusion.2), channel_id=1, source_target_pairs={{0,16},{1,17},{10,26},{11,27},{20,4},{21,5},{30,14},{31,15}} | collective-permute-start | bytes 2654216 | tf_op jit(solution)/shard_map/ppermute | solution.py:104
  69.7 28.0 %collective-permute-start.19 = (bf16[3,8,144,128]{3,2,1,0:T(8,128)(2,1)S(1)}, bf16[3,8,144,128]{3,2,1,0:T(8,128)(2,1)S(1)}, u32[]{:S(2)}, u32[]{:S(2)}) collective-permute-start(bf16[3,8,144,128]{3,2,1,0:T(8,128)(2,1)S(1)} %collective-permute-done.18), channel_id=1, source_target_pairs={{16,24},{17,25},{26,18},{27,19},{4,12},{5,13},{14,6},{15,7}} | collective-permute-start | bytes 2654216 | tf_op jit(solution)/shard_map/ppermute | solution.py:104
  71.0 11.1 %collective-permute-start.13 = (bf16[3,2,2,144,128]{4,3,2,1,0:T(8,128)(2,1)S(1)}, bf16[3,2,2,144,128]{4,3,2,1,0:T(8,128)(2,1)S(1)}, u32[]{:S(2)}, u32[]{:S(2)}) collective-permute-start(bf16[3,2,2,144,128]{4,3,2,1,0:T(8,128)(2,1)S(1)} %collective-permute-done.11), channel_id=1, source_target_pairs={{2,0},{4,2},{6,4},{7,6},{5,7},{3,5},{1,3},{0,1},{10,8},{12,10},{14... | collective-permute-start | bytes 1327112 | tf_op jit(solution)/shard_map/ppermute | solution.py:130
  73.5 11.2 %collective-permute-start.12 = (bf16[3,2,2,144,128]{4,3,2,1,0:T(8,128)(2,1)S(1)}, bf16[3,2,2,144,128]{4,3,2,1,0:T(8,128)(2,1)S(1)}, u32[]{:S(2)}, u32[]{:S(2)}) collective-permute-start(bf16[3,2,2,144,128]{4,3,2,1,0:T(8,128)(2,1)S(1)} %collective-permute-done.10), channel_id=1, source_target_pairs={{0,2},{2,4},{4,6},{6,7},{7,5},{5,3},{3,1},{1,0},{8,10},{10,12},{12... | collective-permute-start | bytes 1327112 | tf_op jit(solution)/shard_map/ppermute | solution.py:129
  73.5 24.2 %copy-start = (bf16[3,2,144,128]{3,2,1,0:T(8,128)(2,1)}, bf16[3,2,144,128]{3,2,1,0:T(8,128)(2,1)S(1)}, u32[]{:S(2)}) copy-start(bf16[3,2,144,128]{3,2,1,0:T(8,128)(2,1)S(1)} %dynamic-slice_bitcast_fusion.2) | copy-start | bytes 663556
  73.6 24.2 %copy-start.1 = (bf16[3,2,144,128]{3,2,1,0:T(8,128)(2,1)}, bf16[3,2,144,128]{3,2,1,0:T(8,128)(2,1)S(1)}, u32[]{:S(2)}) copy-start(bf16[3,2,144,128]{3,2,1,0:T(8,128)(2,1)S(1)} %dynamic-slice_bitcast_fusion.3) | copy-start | bytes 663556
  82.1 21.2 %collective-permute-start.20 = (bf16[3,8,144,128]{3,2,1,0:T(8,128)(2,1)}, bf16[3,8,144,128]{3,2,1,0:T(8,128)(2,1)}, u32[]{:S(2)}, u32[]{:S(2)}) collective-permute-start(bf16[3,8,144,128]{3,2,1,0:T(8,128)(2,1)} %pad_maximum_fusion.2), channel_id=1, source_target_pairs={{0,8},{1,9},{10,2},{11,3},{20,28},{21,29},{30,22},{31,23}} | collective-permute-start | bytes 2654216 | tf_op jit(solution)/shard_map/ppermute | solution.py:104
  84.7 8.0 %collective-permute-start.24 = (bf16[3,4,144,128]{3,2,1,0:T(8,128)(2,1)}, bf16[3,4,144,128]{3,2,1,0:T(8,128)(2,1)}, u32[]{:S(2)}, u32[]{:S(2)}) collective-permute-start(bf16[3,4,144,128]{3,2,1,0:T(8,128)(2,1)} %pad_maximum_fusion.3), channel_id=1, source_target_pairs={{0,16},{1,17},{10,26},{11,27},{20,4},{21,5},{30,14},{31,15}} | collective-permute-start | bytes 1327112 | tf_op jit(solution)/shard_map/ppermute | solution.py:104
  87.3 18.1 %collective-permute-start.22 = (bf16[3,8,144,128]{3,2,1,0:T(8,128)(2,1)}, bf16[3,8,144,128]{3,2,1,0:T(8,128)(2,1)}, u32[]{:S(2)}, u32[]{:S(2)}) collective-permute-start(bf16[3,8,144,128]{3,2,1,0:T(8,128)(2,1)} %collective-permute-done.21), channel_id=1, source_target_pairs={{16,24},{17,25},{26,18},{27,19},{4,12},{5,13},{14,6},{15,7}} | collective-permute-start | bytes 2654216 | tf_op jit(solution)/shard_map/ppermute | solution.py:104
  90.6 16.7 %collective-permute-start.23 = (bf16[3,4,144,128]{3,2,1,0:T(8,128)(2,1)}, bf16[3,4,144,128]{3,2,1,0:T(8,128)(2,1)}, u32[]{:S(2)}, u32[]{:S(2)}) collective-permute-start(bf16[3,4,144,128]{3,2,1,0:T(8,128)(2,1)} %pad_maximum_fusion.3), channel_id=1, source_target_pairs={{0,8},{1,9},{10,2},{11,3},{20,28},{21,29},{30,22},{31,23}} | collective-permute-start | bytes 1327112 | tf_op jit(solution)/shard_map/ppermute | solution.py:104
  92.7 12.0 %collective-permute-start.27 = (bf16[3,4,144,128]{3,2,1,0:T(8,128)(2,1)}, bf16[3,4,144,128]{3,2,1,0:T(8,128)(2,1)}, u32[]{:S(2)}, u32[]{:S(2)}) collective-permute-start(bf16[3,4,144,128]{3,2,1,0:T(8,128)(2,1)} %pad_maximum_fusion.4), channel_id=1, source_target_pairs={{0,16},{1,17},{10,26},{11,27},{20,4},{21,5},{30,14},{31,15}} | collective-permute-start | bytes 1327112 | tf_op jit(solution)/shard_map/ppermute | solution.py:104
  97.8 9.5 %collective-permute-start.25 = (bf16[3,4,144,128]{3,2,1,0:T(8,128)(2,1)}, bf16[3,4,144,128]{3,2,1,0:T(8,128)(2,1)}, u32[]{:S(2)}, u32[]{:S(2)}) collective-permute-start(bf16[3,4,144,128]{3,2,1,0:T(8,128)(2,1)} %collective-permute-done.24), channel_id=1, source_target_pairs={{16,24},{17,25},{26,18},{27,19},{4,12},{5,13},{14,6},{15,7}} | collective-permute-start | bytes 1327112 | tf_op jit(solution)/shard_map/ppermute | solution.py:104
  103.3 5.5 %collective-permute-start.26 = (bf16[3,4,144,128]{3,2,1,0:T(8,128)(2,1)}, bf16[3,4,144,128]{3,2,1,0:T(8,128)(2,1)S(1)}, u32[]{:S(2)}, u32[]{:S(2)}) collective-permute-start(bf16[3,4,144,128]{3,2,1,0:T(8,128)(2,1)} %pad_maximum_fusion.4), channel_id=1, source_target_pairs={{0,8},{1,9},{10,2},{11,3},{20,28},{21,29},{30,22},{31,23}} | collective-permute-start | bytes 1327112 | tf_op jit(solution)/shard_map/ppermute | solution.py:104
  104.7 4.1 %collective-permute-start.28 = (bf16[3,4,144,128]{3,2,1,0:T(8,128)(2,1)}, bf16[3,4,144,128]{3,2,1,0:T(8,128)(2,1)S(1)}, u32[]{:S(2)}, u32[]{:S(2)}) collective-permute-start(bf16[3,4,144,128]{3,2,1,0:T(8,128)(2,1)} %collective-permute-done.27), channel_id=1, source_target_pairs={{16,24},{17,25},{26,18},{27,19},{4,12},{5,13},{14,6},{15,7}} | collective-permute-start | bytes 1327112 | tf_op jit(solution)/shard_map/ppermute | solution.py:104
  (5 other events, 48.3 us)

commit v24 on v20

--- a/solution.py
+++ b/solution.py
@@ -8,7 +8,7 @@
 from jax.sharding import PartitionSpec as P
 
 IBS = 8
-CHUNK = 32
+CHUNK = 48
 META = 16
 
 

time: 124 us -> 124 us (level)
  no operation moved by 1% of the time
where the time goes in v24:
time: 124 us; the launch traced here: 122 us
  starting transfers between devices  46 us (37%)
  waiting for transfers between devices  35 us (28%)
  local copies, waits for them, and re-layouts  18 us (15%)
  other arithmetic  12.5 us (10%)
  Pallas kernels  10.4 us (8%)
    ppermute x7, waiting for transfers between devices, local(): a = lax.ppermute(a, 'col', forward)  35 us
    ppermute x15, starting transfers between devices, send(): lax.ppermute(v, ('row', 'col'), [(a * ncol + cc, b * ncol + cc) for a, b,...  30.8 us
    unnamed x29, local copies, waits for them, and re-layouts  11.2 us
    ppermute x7, starting transfers between devices, local(): a = lax.ppermute(a, 'col', forward)  10.5 us
    pallas_call x1, Pallas kernels, gram_call(): pl.pallas_call(kernel, grid_spec=pltpu.PrefetchScalarGridSpec(num_scalar_...  10.4 us
    unnamed x5, other arithmetic  6.78 us
    ppermute x7, starting transfers between devices, local(): b = lax.ppermute(b, 'col', backward)  4.8 us
    concatenate x5, other arithmetic, local(): own = jnp.concatenate(pending, axis=1)  2.99 us
  transfers between devices with their start and end apart: 29, of which 7 were waited for; matrix products, arithmetic and copies ran while one was open for 18% of the time, Pallas kernels for 0%

profile of v24, /device:TPU:0, one launch (start us, length us, event | category | flops | bytes accessed | tf_op | source)
XLA Modules:
  0.0 122.3 jit_solution(1953698830811758001)
XLA Ops:
  1.7 2.4 %constant_dynamic-update-slice_fusion.14 = (bf16[3,32,2,144,128]{4,3,2,1,0:T(8,128)(2,1)}, bf16[3,4,2,144,128]{4,3,2,1,0:T(8,128)(2,1)S(1)}) fusion(bf16[144]{0:T(256)(128)(2,1)S(1)} %pad.21.clone, bf16[3,4,2,1,128]{4,3,2,1,0:T(2,128)(2,1)S(1)} %broadcast_in_dim.7, bf16[3,4,2,3,128]{4,3,2,1,0:T(4,128)(2,1)S(1)} %broadcast_in_dim.6, ...), kind=kLoop, calls=%fused_computation.42 | loop fusion | flops 3538943 | bytes 2580768
  4.2 3.1 %collective-permute-start = (bf16[3,2,2,144,128]{4,3,2,1,0:T(8,128)(2,1)S(1)}, bf16[3,2,2,144,128]{4,3,2,1,0:T(8,128)(2,1)S(1)}, u32[]{:S(2)}, u32[]{:S(2)}) collective-permute-start(bf16[3,2,2,144,128]{4,3,2,1,0:T(8,128)(2,1)S(1)} %get-tuple-element.5), channel_id=1, source_target_pairs={{0,2},{2,4},{4,6},{6,7},{7,5},{5,3},{3,1},{1,0},{8,10},{10,12},{12... | collective-permute-start | bytes 1327112 | tf_op jit(solution)/shard_map/ppermute | solution.py:129
  7.3 10.1 %collective-permute-done = bf16[3,2,2,144,128]{4,3,2,1,0:T(8,128)(2,1)S(1)} collective-permute-done((bf16[3,2,2,144,128]{4,3,2,1,0:T(8,128)(2,1)S(1)}, bf16[3,2,2,144,128]{4,3,2,1,0:T(8,128)(2,1)S(1)}, u32[]{:S(2)}, u32[]{:S(2)}) %collective-permute-start) | collective-permute-done | bytes 442400 | tf_op jit(solution)/shard_map/ppermute | solution.py:129
  17.4 1.8 %collective-permute-start.2 = (bf16[3,2,2,144,128]{4,3,2,1,0:T(8,128)(2,1)S(1)}, bf16[3,2,2,144,128]{4,3,2,1,0:T(8,128)(2,1)S(1)}, u32[]{:S(2)}, u32[]{:S(2)}) collective-permute-start(bf16[3,2,2,144,128]{4,3,2,1,0:T(8,128)(2,1)S(1)} %collective-permute-done), channel_id=1, source_target_pairs={{0,2},{2,4},{4,6},{6,7},{7,5},{5,3},{3,1},{1,0},{8,10},{10,12},{12... | collective-permute-start | bytes 1327112 | tf_op jit(solution)/shard_map/ppermute | solution.py:129
  19.6 3.7 %collective-permute-start.15 = (bf16[3,8,144,128]{3,2,1,0:T(8,128)(2,1)S(1)}, bf16[3,8,144,128]{3,2,1,0:T(8,128)(2,1)S(1)}, u32[]{:S(2)}, u32[]{:S(2)}) collective-permute-start(bf16[3,8,144,128]{3,2,1,0:T(8,128)(2,1)S(1)} %pad_maximum_fusion), channel_id=1, source_target_pairs={{0,16},{1,17},{10,26},{11,27},{20,4},{21,5},{30,14},{31,15}} | collective-permute-start | bytes 2654216 | tf_op jit(solution)/shard_map/ppermute | solution.py:105
  23.3 1.3 %collective-permute-start.14 = (bf16[3,8,144,128]{3,2,1,0:T(8,128)(2,1)S(1)}, bf16[3,8,144,128]{3,2,1,0:T(8,128)(2,1)S(1)}, u32[]{:S(2)}, u32[]{:S(2)}) collective-permute-start(bf16[3,8,144,128]{3,2,1,0:T(8,128)(2,1)S(1)} %pad_maximum_fusion), channel_id=1, source_target_pairs={{0,8},{1,9},{10,2},{11,3},{20,28},{21,29},{30,22},{31,23}} | collective-permute-start | bytes 2654216 | tf_op jit(solution)/shard_map/ppermute | solution.py:105
  26.4 2.4 %collective-permute-done.2 = bf16[3,2,2,144,128]{4,3,2,1,0:T(8,128)(2,1)S(1)} collective-permute-done((bf16[3,2,2,144,128]{4,3,2,1,0:T(8,128)(2,1)S(1)}, bf16[3,2,2,144,128]{4,3,2,1,0:T(8,128)(2,1)S(1)}, u32[]{:S(2)}, u32[]{:S(2)}) %collective-permute-start.2) | collective-permute-done | bytes 442400 | tf_op jit(solution)/shard_map/ppermute | solution.py:129
  28.8 1.5 %collective-permute-start.4 = (bf16[3,2,2,144,128]{4,3,2,1,0:T(8,128)(2,1)S(1)}, bf16[3,2,2,144,128]{4,3,2,1,0:T(8,128)(2,1)S(1)}, u32[]{:S(2)}, u32[]{:S(2)}) collective-permute-start(bf16[3,2,2,144,128]{4,3,2,1,0:T(8,128)(2,1)S(1)} %collective-permute-done.2), channel_id=1, source_target_pairs={{0,2},{2,4},{4,6},{6,7},{7,5},{5,3},{3,1},{1,0},{8,10},{10,12},{12... | collective-permute-start | bytes 1327112 | tf_op jit(solution)/shard_map/ppermute | solution.py:129
  32.5 6.6 %collective-permute-done.4 = bf16[3,2,2,144,128]{4,3,2,1,0:T(8,128)(2,1)S(1)} collective-permute-done((bf16[3,2,2,144,128]{4,3,2,1,0:T(8,128)(2,1)S(1)}, bf16[3,2,2,144,128]{4,3,2,1,0:T(8,128)(2,1)S(1)}, u32[]{:S(2)}, u32[]{:S(2)}) %collective-permute-start.4) | collective-permute-done | bytes 442400 | tf_op jit(solution)/shard_map/ppermute | solution.py:129
  39.2 1.4 %collective-permute-start.6 = (bf16[3,2,2,144,128]{4,3,2,1,0:T(8,128)(2,1)S(1)}, bf16[3,2,2,144,128]{4,3,2,1,0:T(8,128)(2,1)S(1)}, u32[]{:S(2)}, u32[]{:S(2)}) collective-permute-start(bf16[3,2,2,144,128]{4,3,2,1,0:T(8,128)(2,1)S(1)} %collective-permute-done.4), channel_id=1, source_target_pairs={{0,2},{2,4},{4,6},{6,7},{7,5},{5,3},{3,1},{1,0},{8,10},{10,12},{12... | collective-permute-start | bytes 1327112 | tf_op jit(solution)/shard_map/ppermute | solution.py:129
  41.4 3.3 %collective-permute-start.18 = (bf16[3,8,144,128]{3,2,1,0:T(8,128)(2,1)S(1)}, bf16[3,8,144,128]{3,2,1,0:T(8,128)(2,1)S(1)}, u32[]{:S(2)}, u32[]{:S(2)}) collective-permute-start(bf16[3,8,144,128]{3,2,1,0:T(8,128)(2,1)S(1)} %pad_maximum_fusion.1), channel_id=1, source_target_pairs={{0,16},{1,17},{10,26},{11,27},{20,4},{21,5},{30,14},{31,15}} | collective-permute-start | bytes 2654216 | tf_op jit(solution)/shard_map/ppermute | solution.py:105
  47.1 2.4 %collective-permute-done.6 = bf16[3,2,2,144,128]{4,3,2,1,0:T(8,128)(2,1)S(1)} collective-permute-done((bf16[3,2,2,144,128]{4,3,2,1,0:T(8,128)(2,1)S(1)}, bf16[3,2,2,144,128]{4,3,2,1,0:T(8,128)(2,1)S(1)}, u32[]{:S(2)}, u32[]{:S(2)}) %collective-permute-start.6) | collective-permute-done | bytes 442400 | tf_op jit(solution)/shard_map/ppermute | solution.py:129
  49.5 1.4 %collective-permute-start.8 = (bf16[3,2,2,144,128]{4,3,2,1,0:T(8,128)(2,1)S(1)}, bf16[3,2,2,144,128]{4,3,2,1,0:T(8,128)(2,1)S(1)}, u32[]{:S(2)}, u32[]{:S(2)}) collective-permute-start(bf16[3,2,2,144,128]{4,3,2,1,0:T(8,128)(2,1)S(1)} %collective-permute-done.6), channel_id=1, source_target_pairs={{0,2},{2,4},{4,6},{6,7},{7,5},{5,3},{3,1},{1,0},{8,10},{10,12},{12... | collective-permute-start | bytes 1327112 | tf_op jit(solution)/shard_map/ppermute | solution.py:129
  53.4 6.5 %collective-permute-done.8 = bf16[3,2,2,144,128]{4,3,2,1,0:T(8,128)(2,1)S(1)} collective-permute-done((bf16[3,2,2,144,128]{4,3,2,1,0:T(8,128)(2,1)S(1)}, bf16[3,2,2,144,128]{4,3,2,1,0:T(8,128)(2,1)S(1)}, u32[]{:S(2)}, u32[]{:S(2)}) %collective-permute-start.8) | collective-permute-done | bytes 442400 | tf_op jit(solution)/shard_map/ppermute | solution.py:129
  59.9 1.4 %collective-permute-start.10 = (bf16[3,2,2,144,128]{4,3,2,1,0:T(8,128)(2,1)S(1)}, bf16[3,2,2,144,128]{4,3,2,1,0:T(8,128)(2,1)S(1)}, u32[]{:S(2)}, u32[]{:S(2)}) collective-permute-start(bf16[3,2,2,144,128]{4,3,2,1,0:T(8,128)(2,1)S(1)} %collective-permute-done.8), channel_id=1, source_target_pairs={{0,2},{2,4},{4,6},{6,7},{7,5},{5,3},{3,1},{1,0},{8,10},{10,12},{12... | collective-permute-start | bytes 1327112 | tf_op jit(solution)/shard_map/ppermute | solution.py:129
  64.7 1.3 %collective-permute-start.17 = (bf16[3,8,144,128]{3,2,1,0:T(8,128)(2,1)S(1)}, bf16[3,8,144,128]{3,2,1,0:T(8,128)(2,1)S(1)}, u32[]{:S(2)}, u32[]{:S(2)}) collective-permute-start(bf16[3,8,144,128]{3,2,1,0:T(8,128)(2,1)S(1)} %pad_maximum_fusion.1), channel_id=1, source_target_pairs={{0,8},{1,9},{10,2},{11,3},{20,28},{21,29},{30,22},{31,23}} | collective-permute-start | bytes 2654216 | tf_op jit(solution)/shard_map/ppermute | solution.py:105
  66.1 2.3 %collective-permute-start.21 = (bf16[3,8,144,128]{3,2,1,0:T(8,128)(2,1)}, bf16[3,8,144,128]{3,2,1,0:T(8,128)(2,1)}, u32[]{:S(2)}, u32[]{:S(2)}) collective-permute-start(bf16[3,8,144,128]{3,2,1,0:T(8,128)(2,1)} %pad_maximum_fusion.2), channel_id=1, source_target_pairs={{0,16},{1,17},{10,26},{11,27},{20,4},{21,5},{30,14},{31,15}} | collective-permute-start | bytes 2654216 | tf_op jit(solution)/shard_map/ppermute | solution.py:105
  69.5 1.4 %collective-permute-done.10 = bf16[3,2,2,144,128]{4,3,2,1,0:T(8,128)(2,1)S(1)} collective-permute-done((bf16[3,2,2,144,128]{4,3,2,1,0:T(8,128)(2,1)S(1)}, bf16[3,2,2,144,128]{4,3,2,1,0:T(8,128)(2,1)S(1)}, u32[]{:S(2)}, u32[]{:S(2)}) %collective-permute-start.10) | collective-permute-done | bytes 442400 | tf_op jit(solution)/shard_map/ppermute | solution.py:129
  70.9 2.0 %collective-permute-start.13 = (bf16[3,2,2,144,128]{4,3,2,1,0:T(8,128)(2,1)S(1)}, bf16[3,2,2,144,128]{4,3,2,1,0:T(8,128)(2,1)S(1)}, u32[]{:S(2)}, u32[]{:S(2)}) collective-permute-start(bf16[3,2,2,144,128]{4,3,2,1,0:T(8,128)(2,1)S(1)} %collective-permute-done.11), channel_id=1, source_target_pairs={{2,0},{4,2},{6,4},{7,6},{5,7},{3,5},{1,3},{0,1},{10,8},{12,10},{14... | collective-permute-start | bytes 1327112 | tf_op jit(solution)/shard_map/ppermute | solution.py:130
  75.6 5.6 %collective-permute-done.12 = bf16[3,2,2,144,128]{4,3,2,1,0:T(8,128)(2,1)S(1)} collective-permute-done((bf16[3,2,2,144,128]{4,3,2,1,0:T(8,128)(2,1)S(1)}, bf16[3,2,2,144,128]{4,3,2,1,0:T(8,128)(2,1)S(1)}, u32[]{:S(2)}, u32[]{:S(2)}) %collective-permute-start.12) | collective-permute-done | bytes 442400 | tf_op jit(solution)/shard_map/ppermute | solution.py:129
  81.3 3.2 %collective-permute-start.20 = (bf16[3,8,144,128]{3,2,1,0:T(8,128)(2,1)}, bf16[3,8,144,128]{3,2,1,0:T(8,128)(2,1)}, u32[]{:S(2)}, u32[]{:S(2)}) collective-permute-start(bf16[3,8,144,128]{3,2,1,0:T(8,128)(2,1)} %pad_maximum_fusion.2), channel_id=1, source_target_pairs={{0,8},{1,9},{10,2},{11,3},{20,28},{21,29},{30,22},{31,23}} | collective-permute-start | bytes 2654216 | tf_op jit(solution)/shard_map/ppermute | solution.py:105
  84.5 2.1 %collective-permute-start.24 = (bf16[3,4,144,128]{3,2,1,0:T(8,128)(2,1)}, bf16[3,4,144,128]{3,2,1,0:T(8,128)(2,1)}, u32[]{:S(2)}, u32[]{:S(2)}) collective-permute-start(bf16[3,4,144,128]{3,2,1,0:T(8,128)(2,1)} %pad_maximum_fusion.3), channel_id=1, source_target_pairs={{0,16},{1,17},{10,26},{11,27},{20,4},{21,5},{30,14},{31,15}} | collective-permute-start | bytes 1327112 | tf_op jit(solution)/shard_map/ppermute | solution.py:105
  86.6 1.6 %collective-permute-start.22 = (bf16[3,8,144,128]{3,2,1,0:T(8,128)(2,1)}, bf16[3,8,144,128]{3,2,1,0:T(8,128)(2,1)}, u32[]{:S(2)}, u32[]{:S(2)}) collective-permute-start(bf16[3,8,144,128]{3,2,1,0:T(8,128)(2,1)} %collective-permute-done.21), channel_id=1, source_target_pairs={{16,24},{17,25},{26,18},{27,19},{4,12},{5,13},{14,6},{15,7}} | collective-permute-start | bytes 2654216 | tf_op jit(solution)/shard_map/ppermute | solution.py:105
  89.9 2.1 %collective-permute-start.23 = (bf16[3,4,144,128]{3,2,1,0:T(8,128)(2,1)}, bf16[3,4,144,128]{3,2,1,0:T(8,128)(2,1)}, u32[]{:S(2)}, u32[]{:S(2)}) collective-permute-start(bf16[3,4,144,128]{3,2,1,0:T(8,128)(2,1)} %pad_maximum_fusion.3), channel_id=1, source_target_pairs={{0,8},{1,9},{10,2},{11,3},{20,28},{21,29},{30,22},{31,23}} | collective-permute-start | bytes 1327112 | tf_op jit(solution)/shard_map/ppermute | solution.py:105
  92.0 5.1 %collective-permute-start.27 = (bf16[3,4,144,128]{3,2,1,0:T(8,128)(2,1)}, bf16[3,4,144,128]{3,2,1,0:T(8,128)(2,1)}, u32[]{:S(2)}, u32[]{:S(2)}) collective-permute-start(bf16[3,4,144,128]{3,2,1,0:T(8,128)(2,1)} %pad_maximum_fusion.4), channel_id=1, source_target_pairs={{0,16},{1,17},{10,26},{11,27},{20,4},{21,5},{30,14},{31,15}} | collective-permute-start | bytes 1327112 | tf_op jit(solution)/shard_map/ppermute | solution.py:105
  97.1 1.4 %collective-permute-start.25 = (bf16[3,4,144,128]{3,2,1,0:T(8,128)(2,1)}, bf16[3,4,144,128]{3,2,1,0:T(8,128)(2,1)}, u32[]{:S(2)}, u32[]{:S(2)}) collective-permute-start(bf16[3,4,144,128]{3,2,1,0:T(8,128)(2,1)} %collective-permute-done.24), channel_id=1, source_target_pairs={{16,24},{17,25},{26,18},{27,19},{4,12},{5,13},{14,6},{15,7}} | collective-permute-start | bytes 1327112 | tf_op jit(solution)/shard_map/ppermute | solution.py:105
  99.9 1.7 %slice.19 = bf16[96,2,1,1]{3,2,1,0:T(2,128)(2,1)} slice(bf16[96,2,144,128]{3,2,1,0:T(8,128)(2,1)} %bitcast.44), slice={[0:96], [0:2], [131:132], [0:1]} | slice | bytes 768 | tf_op jit(solution)/shard_map/slice | solution.py:150
  102.6 1.3 %collective-permute-start.26 = (bf16[3,4,144,128]{3,2,1,0:T(8,128)(2,1)}, bf16[3,4,144,128]{3,2,1,0:T(8,128)(2,1)S(1)}, u32[]{:S(2)}, u32[]{:S(2)}) collective-permute-start(bf16[3,4,144,128]{3,2,1,0:T(8,128)(2,1)} %pad_maximum_fusion.4), channel_id=1, source_target_pairs={{0,8},{1,9},{10,2},{11,3},{20,28},{21,29},{30,22},{31,23}} | collective-permute-start | bytes 1327112 | tf_op jit(solution)/shard_map/ppermute | solution.py:105
  104.7 1.9 %select_dynamic-update-slice_fusion = bf16[3,32,144,128]{3,2,1,0:T(8,128)(2,1)S(1)} fusion(bf16[3,32,144,128]{3,2,1,0:T(8,128)(2,1)S(1)} %select_dynamic-update-slice_fusion.1, bf16[3,8,144,128]{3,2,1,0:T(8,128)(2,1)} %collective-permute-done.20, bf16[3,8,144,128]{3,2,1,0:T(8,128)(2,1)} %collective-permute-done.21, ...), kind=kLoop, calls=%fused_computation.4 | loop fusion | flops 4866048 | bytes 4423683
  106.6 1.5 %select_dynamic-update-slice_fusion.4 = bf16[3,32,144,128]{3,2,1,0:T(8,128)(2,1)S(1)} fusion(bf16[3,32,144,128]{3,2,1,0:T(8,128)(2,1)S(1)} %select_dynamic-update-slice_fusion, bf16[3,4,144,128]{3,2,1,0:T(8,128)(2,1)} %collective-permute-done.23, bf16[3,4,144,128]{3,2,1,0:T(8,128)(2,1)} %collective-permute-done.24, ...), kind=kLoop, calls=%fused_computation.10 | loop fusion | flops 1548288 | bytes 2211843
  108.1 1.3 %select_dynamic-update-slice_fusion.3 = bf16[3,32,144,128]{3,2,1,0:T(8,128)(2,1)S(1)} fusion(bf16[3,32,144,128]{3,2,1,0:T(8,128)(2,1)S(1)} %select_dynamic-update-slice_fusion.4, bf16[3,4,144,128]{3,2,1,0:T(8,128)(2,1)S(1)} %collective-permute-done.26, bf16[3,4,144,128]{3,2,1,0:T(8,128)(2,1)} %collective-permute-done.27, ...), kind=kLoop, calls=%fused_computation.9 | loop fusion | flops 1548288 | bytes 2211843 | tf_op jit(solution)/shard_map/concatenate | solution.py:145
  111.9 10.4 %shard_map.37 = f32[2048,1024]{1,0:T(8,128)} custom-call(s32[288]{0:T(512)S(1)} %min.12.offs_ref, bf16[96,2,144,128]{3,2,1,0:T(8,128)(2,1)} %bitcast.45, bf16[96,144,128]{2,1,0:T(8,128)(2,1)S(1)} %bitcast.43), custom_call_target="tpu_custom_call" | custom-call | flops 805306368 | bytes 17825792 | tf_op jit(solution)/shard_map/pallas_call | solution.py:40
  (99 shorter events, 26.6 us)
Async XLA Ops:
  4.2 13.2 %collective-permute-start = (bf16[3,2,2,144,128]{4,3,2,1,0:T(8,128)(2,1)S(1)}, bf16[3,2,2,144,128]{4,3,2,1,0:T(8,128)(2,1)S(1)}, u32[]{:S(2)}, u32[]{:S(2)}) collective-permute-start(bf16[3,2,2,144,128]{4,3,2,1,0:T(8,128)(2,1)S(1)} %get-tuple-element.5), channel_id=1, source_target_pairs={{0,2},{2,4},{4,6},{6,7},{7,5},{5,3},{3,1},{1,0},{8,10},{10,12},{12... | collective-permute-start | bytes 1327112 | tf_op jit(solution)/shard_map/ppermute | solution.py:129
  7.3 11.9 %collective-permute-start.1 = (bf16[3,2,2,144,128]{4,3,2,1,0:T(8,128)(2,1)S(1)}, bf16[3,2,2,144,128]{4,3,2,1,0:T(8,128)(2,1)S(1)}, u32[]{:S(2)}, u32[]{:S(2)}) collective-permute-start(bf16[3,2,2,144,128]{4,3,2,1,0:T(8,128)(2,1)S(1)} %get-tuple-element.6), channel_id=1, source_target_pairs={{2,0},{4,2},{6,4},{7,6},{5,7},{3,5},{1,3},{0,1},{10,8},{12,10},{14... | collective-permute-start | bytes 1327112 | tf_op jit(solution)/shard_map/ppermute | solution.py:130
  17.4 11.4 %collective-permute-start.2 = (bf16[3,2,2,144,128]{4,3,2,1,0:T(8,128)(2,1)S(1)}, bf16[3,2,2,144,128]{4,3,2,1,0:T(8,128)(2,1)S(1)}, u32[]{:S(2)}, u32[]{:S(2)}) collective-permute-start(bf16[3,2,2,144,128]{4,3,2,1,0:T(8,128)(2,1)S(1)} %collective-permute-done), channel_id=1, source_target_pairs={{0,2},{2,4},{4,6},{6,7},{7,5},{5,3},{3,1},{1,0},{8,10},{10,12},{12... | collective-permute-start | bytes 1327112 | tf_op jit(solution)/shard_map/ppermute | solution.py:129
  19.2 11.0 %collective-permute-start.3 = (bf16[3,2,2,144,128]{4,3,2,1,0:T(8,128)(2,1)S(1)}, bf16[3,2,2,144,128]{4,3,2,1,0:T(8,128)(2,1)S(1)}, u32[]{:S(2)}, u32[]{:S(2)}) collective-permute-start(bf16[3,2,2,144,128]{4,3,2,1,0:T(8,128)(2,1)S(1)} %collective-permute-done.1), channel_id=1, source_target_pairs={{2,0},{4,2},{6,4},{7,6},{5,7},{3,5},{1,3},{0,1},{10,8},{12,10},{14... | collective-permute-start | bytes 1327112 | tf_op jit(solution)/shard_map/ppermute | solution.py:130
  19.6 25.0 %collective-permute-start.15 = (bf16[3,8,144,128]{3,2,1,0:T(8,128)(2,1)S(1)}, bf16[3,8,144,128]{3,2,1,0:T(8,128)(2,1)S(1)}, u32[]{:S(2)}, u32[]{:S(2)}) collective-permute-start(bf16[3,8,144,128]{3,2,1,0:T(8,128)(2,1)S(1)} %pad_maximum_fusion), channel_id=1, source_target_pairs={{0,16},{1,17},{10,26},{11,27},{20,4},{21,5},{30,14},{31,15}} | collective-permute-start | bytes 2654216 | tf_op jit(solution)/shard_map/ppermute | solution.py:105
  23.3 41.4 %collective-permute-start.14 = (bf16[3,8,144,128]{3,2,1,0:T(8,128)(2,1)S(1)}, bf16[3,8,144,128]{3,2,1,0:T(8,128)(2,1)S(1)}, u32[]{:S(2)}, u32[]{:S(2)}) collective-permute-start(bf16[3,8,144,128]{3,2,1,0:T(8,128)(2,1)S(1)} %pad_maximum_fusion), channel_id=1, source_target_pairs={{0,8},{1,9},{10,2},{11,3},{20,28},{21,29},{30,22},{31,23}} | collective-permute-start | bytes 2654216 | tf_op jit(solution)/shard_map/ppermute | solution.py:105
  28.8 10.4 %collective-permute-start.4 = (bf16[3,2,2,144,128]{4,3,2,1,0:T(8,128)(2,1)S(1)}, bf16[3,2,2,144,128]{4,3,2,1,0:T(8,128)(2,1)S(1)}, u32[]{:S(2)}, u32[]{:S(2)}) collective-permute-start(bf16[3,2,2,144,128]{4,3,2,1,0:T(8,128)(2,1)S(1)} %collective-permute-done.2), channel_id=1, source_target_pairs={{0,2},{2,4},{4,6},{6,7},{7,5},{5,3},{3,1},{1,0},{8,10},{10,12},{12... | collective-permute-start | bytes 1327112 | tf_op jit(solution)/shard_map/ppermute | solution.py:129
  30.2 10.3 %collective-permute-start.5 = (bf16[3,2,2,144,128]{4,3,2,1,0:T(8,128)(2,1)S(1)}, bf16[3,2,2,144,128]{4,3,2,1,0:T(8,128)(2,1)S(1)}, u32[]{:S(2)}, u32[]{:S(2)}) collective-permute-start(bf16[3,2,2,144,128]{4,3,2,1,0:T(8,128)(2,1)S(1)} %collective-permute-done.3), channel_id=1, source_target_pairs={{2,0},{4,2},{6,4},{7,6},{5,7},{3,5},{1,3},{0,1},{10,8},{12,10},{14... | collective-permute-start | bytes 1327112 | tf_op jit(solution)/shard_map/ppermute | solution.py:130
  39.2 10.3 %collective-permute-start.6 = (bf16[3,2,2,144,128]{4,3,2,1,0:T(8,128)(2,1)S(1)}, bf16[3,2,2,144,128]{4,3,2,1,0:T(8,128)(2,1)S(1)}, u32[]{:S(2)}, u32[]{:S(2)}) collective-permute-start(bf16[3,2,2,144,128]{4,3,2,1,0:T(8,128)(2,1)S(1)} %collective-permute-done.4), channel_id=1, source_target_pairs={{0,2},{2,4},{4,6},{6,7},{7,5},{5,3},{3,1},{1,0},{8,10},{10,12},{12... | collective-permute-start | bytes 1327112 | tf_op jit(solution)/shard_map/ppermute | solution.py:129
  40.6 10.3 %collective-permute-start.7 = (bf16[3,2,2,144,128]{4,3,2,1,0:T(8,128)(2,1)S(1)}, bf16[3,2,2,144,128]{4,3,2,1,0:T(8,128)(2,1)S(1)}, u32[]{:S(2)}, u32[]{:S(2)}) collective-permute-start(bf16[3,2,2,144,128]{4,3,2,1,0:T(8,128)(2,1)S(1)} %collective-permute-done.5), channel_id=1, source_target_pairs={{2,0},{4,2},{6,4},{7,6},{5,7},{3,5},{1,3},{0,1},{10,8},{12,10},{14... | collective-permute-start | bytes 1327112 | tf_op jit(solution)/shard_map/ppermute | solution.py:130
  41.4 26.9 %collective-permute-start.18 = (bf16[3,8,144,128]{3,2,1,0:T(8,128)(2,1)S(1)}, bf16[3,8,144,128]{3,2,1,0:T(8,128)(2,1)S(1)}, u32[]{:S(2)}, u32[]{:S(2)}) collective-permute-start(bf16[3,8,144,128]{3,2,1,0:T(8,128)(2,1)S(1)} %pad_maximum_fusion.1), channel_id=1, source_target_pairs={{0,16},{1,17},{10,26},{11,27},{20,4},{21,5},{30,14},{31,15}} | collective-permute-start | bytes 2654216 | tf_op jit(solution)/shard_map/ppermute | solution.py:105
  44.7 21.4 %collective-permute-start.16 = (bf16[3,8,144,128]{3,2,1,0:T(8,128)(2,1)S(1)}, bf16[3,8,144,128]{3,2,1,0:T(8,128)(2,1)S(1)}, u32[]{:S(2)}, u32[]{:S(2)}) collective-permute-start(bf16[3,8,144,128]{3,2,1,0:T(8,128)(2,1)S(1)} %collective-permute-done.15), channel_id=1, source_target_pairs={{16,24},{17,25},{26,18},{27,19},{4,12},{5,13},{14,6},{15,7}} | collective-permute-start | bytes 2654216 | tf_op jit(solution)/shard_map/ppermute | solution.py:105
  49.5 10.3 %collective-permute-start.8 = (bf16[3,2,2,144,128]{4,3,2,1,0:T(8,128)(2,1)S(1)}, bf16[3,2,2,144,128]{4,3,2,1,0:T(8,128)(2,1)S(1)}, u32[]{:S(2)}, u32[]{:S(2)}) collective-permute-start(bf16[3,2,2,144,128]{4,3,2,1,0:T(8,128)(2,1)S(1)} %collective-permute-done.6), channel_id=1, source_target_pairs={{0,2},{2,4},{4,6},{6,7},{7,5},{5,3},{3,1},{1,0},{8,10},{10,12},{12... | collective-permute-start | bytes 1327112 | tf_op jit(solution)/shard_map/ppermute | solution.py:129
  50.9 10.3 %collective-permute-start.9 = (bf16[3,2,2,144,128]{4,3,2,1,0:T(8,128)(2,1)S(1)}, bf16[3,2,2,144,128]{4,3,2,1,0:T(8,128)(2,1)S(1)}, u32[]{:S(2)}, u32[]{:S(2)}) collective-permute-start(bf16[3,2,2,144,128]{4,3,2,1,0:T(8,128)(2,1)S(1)} %collective-permute-done.7), channel_id=1, source_target_pairs={{2,0},{4,2},{6,4},{7,6},{5,7},{3,5},{1,3},{0,1},{10,8},{12,10},{14... | collective-permute-start | bytes 1327112 | tf_op jit(solution)/shard_map/ppermute | solution.py:130
  51.6 16.8 %copy-start.4 = (bf16[3,2,144,128]{3,2,1,0:T(8,128)(2,1)}, bf16[3,2,144,128]{3,2,1,0:T(8,128)(2,1)S(1)}, u32[]{:S(2)}) copy-start(bf16[3,2,144,128]{3,2,1,0:T(8,128)(2,1)S(1)} %dynamic-slice_bitcast_fusion.7) | copy-start | bytes 663556
  59.9 11.1 %collective-permute-start.10 = (bf16[3,2,2,144,128]{4,3,2,1,0:T(8,128)(2,1)S(1)}, bf16[3,2,2,144,128]{4,3,2,1,0:T(8,128)(2,1)S(1)}, u32[]{:S(2)}, u32[]{:S(2)}) collective-permute-start(bf16[3,2,2,144,128]{4,3,2,1,0:T(8,128)(2,1)S(1)} %collective-permute-done.8), channel_id=1, source_target_pairs={{0,2},{2,4},{4,6},{6,7},{7,5},{5,3},{3,1},{1,0},{8,10},{10,12},{12... | collective-permute-start | bytes 1327112 | tf_op jit(solution)/shard_map/ppermute | solution.py:129
  61.2 9.7 %collective-permute-start.11 = (bf16[3,2,2,144,128]{4,3,2,1,0:T(8,128)(2,1)S(1)}, bf16[3,2,2,144,128]{4,3,2,1,0:T(8,128)(2,1)S(1)}, u32[]{:S(2)}, u32[]{:S(2)}) collective-permute-start(bf16[3,2,2,144,128]{4,3,2,1,0:T(8,128)(2,1)S(1)} %collective-permute-done.9), channel_id=1, source_target_pairs={{2,0},{4,2},{6,4},{7,6},{5,7},{3,5},{1,3},{0,1},{10,8},{12,10},{14... | collective-permute-start | bytes 1327112 | tf_op jit(solution)/shard_map/ppermute | solution.py:130
  64.7 25.2 %collective-permute-start.17 = (bf16[3,8,144,128]{3,2,1,0:T(8,128)(2,1)S(1)}, bf16[3,8,144,128]{3,2,1,0:T(8,128)(2,1)S(1)}, u32[]{:S(2)}, u32[]{:S(2)}) collective-permute-start(bf16[3,8,144,128]{3,2,1,0:T(8,128)(2,1)S(1)} %pad_maximum_fusion.1), channel_id=1, source_target_pairs={{0,8},{1,9},{10,2},{11,3},{20,28},{21,29},{30,22},{31,23}} | collective-permute-start | bytes 2654216 | tf_op jit(solution)/shard_map/ppermute | solution.py:105
  66.1 20.5 %collective-permute-start.21 = (bf16[3,8,144,128]{3,2,1,0:T(8,128)(2,1)}, bf16[3,8,144,128]{3,2,1,0:T(8,128)(2,1)}, u32[]{:S(2)}, u32[]{:S(2)}) collective-permute-start(bf16[3,8,144,128]{3,2,1,0:T(8,128)(2,1)} %pad_maximum_fusion.2), channel_id=1, source_target_pairs={{0,16},{1,17},{10,26},{11,27},{20,4},{21,5},{30,14},{31,15}} | collective-permute-start | bytes 2654216 | tf_op jit(solution)/shard_map/ppermute | solution.py:105
  68.3 28.7 %collective-permute-start.19 = (bf16[3,8,144,128]{3,2,1,0:T(8,128)(2,1)S(1)}, bf16[3,8,144,128]{3,2,1,0:T(8,128)(2,1)S(1)}, u32[]{:S(2)}, u32[]{:S(2)}) collective-permute-start(bf16[3,8,144,128]{3,2,1,0:T(8,128)(2,1)S(1)} %collective-permute-done.18), channel_id=1, source_target_pairs={{16,24},{17,25},{26,18},{27,19},{4,12},{5,13},{14,6},{15,7}} | collective-permute-start | bytes 2654216 | tf_op jit(solution)/shard_map/ppermute | solution.py:105
  70.9 10.3 %collective-permute-start.12 = (bf16[3,2,2,144,128]{4,3,2,1,0:T(8,128)(2,1)S(1)}, bf16[3,2,2,144,128]{4,3,2,1,0:T(8,128)(2,1)S(1)}, u32[]{:S(2)}, u32[]{:S(2)}) collective-permute-start(bf16[3,2,2,144,128]{4,3,2,1,0:T(8,128)(2,1)S(1)} %collective-permute-done.10), channel_id=1, source_target_pairs={{0,2},{2,4},{4,6},{6,7},{7,5},{5,3},{3,1},{1,0},{8,10},{10,12},{12... | collective-permute-start | bytes 1327112 | tf_op jit(solution)/shard_map/ppermute | solution.py:129
  70.9 13.6 %collective-permute-start.13 = (bf16[3,2,2,144,128]{4,3,2,1,0:T(8,128)(2,1)S(1)}, bf16[3,2,2,144,128]{4,3,2,1,0:T(8,128)(2,1)S(1)}, u32[]{:S(2)}, u32[]{:S(2)}) collective-permute-start(bf16[3,2,2,144,128]{4,3,2,1,0:T(8,128)(2,1)S(1)} %collective-permute-done.11), channel_id=1, source_target_pairs={{2,0},{4,2},{6,4},{7,6},{5,7},{3,5},{1,3},{0,1},{10,8},{12,10},{14... | collective-permute-start | bytes 1327112 | tf_op jit(solution)/shard_map/ppermute | solution.py:130
  73.0 24.1 %copy-start = (bf16[3,2,144,128]{3,2,1,0:T(8,128)(2,1)}, bf16[3,2,144,128]{3,2,1,0:T(8,128)(2,1)S(1)}, u32[]{:S(2)}) copy-start(bf16[3,2,144,128]{3,2,1,0:T(8,128)(2,1)S(1)} %dynamic-slice_bitcast_fusion.3) | copy-start | bytes 663556
  73.0 24.1 %copy-start.1 = (bf16[3,2,144,128]{3,2,1,0:T(8,128)(2,1)}, bf16[3,2,144,128]{3,2,1,0:T(8,128)(2,1)S(1)}, u32[]{:S(2)}) copy-start(bf16[3,2,144,128]{3,2,1,0:T(8,128)(2,1)S(1)} %dynamic-slice_bitcast_fusion.2) | copy-start | bytes 663556
  81.3 21.4 %collective-permute-start.20 = (bf16[3,8,144,128]{3,2,1,0:T(8,128)(2,1)}, bf16[3,8,144,128]{3,2,1,0:T(8,128)(2,1)}, u32[]{:S(2)}, u32[]{:S(2)}) collective-permute-start(bf16[3,8,144,128]{3,2,1,0:T(8,128)(2,1)} %pad_maximum_fusion.2), channel_id=1, source_target_pairs={{0,8},{1,9},{10,2},{11,3},{20,28},{21,29},{30,22},{31,23}} | collective-permute-start | bytes 2654216 | tf_op jit(solution)/shard_map/ppermute | solution.py:105
  84.5 7.5 %collective-permute-start.24 = (bf16[3,4,144,128]{3,2,1,0:T(8,128)(2,1)}, bf16[3,4,144,128]{3,2,1,0:T(8,128)(2,1)}, u32[]{:S(2)}, u32[]{:S(2)}) collective-permute-start(bf16[3,4,144,128]{3,2,1,0:T(8,128)(2,1)} %pad_maximum_fusion.3), channel_id=1, source_target_pairs={{0,16},{1,17},{10,26},{11,27},{20,4},{21,5},{30,14},{31,15}} | collective-permute-start | bytes 1327112 | tf_op jit(solution)/shard_map/ppermute | solution.py:105
  86.6 18.1 %collective-permute-start.22 = (bf16[3,8,144,128]{3,2,1,0:T(8,128)(2,1)}, bf16[3,8,144,128]{3,2,1,0:T(8,128)(2,1)}, u32[]{:S(2)}, u32[]{:S(2)}) collective-permute-start(bf16[3,8,144,128]{3,2,1,0:T(8,128)(2,1)} %collective-permute-done.21), channel_id=1, source_target_pairs={{16,24},{17,25},{26,18},{27,19},{4,12},{5,13},{14,6},{15,7}} | collective-permute-start | bytes 2654216 | tf_op jit(solution)/shard_map/ppermute | solution.py:105
  89.9 16.7 %collective-permute-start.23 = (bf16[3,4,144,128]{3,2,1,0:T(8,128)(2,1)}, bf16[3,4,144,128]{3,2,1,0:T(8,128)(2,1)}, u32[]{:S(2)}, u32[]{:S(2)}) collective-permute-start(bf16[3,4,144,128]{3,2,1,0:T(8,128)(2,1)} %pad_maximum_fusion.3), channel_id=1, source_target_pairs={{0,8},{1,9},{10,2},{11,3},{20,28},{21,29},{30,22},{31,23}} | collective-permute-start | bytes 1327112 | tf_op jit(solution)/shard_map/ppermute | solution.py:105
  92.0 12.0 %collective-permute-start.27 = (bf16[3,4,144,128]{3,2,1,0:T(8,128)(2,1)}, bf16[3,4,144,128]{3,2,1,0:T(8,128)(2,1)}, u32[]{:S(2)}, u32[]{:S(2)}) collective-permute-start(bf16[3,4,144,128]{3,2,1,0:T(8,128)(2,1)} %pad_maximum_fusion.4), channel_id=1, source_target_pairs={{0,16},{1,17},{10,26},{11,27},{20,4},{21,5},{30,14},{31,15}} | collective-permute-start | bytes 1327112 | tf_op jit(solution)/shard_map/ppermute | solution.py:105
  97.1 9.5 %collective-permute-start.25 = (bf16[3,4,144,128]{3,2,1,0:T(8,128)(2,1)}, bf16[3,4,144,128]{3,2,1,0:T(8,128)(2,1)}, u32[]{:S(2)}, u32[]{:S(2)}) collective-permute-start(bf16[3,4,144,128]{3,2,1,0:T(8,128)(2,1)} %collective-permute-done.24), channel_id=1, source_target_pairs={{16,24},{17,25},{26,18},{27,19},{4,12},{5,13},{14,6},{15,7}} | collective-permute-start | bytes 1327112 | tf_op jit(solution)/shard_map/ppermute | solution.py:105
  102.6 5.5 %collective-permute-start.26 = (bf16[3,4,144,128]{3,2,1,0:T(8,128)(2,1)}, bf16[3,4,144,128]{3,2,1,0:T(8,128)(2,1)S(1)}, u32[]{:S(2)}, u32[]{:S(2)}) collective-permute-start(bf16[3,4,144,128]{3,2,1,0:T(8,128)(2,1)} %pad_maximum_fusion.4), channel_id=1, source_target_pairs={{0,8},{1,9},{10,2},{11,3},{20,28},{21,29},{30,22},{31,23}} | collective-permute-start | bytes 1327112 | tf_op jit(solution)/shard_map/ppermute | solution.py:105
  104.0 4.1 %collective-permute-start.28 = (bf16[3,4,144,128]{3,2,1,0:T(8,128)(2,1)}, bf16[3,4,144,128]{3,2,1,0:T(8,128)(2,1)S(1)}, u32[]{:S(2)}, u32[]{:S(2)}) collective-permute-start(bf16[3,4,144,128]{3,2,1,0:T(8,128)(2,1)} %collective-permute-done.27), channel_id=1, source_target_pairs={{16,24},{17,25},{26,18},{27,19},{4,12},{5,13},{14,6},{15,7}} | collective-permute-start | bytes 1327112 | tf_op jit(solution)/shard_map/ppermute | solution.py:105
  (5 other events, 47.3 us)

commit v25 on v24

--- a/solution.py
+++ b/solution.py
@@ -147,7 +147,8 @@
     blocks = blocks.reshape(n, local_slots, blk + META, blk)
     column_blocks = column_blocks.reshape(n, blk + META, blk)
 
-    offs = jnp.concatenate([blocks[:, :, blk + 3, 0], column_blocks[:, blk + 3, 0][:, None]], axis=1)
+    c_offs = jnp.concatenate([got[:, :, blk + 3, 0] for got in columns], axis=1).reshape(n, 1)
+    offs = jnp.concatenate([blocks[:, :, blk + 3, 0], c_offs], axis=1)
     offs = jnp.clip(offs.astype(jnp.int32), 0, IBS - 1).reshape(-1)
     return gram_call(offs, blocks, column_blocks)
 

time: 124 us -> 139 us (1.12)
  local copies, waits for them, and re-layouts: 18 us -> 28.9 us
  waiting for transfers between devices: 35 us -> 40.3 us
  starting transfers between devices: 46 us -> 44.4 us
    ppermute x7, waiting for transfers between devices: 0.02 us -> 29.2 us  [local(): b = lax.ppermute(b, 'col', backward)]
    ppermute x7, waiting for transfers between devices: 35 us -> 9.39 us  [local(): a = lax.ppermute(a, 'col', forward)]
    ppermute x7, starting transfers between devices: 10.5 us -> 3.49 us  [local(): a = lax.ppermute(a, 'col', forward)]
    ppermute x7, starting transfers between devices: 4.8 us -> 11.4 us  [local(): b = lax.ppermute(b, 'col', backward)]
    concatenate x1 -> x2, local copies, waits for them, and re-layouts: 0.84 us -> 5.18 us  [local(): blocks = jnp.concatenate(pieces, axis=1)]
    unnamed x29 -> x51, local copies, waits for them, and re-layouts: 11.2 us -> 13.9 us
    squeeze x15, local copies, waits for them, and re-layouts: 0.3 us -> 2.27 us  [pick_slot(): return lax.dynamic_index_in_dim(piece, slot, axis=2, keepdims=False)]
    ppermute x15, waiting for transfers between devices: 0.04 us -> 1.7 us  [send(): lax.ppermute(v, ('row', 'col'), [(a * ncol + cc, b * ncol + cc) for a, b,...]
  transfers between devices with their start and end apart: 29 -> 29, of which waited for: 7 -> 9; matrix products, arithmetic and copies ran while one was open for 18% -> 21% of each run, Pallas kernels for 0% -> 0%
where the time goes in v25:
time: 139 us; the launch traced here: 137 us
  starting transfers between devices  44.4 us (32%)
  waiting for transfers between devices  40.3 us (29%)
  local copies, waits for them, and re-layouts  28.9 us (21%)
  other arithmetic  12.1 us (9%)
  Pallas kernels  10.4 us (7%)
    ppermute x15, starting transfers between devices, send(): lax.ppermute(v, ('row', 'col'), [(a * ncol + cc, b * ncol + cc) for a, b,...  29.6 us
    ppermute x7, waiting for transfers between devices, local(): b = lax.ppermute(b, 'col', backward)  29.2 us
    unnamed x51, local copies, waits for them, and re-layouts  13.9 us
    ppermute x7, starting transfers between devices, local(): b = lax.ppermute(b, 'col', backward)  11.4 us
    pallas_call x1, Pallas kernels, gram_call(): pl.pallas_call(kernel, grid_spec=pltpu.PrefetchScalarGridSpec(num_scalar_...  10.4 us
    ppermute x7, waiting for transfers between devices, local(): a = lax.ppermute(a, 'col', forward)  9.39 us
    unnamed x5, other arithmetic  6.76 us
    concatenate x2, local copies, waits for them, and re-layouts, local(): blocks = jnp.concatenate(pieces, axis=1)  5.18 us
  transfers between devices with their start and end apart: 29, of which 9 were waited for; matrix products, arithmetic and copies ran while one was open for 21% of the time, Pallas kernels for 0%

profile of v25, /device:TPU:0, one launch (start us, length us, event | category | flops | bytes accessed | tf_op | source)
XLA Modules:
  0.0 136.6 jit_solution(10121564994347899340)
XLA Ops:
  1.6 2.4 %constant_dynamic-update-slice_fusion.14 = (bf16[3,32,2,144,128]{4,3,1,0,2:T(8,128)(2,1)}, bf16[3,4,2,144,128]{4,3,1,0,2:T(8,128)(2,1)S(1)}) fusion(bf16[144]{0:T(256)(128)(2,1)S(1)} %pad.21.clone, bf16[3,4,2,1,128]{4,3,1,0,2:T(2,128)(2,1)S(1)} %broadcast_in_dim.7, bf16[3,4,2,3,128]{4,3,1,0,2:T(4,128)(2,1)S(1)} %broadcast_in_dim.6, ...), kind=kLoop, calls=%fused_computation.41 | loop fusion | flops 3538943 | bytes 2580768
  4.1 3.0 %collective-permute-start.1 = (bf16[3,2,2,144,128]{4,3,1,0,2:T(8,128)(2,1)S(1)}, bf16[3,2,2,144,128]{4,3,1,0,2:T(8,128)(2,1)S(1)}, u32[]{:S(2)}, u32[]{:S(2)}) collective-permute-start(bf16[3,2,2,144,128]{4,3,1,0,2:T(8,128)(2,1)S(1)} %get-tuple-element.16), channel_id=1, source_target_pairs={{2,0},{4,2},{6,4},{7,6},{5,7},{3,5},{1,3},{0,1},{10,8},{12,10},{14... | collective-permute-start | bytes 1327112 | tf_op jit(solution)/shard_map/ppermute | solution.py:130
  7.2 10.1 %collective-permute-done.1 = bf16[3,2,2,144,128]{4,3,1,0,2:T(8,128)(2,1)S(1)} collective-permute-done((bf16[3,2,2,144,128]{4,3,1,0,2:T(8,128)(2,1)S(1)}, bf16[3,2,2,144,128]{4,3,1,0,2:T(8,128)(2,1)S(1)}, u32[]{:S(2)}, u32[]{:S(2)}) %collective-permute-start.1) | collective-permute-done | bytes 442400 | tf_op jit(solution)/shard_map/ppermute | solution.py:130
  17.3 1.7 %collective-permute-start.3 = (bf16[3,2,2,144,128]{4,3,1,0,2:T(8,128)(2,1)S(1)}, bf16[3,2,2,144,128]{4,3,1,0,2:T(8,128)(2,1)S(1)}, u32[]{:S(2)}, u32[]{:S(2)}) collective-permute-start(bf16[3,2,2,144,128]{4,3,1,0,2:T(8,128)(2,1)S(1)} %collective-permute-done.1), channel_id=1, source_target_pairs={{2,0},{4,2},{6,4},{7,6},{5,7},{3,5},{1,3},{0,1},{10,8},{12,10},{14... | collective-permute-start | bytes 1327112 | tf_op jit(solution)/shard_map/ppermute | solution.py:130
  19.6 1.3 collective-permute-start.14
  20.9 3.0 %collective-permute-start.15 = (bf16[3,8,144,128]{3,2,1,0:T(8,128)(2,1)S(1)}, bf16[3,8,144,128]{3,2,1,0:T(8,128)(2,1)S(1)}, u32[]{:S(2)}, u32[]{:S(2)}) collective-permute-start(bf16[3,8,144,128]{3,2,1,0:T(8,128)(2,1)S(1)} %pad_maximum_fusion), channel_id=1, source_target_pairs={{0,16},{1,17},{10,26},{11,27},{20,4},{21,5},{30,14},{31,15}} | collective-permute-start | bytes 2654216 | tf_op jit(solution)/shard_map/ppermute | solution.py:105
  25.6 3.1 %collective-permute-done.3 = bf16[3,2,2,144,128]{4,3,1,0,2:T(8,128)(2,1)S(1)} collective-permute-done((bf16[3,2,2,144,128]{4,3,1,0,2:T(8,128)(2,1)S(1)}, bf16[3,2,2,144,128]{4,3,1,0,2:T(8,128)(2,1)S(1)}, u32[]{:S(2)}, u32[]{:S(2)}) %collective-permute-start.3) | collective-permute-done | bytes 442400 | tf_op jit(solution)/shard_map/ppermute | solution.py:130
  28.7 1.4 collective-permute-start.5
  32.5 6.6 %collective-permute-done.5 = bf16[3,2,2,144,128]{4,3,1,0,2:T(8,128)(2,1)S(1)} collective-permute-done((bf16[3,2,2,144,128]{4,3,1,0,2:T(8,128)(2,1)S(1)}, bf16[3,2,2,144,128]{4,3,1,0,2:T(8,128)(2,1)S(1)}, u32[]{:S(2)}, u32[]{:S(2)}) %collective-permute-start.5) | collective-permute-done | bytes 442400 | tf_op jit(solution)/shard_map/ppermute | solution.py:130
  42.2 4.1 %collective-permute-start.18 = (bf16[3,8,144,128]{3,2,1,0:T(8,128)(2,1)}, bf16[3,8,144,128]{3,2,1,0:T(8,128)(2,1)}, u32[]{:S(2)}, u32[]{:S(2)}) collective-permute-start(bf16[3,8,144,128]{3,2,1,0:T(8,128)(2,1)} %pad_maximum_fusion.1), channel_id=1, source_target_pairs={{0,16},{1,17},{10,26},{11,27},{20,4},{21,5},{30,14},{31,15}} | collective-permute-start | bytes 2654216 | tf_op jit(solution)/shard_map/ppermute | solution.py:105
  53.2 4.9 %collective-permute-done.9 = bf16[3,2,2,144,128]{4,3,1,0,2:T(8,128)(2,1)S(1)} collective-permute-done((bf16[3,2,2,144,128]{4,3,1,0,2:T(8,128)(2,1)S(1)}, bf16[3,2,2,144,128]{4,3,1,0,2:T(8,128)(2,1)S(1)}, u32[]{:S(2)}, u32[]{:S(2)}) %collective-permute-start.9) | collective-permute-done | bytes 442400 | tf_op jit(solution)/shard_map/ppermute | solution.py:130
  58.1 2.2 %collective-permute-start.17 = (bf16[3,8,144,128]{3,2,1,0:T(8,128)(2,1)}, bf16[3,8,144,128]{3,2,1,0:T(8,128)(2,1)}, u32[]{:S(2)}, u32[]{:S(2)}) collective-permute-start(bf16[3,8,144,128]{3,2,1,0:T(8,128)(2,1)} %pad_maximum_fusion.1), channel_id=1, source_target_pairs={{0,8},{1,9},{10,2},{11,3},{20,28},{21,29},{30,22},{31,23}} | collective-permute-start | bytes 2654216 | tf_op jit(solution)/shard_map/ppermute | solution.py:105
  61.4 5.4 %collective-permute-start.21 = (bf16[3,8,144,128]{3,2,1,0:T(8,128)(2,1)}, bf16[3,8,144,128]{3,2,1,0:T(8,128)(2,1)}, u32[]{:S(2)}, u32[]{:S(2)}) collective-permute-start(bf16[3,8,144,128]{3,2,1,0:T(8,128)(2,1)} %pad_maximum_fusion.2), channel_id=1, source_target_pairs={{0,16},{1,17},{10,26},{11,27},{20,4},{21,5},{30,14},{31,15}} | collective-permute-start | bytes 2654216 | tf_op jit(solution)/shard_map/ppermute | solution.py:105
  66.8 1.4 collective-permute-start.11
  68.9 1.6 %collective-permute-start.19 = (bf16[3,8,144,128]{3,2,1,0:T(8,128)(2,1)}, bf16[3,8,144,128]{3,2,1,0:T(8,128)(2,1)}, u32[]{:S(2)}, u32[]{:S(2)}) collective-permute-start(bf16[3,8,144,128]{3,2,1,0:T(8,128)(2,1)} %collective-permute-done.18), channel_id=1, source_target_pairs={{16,24},{17,25},{26,18},{27,19},{4,12},{5,13},{14,6},{15,7}} | collective-permute-start | bytes 2654216 | tf_op jit(solution)/shard_map/ppermute | solution.py:105
  72.8 3.9 %collective-permute-done.11 = bf16[3,2,2,144,128]{4,3,1,0,2:T(8,128)(2,1)S(1)} collective-permute-done((bf16[3,2,2,144,128]{4,3,1,0,2:T(8,128)(2,1)S(1)}, bf16[3,2,2,144,128]{4,3,1,0,2:T(8,128)(2,1)S(1)}, u32[]{:S(2)}, u32[]{:S(2)}) %collective-permute-start.11) | collective-permute-done | bytes 442400 | tf_op jit(solution)/shard_map/ppermute | solution.py:130
  76.7 1.4 %collective-permute-start.13 = (bf16[3,2,2,144,128]{4,3,1,0,2:T(8,128)(2,1)S(1)}, bf16[3,2,2,144,128]{4,3,1,0,2:T(8,128)(2,1)S(1)}, u32[]{:S(2)}, u32[]{:S(2)}) collective-permute-start(bf16[3,2,2,144,128]{4,3,1,0,2:T(8,128)(2,1)S(1)} %collective-permute-done.11), channel_id=1, source_target_pairs={{2,0},{4,2},{6,4},{7,6},{5,7},{3,5},{1,3},{0,1},{10,8},{12,10},{14... | collective-permute-start | bytes 1327112 | tf_op jit(solution)/shard_map/ppermute | solution.py:130
  81.3 8.9 %collective-permute-done.12 = bf16[3,2,2,144,128]{4,3,1,0,2:T(8,128)(2,1)S(1)} collective-permute-done((bf16[3,2,2,144,128]{4,3,1,0,2:T(8,128)(2,1)S(1)}, bf16[3,2,2,144,128]{4,3,1,0,2:T(8,128)(2,1)S(1)}, u32[]{:S(2)}, u32[]{:S(2)}) %collective-permute-start.12) | collective-permute-done | bytes 442400 | tf_op jit(solution)/shard_map/ppermute | solution.py:129
  90.3 2.2 %collective-permute-start.20 = (bf16[3,8,144,128]{3,2,1,0:T(8,128)(2,1)}, bf16[3,8,144,128]{3,2,1,0:T(8,128)(2,1)}, u32[]{:S(2)}, u32[]{:S(2)}) collective-permute-start(bf16[3,8,144,128]{3,2,1,0:T(8,128)(2,1)} %pad_maximum_fusion.2), channel_id=1, source_target_pairs={{0,8},{1,9},{10,2},{11,3},{20,28},{21,29},{30,22},{31,23}} | collective-permute-start | bytes 2654216 | tf_op jit(solution)/shard_map/ppermute | solution.py:105
  93.3 2.1 %collective-permute-start.24 = (bf16[3,4,144,128]{3,2,1,0:T(8,128)(2,1)}, bf16[3,4,144,128]{3,2,1,0:T(8,128)(2,1)}, u32[]{:S(2)}, u32[]{:S(2)}) collective-permute-start(bf16[3,4,144,128]{3,2,1,0:T(8,128)(2,1)} %pad_maximum_fusion.3), channel_id=1, source_target_pairs={{0,16},{1,17},{10,26},{11,27},{20,4},{21,5},{30,14},{31,15}} | collective-permute-start | bytes 1327112 | tf_op jit(solution)/shard_map/ppermute | solution.py:105
  95.4 1.6 %collective-permute-start.22 = (bf16[3,8,144,128]{3,2,1,0:T(8,128)(2,1)}, bf16[3,8,144,128]{3,2,1,0:T(8,128)(2,1)}, u32[]{:S(2)}, u32[]{:S(2)}) collective-permute-start(bf16[3,8,144,128]{3,2,1,0:T(8,128)(2,1)} %collective-permute-done.21), channel_id=1, source_target_pairs={{16,24},{17,25},{26,18},{27,19},{4,12},{5,13},{14,6},{15,7}} | collective-permute-start | bytes 2654216 | tf_op jit(solution)/shard_map/ppermute | solution.py:105
  97.8 4.3 %copy.17 = bf16[3,32,2,144,128]{4,3,2,1,0:T(8,128)(2,1)S(1)} copy(bf16[3,32,2,144,128]{4,3,1,0,2:T(8,128)(2,1)} %constant_dynamic-update-slice_fusion) | data formatting | bytes 14155776 | tf_op jit(solution)/shard_map/concatenate | solution.py:144
  102.2 2.9 %copy-done = bf16[3,32,2,144,128]{4,3,2,1,0:T(8,128)(2,1)} copy-done((bf16[3,32,2,144,128]{4,3,2,1,0:T(8,128)(2,1)}, bf16[3,32,2,144,128]{4,3,2,1,0:T(8,128)(2,1)S(1)}, u32[]{:S(2)}) %copy-start) | copy-done | bytes 7077912
  105.8 1.5 %copy.18 = bf16[96,2,1,1]{0,1,3,2:T(2,128)(2,1)} copy(bf16[96,2,1,1]{3,2,1,0:T(2,128)(2,1)} %slice.35) | data formatting | bytes 768 | tf_op jit(solution)/shard_map/slice | solution.py:151
  109.4 1.3 collective-permute-start.23
  110.7 1.3 collective-permute-start.27
  112.8 1.9 %constant_dynamic-update-slice_fusion.18 = (bf16[3,32,144,128]{3,2,1,0:T(8,128)(2,1)S(1)}, bf16[3,8,144,128]{3,2,1,0:T(8,128)(2,1)S(1)}) fusion(bf16[3,32,144,128]{3,2,1,0:T(8,128)(2,1)S(1)} %get-tuple-element.13, bf16[3,8,144,128]{3,2,1,0:T(8,128)(2,1)} %collective-permute-done.17, bf16[3,8,144,128]{3,2,1,0:T(8,128)(2,1)} %collective-permute-done.18, ...), kind=kLoop, calls=%fused_computation.45 | loop fusion | flops 4866048 | bytes 5308419
  114.9 1.3 collective-permute-start.26
  116.2 1.7 %collective-permute-done.27 = bf16[3,4,144,128]{3,2,1,0:T(8,128)(2,1)S(1)} collective-permute-done((bf16[3,4,144,128]{3,2,1,0:T(8,128)(2,1)S(1)}, bf16[3,4,144,128]{3,2,1,0:T(8,128)(2,1)S(1)}, u32[]{:S(2)}, u32[]{:S(2)}) %collective-permute-start.27) | collective-permute-done | bytes 442400 | tf_op jit(solution)/shard_map/ppermute | solution.py:105
  118.6 1.7 %constant_dynamic-update-slice_fusion.17 = (bf16[3,32,144,128]{3,2,1,0:T(8,128)(2,1)S(1)}, bf16[3,8,144,128]{3,2,1,0:T(8,128)(2,1)S(1)}) fusion(bf16[3,32,144,128]{3,2,1,0:T(8,128)(2,1)S(1)} %get-tuple-element.11, bf16[3,8,144,128]{3,2,1,0:T(8,128)(2,1)} %collective-permute-done.20, bf16[3,8,144,128]{3,2,1,0:T(8,128)(2,1)} %collective-permute-done.21, ...), kind=kLoop, calls=%fused_computation.44 | loop fusion | flops 4866048 | bytes 5308419
  121.9 1.3 concatenate.43
  126.3 10.4 %shard_map.37 = f32[2048,1024]{1,0:T(8,128)} custom-call(s32[288]{0:T(512)S(1)} %min.12.offs_ref, bf16[96,2,144,128]{3,2,1,0:T(8,128)(2,1)} %bitcast.43, bf16[96,144,128]{2,1,0:T(8,128)(2,1)S(1)} %bitcast.41), custom_call_target="tpu_custom_call" | custom-call | flops 805306368 | bytes 17825792 | tf_op jit(solution)/shard_map/pallas_call | solution.py:40
  (128 shorter events, 34.2 us)
Async XLA Ops:
  4.1 13.2 %collective-permute-start.1 = (bf16[3,2,2,144,128]{4,3,1,0,2:T(8,128)(2,1)S(1)}, bf16[3,2,2,144,128]{4,3,1,0,2:T(8,128)(2,1)S(1)}, u32[]{:S(2)}, u32[]{:S(2)}) collective-permute-start(bf16[3,2,2,144,128]{4,3,1,0,2:T(8,128)(2,1)S(1)} %get-tuple-element.16), channel_id=1, source_target_pairs={{2,0},{4,2},{6,4},{7,6},{5,7},{3,5},{1,3},{0,1},{10,8},{12,10},{14... | collective-permute-start | bytes 1327112 | tf_op jit(solution)/shard_map/ppermute | solution.py:130
  7.1 11.9 %collective-permute-start = (bf16[3,2,2,144,128]{4,3,1,0,2:T(8,128)(2,1)S(1)}, bf16[3,2,2,144,128]{4,3,1,0,2:T(8,128)(2,1)S(1)}, u32[]{:S(2)}, u32[]{:S(2)}) collective-permute-start(bf16[3,2,2,144,128]{4,3,1,0,2:T(8,128)(2,1)S(1)} %get-tuple-element.15), channel_id=1, source_target_pairs={{0,2},{2,4},{4,6},{6,7},{7,5},{5,3},{3,1},{1,0},{8,10},{10,12},{12... | collective-permute-start | bytes 1327112 | tf_op jit(solution)/shard_map/ppermute | solution.py:129
  17.3 11.4 %collective-permute-start.3 = (bf16[3,2,2,144,128]{4,3,1,0,2:T(8,128)(2,1)S(1)}, bf16[3,2,2,144,128]{4,3,1,0,2:T(8,128)(2,1)S(1)}, u32[]{:S(2)}, u32[]{:S(2)}) collective-permute-start(bf16[3,2,2,144,128]{4,3,1,0,2:T(8,128)(2,1)S(1)} %collective-permute-done.1), channel_id=1, source_target_pairs={{2,0},{4,2},{6,4},{7,6},{5,7},{3,5},{1,3},{0,1},{10,8},{12,10},{14... | collective-permute-start | bytes 1327112 | tf_op jit(solution)/shard_map/ppermute | solution.py:130
  19.0 11.0 %collective-permute-start.2 = (bf16[3,2,2,144,128]{4,3,1,0,2:T(8,128)(2,1)S(1)}, bf16[3,2,2,144,128]{4,3,1,0,2:T(8,128)(2,1)S(1)}, u32[]{:S(2)}, u32[]{:S(2)}) collective-permute-start(bf16[3,2,2,144,128]{4,3,1,0,2:T(8,128)(2,1)S(1)} %collective-permute-done), channel_id=1, source_target_pairs={{0,2},{2,4},{4,6},{6,7},{7,5},{5,3},{3,1},{1,0},{8,10},{10,12},{12... | collective-permute-start | bytes 1327112 | tf_op jit(solution)/shard_map/ppermute | solution.py:129
  19.6 47.2 %collective-permute-start.14 = (bf16[3,8,144,128]{3,2,1,0:T(8,128)(2,1)S(1)}, bf16[3,8,144,128]{3,2,1,0:T(8,128)(2,1)S(1)}, u32[]{:S(2)}, u32[]{:S(2)}) collective-permute-start(bf16[3,8,144,128]{3,2,1,0:T(8,128)(2,1)S(1)} %pad_maximum_fusion), channel_id=1, source_target_pairs={{0,8},{1,9},{10,2},{11,3},{20,28},{21,29},{30,22},{31,23}} | collective-permute-start | bytes 2654216 | tf_op jit(solution)/shard_map/ppermute | solution.py:105
  20.9 25.5 %collective-permute-start.15 = (bf16[3,8,144,128]{3,2,1,0:T(8,128)(2,1)S(1)}, bf16[3,8,144,128]{3,2,1,0:T(8,128)(2,1)S(1)}, u32[]{:S(2)}, u32[]{:S(2)}) collective-permute-start(bf16[3,8,144,128]{3,2,1,0:T(8,128)(2,1)S(1)} %pad_maximum_fusion), channel_id=1, source_target_pairs={{0,16},{1,17},{10,26},{11,27},{20,4},{21,5},{30,14},{31,15}} | collective-permute-start | bytes 2654216 | tf_op jit(solution)/shard_map/ppermute | solution.py:105
  28.7 10.4 %collective-permute-start.5 = (bf16[3,2,2,144,128]{4,3,1,0,2:T(8,128)(2,1)S(1)}, bf16[3,2,2,144,128]{4,3,1,0,2:T(8,128)(2,1)S(1)}, u32[]{:S(2)}, u32[]{:S(2)}) collective-permute-start(bf16[3,2,2,144,128]{4,3,1,0,2:T(8,128)(2,1)S(1)} %collective-permute-done.3), channel_id=1, source_target_pairs={{2,0},{4,2},{6,4},{7,6},{5,7},{3,5},{1,3},{0,1},{10,8},{12,10},{14... | collective-permute-start | bytes 1327112 | tf_op jit(solution)/shard_map/ppermute | solution.py:130
  30.0 10.3 %collective-permute-start.4 = (bf16[3,2,2,144,128]{4,3,1,0,2:T(8,128)(2,1)S(1)}, bf16[3,2,2,144,128]{4,3,1,0,2:T(8,128)(2,1)S(1)}, u32[]{:S(2)}, u32[]{:S(2)}) collective-permute-start(bf16[3,2,2,144,128]{4,3,1,0,2:T(8,128)(2,1)S(1)} %collective-permute-done.2), channel_id=1, source_target_pairs={{0,2},{2,4},{4,6},{6,7},{7,5},{5,3},{3,1},{1,0},{8,10},{10,12},{12... | collective-permute-start | bytes 1327112 | tf_op jit(solution)/shard_map/ppermute | solution.py:129
  30.7 38.1 %copy-start.1 = (bf16[3,2,144,128]{3,2,1,0:T(8,128)(2,1)}, bf16[3,2,144,128]{3,2,1,0:T(8,128)(2,1)S(1)}, u32[]{:S(2)}) copy-start(bf16[3,2,144,128]{3,2,1,0:T(8,128)(2,1)S(1)} %dynamic-slice_bitcast_fusion.10) | copy-start | bytes 663556
  30.7 38.0 %copy-start.2 = (bf16[3,2,144,128]{3,2,1,0:T(8,128)(2,1)}, bf16[3,2,144,128]{3,2,1,0:T(8,128)(2,1)S(1)}, u32[]{:S(2)}) copy-start(bf16[3,2,144,128]{3,2,1,0:T(8,128)(2,1)S(1)} %dynamic-slice_bitcast_fusion.11) | copy-start | bytes 663556
  39.1 10.3 %collective-permute-start.7 = (bf16[3,2,2,144,128]{4,3,1,0,2:T(8,128)(2,1)S(1)}, bf16[3,2,2,144,128]{4,3,1,0,2:T(8,128)(2,1)S(1)}, u32[]{:S(2)}, u32[]{:S(2)}) collective-permute-start(bf16[3,2,2,144,128]{4,3,1,0,2:T(8,128)(2,1)S(1)} %collective-permute-done.5), channel_id=1, source_target_pairs={{2,0},{4,2},{6,4},{7,6},{5,7},{3,5},{1,3},{0,1},{10,8},{12,10},{14... | collective-permute-start | bytes 1327112 | tf_op jit(solution)/shard_map/ppermute | solution.py:130
  40.4 10.3 %collective-permute-start.6 = (bf16[3,2,2,144,128]{4,3,1,0,2:T(8,128)(2,1)S(1)}, bf16[3,2,2,144,128]{4,3,1,0,2:T(8,128)(2,1)S(1)}, u32[]{:S(2)}, u32[]{:S(2)}) collective-permute-start(bf16[3,2,2,144,128]{4,3,1,0,2:T(8,128)(2,1)S(1)} %collective-permute-done.4), channel_id=1, source_target_pairs={{0,2},{2,4},{4,6},{6,7},{7,5},{5,3},{3,1},{1,0},{8,10},{10,12},{12... | collective-permute-start | bytes 1327112 | tf_op jit(solution)/shard_map/ppermute | solution.py:129
  41.1 27.7 %copy-start.3 = (bf16[3,2,144,128]{3,2,1,0:T(8,128)(2,1)}, bf16[3,2,144,128]{3,2,1,0:T(8,128)(2,1)S(1)}, u32[]{:S(2)}) copy-start(bf16[3,2,144,128]{3,2,1,0:T(8,128)(2,1)S(1)} %dynamic-slice_bitcast_fusion.8) | copy-start | bytes 663556
  42.2 26.6 %collective-permute-start.18 = (bf16[3,8,144,128]{3,2,1,0:T(8,128)(2,1)}, bf16[3,8,144,128]{3,2,1,0:T(8,128)(2,1)}, u32[]{:S(2)}, u32[]{:S(2)}) collective-permute-start(bf16[3,8,144,128]{3,2,1,0:T(8,128)(2,1)} %pad_maximum_fusion.1), channel_id=1, source_target_pairs={{0,16},{1,17},{10,26},{11,27},{20,4},{21,5},{30,14},{31,15}} | collective-permute-start | bytes 2654216 | tf_op jit(solution)/shard_map/ppermute | solution.py:105
  46.4 21.8 %collective-permute-start.16 = (bf16[3,8,144,128]{3,2,1,0:T(8,128)(2,1)S(1)}, bf16[3,8,144,128]{3,2,1,0:T(8,128)(2,1)S(1)}, u32[]{:S(2)}, u32[]{:S(2)}) collective-permute-start(bf16[3,8,144,128]{3,2,1,0:T(8,128)(2,1)S(1)} %collective-permute-done.15), channel_id=1, source_target_pairs={{16,24},{17,25},{26,18},{27,19},{4,12},{5,13},{14,6},{15,7}} | collective-permute-start | bytes 2654216 | tf_op jit(solution)/shard_map/ppermute | solution.py:105
  49.4 8.7 %collective-permute-start.9 = (bf16[3,2,2,144,128]{4,3,1,0,2:T(8,128)(2,1)S(1)}, bf16[3,2,2,144,128]{4,3,1,0,2:T(8,128)(2,1)S(1)}, u32[]{:S(2)}, u32[]{:S(2)}) collective-permute-start(bf16[3,2,2,144,128]{4,3,1,0,2:T(8,128)(2,1)S(1)} %collective-permute-done.7), channel_id=1, source_target_pairs={{2,0},{4,2},{6,4},{7,6},{5,7},{3,5},{1,3},{0,1},{10,8},{12,10},{14... | collective-permute-start | bytes 1327112 | tf_op jit(solution)/shard_map/ppermute | solution.py:130
  50.7 9.6 %collective-permute-start.8 = (bf16[3,2,2,144,128]{4,3,1,0,2:T(8,128)(2,1)S(1)}, bf16[3,2,2,144,128]{4,3,1,0,2:T(8,128)(2,1)S(1)}, u32[]{:S(2)}, u32[]{:S(2)}) collective-permute-start(bf16[3,2,2,144,128]{4,3,1,0,2:T(8,128)(2,1)S(1)} %collective-permute-done.6), channel_id=1, source_target_pairs={{0,2},{2,4},{4,6},{6,7},{7,5},{5,3},{3,1},{1,0},{8,10},{10,12},{12... | collective-permute-start | bytes 1327112 | tf_op jit(solution)/shard_map/ppermute | solution.py:129
  58.1 51.3 %collective-permute-start.17 = (bf16[3,8,144,128]{3,2,1,0:T(8,128)(2,1)}, bf16[3,8,144,128]{3,2,1,0:T(8,128)(2,1)}, u32[]{:S(2)}, u32[]{:S(2)}) collective-permute-start(bf16[3,8,144,128]{3,2,1,0:T(8,128)(2,1)} %pad_maximum_fusion.1), channel_id=1, source_target_pairs={{0,8},{1,9},{10,2},{11,3},{20,28},{21,29},{30,22},{31,23}} | collective-permute-start | bytes 2654216 | tf_op jit(solution)/shard_map/ppermute | solution.py:105
  61.4 31.9 %collective-permute-start.21 = (bf16[3,8,144,128]{3,2,1,0:T(8,128)(2,1)}, bf16[3,8,144,128]{3,2,1,0:T(8,128)(2,1)}, u32[]{:S(2)}, u32[]{:S(2)}) collective-permute-start(bf16[3,8,144,128]{3,2,1,0:T(8,128)(2,1)} %pad_maximum_fusion.2), channel_id=1, source_target_pairs={{0,16},{1,17},{10,26},{11,27},{20,4},{21,5},{30,14},{31,15}} | collective-permute-start | bytes 2654216 | tf_op jit(solution)/shard_map/ppermute | solution.py:105
  66.8 9.9 %collective-permute-start.11 = (bf16[3,2,2,144,128]{4,3,1,0,2:T(8,128)(2,1)S(1)}, bf16[3,2,2,144,128]{4,3,1,0,2:T(8,128)(2,1)S(1)}, u32[]{:S(2)}, u32[]{:S(2)}) collective-permute-start(bf16[3,2,2,144,128]{4,3,1,0,2:T(8,128)(2,1)S(1)} %collective-permute-done.9), channel_id=1, source_target_pairs={{2,0},{4,2},{6,4},{7,6},{5,7},{3,5},{1,3},{0,1},{10,8},{12,10},{14... | collective-permute-start | bytes 1327112 | tf_op jit(solution)/shard_map/ppermute | solution.py:130
  68.1 10.5 %collective-permute-start.10 = (bf16[3,2,2,144,128]{4,3,1,0,2:T(8,128)(2,1)S(1)}, bf16[3,2,2,144,128]{4,3,1,0,2:T(8,128)(2,1)S(1)}, u32[]{:S(2)}, u32[]{:S(2)}) collective-permute-start(bf16[3,2,2,144,128]{4,3,1,0,2:T(8,128)(2,1)S(1)} %collective-permute-done.8), channel_id=1, source_target_pairs={{0,2},{2,4},{4,6},{6,7},{7,5},{5,3},{3,1},{1,0},{8,10},{10,12},{12... | collective-permute-start | bytes 1327112 | tf_op jit(solution)/shard_map/ppermute | solution.py:129
  68.9 41.9 %collective-permute-start.19 = (bf16[3,8,144,128]{3,2,1,0:T(8,128)(2,1)}, bf16[3,8,144,128]{3,2,1,0:T(8,128)(2,1)}, u32[]{:S(2)}, u32[]{:S(2)}) collective-permute-start(bf16[3,8,144,128]{3,2,1,0:T(8,128)(2,1)} %collective-permute-done.18), channel_id=1, source_target_pairs={{16,24},{17,25},{26,18},{27,19},{4,12},{5,13},{14,6},{15,7}} | collective-permute-start | bytes 2654216 | tf_op jit(solution)/shard_map/ppermute | solution.py:105
  76.7 18.7 %collective-permute-start.13 = (bf16[3,2,2,144,128]{4,3,1,0,2:T(8,128)(2,1)S(1)}, bf16[3,2,2,144,128]{4,3,1,0,2:T(8,128)(2,1)S(1)}, u32[]{:S(2)}, u32[]{:S(2)}) collective-permute-start(bf16[3,2,2,144,128]{4,3,1,0,2:T(8,128)(2,1)S(1)} %collective-permute-done.11), channel_id=1, source_target_pairs={{2,0},{4,2},{6,4},{7,6},{5,7},{3,5},{1,3},{0,1},{10,8},{12,10},{14... | collective-permute-start | bytes 1327112 | tf_op jit(solution)/shard_map/ppermute | solution.py:130
  78.6 11.7 %collective-permute-start.12 = (bf16[3,2,2,144,128]{4,3,1,0,2:T(8,128)(2,1)S(1)}, bf16[3,2,2,144,128]{4,3,1,0,2:T(8,128)(2,1)S(1)}, u32[]{:S(2)}, u32[]{:S(2)}) collective-permute-start(bf16[3,2,2,144,128]{4,3,1,0,2:T(8,128)(2,1)S(1)} %collective-permute-done.10), channel_id=1, source_target_pairs={{0,2},{2,4},{4,6},{6,7},{7,5},{5,3},{3,1},{1,0},{8,10},{10,12},{12... | collective-permute-start | bytes 1327112 | tf_op jit(solution)/shard_map/ppermute | solution.py:129
  90.3 24.6 %collective-permute-start.20 = (bf16[3,8,144,128]{3,2,1,0:T(8,128)(2,1)}, bf16[3,8,144,128]{3,2,1,0:T(8,128)(2,1)}, u32[]{:S(2)}, u32[]{:S(2)}) collective-permute-start(bf16[3,8,144,128]{3,2,1,0:T(8,128)(2,1)} %pad_maximum_fusion.2), channel_id=1, source_target_pairs={{0,8},{1,9},{10,2},{11,3},{20,28},{21,29},{30,22},{31,23}} | collective-permute-start | bytes 2654216 | tf_op jit(solution)/shard_map/ppermute | solution.py:105
  93.3 18.7 %collective-permute-start.24 = (bf16[3,4,144,128]{3,2,1,0:T(8,128)(2,1)}, bf16[3,4,144,128]{3,2,1,0:T(8,128)(2,1)}, u32[]{:S(2)}, u32[]{:S(2)}) collective-permute-start(bf16[3,4,144,128]{3,2,1,0:T(8,128)(2,1)} %pad_maximum_fusion.3), channel_id=1, source_target_pairs={{0,16},{1,17},{10,26},{11,27},{20,4},{21,5},{30,14},{31,15}} | collective-permute-start | bytes 1327112 | tf_op jit(solution)/shard_map/ppermute | solution.py:105
  95.4 23.1 %collective-permute-start.22 = (bf16[3,8,144,128]{3,2,1,0:T(8,128)(2,1)}, bf16[3,8,144,128]{3,2,1,0:T(8,128)(2,1)}, u32[]{:S(2)}, u32[]{:S(2)}) collective-permute-start(bf16[3,8,144,128]{3,2,1,0:T(8,128)(2,1)} %collective-permute-done.21), channel_id=1, source_target_pairs={{16,24},{17,25},{26,18},{27,19},{4,12},{5,13},{14,6},{15,7}} | collective-permute-start | bytes 2654216 | tf_op jit(solution)/shard_map/ppermute | solution.py:105
  109.4 10.9 %collective-permute-start.23 = (bf16[3,4,144,128]{3,2,1,0:T(8,128)(2,1)}, bf16[3,4,144,128]{3,2,1,0:T(8,128)(2,1)S(1)}, u32[]{:S(2)}, u32[]{:S(2)}) collective-permute-start(bf16[3,4,144,128]{3,2,1,0:T(8,128)(2,1)} %pad_maximum_fusion.3), channel_id=1, source_target_pairs={{0,8},{1,9},{10,2},{11,3},{20,28},{21,29},{30,22},{31,23}} | collective-permute-start | bytes 1327112 | tf_op jit(solution)/shard_map/ppermute | solution.py:105
  110.7 7.1 %collective-permute-start.27 = (bf16[3,4,144,128]{3,2,1,0:T(8,128)(2,1)S(1)}, bf16[3,4,144,128]{3,2,1,0:T(8,128)(2,1)S(1)}, u32[]{:S(2)}, u32[]{:S(2)}) collective-permute-start(bf16[3,4,144,128]{3,2,1,0:T(8,128)(2,1)S(1)} %pad_maximum_fusion.4), channel_id=1, source_target_pairs={{0,16},{1,17},{10,26},{11,27},{20,4},{21,5},{30,14},{31,15}} | collective-permute-start | bytes 1327112 | tf_op jit(solution)/shard_map/ppermute | solution.py:105
  112.1 8.2 %collective-permute-start.25 = (bf16[3,4,144,128]{3,2,1,0:T(8,128)(2,1)}, bf16[3,4,144,128]{3,2,1,0:T(8,128)(2,1)S(1)}, u32[]{:S(2)}, u32[]{:S(2)}) collective-permute-start(bf16[3,4,144,128]{3,2,1,0:T(8,128)(2,1)} %collective-permute-done.24), channel_id=1, source_target_pairs={{16,24},{17,25},{26,18},{27,19},{4,12},{5,13},{14,6},{15,7}} | collective-permute-start | bytes 1327112 | tf_op jit(solution)/shard_map/ppermute | solution.py:105
  114.9 6.6 %collective-permute-start.26 = (bf16[3,4,144,128]{3,2,1,0:T(8,128)(2,1)S(1)}, bf16[3,4,144,128]{3,2,1,0:T(8,128)(2,1)S(1)}, u32[]{:S(2)}, u32[]{:S(2)}) collective-permute-start(bf16[3,4,144,128]{3,2,1,0:T(8,128)(2,1)S(1)} %pad_maximum_fusion.4), channel_id=1, source_target_pairs={{0,8},{1,9},{10,2},{11,3},{20,28},{21,29},{30,22},{31,23}} | collective-permute-start | bytes 1327112 | tf_op jit(solution)/shard_map/ppermute | solution.py:105
  117.8 3.6 %collective-permute-start.28 = (bf16[3,4,144,128]{3,2,1,0:T(8,128)(2,1)S(1)}, bf16[3,4,144,128]{3,2,1,0:T(8,128)(2,1)S(1)}, u32[]{:S(2)}, u32[]{:S(2)}) collective-permute-start(bf16[3,4,144,128]{3,2,1,0:T(8,128)(2,1)S(1)} %collective-permute-done.27), channel_id=1, source_target_pairs={{16,24},{17,25},{26,18},{27,19},{4,12},{5,13},{14,6},{15,7}} | collective-permute-start | bytes 1327112 | tf_op jit(solution)/shard_map/ppermute | solution.py:105
  (16 other events, 198.0 us)

commit v26 on v24

--- a/solution.py
+++ b/solution.py
@@ -120,7 +120,7 @@
     def pick_slot(piece):
         return lax.dynamic_index_in_dim(piece, slot, axis=2, keepdims=False)
 
-    batches = [[k, k + 1] for k in range(0, ncol - 2, 2)] + [[ncol - 2], [ncol - 1]]
+    batches = [[k] for k in range(ncol)]
     half = x.shape[1] // 2
     a, b = x[:, :half], x[:, half:]
     pieces, columns, pending = [], [], []

time: 124 us -> 120 us (0.968)
  waiting for transfers between devices: 35 us -> 13.7 us
  starting transfers between devices: 46 us -> 63 us
    ppermute x7, waiting for transfers between devices: 35 us -> 5.35 us  [local(): a = lax.ppermute(a, 'col', forward)]
    ppermute x15 -> x24, starting transfers between devices: 30.8 us -> 47.8 us  [send(): lax.ppermute(v, ('row', 'col'), [(a * ncol + cc, b * ncol + cc) for a, b,...]
    ppermute x7, waiting for transfers between devices: 0.02 us -> 8.34 us  [local(): b = lax.ppermute(b, 'col', backward)]
    unnamed x29 -> x37, local copies, waits for them, and re-layouts: 11.2 us -> 12.5 us
    concatenate x5 -> x8, other arithmetic: 2.99 us -> 2.8 us  [local(): own = jnp.concatenate(pending, axis=1)]
    unnamed x5 -> x8, other arithmetic: 6.78 us -> 6.64 us
  transfers between devices with their start and end apart: 29 -> 38, of which waited for: 7 -> 7; matrix products, arithmetic and copies ran while one was open for 18% -> 18% of each run, Pallas kernels for 0% -> 0%
where the time goes in v26:
time: 120 us; the launch traced here: 119 us
  starting transfers between devices  63 us (52%)
  local copies, waits for them, and re-layouts  19.2 us (16%)
  waiting for transfers between devices  13.7 us (11%)
  other arithmetic  12.2 us (10%)
  Pallas kernels  10.4 us (9%)
    ppermute x24, starting transfers between devices, send(): lax.ppermute(v, ('row', 'col'), [(a * ncol + cc, b * ncol + cc) for a, b,...  47.8 us
    unnamed x37, local copies, waits for them, and re-layouts  12.5 us
    ppermute x7, starting transfers between devices, local(): a = lax.ppermute(a, 'col', forward)  11.6 us
    pallas_call x1, Pallas kernels, gram_call(): pl.pallas_call(kernel, grid_spec=pltpu.PrefetchScalarGridSpec(num_scalar_...  10.4 us
    ppermute x7, waiting for transfers between devices, local(): b = lax.ppermute(b, 'col', backward)  8.34 us
    unnamed x8, other arithmetic  6.64 us
    ppermute x7, waiting for transfers between devices, local(): a = lax.ppermute(a, 'col', forward)  5.35 us
    ppermute x7, starting transfers between devices, local(): b = lax.ppermute(b, 'col', backward)  3.59 us
  transfers between devices with their start and end apart: 38, of which 7 were waited for; matrix products, arithmetic and copies ran while one was open for 18% of the time, Pallas kernels for 0%

profile of v26, /device:TPU:0, one launch (start us, length us, event | category | flops | bytes accessed | tf_op | source)
XLA Modules:
  0.0 119.2 jit_solution(5697008653390486019)
XLA Ops:
  1.7 2.4 %constant_dynamic-update-slice_fusion.14 = (bf16[3,32,2,144,128]{4,3,2,1,0:T(8,128)(2,1)}, bf16[3,4,2,144,128]{4,3,2,1,0:T(8,128)(2,1)S(1)}) fusion(bf16[144]{0:T(256)(128)(2,1)S(1)} %pad.21.clone, bf16[3,4,2,1,128]{4,3,2,1,0:T(2,128)(2,1)S(1)} %broadcast_in_dim.7, bf16[3,4,2,3,128]{4,3,2,1,0:T(4,128)(2,1)S(1)} %broadcast_in_dim.6, ...), kind=kLoop, calls=%fused_computation.48 | loop fusion | flops 3538943 | bytes 2580768
  4.2 3.1 %collective-permute-start = (bf16[3,2,2,144,128]{4,3,2,1,0:T(8,128)(2,1)S(1)}, bf16[3,2,2,144,128]{4,3,2,1,0:T(8,128)(2,1)S(1)}, u32[]{:S(2)}, u32[]{:S(2)}) collective-permute-start(bf16[3,2,2,144,128]{4,3,2,1,0:T(8,128)(2,1)S(1)} %get-tuple-element.5), channel_id=1, source_target_pairs={{0,2},{2,4},{4,6},{6,7},{7,5},{5,3},{3,1},{1,0},{8,10},{10,12},{12... | collective-permute-start | bytes 1327112 | tf_op jit(solution)/shard_map/ppermute | solution.py:129
  8.1 3.9 %collective-permute-start.15 = (bf16[3,4,144,128]{3,2,1,0:T(8,128)(2,1)S(1)}, bf16[3,4,144,128]{3,2,1,0:T(8,128)(2,1)S(1)}, u32[]{:S(2)}, u32[]{:S(2)}) collective-permute-start(bf16[3,4,144,128]{3,2,1,0:T(8,128)(2,1)S(1)} %pad_maximum_fusion), channel_id=1, source_target_pairs={{0,16},{1,17},{10,26},{11,27},{20,4},{21,5},{30,14},{31,15}} | collective-permute-start | bytes 1327112 | tf_op jit(solution)/shard_map/ppermute | solution.py:105
  12.0 1.3 %collective-permute-start.14 = (bf16[3,4,144,128]{3,2,1,0:T(8,128)(2,1)S(1)}, bf16[3,4,144,128]{3,2,1,0:T(8,128)(2,1)S(1)}, u32[]{:S(2)}, u32[]{:S(2)}) collective-permute-start(bf16[3,4,144,128]{3,2,1,0:T(8,128)(2,1)S(1)} %pad_maximum_fusion), channel_id=1, source_target_pairs={{0,8},{1,9},{10,2},{11,3},{20,28},{21,29},{30,22},{31,23}} | collective-permute-start | bytes 1327112 | tf_op jit(solution)/shard_map/ppermute | solution.py:105
  13.4 4.0 %collective-permute-done = bf16[3,2,2,144,128]{4,3,2,1,0:T(8,128)(2,1)S(1)} collective-permute-done((bf16[3,2,2,144,128]{4,3,2,1,0:T(8,128)(2,1)S(1)}, bf16[3,2,2,144,128]{4,3,2,1,0:T(8,128)(2,1)S(1)}, u32[]{:S(2)}, u32[]{:S(2)}) %collective-permute-start) | collective-permute-done | bytes 442400 | tf_op jit(solution)/shard_map/ppermute | solution.py:129
  17.4 1.8 %collective-permute-start.2 = (bf16[3,2,2,144,128]{4,3,2,1,0:T(8,128)(2,1)S(1)}, bf16[3,2,2,144,128]{4,3,2,1,0:T(8,128)(2,1)S(1)}, u32[]{:S(2)}, u32[]{:S(2)}) collective-permute-start(bf16[3,2,2,144,128]{4,3,2,1,0:T(8,128)(2,1)S(1)} %collective-permute-done), channel_id=1, source_target_pairs={{0,2},{2,4},{4,6},{6,7},{7,5},{5,3},{3,1},{1,0},{8,10},{10,12},{12... | collective-permute-start | bytes 1327112 | tf_op jit(solution)/shard_map/ppermute | solution.py:129
  19.5 3.6 %collective-permute-start.18 = (bf16[3,4,144,128]{3,2,1,0:T(8,128)(2,1)S(1)}, bf16[3,4,144,128]{3,2,1,0:T(8,128)(2,1)S(1)}, u32[]{:S(2)}, u32[]{:S(2)}) collective-permute-start(bf16[3,4,144,128]{3,2,1,0:T(8,128)(2,1)S(1)} %pad_maximum_fusion.1), channel_id=1, source_target_pairs={{0,16},{1,17},{10,26},{11,27},{20,4},{21,5},{30,14},{31,15}} | collective-permute-start | bytes 1327112 | tf_op jit(solution)/shard_map/ppermute | solution.py:105
  25.6 4.3 %collective-permute-done.3 = bf16[3,2,2,144,128]{4,3,2,1,0:T(8,128)(2,1)S(1)} collective-permute-done((bf16[3,2,2,144,128]{4,3,2,1,0:T(8,128)(2,1)S(1)}, bf16[3,2,2,144,128]{4,3,2,1,0:T(8,128)(2,1)S(1)}, u32[]{:S(2)}, u32[]{:S(2)}) %collective-permute-start.3) | collective-permute-done | bytes 442400 | tf_op jit(solution)/shard_map/ppermute | solution.py:130
  30.5 1.5 %collective-permute-start.4 = (bf16[3,2,2,144,128]{4,3,2,1,0:T(8,128)(2,1)S(1)}, bf16[3,2,2,144,128]{4,3,2,1,0:T(8,128)(2,1)S(1)}, u32[]{:S(2)}, u32[]{:S(2)}) collective-permute-start(bf16[3,2,2,144,128]{4,3,2,1,0:T(8,128)(2,1)S(1)} %collective-permute-done.2), channel_id=1, source_target_pairs={{0,2},{2,4},{4,6},{6,7},{7,5},{5,3},{3,1},{1,0},{8,10},{10,12},{12... | collective-permute-start | bytes 1327112 | tf_op jit(solution)/shard_map/ppermute | solution.py:129
  33.8 1.3 %collective-permute-start.17 = (bf16[3,4,144,128]{3,2,1,0:T(8,128)(2,1)S(1)}, bf16[3,4,144,128]{3,2,1,0:T(8,128)(2,1)S(1)}, u32[]{:S(2)}, u32[]{:S(2)}) collective-permute-start(bf16[3,4,144,128]{3,2,1,0:T(8,128)(2,1)S(1)} %pad_maximum_fusion.1), channel_id=1, source_target_pairs={{0,8},{1,9},{10,2},{11,3},{20,28},{21,29},{30,22},{31,23}} | collective-permute-start | bytes 1327112 | tf_op jit(solution)/shard_map/ppermute | solution.py:105
  35.1 2.8 %collective-permute-start.21 = (bf16[3,4,144,128]{3,2,1,0:T(8,128)(2,1)S(1)}, bf16[3,4,144,128]{3,2,1,0:T(8,128)(2,1)S(1)}, u32[]{:S(2)}, u32[]{:S(2)}) collective-permute-start(bf16[3,4,144,128]{3,2,1,0:T(8,128)(2,1)S(1)} %pad_maximum_fusion.2), channel_id=1, source_target_pairs={{0,16},{1,17},{10,26},{11,27},{20,4},{21,5},{30,14},{31,15}} | collective-permute-start | bytes 1327112 | tf_op jit(solution)/shard_map/ppermute | solution.py:105
  43.7 1.3 %collective-permute-start.20 = (bf16[3,4,144,128]{3,2,1,0:T(8,128)(2,1)S(1)}, bf16[3,4,144,128]{3,2,1,0:T(8,128)(2,1)S(1)}, u32[]{:S(2)}, u32[]{:S(2)}) collective-permute-start(bf16[3,4,144,128]{3,2,1,0:T(8,128)(2,1)S(1)} %pad_maximum_fusion.2), channel_id=1, source_target_pairs={{0,8},{1,9},{10,2},{11,3},{20,28},{21,29},{30,22},{31,23}} | collective-permute-start | bytes 1327112 | tf_op jit(solution)/shard_map/ppermute | solution.py:105
  45.0 3.1 %collective-permute-start.24 = (bf16[3,4,144,128]{3,2,1,0:T(8,128)(2,1)S(1)}, bf16[3,4,144,128]{3,2,1,0:T(8,128)(2,1)S(1)}, u32[]{:S(2)}, u32[]{:S(2)}) collective-permute-start(bf16[3,4,144,128]{3,2,1,0:T(8,128)(2,1)S(1)} %pad_maximum_fusion.3), channel_id=1, source_target_pairs={{0,16},{1,17},{10,26},{11,27},{20,4},{21,5},{30,14},{31,15}} | collective-permute-start | bytes 1327112 | tf_op jit(solution)/shard_map/ppermute | solution.py:105
  49.1 1.5 %collective-permute-done.7 = bf16[3,2,2,144,128]{4,3,2,1,0:T(8,128)(2,1)S(1)} collective-permute-done((bf16[3,2,2,144,128]{4,3,2,1,0:T(8,128)(2,1)S(1)}, bf16[3,2,2,144,128]{4,3,2,1,0:T(8,128)(2,1)S(1)}, u32[]{:S(2)}, u32[]{:S(2)}) %collective-permute-start.7) | collective-permute-done | bytes 442400 | tf_op jit(solution)/shard_map/ppermute | solution.py:130
  50.8 1.9 %collective-permute-start.8 = (bf16[3,2,2,144,128]{4,3,2,1,0:T(8,128)(2,1)S(1)}, bf16[3,2,2,144,128]{4,3,2,1,0:T(8,128)(2,1)S(1)}, u32[]{:S(2)}, u32[]{:S(2)}) collective-permute-start(bf16[3,2,2,144,128]{4,3,2,1,0:T(8,128)(2,1)S(1)} %collective-permute-done.6), channel_id=1, source_target_pairs={{0,2},{2,4},{4,6},{6,7},{7,5},{5,3},{3,1},{1,0},{8,10},{10,12},{12... | collective-permute-start | bytes 1327112 | tf_op jit(solution)/shard_map/ppermute | solution.py:129
  54.5 1.3 %collective-permute-start.23 = (bf16[3,4,144,128]{3,2,1,0:T(8,128)(2,1)S(1)}, bf16[3,4,144,128]{3,2,1,0:T(8,128)(2,1)S(1)}, u32[]{:S(2)}, u32[]{:S(2)}) collective-permute-start(bf16[3,4,144,128]{3,2,1,0:T(8,128)(2,1)S(1)} %pad_maximum_fusion.3), channel_id=1, source_target_pairs={{0,8},{1,9},{10,2},{11,3},{20,28},{21,29},{30,22},{31,23}} | collective-permute-start | bytes 1327112 | tf_op jit(solution)/shard_map/ppermute | solution.py:105
  55.8 3.2 %collective-permute-start.27 = (bf16[3,4,144,128]{3,2,1,0:T(8,128)(2,1)S(1)}, bf16[3,4,144,128]{3,2,1,0:T(8,128)(2,1)S(1)}, u32[]{:S(2)}, u32[]{:S(2)}) collective-permute-start(bf16[3,4,144,128]{3,2,1,0:T(8,128)(2,1)S(1)} %pad_maximum_fusion.4), channel_id=1, source_target_pairs={{0,16},{1,17},{10,26},{11,27},{20,4},{21,5},{30,14},{31,15}} | collective-permute-start | bytes 1327112 | tf_op jit(solution)/shard_map/ppermute | solution.py:105
  61.1 1.4 %collective-permute-start.10 = (bf16[3,2,2,144,128]{4,3,2,1,0:T(8,128)(2,1)S(1)}, bf16[3,2,2,144,128]{4,3,2,1,0:T(8,128)(2,1)S(1)}, u32[]{:S(2)}, u32[]{:S(2)}) collective-permute-start(bf16[3,2,2,144,128]{4,3,2,1,0:T(8,128)(2,1)S(1)} %collective-permute-done.8), channel_id=1, source_target_pairs={{0,2},{2,4},{4,6},{6,7},{7,5},{5,3},{3,1},{1,0},{8,10},{10,12},{12... | collective-permute-start | bytes 1327112 | tf_op jit(solution)/shard_map/ppermute | solution.py:129
  66.2 4.1 %collective-permute-start.30 = (bf16[3,4,144,128]{3,2,1,0:T(8,128)(2,1)}, bf16[3,4,144,128]{3,2,1,0:T(8,128)(2,1)}, u32[]{:S(2)}, u32[]{:S(2)}) collective-permute-start(bf16[3,4,144,128]{3,2,1,0:T(8,128)(2,1)} %pad_maximum_fusion.5), channel_id=1, source_target_pairs={{0,16},{1,17},{10,26},{11,27},{20,4},{21,5},{30,14},{31,15}} | collective-permute-start | bytes 1327112 | tf_op jit(solution)/shard_map/ppermute | solution.py:105
  75.2 2.1 %collective-permute-start.29 = (bf16[3,4,144,128]{3,2,1,0:T(8,128)(2,1)}, bf16[3,4,144,128]{3,2,1,0:T(8,128)(2,1)}, u32[]{:S(2)}, u32[]{:S(2)}) collective-permute-start(bf16[3,4,144,128]{3,2,1,0:T(8,128)(2,1)} %pad_maximum_fusion.5), channel_id=1, source_target_pairs={{0,8},{1,9},{10,2},{11,3},{20,28},{21,29},{30,22},{31,23}} | collective-permute-start | bytes 1327112 | tf_op jit(solution)/shard_map/ppermute | solution.py:105
  77.2 3.4 %collective-permute-start.33 = (bf16[3,4,144,128]{3,2,1,0:T(8,128)(2,1)}, bf16[3,4,144,128]{3,2,1,0:T(8,128)(2,1)}, u32[]{:S(2)}, u32[]{:S(2)}) collective-permute-start(bf16[3,4,144,128]{3,2,1,0:T(8,128)(2,1)} %pad_maximum_fusion.6), channel_id=1, source_target_pairs={{0,16},{1,17},{10,26},{11,27},{20,4},{21,5},{30,14},{31,15}} | collective-permute-start | bytes 1327112 | tf_op jit(solution)/shard_map/ppermute | solution.py:105
  80.9 2.1 %collective-permute-start.32 = (bf16[3,4,144,128]{3,2,1,0:T(8,128)(2,1)}, bf16[3,4,144,128]{3,2,1,0:T(8,128)(2,1)}, u32[]{:S(2)}, u32[]{:S(2)}) collective-permute-start(bf16[3,4,144,128]{3,2,1,0:T(8,128)(2,1)} %pad_maximum_fusion.6), channel_id=1, source_target_pairs={{0,8},{1,9},{10,2},{11,3},{20,28},{21,29},{30,22},{31,23}} | collective-permute-start | bytes 1327112 | tf_op jit(solution)/shard_map/ppermute | solution.py:105
  83.0 1.7 %collective-permute-done.13 = bf16[3,2,2,144,128]{4,3,2,1,0:T(8,128)(2,1)S(1)} collective-permute-done((bf16[3,2,2,144,128]{4,3,2,1,0:T(8,128)(2,1)S(1)}, bf16[3,2,2,144,128]{4,3,2,1,0:T(8,128)(2,1)S(1)}, u32[]{:S(2)}, u32[]{:S(2)}) %collective-permute-start.13) | collective-permute-done | bytes 442400 | tf_op jit(solution)/shard_map/ppermute | solution.py:130
  84.7 1.4 %collective-permute-start.31 = (bf16[3,4,144,128]{3,2,1,0:T(8,128)(2,1)}, bf16[3,4,144,128]{3,2,1,0:T(8,128)(2,1)}, u32[]{:S(2)}, u32[]{:S(2)}) collective-permute-start(bf16[3,4,144,128]{3,2,1,0:T(8,128)(2,1)} %collective-permute-done.30), channel_id=1, source_target_pairs={{16,24},{17,25},{26,18},{27,19},{4,12},{5,13},{14,6},{15,7}} | collective-permute-start | bytes 1327112 | tf_op jit(solution)/shard_map/ppermute | solution.py:105
  87.7 4.7 %collective-permute-start.36 = (bf16[3,4,144,128]{3,2,1,0:T(8,128)(2,1)}, bf16[3,4,144,128]{3,2,1,0:T(8,128)(2,1)}, u32[]{:S(2)}, u32[]{:S(2)}) collective-permute-start(bf16[3,4,144,128]{3,2,1,0:T(8,128)(2,1)} %pad_maximum_fusion.7), channel_id=1, source_target_pairs={{0,16},{1,17},{10,26},{11,27},{20,4},{21,5},{30,14},{31,15}} | collective-permute-start | bytes 1327112 | tf_op jit(solution)/shard_map/ppermute | solution.py:105
  94.1 1.4 %collective-permute-start.34 = (bf16[3,4,144,128]{3,2,1,0:T(8,128)(2,1)}, bf16[3,4,144,128]{3,2,1,0:T(8,128)(2,1)}, u32[]{:S(2)}, u32[]{:S(2)}) collective-permute-start(bf16[3,4,144,128]{3,2,1,0:T(8,128)(2,1)} %collective-permute-done.33), channel_id=1, source_target_pairs={{16,24},{17,25},{26,18},{27,19},{4,12},{5,13},{14,6},{15,7}} | collective-permute-start | bytes 1327112 | tf_op jit(solution)/shard_map/ppermute | solution.py:105
  97.2 1.7 %slice.19 = bf16[96,2,1,1]{3,2,1,0:T(2,128)(2,1)} slice(bf16[96,2,144,128]{3,2,1,0:T(8,128)(2,1)} %bitcast.44), slice={[0:96], [0:2], [131:132], [0:1]} | slice | bytes 768 | tf_op jit(solution)/shard_map/slice | solution.py:150
  100.0 1.3 %collective-permute-start.35 = (bf16[3,4,144,128]{3,2,1,0:T(8,128)(2,1)}, bf16[3,4,144,128]{3,2,1,0:T(8,128)(2,1)S(1)}, u32[]{:S(2)}, u32[]{:S(2)}) collective-permute-start(bf16[3,4,144,128]{3,2,1,0:T(8,128)(2,1)} %pad_maximum_fusion.7), channel_id=1, source_target_pairs={{0,8},{1,9},{10,2},{11,3},{20,28},{21,29},{30,22},{31,23}} | collective-permute-start | bytes 1327112 | tf_op jit(solution)/shard_map/ppermute | solution.py:105
  102.0 1.5 %select_dynamic-update-slice_fusion.2 = bf16[3,32,144,128]{3,2,1,0:T(8,128)(2,1)S(1)} fusion(bf16[3,32,144,128]{3,2,1,0:T(8,128)(2,1)S(1)} %select_dynamic-update-slice_fusion.3, bf16[3,4,144,128]{3,2,1,0:T(8,128)(2,1)} %collective-permute-done.29, bf16[3,4,144,128]{3,2,1,0:T(8,128)(2,1)} %collective-permute-done.30, ...), kind=kLoop, calls=%fused_computation.11 | loop fusion | flops 1548288 | bytes 2211843
  103.5 1.5 %select_dynamic-update-slice_fusion.1 = bf16[3,32,144,128]{3,2,1,0:T(8,128)(2,1)S(1)} fusion(bf16[3,32,144,128]{3,2,1,0:T(8,128)(2,1)S(1)} %select_dynamic-update-slice_fusion.2, bf16[3,4,144,128]{3,2,1,0:T(8,128)(2,1)} %collective-permute-done.32, bf16[3,4,144,128]{3,2,1,0:T(8,128)(2,1)} %collective-permute-done.33, ...), kind=kLoop, calls=%fused_computation.10 | loop fusion | flops 1548288 | bytes 2211843
  105.0 1.3 %select_dynamic-update-slice_fusion = bf16[3,32,144,128]{3,2,1,0:T(8,128)(2,1)S(1)} fusion(bf16[3,32,144,128]{3,2,1,0:T(8,128)(2,1)S(1)} %select_dynamic-update-slice_fusion.1, bf16[3,4,144,128]{3,2,1,0:T(8,128)(2,1)S(1)} %collective-permute-done.35, bf16[3,4,144,128]{3,2,1,0:T(8,128)(2,1)} %collective-permute-done.36, ...), kind=kLoop, calls=%fused_computation.9 | loop fusion | flops 1548288 | bytes 2211843 | tf_op jit(solution)/shard_map/concatenate | solution.py:145
  108.8 10.4 %shard_map.37 = f32[2048,1024]{1,0:T(8,128)} custom-call(s32[288]{0:T(512)S(1)} %min.12.offs_ref, bf16[96,2,144,128]{3,2,1,0:T(8,128)(2,1)} %bitcast.45, bf16[96,144,128]{2,1,0:T(8,128)(2,1)S(1)} %bitcast.43), custom_call_target="tpu_custom_call" | custom-call | flops 805306368 | bytes 17825792 | tf_op jit(solution)/shard_map/pallas_call | solution.py:40
  (131 shorter events, 36.2 us)
Async XLA Ops:
  4.2 13.2 %collective-permute-start = (bf16[3,2,2,144,128]{4,3,2,1,0:T(8,128)(2,1)S(1)}, bf16[3,2,2,144,128]{4,3,2,1,0:T(8,128)(2,1)S(1)}, u32[]{:S(2)}, u32[]{:S(2)}) collective-permute-start(bf16[3,2,2,144,128]{4,3,2,1,0:T(8,128)(2,1)S(1)} %get-tuple-element.5), channel_id=1, source_target_pairs={{0,2},{2,4},{4,6},{6,7},{7,5},{5,3},{3,1},{1,0},{8,10},{10,12},{12... | collective-permute-start | bytes 1327112 | tf_op jit(solution)/shard_map/ppermute | solution.py:129
  7.3 11.9 %collective-permute-start.1 = (bf16[3,2,2,144,128]{4,3,2,1,0:T(8,128)(2,1)S(1)}, bf16[3,2,2,144,128]{4,3,2,1,0:T(8,128)(2,1)S(1)}, u32[]{:S(2)}, u32[]{:S(2)}) collective-permute-start(bf16[3,2,2,144,128]{4,3,2,1,0:T(8,128)(2,1)S(1)} %get-tuple-element.6), channel_id=1, source_target_pairs={{2,0},{4,2},{6,4},{7,6},{5,7},{3,5},{1,3},{0,1},{10,8},{12,10},{14... | collective-permute-start | bytes 1327112 | tf_op jit(solution)/shard_map/ppermute | solution.py:130
  8.1 15.1 %collective-permute-start.15 = (bf16[3,4,144,128]{3,2,1,0:T(8,128)(2,1)S(1)}, bf16[3,4,144,128]{3,2,1,0:T(8,128)(2,1)S(1)}, u32[]{:S(2)}, u32[]{:S(2)}) collective-permute-start(bf16[3,4,144,128]{3,2,1,0:T(8,128)(2,1)S(1)} %pad_maximum_fusion), channel_id=1, source_target_pairs={{0,16},{1,17},{10,26},{11,27},{20,4},{21,5},{30,14},{31,15}} | collective-permute-start | bytes 1327112 | tf_op jit(solution)/shard_map/ppermute | solution.py:105
  12.0 21.9 %collective-permute-start.14 = (bf16[3,4,144,128]{3,2,1,0:T(8,128)(2,1)S(1)}, bf16[3,4,144,128]{3,2,1,0:T(8,128)(2,1)S(1)}, u32[]{:S(2)}, u32[]{:S(2)}) collective-permute-start(bf16[3,4,144,128]{3,2,1,0:T(8,128)(2,1)S(1)} %pad_maximum_fusion), channel_id=1, source_target_pairs={{0,8},{1,9},{10,2},{11,3},{20,28},{21,29},{30,22},{31,23}} | collective-permute-start | bytes 1327112 | tf_op jit(solution)/shard_map/ppermute | solution.py:105
  17.4 13.1 %collective-permute-start.2 = (bf16[3,2,2,144,128]{4,3,2,1,0:T(8,128)(2,1)S(1)}, bf16[3,2,2,144,128]{4,3,2,1,0:T(8,128)(2,1)S(1)}, u32[]{:S(2)}, u32[]{:S(2)}) collective-permute-start(bf16[3,2,2,144,128]{4,3,2,1,0:T(8,128)(2,1)S(1)} %collective-permute-done), channel_id=1, source_target_pairs={{0,2},{2,4},{4,6},{6,7},{7,5},{5,3},{3,1},{1,0},{8,10},{10,12},{12... | collective-permute-start | bytes 1327112 | tf_op jit(solution)/shard_map/ppermute | solution.py:129
  19.2 10.8 %collective-permute-start.3 = (bf16[3,2,2,144,128]{4,3,2,1,0:T(8,128)(2,1)S(1)}, bf16[3,2,2,144,128]{4,3,2,1,0:T(8,128)(2,1)S(1)}, u32[]{:S(2)}, u32[]{:S(2)}) collective-permute-start(bf16[3,2,2,144,128]{4,3,2,1,0:T(8,128)(2,1)S(1)} %collective-permute-done.1), channel_id=1, source_target_pairs={{2,0},{4,2},{6,4},{7,6},{5,7},{3,5},{1,3},{0,1},{10,8},{12,10},{14... | collective-permute-start | bytes 1327112 | tf_op jit(solution)/shard_map/ppermute | solution.py:130
  19.5 15.6 %collective-permute-start.18 = (bf16[3,4,144,128]{3,2,1,0:T(8,128)(2,1)S(1)}, bf16[3,4,144,128]{3,2,1,0:T(8,128)(2,1)S(1)}, u32[]{:S(2)}, u32[]{:S(2)}) collective-permute-start(bf16[3,4,144,128]{3,2,1,0:T(8,128)(2,1)S(1)} %pad_maximum_fusion.1), channel_id=1, source_target_pairs={{0,16},{1,17},{10,26},{11,27},{20,4},{21,5},{30,14},{31,15}} | collective-permute-start | bytes 1327112 | tf_op jit(solution)/shard_map/ppermute | solution.py:105
  23.2 14.8 %collective-permute-start.16 = (bf16[3,4,144,128]{3,2,1,0:T(8,128)(2,1)S(1)}, bf16[3,4,144,128]{3,2,1,0:T(8,128)(2,1)S(1)}, u32[]{:S(2)}, u32[]{:S(2)}) collective-permute-start(bf16[3,4,144,128]{3,2,1,0:T(8,128)(2,1)S(1)} %collective-permute-done.15), channel_id=1, source_target_pairs={{16,24},{17,25},{26,18},{27,19},{4,12},{5,13},{14,6},{15,7}} | collective-permute-start | bytes 1327112 | tf_op jit(solution)/shard_map/ppermute | solution.py:105
  29.9 9.8 %collective-permute-start.5 = (bf16[3,2,2,144,128]{4,3,2,1,0:T(8,128)(2,1)S(1)}, bf16[3,2,2,144,128]{4,3,2,1,0:T(8,128)(2,1)S(1)}, u32[]{:S(2)}, u32[]{:S(2)}) collective-permute-start(bf16[3,2,2,144,128]{4,3,2,1,0:T(8,128)(2,1)S(1)} %collective-permute-done.3), channel_id=1, source_target_pairs={{2,0},{4,2},{6,4},{7,6},{5,7},{3,5},{1,3},{0,1},{10,8},{12,10},{14... | collective-permute-start | bytes 1327112 | tf_op jit(solution)/shard_map/ppermute | solution.py:130
  30.5 10.3 %collective-permute-start.4 = (bf16[3,2,2,144,128]{4,3,2,1,0:T(8,128)(2,1)S(1)}, bf16[3,2,2,144,128]{4,3,2,1,0:T(8,128)(2,1)S(1)}, u32[]{:S(2)}, u32[]{:S(2)}) collective-permute-start(bf16[3,2,2,144,128]{4,3,2,1,0:T(8,128)(2,1)S(1)} %collective-permute-done.2), channel_id=1, source_target_pairs={{0,2},{2,4},{4,6},{6,7},{7,5},{5,3},{3,1},{1,0},{8,10},{10,12},{12... | collective-permute-start | bytes 1327112 | tf_op jit(solution)/shard_map/ppermute | solution.py:129
  33.8 9.9 %collective-permute-start.17 = (bf16[3,4,144,128]{3,2,1,0:T(8,128)(2,1)S(1)}, bf16[3,4,144,128]{3,2,1,0:T(8,128)(2,1)S(1)}, u32[]{:S(2)}, u32[]{:S(2)}) collective-permute-start(bf16[3,4,144,128]{3,2,1,0:T(8,128)(2,1)S(1)} %pad_maximum_fusion.1), channel_id=1, source_target_pairs={{0,8},{1,9},{10,2},{11,3},{20,28},{21,29},{30,22},{31,23}} | collective-permute-start | bytes 1327112 | tf_op jit(solution)/shard_map/ppermute | solution.py:105
  35.1 9.9 %collective-permute-start.21 = (bf16[3,4,144,128]{3,2,1,0:T(8,128)(2,1)S(1)}, bf16[3,4,144,128]{3,2,1,0:T(8,128)(2,1)S(1)}, u32[]{:S(2)}, u32[]{:S(2)}) collective-permute-start(bf16[3,4,144,128]{3,2,1,0:T(8,128)(2,1)S(1)} %pad_maximum_fusion.2), channel_id=1, source_target_pairs={{0,16},{1,17},{10,26},{11,27},{20,4},{21,5},{30,14},{31,15}} | collective-permute-start | bytes 1327112 | tf_op jit(solution)/shard_map/ppermute | solution.py:105
  38.0 10.2 %collective-permute-start.19 = (bf16[3,4,144,128]{3,2,1,0:T(8,128)(2,1)S(1)}, bf16[3,4,144,128]{3,2,1,0:T(8,128)(2,1)S(1)}, u32[]{:S(2)}, u32[]{:S(2)}) collective-permute-start(bf16[3,4,144,128]{3,2,1,0:T(8,128)(2,1)S(1)} %collective-permute-done.18), channel_id=1, source_target_pairs={{16,24},{17,25},{26,18},{27,19},{4,12},{5,13},{14,6},{15,7}} | collective-permute-start | bytes 1327112 | tf_op jit(solution)/shard_map/ppermute | solution.py:105
  39.8 10.8 %collective-permute-start.7 = (bf16[3,2,2,144,128]{4,3,2,1,0:T(8,128)(2,1)S(1)}, bf16[3,2,2,144,128]{4,3,2,1,0:T(8,128)(2,1)S(1)}, u32[]{:S(2)}, u32[]{:S(2)}) collective-permute-start(bf16[3,2,2,144,128]{4,3,2,1,0:T(8,128)(2,1)S(1)} %collective-permute-done.5), channel_id=1, source_target_pairs={{2,0},{4,2},{6,4},{7,6},{5,7},{3,5},{1,3},{0,1},{10,8},{12,10},{14... | collective-permute-start | bytes 1327112 | tf_op jit(solution)/shard_map/ppermute | solution.py:130
  40.8 9.9 %collective-permute-start.6 = (bf16[3,2,2,144,128]{4,3,2,1,0:T(8,128)(2,1)S(1)}, bf16[3,2,2,144,128]{4,3,2,1,0:T(8,128)(2,1)S(1)}, u32[]{:S(2)}, u32[]{:S(2)}) collective-permute-start(bf16[3,2,2,144,128]{4,3,2,1,0:T(8,128)(2,1)S(1)} %collective-permute-done.4), channel_id=1, source_target_pairs={{0,2},{2,4},{4,6},{6,7},{7,5},{5,3},{3,1},{1,0},{8,10},{10,12},{12... | collective-permute-start | bytes 1327112 | tf_op jit(solution)/shard_map/ppermute | solution.py:129
  43.7 10.8 %collective-permute-start.20 = (bf16[3,4,144,128]{3,2,1,0:T(8,128)(2,1)S(1)}, bf16[3,4,144,128]{3,2,1,0:T(8,128)(2,1)S(1)}, u32[]{:S(2)}, u32[]{:S(2)}) collective-permute-start(bf16[3,4,144,128]{3,2,1,0:T(8,128)(2,1)S(1)} %pad_maximum_fusion.2), channel_id=1, source_target_pairs={{0,8},{1,9},{10,2},{11,3},{20,28},{21,29},{30,22},{31,23}} | collective-permute-start | bytes 1327112 | tf_op jit(solution)/shard_map/ppermute | solution.py:105
  45.0 14.0 %collective-permute-start.24 = (bf16[3,4,144,128]{3,2,1,0:T(8,128)(2,1)S(1)}, bf16[3,4,144,128]{3,2,1,0:T(8,128)(2,1)S(1)}, u32[]{:S(2)}, u32[]{:S(2)}) collective-permute-start(bf16[3,4,144,128]{3,2,1,0:T(8,128)(2,1)S(1)} %pad_maximum_fusion.3), channel_id=1, source_target_pairs={{0,16},{1,17},{10,26},{11,27},{20,4},{21,5},{30,14},{31,15}} | collective-permute-start | bytes 1327112 | tf_op jit(solution)/shard_map/ppermute | solution.py:105
  50.6 11.9 %collective-permute-start.9 = (bf16[3,2,2,144,128]{4,3,2,1,0:T(8,128)(2,1)S(1)}, bf16[3,2,2,144,128]{4,3,2,1,0:T(8,128)(2,1)S(1)}, u32[]{:S(2)}, u32[]{:S(2)}) collective-permute-start(bf16[3,2,2,144,128]{4,3,2,1,0:T(8,128)(2,1)S(1)} %collective-permute-done.7), channel_id=1, source_target_pairs={{2,0},{4,2},{6,4},{7,6},{5,7},{3,5},{1,3},{0,1},{10,8},{12,10},{14... | collective-permute-start | bytes 1327112 | tf_op jit(solution)/shard_map/ppermute | solution.py:130
  50.8 10.3 %collective-permute-start.8 = (bf16[3,2,2,144,128]{4,3,2,1,0:T(8,128)(2,1)S(1)}, bf16[3,2,2,144,128]{4,3,2,1,0:T(8,128)(2,1)S(1)}, u32[]{:S(2)}, u32[]{:S(2)}) collective-permute-start(bf16[3,2,2,144,128]{4,3,2,1,0:T(8,128)(2,1)S(1)} %collective-permute-done.6), channel_id=1, source_target_pairs={{0,2},{2,4},{4,6},{6,7},{7,5},{5,3},{3,1},{1,0},{8,10},{10,12},{12... | collective-permute-start | bytes 1327112 | tf_op jit(solution)/shard_map/ppermute | solution.py:129
  54.5 10.5 %collective-permute-start.23 = (bf16[3,4,144,128]{3,2,1,0:T(8,128)(2,1)S(1)}, bf16[3,4,144,128]{3,2,1,0:T(8,128)(2,1)S(1)}, u32[]{:S(2)}, u32[]{:S(2)}) collective-permute-start(bf16[3,4,144,128]{3,2,1,0:T(8,128)(2,1)S(1)} %pad_maximum_fusion.3), channel_id=1, source_target_pairs={{0,8},{1,9},{10,2},{11,3},{20,28},{21,29},{30,22},{31,23}} | collective-permute-start | bytes 1327112 | tf_op jit(solution)/shard_map/ppermute | solution.py:105
  55.8 14.5 %collective-permute-start.27 = (bf16[3,4,144,128]{3,2,1,0:T(8,128)(2,1)S(1)}, bf16[3,4,144,128]{3,2,1,0:T(8,128)(2,1)S(1)}, u32[]{:S(2)}, u32[]{:S(2)}) collective-permute-start(bf16[3,4,144,128]{3,2,1,0:T(8,128)(2,1)S(1)} %pad_maximum_fusion.4), channel_id=1, source_target_pairs={{0,16},{1,17},{10,26},{11,27},{20,4},{21,5},{30,14},{31,15}} | collective-permute-start | bytes 1327112 | tf_op jit(solution)/shard_map/ppermute | solution.py:105
  61.1 11.0 %collective-permute-start.10 = (bf16[3,2,2,144,128]{4,3,2,1,0:T(8,128)(2,1)S(1)}, bf16[3,2,2,144,128]{4,3,2,1,0:T(8,128)(2,1)S(1)}, u32[]{:S(2)}, u32[]{:S(2)}) collective-permute-start(bf16[3,2,2,144,128]{4,3,2,1,0:T(8,128)(2,1)S(1)} %collective-permute-done.8), channel_id=1, source_target_pairs={{0,2},{2,4},{4,6},{6,7},{7,5},{5,3},{3,1},{1,0},{8,10},{10,12},{12... | collective-permute-start | bytes 1327112 | tf_op jit(solution)/shard_map/ppermute | solution.py:129
  62.5 10.6 %collective-permute-start.11 = (bf16[3,2,2,144,128]{4,3,2,1,0:T(8,128)(2,1)S(1)}, bf16[3,2,2,144,128]{4,3,2,1,0:T(8,128)(2,1)S(1)}, u32[]{:S(2)}, u32[]{:S(2)}) collective-permute-start(bf16[3,2,2,144,128]{4,3,2,1,0:T(8,128)(2,1)S(1)} %collective-permute-done.9), channel_id=1, source_target_pairs={{2,0},{4,2},{6,4},{7,6},{5,7},{3,5},{1,3},{0,1},{10,8},{12,10},{14... | collective-permute-start | bytes 1327112 | tf_op jit(solution)/shard_map/ppermute | solution.py:130
  64.9 10.2 %collective-permute-start.26 = (bf16[3,4,144,128]{3,2,1,0:T(8,128)(2,1)S(1)}, bf16[3,4,144,128]{3,2,1,0:T(8,128)(2,1)S(1)}, u32[]{:S(2)}, u32[]{:S(2)}) collective-permute-start(bf16[3,4,144,128]{3,2,1,0:T(8,128)(2,1)S(1)} %pad_maximum_fusion.4), channel_id=1, source_target_pairs={{0,8},{1,9},{10,2},{11,3},{20,28},{21,29},{30,22},{31,23}} | collective-permute-start | bytes 1327112 | tf_op jit(solution)/shard_map/ppermute | solution.py:105
  66.2 14.7 %collective-permute-start.30 = (bf16[3,4,144,128]{3,2,1,0:T(8,128)(2,1)}, bf16[3,4,144,128]{3,2,1,0:T(8,128)(2,1)}, u32[]{:S(2)}, u32[]{:S(2)}) collective-permute-start(bf16[3,4,144,128]{3,2,1,0:T(8,128)(2,1)} %pad_maximum_fusion.5), channel_id=1, source_target_pairs={{0,16},{1,17},{10,26},{11,27},{20,4},{21,5},{30,14},{31,15}} | collective-permute-start | bytes 1327112 | tf_op jit(solution)/shard_map/ppermute | solution.py:105
  72.2 14.1 %collective-permute-start.12 = (bf16[3,2,2,144,128]{4,3,2,1,0:T(8,128)(2,1)S(1)}, bf16[3,2,2,144,128]{4,3,2,1,0:T(8,128)(2,1)S(1)}, u32[]{:S(2)}, u32[]{:S(2)}) collective-permute-start(bf16[3,2,2,144,128]{4,3,2,1,0:T(8,128)(2,1)S(1)} %collective-permute-done.10), channel_id=1, source_target_pairs={{0,2},{2,4},{4,6},{6,7},{7,5},{5,3},{3,1},{1,0},{8,10},{10,12},{12... | collective-permute-start | bytes 1327112 | tf_op jit(solution)/shard_map/ppermute | solution.py:129
  73.1 11.6 %collective-permute-start.13 = (bf16[3,2,2,144,128]{4,3,2,1,0:T(8,128)(2,1)S(1)}, bf16[3,2,2,144,128]{4,3,2,1,0:T(8,128)(2,1)S(1)}, u32[]{:S(2)}, u32[]{:S(2)}) collective-permute-start(bf16[3,2,2,144,128]{4,3,2,1,0:T(8,128)(2,1)S(1)} %collective-permute-done.11), channel_id=1, source_target_pairs={{2,0},{4,2},{6,4},{7,6},{5,7},{3,5},{1,3},{0,1},{10,8},{12,10},{14... | collective-permute-start | bytes 1327112 | tf_op jit(solution)/shard_map/ppermute | solution.py:130
  75.2 24.8 %collective-permute-start.29 = (bf16[3,4,144,128]{3,2,1,0:T(8,128)(2,1)}, bf16[3,4,144,128]{3,2,1,0:T(8,128)(2,1)}, u32[]{:S(2)}, u32[]{:S(2)}) collective-permute-start(bf16[3,4,144,128]{3,2,1,0:T(8,128)(2,1)} %pad_maximum_fusion.5), channel_id=1, source_target_pairs={{0,8},{1,9},{10,2},{11,3},{20,28},{21,29},{30,22},{31,23}} | collective-permute-start | bytes 1327112 | tf_op jit(solution)/shard_map/ppermute | solution.py:105
  77.2 16.8 %collective-permute-start.33 = (bf16[3,4,144,128]{3,2,1,0:T(8,128)(2,1)}, bf16[3,4,144,128]{3,2,1,0:T(8,128)(2,1)}, u32[]{:S(2)}, u32[]{:S(2)}) collective-permute-start(bf16[3,4,144,128]{3,2,1,0:T(8,128)(2,1)} %pad_maximum_fusion.6), channel_id=1, source_target_pairs={{0,16},{1,17},{10,26},{11,27},{20,4},{21,5},{30,14},{31,15}} | collective-permute-start | bytes 1327112 | tf_op jit(solution)/shard_map/ppermute | solution.py:105
  80.9 22.5 %collective-permute-start.32 = (bf16[3,4,144,128]{3,2,1,0:T(8,128)(2,1)}, bf16[3,4,144,128]{3,2,1,0:T(8,128)(2,1)}, u32[]{:S(2)}, u32[]{:S(2)}) collective-permute-start(bf16[3,4,144,128]{3,2,1,0:T(8,128)(2,1)} %pad_maximum_fusion.6), channel_id=1, source_target_pairs={{0,8},{1,9},{10,2},{11,3},{20,28},{21,29},{30,22},{31,23}} | collective-permute-start | bytes 1327112 | tf_op jit(solution)/shard_map/ppermute | solution.py:105
  84.7 17.2 %collective-permute-start.31 = (bf16[3,4,144,128]{3,2,1,0:T(8,128)(2,1)}, bf16[3,4,144,128]{3,2,1,0:T(8,128)(2,1)}, u32[]{:S(2)}, u32[]{:S(2)}) collective-permute-start(bf16[3,4,144,128]{3,2,1,0:T(8,128)(2,1)} %collective-permute-done.30), channel_id=1, source_target_pairs={{16,24},{17,25},{26,18},{27,19},{4,12},{5,13},{14,6},{15,7}} | collective-permute-start | bytes 1327112 | tf_op jit(solution)/shard_map/ppermute | solution.py:105
  87.7 13.6 %collective-permute-start.36 = (bf16[3,4,144,128]{3,2,1,0:T(8,128)(2,1)}, bf16[3,4,144,128]{3,2,1,0:T(8,128)(2,1)}, u32[]{:S(2)}, u32[]{:S(2)}) collective-permute-start(bf16[3,4,144,128]{3,2,1,0:T(8,128)(2,1)} %pad_maximum_fusion.7), channel_id=1, source_target_pairs={{0,16},{1,17},{10,26},{11,27},{20,4},{21,5},{30,14},{31,15}} | collective-permute-start | bytes 1327112 | tf_op jit(solution)/shard_map/ppermute | solution.py:105
  (18 other events, 132.7 us)

commit v27 on v26

--- a/solution.py
+++ b/solution.py
@@ -104,18 +104,20 @@
     def send(v, pairs):
         return lax.ppermute(v, ("row", "col"), [(a * ncol + cc, b * ncol + cc) for a, b, cc in pairs])
 
-    def last_fan(own):
+    def last_fan(own, flip):
         heads = [cc // local_slots for cc in range(ncol)]
-        to_partner = send(own, [(h, h ^ 1, cc) for cc, h in enumerate(heads)])
+        land = lambda h, j: ((h + 2 * j) % nrow) ^ flip
         to_d1 = None
         for j in range(1, nx):
-            v = send(own, [(h, (h + 2 * j) % nrow, cc) for cc, h in enumerate(heads)])
-            to_d1 = v if to_d1 is None else jnp.where(which // 2 == j, v, to_d1)
+            v = send(own, [(h, land(h, j), cc) for cc, h in enumerate(heads)])
+            to_d1 = v if to_d1 is None else jnp.where((r // 2 - src // 2 + nx) % nx == j, v, to_d1)
+        to_partner = send(own, [(h, h ^ 1, cc) for cc, h in enumerate(heads)])
         to_d2 = send(
             to_d1,
-            [((h + 2 * j) % nrow, ((h + 2 * j) % nrow) ^ 1, cc) for cc, h in enumerate(heads) for j in range(1, nx)],
+            [(land(h, j), land(h, j) ^ 1, cc) for cc, h in enumerate(heads) for j in range(1, nx)],
         )
-        return jnp.where(is_s, own, jnp.where(is_p, to_partner, jnp.where(is_d1, to_d1, to_d2)))
+        landed = is_d1 if flip == 0 else (which % 2 == 1) & jnp.logical_not(is_p)
+        return jnp.where(is_s, own, jnp.where(is_p, to_partner, jnp.where(landed, to_d1, to_d2)))
 
     def pick_slot(piece):
         return lax.dynamic_index_in_dim(piece, slot, axis=2, keepdims=False)
@@ -138,7 +140,7 @@
                 for j, fan in enumerate(fans, start=1):
                     got = jnp.where(which == j, lax.ppermute(own, ("row", "col"), fan), got)
             else:
-                got = last_fan(own)
+                got = last_fan(own, step % 2)
             columns.append(got)
 
     blocks = jnp.concatenate(pieces, axis=1)

time: 120 us -> 120 us (level)
  waiting for transfers between devices: 13.7 us -> 20 us
  starting transfers between devices: 63 us -> 57.2 us
    ppermute x24, starting transfers between devices: 47.8 us -> 41.9 us  [send(): lax.ppermute(v, ('row', 'col'), [(a * ncol + cc, b * ncol + cc) for a, b,...]
    ppermute x7, waiting for transfers between devices: 8.34 us -> 13.5 us  [local(): b = lax.ppermute(b, 'col', backward)]
    ppermute x7, starting transfers between devices: 11.6 us -> 13.4 us  [local(): a = lax.ppermute(a, 'col', forward)]
    ppermute x7, starting transfers between devices: 3.59 us -> 1.9 us  [local(): b = lax.ppermute(b, 'col', backward)]
  transfers between devices with their start and end apart: 38 -> 38, of which waited for: 7 -> 8; matrix products, arithmetic and copies ran while one was open for 18% -> 18% of each run, Pallas kernels for 0% -> 0%
where the time goes in v27:
time: 120 us
  starting transfers between devices  57.2 us (48%)
  waiting for transfers between devices  20 us (17%)
  local copies, waits for them, and re-layouts  19.2 us (16%)
  other arithmetic  12.2 us (10%)
  Pallas kernels  10.4 us (9%)
    ppermute x24, starting transfers between devices, send(): lax.ppermute(v, ('row', 'col'), [(a * ncol + cc, b * ncol + cc) for a, b,...  41.9 us
    ppermute x7, waiting for transfers between devices, local(): b = lax.ppermute(b, 'col', backward)  13.5 us
    ppermute x7, starting transfers between devices, local(): a = lax.ppermute(a, 'col', forward)  13.4 us
    unnamed x37, local copies, waits for them, and re-layouts  12.5 us
    pallas_call x1, Pallas kernels, gram_call(): pl.pallas_call(kernel, grid_spec=pltpu.PrefetchScalarGridSpec(num_scalar_...  10.4 us
    unnamed x8, other arithmetic  6.64 us
    ppermute x7, waiting for transfers between devices, local(): a = lax.ppermute(a, 'col', forward)  6.47 us
    concatenate x8, other arithmetic, local(): own = jnp.concatenate(pending, axis=1)  2.8 us
  transfers between devices with their start and end apart: 38, of which 8 were waited for; matrix products, arithmetic and copies ran while one was open for 18% of the time, Pallas kernels for 0%

profile of v27, /device:TPU:0, one launch (start us, length us, event | category | flops | bytes accessed | tf_op | source)
XLA Modules:
  0.0 119.6 jit_solution(18024098741279953782)
XLA Ops:
  1.7 2.4 %constant_dynamic-update-slice_fusion.14 = (bf16[3,32,2,144,128]{4,3,2,1,0:T(8,128)(2,1)}, bf16[3,4,2,144,128]{4,3,2,1,0:T(8,128)(2,1)S(1)}) fusion(bf16[144]{0:T(256)(128)(2,1)S(1)} %pad.21.clone, bf16[3,4,2,1,128]{4,3,2,1,0:T(2,128)(2,1)S(1)} %broadcast_in_dim.7, bf16[3,4,2,3,128]{4,3,2,1,0:T(4,128)(2,1)S(1)} %broadcast_in_dim.6, ...), kind=kLoop, calls=%fused_computation.48 | loop fusion | flops 3538943 | bytes 2580768
  4.2 3.1 %collective-permute-start = (bf16[3,2,2,144,128]{4,3,2,1,0:T(8,128)(2,1)S(1)}, bf16[3,2,2,144,128]{4,3,2,1,0:T(8,128)(2,1)S(1)}, u32[]{:S(2)}, u32[]{:S(2)}) collective-permute-start(bf16[3,2,2,144,128]{4,3,2,1,0:T(8,128)(2,1)S(1)} %get-tuple-element.5), channel_id=1, source_target_pairs={{0,2},{2,4},{4,6},{6,7},{7,5},{5,3},{3,1},{1,0},{8,10},{10,12},{12... | collective-permute-start | bytes 1327112 | tf_op jit(solution)/shard_map/ppermute | solution.py:131
  8.1 3.9 %collective-permute-start.15 = (bf16[3,4,144,128]{3,2,1,0:T(8,128)(2,1)S(1)}, bf16[3,4,144,128]{3,2,1,0:T(8,128)(2,1)S(1)}, u32[]{:S(2)}, u32[]{:S(2)}) collective-permute-start(bf16[3,4,144,128]{3,2,1,0:T(8,128)(2,1)S(1)} %pad_maximum_fusion), channel_id=1, source_target_pairs={{0,16},{1,17},{10,26},{11,27},{20,4},{21,5},{30,14},{31,15}} | collective-permute-start | bytes 1327112 | tf_op jit(solution)/shard_map/ppermute | solution.py:105
  12.0 1.3 %collective-permute-start.14 = (bf16[3,4,144,128]{3,2,1,0:T(8,128)(2,1)S(1)}, bf16[3,4,144,128]{3,2,1,0:T(8,128)(2,1)S(1)}, u32[]{:S(2)}, u32[]{:S(2)}) collective-permute-start(bf16[3,4,144,128]{3,2,1,0:T(8,128)(2,1)S(1)} %pad_maximum_fusion), channel_id=1, source_target_pairs={{0,8},{1,9},{10,2},{11,3},{20,28},{21,29},{30,22},{31,23}} | collective-permute-start | bytes 1327112 | tf_op jit(solution)/shard_map/ppermute | solution.py:105
  13.4 4.0 %collective-permute-done = bf16[3,2,2,144,128]{4,3,2,1,0:T(8,128)(2,1)S(1)} collective-permute-done((bf16[3,2,2,144,128]{4,3,2,1,0:T(8,128)(2,1)S(1)}, bf16[3,2,2,144,128]{4,3,2,1,0:T(8,128)(2,1)S(1)}, u32[]{:S(2)}, u32[]{:S(2)}) %collective-permute-start) | collective-permute-done | bytes 442400 | tf_op jit(solution)/shard_map/ppermute | solution.py:131
  17.4 1.8 %collective-permute-start.2 = (bf16[3,2,2,144,128]{4,3,2,1,0:T(8,128)(2,1)S(1)}, bf16[3,2,2,144,128]{4,3,2,1,0:T(8,128)(2,1)S(1)}, u32[]{:S(2)}, u32[]{:S(2)}) collective-permute-start(bf16[3,2,2,144,128]{4,3,2,1,0:T(8,128)(2,1)S(1)} %collective-permute-done), channel_id=1, source_target_pairs={{0,2},{2,4},{4,6},{6,7},{7,5},{5,3},{3,1},{1,0},{8,10},{10,12},{12... | collective-permute-start | bytes 1327112 | tf_op jit(solution)/shard_map/ppermute | solution.py:131
  19.5 1.7 %collective-permute-start.18 = (bf16[3,4,144,128]{3,2,1,0:T(8,128)(2,1)S(1)}, bf16[3,4,144,128]{3,2,1,0:T(8,128)(2,1)S(1)}, u32[]{:S(2)}, u32[]{:S(2)}) collective-permute-start(bf16[3,4,144,128]{3,2,1,0:T(8,128)(2,1)S(1)} %pad_maximum_fusion.1), channel_id=1, source_target_pairs={{0,24},{1,25},{10,18},{11,19},{20,12},{21,13},{30,6},{31,7}} | collective-permute-start | bytes 1327112 | tf_op jit(solution)/shard_map/ppermute | solution.py:105
  23.6 6.3 %collective-permute-done.3 = bf16[3,2,2,144,128]{4,3,2,1,0:T(8,128)(2,1)S(1)} collective-permute-done((bf16[3,2,2,144,128]{4,3,2,1,0:T(8,128)(2,1)S(1)}, bf16[3,2,2,144,128]{4,3,2,1,0:T(8,128)(2,1)S(1)}, u32[]{:S(2)}, u32[]{:S(2)}) %collective-permute-start.3) | collective-permute-done | bytes 442400 | tf_op jit(solution)/shard_map/ppermute | solution.py:132
  30.5 1.5 %collective-permute-start.4 = (bf16[3,2,2,144,128]{4,3,2,1,0:T(8,128)(2,1)S(1)}, bf16[3,2,2,144,128]{4,3,2,1,0:T(8,128)(2,1)S(1)}, u32[]{:S(2)}, u32[]{:S(2)}) collective-permute-start(bf16[3,2,2,144,128]{4,3,2,1,0:T(8,128)(2,1)S(1)} %collective-permute-done.2), channel_id=1, source_target_pairs={{0,2},{2,4},{4,6},{6,7},{7,5},{5,3},{3,1},{1,0},{8,10},{10,12},{12... | collective-permute-start | bytes 1327112 | tf_op jit(solution)/shard_map/ppermute | solution.py:131
  33.8 1.3 %collective-permute-start.17 = (bf16[3,4,144,128]{3,2,1,0:T(8,128)(2,1)S(1)}, bf16[3,4,144,128]{3,2,1,0:T(8,128)(2,1)S(1)}, u32[]{:S(2)}, u32[]{:S(2)}) collective-permute-start(bf16[3,4,144,128]{3,2,1,0:T(8,128)(2,1)S(1)} %pad_maximum_fusion.1), channel_id=1, source_target_pairs={{0,8},{1,9},{10,2},{11,3},{20,28},{21,29},{30,22},{31,23}} | collective-permute-start | bytes 1327112 | tf_op jit(solution)/shard_map/ppermute | solution.py:105
  35.1 2.8 %collective-permute-start.21 = (bf16[3,4,144,128]{3,2,1,0:T(8,128)(2,1)S(1)}, bf16[3,4,144,128]{3,2,1,0:T(8,128)(2,1)S(1)}, u32[]{:S(2)}, u32[]{:S(2)}) collective-permute-start(bf16[3,4,144,128]{3,2,1,0:T(8,128)(2,1)S(1)} %pad_maximum_fusion.2), channel_id=1, source_target_pairs={{0,16},{1,17},{10,26},{11,27},{20,4},{21,5},{30,14},{31,15}} | collective-permute-start | bytes 1327112 | tf_op jit(solution)/shard_map/ppermute | solution.py:105
  45.0 1.3 %collective-permute-start.24 = (bf16[3,4,144,128]{3,2,1,0:T(8,128)(2,1)S(1)}, bf16[3,4,144,128]{3,2,1,0:T(8,128)(2,1)S(1)}, u32[]{:S(2)}, u32[]{:S(2)}) collective-permute-start(bf16[3,4,144,128]{3,2,1,0:T(8,128)(2,1)S(1)} %pad_maximum_fusion.3), channel_id=1, source_target_pairs={{0,24},{1,25},{10,18},{11,19},{20,12},{21,13},{30,6},{31,7}} | collective-permute-start | bytes 1327112 | tf_op jit(solution)/shard_map/ppermute | solution.py:105
  47.3 3.3 %collective-permute-done.7 = bf16[3,2,2,144,128]{4,3,2,1,0:T(8,128)(2,1)S(1)} collective-permute-done((bf16[3,2,2,144,128]{4,3,2,1,0:T(8,128)(2,1)S(1)}, bf16[3,2,2,144,128]{4,3,2,1,0:T(8,128)(2,1)S(1)}, u32[]{:S(2)}, u32[]{:S(2)}) %collective-permute-start.7) | collective-permute-done | bytes 442400 | tf_op jit(solution)/shard_map/ppermute | solution.py:132
  50.8 1.9 %collective-permute-start.8 = (bf16[3,2,2,144,128]{4,3,2,1,0:T(8,128)(2,1)S(1)}, bf16[3,2,2,144,128]{4,3,2,1,0:T(8,128)(2,1)S(1)}, u32[]{:S(2)}, u32[]{:S(2)}) collective-permute-start(bf16[3,2,2,144,128]{4,3,2,1,0:T(8,128)(2,1)S(1)} %collective-permute-done.6), channel_id=1, source_target_pairs={{0,2},{2,4},{4,6},{6,7},{7,5},{5,3},{3,1},{1,0},{8,10},{10,12},{12... | collective-permute-start | bytes 1327112 | tf_op jit(solution)/shard_map/ppermute | solution.py:131
  55.8 2.9 %collective-permute-start.27 = (bf16[3,4,144,128]{3,2,1,0:T(8,128)(2,1)S(1)}, bf16[3,4,144,128]{3,2,1,0:T(8,128)(2,1)S(1)}, u32[]{:S(2)}, u32[]{:S(2)}) collective-permute-start(bf16[3,4,144,128]{3,2,1,0:T(8,128)(2,1)S(1)} %pad_maximum_fusion.4), channel_id=1, source_target_pairs={{0,16},{1,17},{10,26},{11,27},{20,4},{21,5},{30,14},{31,15}} | collective-permute-start | bytes 1327112 | tf_op jit(solution)/shard_map/ppermute | solution.py:105
  59.7 1.4 %collective-permute-done.8 = bf16[3,2,2,144,128]{4,3,2,1,0:T(8,128)(2,1)S(1)} collective-permute-done((bf16[3,2,2,144,128]{4,3,2,1,0:T(8,128)(2,1)S(1)}, bf16[3,2,2,144,128]{4,3,2,1,0:T(8,128)(2,1)S(1)}, u32[]{:S(2)}, u32[]{:S(2)}) %collective-permute-start.8) | collective-permute-done | bytes 442400 | tf_op jit(solution)/shard_map/ppermute | solution.py:131
  61.1 2.1 %collective-permute-start.10 = (bf16[3,2,2,144,128]{4,3,2,1,0:T(8,128)(2,1)S(1)}, bf16[3,2,2,144,128]{4,3,2,1,0:T(8,128)(2,1)S(1)}, u32[]{:S(2)}, u32[]{:S(2)}) collective-permute-start(bf16[3,2,2,144,128]{4,3,2,1,0:T(8,128)(2,1)S(1)} %collective-permute-done.8), channel_id=1, source_target_pairs={{0,2},{2,4},{4,6},{6,7},{7,5},{5,3},{3,1},{1,0},{8,10},{10,12},{12... | collective-permute-start | bytes 1327112 | tf_op jit(solution)/shard_map/ppermute | solution.py:131
  66.3 2.1 %collective-permute-start.30 = (bf16[3,4,144,128]{3,2,1,0:T(8,128)(2,1)}, bf16[3,4,144,128]{3,2,1,0:T(8,128)(2,1)}, u32[]{:S(2)}, u32[]{:S(2)}) collective-permute-start(bf16[3,4,144,128]{3,2,1,0:T(8,128)(2,1)} %pad_maximum_fusion.5), channel_id=1, source_target_pairs={{0,24},{1,25},{10,18},{11,19},{20,12},{21,13},{30,6},{31,7}} | collective-permute-start | bytes 1327112 | tf_op jit(solution)/shard_map/ppermute | solution.py:105
  71.1 2.0 %collective-permute-start.12 = (bf16[3,2,2,144,128]{4,3,2,1,0:T(8,128)(2,1)S(1)}, bf16[3,2,2,144,128]{4,3,2,1,0:T(8,128)(2,1)S(1)}, u32[]{:S(2)}, u32[]{:S(2)}) collective-permute-start(bf16[3,2,2,144,128]{4,3,2,1,0:T(8,128)(2,1)S(1)} %collective-permute-done.10), channel_id=1, source_target_pairs={{0,2},{2,4},{4,6},{6,7},{7,5},{5,3},{3,1},{1,0},{8,10},{10,12},{12... | collective-permute-start | bytes 1327112 | tf_op jit(solution)/shard_map/ppermute | solution.py:131
  74.1 3.1 %collective-permute-start.29 = (bf16[3,4,144,128]{3,2,1,0:T(8,128)(2,1)}, bf16[3,4,144,128]{3,2,1,0:T(8,128)(2,1)}, u32[]{:S(2)}, u32[]{:S(2)}) collective-permute-start(bf16[3,4,144,128]{3,2,1,0:T(8,128)(2,1)} %pad_maximum_fusion.5), channel_id=1, source_target_pairs={{0,8},{1,9},{10,2},{11,3},{20,28},{21,29},{30,22},{31,23}} | collective-permute-start | bytes 1327112 | tf_op jit(solution)/shard_map/ppermute | solution.py:105
  77.2 2.9 %collective-permute-start.33 = (bf16[3,4,144,128]{3,2,1,0:T(8,128)(2,1)}, bf16[3,4,144,128]{3,2,1,0:T(8,128)(2,1)}, u32[]{:S(2)}, u32[]{:S(2)}) collective-permute-start(bf16[3,4,144,128]{3,2,1,0:T(8,128)(2,1)} %pad_maximum_fusion.6), channel_id=1, source_target_pairs={{0,16},{1,17},{10,26},{11,27},{20,4},{21,5},{30,14},{31,15}} | collective-permute-start | bytes 1327112 | tf_op jit(solution)/shard_map/ppermute | solution.py:105
  80.4 2.1 %collective-permute-start.32 = (bf16[3,4,144,128]{3,2,1,0:T(8,128)(2,1)}, bf16[3,4,144,128]{3,2,1,0:T(8,128)(2,1)}, u32[]{:S(2)}, u32[]{:S(2)}) collective-permute-start(bf16[3,4,144,128]{3,2,1,0:T(8,128)(2,1)} %pad_maximum_fusion.6), channel_id=1, source_target_pairs={{0,8},{1,9},{10,2},{11,3},{20,28},{21,29},{30,22},{31,23}} | collective-permute-start | bytes 1327112 | tf_op jit(solution)/shard_map/ppermute | solution.py:105
  82.5 3.1 %collective-permute-done.13 = bf16[3,2,2,144,128]{4,3,2,1,0:T(8,128)(2,1)S(1)} collective-permute-done((bf16[3,2,2,144,128]{4,3,2,1,0:T(8,128)(2,1)S(1)}, bf16[3,2,2,144,128]{4,3,2,1,0:T(8,128)(2,1)S(1)}, u32[]{:S(2)}, u32[]{:S(2)}) %collective-permute-start.13) | collective-permute-done | bytes 442400 | tf_op jit(solution)/shard_map/ppermute | solution.py:132
  85.6 1.4 %collective-permute-start.31 = (bf16[3,4,144,128]{3,2,1,0:T(8,128)(2,1)}, bf16[3,4,144,128]{3,2,1,0:T(8,128)(2,1)}, u32[]{:S(2)}, u32[]{:S(2)}) collective-permute-start(bf16[3,4,144,128]{3,2,1,0:T(8,128)(2,1)} %collective-permute-done.30), channel_id=1, source_target_pairs={{24,16},{25,17},{18,26},{19,27},{12,4},{13,5},{6,14},{7,15}} | collective-permute-start | bytes 1327112 | tf_op jit(solution)/shard_map/ppermute | solution.py:105
  88.6 4.3 %collective-permute-start.36 = (bf16[3,4,144,128]{3,2,1,0:T(8,128)(2,1)}, bf16[3,4,144,128]{3,2,1,0:T(8,128)(2,1)}, u32[]{:S(2)}, u32[]{:S(2)}) collective-permute-start(bf16[3,4,144,128]{3,2,1,0:T(8,128)(2,1)} %pad_maximum_fusion.7), channel_id=1, source_target_pairs={{0,24},{1,25},{10,18},{11,19},{20,12},{21,13},{30,6},{31,7}} | collective-permute-start | bytes 1327112 | tf_op jit(solution)/shard_map/ppermute | solution.py:105
  94.6 1.4 %collective-permute-start.34 = (bf16[3,4,144,128]{3,2,1,0:T(8,128)(2,1)}, bf16[3,4,144,128]{3,2,1,0:T(8,128)(2,1)}, u32[]{:S(2)}, u32[]{:S(2)}) collective-permute-start(bf16[3,4,144,128]{3,2,1,0:T(8,128)(2,1)} %collective-permute-done.33), channel_id=1, source_target_pairs={{16,24},{17,25},{26,18},{27,19},{4,12},{5,13},{14,6},{15,7}} | collective-permute-start | bytes 1327112 | tf_op jit(solution)/shard_map/ppermute | solution.py:105
  97.7 1.7 %slice.19 = bf16[96,2,1,1]{3,2,1,0:T(2,128)(2,1)} slice(bf16[96,2,144,128]{3,2,1,0:T(8,128)(2,1)} %bitcast.44), slice={[0:96], [0:2], [131:132], [0:1]} | slice | bytes 768 | tf_op jit(solution)/shard_map/slice | solution.py:152
  100.4 1.3 %collective-permute-start.35 = (bf16[3,4,144,128]{3,2,1,0:T(8,128)(2,1)}, bf16[3,4,144,128]{3,2,1,0:T(8,128)(2,1)S(1)}, u32[]{:S(2)}, u32[]{:S(2)}) collective-permute-start(bf16[3,4,144,128]{3,2,1,0:T(8,128)(2,1)} %pad_maximum_fusion.7), channel_id=1, source_target_pairs={{0,8},{1,9},{10,2},{11,3},{20,28},{21,29},{30,22},{31,23}} | collective-permute-start | bytes 1327112 | tf_op jit(solution)/shard_map/ppermute | solution.py:105
  102.5 1.5 %select_dynamic-update-slice_fusion.2 = bf16[3,32,144,128]{3,2,1,0:T(8,128)(2,1)S(1)} fusion(bf16[3,32,144,128]{3,2,1,0:T(8,128)(2,1)S(1)} %select_dynamic-update-slice_fusion.3, bf16[3,4,144,128]{3,2,1,0:T(8,128)(2,1)} %collective-permute-done.29, bf16[3,4,144,128]{3,2,1,0:T(8,128)(2,1)} %collective-permute-done.30, ...), kind=kLoop, calls=%fused_computation.11 | loop fusion | flops 1548288 | bytes 2211843
  104.0 1.5 %select_dynamic-update-slice_fusion.1 = bf16[3,32,144,128]{3,2,1,0:T(8,128)(2,1)S(1)} fusion(bf16[3,32,144,128]{3,2,1,0:T(8,128)(2,1)S(1)} %select_dynamic-update-slice_fusion.2, bf16[3,4,144,128]{3,2,1,0:T(8,128)(2,1)} %collective-permute-done.32, bf16[3,4,144,128]{3,2,1,0:T(8,128)(2,1)} %collective-permute-done.33, ...), kind=kLoop, calls=%fused_computation.10 | loop fusion | flops 1548288 | bytes 2211843
  105.4 1.3 %select_dynamic-update-slice_fusion = bf16[3,32,144,128]{3,2,1,0:T(8,128)(2,1)S(1)} fusion(bf16[3,32,144,128]{3,2,1,0:T(8,128)(2,1)S(1)} %select_dynamic-update-slice_fusion.1, bf16[3,4,144,128]{3,2,1,0:T(8,128)(2,1)S(1)} %collective-permute-done.35, bf16[3,4,144,128]{3,2,1,0:T(8,128)(2,1)} %collective-permute-done.36, ...), kind=kLoop, calls=%fused_computation.9 | loop fusion | flops 1548288 | bytes 2211843 | tf_op jit(solution)/shard_map/concatenate | solution.py:147
  109.3 10.4 %shard_map.37 = f32[2048,1024]{1,0:T(8,128)} custom-call(s32[288]{0:T(512)S(1)} %min.12.offs_ref, bf16[96,2,144,128]{3,2,1,0:T(8,128)(2,1)} %bitcast.45, bf16[96,144,128]{2,1,0:T(8,128)(2,1)S(1)} %bitcast.43), custom_call_target="tpu_custom_call" | custom-call | flops 805306368 | bytes 17825792 | tf_op jit(solution)/shard_map/pallas_call | solution.py:40
  (131 shorter events, 35.9 us)
Async XLA Ops:
  4.2 13.2 %collective-permute-start = (bf16[3,2,2,144,128]{4,3,2,1,0:T(8,128)(2,1)S(1)}, bf16[3,2,2,144,128]{4,3,2,1,0:T(8,128)(2,1)S(1)}, u32[]{:S(2)}, u32[]{:S(2)}) collective-permute-start(bf16[3,2,2,144,128]{4,3,2,1,0:T(8,128)(2,1)S(1)} %get-tuple-element.5), channel_id=1, source_target_pairs={{0,2},{2,4},{4,6},{6,7},{7,5},{5,3},{3,1},{1,0},{8,10},{10,12},{12... | collective-permute-start | bytes 1327112 | tf_op jit(solution)/shard_map/ppermute | solution.py:131
  7.3 11.9 %collective-permute-start.1 = (bf16[3,2,2,144,128]{4,3,2,1,0:T(8,128)(2,1)S(1)}, bf16[3,2,2,144,128]{4,3,2,1,0:T(8,128)(2,1)S(1)}, u32[]{:S(2)}, u32[]{:S(2)}) collective-permute-start(bf16[3,2,2,144,128]{4,3,2,1,0:T(8,128)(2,1)S(1)} %get-tuple-element.6), channel_id=1, source_target_pairs={{2,0},{4,2},{6,4},{7,6},{5,7},{3,5},{1,3},{0,1},{10,8},{12,10},{14... | collective-permute-start | bytes 1327112 | tf_op jit(solution)/shard_map/ppermute | solution.py:132
  8.1 13.1 %collective-permute-start.15 = (bf16[3,4,144,128]{3,2,1,0:T(8,128)(2,1)S(1)}, bf16[3,4,144,128]{3,2,1,0:T(8,128)(2,1)S(1)}, u32[]{:S(2)}, u32[]{:S(2)}) collective-permute-start(bf16[3,4,144,128]{3,2,1,0:T(8,128)(2,1)S(1)} %pad_maximum_fusion), channel_id=1, source_target_pairs={{0,16},{1,17},{10,26},{11,27},{20,4},{21,5},{30,14},{31,15}} | collective-permute-start | bytes 1327112 | tf_op jit(solution)/shard_map/ppermute | solution.py:105
  12.0 21.9 %collective-permute-start.14 = (bf16[3,4,144,128]{3,2,1,0:T(8,128)(2,1)S(1)}, bf16[3,4,144,128]{3,2,1,0:T(8,128)(2,1)S(1)}, u32[]{:S(2)}, u32[]{:S(2)}) collective-permute-start(bf16[3,4,144,128]{3,2,1,0:T(8,128)(2,1)S(1)} %pad_maximum_fusion), channel_id=1, source_target_pairs={{0,8},{1,9},{10,2},{11,3},{20,28},{21,29},{30,22},{31,23}} | collective-permute-start | bytes 1327112 | tf_op jit(solution)/shard_map/ppermute | solution.py:105
  17.4 13.1 %collective-permute-start.2 = (bf16[3,2,2,144,128]{4,3,2,1,0:T(8,128)(2,1)S(1)}, bf16[3,2,2,144,128]{4,3,2,1,0:T(8,128)(2,1)S(1)}, u32[]{:S(2)}, u32[]{:S(2)}) collective-permute-start(bf16[3,2,2,144,128]{4,3,2,1,0:T(8,128)(2,1)S(1)} %collective-permute-done), channel_id=1, source_target_pairs={{0,2},{2,4},{4,6},{6,7},{7,5},{5,3},{3,1},{1,0},{8,10},{10,12},{12... | collective-permute-start | bytes 1327112 | tf_op jit(solution)/shard_map/ppermute | solution.py:131
  19.2 10.8 %collective-permute-start.3 = (bf16[3,2,2,144,128]{4,3,2,1,0:T(8,128)(2,1)S(1)}, bf16[3,2,2,144,128]{4,3,2,1,0:T(8,128)(2,1)S(1)}, u32[]{:S(2)}, u32[]{:S(2)}) collective-permute-start(bf16[3,2,2,144,128]{4,3,2,1,0:T(8,128)(2,1)S(1)} %collective-permute-done.1), channel_id=1, source_target_pairs={{2,0},{4,2},{6,4},{7,6},{5,7},{3,5},{1,3},{0,1},{10,8},{12,10},{14... | collective-permute-start | bytes 1327112 | tf_op jit(solution)/shard_map/ppermute | solution.py:132
  19.5 15.6 %collective-permute-start.18 = (bf16[3,4,144,128]{3,2,1,0:T(8,128)(2,1)S(1)}, bf16[3,4,144,128]{3,2,1,0:T(8,128)(2,1)S(1)}, u32[]{:S(2)}, u32[]{:S(2)}) collective-permute-start(bf16[3,4,144,128]{3,2,1,0:T(8,128)(2,1)S(1)} %pad_maximum_fusion.1), channel_id=1, source_target_pairs={{0,24},{1,25},{10,18},{11,19},{20,12},{21,13},{30,6},{31,7}} | collective-permute-start | bytes 1327112 | tf_op jit(solution)/shard_map/ppermute | solution.py:105
  21.2 16.8 %collective-permute-start.16 = (bf16[3,4,144,128]{3,2,1,0:T(8,128)(2,1)S(1)}, bf16[3,4,144,128]{3,2,1,0:T(8,128)(2,1)S(1)}, u32[]{:S(2)}, u32[]{:S(2)}) collective-permute-start(bf16[3,4,144,128]{3,2,1,0:T(8,128)(2,1)S(1)} %collective-permute-done.15), channel_id=1, source_target_pairs={{16,24},{17,25},{26,18},{27,19},{4,12},{5,13},{14,6},{15,7}} | collective-permute-start | bytes 1327112 | tf_op jit(solution)/shard_map/ppermute | solution.py:105
  29.9 9.8 %collective-permute-start.5 = (bf16[3,2,2,144,128]{4,3,2,1,0:T(8,128)(2,1)S(1)}, bf16[3,2,2,144,128]{4,3,2,1,0:T(8,128)(2,1)S(1)}, u32[]{:S(2)}, u32[]{:S(2)}) collective-permute-start(bf16[3,2,2,144,128]{4,3,2,1,0:T(8,128)(2,1)S(1)} %collective-permute-done.3), channel_id=1, source_target_pairs={{2,0},{4,2},{6,4},{7,6},{5,7},{3,5},{1,3},{0,1},{10,8},{12,10},{14... | collective-permute-start | bytes 1327112 | tf_op jit(solution)/shard_map/ppermute | solution.py:132
  30.5 10.3 %collective-permute-start.4 = (bf16[3,2,2,144,128]{4,3,2,1,0:T(8,128)(2,1)S(1)}, bf16[3,2,2,144,128]{4,3,2,1,0:T(8,128)(2,1)S(1)}, u32[]{:S(2)}, u32[]{:S(2)}) collective-permute-start(bf16[3,2,2,144,128]{4,3,2,1,0:T(8,128)(2,1)S(1)} %collective-permute-done.2), channel_id=1, source_target_pairs={{0,2},{2,4},{4,6},{6,7},{7,5},{5,3},{3,1},{1,0},{8,10},{10,12},{12... | collective-permute-start | bytes 1327112 | tf_op jit(solution)/shard_map/ppermute | solution.py:131
  33.8 9.9 %collective-permute-start.17 = (bf16[3,4,144,128]{3,2,1,0:T(8,128)(2,1)S(1)}, bf16[3,4,144,128]{3,2,1,0:T(8,128)(2,1)S(1)}, u32[]{:S(2)}, u32[]{:S(2)}) collective-permute-start(bf16[3,4,144,128]{3,2,1,0:T(8,128)(2,1)S(1)} %pad_maximum_fusion.1), channel_id=1, source_target_pairs={{0,8},{1,9},{10,2},{11,3},{20,28},{21,29},{30,22},{31,23}} | collective-permute-start | bytes 1327112 | tf_op jit(solution)/shard_map/ppermute | solution.py:105
  35.1 9.9 %collective-permute-start.21 = (bf16[3,4,144,128]{3,2,1,0:T(8,128)(2,1)S(1)}, bf16[3,4,144,128]{3,2,1,0:T(8,128)(2,1)S(1)}, u32[]{:S(2)}, u32[]{:S(2)}) collective-permute-start(bf16[3,4,144,128]{3,2,1,0:T(8,128)(2,1)S(1)} %pad_maximum_fusion.2), channel_id=1, source_target_pairs={{0,16},{1,17},{10,26},{11,27},{20,4},{21,5},{30,14},{31,15}} | collective-permute-start | bytes 1327112 | tf_op jit(solution)/shard_map/ppermute | solution.py:105
  39.8 10.8 %collective-permute-start.7 = (bf16[3,2,2,144,128]{4,3,2,1,0:T(8,128)(2,1)S(1)}, bf16[3,2,2,144,128]{4,3,2,1,0:T(8,128)(2,1)S(1)}, u32[]{:S(2)}, u32[]{:S(2)}) collective-permute-start(bf16[3,2,2,144,128]{4,3,2,1,0:T(8,128)(2,1)S(1)} %collective-permute-done.5), channel_id=1, source_target_pairs={{2,0},{4,2},{6,4},{7,6},{5,7},{3,5},{1,3},{0,1},{10,8},{12,10},{14... | collective-permute-start | bytes 1327112 | tf_op jit(solution)/shard_map/ppermute | solution.py:132
  40.8 9.9 %collective-permute-start.6 = (bf16[3,2,2,144,128]{4,3,2,1,0:T(8,128)(2,1)S(1)}, bf16[3,2,2,144,128]{4,3,2,1,0:T(8,128)(2,1)S(1)}, u32[]{:S(2)}, u32[]{:S(2)}) collective-permute-start(bf16[3,2,2,144,128]{4,3,2,1,0:T(8,128)(2,1)S(1)} %collective-permute-done.4), channel_id=1, source_target_pairs={{0,2},{2,4},{4,6},{6,7},{7,5},{5,3},{3,1},{1,0},{8,10},{10,12},{12... | collective-permute-start | bytes 1327112 | tf_op jit(solution)/shard_map/ppermute | solution.py:131
  43.7 10.8 %collective-permute-start.20 = (bf16[3,4,144,128]{3,2,1,0:T(8,128)(2,1)S(1)}, bf16[3,4,144,128]{3,2,1,0:T(8,128)(2,1)S(1)}, u32[]{:S(2)}, u32[]{:S(2)}) collective-permute-start(bf16[3,4,144,128]{3,2,1,0:T(8,128)(2,1)S(1)} %pad_maximum_fusion.2), channel_id=1, source_target_pairs={{0,8},{1,9},{10,2},{11,3},{20,28},{21,29},{30,22},{31,23}} | collective-permute-start | bytes 1327112 | tf_op jit(solution)/shard_map/ppermute | solution.py:105
  45.0 13.7 %collective-permute-start.24 = (bf16[3,4,144,128]{3,2,1,0:T(8,128)(2,1)S(1)}, bf16[3,4,144,128]{3,2,1,0:T(8,128)(2,1)S(1)}, u32[]{:S(2)}, u32[]{:S(2)}) collective-permute-start(bf16[3,4,144,128]{3,2,1,0:T(8,128)(2,1)S(1)} %pad_maximum_fusion.3), channel_id=1, source_target_pairs={{0,24},{1,25},{10,18},{11,19},{20,12},{21,13},{30,6},{31,7}} | collective-permute-start | bytes 1327112 | tf_op jit(solution)/shard_map/ppermute | solution.py:105
  46.3 9.4 %collective-permute-start.22 = (bf16[3,4,144,128]{3,2,1,0:T(8,128)(2,1)S(1)}, bf16[3,4,144,128]{3,2,1,0:T(8,128)(2,1)S(1)}, u32[]{:S(2)}, u32[]{:S(2)}) collective-permute-start(bf16[3,4,144,128]{3,2,1,0:T(8,128)(2,1)S(1)} %collective-permute-done.21), channel_id=1, source_target_pairs={{16,24},{17,25},{26,18},{27,19},{4,12},{5,13},{14,6},{15,7}} | collective-permute-start | bytes 1327112 | tf_op jit(solution)/shard_map/ppermute | solution.py:105
  50.6 12.6 %collective-permute-start.9 = (bf16[3,2,2,144,128]{4,3,2,1,0:T(8,128)(2,1)S(1)}, bf16[3,2,2,144,128]{4,3,2,1,0:T(8,128)(2,1)S(1)}, u32[]{:S(2)}, u32[]{:S(2)}) collective-permute-start(bf16[3,2,2,144,128]{4,3,2,1,0:T(8,128)(2,1)S(1)} %collective-permute-done.7), channel_id=1, source_target_pairs={{2,0},{4,2},{6,4},{7,6},{5,7},{3,5},{1,3},{0,1},{10,8},{12,10},{14... | collective-permute-start | bytes 1327112 | tf_op jit(solution)/shard_map/ppermute | solution.py:132
  50.8 10.4 %collective-permute-start.8 = (bf16[3,2,2,144,128]{4,3,2,1,0:T(8,128)(2,1)S(1)}, bf16[3,2,2,144,128]{4,3,2,1,0:T(8,128)(2,1)S(1)}, u32[]{:S(2)}, u32[]{:S(2)}) collective-permute-start(bf16[3,2,2,144,128]{4,3,2,1,0:T(8,128)(2,1)S(1)} %collective-permute-done.6), channel_id=1, source_target_pairs={{0,2},{2,4},{4,6},{6,7},{7,5},{5,3},{3,1},{1,0},{8,10},{10,12},{12... | collective-permute-start | bytes 1327112 | tf_op jit(solution)/shard_map/ppermute | solution.py:131
  54.5 10.5 %collective-permute-start.23 = (bf16[3,4,144,128]{3,2,1,0:T(8,128)(2,1)S(1)}, bf16[3,4,144,128]{3,2,1,0:T(8,128)(2,1)S(1)}, u32[]{:S(2)}, u32[]{:S(2)}) collective-permute-start(bf16[3,4,144,128]{3,2,1,0:T(8,128)(2,1)S(1)} %pad_maximum_fusion.3), channel_id=1, source_target_pairs={{0,8},{1,9},{10,2},{11,3},{20,28},{21,29},{30,22},{31,23}} | collective-permute-start | bytes 1327112 | tf_op jit(solution)/shard_map/ppermute | solution.py:105
  55.8 12.6 %collective-permute-start.27 = (bf16[3,4,144,128]{3,2,1,0:T(8,128)(2,1)S(1)}, bf16[3,4,144,128]{3,2,1,0:T(8,128)(2,1)S(1)}, u32[]{:S(2)}, u32[]{:S(2)}) collective-permute-start(bf16[3,4,144,128]{3,2,1,0:T(8,128)(2,1)S(1)} %pad_maximum_fusion.4), channel_id=1, source_target_pairs={{0,16},{1,17},{10,26},{11,27},{20,4},{21,5},{30,14},{31,15}} | collective-permute-start | bytes 1327112 | tf_op jit(solution)/shard_map/ppermute | solution.py:105
  61.1 10.0 %collective-permute-start.10 = (bf16[3,2,2,144,128]{4,3,2,1,0:T(8,128)(2,1)S(1)}, bf16[3,2,2,144,128]{4,3,2,1,0:T(8,128)(2,1)S(1)}, u32[]{:S(2)}, u32[]{:S(2)}) collective-permute-start(bf16[3,2,2,144,128]{4,3,2,1,0:T(8,128)(2,1)S(1)} %collective-permute-done.8), channel_id=1, source_target_pairs={{0,2},{2,4},{4,6},{6,7},{7,5},{5,3},{3,1},{1,0},{8,10},{10,12},{12... | collective-permute-start | bytes 1327112 | tf_op jit(solution)/shard_map/ppermute | solution.py:131
  63.2 9.9 %collective-permute-start.11 = (bf16[3,2,2,144,128]{4,3,2,1,0:T(8,128)(2,1)S(1)}, bf16[3,2,2,144,128]{4,3,2,1,0:T(8,128)(2,1)S(1)}, u32[]{:S(2)}, u32[]{:S(2)}) collective-permute-start(bf16[3,2,2,144,128]{4,3,2,1,0:T(8,128)(2,1)S(1)} %collective-permute-done.9), channel_id=1, source_target_pairs={{2,0},{4,2},{6,4},{7,6},{5,7},{3,5},{1,3},{0,1},{10,8},{12,10},{14... | collective-permute-start | bytes 1327112 | tf_op jit(solution)/shard_map/ppermute | solution.py:132
  66.3 14.1 %collective-permute-start.30 = (bf16[3,4,144,128]{3,2,1,0:T(8,128)(2,1)}, bf16[3,4,144,128]{3,2,1,0:T(8,128)(2,1)}, u32[]{:S(2)}, u32[]{:S(2)}) collective-permute-start(bf16[3,4,144,128]{3,2,1,0:T(8,128)(2,1)} %pad_maximum_fusion.5), channel_id=1, source_target_pairs={{0,24},{1,25},{10,18},{11,19},{20,12},{21,13},{30,6},{31,7}} | collective-permute-start | bytes 1327112 | tf_op jit(solution)/shard_map/ppermute | solution.py:105
  71.1 15.9 %collective-permute-start.12 = (bf16[3,2,2,144,128]{4,3,2,1,0:T(8,128)(2,1)S(1)}, bf16[3,2,2,144,128]{4,3,2,1,0:T(8,128)(2,1)S(1)}, u32[]{:S(2)}, u32[]{:S(2)}) collective-permute-start(bf16[3,2,2,144,128]{4,3,2,1,0:T(8,128)(2,1)S(1)} %collective-permute-done.10), channel_id=1, source_target_pairs={{0,2},{2,4},{4,6},{6,7},{7,5},{5,3},{3,1},{1,0},{8,10},{10,12},{12... | collective-permute-start | bytes 1327112 | tf_op jit(solution)/shard_map/ppermute | solution.py:131
  73.1 12.5 %collective-permute-start.13 = (bf16[3,2,2,144,128]{4,3,2,1,0:T(8,128)(2,1)S(1)}, bf16[3,2,2,144,128]{4,3,2,1,0:T(8,128)(2,1)S(1)}, u32[]{:S(2)}, u32[]{:S(2)}) collective-permute-start(bf16[3,2,2,144,128]{4,3,2,1,0:T(8,128)(2,1)S(1)} %collective-permute-done.11), channel_id=1, source_target_pairs={{2,0},{4,2},{6,4},{7,6},{5,7},{3,5},{1,3},{0,1},{10,8},{12,10},{14... | collective-permute-start | bytes 1327112 | tf_op jit(solution)/shard_map/ppermute | solution.py:132
  74.1 26.3 %collective-permute-start.29 = (bf16[3,4,144,128]{3,2,1,0:T(8,128)(2,1)}, bf16[3,4,144,128]{3,2,1,0:T(8,128)(2,1)}, u32[]{:S(2)}, u32[]{:S(2)}) collective-permute-start(bf16[3,4,144,128]{3,2,1,0:T(8,128)(2,1)} %pad_maximum_fusion.5), channel_id=1, source_target_pairs={{0,8},{1,9},{10,2},{11,3},{20,28},{21,29},{30,22},{31,23}} | collective-permute-start | bytes 1327112 | tf_op jit(solution)/shard_map/ppermute | solution.py:105
  77.2 17.4 %collective-permute-start.33 = (bf16[3,4,144,128]{3,2,1,0:T(8,128)(2,1)}, bf16[3,4,144,128]{3,2,1,0:T(8,128)(2,1)}, u32[]{:S(2)}, u32[]{:S(2)}) collective-permute-start(bf16[3,4,144,128]{3,2,1,0:T(8,128)(2,1)} %pad_maximum_fusion.6), channel_id=1, source_target_pairs={{0,16},{1,17},{10,26},{11,27},{20,4},{21,5},{30,14},{31,15}} | collective-permute-start | bytes 1327112 | tf_op jit(solution)/shard_map/ppermute | solution.py:105
  80.4 23.5 %collective-permute-start.32 = (bf16[3,4,144,128]{3,2,1,0:T(8,128)(2,1)}, bf16[3,4,144,128]{3,2,1,0:T(8,128)(2,1)}, u32[]{:S(2)}, u32[]{:S(2)}) collective-permute-start(bf16[3,4,144,128]{3,2,1,0:T(8,128)(2,1)} %pad_maximum_fusion.6), channel_id=1, source_target_pairs={{0,8},{1,9},{10,2},{11,3},{20,28},{21,29},{30,22},{31,23}} | collective-permute-start | bytes 1327112 | tf_op jit(solution)/shard_map/ppermute | solution.py:105
  85.6 16.9 %collective-permute-start.31 = (bf16[3,4,144,128]{3,2,1,0:T(8,128)(2,1)}, bf16[3,4,144,128]{3,2,1,0:T(8,128)(2,1)}, u32[]{:S(2)}, u32[]{:S(2)}) collective-permute-start(bf16[3,4,144,128]{3,2,1,0:T(8,128)(2,1)} %collective-permute-done.30), channel_id=1, source_target_pairs={{24,16},{25,17},{18,26},{19,27},{12,4},{13,5},{6,14},{7,15}} | collective-permute-start | bytes 1327112 | tf_op jit(solution)/shard_map/ppermute | solution.py:105
  88.6 13.2 %collective-permute-start.36 = (bf16[3,4,144,128]{3,2,1,0:T(8,128)(2,1)}, bf16[3,4,144,128]{3,2,1,0:T(8,128)(2,1)}, u32[]{:S(2)}, u32[]{:S(2)}) collective-permute-start(bf16[3,4,144,128]{3,2,1,0:T(8,128)(2,1)} %pad_maximum_fusion.7), channel_id=1, source_target_pairs={{0,24},{1,25},{10,18},{11,19},{20,12},{21,13},{30,6},{31,7}} | collective-permute-start | bytes 1327112 | tf_op jit(solution)/shard_map/ppermute | solution.py:105
  94.6 9.4 %collective-permute-start.34 = (bf16[3,4,144,128]{3,2,1,0:T(8,128)(2,1)}, bf16[3,4,144,128]{3,2,1,0:T(8,128)(2,1)}, u32[]{:S(2)}, u32[]{:S(2)}) collective-permute-start(bf16[3,4,144,128]{3,2,1,0:T(8,128)(2,1)} %collective-permute-done.33), channel_id=1, source_target_pairs={{16,24},{17,25},{26,18},{27,19},{4,12},{5,13},{14,6},{15,7}} | collective-permute-start | bytes 1327112 | tf_op jit(solution)/shard_map/ppermute | solution.py:105
  (18 other events, 135.3 us)

commit v28 on v26

--- a/solution.py
+++ b/solution.py
@@ -8,7 +8,7 @@
 from jax.sharding import PartitionSpec as P
 
 IBS = 8
-CHUNK = 48
+CHUNK = 24
 META = 16
 
 

time: 120 us -> 121 us (level)
  no operation moved by 1% of the time
where the time goes in v28:
time: 121 us; the launch traced here: 120 us
  starting transfers between devices  63 us (52%)
  local copies, waits for them, and re-layouts  19.2 us (16%)
  waiting for transfers between devices  13.7 us (11%)
  other arithmetic  12.2 us (10%)
  Pallas kernels  11.3 us (9%)
    ppermute x24, starting transfers between devices, send(): lax.ppermute(v, ('row', 'col'), [(a * ncol + cc, b * ncol + cc) for a, b,...  47.8 us
    unnamed x37, local copies, waits for them, and re-layouts  12.5 us
    ppermute x7, starting transfers between devices, local(): a = lax.ppermute(a, 'col', forward)  11.6 us
    pallas_call x1, Pallas kernels, gram_call(): pl.pallas_call(kernel, grid_spec=pltpu.PrefetchScalarGridSpec(num_scalar_...  11.3 us
    ppermute x7, waiting for transfers between devices, local(): b = lax.ppermute(b, 'col', backward)  8.34 us
    unnamed x8, other arithmetic  6.64 us
    ppermute x7, waiting for transfers between devices, local(): a = lax.ppermute(a, 'col', forward)  5.35 us
    ppermute x7, starting transfers between devices, local(): b = lax.ppermute(b, 'col', backward)  3.59 us
  transfers between devices with their start and end apart: 38, of which 7 were waited for; matrix products, arithmetic and copies ran while one was open for 18% of the time, Pallas kernels for 0%

profile of v28, /device:TPU:0, one launch (start us, length us, event | category | flops | bytes accessed | tf_op | source)
XLA Modules:
  0.0 120.1 jit_solution(11383819066200800381)
XLA Ops:
  1.7 2.4 %constant_dynamic-update-slice_fusion.14 = (bf16[3,32,2,144,128]{4,3,2,1,0:T(8,128)(2,1)}, bf16[3,4,2,144,128]{4,3,2,1,0:T(8,128)(2,1)S(1)}) fusion(bf16[144]{0:T(256)(128)(2,1)S(1)} %pad.21.clone, bf16[3,4,2,1,128]{4,3,2,1,0:T(2,128)(2,1)S(1)} %broadcast_in_dim.7, bf16[3,4,2,3,128]{4,3,2,1,0:T(4,128)(2,1)S(1)} %broadcast_in_dim.6, ...), kind=kLoop, calls=%fused_computation.48 | loop fusion | flops 3538943 | bytes 2580768
  4.2 3.1 %collective-permute-start = (bf16[3,2,2,144,128]{4,3,2,1,0:T(8,128)(2,1)S(1)}, bf16[3,2,2,144,128]{4,3,2,1,0:T(8,128)(2,1)S(1)}, u32[]{:S(2)}, u32[]{:S(2)}) collective-permute-start(bf16[3,2,2,144,128]{4,3,2,1,0:T(8,128)(2,1)S(1)} %get-tuple-element.5), channel_id=1, source_target_pairs={{0,2},{2,4},{4,6},{6,7},{7,5},{5,3},{3,1},{1,0},{8,10},{10,12},{12... | collective-permute-start | bytes 1327112 | tf_op jit(solution)/shard_map/ppermute | solution.py:129
  8.1 3.9 %collective-permute-start.15 = (bf16[3,4,144,128]{3,2,1,0:T(8,128)(2,1)S(1)}, bf16[3,4,144,128]{3,2,1,0:T(8,128)(2,1)S(1)}, u32[]{:S(2)}, u32[]{:S(2)}) collective-permute-start(bf16[3,4,144,128]{3,2,1,0:T(8,128)(2,1)S(1)} %pad_maximum_fusion), channel_id=1, source_target_pairs={{0,16},{1,17},{10,26},{11,27},{20,4},{21,5},{30,14},{31,15}} | collective-permute-start | bytes 1327112 | tf_op jit(solution)/shard_map/ppermute | solution.py:105
  12.0 1.3 %collective-permute-start.14 = (bf16[3,4,144,128]{3,2,1,0:T(8,128)(2,1)S(1)}, bf16[3,4,144,128]{3,2,1,0:T(8,128)(2,1)S(1)}, u32[]{:S(2)}, u32[]{:S(2)}) collective-permute-start(bf16[3,4,144,128]{3,2,1,0:T(8,128)(2,1)S(1)} %pad_maximum_fusion), channel_id=1, source_target_pairs={{0,8},{1,9},{10,2},{11,3},{20,28},{21,29},{30,22},{31,23}} | collective-permute-start | bytes 1327112 | tf_op jit(solution)/shard_map/ppermute | solution.py:105
  13.4 4.0 %collective-permute-done = bf16[3,2,2,144,128]{4,3,2,1,0:T(8,128)(2,1)S(1)} collective-permute-done((bf16[3,2,2,144,128]{4,3,2,1,0:T(8,128)(2,1)S(1)}, bf16[3,2,2,144,128]{4,3,2,1,0:T(8,128)(2,1)S(1)}, u32[]{:S(2)}, u32[]{:S(2)}) %collective-permute-start) | collective-permute-done | bytes 442400 | tf_op jit(solution)/shard_map/ppermute | solution.py:129
  17.4 1.8 %collective-permute-start.2 = (bf16[3,2,2,144,128]{4,3,2,1,0:T(8,128)(2,1)S(1)}, bf16[3,2,2,144,128]{4,3,2,1,0:T(8,128)(2,1)S(1)}, u32[]{:S(2)}, u32[]{:S(2)}) collective-permute-start(bf16[3,2,2,144,128]{4,3,2,1,0:T(8,128)(2,1)S(1)} %collective-permute-done), channel_id=1, source_target_pairs={{0,2},{2,4},{4,6},{6,7},{7,5},{5,3},{3,1},{1,0},{8,10},{10,12},{12... | collective-permute-start | bytes 1327112 | tf_op jit(solution)/shard_map/ppermute | solution.py:129
  19.5 3.6 %collective-permute-start.18 = (bf16[3,4,144,128]{3,2,1,0:T(8,128)(2,1)S(1)}, bf16[3,4,144,128]{3,2,1,0:T(8,128)(2,1)S(1)}, u32[]{:S(2)}, u32[]{:S(2)}) collective-permute-start(bf16[3,4,144,128]{3,2,1,0:T(8,128)(2,1)S(1)} %pad_maximum_fusion.1), channel_id=1, source_target_pairs={{0,16},{1,17},{10,26},{11,27},{20,4},{21,5},{30,14},{31,15}} | collective-permute-start | bytes 1327112 | tf_op jit(solution)/shard_map/ppermute | solution.py:105
  25.6 4.3 %collective-permute-done.3 = bf16[3,2,2,144,128]{4,3,2,1,0:T(8,128)(2,1)S(1)} collective-permute-done((bf16[3,2,2,144,128]{4,3,2,1,0:T(8,128)(2,1)S(1)}, bf16[3,2,2,144,128]{4,3,2,1,0:T(8,128)(2,1)S(1)}, u32[]{:S(2)}, u32[]{:S(2)}) %collective-permute-start.3) | collective-permute-done | bytes 442400 | tf_op jit(solution)/shard_map/ppermute | solution.py:130
  30.5 1.5 %collective-permute-start.4 = (bf16[3,2,2,144,128]{4,3,2,1,0:T(8,128)(2,1)S(1)}, bf16[3,2,2,144,128]{4,3,2,1,0:T(8,128)(2,1)S(1)}, u32[]{:S(2)}, u32[]{:S(2)}) collective-permute-start(bf16[3,2,2,144,128]{4,3,2,1,0:T(8,128)(2,1)S(1)} %collective-permute-done.2), channel_id=1, source_target_pairs={{0,2},{2,4},{4,6},{6,7},{7,5},{5,3},{3,1},{1,0},{8,10},{10,12},{12... | collective-permute-start | bytes 1327112 | tf_op jit(solution)/shard_map/ppermute | solution.py:129
  33.8 1.3 %collective-permute-start.17 = (bf16[3,4,144,128]{3,2,1,0:T(8,128)(2,1)S(1)}, bf16[3,4,144,128]{3,2,1,0:T(8,128)(2,1)S(1)}, u32[]{:S(2)}, u32[]{:S(2)}) collective-permute-start(bf16[3,4,144,128]{3,2,1,0:T(8,128)(2,1)S(1)} %pad_maximum_fusion.1), channel_id=1, source_target_pairs={{0,8},{1,9},{10,2},{11,3},{20,28},{21,29},{30,22},{31,23}} | collective-permute-start | bytes 1327112 | tf_op jit(solution)/shard_map/ppermute | solution.py:105
  35.1 2.8 %collective-permute-start.21 = (bf16[3,4,144,128]{3,2,1,0:T(8,128)(2,1)S(1)}, bf16[3,4,144,128]{3,2,1,0:T(8,128)(2,1)S(1)}, u32[]{:S(2)}, u32[]{:S(2)}) collective-permute-start(bf16[3,4,144,128]{3,2,1,0:T(8,128)(2,1)S(1)} %pad_maximum_fusion.2), channel_id=1, source_target_pairs={{0,16},{1,17},{10,26},{11,27},{20,4},{21,5},{30,14},{31,15}} | collective-permute-start | bytes 1327112 | tf_op jit(solution)/shard_map/ppermute | solution.py:105
  43.7 1.3 %collective-permute-start.20 = (bf16[3,4,144,128]{3,2,1,0:T(8,128)(2,1)S(1)}, bf16[3,4,144,128]{3,2,1,0:T(8,128)(2,1)S(1)}, u32[]{:S(2)}, u32[]{:S(2)}) collective-permute-start(bf16[3,4,144,128]{3,2,1,0:T(8,128)(2,1)S(1)} %pad_maximum_fusion.2), channel_id=1, source_target_pairs={{0,8},{1,9},{10,2},{11,3},{20,28},{21,29},{30,22},{31,23}} | collective-permute-start | bytes 1327112 | tf_op jit(solution)/shard_map/ppermute | solution.py:105
  45.0 3.1 %collective-permute-start.24 = (bf16[3,4,144,128]{3,2,1,0:T(8,128)(2,1)S(1)}, bf16[3,4,144,128]{3,2,1,0:T(8,128)(2,1)S(1)}, u32[]{:S(2)}, u32[]{:S(2)}) collective-permute-start(bf16[3,4,144,128]{3,2,1,0:T(8,128)(2,1)S(1)} %pad_maximum_fusion.3), channel_id=1, source_target_pairs={{0,16},{1,17},{10,26},{11,27},{20,4},{21,5},{30,14},{31,15}} | collective-permute-start | bytes 1327112 | tf_op jit(solution)/shard_map/ppermute | solution.py:105
  49.1 1.5 %collective-permute-done.7 = bf16[3,2,2,144,128]{4,3,2,1,0:T(8,128)(2,1)S(1)} collective-permute-done((bf16[3,2,2,144,128]{4,3,2,1,0:T(8,128)(2,1)S(1)}, bf16[3,2,2,144,128]{4,3,2,1,0:T(8,128)(2,1)S(1)}, u32[]{:S(2)}, u32[]{:S(2)}) %collective-permute-start.7) | collective-permute-done | bytes 442400 | tf_op jit(solution)/shard_map/ppermute | solution.py:130
  50.8 1.9 %collective-permute-start.8 = (bf16[3,2,2,144,128]{4,3,2,1,0:T(8,128)(2,1)S(1)}, bf16[3,2,2,144,128]{4,3,2,1,0:T(8,128)(2,1)S(1)}, u32[]{:S(2)}, u32[]{:S(2)}) collective-permute-start(bf16[3,2,2,144,128]{4,3,2,1,0:T(8,128)(2,1)S(1)} %collective-permute-done.6), channel_id=1, source_target_pairs={{0,2},{2,4},{4,6},{6,7},{7,5},{5,3},{3,1},{1,0},{8,10},{10,12},{12... | collective-permute-start | bytes 1327112 | tf_op jit(solution)/shard_map/ppermute | solution.py:129
  54.5 1.3 %collective-permute-start.23 = (bf16[3,4,144,128]{3,2,1,0:T(8,128)(2,1)S(1)}, bf16[3,4,144,128]{3,2,1,0:T(8,128)(2,1)S(1)}, u32[]{:S(2)}, u32[]{:S(2)}) collective-permute-start(bf16[3,4,144,128]{3,2,1,0:T(8,128)(2,1)S(1)} %pad_maximum_fusion.3), channel_id=1, source_target_pairs={{0,8},{1,9},{10,2},{11,3},{20,28},{21,29},{30,22},{31,23}} | collective-permute-start | bytes 1327112 | tf_op jit(solution)/shard_map/ppermute | solution.py:105
  55.8 3.2 %collective-permute-start.27 = (bf16[3,4,144,128]{3,2,1,0:T(8,128)(2,1)S(1)}, bf16[3,4,144,128]{3,2,1,0:T(8,128)(2,1)S(1)}, u32[]{:S(2)}, u32[]{:S(2)}) collective-permute-start(bf16[3,4,144,128]{3,2,1,0:T(8,128)(2,1)S(1)} %pad_maximum_fusion.4), channel_id=1, source_target_pairs={{0,16},{1,17},{10,26},{11,27},{20,4},{21,5},{30,14},{31,15}} | collective-permute-start | bytes 1327112 | tf_op jit(solution)/shard_map/ppermute | solution.py:105
  61.1 1.4 %collective-permute-start.10 = (bf16[3,2,2,144,128]{4,3,2,1,0:T(8,128)(2,1)S(1)}, bf16[3,2,2,144,128]{4,3,2,1,0:T(8,128)(2,1)S(1)}, u32[]{:S(2)}, u32[]{:S(2)}) collective-permute-start(bf16[3,2,2,144,128]{4,3,2,1,0:T(8,128)(2,1)S(1)} %collective-permute-done.8), channel_id=1, source_target_pairs={{0,2},{2,4},{4,6},{6,7},{7,5},{5,3},{3,1},{1,0},{8,10},{10,12},{12... | collective-permute-start | bytes 1327112 | tf_op jit(solution)/shard_map/ppermute | solution.py:129
  66.2 4.1 %collective-permute-start.30 = (bf16[3,4,144,128]{3,2,1,0:T(8,128)(2,1)}, bf16[3,4,144,128]{3,2,1,0:T(8,128)(2,1)}, u32[]{:S(2)}, u32[]{:S(2)}) collective-permute-start(bf16[3,4,144,128]{3,2,1,0:T(8,128)(2,1)} %pad_maximum_fusion.5), channel_id=1, source_target_pairs={{0,16},{1,17},{10,26},{11,27},{20,4},{21,5},{30,14},{31,15}} | collective-permute-start | bytes 1327112 | tf_op jit(solution)/shard_map/ppermute | solution.py:105
  75.2 2.1 %collective-permute-start.29 = (bf16[3,4,144,128]{3,2,1,0:T(8,128)(2,1)}, bf16[3,4,144,128]{3,2,1,0:T(8,128)(2,1)}, u32[]{:S(2)}, u32[]{:S(2)}) collective-permute-start(bf16[3,4,144,128]{3,2,1,0:T(8,128)(2,1)} %pad_maximum_fusion.5), channel_id=1, source_target_pairs={{0,8},{1,9},{10,2},{11,3},{20,28},{21,29},{30,22},{31,23}} | collective-permute-start | bytes 1327112 | tf_op jit(solution)/shard_map/ppermute | solution.py:105
  77.2 3.4 %collective-permute-start.33 = (bf16[3,4,144,128]{3,2,1,0:T(8,128)(2,1)}, bf16[3,4,144,128]{3,2,1,0:T(8,128)(2,1)}, u32[]{:S(2)}, u32[]{:S(2)}) collective-permute-start(bf16[3,4,144,128]{3,2,1,0:T(8,128)(2,1)} %pad_maximum_fusion.6), channel_id=1, source_target_pairs={{0,16},{1,17},{10,26},{11,27},{20,4},{21,5},{30,14},{31,15}} | collective-permute-start | bytes 1327112 | tf_op jit(solution)/shard_map/ppermute | solution.py:105
  80.9 2.1 %collective-permute-start.32 = (bf16[3,4,144,128]{3,2,1,0:T(8,128)(2,1)}, bf16[3,4,144,128]{3,2,1,0:T(8,128)(2,1)}, u32[]{:S(2)}, u32[]{:S(2)}) collective-permute-start(bf16[3,4,144,128]{3,2,1,0:T(8,128)(2,1)} %pad_maximum_fusion.6), channel_id=1, source_target_pairs={{0,8},{1,9},{10,2},{11,3},{20,28},{21,29},{30,22},{31,23}} | collective-permute-start | bytes 1327112 | tf_op jit(solution)/shard_map/ppermute | solution.py:105
  83.0 1.7 %collective-permute-done.13 = bf16[3,2,2,144,128]{4,3,2,1,0:T(8,128)(2,1)S(1)} collective-permute-done((bf16[3,2,2,144,128]{4,3,2,1,0:T(8,128)(2,1)S(1)}, bf16[3,2,2,144,128]{4,3,2,1,0:T(8,128)(2,1)S(1)}, u32[]{:S(2)}, u32[]{:S(2)}) %collective-permute-start.13) | collective-permute-done | bytes 442400 | tf_op jit(solution)/shard_map/ppermute | solution.py:130
  84.7 1.4 %collective-permute-start.31 = (bf16[3,4,144,128]{3,2,1,0:T(8,128)(2,1)}, bf16[3,4,144,128]{3,2,1,0:T(8,128)(2,1)}, u32[]{:S(2)}, u32[]{:S(2)}) collective-permute-start(bf16[3,4,144,128]{3,2,1,0:T(8,128)(2,1)} %collective-permute-done.30), channel_id=1, source_target_pairs={{16,24},{17,25},{26,18},{27,19},{4,12},{5,13},{14,6},{15,7}} | collective-permute-start | bytes 1327112 | tf_op jit(solution)/shard_map/ppermute | solution.py:105
  87.7 4.7 %collective-permute-start.36 = (bf16[3,4,144,128]{3,2,1,0:T(8,128)(2,1)}, bf16[3,4,144,128]{3,2,1,0:T(8,128)(2,1)}, u32[]{:S(2)}, u32[]{:S(2)}) collective-permute-start(bf16[3,4,144,128]{3,2,1,0:T(8,128)(2,1)} %pad_maximum_fusion.7), channel_id=1, source_target_pairs={{0,16},{1,17},{10,26},{11,27},{20,4},{21,5},{30,14},{31,15}} | collective-permute-start | bytes 1327112 | tf_op jit(solution)/shard_map/ppermute | solution.py:105
  94.1 1.4 %collective-permute-start.34 = (bf16[3,4,144,128]{3,2,1,0:T(8,128)(2,1)}, bf16[3,4,144,128]{3,2,1,0:T(8,128)(2,1)}, u32[]{:S(2)}, u32[]{:S(2)}) collective-permute-start(bf16[3,4,144,128]{3,2,1,0:T(8,128)(2,1)} %collective-permute-done.33), channel_id=1, source_target_pairs={{16,24},{17,25},{26,18},{27,19},{4,12},{5,13},{14,6},{15,7}} | collective-permute-start | bytes 1327112 | tf_op jit(solution)/shard_map/ppermute | solution.py:105
  97.2 1.7 %slice.19 = bf16[96,2,1,1]{3,2,1,0:T(2,128)(2,1)} slice(bf16[96,2,144,128]{3,2,1,0:T(8,128)(2,1)} %bitcast.44), slice={[0:96], [0:2], [131:132], [0:1]} | slice | bytes 768 | tf_op jit(solution)/shard_map/slice | solution.py:150
  100.0 1.3 %collective-permute-start.35 = (bf16[3,4,144,128]{3,2,1,0:T(8,128)(2,1)}, bf16[3,4,144,128]{3,2,1,0:T(8,128)(2,1)S(1)}, u32[]{:S(2)}, u32[]{:S(2)}) collective-permute-start(bf16[3,4,144,128]{3,2,1,0:T(8,128)(2,1)} %pad_maximum_fusion.7), channel_id=1, source_target_pairs={{0,8},{1,9},{10,2},{11,3},{20,28},{21,29},{30,22},{31,23}} | collective-permute-start | bytes 1327112 | tf_op jit(solution)/shard_map/ppermute | solution.py:105
  102.0 1.5 %select_dynamic-update-slice_fusion.2 = bf16[3,32,144,128]{3,2,1,0:T(8,128)(2,1)S(1)} fusion(bf16[3,32,144,128]{3,2,1,0:T(8,128)(2,1)S(1)} %select_dynamic-update-slice_fusion.3, bf16[3,4,144,128]{3,2,1,0:T(8,128)(2,1)} %collective-permute-done.29, bf16[3,4,144,128]{3,2,1,0:T(8,128)(2,1)} %collective-permute-done.30, ...), kind=kLoop, calls=%fused_computation.11 | loop fusion | flops 1548288 | bytes 2211843
  103.5 1.5 %select_dynamic-update-slice_fusion.1 = bf16[3,32,144,128]{3,2,1,0:T(8,128)(2,1)S(1)} fusion(bf16[3,32,144,128]{3,2,1,0:T(8,128)(2,1)S(1)} %select_dynamic-update-slice_fusion.2, bf16[3,4,144,128]{3,2,1,0:T(8,128)(2,1)} %collective-permute-done.32, bf16[3,4,144,128]{3,2,1,0:T(8,128)(2,1)} %collective-permute-done.33, ...), kind=kLoop, calls=%fused_computation.10 | loop fusion | flops 1548288 | bytes 2211843
  105.0 1.3 %select_dynamic-update-slice_fusion = bf16[3,32,144,128]{3,2,1,0:T(8,128)(2,1)S(1)} fusion(bf16[3,32,144,128]{3,2,1,0:T(8,128)(2,1)S(1)} %select_dynamic-update-slice_fusion.1, bf16[3,4,144,128]{3,2,1,0:T(8,128)(2,1)S(1)} %collective-permute-done.35, bf16[3,4,144,128]{3,2,1,0:T(8,128)(2,1)} %collective-permute-done.36, ...), kind=kLoop, calls=%fused_computation.9 | loop fusion | flops 1548288 | bytes 2211843 | tf_op jit(solution)/shard_map/concatenate | solution.py:145
  108.8 11.3 %shard_map.37 = f32[2048,1024]{1,0:T(8,128)} custom-call(s32[288]{0:T(512)S(1)} %min.12.offs_ref, bf16[96,2,144,128]{3,2,1,0:T(8,128)(2,1)} %bitcast.45, bf16[96,144,128]{2,1,0:T(8,128)(2,1)S(1)} %bitcast.43), custom_call_target="tpu_custom_call" | custom-call | flops 805306368 | bytes 17825792 | tf_op jit(solution)/shard_map/pallas_call | solution.py:40
  (131 shorter events, 36.2 us)
Async XLA Ops:
  4.2 13.2 %collective-permute-start = (bf16[3,2,2,144,128]{4,3,2,1,0:T(8,128)(2,1)S(1)}, bf16[3,2,2,144,128]{4,3,2,1,0:T(8,128)(2,1)S(1)}, u32[]{:S(2)}, u32[]{:S(2)}) collective-permute-start(bf16[3,2,2,144,128]{4,3,2,1,0:T(8,128)(2,1)S(1)} %get-tuple-element.5), channel_id=1, source_target_pairs={{0,2},{2,4},{4,6},{6,7},{7,5},{5,3},{3,1},{1,0},{8,10},{10,12},{12... | collective-permute-start | bytes 1327112 | tf_op jit(solution)/shard_map/ppermute | solution.py:129
  7.3 11.9 %collective-permute-start.1 = (bf16[3,2,2,144,128]{4,3,2,1,0:T(8,128)(2,1)S(1)}, bf16[3,2,2,144,128]{4,3,2,1,0:T(8,128)(2,1)S(1)}, u32[]{:S(2)}, u32[]{:S(2)}) collective-permute-start(bf16[3,2,2,144,128]{4,3,2,1,0:T(8,128)(2,1)S(1)} %get-tuple-element.6), channel_id=1, source_target_pairs={{2,0},{4,2},{6,4},{7,6},{5,7},{3,5},{1,3},{0,1},{10,8},{12,10},{14... | collective-permute-start | bytes 1327112 | tf_op jit(solution)/shard_map/ppermute | solution.py:130
  8.1 15.1 %collective-permute-start.15 = (bf16[3,4,144,128]{3,2,1,0:T(8,128)(2,1)S(1)}, bf16[3,4,144,128]{3,2,1,0:T(8,128)(2,1)S(1)}, u32[]{:S(2)}, u32[]{:S(2)}) collective-permute-start(bf16[3,4,144,128]{3,2,1,0:T(8,128)(2,1)S(1)} %pad_maximum_fusion), channel_id=1, source_target_pairs={{0,16},{1,17},{10,26},{11,27},{20,4},{21,5},{30,14},{31,15}} | collective-permute-start | bytes 1327112 | tf_op jit(solution)/shard_map/ppermute | solution.py:105
  12.0 21.9 %collective-permute-start.14 = (bf16[3,4,144,128]{3,2,1,0:T(8,128)(2,1)S(1)}, bf16[3,4,144,128]{3,2,1,0:T(8,128)(2,1)S(1)}, u32[]{:S(2)}, u32[]{:S(2)}) collective-permute-start(bf16[3,4,144,128]{3,2,1,0:T(8,128)(2,1)S(1)} %pad_maximum_fusion), channel_id=1, source_target_pairs={{0,8},{1,9},{10,2},{11,3},{20,28},{21,29},{30,22},{31,23}} | collective-permute-start | bytes 1327112 | tf_op jit(solution)/shard_map/ppermute | solution.py:105
  17.4 13.1 %collective-permute-start.2 = (bf16[3,2,2,144,128]{4,3,2,1,0:T(8,128)(2,1)S(1)}, bf16[3,2,2,144,128]{4,3,2,1,0:T(8,128)(2,1)S(1)}, u32[]{:S(2)}, u32[]{:S(2)}) collective-permute-start(bf16[3,2,2,144,128]{4,3,2,1,0:T(8,128)(2,1)S(1)} %collective-permute-done), channel_id=1, source_target_pairs={{0,2},{2,4},{4,6},{6,7},{7,5},{5,3},{3,1},{1,0},{8,10},{10,12},{12... | collective-permute-start | bytes 1327112 | tf_op jit(solution)/shard_map/ppermute | solution.py:129
  19.2 10.8 %collective-permute-start.3 = (bf16[3,2,2,144,128]{4,3,2,1,0:T(8,128)(2,1)S(1)}, bf16[3,2,2,144,128]{4,3,2,1,0:T(8,128)(2,1)S(1)}, u32[]{:S(2)}, u32[]{:S(2)}) collective-permute-start(bf16[3,2,2,144,128]{4,3,2,1,0:T(8,128)(2,1)S(1)} %collective-permute-done.1), channel_id=1, source_target_pairs={{2,0},{4,2},{6,4},{7,6},{5,7},{3,5},{1,3},{0,1},{10,8},{12,10},{14... | collective-permute-start | bytes 1327112 | tf_op jit(solution)/shard_map/ppermute | solution.py:130
  19.5 15.6 %collective-permute-start.18 = (bf16[3,4,144,128]{3,2,1,0:T(8,128)(2,1)S(1)}, bf16[3,4,144,128]{3,2,1,0:T(8,128)(2,1)S(1)}, u32[]{:S(2)}, u32[]{:S(2)}) collective-permute-start(bf16[3,4,144,128]{3,2,1,0:T(8,128)(2,1)S(1)} %pad_maximum_fusion.1), channel_id=1, source_target_pairs={{0,16},{1,17},{10,26},{11,27},{20,4},{21,5},{30,14},{31,15}} | collective-permute-start | bytes 1327112 | tf_op jit(solution)/shard_map/ppermute | solution.py:105
  23.2 14.8 %collective-permute-start.16 = (bf16[3,4,144,128]{3,2,1,0:T(8,128)(2,1)S(1)}, bf16[3,4,144,128]{3,2,1,0:T(8,128)(2,1)S(1)}, u32[]{:S(2)}, u32[]{:S(2)}) collective-permute-start(bf16[3,4,144,128]{3,2,1,0:T(8,128)(2,1)S(1)} %collective-permute-done.15), channel_id=1, source_target_pairs={{16,24},{17,25},{26,18},{27,19},{4,12},{5,13},{14,6},{15,7}} | collective-permute-start | bytes 1327112 | tf_op jit(solution)/shard_map/ppermute | solution.py:105
  29.9 9.8 %collective-permute-start.5 = (bf16[3,2,2,144,128]{4,3,2,1,0:T(8,128)(2,1)S(1)}, bf16[3,2,2,144,128]{4,3,2,1,0:T(8,128)(2,1)S(1)}, u32[]{:S(2)}, u32[]{:S(2)}) collective-permute-start(bf16[3,2,2,144,128]{4,3,2,1,0:T(8,128)(2,1)S(1)} %collective-permute-done.3), channel_id=1, source_target_pairs={{2,0},{4,2},{6,4},{7,6},{5,7},{3,5},{1,3},{0,1},{10,8},{12,10},{14... | collective-permute-start | bytes 1327112 | tf_op jit(solution)/shard_map/ppermute | solution.py:130
  30.5 10.3 %collective-permute-start.4 = (bf16[3,2,2,144,128]{4,3,2,1,0:T(8,128)(2,1)S(1)}, bf16[3,2,2,144,128]{4,3,2,1,0:T(8,128)(2,1)S(1)}, u32[]{:S(2)}, u32[]{:S(2)}) collective-permute-start(bf16[3,2,2,144,128]{4,3,2,1,0:T(8,128)(2,1)S(1)} %collective-permute-done.2), channel_id=1, source_target_pairs={{0,2},{2,4},{4,6},{6,7},{7,5},{5,3},{3,1},{1,0},{8,10},{10,12},{12... | collective-permute-start | bytes 1327112 | tf_op jit(solution)/shard_map/ppermute | solution.py:129
  33.8 9.9 %collective-permute-start.17 = (bf16[3,4,144,128]{3,2,1,0:T(8,128)(2,1)S(1)}, bf16[3,4,144,128]{3,2,1,0:T(8,128)(2,1)S(1)}, u32[]{:S(2)}, u32[]{:S(2)}) collective-permute-start(bf16[3,4,144,128]{3,2,1,0:T(8,128)(2,1)S(1)} %pad_maximum_fusion.1), channel_id=1, source_target_pairs={{0,8},{1,9},{10,2},{11,3},{20,28},{21,29},{30,22},{31,23}} | collective-permute-start | bytes 1327112 | tf_op jit(solution)/shard_map/ppermute | solution.py:105
  35.1 9.9 %collective-permute-start.21 = (bf16[3,4,144,128]{3,2,1,0:T(8,128)(2,1)S(1)}, bf16[3,4,144,128]{3,2,1,0:T(8,128)(2,1)S(1)}, u32[]{:S(2)}, u32[]{:S(2)}) collective-permute-start(bf16[3,4,144,128]{3,2,1,0:T(8,128)(2,1)S(1)} %pad_maximum_fusion.2), channel_id=1, source_target_pairs={{0,16},{1,17},{10,26},{11,27},{20,4},{21,5},{30,14},{31,15}} | collective-permute-start | bytes 1327112 | tf_op jit(solution)/shard_map/ppermute | solution.py:105
  38.0 10.2 %collective-permute-start.19 = (bf16[3,4,144,128]{3,2,1,0:T(8,128)(2,1)S(1)}, bf16[3,4,144,128]{3,2,1,0:T(8,128)(2,1)S(1)}, u32[]{:S(2)}, u32[]{:S(2)}) collective-permute-start(bf16[3,4,144,128]{3,2,1,0:T(8,128)(2,1)S(1)} %collective-permute-done.18), channel_id=1, source_target_pairs={{16,24},{17,25},{26,18},{27,19},{4,12},{5,13},{14,6},{15,7}} | collective-permute-start | bytes 1327112 | tf_op jit(solution)/shard_map/ppermute | solution.py:105
  39.8 10.8 %collective-permute-start.7 = (bf16[3,2,2,144,128]{4,3,2,1,0:T(8,128)(2,1)S(1)}, bf16[3,2,2,144,128]{4,3,2,1,0:T(8,128)(2,1)S(1)}, u32[]{:S(2)}, u32[]{:S(2)}) collective-permute-start(bf16[3,2,2,144,128]{4,3,2,1,0:T(8,128)(2,1)S(1)} %collective-permute-done.5), channel_id=1, source_target_pairs={{2,0},{4,2},{6,4},{7,6},{5,7},{3,5},{1,3},{0,1},{10,8},{12,10},{14... | collective-permute-start | bytes 1327112 | tf_op jit(solution)/shard_map/ppermute | solution.py:130
  40.8 9.9 %collective-permute-start.6 = (bf16[3,2,2,144,128]{4,3,2,1,0:T(8,128)(2,1)S(1)}, bf16[3,2,2,144,128]{4,3,2,1,0:T(8,128)(2,1)S(1)}, u32[]{:S(2)}, u32[]{:S(2)}) collective-permute-start(bf16[3,2,2,144,128]{4,3,2,1,0:T(8,128)(2,1)S(1)} %collective-permute-done.4), channel_id=1, source_target_pairs={{0,2},{2,4},{4,6},{6,7},{7,5},{5,3},{3,1},{1,0},{8,10},{10,12},{12... | collective-permute-start | bytes 1327112 | tf_op jit(solution)/shard_map/ppermute | solution.py:129
  43.7 10.8 %collective-permute-start.20 = (bf16[3,4,144,128]{3,2,1,0:T(8,128)(2,1)S(1)}, bf16[3,4,144,128]{3,2,1,0:T(8,128)(2,1)S(1)}, u32[]{:S(2)}, u32[]{:S(2)}) collective-permute-start(bf16[3,4,144,128]{3,2,1,0:T(8,128)(2,1)S(1)} %pad_maximum_fusion.2), channel_id=1, source_target_pairs={{0,8},{1,9},{10,2},{11,3},{20,28},{21,29},{30,22},{31,23}} | collective-permute-start | bytes 1327112 | tf_op jit(solution)/shard_map/ppermute | solution.py:105
  45.0 14.0 %collective-permute-start.24 = (bf16[3,4,144,128]{3,2,1,0:T(8,128)(2,1)S(1)}, bf16[3,4,144,128]{3,2,1,0:T(8,128)(2,1)S(1)}, u32[]{:S(2)}, u32[]{:S(2)}) collective-permute-start(bf16[3,4,144,128]{3,2,1,0:T(8,128)(2,1)S(1)} %pad_maximum_fusion.3), channel_id=1, source_target_pairs={{0,16},{1,17},{10,26},{11,27},{20,4},{21,5},{30,14},{31,15}} | collective-permute-start | bytes 1327112 | tf_op jit(solution)/shard_map/ppermute | solution.py:105
  50.6 11.9 %collective-permute-start.9 = (bf16[3,2,2,144,128]{4,3,2,1,0:T(8,128)(2,1)S(1)}, bf16[3,2,2,144,128]{4,3,2,1,0:T(8,128)(2,1)S(1)}, u32[]{:S(2)}, u32[]{:S(2)}) collective-permute-start(bf16[3,2,2,144,128]{4,3,2,1,0:T(8,128)(2,1)S(1)} %collective-permute-done.7), channel_id=1, source_target_pairs={{2,0},{4,2},{6,4},{7,6},{5,7},{3,5},{1,3},{0,1},{10,8},{12,10},{14... | collective-permute-start | bytes 1327112 | tf_op jit(solution)/shard_map/ppermute | solution.py:130
  50.8 10.3 %collective-permute-start.8 = (bf16[3,2,2,144,128]{4,3,2,1,0:T(8,128)(2,1)S(1)}, bf16[3,2,2,144,128]{4,3,2,1,0:T(8,128)(2,1)S(1)}, u32[]{:S(2)}, u32[]{:S(2)}) collective-permute-start(bf16[3,2,2,144,128]{4,3,2,1,0:T(8,128)(2,1)S(1)} %collective-permute-done.6), channel_id=1, source_target_pairs={{0,2},{2,4},{4,6},{6,7},{7,5},{5,3},{3,1},{1,0},{8,10},{10,12},{12... | collective-permute-start | bytes 1327112 | tf_op jit(solution)/shard_map/ppermute | solution.py:129
  54.5 10.5 %collective-permute-start.23 = (bf16[3,4,144,128]{3,2,1,0:T(8,128)(2,1)S(1)}, bf16[3,4,144,128]{3,2,1,0:T(8,128)(2,1)S(1)}, u32[]{:S(2)}, u32[]{:S(2)}) collective-permute-start(bf16[3,4,144,128]{3,2,1,0:T(8,128)(2,1)S(1)} %pad_maximum_fusion.3), channel_id=1, source_target_pairs={{0,8},{1,9},{10,2},{11,3},{20,28},{21,29},{30,22},{31,23}} | collective-permute-start | bytes 1327112 | tf_op jit(solution)/shard_map/ppermute | solution.py:105
  55.8 14.5 %collective-permute-start.27 = (bf16[3,4,144,128]{3,2,1,0:T(8,128)(2,1)S(1)}, bf16[3,4,144,128]{3,2,1,0:T(8,128)(2,1)S(1)}, u32[]{:S(2)}, u32[]{:S(2)}) collective-permute-start(bf16[3,4,144,128]{3,2,1,0:T(8,128)(2,1)S(1)} %pad_maximum_fusion.4), channel_id=1, source_target_pairs={{0,16},{1,17},{10,26},{11,27},{20,4},{21,5},{30,14},{31,15}} | collective-permute-start | bytes 1327112 | tf_op jit(solution)/shard_map/ppermute | solution.py:105
  61.1 11.0 %collective-permute-start.10 = (bf16[3,2,2,144,128]{4,3,2,1,0:T(8,128)(2,1)S(1)}, bf16[3,2,2,144,128]{4,3,2,1,0:T(8,128)(2,1)S(1)}, u32[]{:S(2)}, u32[]{:S(2)}) collective-permute-start(bf16[3,2,2,144,128]{4,3,2,1,0:T(8,128)(2,1)S(1)} %collective-permute-done.8), channel_id=1, source_target_pairs={{0,2},{2,4},{4,6},{6,7},{7,5},{5,3},{3,1},{1,0},{8,10},{10,12},{12... | collective-permute-start | bytes 1327112 | tf_op jit(solution)/shard_map/ppermute | solution.py:129
  62.5 10.6 %collective-permute-start.11 = (bf16[3,2,2,144,128]{4,3,2,1,0:T(8,128)(2,1)S(1)}, bf16[3,2,2,144,128]{4,3,2,1,0:T(8,128)(2,1)S(1)}, u32[]{:S(2)}, u32[]{:S(2)}) collective-permute-start(bf16[3,2,2,144,128]{4,3,2,1,0:T(8,128)(2,1)S(1)} %collective-permute-done.9), channel_id=1, source_target_pairs={{2,0},{4,2},{6,4},{7,6},{5,7},{3,5},{1,3},{0,1},{10,8},{12,10},{14... | collective-permute-start | bytes 1327112 | tf_op jit(solution)/shard_map/ppermute | solution.py:130
  64.9 10.2 %collective-permute-start.26 = (bf16[3,4,144,128]{3,2,1,0:T(8,128)(2,1)S(1)}, bf16[3,4,144,128]{3,2,1,0:T(8,128)(2,1)S(1)}, u32[]{:S(2)}, u32[]{:S(2)}) collective-permute-start(bf16[3,4,144,128]{3,2,1,0:T(8,128)(2,1)S(1)} %pad_maximum_fusion.4), channel_id=1, source_target_pairs={{0,8},{1,9},{10,2},{11,3},{20,28},{21,29},{30,22},{31,23}} | collective-permute-start | bytes 1327112 | tf_op jit(solution)/shard_map/ppermute | solution.py:105
  66.2 14.7 %collective-permute-start.30 = (bf16[3,4,144,128]{3,2,1,0:T(8,128)(2,1)}, bf16[3,4,144,128]{3,2,1,0:T(8,128)(2,1)}, u32[]{:S(2)}, u32[]{:S(2)}) collective-permute-start(bf16[3,4,144,128]{3,2,1,0:T(8,128)(2,1)} %pad_maximum_fusion.5), channel_id=1, source_target_pairs={{0,16},{1,17},{10,26},{11,27},{20,4},{21,5},{30,14},{31,15}} | collective-permute-start | bytes 1327112 | tf_op jit(solution)/shard_map/ppermute | solution.py:105
  72.2 14.1 %collective-permute-start.12 = (bf16[3,2,2,144,128]{4,3,2,1,0:T(8,128)(2,1)S(1)}, bf16[3,2,2,144,128]{4,3,2,1,0:T(8,128)(2,1)S(1)}, u32[]{:S(2)}, u32[]{:S(2)}) collective-permute-start(bf16[3,2,2,144,128]{4,3,2,1,0:T(8,128)(2,1)S(1)} %collective-permute-done.10), channel_id=1, source_target_pairs={{0,2},{2,4},{4,6},{6,7},{7,5},{5,3},{3,1},{1,0},{8,10},{10,12},{12... | collective-permute-start | bytes 1327112 | tf_op jit(solution)/shard_map/ppermute | solution.py:129
  73.1 11.6 %collective-permute-start.13 = (bf16[3,2,2,144,128]{4,3,2,1,0:T(8,128)(2,1)S(1)}, bf16[3,2,2,144,128]{4,3,2,1,0:T(8,128)(2,1)S(1)}, u32[]{:S(2)}, u32[]{:S(2)}) collective-permute-start(bf16[3,2,2,144,128]{4,3,2,1,0:T(8,128)(2,1)S(1)} %collective-permute-done.11), channel_id=1, source_target_pairs={{2,0},{4,2},{6,4},{7,6},{5,7},{3,5},{1,3},{0,1},{10,8},{12,10},{14... | collective-permute-start | bytes 1327112 | tf_op jit(solution)/shard_map/ppermute | solution.py:130
  75.2 24.8 %collective-permute-start.29 = (bf16[3,4,144,128]{3,2,1,0:T(8,128)(2,1)}, bf16[3,4,144,128]{3,2,1,0:T(8,128)(2,1)}, u32[]{:S(2)}, u32[]{:S(2)}) collective-permute-start(bf16[3,4,144,128]{3,2,1,0:T(8,128)(2,1)} %pad_maximum_fusion.5), channel_id=1, source_target_pairs={{0,8},{1,9},{10,2},{11,3},{20,28},{21,29},{30,22},{31,23}} | collective-permute-start | bytes 1327112 | tf_op jit(solution)/shard_map/ppermute | solution.py:105
  77.2 16.8 %collective-permute-start.33 = (bf16[3,4,144,128]{3,2,1,0:T(8,128)(2,1)}, bf16[3,4,144,128]{3,2,1,0:T(8,128)(2,1)}, u32[]{:S(2)}, u32[]{:S(2)}) collective-permute-start(bf16[3,4,144,128]{3,2,1,0:T(8,128)(2,1)} %pad_maximum_fusion.6), channel_id=1, source_target_pairs={{0,16},{1,17},{10,26},{11,27},{20,4},{21,5},{30,14},{31,15}} | collective-permute-start | bytes 1327112 | tf_op jit(solution)/shard_map/ppermute | solution.py:105
  80.9 22.5 %collective-permute-start.32 = (bf16[3,4,144,128]{3,2,1,0:T(8,128)(2,1)}, bf16[3,4,144,128]{3,2,1,0:T(8,128)(2,1)}, u32[]{:S(2)}, u32[]{:S(2)}) collective-permute-start(bf16[3,4,144,128]{3,2,1,0:T(8,128)(2,1)} %pad_maximum_fusion.6), channel_id=1, source_target_pairs={{0,8},{1,9},{10,2},{11,3},{20,28},{21,29},{30,22},{31,23}} | collective-permute-start | bytes 1327112 | tf_op jit(solution)/shard_map/ppermute | solution.py:105
  84.7 17.2 %collective-permute-start.31 = (bf16[3,4,144,128]{3,2,1,0:T(8,128)(2,1)}, bf16[3,4,144,128]{3,2,1,0:T(8,128)(2,1)}, u32[]{:S(2)}, u32[]{:S(2)}) collective-permute-start(bf16[3,4,144,128]{3,2,1,0:T(8,128)(2,1)} %collective-permute-done.30), channel_id=1, source_target_pairs={{16,24},{17,25},{26,18},{27,19},{4,12},{5,13},{14,6},{15,7}} | collective-permute-start | bytes 1327112 | tf_op jit(solution)/shard_map/ppermute | solution.py:105
  87.7 13.6 %collective-permute-start.36 = (bf16[3,4,144,128]{3,2,1,0:T(8,128)(2,1)}, bf16[3,4,144,128]{3,2,1,0:T(8,128)(2,1)}, u32[]{:S(2)}, u32[]{:S(2)}) collective-permute-start(bf16[3,4,144,128]{3,2,1,0:T(8,128)(2,1)} %pad_maximum_fusion.7), channel_id=1, source_target_pairs={{0,16},{1,17},{10,26},{11,27},{20,4},{21,5},{30,14},{31,15}} | collective-permute-start | bytes 1327112 | tf_op jit(solution)/shard_map/ppermute | solution.py:105
  (18 other events, 132.7 us)

commit v29 on v28

--- a/solution.py
+++ b/solution.py
@@ -8,7 +8,7 @@
 from jax.sharding import PartitionSpec as P
 
 IBS = 8
-CHUNK = 24
+CHUNK = 32
 META = 16
 
 

time: 121 us -> 120 us (level)
  no operation moved by 1% of the time
where the time goes in v29:
time: 120 us
  starting transfers between devices  63 us (52%)
  local copies, waits for them, and re-layouts  19.2 us (16%)
  waiting for transfers between devices  13.7 us (11%)
  other arithmetic  12.2 us (10%)
  Pallas kernels  10.8 us (9%)
    ppermute x24, starting transfers between devices, send(): lax.ppermute(v, ('row', 'col'), [(a * ncol + cc, b * ncol + cc) for a, b,...  47.8 us
    unnamed x37, local copies, waits for them, and re-layouts  12.5 us
    ppermute x7, starting transfers between devices, local(): a = lax.ppermute(a, 'col', forward)  11.6 us
    pallas_call x1, Pallas kernels, gram_call(): pl.pallas_call(kernel, grid_spec=pltpu.PrefetchScalarGridSpec(num_scalar_...  10.8 us
    ppermute x7, waiting for transfers between devices, local(): b = lax.ppermute(b, 'col', backward)  8.34 us
    unnamed x8, other arithmetic  6.64 us
    ppermute x7, waiting for transfers between devices, local(): a = lax.ppermute(a, 'col', forward)  5.35 us
    ppermute x7, starting transfers between devices, local(): b = lax.ppermute(b, 'col', backward)  3.59 us
  transfers between devices with their start and end apart: 38, of which 7 were waited for; matrix products, arithmetic and copies ran while one was open for 18% of the time, Pallas kernels for 0%

profile of v29, /device:TPU:0, one launch (start us, length us, event | category | flops | bytes accessed | tf_op | source)
XLA Modules:
  0.0 119.6 jit_solution(15812897863314561849)
XLA Ops:
  1.7 2.4 %constant_dynamic-update-slice_fusion.14 = (bf16[3,32,2,144,128]{4,3,2,1,0:T(8,128)(2,1)}, bf16[3,4,2,144,128]{4,3,2,1,0:T(8,128)(2,1)S(1)}) fusion(bf16[144]{0:T(256)(128)(2,1)S(1)} %pad.21.clone, bf16[3,4,2,1,128]{4,3,2,1,0:T(2,128)(2,1)S(1)} %broadcast_in_dim.7, bf16[3,4,2,3,128]{4,3,2,1,0:T(4,128)(2,1)S(1)} %broadcast_in_dim.6, ...), kind=kLoop, calls=%fused_computation.48 | loop fusion | flops 3538943 | bytes 2580768
  4.2 3.1 %collective-permute-start = (bf16[3,2,2,144,128]{4,3,2,1,0:T(8,128)(2,1)S(1)}, bf16[3,2,2,144,128]{4,3,2,1,0:T(8,128)(2,1)S(1)}, u32[]{:S(2)}, u32[]{:S(2)}) collective-permute-start(bf16[3,2,2,144,128]{4,3,2,1,0:T(8,128)(2,1)S(1)} %get-tuple-element.5), channel_id=1, source_target_pairs={{0,2},{2,4},{4,6},{6,7},{7,5},{5,3},{3,1},{1,0},{8,10},{10,12},{12... | collective-permute-start | bytes 1327112 | tf_op jit(solution)/shard_map/ppermute | solution.py:129
  8.1 3.9 %collective-permute-start.15 = (bf16[3,4,144,128]{3,2,1,0:T(8,128)(2,1)S(1)}, bf16[3,4,144,128]{3,2,1,0:T(8,128)(2,1)S(1)}, u32[]{:S(2)}, u32[]{:S(2)}) collective-permute-start(bf16[3,4,144,128]{3,2,1,0:T(8,128)(2,1)S(1)} %pad_maximum_fusion), channel_id=1, source_target_pairs={{0,16},{1,17},{10,26},{11,27},{20,4},{21,5},{30,14},{31,15}} | collective-permute-start | bytes 1327112 | tf_op jit(solution)/shard_map/ppermute | solution.py:105
  12.0 1.3 %collective-permute-start.14 = (bf16[3,4,144,128]{3,2,1,0:T(8,128)(2,1)S(1)}, bf16[3,4,144,128]{3,2,1,0:T(8,128)(2,1)S(1)}, u32[]{:S(2)}, u32[]{:S(2)}) collective-permute-start(bf16[3,4,144,128]{3,2,1,0:T(8,128)(2,1)S(1)} %pad_maximum_fusion), channel_id=1, source_target_pairs={{0,8},{1,9},{10,2},{11,3},{20,28},{21,29},{30,22},{31,23}} | collective-permute-start | bytes 1327112 | tf_op jit(solution)/shard_map/ppermute | solution.py:105
  13.4 4.0 %collective-permute-done = bf16[3,2,2,144,128]{4,3,2,1,0:T(8,128)(2,1)S(1)} collective-permute-done((bf16[3,2,2,144,128]{4,3,2,1,0:T(8,128)(2,1)S(1)}, bf16[3,2,2,144,128]{4,3,2,1,0:T(8,128)(2,1)S(1)}, u32[]{:S(2)}, u32[]{:S(2)}) %collective-permute-start) | collective-permute-done | bytes 442400 | tf_op jit(solution)/shard_map/ppermute | solution.py:129
  17.4 1.8 %collective-permute-start.2 = (bf16[3,2,2,144,128]{4,3,2,1,0:T(8,128)(2,1)S(1)}, bf16[3,2,2,144,128]{4,3,2,1,0:T(8,128)(2,1)S(1)}, u32[]{:S(2)}, u32[]{:S(2)}) collective-permute-start(bf16[3,2,2,144,128]{4,3,2,1,0:T(8,128)(2,1)S(1)} %collective-permute-done), channel_id=1, source_target_pairs={{0,2},{2,4},{4,6},{6,7},{7,5},{5,3},{3,1},{1,0},{8,10},{10,12},{12... | collective-permute-start | bytes 1327112 | tf_op jit(solution)/shard_map/ppermute | solution.py:129
  19.5 3.6 %collective-permute-start.18 = (bf16[3,4,144,128]{3,2,1,0:T(8,128)(2,1)S(1)}, bf16[3,4,144,128]{3,2,1,0:T(8,128)(2,1)S(1)}, u32[]{:S(2)}, u32[]{:S(2)}) collective-permute-start(bf16[3,4,144,128]{3,2,1,0:T(8,128)(2,1)S(1)} %pad_maximum_fusion.1), channel_id=1, source_target_pairs={{0,16},{1,17},{10,26},{11,27},{20,4},{21,5},{30,14},{31,15}} | collective-permute-start | bytes 1327112 | tf_op jit(solution)/shard_map/ppermute | solution.py:105
  25.6 4.3 %collective-permute-done.3 = bf16[3,2,2,144,128]{4,3,2,1,0:T(8,128)(2,1)S(1)} collective-permute-done((bf16[3,2,2,144,128]{4,3,2,1,0:T(8,128)(2,1)S(1)}, bf16[3,2,2,144,128]{4,3,2,1,0:T(8,128)(2,1)S(1)}, u32[]{:S(2)}, u32[]{:S(2)}) %collective-permute-start.3) | collective-permute-done | bytes 442400 | tf_op jit(solution)/shard_map/ppermute | solution.py:130
  30.5 1.5 %collective-permute-start.4 = (bf16[3,2,2,144,128]{4,3,2,1,0:T(8,128)(2,1)S(1)}, bf16[3,2,2,144,128]{4,3,2,1,0:T(8,128)(2,1)S(1)}, u32[]{:S(2)}, u32[]{:S(2)}) collective-permute-start(bf16[3,2,2,144,128]{4,3,2,1,0:T(8,128)(2,1)S(1)} %collective-permute-done.2), channel_id=1, source_target_pairs={{0,2},{2,4},{4,6},{6,7},{7,5},{5,3},{3,1},{1,0},{8,10},{10,12},{12... | collective-permute-start | bytes 1327112 | tf_op jit(solution)/shard_map/ppermute | solution.py:129
  33.8 1.3 %collective-permute-start.17 = (bf16[3,4,144,128]{3,2,1,0:T(8,128)(2,1)S(1)}, bf16[3,4,144,128]{3,2,1,0:T(8,128)(2,1)S(1)}, u32[]{:S(2)}, u32[]{:S(2)}) collective-permute-start(bf16[3,4,144,128]{3,2,1,0:T(8,128)(2,1)S(1)} %pad_maximum_fusion.1), channel_id=1, source_target_pairs={{0,8},{1,9},{10,2},{11,3},{20,28},{21,29},{30,22},{31,23}} | collective-permute-start | bytes 1327112 | tf_op jit(solution)/shard_map/ppermute | solution.py:105
  35.1 2.8 %collective-permute-start.21 = (bf16[3,4,144,128]{3,2,1,0:T(8,128)(2,1)S(1)}, bf16[3,4,144,128]{3,2,1,0:T(8,128)(2,1)S(1)}, u32[]{:S(2)}, u32[]{:S(2)}) collective-permute-start(bf16[3,4,144,128]{3,2,1,0:T(8,128)(2,1)S(1)} %pad_maximum_fusion.2), channel_id=1, source_target_pairs={{0,16},{1,17},{10,26},{11,27},{20,4},{21,5},{30,14},{31,15}} | collective-permute-start | bytes 1327112 | tf_op jit(solution)/shard_map/ppermute | solution.py:105
  43.7 1.3 %collective-permute-start.20 = (bf16[3,4,144,128]{3,2,1,0:T(8,128)(2,1)S(1)}, bf16[3,4,144,128]{3,2,1,0:T(8,128)(2,1)S(1)}, u32[]{:S(2)}, u32[]{:S(2)}) collective-permute-start(bf16[3,4,144,128]{3,2,1,0:T(8,128)(2,1)S(1)} %pad_maximum_fusion.2), channel_id=1, source_target_pairs={{0,8},{1,9},{10,2},{11,3},{20,28},{21,29},{30,22},{31,23}} | collective-permute-start | bytes 1327112 | tf_op jit(solution)/shard_map/ppermute | solution.py:105
  45.0 3.1 %collective-permute-start.24 = (bf16[3,4,144,128]{3,2,1,0:T(8,128)(2,1)S(1)}, bf16[3,4,144,128]{3,2,1,0:T(8,128)(2,1)S(1)}, u32[]{:S(2)}, u32[]{:S(2)}) collective-permute-start(bf16[3,4,144,128]{3,2,1,0:T(8,128)(2,1)S(1)} %pad_maximum_fusion.3), channel_id=1, source_target_pairs={{0,16},{1,17},{10,26},{11,27},{20,4},{21,5},{30,14},{31,15}} | collective-permute-start | bytes 1327112 | tf_op jit(solution)/shard_map/ppermute | solution.py:105
  49.1 1.5 %collective-permute-done.7 = bf16[3,2,2,144,128]{4,3,2,1,0:T(8,128)(2,1)S(1)} collective-permute-done((bf16[3,2,2,144,128]{4,3,2,1,0:T(8,128)(2,1)S(1)}, bf16[3,2,2,144,128]{4,3,2,1,0:T(8,128)(2,1)S(1)}, u32[]{:S(2)}, u32[]{:S(2)}) %collective-permute-start.7) | collective-permute-done | bytes 442400 | tf_op jit(solution)/shard_map/ppermute | solution.py:130
  50.8 1.9 %collective-permute-start.8 = (bf16[3,2,2,144,128]{4,3,2,1,0:T(8,128)(2,1)S(1)}, bf16[3,2,2,144,128]{4,3,2,1,0:T(8,128)(2,1)S(1)}, u32[]{:S(2)}, u32[]{:S(2)}) collective-permute-start(bf16[3,2,2,144,128]{4,3,2,1,0:T(8,128)(2,1)S(1)} %collective-permute-done.6), channel_id=1, source_target_pairs={{0,2},{2,4},{4,6},{6,7},{7,5},{5,3},{3,1},{1,0},{8,10},{10,12},{12... | collective-permute-start | bytes 1327112 | tf_op jit(solution)/shard_map/ppermute | solution.py:129
  54.5 1.3 %collective-permute-start.23 = (bf16[3,4,144,128]{3,2,1,0:T(8,128)(2,1)S(1)}, bf16[3,4,144,128]{3,2,1,0:T(8,128)(2,1)S(1)}, u32[]{:S(2)}, u32[]{:S(2)}) collective-permute-start(bf16[3,4,144,128]{3,2,1,0:T(8,128)(2,1)S(1)} %pad_maximum_fusion.3), channel_id=1, source_target_pairs={{0,8},{1,9},{10,2},{11,3},{20,28},{21,29},{30,22},{31,23}} | collective-permute-start | bytes 1327112 | tf_op jit(solution)/shard_map/ppermute | solution.py:105
  55.8 3.2 %collective-permute-start.27 = (bf16[3,4,144,128]{3,2,1,0:T(8,128)(2,1)S(1)}, bf16[3,4,144,128]{3,2,1,0:T(8,128)(2,1)S(1)}, u32[]{:S(2)}, u32[]{:S(2)}) collective-permute-start(bf16[3,4,144,128]{3,2,1,0:T(8,128)(2,1)S(1)} %pad_maximum_fusion.4), channel_id=1, source_target_pairs={{0,16},{1,17},{10,26},{11,27},{20,4},{21,5},{30,14},{31,15}} | collective-permute-start | bytes 1327112 | tf_op jit(solution)/shard_map/ppermute | solution.py:105
  61.1 1.4 %collective-permute-start.10 = (bf16[3,2,2,144,128]{4,3,2,1,0:T(8,128)(2,1)S(1)}, bf16[3,2,2,144,128]{4,3,2,1,0:T(8,128)(2,1)S(1)}, u32[]{:S(2)}, u32[]{:S(2)}) collective-permute-start(bf16[3,2,2,144,128]{4,3,2,1,0:T(8,128)(2,1)S(1)} %collective-permute-done.8), channel_id=1, source_target_pairs={{0,2},{2,4},{4,6},{6,7},{7,5},{5,3},{3,1},{1,0},{8,10},{10,12},{12... | collective-permute-start | bytes 1327112 | tf_op jit(solution)/shard_map/ppermute | solution.py:129
  66.2 4.1 %collective-permute-start.30 = (bf16[3,4,144,128]{3,2,1,0:T(8,128)(2,1)}, bf16[3,4,144,128]{3,2,1,0:T(8,128)(2,1)}, u32[]{:S(2)}, u32[]{:S(2)}) collective-permute-start(bf16[3,4,144,128]{3,2,1,0:T(8,128)(2,1)} %pad_maximum_fusion.5), channel_id=1, source_target_pairs={{0,16},{1,17},{10,26},{11,27},{20,4},{21,5},{30,14},{31,15}} | collective-permute-start | bytes 1327112 | tf_op jit(solution)/shard_map/ppermute | solution.py:105
  75.2 2.1 %collective-permute-start.29 = (bf16[3,4,144,128]{3,2,1,0:T(8,128)(2,1)}, bf16[3,4,144,128]{3,2,1,0:T(8,128)(2,1)}, u32[]{:S(2)}, u32[]{:S(2)}) collective-permute-start(bf16[3,4,144,128]{3,2,1,0:T(8,128)(2,1)} %pad_maximum_fusion.5), channel_id=1, source_target_pairs={{0,8},{1,9},{10,2},{11,3},{20,28},{21,29},{30,22},{31,23}} | collective-permute-start | bytes 1327112 | tf_op jit(solution)/shard_map/ppermute | solution.py:105
  77.2 3.4 %collective-permute-start.33 = (bf16[3,4,144,128]{3,2,1,0:T(8,128)(2,1)}, bf16[3,4,144,128]{3,2,1,0:T(8,128)(2,1)}, u32[]{:S(2)}, u32[]{:S(2)}) collective-permute-start(bf16[3,4,144,128]{3,2,1,0:T(8,128)(2,1)} %pad_maximum_fusion.6), channel_id=1, source_target_pairs={{0,16},{1,17},{10,26},{11,27},{20,4},{21,5},{30,14},{31,15}} | collective-permute-start | bytes 1327112 | tf_op jit(solution)/shard_map/ppermute | solution.py:105
  80.9 2.1 %collective-permute-start.32 = (bf16[3,4,144,128]{3,2,1,0:T(8,128)(2,1)}, bf16[3,4,144,128]{3,2,1,0:T(8,128)(2,1)}, u32[]{:S(2)}, u32[]{:S(2)}) collective-permute-start(bf16[3,4,144,128]{3,2,1,0:T(8,128)(2,1)} %pad_maximum_fusion.6), channel_id=1, source_target_pairs={{0,8},{1,9},{10,2},{11,3},{20,28},{21,29},{30,22},{31,23}} | collective-permute-start | bytes 1327112 | tf_op jit(solution)/shard_map/ppermute | solution.py:105
  83.0 1.7 %collective-permute-done.13 = bf16[3,2,2,144,128]{4,3,2,1,0:T(8,128)(2,1)S(1)} collective-permute-done((bf16[3,2,2,144,128]{4,3,2,1,0:T(8,128)(2,1)S(1)}, bf16[3,2,2,144,128]{4,3,2,1,0:T(8,128)(2,1)S(1)}, u32[]{:S(2)}, u32[]{:S(2)}) %collective-permute-start.13) | collective-permute-done | bytes 442400 | tf_op jit(solution)/shard_map/ppermute | solution.py:130
  84.7 1.4 %collective-permute-start.31 = (bf16[3,4,144,128]{3,2,1,0:T(8,128)(2,1)}, bf16[3,4,144,128]{3,2,1,0:T(8,128)(2,1)}, u32[]{:S(2)}, u32[]{:S(2)}) collective-permute-start(bf16[3,4,144,128]{3,2,1,0:T(8,128)(2,1)} %collective-permute-done.30), channel_id=1, source_target_pairs={{16,24},{17,25},{26,18},{27,19},{4,12},{5,13},{14,6},{15,7}} | collective-permute-start | bytes 1327112 | tf_op jit(solution)/shard_map/ppermute | solution.py:105
  87.7 4.7 %collective-permute-start.36 = (bf16[3,4,144,128]{3,2,1,0:T(8,128)(2,1)}, bf16[3,4,144,128]{3,2,1,0:T(8,128)(2,1)}, u32[]{:S(2)}, u32[]{:S(2)}) collective-permute-start(bf16[3,4,144,128]{3,2,1,0:T(8,128)(2,1)} %pad_maximum_fusion.7), channel_id=1, source_target_pairs={{0,16},{1,17},{10,26},{11,27},{20,4},{21,5},{30,14},{31,15}} | collective-permute-start | bytes 1327112 | tf_op jit(solution)/shard_map/ppermute | solution.py:105
  94.1 1.4 %collective-permute-start.34 = (bf16[3,4,144,128]{3,2,1,0:T(8,128)(2,1)}, bf16[3,4,144,128]{3,2,1,0:T(8,128)(2,1)}, u32[]{:S(2)}, u32[]{:S(2)}) collective-permute-start(bf16[3,4,144,128]{3,2,1,0:T(8,128)(2,1)} %collective-permute-done.33), channel_id=1, source_target_pairs={{16,24},{17,25},{26,18},{27,19},{4,12},{5,13},{14,6},{15,7}} | collective-permute-start | bytes 1327112 | tf_op jit(solution)/shard_map/ppermute | solution.py:105
  97.2 1.7 %slice.19 = bf16[96,2,1,1]{3,2,1,0:T(2,128)(2,1)} slice(bf16[96,2,144,128]{3,2,1,0:T(8,128)(2,1)} %bitcast.44), slice={[0:96], [0:2], [131:132], [0:1]} | slice | bytes 768 | tf_op jit(solution)/shard_map/slice | solution.py:150
  100.0 1.3 %collective-permute-start.35 = (bf16[3,4,144,128]{3,2,1,0:T(8,128)(2,1)}, bf16[3,4,144,128]{3,2,1,0:T(8,128)(2,1)S(1)}, u32[]{:S(2)}, u32[]{:S(2)}) collective-permute-start(bf16[3,4,144,128]{3,2,1,0:T(8,128)(2,1)} %pad_maximum_fusion.7), channel_id=1, source_target_pairs={{0,8},{1,9},{10,2},{11,3},{20,28},{21,29},{30,22},{31,23}} | collective-permute-start | bytes 1327112 | tf_op jit(solution)/shard_map/ppermute | solution.py:105
  102.0 1.5 %select_dynamic-update-slice_fusion.2 = bf16[3,32,144,128]{3,2,1,0:T(8,128)(2,1)S(1)} fusion(bf16[3,32,144,128]{3,2,1,0:T(8,128)(2,1)S(1)} %select_dynamic-update-slice_fusion.3, bf16[3,4,144,128]{3,2,1,0:T(8,128)(2,1)} %collective-permute-done.29, bf16[3,4,144,128]{3,2,1,0:T(8,128)(2,1)} %collective-permute-done.30, ...), kind=kLoop, calls=%fused_computation.11 | loop fusion | flops 1548288 | bytes 2211843
  103.5 1.5 %select_dynamic-update-slice_fusion.1 = bf16[3,32,144,128]{3,2,1,0:T(8,128)(2,1)S(1)} fusion(bf16[3,32,144,128]{3,2,1,0:T(8,128)(2,1)S(1)} %select_dynamic-update-slice_fusion.2, bf16[3,4,144,128]{3,2,1,0:T(8,128)(2,1)} %collective-permute-done.32, bf16[3,4,144,128]{3,2,1,0:T(8,128)(2,1)} %collective-permute-done.33, ...), kind=kLoop, calls=%fused_computation.10 | loop fusion | flops 1548288 | bytes 2211843
  105.0 1.3 %select_dynamic-update-slice_fusion = bf16[3,32,144,128]{3,2,1,0:T(8,128)(2,1)S(1)} fusion(bf16[3,32,144,128]{3,2,1,0:T(8,128)(2,1)S(1)} %select_dynamic-update-slice_fusion.1, bf16[3,4,144,128]{3,2,1,0:T(8,128)(2,1)S(1)} %collective-permute-done.35, bf16[3,4,144,128]{3,2,1,0:T(8,128)(2,1)} %collective-permute-done.36, ...), kind=kLoop, calls=%fused_computation.9 | loop fusion | flops 1548288 | bytes 2211843 | tf_op jit(solution)/shard_map/concatenate | solution.py:145
  108.8 10.8 %shard_map.37 = f32[2048,1024]{1,0:T(8,128)} custom-call(s32[288]{0:T(512)S(1)} %min.12.offs_ref, bf16[96,2,144,128]{3,2,1,0:T(8,128)(2,1)} %bitcast.45, bf16[96,144,128]{2,1,0:T(8,128)(2,1)S(1)} %bitcast.43), custom_call_target="tpu_custom_call" | custom-call | flops 805306368 | bytes 17825792 | tf_op jit(solution)/shard_map/pallas_call | solution.py:40
  (131 shorter events, 36.2 us)
Async XLA Ops:
  4.2 13.2 %collective-permute-start = (bf16[3,2,2,144,128]{4,3,2,1,0:T(8,128)(2,1)S(1)}, bf16[3,2,2,144,128]{4,3,2,1,0:T(8,128)(2,1)S(1)}, u32[]{:S(2)}, u32[]{:S(2)}) collective-permute-start(bf16[3,2,2,144,128]{4,3,2,1,0:T(8,128)(2,1)S(1)} %get-tuple-element.5), channel_id=1, source_target_pairs={{0,2},{2,4},{4,6},{6,7},{7,5},{5,3},{3,1},{1,0},{8,10},{10,12},{12... | collective-permute-start | bytes 1327112 | tf_op jit(solution)/shard_map/ppermute | solution.py:129
  7.3 11.9 %collective-permute-start.1 = (bf16[3,2,2,144,128]{4,3,2,1,0:T(8,128)(2,1)S(1)}, bf16[3,2,2,144,128]{4,3,2,1,0:T(8,128)(2,1)S(1)}, u32[]{:S(2)}, u32[]{:S(2)}) collective-permute-start(bf16[3,2,2,144,128]{4,3,2,1,0:T(8,128)(2,1)S(1)} %get-tuple-element.6), channel_id=1, source_target_pairs={{2,0},{4,2},{6,4},{7,6},{5,7},{3,5},{1,3},{0,1},{10,8},{12,10},{14... | collective-permute-start | bytes 1327112 | tf_op jit(solution)/shard_map/ppermute | solution.py:130
  8.1 15.1 %collective-permute-start.15 = (bf16[3,4,144,128]{3,2,1,0:T(8,128)(2,1)S(1)}, bf16[3,4,144,128]{3,2,1,0:T(8,128)(2,1)S(1)}, u32[]{:S(2)}, u32[]{:S(2)}) collective-permute-start(bf16[3,4,144,128]{3,2,1,0:T(8,128)(2,1)S(1)} %pad_maximum_fusion), channel_id=1, source_target_pairs={{0,16},{1,17},{10,26},{11,27},{20,4},{21,5},{30,14},{31,15}} | collective-permute-start | bytes 1327112 | tf_op jit(solution)/shard_map/ppermute | solution.py:105
  12.0 21.9 %collective-permute-start.14 = (bf16[3,4,144,128]{3,2,1,0:T(8,128)(2,1)S(1)}, bf16[3,4,144,128]{3,2,1,0:T(8,128)(2,1)S(1)}, u32[]{:S(2)}, u32[]{:S(2)}) collective-permute-start(bf16[3,4,144,128]{3,2,1,0:T(8,128)(2,1)S(1)} %pad_maximum_fusion), channel_id=1, source_target_pairs={{0,8},{1,9},{10,2},{11,3},{20,28},{21,29},{30,22},{31,23}} | collective-permute-start | bytes 1327112 | tf_op jit(solution)/shard_map/ppermute | solution.py:105
  17.4 13.1 %collective-permute-start.2 = (bf16[3,2,2,144,128]{4,3,2,1,0:T(8,128)(2,1)S(1)}, bf16[3,2,2,144,128]{4,3,2,1,0:T(8,128)(2,1)S(1)}, u32[]{:S(2)}, u32[]{:S(2)}) collective-permute-start(bf16[3,2,2,144,128]{4,3,2,1,0:T(8,128)(2,1)S(1)} %collective-permute-done), channel_id=1, source_target_pairs={{0,2},{2,4},{4,6},{6,7},{7,5},{5,3},{3,1},{1,0},{8,10},{10,12},{12... | collective-permute-start | bytes 1327112 | tf_op jit(solution)/shard_map/ppermute | solution.py:129
  19.2 10.8 %collective-permute-start.3 = (bf16[3,2,2,144,128]{4,3,2,1,0:T(8,128)(2,1)S(1)}, bf16[3,2,2,144,128]{4,3,2,1,0:T(8,128)(2,1)S(1)}, u32[]{:S(2)}, u32[]{:S(2)}) collective-permute-start(bf16[3,2,2,144,128]{4,3,2,1,0:T(8,128)(2,1)S(1)} %collective-permute-done.1), channel_id=1, source_target_pairs={{2,0},{4,2},{6,4},{7,6},{5,7},{3,5},{1,3},{0,1},{10,8},{12,10},{14... | collective-permute-start | bytes 1327112 | tf_op jit(solution)/shard_map/ppermute | solution.py:130
  19.5 15.6 %collective-permute-start.18 = (bf16[3,4,144,128]{3,2,1,0:T(8,128)(2,1)S(1)}, bf16[3,4,144,128]{3,2,1,0:T(8,128)(2,1)S(1)}, u32[]{:S(2)}, u32[]{:S(2)}) collective-permute-start(bf16[3,4,144,128]{3,2,1,0:T(8,128)(2,1)S(1)} %pad_maximum_fusion.1), channel_id=1, source_target_pairs={{0,16},{1,17},{10,26},{11,27},{20,4},{21,5},{30,14},{31,15}} | collective-permute-start | bytes 1327112 | tf_op jit(solution)/shard_map/ppermute | solution.py:105
  23.2 14.8 %collective-permute-start.16 = (bf16[3,4,144,128]{3,2,1,0:T(8,128)(2,1)S(1)}, bf16[3,4,144,128]{3,2,1,0:T(8,128)(2,1)S(1)}, u32[]{:S(2)}, u32[]{:S(2)}) collective-permute-start(bf16[3,4,144,128]{3,2,1,0:T(8,128)(2,1)S(1)} %collective-permute-done.15), channel_id=1, source_target_pairs={{16,24},{17,25},{26,18},{27,19},{4,12},{5,13},{14,6},{15,7}} | collective-permute-start | bytes 1327112 | tf_op jit(solution)/shard_map/ppermute | solution.py:105
  29.9 9.8 %collective-permute-start.5 = (bf16[3,2,2,144,128]{4,3,2,1,0:T(8,128)(2,1)S(1)}, bf16[3,2,2,144,128]{4,3,2,1,0:T(8,128)(2,1)S(1)}, u32[]{:S(2)}, u32[]{:S(2)}) collective-permute-start(bf16[3,2,2,144,128]{4,3,2,1,0:T(8,128)(2,1)S(1)} %collective-permute-done.3), channel_id=1, source_target_pairs={{2,0},{4,2},{6,4},{7,6},{5,7},{3,5},{1,3},{0,1},{10,8},{12,10},{14... | collective-permute-start | bytes 1327112 | tf_op jit(solution)/shard_map/ppermute | solution.py:130
  30.5 10.3 %collective-permute-start.4 = (bf16[3,2,2,144,128]{4,3,2,1,0:T(8,128)(2,1)S(1)}, bf16[3,2,2,144,128]{4,3,2,1,0:T(8,128)(2,1)S(1)}, u32[]{:S(2)}, u32[]{:S(2)}) collective-permute-start(bf16[3,2,2,144,128]{4,3,2,1,0:T(8,128)(2,1)S(1)} %collective-permute-done.2), channel_id=1, source_target_pairs={{0,2},{2,4},{4,6},{6,7},{7,5},{5,3},{3,1},{1,0},{8,10},{10,12},{12... | collective-permute-start | bytes 1327112 | tf_op jit(solution)/shard_map/ppermute | solution.py:129
  33.8 9.9 %collective-permute-start.17 = (bf16[3,4,144,128]{3,2,1,0:T(8,128)(2,1)S(1)}, bf16[3,4,144,128]{3,2,1,0:T(8,128)(2,1)S(1)}, u32[]{:S(2)}, u32[]{:S(2)}) collective-permute-start(bf16[3,4,144,128]{3,2,1,0:T(8,128)(2,1)S(1)} %pad_maximum_fusion.1), channel_id=1, source_target_pairs={{0,8},{1,9},{10,2},{11,3},{20,28},{21,29},{30,22},{31,23}} | collective-permute-start | bytes 1327112 | tf_op jit(solution)/shard_map/ppermute | solution.py:105
  35.1 9.9 %collective-permute-start.21 = (bf16[3,4,144,128]{3,2,1,0:T(8,128)(2,1)S(1)}, bf16[3,4,144,128]{3,2,1,0:T(8,128)(2,1)S(1)}, u32[]{:S(2)}, u32[]{:S(2)}) collective-permute-start(bf16[3,4,144,128]{3,2,1,0:T(8,128)(2,1)S(1)} %pad_maximum_fusion.2), channel_id=1, source_target_pairs={{0,16},{1,17},{10,26},{11,27},{20,4},{21,5},{30,14},{31,15}} | collective-permute-start | bytes 1327112 | tf_op jit(solution)/shard_map/ppermute | solution.py:105
  38.0 10.2 %collective-permute-start.19 = (bf16[3,4,144,128]{3,2,1,0:T(8,128)(2,1)S(1)}, bf16[3,4,144,128]{3,2,1,0:T(8,128)(2,1)S(1)}, u32[]{:S(2)}, u32[]{:S(2)}) collective-permute-start(bf16[3,4,144,128]{3,2,1,0:T(8,128)(2,1)S(1)} %collective-permute-done.18), channel_id=1, source_target_pairs={{16,24},{17,25},{26,18},{27,19},{4,12},{5,13},{14,6},{15,7}} | collective-permute-start | bytes 1327112 | tf_op jit(solution)/shard_map/ppermute | solution.py:105
  39.8 10.8 %collective-permute-start.7 = (bf16[3,2,2,144,128]{4,3,2,1,0:T(8,128)(2,1)S(1)}, bf16[3,2,2,144,128]{4,3,2,1,0:T(8,128)(2,1)S(1)}, u32[]{:S(2)}, u32[]{:S(2)}) collective-permute-start(bf16[3,2,2,144,128]{4,3,2,1,0:T(8,128)(2,1)S(1)} %collective-permute-done.5), channel_id=1, source_target_pairs={{2,0},{4,2},{6,4},{7,6},{5,7},{3,5},{1,3},{0,1},{10,8},{12,10},{14... | collective-permute-start | bytes 1327112 | tf_op jit(solution)/shard_map/ppermute | solution.py:130
  40.8 9.9 %collective-permute-start.6 = (bf16[3,2,2,144,128]{4,3,2,1,0:T(8,128)(2,1)S(1)}, bf16[3,2,2,144,128]{4,3,2,1,0:T(8,128)(2,1)S(1)}, u32[]{:S(2)}, u32[]{:S(2)}) collective-permute-start(bf16[3,2,2,144,128]{4,3,2,1,0:T(8,128)(2,1)S(1)} %collective-permute-done.4), channel_id=1, source_target_pairs={{0,2},{2,4},{4,6},{6,7},{7,5},{5,3},{3,1},{1,0},{8,10},{10,12},{12... | collective-permute-start | bytes 1327112 | tf_op jit(solution)/shard_map/ppermute | solution.py:129
  43.7 10.8 %collective-permute-start.20 = (bf16[3,4,144,128]{3,2,1,0:T(8,128)(2,1)S(1)}, bf16[3,4,144,128]{3,2,1,0:T(8,128)(2,1)S(1)}, u32[]{:S(2)}, u32[]{:S(2)}) collective-permute-start(bf16[3,4,144,128]{3,2,1,0:T(8,128)(2,1)S(1)} %pad_maximum_fusion.2), channel_id=1, source_target_pairs={{0,8},{1,9},{10,2},{11,3},{20,28},{21,29},{30,22},{31,23}} | collective-permute-start | bytes 1327112 | tf_op jit(solution)/shard_map/ppermute | solution.py:105
  45.0 14.0 %collective-permute-start.24 = (bf16[3,4,144,128]{3,2,1,0:T(8,128)(2,1)S(1)}, bf16[3,4,144,128]{3,2,1,0:T(8,128)(2,1)S(1)}, u32[]{:S(2)}, u32[]{:S(2)}) collective-permute-start(bf16[3,4,144,128]{3,2,1,0:T(8,128)(2,1)S(1)} %pad_maximum_fusion.3), channel_id=1, source_target_pairs={{0,16},{1,17},{10,26},{11,27},{20,4},{21,5},{30,14},{31,15}} | collective-permute-start | bytes 1327112 | tf_op jit(solution)/shard_map/ppermute | solution.py:105
  50.6 11.9 %collective-permute-start.9 = (bf16[3,2,2,144,128]{4,3,2,1,0:T(8,128)(2,1)S(1)}, bf16[3,2,2,144,128]{4,3,2,1,0:T(8,128)(2,1)S(1)}, u32[]{:S(2)}, u32[]{:S(2)}) collective-permute-start(bf16[3,2,2,144,128]{4,3,2,1,0:T(8,128)(2,1)S(1)} %collective-permute-done.7), channel_id=1, source_target_pairs={{2,0},{4,2},{6,4},{7,6},{5,7},{3,5},{1,3},{0,1},{10,8},{12,10},{14... | collective-permute-start | bytes 1327112 | tf_op jit(solution)/shard_map/ppermute | solution.py:130
  50.8 10.3 %collective-permute-start.8 = (bf16[3,2,2,144,128]{4,3,2,1,0:T(8,128)(2,1)S(1)}, bf16[3,2,2,144,128]{4,3,2,1,0:T(8,128)(2,1)S(1)}, u32[]{:S(2)}, u32[]{:S(2)}) collective-permute-start(bf16[3,2,2,144,128]{4,3,2,1,0:T(8,128)(2,1)S(1)} %collective-permute-done.6), channel_id=1, source_target_pairs={{0,2},{2,4},{4,6},{6,7},{7,5},{5,3},{3,1},{1,0},{8,10},{10,12},{12... | collective-permute-start | bytes 1327112 | tf_op jit(solution)/shard_map/ppermute | solution.py:129
  54.5 10.5 %collective-permute-start.23 = (bf16[3,4,144,128]{3,2,1,0:T(8,128)(2,1)S(1)}, bf16[3,4,144,128]{3,2,1,0:T(8,128)(2,1)S(1)}, u32[]{:S(2)}, u32[]{:S(2)}) collective-permute-start(bf16[3,4,144,128]{3,2,1,0:T(8,128)(2,1)S(1)} %pad_maximum_fusion.3), channel_id=1, source_target_pairs={{0,8},{1,9},{10,2},{11,3},{20,28},{21,29},{30,22},{31,23}} | collective-permute-start | bytes 1327112 | tf_op jit(solution)/shard_map/ppermute | solution.py:105
  55.8 14.5 %collective-permute-start.27 = (bf16[3,4,144,128]{3,2,1,0:T(8,128)(2,1)S(1)}, bf16[3,4,144,128]{3,2,1,0:T(8,128)(2,1)S(1)}, u32[]{:S(2)}, u32[]{:S(2)}) collective-permute-start(bf16[3,4,144,128]{3,2,1,0:T(8,128)(2,1)S(1)} %pad_maximum_fusion.4), channel_id=1, source_target_pairs={{0,16},{1,17},{10,26},{11,27},{20,4},{21,5},{30,14},{31,15}} | collective-permute-start | bytes 1327112 | tf_op jit(solution)/shard_map/ppermute | solution.py:105
  61.1 11.0 %collective-permute-start.10 = (bf16[3,2,2,144,128]{4,3,2,1,0:T(8,128)(2,1)S(1)}, bf16[3,2,2,144,128]{4,3,2,1,0:T(8,128)(2,1)S(1)}, u32[]{:S(2)}, u32[]{:S(2)}) collective-permute-start(bf16[3,2,2,144,128]{4,3,2,1,0:T(8,128)(2,1)S(1)} %collective-permute-done.8), channel_id=1, source_target_pairs={{0,2},{2,4},{4,6},{6,7},{7,5},{5,3},{3,1},{1,0},{8,10},{10,12},{12... | collective-permute-start | bytes 1327112 | tf_op jit(solution)/shard_map/ppermute | solution.py:129
  62.5 10.6 %collective-permute-start.11 = (bf16[3,2,2,144,128]{4,3,2,1,0:T(8,128)(2,1)S(1)}, bf16[3,2,2,144,128]{4,3,2,1,0:T(8,128)(2,1)S(1)}, u32[]{:S(2)}, u32[]{:S(2)}) collective-permute-start(bf16[3,2,2,144,128]{4,3,2,1,0:T(8,128)(2,1)S(1)} %collective-permute-done.9), channel_id=1, source_target_pairs={{2,0},{4,2},{6,4},{7,6},{5,7},{3,5},{1,3},{0,1},{10,8},{12,10},{14... | collective-permute-start | bytes 1327112 | tf_op jit(solution)/shard_map/ppermute | solution.py:130
  64.9 10.2 %collective-permute-start.26 = (bf16[3,4,144,128]{3,2,1,0:T(8,128)(2,1)S(1)}, bf16[3,4,144,128]{3,2,1,0:T(8,128)(2,1)S(1)}, u32[]{:S(2)}, u32[]{:S(2)}) collective-permute-start(bf16[3,4,144,128]{3,2,1,0:T(8,128)(2,1)S(1)} %pad_maximum_fusion.4), channel_id=1, source_target_pairs={{0,8},{1,9},{10,2},{11,3},{20,28},{21,29},{30,22},{31,23}} | collective-permute-start | bytes 1327112 | tf_op jit(solution)/shard_map/ppermute | solution.py:105
  66.2 14.7 %collective-permute-start.30 = (bf16[3,4,144,128]{3,2,1,0:T(8,128)(2,1)}, bf16[3,4,144,128]{3,2,1,0:T(8,128)(2,1)}, u32[]{:S(2)}, u32[]{:S(2)}) collective-permute-start(bf16[3,4,144,128]{3,2,1,0:T(8,128)(2,1)} %pad_maximum_fusion.5), channel_id=1, source_target_pairs={{0,16},{1,17},{10,26},{11,27},{20,4},{21,5},{30,14},{31,15}} | collective-permute-start | bytes 1327112 | tf_op jit(solution)/shard_map/ppermute | solution.py:105
  72.2 14.1 %collective-permute-start.12 = (bf16[3,2,2,144,128]{4,3,2,1,0:T(8,128)(2,1)S(1)}, bf16[3,2,2,144,128]{4,3,2,1,0:T(8,128)(2,1)S(1)}, u32[]{:S(2)}, u32[]{:S(2)}) collective-permute-start(bf16[3,2,2,144,128]{4,3,2,1,0:T(8,128)(2,1)S(1)} %collective-permute-done.10), channel_id=1, source_target_pairs={{0,2},{2,4},{4,6},{6,7},{7,5},{5,3},{3,1},{1,0},{8,10},{10,12},{12... | collective-permute-start | bytes 1327112 | tf_op jit(solution)/shard_map/ppermute | solution.py:129
  73.1 11.6 %collective-permute-start.13 = (bf16[3,2,2,144,128]{4,3,2,1,0:T(8,128)(2,1)S(1)}, bf16[3,2,2,144,128]{4,3,2,1,0:T(8,128)(2,1)S(1)}, u32[]{:S(2)}, u32[]{:S(2)}) collective-permute-start(bf16[3,2,2,144,128]{4,3,2,1,0:T(8,128)(2,1)S(1)} %collective-permute-done.11), channel_id=1, source_target_pairs={{2,0},{4,2},{6,4},{7,6},{5,7},{3,5},{1,3},{0,1},{10,8},{12,10},{14... | collective-permute-start | bytes 1327112 | tf_op jit(solution)/shard_map/ppermute | solution.py:130
  75.2 24.8 %collective-permute-start.29 = (bf16[3,4,144,128]{3,2,1,0:T(8,128)(2,1)}, bf16[3,4,144,128]{3,2,1,0:T(8,128)(2,1)}, u32[]{:S(2)}, u32[]{:S(2)}) collective-permute-start(bf16[3,4,144,128]{3,2,1,0:T(8,128)(2,1)} %pad_maximum_fusion.5), channel_id=1, source_target_pairs={{0,8},{1,9},{10,2},{11,3},{20,28},{21,29},{30,22},{31,23}} | collective-permute-start | bytes 1327112 | tf_op jit(solution)/shard_map/ppermute | solution.py:105
  77.2 16.8 %collective-permute-start.33 = (bf16[3,4,144,128]{3,2,1,0:T(8,128)(2,1)}, bf16[3,4,144,128]{3,2,1,0:T(8,128)(2,1)}, u32[]{:S(2)}, u32[]{:S(2)}) collective-permute-start(bf16[3,4,144,128]{3,2,1,0:T(8,128)(2,1)} %pad_maximum_fusion.6), channel_id=1, source_target_pairs={{0,16},{1,17},{10,26},{11,27},{20,4},{21,5},{30,14},{31,15}} | collective-permute-start | bytes 1327112 | tf_op jit(solution)/shard_map/ppermute | solution.py:105
  80.9 22.5 %collective-permute-start.32 = (bf16[3,4,144,128]{3,2,1,0:T(8,128)(2,1)}, bf16[3,4,144,128]{3,2,1,0:T(8,128)(2,1)}, u32[]{:S(2)}, u32[]{:S(2)}) collective-permute-start(bf16[3,4,144,128]{3,2,1,0:T(8,128)(2,1)} %pad_maximum_fusion.6), channel_id=1, source_target_pairs={{0,8},{1,9},{10,2},{11,3},{20,28},{21,29},{30,22},{31,23}} | collective-permute-start | bytes 1327112 | tf_op jit(solution)/shard_map/ppermute | solution.py:105
  84.7 17.2 %collective-permute-start.31 = (bf16[3,4,144,128]{3,2,1,0:T(8,128)(2,1)}, bf16[3,4,144,128]{3,2,1,0:T(8,128)(2,1)}, u32[]{:S(2)}, u32[]{:S(2)}) collective-permute-start(bf16[3,4,144,128]{3,2,1,0:T(8,128)(2,1)} %collective-permute-done.30), channel_id=1, source_target_pairs={{16,24},{17,25},{26,18},{27,19},{4,12},{5,13},{14,6},{15,7}} | collective-permute-start | bytes 1327112 | tf_op jit(solution)/shard_map/ppermute | solution.py:105
  87.7 13.6 %collective-permute-start.36 = (bf16[3,4,144,128]{3,2,1,0:T(8,128)(2,1)}, bf16[3,4,144,128]{3,2,1,0:T(8,128)(2,1)}, u32[]{:S(2)}, u32[]{:S(2)}) collective-permute-start(bf16[3,4,144,128]{3,2,1,0:T(8,128)(2,1)} %pad_maximum_fusion.7), channel_id=1, source_target_pairs={{0,16},{1,17},{10,26},{11,27},{20,4},{21,5},{30,14},{31,15}} | collective-permute-start | bytes 1327112 | tf_op jit(solution)/shard_map/ppermute | solution.py:105
  (18 other events, 132.7 us)

commit v30 on v26

--- a/solution.py
+++ b/solution.py
@@ -118,7 +118,10 @@
         return jnp.where(is_s, own, jnp.where(is_p, to_partner, jnp.where(is_d1, to_d1, to_d2)))
 
     def pick_slot(piece):
-        return lax.dynamic_index_in_dim(piece, slot, axis=2, keepdims=False)
+        picked = piece[:, :, 0]
+        for k in range(1, local_slots):
+            picked = jnp.where(slot == k, piece[:, :, k], picked)
+        return picked
 
     batches = [[k] for k in range(ncol)]
     half = x.shape[1] // 2

time: 120 us -> 152 us (1.27)
  waiting for transfers between devices: 13.7 us -> 41.5 us
    ppermute x7, waiting for transfers between devices: 8.34 us -> 40.2 us  [local(): b = lax.ppermute(b, 'col', backward)]
    ppermute x7, starting transfers between devices: 11.6 us -> 3.31 us  [local(): a = lax.ppermute(a, 'col', forward)]
    ppermute x7, starting transfers between devices: 3.59 us -> 11.6 us  [local(): b = lax.ppermute(b, 'col', backward)]
    ppermute x7, waiting for transfers between devices: 5.35 us -> 1.31 us  [local(): a = lax.ppermute(a, 'col', forward)]
    ppermute x24, starting transfers between devices: 47.8 us -> 49.4 us  [send(): lax.ppermute(v, ('row', 'col'), [(a * ncol + cc, b * ncol + cc) for a, b,...]
    unnamed x37 -> x35, local copies, waits for them, and re-layouts: 12.5 us -> 13.8 us
  transfers between devices with their start and end apart: 38 -> 38, of which waited for: 7 -> 8; matrix products, arithmetic and copies ran while one was open for 18% -> 15% of each run, Pallas kernels for 0% -> 0%
where the time goes in v30:
time: 152 us; the launch traced here: 151 us
  starting transfers between devices  64.3 us (42%)
  waiting for transfers between devices  41.5 us (27%)
  local copies, waits for them, and re-layouts  20.2 us (13%)
  other arithmetic  13.6 us (9%)
  Pallas kernels  10.4 us (7%)
    ppermute x24, starting transfers between devices, send(): lax.ppermute(v, ('row', 'col'), [(a * ncol + cc, b * ncol + cc) for a, b,...  49.4 us
    ppermute x7, waiting for transfers between devices, local(): b = lax.ppermute(b, 'col', backward)  40.2 us
    unnamed x35, local copies, waits for them, and re-layouts  13.8 us
    ppermute x7, starting transfers between devices, local(): b = lax.ppermute(b, 'col', backward)  11.6 us
    pallas_call x1, Pallas kernels, gram_call(): pl.pallas_call(kernel, grid_spec=pltpu.PrefetchScalarGridSpec(num_scalar_...  10.4 us
    unnamed x8, other arithmetic  7.69 us
    ppermute x7, starting transfers between devices, local(): a = lax.ppermute(a, 'col', forward)  3.31 us
  transfers between devices with their start and end apart: 38, of which 8 were waited for; matrix products, arithmetic and copies ran while one was open for 15% of the time, Pallas kernels for 0%

profile of v30, /device:TPU:0, one launch (start us, length us, event | category | flops | bytes accessed | tf_op | source)
XLA Modules:
  0.0 150.9 jit_solution(6419236431957413787)
XLA Ops:
  1.7 2.4 %constant_dynamic-update-slice_fusion = (bf16[3,32,2,144,128]{4,3,2,1,0:T(8,128)(2,1)}, bf16[3,4,2,144,128]{4,3,2,1,0:T(8,128)(2,1)S(1)}) fusion(bf16[144]{0:T(256)(128)(2,1)S(1)} %pad.21.clone, bf16[3,4,2,1,128]{4,3,2,1,0:T(2,128)(2,1)S(1)} %broadcast_in_dim.7, bf16[3,4,2,3,128]{4,3,2,1,0:T(4,128)(2,1)S(1)} %broadcast_in_dim.6, ...), kind=kLoop, calls=%fused_computation.66 | loop fusion | flops 3538943 | bytes 2580768
  4.3 3.1 %collective-permute-start = (bf16[3,2,2,144,128]{4,3,1,0,2:T(8,128)(2,1)S(1)}, bf16[3,2,2,144,128]{4,3,1,0,2:T(8,128)(2,1)S(1)}, u32[]{:S(2)}, u32[]{:S(2)}) collective-permute-start(bf16[3,2,2,144,128]{4,3,1,0,2:T(8,128)(2,1)S(1)} %copy.49), channel_id=1, source_target_pairs={{0,2},{2,4},{4,6},{6,7},{7,5},{5,3},{3,1},{1,0},{8,10},{10,12},{12... | collective-permute-start | bytes 1327112 | tf_op jit(solution)/shard_map/ppermute | solution.py:132
  8.9 3.8 %collective-permute-start.15 = (bf16[3,4,144,128]{3,2,1,0:T(8,128)(2,1)S(1)}, bf16[3,4,144,128]{3,2,1,0:T(8,128)(2,1)S(1)}, u32[]{:S(2)}, u32[]{:S(2)}) collective-permute-start(bf16[3,4,144,128]{3,2,1,0:T(8,128)(2,1)S(1)} %pad_maximum_fusion), channel_id=1, source_target_pairs={{0,16},{1,17},{10,26},{11,27},{20,4},{21,5},{30,14},{31,15}} | collective-permute-start | bytes 1327112 | tf_op jit(solution)/shard_map/ppermute | solution.py:105
  14.2 4.9 %collective-permute-done.1 = bf16[3,2,2,144,128]{4,3,1,0,2:T(8,128)(2,1)S(1)} collective-permute-done((bf16[3,2,2,144,128]{4,3,1,0,2:T(8,128)(2,1)S(1)}, bf16[3,2,2,144,128]{4,3,1,0,2:T(8,128)(2,1)S(1)}, u32[]{:S(2)}, u32[]{:S(2)}) %collective-permute-start.1) | collective-permute-done | bytes 442400 | tf_op jit(solution)/shard_map/ppermute | solution.py:133
  19.2 3.4 %collective-permute-start.18 = (bf16[3,4,144,128]{3,2,1,0:T(8,128)(2,1)S(1)}, bf16[3,4,144,128]{3,2,1,0:T(8,128)(2,1)S(1)}, u32[]{:S(2)}, u32[]{:S(2)}) collective-permute-start(bf16[3,4,144,128]{3,2,1,0:T(8,128)(2,1)S(1)} %pad_maximum_fusion.1), channel_id=1, source_target_pairs={{0,16},{1,17},{10,26},{11,27},{20,4},{21,5},{30,14},{31,15}} | collective-permute-start | bytes 1327112 | tf_op jit(solution)/shard_map/ppermute | solution.py:105
  22.7 2.0 %collective-permute-start.3 = (bf16[3,2,2,144,128]{4,3,1,0,2:T(8,128)(2,1)S(1)}, bf16[3,2,2,144,128]{4,3,1,0,2:T(8,128)(2,1)S(1)}, u32[]{:S(2)}, u32[]{:S(2)}) collective-permute-start(bf16[3,2,2,144,128]{4,3,1,0,2:T(8,128)(2,1)S(1)} %collective-permute-done.1), channel_id=1, source_target_pairs={{2,0},{4,2},{6,4},{7,6},{5,7},{3,5},{1,3},{0,1},{10,8},{12,10},{14... | collective-permute-start | bytes 1327112 | tf_op jit(solution)/shard_map/ppermute | solution.py:133
  27.8 6.7 %collective-permute-done.3 = bf16[3,2,2,144,128]{4,3,1,0,2:T(8,128)(2,1)S(1)} collective-permute-done((bf16[3,2,2,144,128]{4,3,1,0,2:T(8,128)(2,1)S(1)}, bf16[3,2,2,144,128]{4,3,1,0,2:T(8,128)(2,1)S(1)}, u32[]{:S(2)}, u32[]{:S(2)}) %collective-permute-start.3) | collective-permute-done | bytes 442400 | tf_op jit(solution)/shard_map/ppermute | solution.py:133
  35.2 2.2 %collective-permute-start.21 = (bf16[3,4,144,128]{3,2,1,0:T(8,128)(2,1)S(1)}, bf16[3,4,144,128]{3,2,1,0:T(8,128)(2,1)S(1)}, u32[]{:S(2)}, u32[]{:S(2)}) collective-permute-start(bf16[3,4,144,128]{3,2,1,0:T(8,128)(2,1)S(1)} %pad_maximum_fusion.2), channel_id=1, source_target_pairs={{0,16},{1,17},{10,26},{11,27},{20,4},{21,5},{30,14},{31,15}} | collective-permute-start | bytes 1327112 | tf_op jit(solution)/shard_map/ppermute | solution.py:105
  38.2 1.4 collective-permute-start.5
  42.6 2.9 %collective-permute-start.20 = (bf16[3,4,144,128]{3,2,1,0:T(8,128)(2,1)S(1)}, bf16[3,4,144,128]{3,2,1,0:T(8,128)(2,1)S(1)}, u32[]{:S(2)}, u32[]{:S(2)}) collective-permute-start(bf16[3,4,144,128]{3,2,1,0:T(8,128)(2,1)S(1)} %pad_maximum_fusion.2), channel_id=1, source_target_pairs={{0,8},{1,9},{10,2},{11,3},{20,28},{21,29},{30,22},{31,23}} | collective-permute-start | bytes 1327112 | tf_op jit(solution)/shard_map/ppermute | solution.py:105
  47.5 2.6 %collective-permute-done.5 = bf16[3,2,2,144,128]{4,3,1,0,2:T(8,128)(2,1)S(1)} collective-permute-done((bf16[3,2,2,144,128]{4,3,1,0,2:T(8,128)(2,1)S(1)}, bf16[3,2,2,144,128]{4,3,1,0,2:T(8,128)(2,1)S(1)}, u32[]{:S(2)}, u32[]{:S(2)}) %collective-permute-start.5) | collective-permute-done | bytes 442400 | tf_op jit(solution)/shard_map/ppermute | solution.py:133
  50.1 4.0 %collective-permute-start.24 = (bf16[3,4,144,128]{3,2,1,0:T(8,128)(2,1)S(1)}, bf16[3,4,144,128]{3,2,1,0:T(8,128)(2,1)S(1)}, u32[]{:S(2)}, u32[]{:S(2)}) collective-permute-start(bf16[3,4,144,128]{3,2,1,0:T(8,128)(2,1)S(1)} %pad_maximum_fusion.3), channel_id=1, source_target_pairs={{0,16},{1,17},{10,26},{11,27},{20,4},{21,5},{30,14},{31,15}} | collective-permute-start | bytes 1327112 | tf_op jit(solution)/shard_map/ppermute | solution.py:105
  54.2 2.0 %collective-permute-start.7 = (bf16[3,2,2,144,128]{4,3,1,0,2:T(8,128)(2,1)S(1)}, bf16[3,2,2,144,128]{4,3,1,0,2:T(8,128)(2,1)S(1)}, u32[]{:S(2)}, u32[]{:S(2)}) collective-permute-start(bf16[3,2,2,144,128]{4,3,1,0,2:T(8,128)(2,1)S(1)} %collective-permute-done.5), channel_id=1, source_target_pairs={{2,0},{4,2},{6,4},{7,6},{5,7},{3,5},{1,3},{0,1},{10,8},{12,10},{14... | collective-permute-start | bytes 1327112 | tf_op jit(solution)/shard_map/ppermute | solution.py:133
  59.5 7.4 %collective-permute-done.7 = bf16[3,2,2,144,128]{4,3,1,0,2:T(8,128)(2,1)S(1)} collective-permute-done((bf16[3,2,2,144,128]{4,3,1,0,2:T(8,128)(2,1)S(1)}, bf16[3,2,2,144,128]{4,3,1,0,2:T(8,128)(2,1)S(1)}, u32[]{:S(2)}, u32[]{:S(2)}) %collective-permute-start.7) | collective-permute-done | bytes 442400 | tf_op jit(solution)/shard_map/ppermute | solution.py:133
  67.7 2.2 %collective-permute-start.27 = (bf16[3,4,144,128]{3,2,1,0:T(8,128)(2,1)S(1)}, bf16[3,4,144,128]{3,2,1,0:T(8,128)(2,1)S(1)}, u32[]{:S(2)}, u32[]{:S(2)}) collective-permute-start(bf16[3,4,144,128]{3,2,1,0:T(8,128)(2,1)S(1)} %pad_maximum_fusion.4), channel_id=1, source_target_pairs={{0,16},{1,17},{10,26},{11,27},{20,4},{21,5},{30,14},{31,15}} | collective-permute-start | bytes 1327112 | tf_op jit(solution)/shard_map/ppermute | solution.py:105
  70.0 2.0 %collective-permute-start.9 = (bf16[3,2,2,144,128]{4,3,1,0,2:T(8,128)(2,1)S(1)}, bf16[3,2,2,144,128]{4,3,1,0,2:T(8,128)(2,1)S(1)}, u32[]{:S(2)}, u32[]{:S(2)}) collective-permute-start(bf16[3,2,2,144,128]{4,3,1,0,2:T(8,128)(2,1)S(1)} %collective-permute-done.7), channel_id=1, source_target_pairs={{2,0},{4,2},{6,4},{7,6},{5,7},{3,5},{1,3},{0,1},{10,8},{12,10},{14... | collective-permute-start | bytes 1327112 | tf_op jit(solution)/shard_map/ppermute | solution.py:133
  75.3 7.4 %collective-permute-done.9 = bf16[3,2,2,144,128]{4,3,1,0,2:T(8,128)(2,1)S(1)} collective-permute-done((bf16[3,2,2,144,128]{4,3,1,0,2:T(8,128)(2,1)S(1)}, bf16[3,2,2,144,128]{4,3,1,0,2:T(8,128)(2,1)S(1)}, u32[]{:S(2)}, u32[]{:S(2)}) %collective-permute-start.9) | collective-permute-done | bytes 442400 | tf_op jit(solution)/shard_map/ppermute | solution.py:133
  84.3 3.6 %collective-permute-start.30 = (bf16[3,4,144,128]{3,2,1,0:T(8,128)(2,1)}, bf16[3,4,144,128]{3,2,1,0:T(8,128)(2,1)}, u32[]{:S(2)}, u32[]{:S(2)}) collective-permute-start(bf16[3,4,144,128]{3,2,1,0:T(8,128)(2,1)} %pad_maximum_fusion.5), channel_id=1, source_target_pairs={{0,16},{1,17},{10,26},{11,27},{20,4},{21,5},{30,14},{31,15}} | collective-permute-start | bytes 1327112 | tf_op jit(solution)/shard_map/ppermute | solution.py:105
  88.0 2.1 %collective-permute-start.11 = (bf16[3,2,2,144,128]{4,3,1,0,2:T(8,128)(2,1)S(1)}, bf16[3,2,2,144,128]{4,3,1,0,2:T(8,128)(2,1)S(1)}, u32[]{:S(2)}, u32[]{:S(2)}) collective-permute-start(bf16[3,2,2,144,128]{4,3,1,0,2:T(8,128)(2,1)S(1)} %collective-permute-done.9), channel_id=1, source_target_pairs={{2,0},{4,2},{6,4},{7,6},{5,7},{3,5},{1,3},{0,1},{10,8},{12,10},{14... | collective-permute-start | bytes 1327112 | tf_op jit(solution)/shard_map/ppermute | solution.py:133
  92.1 2.1 %collective-permute-start.29 = (bf16[3,4,144,128]{3,2,1,0:T(8,128)(2,1)}, bf16[3,4,144,128]{3,2,1,0:T(8,128)(2,1)}, u32[]{:S(2)}, u32[]{:S(2)}) collective-permute-start(bf16[3,4,144,128]{3,2,1,0:T(8,128)(2,1)} %pad_maximum_fusion.5), channel_id=1, source_target_pairs={{0,8},{1,9},{10,2},{11,3},{20,28},{21,29},{30,22},{31,23}} | collective-permute-start | bytes 1327112 | tf_op jit(solution)/shard_map/ppermute | solution.py:105
  94.2 6.7 %collective-permute-done.11 = bf16[3,2,2,144,128]{4,3,1,0,2:T(8,128)(2,1)S(1)} collective-permute-done((bf16[3,2,2,144,128]{4,3,1,0,2:T(8,128)(2,1)S(1)}, bf16[3,2,2,144,128]{4,3,1,0,2:T(8,128)(2,1)S(1)}, u32[]{:S(2)}, u32[]{:S(2)}) %collective-permute-start.11) | collective-permute-done | bytes 442400 | tf_op jit(solution)/shard_map/ppermute | solution.py:133
  102.5 2.7 %collective-permute-start.33 = (bf16[3,4,144,128]{3,2,1,0:T(8,128)(2,1)}, bf16[3,4,144,128]{3,2,1,0:T(8,128)(2,1)}, u32[]{:S(2)}, u32[]{:S(2)}) collective-permute-start(bf16[3,4,144,128]{3,2,1,0:T(8,128)(2,1)} %pad_maximum_fusion.6), channel_id=1, source_target_pairs={{0,16},{1,17},{10,26},{11,27},{20,4},{21,5},{30,14},{31,15}} | collective-permute-start | bytes 1327112 | tf_op jit(solution)/shard_map/ppermute | solution.py:105
  105.3 2.0 %collective-permute-start.13 = (bf16[3,2,2,144,128]{4,3,1,0,2:T(8,128)(2,1)S(1)}, bf16[3,2,2,144,128]{4,3,1,0,2:T(8,128)(2,1)S(1)}, u32[]{:S(2)}, u32[]{:S(2)}) collective-permute-start(bf16[3,2,2,144,128]{4,3,1,0,2:T(8,128)(2,1)S(1)} %collective-permute-done.11), channel_id=1, source_target_pairs={{2,0},{4,2},{6,4},{7,6},{5,7},{3,5},{1,3},{0,1},{10,8},{12,10},{14... | collective-permute-start | bytes 1327112 | tf_op jit(solution)/shard_map/ppermute | solution.py:133
  109.3 3.8 %collective-permute-start.32 = (bf16[3,4,144,128]{3,2,1,0:T(8,128)(2,1)}, bf16[3,4,144,128]{3,2,1,0:T(8,128)(2,1)}, u32[]{:S(2)}, u32[]{:S(2)}) collective-permute-start(bf16[3,4,144,128]{3,2,1,0:T(8,128)(2,1)} %pad_maximum_fusion.6), channel_id=1, source_target_pairs={{0,8},{1,9},{10,2},{11,3},{20,28},{21,29},{30,22},{31,23}} | collective-permute-start | bytes 1327112 | tf_op jit(solution)/shard_map/ppermute | solution.py:105
  113.1 4.5 %collective-permute-done.13 = bf16[3,2,2,144,128]{4,3,1,0,2:T(8,128)(2,1)S(1)} collective-permute-done((bf16[3,2,2,144,128]{4,3,1,0,2:T(8,128)(2,1)S(1)}, bf16[3,2,2,144,128]{4,3,1,0,2:T(8,128)(2,1)S(1)}, u32[]{:S(2)}, u32[]{:S(2)}) %collective-permute-start.13) | collective-permute-done | bytes 442400 | tf_op jit(solution)/shard_map/ppermute | solution.py:133
  117.5 1.4 collective-permute-start.31
  120.5 5.2 %collective-permute-start.36 = (bf16[3,4,144,128]{3,2,1,0:T(8,128)(2,1)}, bf16[3,4,144,128]{3,2,1,0:T(8,128)(2,1)}, u32[]{:S(2)}, u32[]{:S(2)}) collective-permute-start(bf16[3,4,144,128]{3,2,1,0:T(8,128)(2,1)} %pad_maximum_fusion.7), channel_id=1, source_target_pairs={{0,16},{1,17},{10,26},{11,27},{20,4},{21,5},{30,14},{31,15}} | collective-permute-start | bytes 1327112 | tf_op jit(solution)/shard_map/ppermute | solution.py:105
  125.8 1.4 collective-permute-start.34
  128.9 1.7 %slice.151 = bf16[96,2,1,1]{3,2,1,0:T(2,128)(2,1)} slice(bf16[96,2,144,128]{3,2,1,0:T(8,128)(2,1)} %bitcast.58), slice={[0:96], [0:2], [131:132], [0:1]} | slice | bytes 768 | tf_op jit(solution)/shard_map/slice | solution.py:153
  133.7 1.5 select_dynamic-update-slice_fusion.2
  135.2 1.5 select_dynamic-update-slice_fusion.1
  140.5 10.4 %shard_map.37 = f32[2048,1024]{1,0:T(8,128)} custom-call(s32[288]{0:T(512)S(1)} %min.12.offs_ref, bf16[96,2,144,128]{3,2,1,0:T(8,128)(2,1)} %bitcast.59, bf16[96,144,128]{2,1,0:T(8,128)(2,1)S(1)} %bitcast.57), custom_call_target="tpu_custom_call" | custom-call | flops 805306368 | bytes 17825792 | tf_op jit(solution)/shard_map/pallas_call | solution.py:40
  (130 shorter events, 39.1 us)
Async XLA Ops:
  4.3 14.8 %collective-permute-start = (bf16[3,2,2,144,128]{4,3,1,0,2:T(8,128)(2,1)S(1)}, bf16[3,2,2,144,128]{4,3,1,0,2:T(8,128)(2,1)S(1)}, u32[]{:S(2)}, u32[]{:S(2)}) collective-permute-start(bf16[3,2,2,144,128]{4,3,1,0,2:T(8,128)(2,1)S(1)} %copy.49), channel_id=1, source_target_pairs={{0,2},{2,4},{4,6},{6,7},{7,5},{5,3},{3,1},{1,0},{8,10},{10,12},{12... | collective-permute-start | bytes 1327112 | tf_op jit(solution)/shard_map/ppermute | solution.py:132
  7.4 11.7 %collective-permute-start.1 = (bf16[3,2,2,144,128]{4,3,1,0,2:T(8,128)(2,1)S(1)}, bf16[3,2,2,144,128]{4,3,1,0,2:T(8,128)(2,1)S(1)}, u32[]{:S(2)}, u32[]{:S(2)}) collective-permute-start(bf16[3,2,2,144,128]{4,3,1,0,2:T(8,128)(2,1)S(1)} %copy.50), channel_id=1, source_target_pairs={{2,0},{4,2},{6,4},{7,6},{5,7},{3,5},{1,3},{0,1},{10,8},{12,10},{14... | collective-permute-start | bytes 1327112 | tf_op jit(solution)/shard_map/ppermute | solution.py:133
  8.9 17.5 %collective-permute-start.15 = (bf16[3,4,144,128]{3,2,1,0:T(8,128)(2,1)S(1)}, bf16[3,4,144,128]{3,2,1,0:T(8,128)(2,1)S(1)}, u32[]{:S(2)}, u32[]{:S(2)}) collective-permute-start(bf16[3,4,144,128]{3,2,1,0:T(8,128)(2,1)S(1)} %pad_maximum_fusion), channel_id=1, source_target_pairs={{0,16},{1,17},{10,26},{11,27},{20,4},{21,5},{30,14},{31,15}} | collective-permute-start | bytes 1327112 | tf_op jit(solution)/shard_map/ppermute | solution.py:105
  12.8 24.7 %collective-permute-start.14 = (bf16[3,4,144,128]{3,2,1,0:T(8,128)(2,1)S(1)}, bf16[3,4,144,128]{3,2,1,0:T(8,128)(2,1)S(1)}, u32[]{:S(2)}, u32[]{:S(2)}) collective-permute-start(bf16[3,4,144,128]{3,2,1,0:T(8,128)(2,1)S(1)} %pad_maximum_fusion), channel_id=1, source_target_pairs={{0,8},{1,9},{10,2},{11,3},{20,28},{21,29},{30,22},{31,23}} | collective-permute-start | bytes 1327112 | tf_op jit(solution)/shard_map/ppermute | solution.py:105
  19.2 23.4 %collective-permute-start.18 = (bf16[3,4,144,128]{3,2,1,0:T(8,128)(2,1)S(1)}, bf16[3,4,144,128]{3,2,1,0:T(8,128)(2,1)S(1)}, u32[]{:S(2)}, u32[]{:S(2)}) collective-permute-start(bf16[3,4,144,128]{3,2,1,0:T(8,128)(2,1)S(1)} %pad_maximum_fusion.1), channel_id=1, source_target_pairs={{0,16},{1,17},{10,26},{11,27},{20,4},{21,5},{30,14},{31,15}} | collective-permute-start | bytes 1327112 | tf_op jit(solution)/shard_map/ppermute | solution.py:105
  22.6 12.5 %collective-permute-start.2 = (bf16[3,2,2,144,128]{4,3,1,0,2:T(8,128)(2,1)S(1)}, bf16[3,2,2,144,128]{4,3,1,0,2:T(8,128)(2,1)S(1)}, u32[]{:S(2)}, u32[]{:S(2)}) collective-permute-start(bf16[3,2,2,144,128]{4,3,1,0,2:T(8,128)(2,1)S(1)} %collective-permute-done), channel_id=1, source_target_pairs={{0,2},{2,4},{4,6},{6,7},{7,5},{5,3},{3,1},{1,0},{8,10},{10,12},{12... | collective-permute-start | bytes 1327112 | tf_op jit(solution)/shard_map/ppermute | solution.py:132
  22.7 11.7 %collective-permute-start.3 = (bf16[3,2,2,144,128]{4,3,1,0,2:T(8,128)(2,1)S(1)}, bf16[3,2,2,144,128]{4,3,1,0,2:T(8,128)(2,1)S(1)}, u32[]{:S(2)}, u32[]{:S(2)}) collective-permute-start(bf16[3,2,2,144,128]{4,3,1,0,2:T(8,128)(2,1)S(1)} %collective-permute-done.1), channel_id=1, source_target_pairs={{2,0},{4,2},{6,4},{7,6},{5,7},{3,5},{1,3},{0,1},{10,8},{12,10},{14... | collective-permute-start | bytes 1327112 | tf_op jit(solution)/shard_map/ppermute | solution.py:133
  26.4 27.7 %collective-permute-start.17 = (bf16[3,4,144,128]{3,2,1,0:T(8,128)(2,1)S(1)}, bf16[3,4,144,128]{3,2,1,0:T(8,128)(2,1)S(1)}, u32[]{:S(2)}, u32[]{:S(2)}) collective-permute-start(bf16[3,4,144,128]{3,2,1,0:T(8,128)(2,1)S(1)} %pad_maximum_fusion.1), channel_id=1, source_target_pairs={{0,8},{1,9},{10,2},{11,3},{20,28},{21,29},{30,22},{31,23}} | collective-permute-start | bytes 1327112 | tf_op jit(solution)/shard_map/ppermute | solution.py:105
  35.2 22.9 %collective-permute-start.21 = (bf16[3,4,144,128]{3,2,1,0:T(8,128)(2,1)S(1)}, bf16[3,4,144,128]{3,2,1,0:T(8,128)(2,1)S(1)}, u32[]{:S(2)}, u32[]{:S(2)}) collective-permute-start(bf16[3,4,144,128]{3,2,1,0:T(8,128)(2,1)S(1)} %pad_maximum_fusion.2), channel_id=1, source_target_pairs={{0,16},{1,17},{10,26},{11,27},{20,4},{21,5},{30,14},{31,15}} | collective-permute-start | bytes 1327112 | tf_op jit(solution)/shard_map/ppermute | solution.py:105
  37.5 9.3 %collective-permute-start.4 = (bf16[3,2,2,144,128]{4,3,1,0,2:T(8,128)(2,1)S(1)}, bf16[3,2,2,144,128]{4,3,1,0,2:T(8,128)(2,1)S(1)}, u32[]{:S(2)}, u32[]{:S(2)}) collective-permute-start(bf16[3,2,2,144,128]{4,3,1,0,2:T(8,128)(2,1)S(1)} %collective-permute-done.2), channel_id=1, source_target_pairs={{0,2},{2,4},{4,6},{6,7},{7,5},{5,3},{3,1},{1,0},{8,10},{10,12},{12... | collective-permute-start | bytes 1327112 | tf_op jit(solution)/shard_map/ppermute | solution.py:132
  38.2 11.8 %collective-permute-start.5 = (bf16[3,2,2,144,128]{4,3,1,0,2:T(8,128)(2,1)S(1)}, bf16[3,2,2,144,128]{4,3,1,0,2:T(8,128)(2,1)S(1)}, u32[]{:S(2)}, u32[]{:S(2)}) collective-permute-start(bf16[3,2,2,144,128]{4,3,1,0,2:T(8,128)(2,1)S(1)} %collective-permute-done.3), channel_id=1, source_target_pairs={{2,0},{4,2},{6,4},{7,6},{5,7},{3,5},{1,3},{0,1},{10,8},{12,10},{14... | collective-permute-start | bytes 1327112 | tf_op jit(solution)/shard_map/ppermute | solution.py:133
  42.6 27.3 %collective-permute-start.20 = (bf16[3,4,144,128]{3,2,1,0:T(8,128)(2,1)S(1)}, bf16[3,4,144,128]{3,2,1,0:T(8,128)(2,1)S(1)}, u32[]{:S(2)}, u32[]{:S(2)}) collective-permute-start(bf16[3,4,144,128]{3,2,1,0:T(8,128)(2,1)S(1)} %pad_maximum_fusion.2), channel_id=1, source_target_pairs={{0,8},{1,9},{10,2},{11,3},{20,28},{21,29},{30,22},{31,23}} | collective-permute-start | bytes 1327112 | tf_op jit(solution)/shard_map/ppermute | solution.py:105
  46.8 7.4 %collective-permute-start.19 = (bf16[3,4,144,128]{3,2,1,0:T(8,128)(2,1)S(1)}, bf16[3,4,144,128]{3,2,1,0:T(8,128)(2,1)S(1)}, u32[]{:S(2)}, u32[]{:S(2)}) collective-permute-start(bf16[3,4,144,128]{3,2,1,0:T(8,128)(2,1)S(1)} %collective-permute-done.18), channel_id=1, source_target_pairs={{16,24},{17,25},{26,18},{27,19},{4,12},{5,13},{14,6},{15,7}} | collective-permute-start | bytes 1327112 | tf_op jit(solution)/shard_map/ppermute | solution.py:105
  50.1 23.8 %collective-permute-start.24 = (bf16[3,4,144,128]{3,2,1,0:T(8,128)(2,1)S(1)}, bf16[3,4,144,128]{3,2,1,0:T(8,128)(2,1)S(1)}, u32[]{:S(2)}, u32[]{:S(2)}) collective-permute-start(bf16[3,4,144,128]{3,2,1,0:T(8,128)(2,1)S(1)} %pad_maximum_fusion.3), channel_id=1, source_target_pairs={{0,16},{1,17},{10,26},{11,27},{20,4},{21,5},{30,14},{31,15}} | collective-permute-start | bytes 1327112 | tf_op jit(solution)/shard_map/ppermute | solution.py:105
  54.1 13.5 %collective-permute-start.6 = (bf16[3,2,2,144,128]{4,3,1,0,2:T(8,128)(2,1)S(1)}, bf16[3,2,2,144,128]{4,3,1,0,2:T(8,128)(2,1)S(1)}, u32[]{:S(2)}, u32[]{:S(2)}) collective-permute-start(bf16[3,2,2,144,128]{4,3,1,0,2:T(8,128)(2,1)S(1)} %collective-permute-done.4), channel_id=1, source_target_pairs={{0,2},{2,4},{4,6},{6,7},{7,5},{5,3},{3,1},{1,0},{8,10},{10,12},{12... | collective-permute-start | bytes 1327112 | tf_op jit(solution)/shard_map/ppermute | solution.py:132
  54.2 12.7 %collective-permute-start.7 = (bf16[3,2,2,144,128]{4,3,1,0,2:T(8,128)(2,1)S(1)}, bf16[3,2,2,144,128]{4,3,1,0,2:T(8,128)(2,1)S(1)}, u32[]{:S(2)}, u32[]{:S(2)}) collective-permute-start(bf16[3,2,2,144,128]{4,3,1,0,2:T(8,128)(2,1)S(1)} %collective-permute-done.5), channel_id=1, source_target_pairs={{2,0},{4,2},{6,4},{7,6},{5,7},{3,5},{1,3},{0,1},{10,8},{12,10},{14... | collective-permute-start | bytes 1327112 | tf_op jit(solution)/shard_map/ppermute | solution.py:133
  58.2 29.8 %collective-permute-start.23 = (bf16[3,4,144,128]{3,2,1,0:T(8,128)(2,1)S(1)}, bf16[3,4,144,128]{3,2,1,0:T(8,128)(2,1)S(1)}, u32[]{:S(2)}, u32[]{:S(2)}) collective-permute-start(bf16[3,4,144,128]{3,2,1,0:T(8,128)(2,1)S(1)} %pad_maximum_fusion.3), channel_id=1, source_target_pairs={{0,8},{1,9},{10,2},{11,3},{20,28},{21,29},{30,22},{31,23}} | collective-permute-start | bytes 1327112 | tf_op jit(solution)/shard_map/ppermute | solution.py:105
  67.7 24.4 %collective-permute-start.27 = (bf16[3,4,144,128]{3,2,1,0:T(8,128)(2,1)S(1)}, bf16[3,4,144,128]{3,2,1,0:T(8,128)(2,1)S(1)}, u32[]{:S(2)}, u32[]{:S(2)}) collective-permute-start(bf16[3,4,144,128]{3,2,1,0:T(8,128)(2,1)S(1)} %pad_maximum_fusion.4), channel_id=1, source_target_pairs={{0,16},{1,17},{10,26},{11,27},{20,4},{21,5},{30,14},{31,15}} | collective-permute-start | bytes 1327112 | tf_op jit(solution)/shard_map/ppermute | solution.py:105
  69.9 13.6 %collective-permute-start.8 = (bf16[3,2,2,144,128]{4,3,1,0,2:T(8,128)(2,1)S(1)}, bf16[3,2,2,144,128]{4,3,1,0,2:T(8,128)(2,1)S(1)}, u32[]{:S(2)}, u32[]{:S(2)}) collective-permute-start(bf16[3,2,2,144,128]{4,3,1,0,2:T(8,128)(2,1)S(1)} %collective-permute-done.6), channel_id=1, source_target_pairs={{0,2},{2,4},{4,6},{6,7},{7,5},{5,3},{3,1},{1,0},{8,10},{10,12},{12... | collective-permute-start | bytes 1327112 | tf_op jit(solution)/shard_map/ppermute | solution.py:132
  70.0 12.8 %collective-permute-start.9 = (bf16[3,2,2,144,128]{4,3,1,0,2:T(8,128)(2,1)S(1)}, bf16[3,2,2,144,128]{4,3,1,0,2:T(8,128)(2,1)S(1)}, u32[]{:S(2)}, u32[]{:S(2)}) collective-permute-start(bf16[3,2,2,144,128]{4,3,1,0,2:T(8,128)(2,1)S(1)} %collective-permute-done.7), channel_id=1, source_target_pairs={{2,0},{4,2},{6,4},{7,6},{5,7},{3,5},{1,3},{0,1},{10,8},{12,10},{14... | collective-permute-start | bytes 1327112 | tf_op jit(solution)/shard_map/ppermute | solution.py:133
  74.0 31.3 %collective-permute-start.26 = (bf16[3,4,144,128]{3,2,1,0:T(8,128)(2,1)S(1)}, bf16[3,4,144,128]{3,2,1,0:T(8,128)(2,1)S(1)}, u32[]{:S(2)}, u32[]{:S(2)}) collective-permute-start(bf16[3,4,144,128]{3,2,1,0:T(8,128)(2,1)S(1)} %pad_maximum_fusion.4), channel_id=1, source_target_pairs={{0,8},{1,9},{10,2},{11,3},{20,28},{21,29},{30,22},{31,23}} | collective-permute-start | bytes 1327112 | tf_op jit(solution)/shard_map/ppermute | solution.py:105
  84.3 24.9 %collective-permute-start.30 = (bf16[3,4,144,128]{3,2,1,0:T(8,128)(2,1)}, bf16[3,4,144,128]{3,2,1,0:T(8,128)(2,1)}, u32[]{:S(2)}, u32[]{:S(2)}) collective-permute-start(bf16[3,4,144,128]{3,2,1,0:T(8,128)(2,1)} %pad_maximum_fusion.5), channel_id=1, source_target_pairs={{0,16},{1,17},{10,26},{11,27},{20,4},{21,5},{30,14},{31,15}} | collective-permute-start | bytes 1327112 | tf_op jit(solution)/shard_map/ppermute | solution.py:105
  88.0 13.6 %collective-permute-start.10 = (bf16[3,2,2,144,128]{4,3,1,0,2:T(8,128)(2,1)S(1)}, bf16[3,2,2,144,128]{4,3,1,0,2:T(8,128)(2,1)S(1)}, u32[]{:S(2)}, u32[]{:S(2)}) collective-permute-start(bf16[3,2,2,144,128]{4,3,1,0,2:T(8,128)(2,1)S(1)} %collective-permute-done.8), channel_id=1, source_target_pairs={{0,2},{2,4},{4,6},{6,7},{7,5},{5,3},{3,1},{1,0},{8,10},{10,12},{12... | collective-permute-start | bytes 1327112 | tf_op jit(solution)/shard_map/ppermute | solution.py:132
  88.0 12.9 %collective-permute-start.11 = (bf16[3,2,2,144,128]{4,3,1,0,2:T(8,128)(2,1)S(1)}, bf16[3,2,2,144,128]{4,3,1,0,2:T(8,128)(2,1)S(1)}, u32[]{:S(2)}, u32[]{:S(2)}) collective-permute-start(bf16[3,2,2,144,128]{4,3,1,0,2:T(8,128)(2,1)S(1)} %collective-permute-done.9), channel_id=1, source_target_pairs={{2,0},{4,2},{6,4},{7,6},{5,7},{3,5},{1,3},{0,1},{10,8},{12,10},{14... | collective-permute-start | bytes 1327112 | tf_op jit(solution)/shard_map/ppermute | solution.py:133
  92.1 39.6 %collective-permute-start.29 = (bf16[3,4,144,128]{3,2,1,0:T(8,128)(2,1)}, bf16[3,4,144,128]{3,2,1,0:T(8,128)(2,1)}, u32[]{:S(2)}, u32[]{:S(2)}) collective-permute-start(bf16[3,4,144,128]{3,2,1,0:T(8,128)(2,1)} %pad_maximum_fusion.5), channel_id=1, source_target_pairs={{0,8},{1,9},{10,2},{11,3},{20,28},{21,29},{30,22},{31,23}} | collective-permute-start | bytes 1327112 | tf_op jit(solution)/shard_map/ppermute | solution.py:105
  102.5 23.2 %collective-permute-start.33 = (bf16[3,4,144,128]{3,2,1,0:T(8,128)(2,1)}, bf16[3,4,144,128]{3,2,1,0:T(8,128)(2,1)}, u32[]{:S(2)}, u32[]{:S(2)}) collective-permute-start(bf16[3,4,144,128]{3,2,1,0:T(8,128)(2,1)} %pad_maximum_fusion.6), channel_id=1, source_target_pairs={{0,16},{1,17},{10,26},{11,27},{20,4},{21,5},{30,14},{31,15}} | collective-permute-start | bytes 1327112 | tf_op jit(solution)/shard_map/ppermute | solution.py:105
  105.3 13.7 %collective-permute-start.12 = (bf16[3,2,2,144,128]{4,3,1,0,2:T(8,128)(2,1)S(1)}, bf16[3,2,2,144,128]{4,3,1,0,2:T(8,128)(2,1)S(1)}, u32[]{:S(2)}, u32[]{:S(2)}) collective-permute-start(bf16[3,2,2,144,128]{4,3,1,0,2:T(8,128)(2,1)S(1)} %collective-permute-done.10), channel_id=1, source_target_pairs={{0,2},{2,4},{4,6},{6,7},{7,5},{5,3},{3,1},{1,0},{8,10},{10,12},{12... | collective-permute-start | bytes 1327112 | tf_op jit(solution)/shard_map/ppermute | solution.py:132
  105.3 12.2 %collective-permute-start.13 = (bf16[3,2,2,144,128]{4,3,1,0,2:T(8,128)(2,1)S(1)}, bf16[3,2,2,144,128]{4,3,1,0,2:T(8,128)(2,1)S(1)}, u32[]{:S(2)}, u32[]{:S(2)}) collective-permute-start(bf16[3,2,2,144,128]{4,3,1,0,2:T(8,128)(2,1)S(1)} %collective-permute-done.11), channel_id=1, source_target_pairs={{2,0},{4,2},{6,4},{7,6},{5,7},{3,5},{1,3},{0,1},{10,8},{12,10},{14... | collective-permute-start | bytes 1327112 | tf_op jit(solution)/shard_map/ppermute | solution.py:133
  109.3 25.8 %collective-permute-start.32 = (bf16[3,4,144,128]{3,2,1,0:T(8,128)(2,1)}, bf16[3,4,144,128]{3,2,1,0:T(8,128)(2,1)}, u32[]{:S(2)}, u32[]{:S(2)}) collective-permute-start(bf16[3,4,144,128]{3,2,1,0:T(8,128)(2,1)} %pad_maximum_fusion.6), channel_id=1, source_target_pairs={{0,8},{1,9},{10,2},{11,3},{20,28},{21,29},{30,22},{31,23}} | collective-permute-start | bytes 1327112 | tf_op jit(solution)/shard_map/ppermute | solution.py:105
  117.5 16.1 %collective-permute-start.31 = (bf16[3,4,144,128]{3,2,1,0:T(8,128)(2,1)}, bf16[3,4,144,128]{3,2,1,0:T(8,128)(2,1)}, u32[]{:S(2)}, u32[]{:S(2)}) collective-permute-start(bf16[3,4,144,128]{3,2,1,0:T(8,128)(2,1)} %collective-permute-done.30), channel_id=1, source_target_pairs={{16,24},{17,25},{26,18},{27,19},{4,12},{5,13},{14,6},{15,7}} | collective-permute-start | bytes 1327112 | tf_op jit(solution)/shard_map/ppermute | solution.py:105
  120.5 12.4 %collective-permute-start.36 = (bf16[3,4,144,128]{3,2,1,0:T(8,128)(2,1)}, bf16[3,4,144,128]{3,2,1,0:T(8,128)(2,1)}, u32[]{:S(2)}, u32[]{:S(2)}) collective-permute-start(bf16[3,4,144,128]{3,2,1,0:T(8,128)(2,1)} %pad_maximum_fusion.7), channel_id=1, source_target_pairs={{0,16},{1,17},{10,26},{11,27},{20,4},{21,5},{30,14},{31,15}} | collective-permute-start | bytes 1327112 | tf_op jit(solution)/shard_map/ppermute | solution.py:105
  125.8 9.4 %collective-permute-start.34 = (bf16[3,4,144,128]{3,2,1,0:T(8,128)(2,1)}, bf16[3,4,144,128]{3,2,1,0:T(8,128)(2,1)}, u32[]{:S(2)}, u32[]{:S(2)}) collective-permute-start(bf16[3,4,144,128]{3,2,1,0:T(8,128)(2,1)} %collective-permute-done.33), channel_id=1, source_target_pairs={{16,24},{17,25},{26,18},{27,19},{4,12},{5,13},{14,6},{15,7}} | collective-permute-start | bytes 1327112 | tf_op jit(solution)/shard_map/ppermute | solution.py:105
  (16 other events, 61.3 us)
